TPU v7x, 32 devices: a whole 2x2x4 slice. The times are simulated.
32 devices in a mesh: groups: 2 (over y), lat: 4 (over x, core), lon: 4 (over z).
Axes of the slice: x: 2, y: 2, z: 4, core: 2. Of those that a mesh axis runs over, the one named last changes fastest.
Arguments:
- tracers: float32 [256, 256, 128], P(('groups', 'lat'), 'lon'), parts along dimension 0, may hold values from 0.3 to 12.6, as said below
- shifts: float32 [4, 3, 16, 32], P('groups'), parts along dimension 0, may hold values from 0 to 1
- diffusivity: float32 [128], P('lat'), may hold values from 0.02 to 0.2, as said below
- source_patch: int32 [4, 16, 32], P('groups'), parts along dimension 0, may hold values from 0 to 511, as said below
Outputs:
- advanced: float32 [256, 256, 128], P(('groups', 'lat'), 'lon'), parts along dimension 0
There are 2 independent parts, one for each index of `groups`. A program takes and returns all parts, laid end to end along the dimension named above; an argument that names none is the same for every part. Nothing has to cross between parts.
Inputs may be any that keep to these rules, and one draw needn't show every extreme that they name: `source_patch`: entry [s, r, c] is the global index of the departure patch of destination patch (r, c) in step s; the departure patch lies in the same tile of 8 patch columns as the destination, and in the same band of 4 patch rows or in one of the two bands on either side. For each step, tile, destination band and other source band, at most 4 destination patches take their departure patch there, and every destination band has a source band that gives exactly 4. `tracers`: positive mixing ratios. `diffusivity`: positive diffusion numbers.
All inputs are finite; a program needn't handle non-finite values.
Results may differ from a plain program's by a relative error of at most 0.0003.
Values sent between devices are 32-bit elements; how exact they have to be, the bound alone decides.
No kernel may reach another device: no remote copies, remote signals or barrier semaphores. Data moves between devices by JAX's collectives and lax.ppermute only.
A program may use at most 64 MiB of HBM per device.

v0:
```python
import math

import jax
import jax.numpy as jnp
from jax import lax
from jax.sharding import PartitionSpec as P

LEV = 4
STEPS = 2
CAP = 4


def from_behind(block, axis, distance):
    devices = range(lax.axis_size(axis))
    route = [(i - distance, i) for i in devices if i - distance in devices]
    return lax.ppermute(block, axis, route)


def extended(cells, sides, width, closed):
    for axis, dim in sides:
        count = lax.axis_size(axis)
        ends = count if closed else count - 1
        head = lax.slice_in_dim(cells, 0, width, axis=dim)
        tail = lax.slice_in_dim(cells, cells.shape[dim] - width, cells.shape[dim], axis=dim)
        cells = jnp.concatenate(
            [
                lax.ppermute(tail, axis, [(i, (i + 1) % count) for i in range(ends)]),
                cells,
                lax.ppermute(head, axis, [((i + 1) % count, i) for i in range(ends)]),
            ],
            axis=dim,
        )
    return cells


def cubic_weights(fraction):
    first_term = -fraction * (fraction - 1.0) * (fraction - 2.0) / 6.0
    second_term = (fraction + 1.0) * (fraction - 1.0) * (fraction - 2.0) / 2.0
    third_term = -(fraction + 1.0) * fraction * (fraction - 2.0) / 2.0
    fourth_term = (fraction + 1.0) * fraction * (fraction - 1.0) / 6.0
    return (first_term, second_term, third_term, fourth_term)


def cubic_matrix(fraction, extent):
    places = jnp.arange(extent)
    running = jnp.zeros(fraction.shape + (extent, extent), jnp.float32)
    for offset, weight in zip(range(-1, 3), cubic_weights(fraction)):
        target_col = jnp.clip(places + offset, 0, extent - 1)
        indicator = (target_col[:, None] == places[None, :]).astype(jnp.float32)
        running = running + weight[..., None, None] * indicator
    return running


def interpolate(patches, fraction_y, fraction_x, fraction_z):
    patch_count = patches.shape[0]
    value_count = patches.shape[2]
    weight_y = cubic_matrix(fraction_y, 8)
    weight_x = cubic_matrix(fraction_x, 8)
    plane_weights = jnp.einsum(
        "nac,nbd->nabcd", weight_y, weight_x, precision=lax.Precision.HIGHEST
    ).reshape(patch_count, 64, 64)
    flat_result = jnp.einsum(
        "nij,njv->niv", plane_weights, patches, precision=lax.Precision.HIGHEST
    )
    stacked = flat_result.reshape(patch_count, 64, LEV, value_count // LEV)
    weight_z = cubic_matrix(fraction_z, LEV)
    levelled = jnp.einsum("nlm,nimt->nilt", weight_z, stacked, precision=lax.Precision.HIGHEST)
    return levelled.reshape(patch_count, 64, value_count)


def to_patches(state_field):
    band_rows = state_field.shape[0] // 8
    band_cols = state_field.shape[1] // 8
    return (
        state_field.reshape(band_rows, 8, band_cols, 8, -1)
        .transpose(0, 2, 1, 3, 4)
        .reshape(band_rows * band_cols, 64, -1)
    )


def from_patches(patches, band_rows, band_cols):
    return (
        patches.reshape(band_rows, band_cols, 8, 8, -1)
        .transpose(0, 2, 1, 3, 4)
        .reshape(band_rows * 8, band_cols * 8, -1)
    )


def column_area(first_row, row_count, total_rows):
    latitude = ((first_row + jnp.arange(row_count)).astype(jnp.float32) + 0.5) * (
        math.pi / total_rows
    ) - 0.5 * math.pi
    return jnp.cos(latitude)


def column_mass(state_field, weights):
    return jnp.sum(weights[:, None, None] * state_field, axis=(0, 1))


def local(tracers, shifts, diffusivity, source_patch):
    lat_count = lax.axis_size("lat")
    lat_index = lax.axis_index("lat")
    lon_index = lax.axis_index("lon")
    row_count, col_count, value_count = tracers.shape
    band_rows = row_count // 8
    band_cols = col_count // 8
    per_device = band_rows * band_cols
    total_cols = source_patch.shape[2]
    band_offsets = (-2, -1, 1, 2)
    weights = column_area(lat_index * row_count, row_count, row_count * lat_count)
    devices = jnp.arange(lat_count)
    slot_range = jnp.arange(CAP)
    state_field = tracers
    target = lax.psum(column_mass(tracers, weights), ("lat", "lon"))
    for step_index in range(STEPS):
        column_ids = lax.dynamic_slice_in_dim(
            source_patch[step_index], lon_index * band_cols, band_cols, 1
        ).reshape(lat_count, per_device)
        fractions = lax.dynamic_slice_in_dim(
            shifts[step_index], lon_index * band_cols, band_cols, 2
        ).reshape(3, lat_count, per_device)
        source_row = column_ids // total_cols
        source_dev = source_row // band_rows
        source_local = (
            source_row % band_rows * band_cols + column_ids % total_cols - lon_index * band_cols
        )
        remote = source_dev != devices[:, None]
        matches = (source_dev[:, :, None] == devices[None, None, :]) & remote[:, :, None]
        slot_ranks = jnp.cumsum(matches.astype(jnp.int32), axis=1) - 1
        slot_of = jnp.sum(jnp.where(matches, slot_ranks, 0), axis=2)
        owned_here = remote & (source_dev == lat_index)
        sending = owned_here[:, :, None] & (slot_of[:, :, None] == slot_range[None, None, :])
        send_local = jnp.sum(jnp.where(sending, source_local[:, :, None], 0), axis=1)
        near_local = jnp.stack(
            [
                lax.dynamic_index_in_dim(send_local, lat_index + offset, 0, keepdims=False)
                for offset in band_offsets
            ]
        )
        own_patches = to_patches(state_field)
        send_patches = own_patches[near_local.reshape(-1)]
        my_dev = lax.dynamic_index_in_dim(source_dev, lat_index, 0, keepdims=False)
        my_slot = lax.dynamic_index_in_dim(slot_of, lat_index, 0, keepdims=False)
        my_local = lax.dynamic_index_in_dim(source_local, lat_index, 0, keepdims=False)
        my_remote = lax.dynamic_index_in_dim(remote, lat_index, 0, keepdims=False)
        my_frac = lax.dynamic_index_in_dim(fractions, lat_index, 1, keepdims=False)
        my_offset = lat_index - my_dev
        pick_index = jnp.where(my_offset < 0, my_offset + 2, my_offset + 1) * CAP + my_slot
        send_frac = jnp.sum(jnp.where(sending[None], fractions[:, :, :, None], 0.0), axis=2)
        near_frac = jnp.stack(
            [
                lax.dynamic_index_in_dim(send_frac, lat_index + offset, 1, keepdims=False)
                for offset in band_offsets
            ],
            axis=1,
        ).reshape(3, -1)
        outgoing = interpolate(send_patches, near_frac[0], near_frac[1], near_frac[2])
        outgoing = outgoing.reshape(4, CAP, 64, value_count)
        arrived = jnp.stack(
            [
                from_behind(outgoing[slot_place], "lat", offset)
                for slot_place, offset in enumerate(band_offsets)
            ]
        )
        arrived = arrived.reshape(4 * CAP, 64, value_count)
        local_done = interpolate(own_patches[my_local], my_frac[0], my_frac[1], my_frac[2])
        finished = jnp.where(my_remote[:, None, None], arrived[pick_index], local_done)
        advected = from_patches(finished, band_rows, band_cols)
        lon_wide = extended(advected, (("lon", 1),), 1, True)
        lat_wide = extended(advected, (("lat", 0),), 1, False)
        laplace = lat_wide[2:] + lat_wide[:-2] + lon_wide[:, 2:] + lon_wide[:, :-2] - 4.0 * advected
        diffused = advected + diffusivity[:, None, None] * laplace
        step_total = lax.psum(column_mass(diffused, weights), ("lat", "lon"))
        state_field = diffused * (target / step_total)[None, None, :]
    return state_field


def solution(mesh):
    return jax.shard_map(
        local,
        mesh=mesh,
        in_specs=(
            P(("groups", "lat"), "lon", None),
            P("groups", None, None, None),
            P("lat"),
            P("groups", None, None),
        ),
        out_specs=P(("groups", "lat"), "lon", None),
        check_vma=False,
    )
```

profile of v0, /device:TPU:0, one launch (start us, length us, event | category | flops | bytes accessed | tf_op | source)
XLA Modules:
  0.0 196.2 jit_solution(16985384277161938453)
XLA Ops:
  9.6 2.9 %fusion.150 = f32[16,64,128]{1,2,0:T(8,128)S(1)} fusion(f32[16,64,64]{2,1,0:T(8,128)} %copy.62, f32[16,64,128]{2,1,0:T(8,128)S(1)} %gather_fusion), kind=kOutput, calls=%fused_computation.360 | convolution fusion | flops 100663296 | bytes 1310720 | tf_op jit(solution)/shard_map/nij,njv->niv/dot_general | solution.py:62
  12.5 2.5 %convolution_bitcast_fusion.1 = f32[16,64,4,32]{1,2,3,0:T(4,128)S(1)} fusion(f32[16,64,4,32]{1,3,2,0:T(8,128)S(1)} %bitcast.153, f32[4,4]{1,0:T(4,128)S(1)} %fusion.111, f32[16]{0:T(128)S(1)} %get-tuple-element.115, f32[4,4]{1,0:T(4,128)S(1)} %fusion.110, f32[16]{0:T(128)S(1)} %get-tuple-element.116, f32[4,4]{1,0:T(4,128)S(1)} %fusion.109, ...), kind=kOutput, calls=%fused_computation.13 | convolution fusion | flops 6293248 | bytes 1049088 | tf_op jit(solution)/shard_map/nlm,nimt->nilt/dot_general | solution.py:67
  19.2 3.7 %collective-permute-start.2 = (f32[4,64,128]{1,2,0:T(8,128)}, f32[4,64,128]{1,2,0:T(8,128)}, u32[]{:S(2)}, u32[]{:S(2)}) collective-permute-start(f32[4,64,128]{1,2,0:T(8,128)} %bitcast.16), channel_id=1, source_target_pairs={{0,4},{4,8},{8,12},{1,5},{5,9},{9,13},{2,6},{6,10},{10,14},{3,7},{... | collective-permute-start | bytes 393224 | tf_op jit(solution)/shard_map/ppermute | solution.py:16
  23.7 6.3 %collective-permute-start.3 = (f32[4,64,128]{1,2,0:T(8,128)}, f32[4,64,128]{1,2,0:T(8,128)}, u32[]{:S(2)}, u32[]{:S(2)}) collective-permute-start(f32[4,64,128]{1,2,0:T(8,128)} %bitcast.18), channel_id=1, source_target_pairs={{0,8},{4,12},{1,9},{5,13},{2,10},{6,14},{3,11},{7,15},{16,24},{20,... | collective-permute-start | bytes 393224 | tf_op jit(solution)/shard_map/ppermute | solution.py:16
  34.1 1.7 copy.70
  41.7 3.5 %fusion.151 = f32[32,64,128]{1,2,0:T(8,128)S(1)} fusion(f32[32,64,64]{2,1,0:T(8,128)S(1)} %copy-done.1, f32[32,64,128]{2,1,0:T(8,128)S(1)} %gather_fusion.2), kind=kOutput, calls=%fused_computation.361 | convolution fusion | flops 201326592 | bytes 2621440 | tf_op jit(solution)/shard_map/nij,njv->niv/dot_general | solution.py:62
  45.2 1.6 broadcast_multiply_fusion
  47.1 5.6 %fusion.4 = f32[32,64,4,32]{1,2,3,0:T(4,128)} fusion(f32[32,64,4,32]{1,3,2,0:T(8,128)S(1)} %bitcast.143, f32[4,4]{1,0:T(4,128)S(1)} %copy-done.10, f32[32]{0:T(128)S(1)} %get-tuple-element.105, f32[4,4]{1,0:T(4,128)S(1)} %copy-done.8, f32[32]{0:T(128)S(1)} %get-tuple-element.106, f32[4,4]{1,0:T(4,128)S(1)} %copy-done.6, f32[32]{0:T(128)S(1)} %get-tuple-element.104, ...), kind=kOutput, calls=%fused_computation.10 | convolution fusion | flops 12586496 | bytes 2097920 | tf_op jit(solution)/shard_map/nlm,nimt->nilt/dot_general | solution.py:67
  53.4 4.8 %copy.73 = f32[32,64,4,32]{3,2,1,0:T(4,128)} copy(f32[32,64,4,32]{1,2,3,0:T(4,128)} %fusion.4) | data formatting | bytes 2097152 | tf_op jit(solution)/shard_map/nlm,nimt->nilt/transpose | solution.py:67
  58.2 4.5 %reshape.1437 = f32[4,8,8,8,128]{4,3,2,1,0:T(8,128)} reshape(f32[32,64,4,32]{3,2,1,0:T(4,128)} %copy.73) | data formatting | bytes 2097152 | tf_op jit(solution)/shard_map/reshape | solution.py:68
  62.9 2.3 %pad_maximum_fusion.8 = f32[4,4,64,128]{2,3,1,0:T(8,128)} fusion(f32[1,4,64,128]{2,3,1,0:T(8,128)} %bitcast.19, f32[1,4,64,128]{2,3,1,0:T(8,128)} %bitcast.17, f32[1,4,64,128]{2,3,1,0:T(8,128)} %bitcast.15, f32[1,4,64,128]{2,3,1,0:T(8,128)} %bitcast.13), kind=kLoop, calls=%fused_computation.34 | loop fusion | flops 393216 | bytes 1048576 | tf_op jit(solution)/shard_map/stack | solution.py:159
  65.2 1.5 copy.69
  66.7 1.6 gather_fusion.1
  68.3 1.7 select_bitcast_fusion.1
  71.5 3.0 %collective-permute-start.5 = (f32[1,64,128]{2,1,0:T(8,128)S(1)}, f32[1,64,128]{2,1,0:T(8,128)S(1)}, u32[]{:S(2)}, u32[]{:S(2)}) collective-permute-start(f32[1,64,128]{2,1,0:T(8,128)S(1)} %get-tuple-element.36), channel_id=1, source_target_pairs={{0,4},{4,8},{8,12},{1,5},{5,9},{9,13},{2,6},{6,10},{10,14},{3,7},{... | collective-permute-start | bytes 98312 | tf_op jit(solution)/shard_map/ppermute | solution.py:27
  74.5 4.8 %collective-permute-start.6 = (f32[32,1,128]{2,1,0:T(1,128)S(1)}, f32[32,1,128]{2,1,0:T(1,128)S(1)}, u32[]{:S(2)}, u32[]{:S(2)}) collective-permute-start(f32[32,1,128]{2,1,0:T(1,128)S(1)} %get-tuple-element.37), channel_id=1, source_target_pairs={{1,0},{2,1},{3,2},{0,3},{5,4},{6,5},{7,6},{4,7},{9,8},{10,9},{11,1... | collective-permute-start | bytes 49160 | tf_op jit(solution)/shard_map/ppermute | solution.py:29
  79.4 3.3 %copy.84 = f32[32,64,64]{2,1,0:T(8,128)} copy(f32[32,64,64]{0,2,1:T(8,128)} %bitcast.142) | data formatting | bytes 1048576 | tf_op jit(solution)/shard_map/reshape | solution.py:61
  84.9 1.9 multiply_reduce_fusion.1
  86.8 30.4 %all-reduce = (f32[128]{0:T(128)S(1)}, f32[128]{0:T(128)S(1)}) all-reduce(f32[128]{0:T(128)S(1)} %get-tuple-element.6, f32[128]{0:T(128)S(1)} %get-tuple-element.5), channel_id=1, replica_groups=mesh['groups'=2,'lat'=4,'lon'=4] {'lat','lon'}, use_global_device_ids=true, to_apply=%region_8.9 | all-reduce | flops 256 | bytes 2048 | tf_op jit(solution)/shard_map/psum | solution.py:114
  119.4 1.8 fusion.152
  121.3 2.5 %convolution_bitcast_fusion = f32[16,64,4,32]{1,2,3,0:T(4,128)S(1)} fusion(f32[16,64,4,32]{1,3,2,0:T(8,128)S(1)} %bitcast.154, f32[16]{0:T(128)S(1)} %copy-done.24, f32[16]{0:T(128)S(1)} %copy-done.25, f32[16]{0:T(128)S(1)} %copy-done.23, f32[16]{0:T(128)S(1)} %copy-done.22, f32[4,4]{1,0:T(4,128)S(1)} %copy-done.10, f32[4,4]{1,0:T(4,128)S(1)} %copy-done.8, ...), kind=kOutput, calls=%fused_computation.12 | convolution fusion | flops 6293248 | bytes 1049088 | tf_op jit(solution)/shard_map/nlm,nimt->nilt/dot_general | solution.py:67
  126.7 3.7 %collective-permute-start.10 = (f32[4,64,128]{1,2,0:T(8,128)S(1)}, f32[4,64,128]{1,2,0:T(8,128)}, u32[]{:S(2)}, u32[]{:S(2)}) collective-permute-start(f32[4,64,128]{1,2,0:T(8,128)S(1)} %bitcast.161), channel_id=1, source_target_pairs={{0,4},{4,8},{8,12},{1,5},{5,9},{9,13},{2,6},{6,10},{10,14},{3,7},{... | collective-permute-start | bytes 393224 | tf_op jit(solution)/shard_map/ppermute | solution.py:16
  130.5 6.3 %collective-permute-start.11 = (f32[4,64,128]{1,2,0:T(8,128)S(1)}, f32[4,64,128]{1,2,0:T(8,128)}, u32[]{:S(2)}, u32[]{:S(2)}) collective-permute-start(f32[4,64,128]{1,2,0:T(8,128)S(1)} %bitcast.162), channel_id=1, source_target_pairs={{0,8},{4,12},{1,9},{5,13},{2,10},{6,14},{3,11},{7,15},{16,24},{20,... | collective-permute-start | bytes 393224 | tf_op jit(solution)/shard_map/ppermute | solution.py:16
  136.8 3.5 %fusion.153 = f32[32,64,128]{1,2,0:T(8,128)S(1)} fusion(f32[32,64,64]{2,1,0:T(8,128)S(1)} %copy-done, f32[32,64,128]{2,1,0:T(8,128)S(1)} %gather_fusion.5), kind=kOutput, calls=%fused_computation.363 | convolution fusion | flops 201326592 | bytes 2621440 | tf_op jit(solution)/shard_map/nij,njv->niv/dot_general | solution.py:62
  140.3 4.5 %fusion.7 = f32[32,64,4,32]{1,2,3,0:T(4,128)S(1)} fusion(f32[32,64,4,32]{1,3,2,0:T(8,128)S(1)} %bitcast.144, f32[32]{0:T(128)S(1)} %copy-done.30, f32[32]{0:T(128)S(1)} %copy-done.31, f32[32]{0:T(128)S(1)} %copy-done.29, f32[32]{0:T(128)S(1)} %copy-done.27, f32[4,4]{1,0:T(4,128)S(1)} %copy-done.10, f32[4,4]{1,0:T(4,128)S(1)} %copy-done.8, ...), kind=kOutput, calls=%fused_computation.11 | convolution fusion | flops 12586496 | bytes 2097920 | tf_op jit(solution)/shard_map/nlm,nimt->nilt/dot_general | solution.py:67
  144.8 3.2 %copy.87 = f32[32,64,4,32]{3,2,1,0:T(4,128)} copy(f32[32,64,4,32]{1,2,3,0:T(4,128)S(1)} %fusion.7) | data formatting | bytes 2097152 | tf_op jit(solution)/shard_map/nlm,nimt->nilt/transpose | solution.py:67
  148.0 3.7 %reshape.1446 = f32[4,8,8,8,128]{4,3,2,1,0:T(8,128)S(1)} reshape(f32[32,64,4,32]{3,2,1,0:T(4,128)} %copy.87) | data formatting | bytes 2097152 | tf_op jit(solution)/shard_map/reshape | solution.py:68
  155.5 3.0 %collective-permute-start.13 = (f32[1,64,128]{2,1,0:T(8,128)S(1)}, f32[1,64,128]{2,1,0:T(8,128)S(1)}, u32[]{:S(2)}, u32[]{:S(2)}) collective-permute-start(f32[1,64,128]{2,1,0:T(8,128)S(1)} %get-tuple-element.28), channel_id=1, source_target_pairs={{0,4},{4,8},{8,12},{1,5},{5,9},{9,13},{2,6},{6,10},{10,14},{3,7},{... | collective-permute-start | bytes 98312 | tf_op jit(solution)/shard_map/ppermute | solution.py:27
  158.7 2.0 %collective-permute-start.15 = (f32[32,1,128]{2,1,0:T(1,128)S(1)}, f32[32,1,128]{2,1,0:T(1,128)S(1)}, u32[]{:S(2)}, u32[]{:S(2)}) collective-permute-start(f32[32,1,128]{2,1,0:T(1,128)S(1)} %get-tuple-element.30), channel_id=1, source_target_pairs={{0,1},{1,2},{2,3},{3,0},{4,5},{5,6},{6,7},{7,4},{8,9},{9,10},{10,1... | collective-permute-start | bytes 49160 | tf_op jit(solution)/shard_map/ppermute | solution.py:27
  160.7 1.7 collective-permute-done.14
  162.4 1.9 collective-permute-done.15
  165.0 29.8 %psum.23 = f32[128]{0:T(128)S(1)} all-reduce(f32[128]{0:T(128)S(1)} %multiply_reduce_fusion), channel_id=1, replica_groups=mesh['groups'=2,'lat'=4,'lon'=4] {'lat','lon'}, use_global_device_ids=true, to_apply=%region_13.14 | all-reduce | flops 128 | bytes 1024 | tf_op jit(solution)/shard_map/psum | solution.py:173
  (212 shorter events, 39.9 us)
Async XLA Ops:
  3.8 8.7 %copy-start.3 = (f32[4,4]{1,0:T(4,128)}, f32[4,4]{1,0:T(4,128)S(1)}, u32[]{:S(2)}) copy-start(f32[4,4]{1,0:T(4,128)S(1)} %fusion.108) | copy-start | bytes 196
  3.9 8.6 %copy-start.5 = (f32[4,4]{1,0:T(4,128)}, f32[4,4]{1,0:T(4,128)S(1)}, u32[]{:S(2)}) copy-start(f32[4,4]{1,0:T(4,128)S(1)} %fusion.109) | copy-start | bytes 196
  3.9 8.6 %copy-start.7 = (f32[4,4]{1,0:T(4,128)}, f32[4,4]{1,0:T(4,128)S(1)}, u32[]{:S(2)}) copy-start(f32[4,4]{1,0:T(4,128)S(1)} %fusion.110) | copy-start | bytes 196
  4.0 8.5 %copy-start.9 = (f32[4,4]{1,0:T(4,128)}, f32[4,4]{1,0:T(4,128)S(1)}, u32[]{:S(2)}) copy-start(f32[4,4]{1,0:T(4,128)S(1)} %fusion.111) | copy-start | bytes 196
  5.4 27.5 %copy-start.11 = (s32[4,32]{1,0:T(4,128)}, s32[4,32]{1,0:T(4,128)S(1)}, u32[]{:S(2)}) copy-start(s32[4,32]{1,0:T(4,128)S(1)} %select_reduce_fusion.3) | copy-start | bytes 1540
  15.0 17.8 %copy-start.21 = (pred[4,32]{1,0:T(4,128)(4,1)S(1)}, pred[4,32]{1,0:T(4,128)(4,1)}, u32[]{:S(2)}) copy-start(pred[4,32]{1,0:T(4,128)(4,1)} %copy-done.20) | copy-start | bytes 388
  15.2 47.7 %collective-permute-start = (f32[4,64,128]{1,2,0:T(8,128)S(1)}, f32[4,64,128]{1,2,0:T(8,128)}, u32[]{:S(2)}, u32[]{:S(2)}) collective-permute-start(f32[4,64,128]{1,2,0:T(8,128)S(1)} %bitcast.158), channel_id=1, source_target_pairs={{8,0},{12,4},{9,1},{13,5},{10,2},{14,6},{11,3},{15,7},{24,16},{28,... | collective-permute-start | bytes 393224 | tf_op jit(solution)/shard_map/ppermute | solution.py:16
  17.2 45.7 %collective-permute-start.1 = (f32[4,64,128]{1,2,0:T(8,128)}, f32[4,64,128]{1,2,0:T(8,128)}, u32[]{:S(2)}, u32[]{:S(2)}) collective-permute-start(f32[4,64,128]{1,2,0:T(8,128)} %bitcast.14), channel_id=1, source_target_pairs={{4,0},{8,4},{12,8},{5,1},{9,5},{13,9},{6,2},{10,6},{14,10},{7,3},{... | collective-permute-start | bytes 393224 | tf_op jit(solution)/shard_map/ppermute | solution.py:16
  19.2 43.6 %collective-permute-start.2 = (f32[4,64,128]{1,2,0:T(8,128)}, f32[4,64,128]{1,2,0:T(8,128)}, u32[]{:S(2)}, u32[]{:S(2)}) collective-permute-start(f32[4,64,128]{1,2,0:T(8,128)} %bitcast.16), channel_id=1, source_target_pairs={{0,4},{4,8},{8,12},{1,5},{5,9},{9,13},{2,6},{6,10},{10,14},{3,7},{... | collective-permute-start | bytes 393224 | tf_op jit(solution)/shard_map/ppermute | solution.py:16
  23.7 39.2 %collective-permute-start.3 = (f32[4,64,128]{1,2,0:T(8,128)}, f32[4,64,128]{1,2,0:T(8,128)}, u32[]{:S(2)}, u32[]{:S(2)}) collective-permute-start(f32[4,64,128]{1,2,0:T(8,128)} %bitcast.18), channel_id=1, source_target_pairs={{0,8},{4,12},{1,9},{5,13},{2,10},{6,14},{3,11},{7,15},{16,24},{20,... | collective-permute-start | bytes 393224 | tf_op jit(solution)/shard_map/ppermute | solution.py:16
  34.1 6.2 %copy-start.13 = (s32[4,4]{1,0:T(4,128)S(1)}, s32[4,4]{1,0:T(4,128)}, u32[]{:S(2)}) copy-start(s32[4,4]{1,0:T(4,128)} %select_reduce_fusion) | copy-start | bytes 196
  34.1 6.9 %copy-start.14 = (f32[1,4,4]{2,1,0:T(4,128)S(1)}, f32[1,4,4]{2,1,0:T(4,128)}, u32[]{:S(2)}) copy-start(f32[1,4,4]{2,1,0:T(4,128)} %get-tuple-element.57) | copy-start | bytes 196
  35.8 5.8 %copy-start.1 = (f32[32,64,64]{2,1,0:T(8,128)S(1)}, f32[32,64,64]{2,1,0:T(8,128)}, u32[]{:S(2)}) copy-start(f32[32,64,64]{2,1,0:T(8,128)} %copy.70) | copy-start | bytes 1572868
  47.1 6.3 %copy-start.19 = (pred[4,32]{1,0:T(4,128)(4,1)S(1)}, pred[4,32]{1,0:T(4,128)(4,1)}, u32[]{:S(2)}) copy-start(pred[4,32]{1,0:T(4,128)(4,1)} %copy-done.18) | copy-start | bytes 388
  68.3 11.1 %copy-start.17 = (pred[4,32]{1,0:T(4,128)(4,1)S(1)}, pred[4,32]{1,0:T(4,128)(4,1)}, u32[]{:S(2)}) copy-start(pred[4,32]{1,0:T(4,128)(4,1)} %copy-done.16) | copy-start | bytes 388
  70.2 14.7 %collective-permute-start.4 = (f32[1,64,128]{2,1,0:T(8,128)S(1)}, f32[1,64,128]{2,1,0:T(8,128)S(1)}, u32[]{:S(2)}, u32[]{:S(2)}) collective-permute-start(f32[1,64,128]{2,1,0:T(8,128)S(1)} %get-tuple-element.35), channel_id=1, source_target_pairs={{4,0},{8,4},{12,8},{5,1},{9,5},{13,9},{6,2},{10,6},{14,10},{7,3},{... | collective-permute-start | bytes 98312 | tf_op jit(solution)/shard_map/ppermute | solution.py:29
  71.5 13.4 %collective-permute-start.5 = (f32[1,64,128]{2,1,0:T(8,128)S(1)}, f32[1,64,128]{2,1,0:T(8,128)S(1)}, u32[]{:S(2)}, u32[]{:S(2)}) collective-permute-start(f32[1,64,128]{2,1,0:T(8,128)S(1)} %get-tuple-element.36), channel_id=1, source_target_pairs={{0,4},{4,8},{8,12},{1,5},{5,9},{9,13},{2,6},{6,10},{10,14},{3,7},{... | collective-permute-start | bytes 98312 | tf_op jit(solution)/shard_map/ppermute | solution.py:27
  74.5 9.7 %collective-permute-start.6 = (f32[32,1,128]{2,1,0:T(1,128)S(1)}, f32[32,1,128]{2,1,0:T(1,128)S(1)}, u32[]{:S(2)}, u32[]{:S(2)}) collective-permute-start(f32[32,1,128]{2,1,0:T(1,128)S(1)} %get-tuple-element.37), channel_id=1, source_target_pairs={{1,0},{2,1},{3,2},{0,3},{5,4},{6,5},{7,6},{4,7},{9,8},{10,9},{11,1... | collective-permute-start | bytes 49160 | tf_op jit(solution)/shard_map/ppermute | solution.py:29
  79.3 5.5 %collective-permute-start.7 = (f32[32,1,128]{2,1,0:T(1,128)S(1)}, f32[32,1,128]{2,1,0:T(1,128)S(1)}, u32[]{:S(2)}, u32[]{:S(2)}) collective-permute-start(f32[32,1,128]{2,1,0:T(1,128)S(1)} %get-tuple-element.38), channel_id=1, source_target_pairs={{0,1},{1,2},{2,3},{3,0},{4,5},{5,6},{6,7},{7,4},{8,9},{9,10},{10,1... | collective-permute-start | bytes 49160 | tf_op jit(solution)/shard_map/ppermute | solution.py:27
  123.8 13.0 %copy-start = (f32[32,64,64]{2,1,0:T(8,128)S(1)}, f32[32,64,64]{2,1,0:T(8,128)}, u32[]{:S(2)}) copy-start(f32[32,64,64]{2,1,0:T(8,128)} %copy.84) | copy-start | bytes 1572868
  123.9 27.8 %collective-permute-start.8 = (f32[4,64,128]{1,2,0:T(8,128)S(1)}, f32[4,64,128]{1,2,0:T(8,128)S(1)}, u32[]{:S(2)}, u32[]{:S(2)}) collective-permute-start(f32[4,64,128]{1,2,0:T(8,128)S(1)} %bitcast.159), channel_id=1, source_target_pairs={{8,0},{12,4},{9,1},{13,5},{10,2},{14,6},{11,3},{15,7},{24,16},{28,... | collective-permute-start | bytes 393224 | tf_op jit(solution)/shard_map/ppermute | solution.py:16
  125.4 26.4 %collective-permute-start.9 = (f32[4,64,128]{1,2,0:T(8,128)S(1)}, f32[4,64,128]{1,2,0:T(8,128)}, u32[]{:S(2)}, u32[]{:S(2)}) collective-permute-start(f32[4,64,128]{1,2,0:T(8,128)S(1)} %bitcast.160), channel_id=1, source_target_pairs={{4,0},{8,4},{12,8},{5,1},{9,5},{13,9},{6,2},{10,6},{14,10},{7,3},{... | collective-permute-start | bytes 393224 | tf_op jit(solution)/shard_map/ppermute | solution.py:16
  126.7 25.0 %collective-permute-start.10 = (f32[4,64,128]{1,2,0:T(8,128)S(1)}, f32[4,64,128]{1,2,0:T(8,128)}, u32[]{:S(2)}, u32[]{:S(2)}) collective-permute-start(f32[4,64,128]{1,2,0:T(8,128)S(1)} %bitcast.161), channel_id=1, source_target_pairs={{0,4},{4,8},{8,12},{1,5},{5,9},{9,13},{2,6},{6,10},{10,14},{3,7},{... | collective-permute-start | bytes 393224 | tf_op jit(solution)/shard_map/ppermute | solution.py:16
  130.5 9.8 %copy-start.27 = (f32[32]{0:T(128)S(1)}, f32[32]{0:T(128)}, u32[]{:S(2)}) copy-start(f32[32]{0:T(128)} %get-tuple-element.9) | copy-start | bytes 388
  130.5 9.8 %copy-start.29 = (f32[32]{0:T(128)S(1)}, f32[32]{0:T(128)}, u32[]{:S(2)}) copy-start(f32[32]{0:T(128)} %get-tuple-element.83) | copy-start | bytes 388
  130.5 9.8 %copy-start.30 = (f32[32]{0:T(128)S(1)}, f32[32]{0:T(128)}, u32[]{:S(2)}) copy-start(f32[32]{0:T(128)} %get-tuple-element.84) | copy-start | bytes 388
  130.5 9.8 %copy-start.31 = (f32[32]{0:T(128)S(1)}, f32[32]{0:T(128)}, u32[]{:S(2)}) copy-start(f32[32]{0:T(128)} %get-tuple-element.85) | copy-start | bytes 388
  130.5 21.2 %collective-permute-start.11 = (f32[4,64,128]{1,2,0:T(8,128)S(1)}, f32[4,64,128]{1,2,0:T(8,128)}, u32[]{:S(2)}, u32[]{:S(2)}) collective-permute-start(f32[4,64,128]{1,2,0:T(8,128)S(1)} %bitcast.162), channel_id=1, source_target_pairs={{0,8},{4,12},{1,9},{5,13},{2,10},{6,14},{3,11},{7,15},{16,24},{20,... | collective-permute-start | bytes 393224 | tf_op jit(solution)/shard_map/ppermute | solution.py:16
  154.2 10.0 %collective-permute-start.12 = (f32[1,64,128]{2,1,0:T(8,128)S(1)}, f32[1,64,128]{2,1,0:T(8,128)S(1)}, u32[]{:S(2)}, u32[]{:S(2)}) collective-permute-start(f32[1,64,128]{2,1,0:T(8,128)S(1)} %get-tuple-element.27), channel_id=1, source_target_pairs={{4,0},{8,4},{12,8},{5,1},{9,5},{13,9},{6,2},{10,6},{14,10},{7,3},{... | collective-permute-start | bytes 98312 | tf_op jit(solution)/shard_map/ppermute | solution.py:29
  155.5 8.7 %collective-permute-start.13 = (f32[1,64,128]{2,1,0:T(8,128)S(1)}, f32[1,64,128]{2,1,0:T(8,128)S(1)}, u32[]{:S(2)}, u32[]{:S(2)}) collective-permute-start(f32[1,64,128]{2,1,0:T(8,128)S(1)} %get-tuple-element.28), channel_id=1, source_target_pairs={{0,4},{4,8},{8,12},{1,5},{5,9},{9,13},{2,6},{6,10},{10,14},{3,7},{... | collective-permute-start | bytes 98312 | tf_op jit(solution)/shard_map/ppermute | solution.py:27
  158.6 3.8 %collective-permute-start.14 = (f32[32,1,128]{2,1,0:T(1,128)S(1)}, f32[32,1,128]{2,1,0:T(1,128)S(1)}, u32[]{:S(2)}, u32[]{:S(2)}) collective-permute-start(f32[32,1,128]{2,1,0:T(1,128)S(1)} %get-tuple-element.29), channel_id=1, source_target_pairs={{1,0},{2,1},{3,2},{0,3},{5,4},{6,5},{7,6},{4,7},{9,8},{10,9},{11,1... | collective-permute-start | bytes 49160 | tf_op jit(solution)/shard_map/ppermute | solution.py:29
  158.7 5.6 %collective-permute-start.15 = (f32[32,1,128]{2,1,0:T(1,128)S(1)}, f32[32,1,128]{2,1,0:T(1,128)S(1)}, u32[]{:S(2)}, u32[]{:S(2)}) collective-permute-start(f32[32,1,128]{2,1,0:T(1,128)S(1)} %get-tuple-element.30), channel_id=1, source_target_pairs={{0,1},{1,2},{2,3},{3,0},{4,5},{5,6},{6,7},{7,4},{8,9},{9,10},{10,1... | collective-permute-start | bytes 49160 | tf_op jit(solution)/shard_map/ppermute | solution.py:27
  (16 other events, 35.7 us)
where the time goes:
time: 197 us; the launch traced here: 196 us
  blocking collectives  60.2 us (31%)
  starting transfers between devices  40.9 us (21%)
  local copies, waits for them, and re-layouts  39.2 us (20%)
  matrix products  26.7 us (14%)
  other arithmetic  24.1 us (12%)
  waiting for transfers between devices  4.2 us (2%)
    psum x1, blocking collectives, local(): target = lax.psum(column_mass(tracers, weights), ('lat', 'lon'))  30.4 us
    psum x1, blocking collectives, local(): step_total = lax.psum(column_mass(diffused, weights), ('lat', 'lon'))  29.8 us
    ppermute x8, starting transfers between devices, from_behind(): return lax.ppermute(block, axis, route)  25.3 us
    dot_general x4, matrix products, interpolate(): jnp.einsum('nlm,nimt->nilt', weight_z, stacked, precision=lax.Precision.H...  15.1 us
    dot_general x4, matrix products, interpolate(): jnp.einsum('nij,njv->niv', plane_weights, patches, precision=lax.Precisio...  11.6 us
    reshape x2, local copies, waits for them, and re-layouts, interpolate(): return levelled.reshape(patch_count, 64, value_count)  8.25 us
    ppermute x4, starting transfers between devices, extended(): lax.ppermute(tail, axis, [(i, (i + 1) % count) for i in range(ends)])  8.08 us
    transpose x2, local copies, waits for them, and re-layouts, interpolate(): jnp.einsum('nlm,nimt->nilt', weight_z, stacked, precision=lax.Precision.H...  8.02 us
  transfers between devices with their start and end apart: 16, of which 3 were waited for; matrix products, arithmetic and copies ran while one was open for 28% of the time, Pallas kernels for 0%

commit v1 on v0

--- a/solution.py
+++ b/solution.py
@@ -14,6 +14,21 @@
     devices = range(lax.axis_size(axis))
     route = [(i - distance, i) for i in devices if i - distance in devices]
     return lax.ppermute(block, axis, route)
+
+
+def all_sum(value, axes):
+    for axis in axes:
+        count = lax.axis_size(axis)
+        if count & (count - 1):
+            value = lax.psum(value, axis)
+            continue
+        distance = 1
+        while distance < count:
+            value = value + lax.ppermute(
+                value, axis, [(i, i ^ distance) for i in range(count)]
+            )
+            distance *= 2
+    return value
 
 
 def extended(cells, sides, width, closed):
@@ -111,7 +126,8 @@
     devices = jnp.arange(lat_count)
     slot_range = jnp.arange(CAP)
     state_field = tracers
-    target = lax.psum(column_mass(tracers, weights), ("lat", "lon"))
+    target_part = column_mass(tracers, weights)
+    target = None
     for step_index in range(STEPS):
         column_ids = lax.dynamic_slice_in_dim(
             source_patch[step_index], lon_index * band_cols, band_cols, 1
@@ -170,7 +186,13 @@
         lat_wide = extended(advected, (("lat", 0),), 1, False)
         laplace = lat_wide[2:] + lat_wide[:-2] + lon_wide[:, 2:] + lon_wide[:, :-2] - 4.0 * advected
         diffused = advected + diffusivity[:, None, None] * laplace
-        step_total = lax.psum(column_mass(diffused, weights), ("lat", "lon"))
+        if target is None:
+            both = all_sum(
+                jnp.concatenate([target_part, column_mass(diffused, weights)]), ("lon", "lat")
+            )
+            target, step_total = both[:value_count], both[value_count:]
+        else:
+            step_total = all_sum(column_mass(diffused, weights), ("lon", "lat"))
         state_field = diffused * (target / step_total)[None, None, :]
     return state_field
 

time: 197 us -> 160 us (0.81)
  the two profiles are of different devices: /device:TPU:0 before, /device:TPU:1 now
where the time goes in v1:
time: 160 us; the launch traced here: 158 us
  starting transfers between devices  46.9 us (29%)
  local copies, waits for them, and re-layouts  39.6 us (25%)
  matrix products  26.6 us (17%)
  waiting for transfers between devices  22.7 us (14%)
  other arithmetic  21 us (13%)
    ppermute x8, starting transfers between devices, from_behind(): return lax.ppermute(block, axis, route)  22.1 us
    ppermute x8, waiting for transfers between devices, all_sum(): lax.ppermute(value, axis, [(i, i ^ distance) for i in range(count)])  15.4 us
    dot_general x4, matrix products, interpolate(): jnp.einsum('nlm,nimt->nilt', weight_z, stacked, precision=lax.Precision.H...  15.1 us
    dot_general x4, matrix products, interpolate(): jnp.einsum('nij,njv->niv', plane_weights, patches, precision=lax.Precisio...  11.6 us
    ppermute x4, starting transfers between devices, extended(): lax.ppermute(head, axis, [((i + 1) % count, i) for i in range(ends)])  11.2 us
    reshape x2, local copies, waits for them, and re-layouts, interpolate(): return levelled.reshape(patch_count, 64, value_count)  8.24 us
    transpose x2, local copies, waits for them, and re-layouts, interpolate(): jnp.einsum('nlm,nimt->nilt', weight_z, stacked, precision=lax.Precision.H...  8 us
    reshape x4, local copies, waits for them, and re-layouts, interpolate(): plane_weights = jnp.einsum('nac,nbd->nabcd', weight_y, weight_x, precisio...  7.96 us
  transfers between devices with their start and end apart: 24, of which 11 were waited for; matrix products, arithmetic and copies ran while one was open for 34% of the time, Pallas kernels for 0%

profile of v1, /device:TPU:1, one launch (start us, length us, event | category | flops | bytes accessed | tf_op | source)
XLA Modules:
  0.0 157.8 jit_solution(17607527095406759475)
XLA Ops:
  9.3 2.9 %fusion.151 = f32[16,64,128]{1,2,0:T(8,128)S(1)} fusion(f32[16,64,64]{2,1,0:T(8,128)} %copy.62, f32[16,64,128]{2,1,0:T(8,128)S(1)} %gather_fusion), kind=kOutput, calls=%fused_computation.364 | convolution fusion | flops 100663296 | bytes 1310720 | tf_op jit(solution)/shard_map/nij,njv->niv/dot_general | solution.py:77
  12.2 2.5 %convolution_bitcast_fusion.1 = f32[16,64,4,32]{1,2,3,0:T(4,128)S(1)} fusion(f32[16,64,4,32]{1,3,2,0:T(8,128)S(1)} %bitcast.153, f32[4,4]{1,0:T(4,128)S(1)} %fusion.111, f32[16]{0:T(128)S(1)} %get-tuple-element.105, f32[4,4]{1,0:T(4,128)S(1)} %fusion.110, f32[16]{0:T(128)S(1)} %get-tuple-element.106, f32[4,4]{1,0:T(4,128)S(1)} %fusion.109, ...), kind=kOutput, calls=%fused_computation.13 | convolution fusion | flops 6293248 | bytes 1049088 | tf_op jit(solution)/shard_map/nlm,nimt->nilt/dot_general | solution.py:82
  16.9 2.0 %collective-permute-start.1 = (f32[4,64,128]{1,2,0:T(8,128)}, f32[4,64,128]{1,2,0:T(8,128)}, u32[]{:S(2)}, u32[]{:S(2)}) collective-permute-start(f32[4,64,128]{1,2,0:T(8,128)} %bitcast.14), channel_id=1, source_target_pairs={{4,0},{8,4},{12,8},{5,1},{9,5},{13,9},{6,2},{10,6},{14,10},{7,3},{... | collective-permute-start | bytes 393224 | tf_op jit(solution)/shard_map/ppermute | solution.py:16
  19.6 5.2 %collective-permute-start.2 = (f32[4,64,128]{1,2,0:T(8,128)}, f32[4,64,128]{1,2,0:T(8,128)}, u32[]{:S(2)}, u32[]{:S(2)}) collective-permute-start(f32[4,64,128]{1,2,0:T(8,128)} %bitcast.16), channel_id=1, source_target_pairs={{0,4},{4,8},{8,12},{1,5},{5,9},{9,13},{2,6},{6,10},{10,14},{3,7},{... | collective-permute-start | bytes 393224 | tf_op jit(solution)/shard_map/ppermute | solution.py:16
  25.5 2.8 %collective-permute-start.3 = (f32[4,64,128]{1,2,0:T(8,128)}, f32[4,64,128]{1,2,0:T(8,128)}, u32[]{:S(2)}, u32[]{:S(2)}) collective-permute-start(f32[4,64,128]{1,2,0:T(8,128)} %bitcast.18), channel_id=1, source_target_pairs={{0,8},{4,12},{1,9},{5,13},{2,10},{6,14},{3,11},{7,15},{16,24},{20,... | collective-permute-start | bytes 393224 | tf_op jit(solution)/shard_map/ppermute | solution.py:16
  39.4 3.5 %fusion.152 = f32[32,64,128]{1,2,0:T(8,128)S(1)} fusion(f32[32,64,64]{2,1,0:T(8,128)S(1)} %copy-done.2, f32[32,64,128]{2,1,0:T(8,128)S(1)} %gather_fusion.2), kind=kOutput, calls=%fused_computation.365 | convolution fusion | flops 201326592 | bytes 2621440 | tf_op jit(solution)/shard_map/nij,njv->niv/dot_general | solution.py:77
  44.9 5.5 %fusion.4 = f32[32,64,4,32]{1,2,3,0:T(4,128)} fusion(f32[32,64,4,32]{1,3,2,0:T(8,128)S(1)} %bitcast.143, f32[4,4]{1,0:T(4,128)S(1)} %fusion.111, f32[32]{0:T(128)S(1)} %get-tuple-element.95, f32[4,4]{1,0:T(4,128)S(1)} %fusion.110, f32[32]{0:T(128)S(1)} %get-tuple-element.96, f32[4,4]{1,0:T(4,128)S(1)} %fusion.109, f32[32]{0:T(128)S(1)} %get-tuple-element.94, ...), kind=kOutput, calls=%fused_computation.10 | convolution fusion | flops 12586496 | bytes 2097920 | tf_op jit(solution)/shard_map/nlm,nimt->nilt/dot_general | solution.py:82
  50.5 4.8 %copy.73 = f32[32,64,4,32]{3,2,1,0:T(4,128)} copy(f32[32,64,4,32]{1,2,3,0:T(4,128)} %fusion.4) | data formatting | bytes 2097152 | tf_op jit(solution)/shard_map/nlm,nimt->nilt/transpose | solution.py:82
  55.3 4.5 %reshape.1437 = f32[4,8,8,8,128]{4,3,2,1,0:T(8,128)} reshape(f32[32,64,4,32]{3,2,1,0:T(4,128)} %copy.73) | data formatting | bytes 2097152 | tf_op jit(solution)/shard_map/reshape | solution.py:83
  60.0 2.3 %pad_maximum_fusion.8 = f32[4,4,64,128]{2,3,1,0:T(8,128)} fusion(f32[1,4,64,128]{2,3,1,0:T(8,128)} %bitcast.19, f32[1,4,64,128]{2,3,1,0:T(8,128)} %bitcast.17, f32[1,4,64,128]{2,3,1,0:T(8,128)} %bitcast.15, f32[1,4,64,128]{2,3,1,0:T(8,128)} %bitcast.13), kind=kLoop, calls=%fused_computation.34 | loop fusion | flops 393216 | bytes 1048576 | tf_op jit(solution)/shard_map/stack | solution.py:175
  67.4 3.3 %collective-permute-start.4 = (f32[1,64,128]{2,1,0:T(8,128)S(1)}, f32[1,64,128]{2,1,0:T(8,128)S(1)}, u32[]{:S(2)}, u32[]{:S(2)}) collective-permute-start(f32[1,64,128]{2,1,0:T(8,128)S(1)} %get-tuple-element.33), channel_id=1, source_target_pairs={{4,0},{8,4},{12,8},{5,1},{9,5},{13,9},{6,2},{10,6},{14,10},{7,3},{... | collective-permute-start | bytes 98312 | tf_op jit(solution)/shard_map/ppermute | solution.py:44
  70.7 2.2 %collective-permute-start.5 = (f32[1,64,128]{2,1,0:T(8,128)S(1)}, f32[1,64,128]{2,1,0:T(8,128)S(1)}, u32[]{:S(2)}, u32[]{:S(2)}) collective-permute-start(f32[1,64,128]{2,1,0:T(8,128)S(1)} %get-tuple-element.34), channel_id=1, source_target_pairs={{0,4},{4,8},{8,12},{1,5},{5,9},{9,13},{2,6},{6,10},{10,14},{3,7},{... | collective-permute-start | bytes 98312 | tf_op jit(solution)/shard_map/ppermute | solution.py:42
  73.0 4.5 %collective-permute-start.6 = (f32[32,1,128]{2,1,0:T(1,128)S(1)}, f32[32,1,128]{2,1,0:T(1,128)S(1)}, u32[]{:S(2)}, u32[]{:S(2)}) collective-permute-start(f32[32,1,128]{2,1,0:T(1,128)S(1)} %get-tuple-element.35), channel_id=1, source_target_pairs={{1,0},{2,1},{3,2},{0,3},{5,4},{6,5},{7,6},{4,7},{9,8},{10,9},{11,1... | collective-permute-start | bytes 49160 | tf_op jit(solution)/shard_map/ppermute | solution.py:44
  78.4 3.5 %collective-permute-done.7 = f32[32,1,128]{2,1,0:T(1,128)S(1)} collective-permute-done((f32[32,1,128]{2,1,0:T(1,128)S(1)}, f32[32,1,128]{2,1,0:T(1,128)S(1)}, u32[]{:S(2)}, u32[]{:S(2)}) %collective-permute-start.7) | collective-permute-done | bytes 16416 | tf_op jit(solution)/shard_map/ppermute | solution.py:42
  82.8 2.4 %collective-permute-done.8 = f32[256]{0:T(256)S(1)} collective-permute-done((f32[256]{0:T(256)S(1)}, f32[256]{0:T(256)S(1)}, u32[]{:S(2)}, u32[]{:S(2)}) %collective-permute-start.8) | collective-permute-done | bytes 1056 | tf_op jit(solution)/shard_map/ppermute | solution.py:27
  85.2 3.3 %collective-permute-done.9 = f32[256]{0:T(256)S(1)} collective-permute-done((f32[256]{0:T(256)S(1)}, f32[256]{0:T(256)S(1)}, u32[]{:S(2)}, u32[]{:S(2)}) %collective-permute-start.9) | collective-permute-done | bytes 1056 | tf_op jit(solution)/shard_map/ppermute | solution.py:27
  88.5 3.9 %collective-permute-start.10 = (f32[256]{0:T(256)S(1)}, f32[256]{0:T(256)S(1)}, u32[]{:S(2)}, u32[]{:S(2)}) collective-permute-start(f32[256]{0:T(256)S(1)} %add.1120), channel_id=1, source_target_pairs={{0,4},{4,0},{8,12},{12,8},{1,5},{5,1},{9,13},{13,9},{2,6},{6,2},{1... | collective-permute-start | bytes 3080 | tf_op jit(solution)/shard_map/ppermute | solution.py:27
  93.3 3.3 %copy.84 = f32[32,64,64]{2,1,0:T(8,128)} copy(f32[32,64,64]{0,2,1:T(8,128)} %bitcast.142) | data formatting | bytes 1048576 | tf_op jit(solution)/shard_map/reshape | solution.py:76
  101.8 2.5 %convolution_bitcast_fusion = f32[16,64,4,32]{1,2,3,0:T(4,128)S(1)} fusion(f32[16,64,4,32]{1,3,2,0:T(8,128)S(1)} %bitcast.154, f32[16]{0:T(128)S(1)} %copy-done.11, f32[16]{0:T(128)S(1)} %copy-done.12, f32[16]{0:T(128)S(1)} %copy-done.10, f32[16]{0:T(128)S(1)} %get-tuple-element.90, f32[4,4]{1,0:T(4,128)S(1)} %fusion.111, f32[4,4]{1,0:T(4,128)S(1)} %fusion.110, ...), kind=kOutput, calls=%fused_computation.12 | convolution fusion | flops 6293248 | bytes 1049088 | tf_op jit(solution)/shard_map/nlm,nimt->nilt/dot_general | solution.py:82
  105.9 2.5 %collective-permute-start.13 = (f32[4,64,128]{1,2,0:T(8,128)S(1)}, f32[4,64,128]{1,2,0:T(8,128)}, u32[]{:S(2)}, u32[]{:S(2)}) collective-permute-start(f32[4,64,128]{1,2,0:T(8,128)S(1)} %bitcast.160), channel_id=1, source_target_pairs={{4,0},{8,4},{12,8},{5,1},{9,5},{13,9},{6,2},{10,6},{14,10},{7,3},{... | collective-permute-start | bytes 393224 | tf_op jit(solution)/shard_map/ppermute | solution.py:16
  108.4 4.2 %collective-permute-start.14 = (f32[4,64,128]{1,2,0:T(8,128)S(1)}, f32[4,64,128]{1,2,0:T(8,128)}, u32[]{:S(2)}, u32[]{:S(2)}) collective-permute-start(f32[4,64,128]{1,2,0:T(8,128)S(1)} %bitcast.161), channel_id=1, source_target_pairs={{0,4},{4,8},{8,12},{1,5},{5,9},{9,13},{2,6},{6,10},{10,14},{3,7},{... | collective-permute-start | bytes 393224 | tf_op jit(solution)/shard_map/ppermute | solution.py:16
  112.7 2.8 %collective-permute-start.15 = (f32[4,64,128]{1,2,0:T(8,128)S(1)}, f32[4,64,128]{1,2,0:T(8,128)}, u32[]{:S(2)}, u32[]{:S(2)}) collective-permute-start(f32[4,64,128]{1,2,0:T(8,128)S(1)} %bitcast.162), channel_id=1, source_target_pairs={{0,8},{4,12},{1,9},{5,13},{2,10},{6,14},{3,11},{7,15},{16,24},{20,... | collective-permute-start | bytes 393224 | tf_op jit(solution)/shard_map/ppermute | solution.py:16
  115.5 3.5 %fusion.154 = f32[32,64,128]{1,2,0:T(8,128)S(1)} fusion(f32[32,64,64]{2,1,0:T(8,128)S(1)} %copy-done.1, f32[32,64,128]{2,1,0:T(8,128)S(1)} %gather_fusion.5), kind=kOutput, calls=%fused_computation.367 | convolution fusion | flops 201326592 | bytes 2621440 | tf_op jit(solution)/shard_map/nij,njv->niv/dot_general | solution.py:77
  119.0 4.5 %fusion.7 = f32[32,64,4,32]{1,2,3,0:T(4,128)S(1)} fusion(f32[32,64,4,32]{1,3,2,0:T(8,128)S(1)} %bitcast.144, f32[32]{0:T(128)S(1)} %copy-done.17, f32[32]{0:T(128)S(1)} %copy-done.18, f32[32]{0:T(128)S(1)} %copy-done.16, f32[32]{0:T(128)S(1)} %copy-done.14, f32[4,4]{1,0:T(4,128)S(1)} %fusion.111, f32[4,4]{1,0:T(4,128)S(1)} %fusion.110, ...), kind=kOutput, calls=%fused_computation.11 | convolution fusion | flops 12586496 | bytes 2097920 | tf_op jit(solution)/shard_map/nlm,nimt->nilt/dot_general | solution.py:82
  123.5 3.2 %copy.87 = f32[32,64,4,32]{3,2,1,0:T(4,128)} copy(f32[32,64,4,32]{1,2,3,0:T(4,128)S(1)} %fusion.7) | data formatting | bytes 2097152 | tf_op jit(solution)/shard_map/nlm,nimt->nilt/transpose | solution.py:82
  126.7 3.7 %reshape.1446 = f32[4,8,8,8,128]{4,3,2,1,0:T(8,128)S(1)} reshape(f32[32,64,4,32]{3,2,1,0:T(4,128)} %copy.87) | data formatting | bytes 2097152 | tf_op jit(solution)/shard_map/reshape | solution.py:83
  132.9 3.3 %collective-permute-start.16 = (f32[1,64,128]{2,1,0:T(8,128)S(1)}, f32[1,64,128]{2,1,0:T(8,128)S(1)}, u32[]{:S(2)}, u32[]{:S(2)}) collective-permute-start(f32[1,64,128]{2,1,0:T(8,128)S(1)} %get-tuple-element.25), channel_id=1, source_target_pairs={{4,0},{8,4},{12,8},{5,1},{9,5},{13,9},{6,2},{10,6},{14,10},{7,3},{... | collective-permute-start | bytes 98312 | tf_op jit(solution)/shard_map/ppermute | solution.py:44
  136.3 2.2 %collective-permute-start.17 = (f32[1,64,128]{2,1,0:T(8,128)S(1)}, f32[1,64,128]{2,1,0:T(8,128)S(1)}, u32[]{:S(2)}, u32[]{:S(2)}) collective-permute-start(f32[1,64,128]{2,1,0:T(8,128)S(1)} %get-tuple-element.26), channel_id=1, source_target_pairs={{0,4},{4,8},{8,12},{1,5},{5,9},{9,13},{2,6},{6,10},{10,14},{3,7},{... | collective-permute-start | bytes 98312 | tf_op jit(solution)/shard_map/ppermute | solution.py:42
  143.8 2.4 %collective-permute-done.20 = f32[128]{0:T(128)S(1)} collective-permute-done((f32[128]{0:T(128)S(1)}, f32[128]{0:T(128)S(1)}, u32[]{:S(2)}, u32[]{:S(2)}) %collective-permute-start.20) | collective-permute-done | bytes 544 | tf_op jit(solution)/shard_map/ppermute | solution.py:27
  146.2 3.3 %collective-permute-done.21 = f32[128]{0:T(128)S(1)} collective-permute-done((f32[128]{0:T(128)S(1)}, f32[128]{0:T(128)S(1)}, u32[]{:S(2)}, u32[]{:S(2)}) %collective-permute-start.21) | collective-permute-done | bytes 544 | tf_op jit(solution)/shard_map/ppermute | solution.py:27
  149.5 3.6 %collective-permute-start.22 = (f32[128]{0:T(128)S(1)}, f32[128]{0:T(128)S(1)}, u32[]{:S(2)}, u32[]{:S(2)}) collective-permute-start(f32[128]{0:T(128)S(1)} %add.1153), channel_id=1, source_target_pairs={{0,4},{4,0},{8,12},{12,8},{1,5},{5,1},{9,13},{13,9},{2,6},{6,2},{1... | collective-permute-start | bytes 1544 | tf_op jit(solution)/shard_map/ppermute | solution.py:27
  153.9 2.4 %collective-permute-done.23 = f32[128]{0:T(128)S(1)} collective-permute-done((f32[128]{0:T(128)S(1)}, f32[128]{0:T(128)S(1)}, u32[]{:S(2)}, u32[]{:S(2)}) %collective-permute-start.23) | collective-permute-done | bytes 544 | tf_op jit(solution)/shard_map/ppermute | solution.py:27
  (210 shorter events, 50.4 us)
Async XLA Ops:
  14.9 45.1 %collective-permute-start = (f32[4,64,128]{1,2,0:T(8,128)S(1)}, f32[4,64,128]{1,2,0:T(8,128)}, u32[]{:S(2)}, u32[]{:S(2)}) collective-permute-start(f32[4,64,128]{1,2,0:T(8,128)S(1)} %bitcast.158), channel_id=1, source_target_pairs={{8,0},{12,4},{9,1},{13,5},{10,2},{14,6},{11,3},{15,7},{24,16},{28,... | collective-permute-start | bytes 393224 | tf_op jit(solution)/shard_map/ppermute | solution.py:16
  16.9 43.1 %collective-permute-start.1 = (f32[4,64,128]{1,2,0:T(8,128)}, f32[4,64,128]{1,2,0:T(8,128)}, u32[]{:S(2)}, u32[]{:S(2)}) collective-permute-start(f32[4,64,128]{1,2,0:T(8,128)} %bitcast.14), channel_id=1, source_target_pairs={{4,0},{8,4},{12,8},{5,1},{9,5},{13,9},{6,2},{10,6},{14,10},{7,3},{... | collective-permute-start | bytes 393224 | tf_op jit(solution)/shard_map/ppermute | solution.py:16
  19.6 40.4 %collective-permute-start.2 = (f32[4,64,128]{1,2,0:T(8,128)}, f32[4,64,128]{1,2,0:T(8,128)}, u32[]{:S(2)}, u32[]{:S(2)}) collective-permute-start(f32[4,64,128]{1,2,0:T(8,128)} %bitcast.16), channel_id=1, source_target_pairs={{0,4},{4,8},{8,12},{1,5},{5,9},{9,13},{2,6},{6,10},{10,14},{3,7},{... | collective-permute-start | bytes 393224 | tf_op jit(solution)/shard_map/ppermute | solution.py:16
  25.5 34.5 %collective-permute-start.3 = (f32[4,64,128]{1,2,0:T(8,128)}, f32[4,64,128]{1,2,0:T(8,128)}, u32[]{:S(2)}, u32[]{:S(2)}) collective-permute-start(f32[4,64,128]{1,2,0:T(8,128)} %bitcast.18), channel_id=1, source_target_pairs={{0,8},{4,12},{1,9},{5,13},{2,10},{6,14},{3,11},{7,15},{16,24},{20,... | collective-permute-start | bytes 393224 | tf_op jit(solution)/shard_map/ppermute | solution.py:16
  32.8 6.7 %copy-start.2 = (f32[32,64,64]{2,1,0:T(8,128)S(1)}, f32[32,64,64]{2,1,0:T(8,128)}, u32[]{:S(2)}) copy-start(f32[32,64,64]{2,1,0:T(8,128)} %copy.70) | copy-start | bytes 1572868
  65.4 16.5 %copy-start = (f32[32,64,128]{2,1,0:T(8,128)S(1)}, f32[32,64,128]{2,1,0:T(8,128)}, u32[]{:S(2)}) copy-start(f32[32,64,128]{2,1,0:T(8,128)} %param.4) | copy-start | bytes 3145732
  65.4 16.5 %copy-start.4 = (f32[32]{0:T(128)S(1)}, f32[32]{0:T(128)}, u32[]{:S(2)}) copy-start(f32[32]{0:T(128)} %param.6) | copy-start | bytes 388
  67.2 18.0 %copy-start.19 = (s32[16]{0:T(128)S(1)}, s32[16]{0:T(128)}, u32[]{:S(2)}) copy-start(s32[16]{0:T(128)} %fusion.121) | copy-start | bytes 196
  67.2 26.0 %copy-start.6 = (pred[4,32]{1,0:T(4,128)(4,1)S(1)}, pred[4,32]{1,0:T(4,128)(4,1)}, u32[]{:S(2)}) copy-start(pred[4,32]{1,0:T(4,128)(4,1)} %copy-done.5) | copy-start | bytes 388
  67.4 14.5 %collective-permute-start.4 = (f32[1,64,128]{2,1,0:T(8,128)S(1)}, f32[1,64,128]{2,1,0:T(8,128)S(1)}, u32[]{:S(2)}, u32[]{:S(2)}) collective-permute-start(f32[1,64,128]{2,1,0:T(8,128)S(1)} %get-tuple-element.33), channel_id=1, source_target_pairs={{4,0},{8,4},{12,8},{5,1},{9,5},{13,9},{6,2},{10,6},{14,10},{7,3},{... | collective-permute-start | bytes 98312 | tf_op jit(solution)/shard_map/ppermute | solution.py:44
  70.7 11.2 %collective-permute-start.5 = (f32[1,64,128]{2,1,0:T(8,128)S(1)}, f32[1,64,128]{2,1,0:T(8,128)S(1)}, u32[]{:S(2)}, u32[]{:S(2)}) collective-permute-start(f32[1,64,128]{2,1,0:T(8,128)S(1)} %get-tuple-element.34), channel_id=1, source_target_pairs={{0,4},{4,8},{8,12},{1,5},{5,9},{9,13},{2,6},{6,10},{10,14},{3,7},{... | collective-permute-start | bytes 98312 | tf_op jit(solution)/shard_map/ppermute | solution.py:42
  73.0 5.4 %collective-permute-start.6 = (f32[32,1,128]{2,1,0:T(1,128)S(1)}, f32[32,1,128]{2,1,0:T(1,128)S(1)}, u32[]{:S(2)}, u32[]{:S(2)}) collective-permute-start(f32[32,1,128]{2,1,0:T(1,128)S(1)} %get-tuple-element.35), channel_id=1, source_target_pairs={{1,0},{2,1},{3,2},{0,3},{5,4},{6,5},{7,6},{4,7},{9,8},{10,9},{11,1... | collective-permute-start | bytes 49160 | tf_op jit(solution)/shard_map/ppermute | solution.py:44
  77.5 4.4 %collective-permute-start.7 = (f32[32,1,128]{2,1,0:T(1,128)S(1)}, f32[32,1,128]{2,1,0:T(1,128)S(1)}, u32[]{:S(2)}, u32[]{:S(2)}) collective-permute-start(f32[32,1,128]{2,1,0:T(1,128)S(1)} %get-tuple-element.36), channel_id=1, source_target_pairs={{0,1},{1,2},{2,3},{3,0},{4,5},{5,6},{6,7},{7,4},{8,9},{9,10},{10,1... | collective-permute-start | bytes 49160 | tf_op jit(solution)/shard_map/ppermute | solution.py:42
  82.7 2.5 %collective-permute-start.8 = (f32[256]{0:T(256)S(1)}, f32[256]{0:T(256)S(1)}, u32[]{:S(2)}, u32[]{:S(2)}) collective-permute-start(f32[256]{0:T(256)S(1)} %pad_maximum_fusion.12), channel_id=1, source_target_pairs={{0,1},{1,0},{2,3},{3,2},{4,5},{5,4},{6,7},{7,6},{8,9},{9,8},{10,11... | collective-permute-start | bytes 3080 | tf_op jit(solution)/shard_map/ppermute | solution.py:27
  85.2 3.3 %collective-permute-start.9 = (f32[256]{0:T(256)S(1)}, f32[256]{0:T(256)S(1)}, u32[]{:S(2)}, u32[]{:S(2)}) collective-permute-start(f32[256]{0:T(256)S(1)} %fusion.134), channel_id=1, source_target_pairs={{0,2},{1,3},{2,0},{3,1},{4,6},{5,7},{6,4},{7,5},{8,10},{9,11},{10,... | collective-permute-start | bytes 3080 | tf_op jit(solution)/shard_map/ppermute | solution.py:27
  88.5 4.7 %collective-permute-start.10 = (f32[256]{0:T(256)S(1)}, f32[256]{0:T(256)S(1)}, u32[]{:S(2)}, u32[]{:S(2)}) collective-permute-start(f32[256]{0:T(256)S(1)} %add.1120), channel_id=1, source_target_pairs={{0,4},{4,0},{8,12},{12,8},{1,5},{5,1},{9,13},{13,9},{2,6},{6,2},{1... | collective-permute-start | bytes 3080 | tf_op jit(solution)/shard_map/ppermute | solution.py:27
  93.2 4.9 %collective-permute-start.11 = (f32[256]{0:T(256)S(1)}, f32[256]{0:T(256)S(1)}, u32[]{:S(2)}, u32[]{:S(2)}) collective-permute-start(f32[256]{0:T(256)S(1)} %add.1121), channel_id=1, source_target_pairs={{0,8},{4,12},{8,0},{12,4},{1,9},{5,13},{9,1},{13,5},{2,10},{6,14},... | collective-permute-start | bytes 3080 | tf_op jit(solution)/shard_map/ppermute | solution.py:27
  104.4 11.2 %copy-start.1 = (f32[32,64,64]{2,1,0:T(8,128)S(1)}, f32[32,64,64]{2,1,0:T(8,128)}, u32[]{:S(2)}) copy-start(f32[32,64,64]{2,1,0:T(8,128)} %copy.84) | copy-start | bytes 1572868
  104.5 25.9 %collective-permute-start.12 = (f32[4,64,128]{1,2,0:T(8,128)S(1)}, f32[4,64,128]{1,2,0:T(8,128)S(1)}, u32[]{:S(2)}, u32[]{:S(2)}) collective-permute-start(f32[4,64,128]{1,2,0:T(8,128)S(1)} %bitcast.159), channel_id=1, source_target_pairs={{8,0},{12,4},{9,1},{13,5},{10,2},{14,6},{11,3},{15,7},{24,16},{28,... | collective-permute-start | bytes 393224 | tf_op jit(solution)/shard_map/ppermute | solution.py:16
  105.9 24.5 %collective-permute-start.13 = (f32[4,64,128]{1,2,0:T(8,128)S(1)}, f32[4,64,128]{1,2,0:T(8,128)}, u32[]{:S(2)}, u32[]{:S(2)}) collective-permute-start(f32[4,64,128]{1,2,0:T(8,128)S(1)} %bitcast.160), channel_id=1, source_target_pairs={{4,0},{8,4},{12,8},{5,1},{9,5},{13,9},{6,2},{10,6},{14,10},{7,3},{... | collective-permute-start | bytes 393224 | tf_op jit(solution)/shard_map/ppermute | solution.py:16
  108.4 22.0 %collective-permute-start.14 = (f32[4,64,128]{1,2,0:T(8,128)S(1)}, f32[4,64,128]{1,2,0:T(8,128)}, u32[]{:S(2)}, u32[]{:S(2)}) collective-permute-start(f32[4,64,128]{1,2,0:T(8,128)S(1)} %bitcast.161), channel_id=1, source_target_pairs={{0,4},{4,8},{8,12},{1,5},{5,9},{9,13},{2,6},{6,10},{10,14},{3,7},{... | collective-permute-start | bytes 393224 | tf_op jit(solution)/shard_map/ppermute | solution.py:16
  112.7 6.3 %copy-start.14 = (f32[32]{0:T(128)S(1)}, f32[32]{0:T(128)}, u32[]{:S(2)}) copy-start(f32[32]{0:T(128)} %get-tuple-element.7) | copy-start | bytes 388
  112.7 6.3 %copy-start.16 = (f32[32]{0:T(128)S(1)}, f32[32]{0:T(128)}, u32[]{:S(2)}) copy-start(f32[32]{0:T(128)} %get-tuple-element.81) | copy-start | bytes 388
  112.7 17.8 %collective-permute-start.15 = (f32[4,64,128]{1,2,0:T(8,128)S(1)}, f32[4,64,128]{1,2,0:T(8,128)}, u32[]{:S(2)}, u32[]{:S(2)}) collective-permute-start(f32[4,64,128]{1,2,0:T(8,128)S(1)} %bitcast.162), channel_id=1, source_target_pairs={{0,8},{4,12},{1,9},{5,13},{2,10},{6,14},{3,11},{7,15},{16,24},{20,... | collective-permute-start | bytes 393224 | tf_op jit(solution)/shard_map/ppermute | solution.py:16
  132.9 10.1 %collective-permute-start.16 = (f32[1,64,128]{2,1,0:T(8,128)S(1)}, f32[1,64,128]{2,1,0:T(8,128)S(1)}, u32[]{:S(2)}, u32[]{:S(2)}) collective-permute-start(f32[1,64,128]{2,1,0:T(8,128)S(1)} %get-tuple-element.25), channel_id=1, source_target_pairs={{4,0},{8,4},{12,8},{5,1},{9,5},{13,9},{6,2},{10,6},{14,10},{7,3},{... | collective-permute-start | bytes 98312 | tf_op jit(solution)/shard_map/ppermute | solution.py:44
  136.3 6.8 %collective-permute-start.17 = (f32[1,64,128]{2,1,0:T(8,128)S(1)}, f32[1,64,128]{2,1,0:T(8,128)S(1)}, u32[]{:S(2)}, u32[]{:S(2)}) collective-permute-start(f32[1,64,128]{2,1,0:T(8,128)S(1)} %get-tuple-element.26), channel_id=1, source_target_pairs={{0,4},{4,8},{8,12},{1,5},{5,9},{9,13},{2,6},{6,10},{10,14},{3,7},{... | collective-permute-start | bytes 98312 | tf_op jit(solution)/shard_map/ppermute | solution.py:42
  138.5 2.6 %collective-permute-start.18 = (f32[32,1,128]{2,1,0:T(1,128)S(1)}, f32[32,1,128]{2,1,0:T(1,128)S(1)}, u32[]{:S(2)}, u32[]{:S(2)}) collective-permute-start(f32[32,1,128]{2,1,0:T(1,128)S(1)} %get-tuple-element.27), channel_id=1, source_target_pairs={{1,0},{2,1},{3,2},{0,3},{5,4},{6,5},{7,6},{4,7},{9,8},{10,9},{11,1... | collective-permute-start | bytes 49160 | tf_op jit(solution)/shard_map/ppermute | solution.py:44
  138.6 4.4 %collective-permute-start.19 = (f32[32,1,128]{2,1,0:T(1,128)S(1)}, f32[32,1,128]{2,1,0:T(1,128)S(1)}, u32[]{:S(2)}, u32[]{:S(2)}) collective-permute-start(f32[32,1,128]{2,1,0:T(1,128)S(1)} %get-tuple-element.28), channel_id=1, source_target_pairs={{0,1},{1,2},{2,3},{3,0},{4,5},{5,6},{6,7},{7,4},{8,9},{9,10},{10,1... | collective-permute-start | bytes 49160 | tf_op jit(solution)/shard_map/ppermute | solution.py:42
  143.7 2.4 %collective-permute-start.20 = (f32[128]{0:T(128)S(1)}, f32[128]{0:T(128)S(1)}, u32[]{:S(2)}, u32[]{:S(2)}) collective-permute-start(f32[128]{0:T(128)S(1)} %multiply_reduce_fusion), channel_id=1, source_target_pairs={{0,1},{1,0},{2,3},{3,2},{4,5},{5,4},{6,7},{7,6},{8,9},{9,8},{10,11... | collective-permute-start | bytes 1544 | tf_op jit(solution)/shard_map/ppermute | solution.py:27
  146.2 3.3 %collective-permute-start.21 = (f32[128]{0:T(128)S(1)}, f32[128]{0:T(128)S(1)}, u32[]{:S(2)}, u32[]{:S(2)}) collective-permute-start(f32[128]{0:T(128)S(1)} %add.1152), channel_id=1, source_target_pairs={{0,2},{1,3},{2,0},{3,1},{4,6},{5,7},{6,4},{7,5},{8,10},{9,11},{10,... | collective-permute-start | bytes 1544 | tf_op jit(solution)/shard_map/ppermute | solution.py:27
  149.5 4.4 %collective-permute-start.22 = (f32[128]{0:T(128)S(1)}, f32[128]{0:T(128)S(1)}, u32[]{:S(2)}, u32[]{:S(2)}) collective-permute-start(f32[128]{0:T(128)S(1)} %add.1153), channel_id=1, source_target_pairs={{0,4},{4,0},{8,12},{12,8},{1,5},{5,1},{9,13},{13,9},{2,6},{6,2},{1... | collective-permute-start | bytes 1544 | tf_op jit(solution)/shard_map/ppermute | solution.py:27
  153.9 2.4 %collective-permute-start.23 = (f32[128]{0:T(128)S(1)}, f32[128]{0:T(128)S(1)}, u32[]{:S(2)}, u32[]{:S(2)}) collective-permute-start(f32[128]{0:T(128)S(1)} %add.1154), channel_id=1, source_target_pairs={{0,8},{4,12},{8,0},{12,4},{1,9},{5,13},{9,1},{13,5},{2,10},{6,14},... | collective-permute-start | bytes 1544 | tf_op jit(solution)/shard_map/ppermute | solution.py:27
  (12 other events, 37.0 us)

commit v2 on v1

v2 whole, which is shorter than its diff:
```python
import math

import jax
import jax.numpy as jnp
from jax import lax
from jax.sharding import PartitionSpec as P

LEV = 4
STEPS = 2
CAP = 4


def from_behind(block, axis, distance):
    devices = range(lax.axis_size(axis))
    route = [(i - distance, i) for i in devices if i - distance in devices]
    return lax.ppermute(block, axis, route)


def all_sum(value, axes):
    for axis in axes:
        count = lax.axis_size(axis)
        if count & (count - 1):
            value = lax.psum(value, axis)
            continue
        distance = 1
        while distance < count:
            value = value + lax.ppermute(
                value, axis, [(i, i ^ distance) for i in range(count)]
            )
            distance *= 2
    return value


def extended(cells, sides, width, closed):
    for axis, dim in sides:
        count = lax.axis_size(axis)
        ends = count if closed else count - 1
        head = lax.slice_in_dim(cells, 0, width, axis=dim)
        tail = lax.slice_in_dim(cells, cells.shape[dim] - width, cells.shape[dim], axis=dim)
        cells = jnp.concatenate(
            [
                lax.ppermute(tail, axis, [(i, (i + 1) % count) for i in range(ends)]),
                cells,
                lax.ppermute(head, axis, [((i + 1) % count, i) for i in range(ends)]),
            ],
            axis=dim,
        )
    return cells


def cubic_weights(fraction):
    first_term = -fraction * (fraction - 1.0) * (fraction - 2.0) / 6.0
    second_term = (fraction + 1.0) * (fraction - 1.0) * (fraction - 2.0) / 2.0
    third_term = -(fraction + 1.0) * fraction * (fraction - 2.0) / 2.0
    fourth_term = (fraction + 1.0) * fraction * (fraction - 1.0) / 6.0
    return (first_term, second_term, third_term, fourth_term)


def cubic_matrix(fraction, extent):
    places = jnp.arange(extent)
    running = jnp.zeros(fraction.shape + (extent, extent), jnp.float32)
    for offset, weight in zip(range(-1, 3), cubic_weights(fraction)):
        target_col = jnp.clip(places + offset, 0, extent - 1)
        indicator = (target_col[:, None] == places[None, :]).astype(jnp.float32)
        running = running + weight[..., None, None] * indicator
    return running


def spatial(patches, fraction_y, fraction_x):
    patch_count = patches.shape[0]
    weight_y = cubic_matrix(fraction_y, 8)
    weight_x = cubic_matrix(fraction_x, 8)
    plane_weights = jnp.einsum(
        "nac,nbd->nabcd", weight_y, weight_x, precision=lax.Precision.HIGHEST
    ).reshape(patch_count, 64, 64)
    return jnp.einsum("nij,njv->niv", plane_weights, patches, precision=lax.Precision.HIGHEST)


def levels(flat, fraction_z):
    patch_count, cols, value_count = flat.shape
    stacked = flat.reshape(patch_count, cols, LEV, value_count // LEV)
    weight_z = cubic_matrix(fraction_z, LEV)
    levelled = jnp.einsum("nlm,nimt->nilt", weight_z, stacked, precision=lax.Precision.HIGHEST)
    return levelled.reshape(patch_count, cols, value_count)


def to_patches(state_field):
    band_rows = state_field.shape[0] // 8
    band_cols = state_field.shape[1] // 8
    return (
        state_field.reshape(band_rows, 8, band_cols, 8, -1)
        .transpose(0, 2, 1, 3, 4)
        .reshape(band_rows * band_cols, 64, -1)
    )


def from_patches(patches, band_rows, band_cols):
    return (
        patches.reshape(band_rows, band_cols, 8, 8, -1)
        .transpose(0, 2, 1, 3, 4)
        .reshape(band_rows * 8, band_cols * 8, -1)
    )


def column_area(first_row, row_count, total_rows):
    latitude = ((first_row + jnp.arange(row_count)).astype(jnp.float32) + 0.5) * (
        math.pi / total_rows
    ) - 0.5 * math.pi
    return jnp.cos(latitude)


def column_mass(state_field, weights):
    return jnp.sum(weights[:, None, None] * state_field, axis=(0, 1))


def diffuse(advected, diffusivity, row_dim):
    col_dim = row_dim + 1
    rows = advected.shape[row_dim]
    cols = advected.shape[col_dim]
    lon_wide = extended(advected, (("lon", col_dim),), 1, True)
    lat_wide = extended(advected, (("lat", row_dim),), 1, False)
    laplace = (
        lax.slice_in_dim(lat_wide, 2, rows + 2, axis=row_dim)
        + lax.slice_in_dim(lat_wide, 0, rows, axis=row_dim)
        + lax.slice_in_dim(lon_wide, 2, cols + 2, axis=col_dim)
        + lax.slice_in_dim(lon_wide, 0, cols, axis=col_dim)
        - 4.0 * advected
    )
    k_shape = [1] * advected.ndim
    k_shape[row_dim] = rows
    return advected + diffusivity.reshape(k_shape) * laplace


def departed(state_field, source_ids, shifts_now):
    lat_count = lax.axis_size("lat")
    lat_index = lax.axis_index("lat")
    lon_index = lax.axis_index("lon")
    row_count, col_count, value_count = state_field.shape
    band_rows = row_count // 8
    band_cols = col_count // 8
    per_device = band_rows * band_cols
    total_cols = source_ids.shape[1]
    band_offsets = (-2, -1, 1, 2)
    devices = jnp.arange(lat_count)
    slot_range = jnp.arange(CAP)
    column_ids = lax.dynamic_slice_in_dim(
        source_ids, lon_index * band_cols, band_cols, 1
    ).reshape(lat_count, per_device)
    fractions = lax.dynamic_slice_in_dim(
        shifts_now, lon_index * band_cols, band_cols, 2
    ).reshape(3, lat_count, per_device)
    source_row = column_ids // total_cols
    source_dev = source_row // band_rows
    source_local = (
        source_row % band_rows * band_cols + column_ids % total_cols - lon_index * band_cols
    )
    remote = source_dev != devices[:, None]
    matches = (source_dev[:, :, None] == devices[None, None, :]) & remote[:, :, None]
    slot_ranks = jnp.cumsum(matches.astype(jnp.int32), axis=1) - 1
    slot_of = jnp.sum(jnp.where(matches, slot_ranks, 0), axis=2)
    owned_here = remote & (source_dev == lat_index)
    sending = owned_here[:, :, None] & (slot_of[:, :, None] == slot_range[None, None, :])
    send_local = jnp.sum(jnp.where(sending, source_local[:, :, None], 0), axis=1)
    near_local = jnp.stack(
        [
            lax.dynamic_index_in_dim(send_local, lat_index + offset, 0, keepdims=False)
            for offset in band_offsets
        ]
    )
    own_patches = to_patches(state_field)
    outgoing = own_patches[near_local.reshape(-1)].reshape(4, CAP, 64, value_count)
    my_dev = lax.dynamic_index_in_dim(source_dev, lat_index, 0, keepdims=False)
    my_slot = lax.dynamic_index_in_dim(slot_of, lat_index, 0, keepdims=False)
    my_local = lax.dynamic_index_in_dim(source_local, lat_index, 0, keepdims=False)
    my_remote = lax.dynamic_index_in_dim(remote, lat_index, 0, keepdims=False)
    my_frac = lax.dynamic_index_in_dim(fractions, lat_index, 1, keepdims=False)
    my_offset = lat_index - my_dev
    pick_index = jnp.where(my_offset < 0, my_offset + 2, my_offset + 1) * CAP + my_slot
    arrived = jnp.stack(
        [
            from_behind(outgoing[slot_place], "lat", offset)
            for slot_place, offset in enumerate(band_offsets)
        ]
    ).reshape(4 * CAP, 64, value_count)
    patches = jnp.where(my_remote[:, None, None], arrived[pick_index], own_patches[my_local])
    return patches, my_frac


def local(tracers, shifts, diffusivity, source_patch):
    lat_count = lax.axis_size("lat")
    lat_index = lax.axis_index("lat")
    row_count, col_count, value_count = tracers.shape
    band_rows = row_count // 8
    band_cols = col_count // 8
    per_device = band_rows * band_cols
    per_level = value_count // LEV
    total_rows = row_count * lat_count
    weights = column_area(lat_index * row_count, row_count, total_rows)
    target_part = column_mass(tracers, weights)

    patches, frac = departed(tracers, source_patch[0], shifts[0])
    advected = from_patches(levels(spatial(patches, frac[0], frac[1]), frac[2]), band_rows, band_cols)
    first = diffuse(advected, diffusivity, 0)
    first_part = column_mass(first, weights)

    patches, frac = departed(first, source_patch[1], shifts[1])
    planar = spatial(patches, frac[0], frac[1])
    weight_z = cubic_matrix(frac[2], LEV)

    k_wide = extended(diffusivity, (("lat", 0),), 1, False)
    area_wide = column_area(lat_index * row_count - 1, row_count + 2, total_rows)
    flux = area_wide * k_wide
    g = weights - 2.0 * flux[1:-1] + flux[:-2] + flux[2:]
    g_cols = jnp.broadcast_to(g.reshape(band_rows, 1, 8, 1), (band_rows, band_cols, 8, 8))
    weighted = jnp.einsum(
        "pi,piv->pv", g_cols.reshape(per_device, 64), planar, precision=lax.Precision.HIGHEST
    ).reshape(per_device, LEV, per_level)
    mix_part = jnp.einsum(
        "plm,pmt->lmt", weight_z, weighted, precision=lax.Precision.HIGHEST
    )
    totals = all_sum(
        jnp.concatenate([target_part, first_part, mix_part.reshape(-1)]), ("lon", "lat")
    )
    target = totals[:value_count]
    first_mass = totals[value_count : 2 * value_count]
    mix = totals[2 * value_count :].reshape(LEV, LEV, per_level)
    first_ratio = (target / first_mass).reshape(LEV, per_level)
    second_mass = jnp.sum(first_ratio[None] * mix, axis=1).reshape(value_count)
    second_ratio = target / second_mass

    parts = []
    for source_level in range(LEV):
        block = planar[:, :, source_level * per_level : (source_level + 1) * per_level]
        spread = jnp.concatenate(
            [weight_z[:, level, source_level][:, None, None] * block for level in range(LEV)],
            axis=2,
        )
        parts.append(from_patches(spread, band_rows, band_cols))
    spread_diffused = diffuse(jnp.stack(parts), diffusivity, 1)
    factor = jnp.tile(first_ratio, (1, LEV))
    combined = jnp.sum(factor[:, None, None, :] * spread_diffused, axis=0)
    return combined * second_ratio[None, None, :]


def solution(mesh):
    return jax.shard_map(
        local,
        mesh=mesh,
        in_specs=(
            P(("groups", "lat"), "lon", None),
            P("groups", None, None, None),
            P("lat"),
            P("groups", None, None),
        ),
        out_specs=P(("groups", "lat"), "lon", None),
        check_vma=False,
    )
```

time: 160 us -> 135 us (0.84)
  matrix products: 26.6 us -> 13 us
  waiting for transfers between devices: 22.7 us -> 10.5 us
  local copies, waits for them, and re-layouts: 39.6 us -> 31 us
  other arithmetic: 21 us -> 28.5 us
  starting transfers between devices: 46.9 us -> 49.6 us
    dot_general x8 -> x5, matrix products: 26.6 us -> 13 us  [the longest x2 7.52 us: spatial(): jnp.einsum('nij,njv->niv', plane_weights, patches, precision=lax.Precisio...]
    ppermute x8 -> x4, waiting for transfers between devices: 15.4 us -> 2.4 us  [all_sum(): lax.ppermute(value, axis, [(i, i ^ distance) for i in range(count)])]
    reshape x10 -> x16, local copies, waits for them, and re-layouts: 16.5 us -> 6.91 us  [the longest x2 4.27 us: spatial(): plane_weights = jnp.einsum('nac,nbd->nabcd', weight_y, weight_x, precisio...]
    ppermute x4 -> x5, starting transfers between devices: 5.95 us -> 13.5 us  [extended(): lax.ppermute(tail, axis, [(i, (i + 1) % count) for i in range(ends)])]
    reduce_sum x6, other arithmetic: 1.52 us -> 8.45 us  [the longest x1 7.11 us: local(): combined = jnp.sum(factor[:, None, None, :] * spread_diffused, axis=0)]
    transpose x2, local copies, waits for them, and re-layouts: 8 us -> 3.18 us  [the longest x1 3.17 us: levels(): jnp.einsum('nlm,nimt->nilt', weight_z, stacked, precision=lax.Precision.H...]
    concatenate x1 -> x5, other arithmetic: 0.01 us -> 3.52 us  [the longest x4 3.51 us: local(): jnp.concatenate([weight_z[:, level, source_level][:, None, None] * block...]
    mul x2 -> x5, other arithmetic: 1.91 us -> 4.81 us  [the longest x2 2.34 us: local(): weight_z[:, level, source_level][:, None, None] * block]
  transfers between devices with their start and end apart: 24 -> 22, of which waited for: 11 -> 6; matrix products, arithmetic and copies ran while one was open for 34% -> 22% of each run, Pallas kernels for 0% -> 0%
where the time goes in v2:
time: 135 us; the launch traced here: 134 us
  starting transfers between devices  49.6 us (37%)
  local copies, waits for them, and re-layouts  31 us (23%)
  other arithmetic  28.5 us (21%)
  matrix products  13 us (10%)
  waiting for transfers between devices  10.5 us (8%)
    ppermute x8, starting transfers between devices, from_behind(): return lax.ppermute(block, axis, route)  20 us
    ppermute x5, starting transfers between devices, extended(): lax.ppermute(tail, axis, [(i, (i + 1) % count) for i in range(ends)])  13.5 us
    ppermute x5, starting transfers between devices, extended(): lax.ppermute(head, axis, [((i + 1) % count, i) for i in range(ends)])  10.9 us
    dot_general x2, matrix products, spatial(): jnp.einsum('nij,njv->niv', plane_weights, patches, precision=lax.Precisio...  7.52 us
    reduce_sum x1, other arithmetic, local(): combined = jnp.sum(factor[:, None, None, :] * spread_diffused, axis=0)  7.11 us
    ppermute x4, starting transfers between devices, all_sum(): lax.ppermute(value, axis, [(i, i ^ distance) for i in range(count)])  5.16 us
    dot_general x1, matrix products, levels(): jnp.einsum('nlm,nimt->nilt', weight_z, stacked, precision=lax.Precision.H...  4.37 us
    reshape x2, local copies, waits for them, and re-layouts, spatial(): plane_weights = jnp.einsum('nac,nbd->nabcd', weight_y, weight_x, precisio...  4.27 us
  transfers between devices with their start and end apart: 22, of which 6 were waited for; matrix products, arithmetic and copies ran while one was open for 22% of the time, Pallas kernels for 0%

profile of v2, /device:TPU:1, one launch (start us, length us, event | category | flops | bytes accessed | tf_op | source)
XLA Modules:
  0.0 133.5 jit_solution(8172288454888364377)
XLA Ops:
  1.8 1.3 %copy.37 = f32[4,8,8,8,128]{4,3,2,1,0:T(8,128)S(1)} copy(f32[4,8,8,8,128]{4,3,1,2,0:T(8,128)} %bitcast.166) | data formatting | bytes 2097152 | tf_op jit(solution)/shard_map/transpose | solution.py:92
  4.5 2.0 %collective-permute-start.1 = (f32[4,64,128]{2,1,0:T(8,128)}, f32[4,64,128]{2,1,0:T(8,128)S(1)}, u32[]{:S(2)}, u32[]{:S(2)}) collective-permute-start(f32[4,64,128]{2,1,0:T(8,128)} %get-tuple-element.56), channel_id=1, source_target_pairs={{4,0},{8,4},{12,8},{5,1},{9,5},{13,9},{6,2},{10,6},{14,10},{7,3},{... | collective-permute-start | bytes 393224 | tf_op jit(solution)/shard_map/ppermute | solution.py:16
  6.5 4.5 %collective-permute-start.2 = (f32[4,64,128]{2,1,0:T(8,128)}, f32[4,64,128]{2,1,0:T(8,128)}, u32[]{:S(2)}, u32[]{:S(2)}) collective-permute-start(f32[4,64,128]{2,1,0:T(8,128)} %get-tuple-element.55), channel_id=1, source_target_pairs={{0,4},{4,8},{8,12},{1,5},{5,9},{9,13},{2,6},{6,10},{10,14},{3,7},{... | collective-permute-start | bytes 393224 | tf_op jit(solution)/shard_map/ppermute | solution.py:16
  11.0 2.1 %collective-permute-start.3 = (f32[4,64,128]{2,1,0:T(8,128)}, f32[4,64,128]{2,1,0:T(8,128)}, u32[]{:S(2)}, u32[]{:S(2)}) collective-permute-start(f32[4,64,128]{2,1,0:T(8,128)} %get-tuple-element.57), channel_id=1, source_target_pairs={{0,8},{4,12},{1,9},{5,13},{2,10},{6,14},{3,11},{7,15},{16,24},{20,... | collective-permute-start | bytes 393224 | tf_op jit(solution)/shard_map/ppermute | solution.py:16
  15.0 6.2 %collective-permute-start.8 = (f32[1]{0:T(128)}, f32[1]{0:T(128)}, u32[]{:S(2)}, u32[]{:S(2)}) collective-permute-start(f32[1]{0:T(128)} %get-tuple-element.102), channel_id=1, source_target_pairs={{0,4},{4,8},{8,12},{1,5},{5,9},{9,13},{2,6},{6,10},{10,14},{3,7},{... | collective-permute-start | bytes 20 | tf_op jit(solution)/shard_map/ppermute | solution.py:42
  26.5 1.6 %broadcast_multiply_fusion = f32[32,8,8,8,8]{0,2,4,1,3:T(8,128)} fusion(f32[32,8,8]{0,2,1:T(8,128)S(1)} %multiply_add_fusion, f32[32,8,8]{0,2,1:T(8,128)S(1)} %get-tuple-element.64), kind=kLoop, calls=%fused_computation.51 | loop fusion | flops 131072 | bytes 540672 | tf_op jit(solution)/shard_map/nac,nbd->nabcd/dot_general | solution.py:73
  28.1 1.7 %copy.38 = f32[32,64,64]{2,1,0:T(8,128)} copy(f32[32,64,64]{0,2,1:T(8,128)S(1)} %bitcast.149) | data formatting | bytes 1048576 | tf_op jit(solution)/shard_map/reshape | solution.py:75
  29.8 1.6 %gather_fusion.2 = f32[32,64,128]{2,1,0:T(8,128)} fusion(f32[32,64,128]{2,1,0:T(8,128)S(1)} %bitcast.153, s32[1024]{0:T(1024)S(1)} %pad_clamp_fusion.3), kind=kCustom, calls=%fused_computation.2 | custom fusion | bytes 2097280 | tf_op jit(solution)/shard_map/gather | solution.py:185
  31.5 2.5 %copy.45 = f32[32,64,64]{2,1,0:T(8,128)S(1)} copy(f32[32,64,64]{0,2,1:T(8,128)} %bitcast.150) | data formatting | bytes 1048576 | tf_op jit(solution)/shard_map/reshape | solution.py:75
  34.1 1.9 %collective-permute-start.9 = (f32[1]{0:T(128)}, f32[1]{0:T(128)}, u32[]{:S(2)}, u32[]{:S(2)}) collective-permute-start(f32[1]{0:T(128)} %get-tuple-element.103), channel_id=1, source_target_pairs={{4,0},{8,4},{12,8},{5,1},{9,5},{13,9},{6,2},{10,6},{14,10},{7,3},{... | collective-permute-start | bytes 20 | tf_op jit(solution)/shard_map/ppermute | solution.py:44
  36.0 3.2 %collective-permute-done.9 = f32[1]{0:T(128)} collective-permute-done((f32[1]{0:T(128)}, f32[1]{0:T(128)}, u32[]{:S(2)}, u32[]{:S(2)}) %collective-permute-start.9) | collective-permute-done | bytes 36 | tf_op jit(solution)/shard_map/ppermute | solution.py:44
  41.7 1.6 %gather_fusion.1 = f32[32,64,128]{2,1,0:T(8,128)} fusion(f32[16,64,128]{2,1,0:T(8,128)S(1)} %bitcast.156, s32[1024]{0:T(1024)S(1)} %pad_clamp_fusion.4), kind=kCustom, calls=%fused_computation.1 | custom fusion | bytes 2097280 | tf_op jit(solution)/shard_map/gather | solution.py:185
  43.3 5.1 %fusion.21 = f32[32,64,128]{1,2,0:T(8,128)S(1)} fusion(f32[32,64,64]{2,1,0:T(8,128)S(1)} %copy-done.1, f32[32,64,128]{2,1,0:T(8,128)} %gather_fusion.1, f32[32,64,128]{2,1,0:T(8,128)} %gather_fusion.2, pred[32]{0:T(512)(128)(4,1)S(1)} %copy-done.25), kind=kOutput, calls=%fused_computation.53 | convolution fusion | flops 201588736 | bytes 3670048 | tf_op jit(solution)/shard_map/nij,njv->niv/dot_general | solution.py:76
  48.4 4.4 %fusion.10 = f32[32,64,4,32]{1,2,3,0:T(4,128)S(1)} fusion(f32[32,4,4,1]{2,1,3,0:T(4,128)S(1)} %copy.54, f32[32,64,4,32]{1,3,2,0:T(8,128)S(1)} %bitcast.151), kind=kOutput, calls=%fused_computation.33 | convolution fusion | flops 12582912 | bytes 2099200 | tf_op jit(solution)/shard_map/nlm,nimt->nilt/dot_general | solution.py:83
  52.8 3.2 %copy.42 = f32[32,64,4,32]{3,2,1,0:T(4,128)} copy(f32[32,64,4,32]{1,2,3,0:T(4,128)S(1)} %fusion.10) | data formatting | bytes 2097152 | tf_op jit(solution)/shard_map/nlm,nimt->nilt/transpose | solution.py:83
  55.9 3.7 %reshape_reshape.3 = f32[4,8,8,8,128]{4,3,2,1,0:T(8,128)S(1)} reshape(f32[32,64,4,32]{3,2,1,0:T(4,128)} %copy.42) | data formatting | bytes 2097152 | tf_op jit(solution)/shard_map/reshape;reshape | solution.py:99
  59.8 1.9 %collective-permute-start.4 = (f32[1,64,128]{2,1,0:T(8,128)S(1)}, f32[1,64,128]{2,1,0:T(8,128)S(1)}, u32[]{:S(2)}, u32[]{:S(2)}) collective-permute-start(f32[1,64,128]{2,1,0:T(8,128)S(1)} %get-tuple-element.46), channel_id=1, source_target_pairs={{4,0},{8,4},{12,8},{5,1},{9,5},{13,9},{6,2},{10,6},{14,10},{7,3},{... | collective-permute-start | bytes 98312 | tf_op jit(solution)/shard_map/ppermute | solution.py:44
  61.8 3.6 %collective-permute-start.5 = (f32[1,64,128]{2,1,0:T(8,128)S(1)}, f32[1,64,128]{2,1,0:T(8,128)S(1)}, u32[]{:S(2)}, u32[]{:S(2)}) collective-permute-start(f32[1,64,128]{2,1,0:T(8,128)S(1)} %get-tuple-element.47), channel_id=1, source_target_pairs={{0,4},{4,8},{8,12},{1,5},{5,9},{9,13},{2,6},{6,10},{10,14},{3,7},{... | collective-permute-start | bytes 98312 | tf_op jit(solution)/shard_map/ppermute | solution.py:42
  65.4 3.4 %collective-permute-start.6 = (f32[32,1,128]{2,1,0:T(1,128)S(1)}, f32[32,1,128]{2,1,0:T(1,128)S(1)}, u32[]{:S(2)}, u32[]{:S(2)}) collective-permute-start(f32[32,1,128]{2,1,0:T(1,128)S(1)} %get-tuple-element.48), channel_id=1, source_target_pairs={{1,0},{2,1},{3,2},{0,3},{5,4},{6,5},{7,6},{4,7},{9,8},{10,9},{11,1... | collective-permute-start | bytes 49160 | tf_op jit(solution)/shard_map/ppermute | solution.py:44
  69.6 3.5 %collective-permute-done.7 = f32[32,1,128]{2,1,0:T(1,128)S(1)} collective-permute-done((f32[32,1,128]{2,1,0:T(1,128)S(1)}, f32[32,1,128]{2,1,0:T(1,128)S(1)}, u32[]{:S(2)}, u32[]{:S(2)}) %collective-permute-start.7) | collective-permute-done | bytes 16416 | tf_op jit(solution)/shard_map/ppermute | solution.py:42
  73.2 2.5 %multiply_reduce_fusion.1 = (f32[128]{0:T(128)}, f32[128]{0:T(128)}, f32[32,64,128]{2,1,0:T(8,128)S(1)}) fusion(f32[32,64,128]{2,1,0:T(8,128)} %param.4, f32[32]{0:T(128)S(1)} %add_cosine_fusion, f32[32,64,128]{2,1,0:T(8,128)S(1)} %bitcast.160, f32[32,1,128]{2,1,0:T(1,128)S(1)} %collective-permute-done.7, f32[32,1,128]{2,1,0:T(1,128)S(1)} %collective-permute-done.6, ...), kind=kLoop, calls=%fused_computation.56 | loop fusion | flops 3931904 | bytes 3245312 | tf_op jit(solution)/shard_map/reduce_sum | solution.py:113
  78.4 2.1 %collective-permute-start.11 = (f32[4,64,128]{2,1,0:T(8,128)}, f32[4,64,128]{2,1,0:T(8,128)}, u32[]{:S(2)}, u32[]{:S(2)}) collective-permute-start(f32[4,64,128]{2,1,0:T(8,128)} %get-tuple-element.52), channel_id=1, source_target_pairs={{4,0},{8,4},{12,8},{5,1},{9,5},{13,9},{6,2},{10,6},{14,10},{7,3},{... | collective-permute-start | bytes 393224 | tf_op jit(solution)/shard_map/ppermute | solution.py:16
  80.5 4.2 %collective-permute-start.12 = (f32[4,64,128]{2,1,0:T(8,128)S(1)}, f32[4,64,128]{2,1,0:T(8,128)}, u32[]{:S(2)}, u32[]{:S(2)}) collective-permute-start(f32[4,64,128]{2,1,0:T(8,128)S(1)} %get-tuple-element.51), channel_id=1, source_target_pairs={{0,4},{4,8},{8,12},{1,5},{5,9},{9,13},{2,6},{6,10},{10,14},{3,7},{... | collective-permute-start | bytes 393224 | tf_op jit(solution)/shard_map/ppermute | solution.py:16
  84.7 2.7 %collective-permute-start.13 = (f32[4,64,128]{2,1,0:T(8,128)S(1)}, f32[4,64,128]{2,1,0:T(8,128)}, u32[]{:S(2)}, u32[]{:S(2)}) collective-permute-start(f32[4,64,128]{2,1,0:T(8,128)S(1)} %get-tuple-element.53), channel_id=1, source_target_pairs={{0,8},{4,12},{1,9},{5,13},{2,10},{6,14},{3,11},{7,15},{16,24},{20,... | collective-permute-start | bytes 393224 | tf_op jit(solution)/shard_map/ppermute | solution.py:16
  90.2 1.7 %gather_fusion.4 = f32[32,64,128]{2,1,0:T(8,128)} fusion(f32[16,64,128]{2,1,0:T(8,128)S(1)} %bitcast.157, s32[1024]{0:T(1024)} %pad_clamp_fusion.1), kind=kCustom, calls=%fused_computation.4 | custom fusion | bytes 2097280 | tf_op jit(solution)/shard_map/gather | solution.py:185
  91.9 2.4 %fusion.19 = f32[32,64,128]{2,1,0:T(8,128)S(1)} fusion(f32[32,64,64]{2,1,0:T(8,128)S(1)} %copy.45, f32[32,64,128]{2,1,0:T(8,128)} %gather_fusion.4, f32[32,64,128]{2,1,0:T(8,128)S(1)} %gather_fusion.5, pred[32]{0:T(512)(128)(4,1)} %fusion.52), kind=kOutput, calls=%fused_computation.49 | convolution fusion | flops 201588736 | bytes 3670048 | tf_op jit(solution)/shard_map/nij,njv->niv/dot_general | solution.py:76
  103.6 2.3 %collective-permute-done.15 = f32[768]{0:T(1024)S(1)} collective-permute-done((f32[768]{0:T(1024)S(1)}, f32[768]{0:T(1024)S(1)}, u32[]{:S(2)}, u32[]{:S(2)}) %collective-permute-start.15) | collective-permute-done | bytes 3104 | tf_op jit(solution)/shard_map/ppermute | solution.py:27
  105.9 2.7 %collective-permute-start.16 = (f32[768]{0:T(1024)S(1)}, f32[768]{0:T(1024)S(1)}, u32[]{:S(2)}, u32[]{:S(2)}) collective-permute-start(f32[768]{0:T(1024)S(1)} %add.828), channel_id=1, source_target_pairs={{0,4},{4,0},{8,12},{12,8},{1,5},{5,1},{9,13},{13,9},{2,6},{6,2},{1... | collective-permute-start | bytes 9224 | tf_op jit(solution)/shard_map/ppermute | solution.py:27
  109.5 2.3 %collective-permute-start.17 = (f32[768]{0:T(1024)S(1)}, f32[768]{0:T(1024)S(1)}, u32[]{:S(2)}, u32[]{:S(2)}) collective-permute-start(f32[768]{0:T(1024)S(1)} %add.829), channel_id=1, source_target_pairs={{0,8},{4,12},{8,0},{12,4},{1,9},{5,13},{9,1},{13,5},{2,10},{6,14},... | collective-permute-start | bytes 9224 | tf_op jit(solution)/shard_map/ppermute | solution.py:27
  112.4 2.5 %collective-permute-start.18 = (f32[4,1,64,128]{3,2,1,0:T(8,128)}, f32[4,1,64,128]{3,2,1,0:T(8,128)S(1)}, u32[]{:S(2)}, u32[]{:S(2)}) collective-permute-start(f32[4,1,64,128]{3,2,1,0:T(8,128)} %get-tuple-element.26), channel_id=1, source_target_pairs={{4,0},{8,4},{12,8},{5,1},{9,5},{13,9},{6,2},{10,6},{14,10},{7,3},{... | collective-permute-start | bytes 393224 | tf_op jit(solution)/shard_map/ppermute | solution.py:44
  115.0 3.0 %collective-permute-start.19 = (f32[4,1,64,128]{3,2,1,0:T(8,128)S(1)}, f32[4,1,64,128]{3,2,1,0:T(8,128)S(1)}, u32[]{:S(2)}, u32[]{:S(2)}) collective-permute-start(f32[4,1,64,128]{3,2,1,0:T(8,128)S(1)} %get-tuple-element.27), channel_id=1, source_target_pairs={{0,4},{4,8},{8,12},{1,5},{5,9},{9,13},{2,6},{6,10},{10,14},{3,7},{... | collective-permute-start | bytes 393224 | tf_op jit(solution)/shard_map/ppermute | solution.py:42
  125.3 7.1 %fusion.5 = f32[32,64,128]{2,1,0:T(8,128)S(1)} fusion(f32[4,32,1,128]{3,2,1,0:T(1,128)} %collective-permute-done.21, f32[1,32,64,128]{3,2,1,0:T(8,128)} %bitcast.148, f32[1,32,64,128]{3,2,1,0:T(8,128)S(1)} %bitcast.146, f32[1,32,64,128]{3,2,1,0:T(8,128)S(1)} %bitcast.144, f32[1,32,64,128]{3,2,1,0:T(8,128)S(1)} %bitcast.142, ...), kind=kLoop, calls=%fused_computation.12 | loop fusion | flops 29097984 | bytes 5638272 | tf_op jit(solution)/shard_map/reduce_sum | solution.py:241
  (197 shorter events, 37.9 us)
Async XLA Ops:
  0.0 14.3 %copy-start.4 = (f32[32]{0:T(128)S(1)}, f32[32]{0:T(128)}, u32[]{:S(2)}) copy-start(f32[32]{0:T(128)} %param.6) | copy-start | bytes 388
  0.0 21.8 %copy-start.3 = (f32[2,3,16,32]{3,2,1,0:T(8,128)S(1)}, f32[2,3,16,32]{3,2,1,0:T(8,128)}, u32[]{:S(2)}) copy-start(f32[2,3,16,32]{3,2,1,0:T(8,128)} %param.5) | copy-start | bytes 36868
  4.5 36.1 %collective-permute-start.1 = (f32[4,64,128]{2,1,0:T(8,128)}, f32[4,64,128]{2,1,0:T(8,128)S(1)}, u32[]{:S(2)}, u32[]{:S(2)}) collective-permute-start(f32[4,64,128]{2,1,0:T(8,128)} %get-tuple-element.56), channel_id=1, source_target_pairs={{4,0},{8,4},{12,8},{5,1},{9,5},{13,9},{6,2},{10,6},{14,10},{7,3},{... | collective-permute-start | bytes 393224 | tf_op jit(solution)/shard_map/ppermute | solution.py:16
  6.5 34.1 %collective-permute-start.2 = (f32[4,64,128]{2,1,0:T(8,128)}, f32[4,64,128]{2,1,0:T(8,128)}, u32[]{:S(2)}, u32[]{:S(2)}) collective-permute-start(f32[4,64,128]{2,1,0:T(8,128)} %get-tuple-element.55), channel_id=1, source_target_pairs={{0,4},{4,8},{8,12},{1,5},{5,9},{9,13},{2,6},{6,10},{10,14},{3,7},{... | collective-permute-start | bytes 393224 | tf_op jit(solution)/shard_map/ppermute | solution.py:16
  11.0 29.6 %collective-permute-start.3 = (f32[4,64,128]{2,1,0:T(8,128)}, f32[4,64,128]{2,1,0:T(8,128)}, u32[]{:S(2)}, u32[]{:S(2)}) collective-permute-start(f32[4,64,128]{2,1,0:T(8,128)} %get-tuple-element.57), channel_id=1, source_target_pairs={{0,8},{4,12},{1,9},{5,13},{2,10},{6,14},{3,11},{7,15},{16,24},{20,... | collective-permute-start | bytes 393224 | tf_op jit(solution)/shard_map/ppermute | solution.py:16
  13.0 27.6 %collective-permute-start = (f32[4,64,128]{2,1,0:T(8,128)S(1)}, f32[4,64,128]{2,1,0:T(8,128)}, u32[]{:S(2)}, u32[]{:S(2)}) collective-permute-start(f32[4,64,128]{2,1,0:T(8,128)S(1)} %get-tuple-element.54), channel_id=1, source_target_pairs={{8,0},{12,4},{9,1},{13,5},{10,2},{14,6},{11,3},{15,7},{24,16},{28,... | collective-permute-start | bytes 393224 | tf_op jit(solution)/shard_map/ppermute | solution.py:16
  15.0 19.1 %collective-permute-start.8 = (f32[1]{0:T(128)}, f32[1]{0:T(128)}, u32[]{:S(2)}, u32[]{:S(2)}) collective-permute-start(f32[1]{0:T(128)} %get-tuple-element.102), channel_id=1, source_target_pairs={{0,4},{4,8},{8,12},{1,5},{5,9},{9,13},{2,6},{6,10},{10,14},{3,7},{... | collective-permute-start | bytes 20 | tf_op jit(solution)/shard_map/ppermute | solution.py:42
  29.8 13.5 %copy-start.1 = (f32[32,64,64]{2,1,0:T(8,128)S(1)}, f32[32,64,64]{2,1,0:T(8,128)}, u32[]{:S(2)}) copy-start(f32[32,64,64]{2,1,0:T(8,128)} %copy.38) | copy-start | bytes 1572868
  29.8 13.5 %copy-start.25 = (pred[32]{0:T(512)(128)(4,1)S(1)}, pred[32]{0:T(512)(128)(4,1)}, u32[]{:S(2)}) copy-start(pred[32]{0:T(512)(128)(4,1)} %fusion.51) | copy-start | bytes 100
  34.1 5.2 %collective-permute-start.9 = (f32[1]{0:T(128)}, f32[1]{0:T(128)}, u32[]{:S(2)}, u32[]{:S(2)}) collective-permute-start(f32[1]{0:T(128)} %get-tuple-element.103), channel_id=1, source_target_pairs={{4,0},{8,4},{12,8},{5,1},{9,5},{13,9},{6,2},{10,6},{14,10},{7,3},{... | collective-permute-start | bytes 20 | tf_op jit(solution)/shard_map/ppermute | solution.py:44
  59.8 13.3 %collective-permute-start.4 = (f32[1,64,128]{2,1,0:T(8,128)S(1)}, f32[1,64,128]{2,1,0:T(8,128)S(1)}, u32[]{:S(2)}, u32[]{:S(2)}) collective-permute-start(f32[1,64,128]{2,1,0:T(8,128)S(1)} %get-tuple-element.46), channel_id=1, source_target_pairs={{4,0},{8,4},{12,8},{5,1},{9,5},{13,9},{6,2},{10,6},{14,10},{7,3},{... | collective-permute-start | bytes 98312 | tf_op jit(solution)/shard_map/ppermute | solution.py:44
  61.8 11.4 %collective-permute-start.5 = (f32[1,64,128]{2,1,0:T(8,128)S(1)}, f32[1,64,128]{2,1,0:T(8,128)S(1)}, u32[]{:S(2)}, u32[]{:S(2)}) collective-permute-start(f32[1,64,128]{2,1,0:T(8,128)S(1)} %get-tuple-element.47), channel_id=1, source_target_pairs={{0,4},{4,8},{8,12},{1,5},{5,9},{9,13},{2,6},{6,10},{10,14},{3,7},{... | collective-permute-start | bytes 98312 | tf_op jit(solution)/shard_map/ppermute | solution.py:42
  65.4 4.2 %collective-permute-start.6 = (f32[32,1,128]{2,1,0:T(1,128)S(1)}, f32[32,1,128]{2,1,0:T(1,128)S(1)}, u32[]{:S(2)}, u32[]{:S(2)}) collective-permute-start(f32[32,1,128]{2,1,0:T(1,128)S(1)} %get-tuple-element.48), channel_id=1, source_target_pairs={{1,0},{2,1},{3,2},{0,3},{5,4},{6,5},{7,6},{4,7},{9,8},{10,9},{11,1... | collective-permute-start | bytes 49160 | tf_op jit(solution)/shard_map/ppermute | solution.py:44
  68.8 4.4 %collective-permute-start.7 = (f32[32,1,128]{2,1,0:T(1,128)S(1)}, f32[32,1,128]{2,1,0:T(1,128)S(1)}, u32[]{:S(2)}, u32[]{:S(2)}) collective-permute-start(f32[32,1,128]{2,1,0:T(1,128)S(1)} %get-tuple-element.49), channel_id=1, source_target_pairs={{0,1},{1,2},{2,3},{3,0},{4,5},{5,6},{6,7},{7,4},{8,9},{9,10},{10,1... | collective-permute-start | bytes 49160 | tf_op jit(solution)/shard_map/ppermute | solution.py:42
  77.1 11.8 %collective-permute-start.10 = (f32[4,64,128]{2,1,0:T(8,128)}, f32[4,64,128]{2,1,0:T(8,128)S(1)}, u32[]{:S(2)}, u32[]{:S(2)}) collective-permute-start(f32[4,64,128]{2,1,0:T(8,128)} %get-tuple-element.50), channel_id=1, source_target_pairs={{8,0},{12,4},{9,1},{13,5},{10,2},{14,6},{11,3},{15,7},{24,16},{28,... | collective-permute-start | bytes 393224 | tf_op jit(solution)/shard_map/ppermute | solution.py:16
  78.4 10.6 %collective-permute-start.11 = (f32[4,64,128]{2,1,0:T(8,128)}, f32[4,64,128]{2,1,0:T(8,128)}, u32[]{:S(2)}, u32[]{:S(2)}) collective-permute-start(f32[4,64,128]{2,1,0:T(8,128)} %get-tuple-element.52), channel_id=1, source_target_pairs={{4,0},{8,4},{12,8},{5,1},{9,5},{13,9},{6,2},{10,6},{14,10},{7,3},{... | collective-permute-start | bytes 393224 | tf_op jit(solution)/shard_map/ppermute | solution.py:16
  80.5 8.5 %collective-permute-start.12 = (f32[4,64,128]{2,1,0:T(8,128)S(1)}, f32[4,64,128]{2,1,0:T(8,128)}, u32[]{:S(2)}, u32[]{:S(2)}) collective-permute-start(f32[4,64,128]{2,1,0:T(8,128)S(1)} %get-tuple-element.51), channel_id=1, source_target_pairs={{0,4},{4,8},{8,12},{1,5},{5,9},{9,13},{2,6},{6,10},{10,14},{3,7},{... | collective-permute-start | bytes 393224 | tf_op jit(solution)/shard_map/ppermute | solution.py:16
  84.7 4.3 %collective-permute-start.13 = (f32[4,64,128]{2,1,0:T(8,128)S(1)}, f32[4,64,128]{2,1,0:T(8,128)}, u32[]{:S(2)}, u32[]{:S(2)}) collective-permute-start(f32[4,64,128]{2,1,0:T(8,128)S(1)} %get-tuple-element.53), channel_id=1, source_target_pairs={{0,8},{4,12},{1,9},{5,13},{2,10},{6,14},{3,11},{7,15},{16,24},{20,... | collective-permute-start | bytes 393224 | tf_op jit(solution)/shard_map/ppermute | solution.py:16
  89.0 6.8 %copy-start.15 = (f32[32]{0:T(128)S(1)}, f32[32]{0:T(128)}, u32[]{:S(2)}) copy-start(f32[32]{0:T(128)} %get-tuple-element.65) | copy-start | bytes 388
  89.1 6.8 %copy-start.16 = (f32[32]{0:T(128)S(1)}, f32[32]{0:T(128)}, u32[]{:S(2)}) copy-start(f32[32]{0:T(128)} %get-tuple-element.71) | copy-start | bytes 388
  89.1 6.8 %copy-start.17 = (f32[32]{0:T(128)S(1)}, f32[32]{0:T(128)}, u32[]{:S(2)}) copy-start(f32[32]{0:T(128)} %get-tuple-element.72) | copy-start | bytes 388
  89.1 6.8 %copy-start.18 = (f32[32]{0:T(128)S(1)}, f32[32]{0:T(128)}, u32[]{:S(2)}) copy-start(f32[32]{0:T(128)} %get-tuple-element.74) | copy-start | bytes 388
  89.1 6.8 %copy-start.19 = (f32[32]{0:T(128)S(1)}, f32[32]{0:T(128)}, u32[]{:S(2)}) copy-start(f32[32]{0:T(128)} %get-tuple-element.75) | copy-start | bytes 388
  95.7 6.7 %collective-permute-start.14 = (f32[768]{0:T(1024)S(1)}, f32[768]{0:T(1024)S(1)}, u32[]{:S(2)}, u32[]{:S(2)}) collective-permute-start(f32[768]{0:T(1024)S(1)} %pad_maximum_fusion.27), channel_id=1, source_target_pairs={{0,1},{1,0},{2,3},{3,2},{4,5},{5,4},{6,7},{7,6},{8,9},{9,8},{10,11... | collective-permute-start | bytes 9224 | tf_op jit(solution)/shard_map/ppermute | solution.py:27
  102.5 3.4 %collective-permute-start.15 = (f32[768]{0:T(1024)S(1)}, f32[768]{0:T(1024)S(1)}, u32[]{:S(2)}, u32[]{:S(2)}) collective-permute-start(f32[768]{0:T(1024)S(1)} %fusion.73), channel_id=1, source_target_pairs={{0,2},{1,3},{2,0},{3,1},{4,6},{5,7},{6,4},{7,5},{8,10},{9,11},{10,... | collective-permute-start | bytes 9224 | tf_op jit(solution)/shard_map/ppermute | solution.py:27
  105.9 3.6 %collective-permute-start.16 = (f32[768]{0:T(1024)S(1)}, f32[768]{0:T(1024)S(1)}, u32[]{:S(2)}, u32[]{:S(2)}) collective-permute-start(f32[768]{0:T(1024)S(1)} %add.828), channel_id=1, source_target_pairs={{0,4},{4,0},{8,12},{12,8},{1,5},{5,1},{9,13},{13,9},{2,6},{6,2},{1... | collective-permute-start | bytes 9224 | tf_op jit(solution)/shard_map/ppermute | solution.py:27
  109.5 10.3 %collective-permute-start.17 = (f32[768]{0:T(1024)S(1)}, f32[768]{0:T(1024)S(1)}, u32[]{:S(2)}, u32[]{:S(2)}) collective-permute-start(f32[768]{0:T(1024)S(1)} %add.829), channel_id=1, source_target_pairs={{0,8},{4,12},{8,0},{12,4},{1,9},{5,13},{9,1},{13,5},{2,10},{6,14},... | collective-permute-start | bytes 9224 | tf_op jit(solution)/shard_map/ppermute | solution.py:27
  112.4 12.9 %collective-permute-start.18 = (f32[4,1,64,128]{3,2,1,0:T(8,128)}, f32[4,1,64,128]{3,2,1,0:T(8,128)S(1)}, u32[]{:S(2)}, u32[]{:S(2)}) collective-permute-start(f32[4,1,64,128]{3,2,1,0:T(8,128)} %get-tuple-element.26), channel_id=1, source_target_pairs={{4,0},{8,4},{12,8},{5,1},{9,5},{13,9},{6,2},{10,6},{14,10},{7,3},{... | collective-permute-start | bytes 393224 | tf_op jit(solution)/shard_map/ppermute | solution.py:44
  115.0 10.4 %collective-permute-start.19 = (f32[4,1,64,128]{3,2,1,0:T(8,128)S(1)}, f32[4,1,64,128]{3,2,1,0:T(8,128)S(1)}, u32[]{:S(2)}, u32[]{:S(2)}) collective-permute-start(f32[4,1,64,128]{3,2,1,0:T(8,128)S(1)} %get-tuple-element.27), channel_id=1, source_target_pairs={{0,4},{4,8},{8,12},{1,5},{5,9},{9,13},{2,6},{6,10},{10,14},{3,7},{... | collective-permute-start | bytes 393224 | tf_op jit(solution)/shard_map/ppermute | solution.py:42
  118.0 6.6 %collective-permute-start.20 = (f32[4,32,1,128]{3,2,1,0:T(1,128)}, f32[4,32,1,128]{3,2,1,0:T(1,128)}, u32[]{:S(2)}, u32[]{:S(2)}) collective-permute-start(f32[4,32,1,128]{3,2,1,0:T(1,128)} %get-tuple-element.28), channel_id=1, source_target_pairs={{1,0},{2,1},{3,2},{0,3},{5,4},{6,5},{7,6},{4,7},{9,8},{10,9},{11,1... | collective-permute-start | bytes 196616 | tf_op jit(solution)/shard_map/ppermute | solution.py:44
  119.2 6.1 %collective-permute-start.21 = (f32[4,32,1,128]{3,2,1,0:T(1,128)}, f32[4,32,1,128]{3,2,1,0:T(1,128)}, u32[]{:S(2)}, u32[]{:S(2)}) collective-permute-start(f32[4,32,1,128]{3,2,1,0:T(1,128)} %get-tuple-element.29), channel_id=1, source_target_pairs={{0,1},{1,2},{2,3},{3,0},{4,5},{5,6},{6,7},{7,4},{8,9},{9,10},{10,1... | collective-permute-start | bytes 196616 | tf_op jit(solution)/shard_map/ppermute | solution.py:42
  124.6 7.8 %copy-start.24 = (f32[128]{0:T(128)S(1)}, f32[128]{0:T(128)}, u32[]{:S(2)}) copy-start(f32[128]{0:T(128)} %slice_divide_fusion.1) | copy-start | bytes 1540
  (16 other events, 54.3 us)

commit v3 on v2

--- a/solution.py
+++ b/solution.py
@@ -66,22 +66,46 @@
     return running
 
 
+def tap_sources(target, extent):
+    return sorted({min(max(target + offset, 0), extent - 1) for offset in range(-1, 3)})
+
+
+def plane_weights(fraction_y, fraction_x):
+    rows = lax.broadcasted_iota(jnp.int32, (1, 64, 64), 1)
+    cols = lax.broadcasted_iota(jnp.int32, (1, 64, 64), 2)
+
+    def along(fraction, source, target):
+        running = jnp.zeros((fraction.shape[0], 64, 64), jnp.float32)
+        for offset, weight in zip(range(-1, 3), cubic_weights(fraction)):
+            indicator = (jnp.clip(source + offset, 0, 7) == target).astype(jnp.float32)
+            running = running + weight[:, None, None] * indicator
+        return running
+
+    return along(fraction_y, rows // 8, cols // 8) * along(fraction_x, rows % 8, cols % 8)
+
+
 def spatial(patches, fraction_y, fraction_x):
-    patch_count = patches.shape[0]
-    weight_y = cubic_matrix(fraction_y, 8)
-    weight_x = cubic_matrix(fraction_x, 8)
-    plane_weights = jnp.einsum(
-        "nac,nbd->nabcd", weight_y, weight_x, precision=lax.Precision.HIGHEST
-    ).reshape(patch_count, 64, 64)
-    return jnp.einsum("nij,njv->niv", plane_weights, patches, precision=lax.Precision.HIGHEST)
+    return jnp.einsum(
+        "nij,njv->niv",
+        plane_weights(fraction_y, fraction_x),
+        patches,
+        precision=lax.Precision.HIGHEST,
+    )
 
 
 def levels(flat, fraction_z):
-    patch_count, cols, value_count = flat.shape
-    stacked = flat.reshape(patch_count, cols, LEV, value_count // LEV)
+    value_count = flat.shape[2]
+    per_level = value_count // LEV
     weight_z = cubic_matrix(fraction_z, LEV)
-    levelled = jnp.einsum("nlm,nimt->nilt", weight_z, stacked, precision=lax.Precision.HIGHEST)
-    return levelled.reshape(patch_count, cols, value_count)
+    blocks = [flat[:, :, m * per_level : (m + 1) * per_level] for m in range(LEV)]
+    out = []
+    for level in range(LEV):
+        acc = None
+        for m in tap_sources(level, LEV):
+            term = weight_z[:, level, m][:, None, None] * blocks[m]
+            acc = term if acc is None else acc + term
+        out.append(acc)
+    return jnp.concatenate(out, axis=2)
 
 
 def to_patches(state_field):
@@ -129,6 +153,32 @@
     k_shape = [1] * advected.ndim
     k_shape[row_dim] = rows
     return advected + diffusivity.reshape(k_shape) * laplace
+
+
+def diffuse_first(advected, diffusivity):
+    rows, cols, value_count = advected.shape
+    count = lax.axis_size("lat")
+
+    def pack(row, number):
+        return jnp.concatenate(
+            [row, jnp.broadcast_to(number, (1, 1, value_count))], axis=1
+        )
+
+    from_above = lax.ppermute(
+        pack(advected[rows - 1 :], diffusivity[rows - 1]),
+        "lat",
+        [(i, i + 1) for i in range(count - 1)],
+    )
+    from_below = lax.ppermute(
+        pack(advected[:1], diffusivity[0]), "lat", [(i + 1, i) for i in range(count - 1)]
+    )
+    lat_wide = jnp.concatenate([from_above[:, :cols], advected, from_below[:, :cols]], axis=0)
+    k_wide = jnp.concatenate([from_above[0, cols, :1], diffusivity, from_below[0, cols, :1]])
+    lon_wide = extended(advected, (("lon", 1),), 1, True)
+    laplace = (
+        lat_wide[2:] + lat_wide[:-2] + lon_wide[:, 2:] + lon_wide[:, :-2] - 4.0 * advected
+    )
+    return advected + diffusivity[:, None, None] * laplace, k_wide
 
 
 def departed(state_field, source_ids, shifts_now):
@@ -200,14 +250,13 @@
 
     patches, frac = departed(tracers, source_patch[0], shifts[0])
     advected = from_patches(levels(spatial(patches, frac[0], frac[1]), frac[2]), band_rows, band_cols)
-    first = diffuse(advected, diffusivity, 0)
+    first, k_wide = diffuse_first(advected, diffusivity)
     first_part = column_mass(first, weights)
 
     patches, frac = departed(first, source_patch[1], shifts[1])
     planar = spatial(patches, frac[0], frac[1])
     weight_z = cubic_matrix(frac[2], LEV)
 
-    k_wide = extended(diffusivity, (("lat", 0),), 1, False)
     area_wide = column_area(lat_index * row_count - 1, row_count + 2, total_rows)
     flux = area_wide * k_wide
     g = weights - 2.0 * flux[1:-1] + flux[:-2] + flux[2:]
@@ -221,13 +270,6 @@
     totals = all_sum(
         jnp.concatenate([target_part, first_part, mix_part.reshape(-1)]), ("lon", "lat")
     )
-    target = totals[:value_count]
-    first_mass = totals[value_count : 2 * value_count]
-    mix = totals[2 * value_count :].reshape(LEV, LEV, per_level)
-    first_ratio = (target / first_mass).reshape(LEV, per_level)
-    second_mass = jnp.sum(first_ratio[None] * mix, axis=1).reshape(value_count)
-    second_ratio = target / second_mass
-
     parts = []
     for source_level in range(LEV):
         block = planar[:, :, source_level * per_level : (source_level + 1) * per_level]
@@ -237,6 +279,14 @@
         )
         parts.append(from_patches(spread, band_rows, band_cols))
     spread_diffused = diffuse(jnp.stack(parts), diffusivity, 1)
+    spread_diffused, totals = lax.optimization_barrier((spread_diffused, totals))
+    target = totals[:value_count]
+    first_mass = totals[value_count : 2 * value_count]
+    mix = totals[2 * value_count :].reshape(LEV, LEV, per_level)
+    first_ratio = (target / first_mass).reshape(LEV, per_level)
+    second_mass = jnp.sum(first_ratio[None] * mix, axis=1).reshape(value_count)
+    second_ratio = target / second_mass
+
     factor = jnp.tile(first_ratio, (1, LEV))
     combined = jnp.sum(factor[:, None, None, :] * spread_diffused, axis=0)
     return combined * second_ratio[None, None, :]

time: 135 us -> 97.2 us (0.72)
  the two profiles are of different devices: /device:TPU:1 before, /device:TPU:0 now
where the time goes in v3:
time: 97.2 us; the launch traced here: 96.7 us
  starting transfers between devices  38.1 us (39%)
  other arithmetic  26.8 us (28%)
  local copies, waits for them, and re-layouts  13.1 us (13%)
  waiting for transfers between devices  11.6 us (12%)
  matrix products  6.28 us (6%)
    ppermute x8, starting transfers between devices, from_behind(): return lax.ppermute(block, axis, route)  20.8 us
    ppermute x4, waiting for transfers between devices, all_sum(): lax.ppermute(value, axis, [(i, i ^ distance) for i in range(count)])  7.32 us
    ppermute x3, starting transfers between devices, extended(): lax.ppermute(head, axis, [((i + 1) % count, i) for i in range(ends)])  7.21 us
    dot_general x2, matrix products, spatial(): jnp.einsum('nij,njv->niv', plane_weights(fraction_y, fraction_x), patches...  5.14 us
    add x1, other arithmetic, diffuse(): return advected + diffusivity.reshape(k_shape) * laplace  5.03 us
    ppermute x3, starting transfers between devices, extended(): lax.ppermute(tail, axis, [(i, (i + 1) % count) for i in range(ends)])  4.05 us
    concatenate x4, other arithmetic, local(): jnp.concatenate([weight_z[:, level, source_level][:, None, None] * block...  3.52 us
    ppermute x4, starting transfers between devices, all_sum(): lax.ppermute(value, axis, [(i, i ^ distance) for i in range(count)])  3.41 us
  transfers between devices with their start and end apart: 20, of which 5 were waited for; matrix products, arithmetic and copies ran while one was open for 20% of the time, Pallas kernels for 0%

profile of v3, /device:TPU:0, one launch (start us, length us, event | category | flops | bytes accessed | tf_op | source)
XLA Modules:
  0.0 96.7 jit_solution(9376997485575921000)
XLA Ops:
  1.8 1.3 %copy.25 = f32[4,8,8,8,128]{4,3,2,1,0:T(8,128)S(1)} copy(f32[4,8,8,8,128]{4,3,1,2,0:T(8,128)} %bitcast.179) | data formatting | bytes 2097152 | tf_op jit(solution)/shard_map/transpose | solution.py:116
  3.8 1.3 %collective-permute-start = (f32[4,64,128]{2,1,0:T(8,128)S(1)}, f32[4,64,128]{2,1,0:T(8,128)S(1)}, u32[]{:S(2)}, u32[]{:S(2)}) collective-permute-start(f32[4,64,128]{2,1,0:T(8,128)S(1)} %get-tuple-element.61), channel_id=1, source_target_pairs={{8,0},{12,4},{9,1},{13,5},{10,2},{14,6},{11,3},{15,7},{24,16},{28,... | collective-permute-start | bytes 393224 | tf_op jit(solution)/shard_map/ppermute | solution.py:16
  5.1 1.3 %collective-permute-start.1 = (f32[4,64,128]{2,1,0:T(8,128)S(1)}, f32[4,64,128]{2,1,0:T(8,128)S(1)}, u32[]{:S(2)}, u32[]{:S(2)}) collective-permute-start(f32[4,64,128]{2,1,0:T(8,128)S(1)} %get-tuple-element.63), channel_id=1, source_target_pairs={{4,0},{8,4},{12,8},{5,1},{9,5},{13,9},{6,2},{10,6},{14,10},{7,3},{... | collective-permute-start | bytes 393224 | tf_op jit(solution)/shard_map/ppermute | solution.py:16
  6.4 3.0 %collective-permute-start.2 = (f32[4,64,128]{2,1,0:T(8,128)S(1)}, f32[4,64,128]{2,1,0:T(8,128)S(1)}, u32[]{:S(2)}, u32[]{:S(2)}) collective-permute-start(f32[4,64,128]{2,1,0:T(8,128)S(1)} %get-tuple-element.62), channel_id=1, source_target_pairs={{0,4},{4,8},{8,12},{1,5},{5,9},{9,13},{2,6},{6,10},{10,14},{3,7},{... | collective-permute-start | bytes 393224 | tf_op jit(solution)/shard_map/ppermute | solution.py:16
  9.4 4.9 %collective-permute-start.3 = (f32[4,64,128]{2,1,0:T(8,128)S(1)}, f32[4,64,128]{2,1,0:T(8,128)S(1)}, u32[]{:S(2)}, u32[]{:S(2)}) collective-permute-start(f32[4,64,128]{2,1,0:T(8,128)S(1)} %get-tuple-element.64), channel_id=1, source_target_pairs={{0,8},{4,12},{1,9},{5,13},{2,10},{6,14},{3,11},{7,15},{16,24},{20,... | collective-permute-start | bytes 393224 | tf_op jit(solution)/shard_map/ppermute | solution.py:16
  23.8 2.6 %fusion.14 = f32[32,64,128]{2,1,0:T(8,128)S(1)} fusion(f32[32,64,128]{2,1,0:T(8,128)S(1)} %gather_fusion.1, f32[32,64,128]{2,1,0:T(8,128)S(1)} %gather_fusion.2, f32[32]{0:T(128)} %get-tuple-element.144, f32[32]{0:T(128)} %get-tuple-element.145, f32[32]{0:T(128)} %get-tuple-element.143, f32[32]{0:T(128)} %get-tuple-element.105, f32[32]{0:T(128)} %get-tuple-element.141, ...), kind=kOutput, calls=%fused_computation.54 | convolution fusion | flops 203554816 | bytes 3277856 | tf_op jit(solution)/shard_map/nij,njv->niv/dot_general | solution.py:88
  26.5 1.1 %multiply_add_fusion.2 = f32[32,64,32]{2,1,0:T(8,128)S(1)} fusion(f32[32,64,128]{2,1,0:T(8,128)S(1)} %fusion.14, f32[32]{0:T(128)S(1)} %get-tuple-element.93, f32[32]{0:T(128)S(1)} %copy-done.3, f32[32]{0:T(128)S(1)} %copy-done.4, f32[32]{0:T(128)S(1)} %copy-done.5), kind=kLoop, calls=%fused_computation.52 | loop fusion | flops 458752 | bytes 1311232 | tf_op jit(solution)/shard_map/add | solution.py:106
  27.6 1.3 %multiply_add_fusion.3 = (f32[32,64,32]{2,1,0:T(8,128)S(1)}, f32[32,64,32]{2,1,0:T(8,128)S(1)}, f32[32,64,32]{2,1,0:T(8,128)S(1)}) fusion(f32[32,64,128]{2,1,0:T(8,128)S(1)} %fusion.14, f32[32]{0:T(128)S(1)} %get-tuple-element.97, f32[32]{0:T(128)S(1)} %get-tuple-element.98, f32[32]{0:T(128)S(1)} %get-tuple-element.87, f32[32]{0:T(128)S(1)} %get-tuple-element.90, ...), kind=kLoop, calls=%fused_computation.53 | loop fusion | flops 851968 | bytes 1836032 | tf_op jit(solution)/shard_map/add | solution.py:106
  30.7 1.3 %collective-permute-start.5 = (f32[1,65,128]{2,1,0:T(8,128)S(1)}, f32[1,65,128]{2,1,0:T(8,128)S(1)}, u32[]{:S(2)}, u32[]{:S(2)}) collective-permute-start(f32[1,65,128]{2,1,0:T(8,128)S(1)} %concatenate.58), channel_id=1, source_target_pairs={{0,4},{4,8},{8,12},{1,5},{5,9},{9,13},{2,6},{6,10},{10,14},{3,7},{... | collective-permute-start | bytes 99848 | tf_op jit(solution)/shard_map/ppermute | solution.py:167
  32.5 1.3 %collective-permute-start.4 = (f32[1,65,128]{2,1,0:T(8,128)S(1)}, f32[1,65,128]{2,1,0:T(8,128)S(1)}, u32[]{:S(2)}, u32[]{:S(2)}) collective-permute-start(f32[1,65,128]{2,1,0:T(8,128)S(1)} %concatenate.56), channel_id=1, source_target_pairs={{4,0},{8,4},{12,8},{5,1},{9,5},{13,9},{6,2},{10,6},{14,10},{7,3},{... | collective-permute-start | bytes 99848 | tf_op jit(solution)/shard_map/ppermute | solution.py:172
  33.9 4.8 %collective-permute-start.6 = (f32[32,1,128]{2,1,0:T(1,128)S(1)}, f32[32,1,128]{2,1,0:T(1,128)S(1)}, u32[]{:S(2)}, u32[]{:S(2)}) collective-permute-start(f32[32,1,128]{2,1,0:T(1,128)S(1)} %get-tuple-element.52), channel_id=1, source_target_pairs={{1,0},{2,1},{3,2},{0,3},{5,4},{6,5},{7,6},{4,7},{9,8},{10,9},{11,1... | collective-permute-start | bytes 49160 | tf_op jit(solution)/shard_map/ppermute | solution.py:44
  39.8 1.3 %maximum_multiply_fusion = f32[34]{0:T(128)S(1)} fusion(f32[1]{0:T(128)} %bitcast.80, f32[32]{0:T(128)S(1)} %copy-done.2, f32[1]{0:T(128)} %bitcast.79, s32[]{:T(128)S(6)} %sub.214), kind=kLoop, calls=%fused_computation.337 | loop fusion | flops 272 | bytes 276 | tf_op jit(solution)/shard_map/mul | solution.py:261
  41.5 2.8 %collective-permute-done.7 = f32[32,1,128]{2,1,0:T(1,128)S(1)} collective-permute-done((f32[32,1,128]{2,1,0:T(1,128)S(1)}, f32[32,1,128]{2,1,0:T(1,128)S(1)}, u32[]{:S(2)}, u32[]{:S(2)}) %collective-permute-start.7) | collective-permute-done | bytes 16416 | tf_op jit(solution)/shard_map/ppermute | solution.py:42
  45.8 1.3 %collective-permute-start.8 = (f32[4,64,128]{2,1,0:T(8,128)S(1)}, f32[4,64,128]{2,1,0:T(8,128)S(1)}, u32[]{:S(2)}, u32[]{:S(2)}) collective-permute-start(f32[4,64,128]{2,1,0:T(8,128)S(1)} %get-tuple-element.57), channel_id=1, source_target_pairs={{8,0},{12,4},{9,1},{13,5},{10,2},{14,6},{11,3},{15,7},{24,16},{28,... | collective-permute-start | bytes 393224 | tf_op jit(solution)/shard_map/ppermute | solution.py:16
  47.1 1.3 %collective-permute-start.9 = (f32[4,64,128]{2,1,0:T(8,128)S(1)}, f32[4,64,128]{2,1,0:T(8,128)S(1)}, u32[]{:S(2)}, u32[]{:S(2)}) collective-permute-start(f32[4,64,128]{2,1,0:T(8,128)S(1)} %get-tuple-element.59), channel_id=1, source_target_pairs={{4,0},{8,4},{12,8},{5,1},{9,5},{13,9},{6,2},{10,6},{14,10},{7,3},{... | collective-permute-start | bytes 393224 | tf_op jit(solution)/shard_map/ppermute | solution.py:16
  48.4 3.0 %collective-permute-start.10 = (f32[4,64,128]{2,1,0:T(8,128)S(1)}, f32[4,64,128]{2,1,0:T(8,128)S(1)}, u32[]{:S(2)}, u32[]{:S(2)}) collective-permute-start(f32[4,64,128]{2,1,0:T(8,128)S(1)} %get-tuple-element.58), channel_id=1, source_target_pairs={{0,4},{4,8},{8,12},{1,5},{5,9},{9,13},{2,6},{6,10},{10,14},{3,7},{... | collective-permute-start | bytes 393224 | tf_op jit(solution)/shard_map/ppermute | solution.py:16
  51.5 4.7 %collective-permute-start.11 = (f32[4,64,128]{2,1,0:T(8,128)S(1)}, f32[4,64,128]{2,1,0:T(8,128)S(1)}, u32[]{:S(2)}, u32[]{:S(2)}) collective-permute-start(f32[4,64,128]{2,1,0:T(8,128)S(1)} %get-tuple-element.60), channel_id=1, source_target_pairs={{0,8},{4,12},{1,9},{5,13},{2,10},{6,14},{3,11},{7,15},{16,24},{20,... | collective-permute-start | bytes 393224 | tf_op jit(solution)/shard_map/ppermute | solution.py:16
  57.1 1.4 %collective-permute-done.11 = f32[4,64,128]{2,1,0:T(8,128)S(1)} collective-permute-done((f32[4,64,128]{2,1,0:T(8,128)S(1)}, f32[4,64,128]{2,1,0:T(8,128)S(1)}, u32[]{:S(2)}, u32[]{:S(2)}) %collective-permute-start.11) | collective-permute-done | bytes 131104 | tf_op jit(solution)/shard_map/ppermute | solution.py:16
  59.2 2.6 %fusion.12 = f32[32,64,128]{2,1,0:T(8,128)S(1)} fusion(f32[32,64,128]{2,1,0:T(8,128)S(1)} %gather_fusion.4, f32[32,64,128]{2,1,0:T(8,128)S(1)} %gather_fusion.5, f32[64,64]{1,0:T(8,128)S(1)} %get-tuple-element.120, f32[32]{0:T(128)} %get-tuple-element.133, f32[64,64]{1,0:T(8,128)S(1)} %get-tuple-element.121, f32[32]{0:T(128)} %get-tuple-element.134, ...), kind=kOutput, calls=%fused_computation.48 | convolution fusion | flops 203554816 | bytes 3277856 | tf_op jit(solution)/shard_map/nij,njv->niv/dot_general | solution.py:88
  63.2 1.1 %slice_multiply_fusion.15 = (f32[32,64,32]{2,1,0:T(8,128)S(1)}, f32[32,64,32]{2,1,0:T(8,128)S(1)}, f32[32,64,32]{2,1,0:T(8,128)S(1)}, f32[32,64,32]{2,1,0:T(8,12...) fusion(f32[32,64,128]{2,1,0:T(8,128)S(1)} %fusion.12, ...), kind=kLoop, calls=%fused_computation.101 | loop fusion | flops 589824 | bytes 3146880 | tf_op jit(solution)/shard_map/mul | solution.py:277
  65.4 1.2 %slice_multiply_fusion.11 = (f32[32,64,32]{2,1,0:T(8,128)S(1)}, f32[32,64,32]{2,1,0:T(8,128)S(1)}, f32[32,64,32]{2,1,0:T(8,128)S(1)}, f32[32,64,32]{2,1,0:T(8,12...) fusion(f32[32,64,128]{2,1,0:T(8,128)S(1)} %fusion.12, ...), kind=kLoop, calls=%fused_computation.97 | loop fusion | flops 458752 | bytes 2622336 | tf_op jit(solution)/shard_map/mul | solution.py:277
  70.2 1.3 %collective-permute-start.12 = (f32[4,1,64,128]{3,2,1,0:T(8,128)S(1)}, f32[4,1,64,128]{3,2,1,0:T(8,128)S(1)}, u32[]{:S(2)}, u32[]{:S(2)}) collective-permute-start(f32[4,1,64,128]{3,2,1,0:T(8,128)S(1)} %get-tuple-element.30), channel_id=1, source_target_pairs={{4,0},{8,4},{12,8},{5,1},{9,5},{13,9},{6,2},{10,6},{14,10},{7,3},{... | collective-permute-start | bytes 393224 | tf_op jit(solution)/shard_map/ppermute | solution.py:44
  71.5 3.0 %collective-permute-start.13 = (f32[4,1,64,128]{3,2,1,0:T(8,128)S(1)}, f32[4,1,64,128]{3,2,1,0:T(8,128)S(1)}, u32[]{:S(2)}, u32[]{:S(2)}) collective-permute-start(f32[4,1,64,128]{3,2,1,0:T(8,128)S(1)} %get-tuple-element.31), channel_id=1, source_target_pairs={{0,4},{4,8},{8,12},{1,5},{5,9},{9,13},{2,6},{6,10},{10,14},{3,7},{... | collective-permute-start | bytes 393224 | tf_op jit(solution)/shard_map/ppermute | solution.py:42
  74.5 1.1 %collective-permute-start.14 = (f32[4,32,1,128]{3,2,1,0:T(1,128)S(1)}, f32[4,32,1,128]{3,2,1,0:T(1,128)S(1)}, u32[]{:S(2)}, u32[]{:S(2)}) collective-permute-start(f32[4,32,1,128]{3,2,1,0:T(1,128)S(1)} %get-tuple-element.32), channel_id=1, source_target_pairs={{1,0},{2,1},{3,2},{0,3},{5,4},{6,5},{7,6},{4,7},{9,8},{10,9},{11,1... | collective-permute-start | bytes 196616 | tf_op jit(solution)/shard_map/ppermute | solution.py:44
  75.6 1.0 %collective-permute-start.15 = (f32[4,32,1,128]{3,2,1,0:T(1,128)S(1)}, f32[4,32,1,128]{3,2,1,0:T(1,128)S(1)}, u32[]{:S(2)}, u32[]{:S(2)}) collective-permute-start(f32[4,32,1,128]{3,2,1,0:T(1,128)S(1)} %get-tuple-element.33), channel_id=1, source_target_pairs={{0,1},{1,2},{2,3},{3,0},{4,5},{5,6},{6,7},{7,4},{8,9},{9,10},{10,1... | collective-permute-start | bytes 196616 | tf_op jit(solution)/shard_map/ppermute | solution.py:42
  76.6 1.6 %collective-permute-start.17 = (f32[768]{0:T(1024)S(1)}, f32[768]{0:T(1024)S(1)}, u32[]{:S(2)}, u32[]{:S(2)}) collective-permute-start(f32[768]{0:T(1024)S(1)} %fusion.138), channel_id=1, source_target_pairs={{0,2},{1,3},{2,0},{3,1},{4,6},{5,7},{6,4},{7,5},{8,10},{9,11},{10,... | collective-permute-start | bytes 9224 | tf_op jit(solution)/shard_map/ppermute | solution.py:27
  78.3 4.3 %collective-permute-done.17 = f32[768]{0:T(1024)S(1)} collective-permute-done((f32[768]{0:T(1024)S(1)}, f32[768]{0:T(1024)S(1)}, u32[]{:S(2)}, u32[]{:S(2)}) %collective-permute-start.17) | collective-permute-done | bytes 3104 | tf_op jit(solution)/shard_map/ppermute | solution.py:27
  83.7 1.5 %collective-permute-start.19 = (f32[768]{0:T(1024)S(1)}, f32[768]{0:T(1024)S(1)}, u32[]{:S(2)}, u32[]{:S(2)}) collective-permute-start(f32[768]{0:T(1024)S(1)} %add.920), channel_id=1, source_target_pairs={{0,8},{4,12},{8,0},{12,4},{1,9},{5,13},{9,1},{13,5},{2,10},{6,14},... | collective-permute-start | bytes 9224 | tf_op jit(solution)/shard_map/ppermute | solution.py:27
  85.2 2.1 %collective-permute-done.19 = f32[768]{0:T(1024)S(1)} collective-permute-done((f32[768]{0:T(1024)S(1)}, f32[768]{0:T(1024)S(1)}, u32[]{:S(2)}, u32[]{:S(2)}) %collective-permute-start.19) | collective-permute-done | bytes 3104 | tf_op jit(solution)/shard_map/ppermute | solution.py:27
  87.3 5.0 %fusion.3 = f32[4,32,64,128]{3,2,1,0:T(8,128)} fusion(f32[4,32,1,128]{3,2,1,0:T(1,128)S(1)} %collective-permute-done.15, f32[1,32,64,128]{3,2,1,0:T(8,128)S(1)} %bitcast.164, f32[1,32,64,128]{3,2,1,0:T(8,128)S(1)} %bitcast.162, f32[1,32,64,128]{3,2,1,0:T(8,128)S(1)} %bitcast.160, f32[1,32,64,128]{3,2,1,0:T(8,128)S(1)} %bitcast.158, ...), kind=kLoop, calls=%fused_computation.10 | loop fusion | flops 27262976 | bytes 8781952 | tf_op jit(solution)/shard_map/add | solution.py:155
  92.8 2.9 %multiply_reduce_fusion = f32[32,64,128]{2,1,0:T(8,128)S(1)} fusion(f32[4,32,64,128]{3,2,1,0:T(8,128)} %fusion.3, f32[4,128]{1,0:T(4,128)S(1)} %tile.8), kind=kLoop, calls=%fused_computation.29 | loop fusion | flops 1835008 | bytes 5244928 | tf_op jit(solution)/shard_map/reduce_sum | solution.py:291
  95.6 1.1 %broadcast_multiply_fusion = f32[32,64,128]{2,1,0:T(8,128)} fusion(f32[32,64,128]{2,1,0:T(8,128)S(1)} %multiply_reduce_fusion, f32[128]{0:T(128)S(1)} %slice_divide_fusion.1), kind=kLoop, calls=%fused_computation.104 | loop fusion | flops 262144 | bytes 2097664 | tf_op jit(solution)/shard_map/mul | solution.py:292
  (167 shorter events, 25.9 us)
Async XLA Ops:
  0.0 15.0 %copy-start.1 = (f32[2,3,16,32]{3,2,1,0:T(8,128)S(1)}, f32[2,3,16,32]{3,2,1,0:T(8,128)}, u32[]{:S(2)}) copy-start(f32[2,3,16,32]{3,2,1,0:T(8,128)} %param.5) | copy-start | bytes 36868
  0.0 22.4 %copy-start.2 = (f32[32]{0:T(128)S(1)}, f32[32]{0:T(128)}, u32[]{:S(2)}) copy-start(f32[32]{0:T(128)} %param.6) | copy-start | bytes 388
  3.8 19.3 %collective-permute-start = (f32[4,64,128]{2,1,0:T(8,128)S(1)}, f32[4,64,128]{2,1,0:T(8,128)S(1)}, u32[]{:S(2)}, u32[]{:S(2)}) collective-permute-start(f32[4,64,128]{2,1,0:T(8,128)S(1)} %get-tuple-element.61), channel_id=1, source_target_pairs={{8,0},{12,4},{9,1},{13,5},{10,2},{14,6},{11,3},{15,7},{24,16},{28,... | collective-permute-start | bytes 393224 | tf_op jit(solution)/shard_map/ppermute | solution.py:16
  5.1 18.0 %collective-permute-start.1 = (f32[4,64,128]{2,1,0:T(8,128)S(1)}, f32[4,64,128]{2,1,0:T(8,128)S(1)}, u32[]{:S(2)}, u32[]{:S(2)}) collective-permute-start(f32[4,64,128]{2,1,0:T(8,128)S(1)} %get-tuple-element.63), channel_id=1, source_target_pairs={{4,0},{8,4},{12,8},{5,1},{9,5},{13,9},{6,2},{10,6},{14,10},{7,3},{... | collective-permute-start | bytes 393224 | tf_op jit(solution)/shard_map/ppermute | solution.py:16
  6.4 16.7 %collective-permute-start.2 = (f32[4,64,128]{2,1,0:T(8,128)S(1)}, f32[4,64,128]{2,1,0:T(8,128)S(1)}, u32[]{:S(2)}, u32[]{:S(2)}) collective-permute-start(f32[4,64,128]{2,1,0:T(8,128)S(1)} %get-tuple-element.62), channel_id=1, source_target_pairs={{0,4},{4,8},{8,12},{1,5},{5,9},{9,13},{2,6},{6,10},{10,14},{3,7},{... | collective-permute-start | bytes 393224 | tf_op jit(solution)/shard_map/ppermute | solution.py:16
  9.4 13.7 %collective-permute-start.3 = (f32[4,64,128]{2,1,0:T(8,128)S(1)}, f32[4,64,128]{2,1,0:T(8,128)S(1)}, u32[]{:S(2)}, u32[]{:S(2)}) collective-permute-start(f32[4,64,128]{2,1,0:T(8,128)S(1)} %get-tuple-element.64), channel_id=1, source_target_pairs={{0,8},{4,12},{1,9},{5,13},{2,10},{6,14},{3,11},{7,15},{16,24},{20,... | collective-permute-start | bytes 393224 | tf_op jit(solution)/shard_map/ppermute | solution.py:16
  22.4 4.0 %copy-start.3 = (f32[32]{0:T(128)S(1)}, f32[32]{0:T(128)}, u32[]{:S(2)}) copy-start(f32[32]{0:T(128)} %get-tuple-element.94) | copy-start | bytes 388
  22.4 4.0 %copy-start.4 = (f32[32]{0:T(128)S(1)}, f32[32]{0:T(128)}, u32[]{:S(2)}) copy-start(f32[32]{0:T(128)} %get-tuple-element.95) | copy-start | bytes 388
  22.5 4.0 %copy-start.5 = (f32[32]{0:T(128)S(1)}, f32[32]{0:T(128)}, u32[]{:S(2)}) copy-start(f32[32]{0:T(128)} %get-tuple-element.96) | copy-start | bytes 388
  28.9 15.3 %copy-start = (f32[32,64,128]{2,1,0:T(8,128)S(1)}, f32[32,64,128]{2,1,0:T(8,128)}, u32[]{:S(2)}) copy-start(f32[32,64,128]{2,1,0:T(8,128)} %param.4) | copy-start | bytes 3145732
  28.9 15.3 %copy-start.12 = (f32[32]{0:T(128)S(1)}, f32[32]{0:T(128)}, u32[]{:S(2)}) copy-start(f32[32]{0:T(128)} %add_cosine_fusion) | copy-start | bytes 388
  30.7 8.0 %collective-permute-start.5 = (f32[1,65,128]{2,1,0:T(8,128)S(1)}, f32[1,65,128]{2,1,0:T(8,128)S(1)}, u32[]{:S(2)}, u32[]{:S(2)}) collective-permute-start(f32[1,65,128]{2,1,0:T(8,128)S(1)} %concatenate.58), channel_id=1, source_target_pairs={{0,4},{4,8},{8,12},{1,5},{5,9},{9,13},{2,6},{6,10},{10,14},{3,7},{... | collective-permute-start | bytes 99848 | tf_op jit(solution)/shard_map/ppermute | solution.py:167
  32.5 6.7 %collective-permute-start.4 = (f32[1,65,128]{2,1,0:T(8,128)S(1)}, f32[1,65,128]{2,1,0:T(8,128)S(1)}, u32[]{:S(2)}, u32[]{:S(2)}) collective-permute-start(f32[1,65,128]{2,1,0:T(8,128)S(1)} %concatenate.56), channel_id=1, source_target_pairs={{4,0},{8,4},{12,8},{5,1},{9,5},{13,9},{6,2},{10,6},{14,10},{7,3},{... | collective-permute-start | bytes 99848 | tf_op jit(solution)/shard_map/ppermute | solution.py:172
  33.9 7.6 %collective-permute-start.6 = (f32[32,1,128]{2,1,0:T(1,128)S(1)}, f32[32,1,128]{2,1,0:T(1,128)S(1)}, u32[]{:S(2)}, u32[]{:S(2)}) collective-permute-start(f32[32,1,128]{2,1,0:T(1,128)S(1)} %get-tuple-element.52), channel_id=1, source_target_pairs={{1,0},{2,1},{3,2},{0,3},{5,4},{6,5},{7,6},{4,7},{9,8},{10,9},{11,1... | collective-permute-start | bytes 49160 | tf_op jit(solution)/shard_map/ppermute | solution.py:44
  38.7 5.6 %collective-permute-start.7 = (f32[32,1,128]{2,1,0:T(1,128)S(1)}, f32[32,1,128]{2,1,0:T(1,128)S(1)}, u32[]{:S(2)}, u32[]{:S(2)}) collective-permute-start(f32[32,1,128]{2,1,0:T(1,128)S(1)} %get-tuple-element.53), channel_id=1, source_target_pairs={{0,1},{1,2},{2,3},{3,0},{4,5},{5,6},{6,7},{7,4},{8,9},{9,10},{10,1... | collective-permute-start | bytes 49160 | tf_op jit(solution)/shard_map/ppermute | solution.py:42
  45.1 14.1 %copy-start.6 = (f32[32]{0:T(128)S(1)}, f32[32]{0:T(128)}, u32[]{:S(2)}) copy-start(f32[32]{0:T(128)} %get-tuple-element.99) | copy-start | bytes 388
  45.1 14.1 %copy-start.7 = (f32[32]{0:T(128)S(1)}, f32[32]{0:T(128)}, u32[]{:S(2)}) copy-start(f32[32]{0:T(128)} %get-tuple-element.101) | copy-start | bytes 388
  45.1 14.1 %copy-start.9 = (f32[32]{0:T(128)S(1)}, f32[32]{0:T(128)}, u32[]{:S(2)}) copy-start(f32[32]{0:T(128)} %get-tuple-element.129) | copy-start | bytes 388
  45.2 14.1 %copy-start.10 = (f32[32]{0:T(128)S(1)}, f32[32]{0:T(128)}, u32[]{:S(2)}) copy-start(f32[32]{0:T(128)} %get-tuple-element.130) | copy-start | bytes 388
  45.2 14.1 %copy-start.11 = (f32[32]{0:T(128)S(1)}, f32[32]{0:T(128)}, u32[]{:S(2)}) copy-start(f32[32]{0:T(128)} %get-tuple-element.131) | copy-start | bytes 388
  45.8 11.3 %collective-permute-start.8 = (f32[4,64,128]{2,1,0:T(8,128)S(1)}, f32[4,64,128]{2,1,0:T(8,128)S(1)}, u32[]{:S(2)}, u32[]{:S(2)}) collective-permute-start(f32[4,64,128]{2,1,0:T(8,128)S(1)} %get-tuple-element.57), channel_id=1, source_target_pairs={{8,0},{12,4},{9,1},{13,5},{10,2},{14,6},{11,3},{15,7},{24,16},{28,... | collective-permute-start | bytes 393224 | tf_op jit(solution)/shard_map/ppermute | solution.py:16
  47.1 10.0 %collective-permute-start.9 = (f32[4,64,128]{2,1,0:T(8,128)S(1)}, f32[4,64,128]{2,1,0:T(8,128)S(1)}, u32[]{:S(2)}, u32[]{:S(2)}) collective-permute-start(f32[4,64,128]{2,1,0:T(8,128)S(1)} %get-tuple-element.59), channel_id=1, source_target_pairs={{4,0},{8,4},{12,8},{5,1},{9,5},{13,9},{6,2},{10,6},{14,10},{7,3},{... | collective-permute-start | bytes 393224 | tf_op jit(solution)/shard_map/ppermute | solution.py:16
  48.4 8.7 %collective-permute-start.10 = (f32[4,64,128]{2,1,0:T(8,128)S(1)}, f32[4,64,128]{2,1,0:T(8,128)S(1)}, u32[]{:S(2)}, u32[]{:S(2)}) collective-permute-start(f32[4,64,128]{2,1,0:T(8,128)S(1)} %get-tuple-element.58), channel_id=1, source_target_pairs={{0,4},{4,8},{8,12},{1,5},{5,9},{9,13},{2,6},{6,10},{10,14},{3,7},{... | collective-permute-start | bytes 393224 | tf_op jit(solution)/shard_map/ppermute | solution.py:16
  51.5 7.1 %collective-permute-start.11 = (f32[4,64,128]{2,1,0:T(8,128)S(1)}, f32[4,64,128]{2,1,0:T(8,128)S(1)}, u32[]{:S(2)}, u32[]{:S(2)}) collective-permute-start(f32[4,64,128]{2,1,0:T(8,128)S(1)} %get-tuple-element.60), channel_id=1, source_target_pairs={{0,8},{4,12},{1,9},{5,13},{2,10},{6,14},{3,11},{7,15},{16,24},{20,... | collective-permute-start | bytes 393224 | tf_op jit(solution)/shard_map/ppermute | solution.py:16
  63.2 13.5 %collective-permute-start.16 = (f32[768]{0:T(1024)S(1)}, f32[768]{0:T(1024)S(1)}, u32[]{:S(2)}, u32[]{:S(2)}) collective-permute-start(f32[768]{0:T(1024)S(1)} %pad_maximum_fusion.28), channel_id=1, source_target_pairs={{0,1},{1,0},{2,3},{3,2},{4,5},{5,4},{6,7},{7,6},{8,9},{9,8},{10,11... | collective-permute-start | bytes 9224 | tf_op jit(solution)/shard_map/ppermute | solution.py:27
  70.2 17.2 %collective-permute-start.12 = (f32[4,1,64,128]{3,2,1,0:T(8,128)S(1)}, f32[4,1,64,128]{3,2,1,0:T(8,128)S(1)}, u32[]{:S(2)}, u32[]{:S(2)}) collective-permute-start(f32[4,1,64,128]{3,2,1,0:T(8,128)S(1)} %get-tuple-element.30), channel_id=1, source_target_pairs={{4,0},{8,4},{12,8},{5,1},{9,5},{13,9},{6,2},{10,6},{14,10},{7,3},{... | collective-permute-start | bytes 393224 | tf_op jit(solution)/shard_map/ppermute | solution.py:44
  71.5 15.9 %collective-permute-start.13 = (f32[4,1,64,128]{3,2,1,0:T(8,128)S(1)}, f32[4,1,64,128]{3,2,1,0:T(8,128)S(1)}, u32[]{:S(2)}, u32[]{:S(2)}) collective-permute-start(f32[4,1,64,128]{3,2,1,0:T(8,128)S(1)} %get-tuple-element.31), channel_id=1, source_target_pairs={{0,4},{4,8},{8,12},{1,5},{5,9},{9,13},{2,6},{6,10},{10,14},{3,7},{... | collective-permute-start | bytes 393224 | tf_op jit(solution)/shard_map/ppermute | solution.py:42
  74.5 12.8 %collective-permute-start.14 = (f32[4,32,1,128]{3,2,1,0:T(1,128)S(1)}, f32[4,32,1,128]{3,2,1,0:T(1,128)S(1)}, u32[]{:S(2)}, u32[]{:S(2)}) collective-permute-start(f32[4,32,1,128]{3,2,1,0:T(1,128)S(1)} %get-tuple-element.32), channel_id=1, source_target_pairs={{1,0},{2,1},{3,2},{0,3},{5,4},{6,5},{7,6},{4,7},{9,8},{10,9},{11,1... | collective-permute-start | bytes 196616 | tf_op jit(solution)/shard_map/ppermute | solution.py:44
  75.6 11.7 %collective-permute-start.15 = (f32[4,32,1,128]{3,2,1,0:T(1,128)S(1)}, f32[4,32,1,128]{3,2,1,0:T(1,128)S(1)}, u32[]{:S(2)}, u32[]{:S(2)}) collective-permute-start(f32[4,32,1,128]{3,2,1,0:T(1,128)S(1)} %get-tuple-element.33), channel_id=1, source_target_pairs={{0,1},{1,2},{2,3},{3,0},{4,5},{5,6},{6,7},{7,4},{8,9},{9,10},{10,1... | collective-permute-start | bytes 196616 | tf_op jit(solution)/shard_map/ppermute | solution.py:42
  76.6 5.9 %collective-permute-start.17 = (f32[768]{0:T(1024)S(1)}, f32[768]{0:T(1024)S(1)}, u32[]{:S(2)}, u32[]{:S(2)}) collective-permute-start(f32[768]{0:T(1024)S(1)} %fusion.138), channel_id=1, source_target_pairs={{0,2},{1,3},{2,0},{3,1},{4,6},{5,7},{6,4},{7,5},{8,10},{9,11},{10,... | collective-permute-start | bytes 9224 | tf_op jit(solution)/shard_map/ppermute | solution.py:27
  82.5 1.2 %collective-permute-start.18 = (f32[768]{0:T(1024)S(1)}, f32[768]{0:T(1024)S(1)}, u32[]{:S(2)}, u32[]{:S(2)}) collective-permute-start(f32[768]{0:T(1024)S(1)} %add.919), channel_id=1, source_target_pairs={{0,4},{4,0},{8,12},{12,8},{1,5},{5,1},{9,13},{13,9},{2,6},{6,2},{1... | collective-permute-start | bytes 9224 | tf_op jit(solution)/shard_map/ppermute | solution.py:27
  83.7 3.6 %collective-permute-start.19 = (f32[768]{0:T(1024)S(1)}, f32[768]{0:T(1024)S(1)}, u32[]{:S(2)}, u32[]{:S(2)}) collective-permute-start(f32[768]{0:T(1024)S(1)} %add.920), channel_id=1, source_target_pairs={{0,8},{4,12},{8,0},{12,4},{1,9},{5,13},{9,1},{13,5},{2,10},{6,14},... | collective-permute-start | bytes 9224 | tf_op jit(solution)/shard_map/ppermute | solution.py:27
  (1 other events, 2.6 us)

commit v4 on v3

--- a/solution.py
+++ b/solution.py
@@ -10,13 +10,8 @@
 CAP = 4
 
 
-def from_behind(block, axis, distance):
-    devices = range(lax.axis_size(axis))
-    route = [(i - distance, i) for i in devices if i - distance in devices]
-    return lax.ppermute(block, axis, route)
-
-
-def all_sum(value, axes):
+def all_sum(value, axes, rider=None):
+    rider_done = None
     for axis in axes:
         count = lax.axis_size(axis)
         if count & (count - 1):
@@ -27,8 +22,13 @@
             value = value + lax.ppermute(
                 value, axis, [(i, i ^ distance) for i in range(count)]
             )
+            if rider is not None:
+                value, rider = lax.optimization_barrier((value, rider))
+                rider_done, rider = rider, None
             distance *= 2
-    return value
+    if rider_done is None and rider is None:
+        return value
+    return value, rider if rider_done is None else rider_done
 
 
 def extended(cells, sides, width, closed):
@@ -190,7 +190,6 @@
     band_cols = col_count // 8
     per_device = band_rows * band_cols
     total_cols = source_ids.shape[1]
-    band_offsets = (-2, -1, 1, 2)
     devices = jnp.arange(lat_count)
     slot_range = jnp.arange(CAP)
     column_ids = lax.dynamic_slice_in_dim(
@@ -211,27 +210,17 @@
     owned_here = remote & (source_dev == lat_index)
     sending = owned_here[:, :, None] & (slot_of[:, :, None] == slot_range[None, None, :])
     send_local = jnp.sum(jnp.where(sending, source_local[:, :, None], 0), axis=1)
-    near_local = jnp.stack(
-        [
-            lax.dynamic_index_in_dim(send_local, lat_index + offset, 0, keepdims=False)
-            for offset in band_offsets
-        ]
-    )
     own_patches = to_patches(state_field)
-    outgoing = own_patches[near_local.reshape(-1)].reshape(4, CAP, 64, value_count)
+    outgoing = own_patches[send_local.reshape(-1)].reshape(lat_count, CAP, 64, value_count)
     my_dev = lax.dynamic_index_in_dim(source_dev, lat_index, 0, keepdims=False)
     my_slot = lax.dynamic_index_in_dim(slot_of, lat_index, 0, keepdims=False)
     my_local = lax.dynamic_index_in_dim(source_local, lat_index, 0, keepdims=False)
     my_remote = lax.dynamic_index_in_dim(remote, lat_index, 0, keepdims=False)
     my_frac = lax.dynamic_index_in_dim(fractions, lat_index, 1, keepdims=False)
-    my_offset = lat_index - my_dev
-    pick_index = jnp.where(my_offset < 0, my_offset + 2, my_offset + 1) * CAP + my_slot
-    arrived = jnp.stack(
-        [
-            from_behind(outgoing[slot_place], "lat", offset)
-            for slot_place, offset in enumerate(band_offsets)
-        ]
-    ).reshape(4 * CAP, 64, value_count)
+    arrived = lax.all_to_all(outgoing, "lat", 0, 0, tiled=True).reshape(
+        lat_count * CAP, 64, value_count
+    )
+    pick_index = my_dev * CAP + my_slot
     patches = jnp.where(my_remote[:, None, None], arrived[pick_index], own_patches[my_local])
     return patches, my_frac
 
@@ -267,9 +256,6 @@
     mix_part = jnp.einsum(
         "plm,pmt->lmt", weight_z, weighted, precision=lax.Precision.HIGHEST
     )
-    totals = all_sum(
-        jnp.concatenate([target_part, first_part, mix_part.reshape(-1)]), ("lon", "lat")
-    )
     parts = []
     for source_level in range(LEV):
         block = planar[:, :, source_level * per_level : (source_level + 1) * per_level]
@@ -279,7 +265,10 @@
         )
         parts.append(from_patches(spread, band_rows, band_cols))
     spread_diffused = diffuse(jnp.stack(parts), diffusivity, 1)
-    spread_diffused, totals = lax.optimization_barrier((spread_diffused, totals))
+    totals, spread_diffused = all_sum(
+        jnp.concatenate([target_part, first_part, mix_part.reshape(-1)]), ("lon", "lat"),
+        spread_diffused,
+    )
     target = totals[:value_count]
     first_mass = totals[value_count : 2 * value_count]
     mix = totals[2 * value_count :].reshape(LEV, LEV, per_level)

time: 97.2 us -> 92.4 us (0.951)
  the two profiles are of different devices: /device:TPU:0 before, /device:TPU:1 now
where the time goes in v4:
time: 92.4 us; the launch traced here: 90.8 us
  starting transfers between devices  32.8 us (35%)
  other arithmetic  22.8 us (25%)
  waiting for transfers between devices  14.5 us (16%)
  local copies, waits for them, and re-layouts  13.9 us (15%)
  matrix products  6.15 us (7%)
    ppermute x3, starting transfers between devices, extended(): lax.ppermute(head, axis, [((i + 1) % count, i) for i in range(ends)])  11 us
    all_to_all x2, waiting for transfers between devices, departed(): lax.all_to_all(outgoing, 'lat', 0, 0, tiled=True)  8.59 us
    all_to_all x2, starting transfers between devices, departed(): lax.all_to_all(outgoing, 'lat', 0, 0, tiled=True)  8.24 us
    ppermute x4, starting transfers between devices, all_sum(): lax.ppermute(value, axis, [(i, i ^ distance) for i in range(count)])  5.87 us
    dot_general x2, matrix products, spatial(): jnp.einsum('nij,njv->niv', plane_weights(fraction_y, fraction_x), patches...  5.01 us
    add x1, other arithmetic, diffuse(): return advected + diffusivity.reshape(k_shape) * laplace  4.98 us
    concatenate x4, other arithmetic, local(): jnp.concatenate([weight_z[:, level, source_level][:, None, None] * block...  3.52 us
    ppermute x4, waiting for transfers between devices, all_sum(): lax.ppermute(value, axis, [(i, i ^ distance) for i in range(count)])  3.08 us
  transfers between devices with their start and end apart: 14, of which 8 were waited for; matrix products, arithmetic and copies ran while one was open for 16% of the time, Pallas kernels for 0%

profile of v4, /device:TPU:1, one launch (start us, length us, event | category | flops | bytes accessed | tf_op | source)
XLA Modules:
  0.0 90.8 jit_solution(15206857494607342368)
XLA Ops:
  1.8 1.4 %copy.25 = f32[4,8,8,8,128]{4,3,2,1,0:T(8,128)S(1)} copy(f32[4,8,8,8,128]{4,3,1,2,0:T(8,128)} %bitcast.173) | data formatting | bytes 2097152 | tf_op jit(solution)/shard_map/transpose | solution.py:116
  3.1 1.4 %gather_fusion = f32[16,64,128]{2,1,0:T(8,128)} fusion(f32[32,64,128]{2,1,0:T(8,128)S(1)} %bitcast.159, s32[1024]{0:T(1024)S(1)} %pad_clamp_fusion.5), kind=kCustom, calls=%fused_computation | custom fusion | bytes 1048640 | tf_op jit(solution)/shard_map/gather | solution.py:214
  4.5 4.3 %all-to-all-start = ((f32[4,4,64,128]{3,2,1,0:T(8,128)}), f32[4,4,64,128]{3,2,1,0:T(8,128)S(1)}, u32[]{:S(2)}, u32[]{:S(2)}) async-start(f32[4,4,64,128]{3,2,1,0:T(8,128)} %bitcast.9), calls=%async_computation | async-start | bytes 1048576 | tf_op jit(solution)/shard_map/all_to_all | solution.py:220
  11.9 4.6 %all-to-all-done = f32[4,4,64,128]{3,2,1,0:T(8,128)S(1)} async-done(((f32[4,4,64,128]{3,2,1,0:T(8,128)}), f32[4,4,64,128]{3,2,1,0:T(8,128)S(1)}, u32[]{:S(2)}, u32[]{:S(2)}) %all-to-all-start) | async-done | bytes 524320 | tf_op jit(solution)/shard_map/all_to_all | solution.py:220
  17.2 1.9 %fusion.29 = f32[32,64,128]{2,1,0:T(8,128)S(1)} fusion(f32[32,64,128]{2,1,0:T(8,128)S(1)} %gather_fusion.1, f32[32,64,128]{2,1,0:T(8,128)S(1)} %gather_fusion.2, f32[64,64]{1,0:T(8,128)S(1)} %get-tuple-element.104, f32[32]{0:T(128)S(1)} %get-tuple-element.128, f32[64,64]{1,0:T(8,128)S(1)} %get-tuple-element.105, f32[32]{0:T(128)S(1)} %get-tuple-element.129, ...), kind=kOutput, calls=%fused_computation.68 | convolution fusion | flops 203554816 | bytes 3277856 | tf_op jit(solution)/shard_map/nij,njv->niv/dot_general | solution.py:88
  19.1 1.1 %multiply_add_fusion.2 = f32[32,64,32]{2,1,0:T(8,128)S(1)} fusion(f32[32,64,128]{2,1,0:T(8,128)S(1)} %fusion.29, f32[32]{0:T(128)S(1)} %get-tuple-element.85, f32[32]{0:T(128)S(1)} %get-tuple-element.86, f32[32]{0:T(128)S(1)} %get-tuple-element.87, f32[32]{0:T(128)S(1)} %get-tuple-element.88), kind=kLoop, calls=%fused_computation.66 | loop fusion | flops 458752 | bytes 1311232 | tf_op jit(solution)/shard_map/add | solution.py:106
  20.2 1.3 %multiply_add_fusion.3 = (f32[32,64,32]{2,1,0:T(8,128)S(1)}, f32[32,64,32]{2,1,0:T(8,128)S(1)}, f32[32,64,32]{2,1,0:T(8,128)S(1)}) fusion(f32[32,64,128]{2,1,0:T(8,128)S(1)} %fusion.29, f32[32]{0:T(128)S(1)} %get-tuple-element.89, f32[32]{0:T(128)S(1)} %get-tuple-element.90, f32[32]{0:T(128)S(1)} %get-tuple-element.79, f32[32]{0:T(128)S(1)} %get-tuple-element.82, ...), kind=kLoop, calls=%fused_computation.67 | loop fusion | flops 851968 | bytes 1836032 | tf_op jit(solution)/shard_map/add | solution.py:106
  22.6 4.2 %collective-permute-start.2 = (f32[32,1,128]{2,1,0:T(1,128)S(1)}, f32[32,1,128]{2,1,0:T(1,128)S(1)}, u32[]{:S(2)}, u32[]{:S(2)}) collective-permute-start(f32[32,1,128]{2,1,0:T(1,128)S(1)} %get-tuple-element.50), channel_id=1, source_target_pairs={{1,0},{2,1},{3,2},{0,3},{5,4},{6,5},{7,6},{4,7},{9,8},{10,9},{11,1... | collective-permute-start | bytes 49160 | tf_op jit(solution)/shard_map/ppermute | solution.py:44
  27.5 3.1 %collective-permute-start = (f32[1,65,128]{2,1,0:T(8,128)S(1)}, f32[1,65,128]{2,1,0:T(8,128)S(1)}, u32[]{:S(2)}, u32[]{:S(2)}) collective-permute-start(f32[1,65,128]{2,1,0:T(8,128)S(1)} %concatenate.56), channel_id=1, source_target_pairs={{4,0},{8,4},{12,8},{5,1},{9,5},{13,9},{6,2},{10,6},{14,10},{7,3},{... | collective-permute-start | bytes 99848 | tf_op jit(solution)/shard_map/ppermute | solution.py:172
  31.2 2.5 %collective-permute-start.1 = (f32[1,65,128]{2,1,0:T(8,128)S(1)}, f32[1,65,128]{2,1,0:T(8,128)S(1)}, u32[]{:S(2)}, u32[]{:S(2)}) collective-permute-start(f32[1,65,128]{2,1,0:T(8,128)S(1)} %concatenate.58), channel_id=1, source_target_pairs={{0,4},{4,8},{8,12},{1,5},{5,9},{9,13},{2,6},{6,10},{10,14},{3,7},{... | collective-permute-start | bytes 99848 | tf_op jit(solution)/shard_map/ppermute | solution.py:167
  33.8 1.0 %collective-permute-done.1 = f32[1,65,128]{2,1,0:T(8,128)S(1)} collective-permute-done((f32[1,65,128]{2,1,0:T(8,128)S(1)}, f32[1,65,128]{2,1,0:T(8,128)S(1)}, u32[]{:S(2)}, u32[]{:S(2)}) %collective-permute-start.1) | collective-permute-done | bytes 33312 | tf_op jit(solution)/shard_map/ppermute | solution.py:167
  35.6 1.4 %gather_fusion.3 = f32[16,64,128]{2,1,0:T(8,128)} fusion(f32[32,64,128]{2,1,0:T(8,128)S(1)} %bitcast.161, s32[1024]{0:T(1024)S(1)} %pad_clamp_fusion.2), kind=kCustom, calls=%fused_computation.3 | custom fusion | bytes 1048640 | tf_op jit(solution)/shard_map/gather | solution.py:214
  37.0 4.0 %all-to-all-start.1 = ((f32[4,4,64,128]{3,2,1,0:T(8,128)}), f32[4,4,64,128]{3,2,1,0:T(8,128)S(1)}, u32[]{:S(2)}, u32[]{:S(2)}) async-start(f32[4,4,64,128]{3,2,1,0:T(8,128)} %bitcast.41), calls=%async_computation.1 | async-start | bytes 1048576 | tf_op jit(solution)/shard_map/all_to_all | solution.py:220
  42.1 1.3 %maximum_multiply_fusion = f32[34]{0:T(128)S(1)} fusion(f32[1]{0:T(128)} %bitcast.32, f32[32]{0:T(128)S(1)} %copy-done.2, f32[1]{0:T(128)} %bitcast.31, s32[]{:T(128)S(6)} %sub.174), kind=kLoop, calls=%fused_computation.321 | loop fusion | flops 272 | bytes 276 | tf_op jit(solution)/shard_map/mul | solution.py:250
  44.6 3.9 %all-to-all-done.1 = f32[4,4,64,128]{3,2,1,0:T(8,128)S(1)} async-done(((f32[4,4,64,128]{3,2,1,0:T(8,128)}), f32[4,4,64,128]{3,2,1,0:T(8,128)S(1)}, u32[]{:S(2)}, u32[]{:S(2)}) %all-to-all-start.1) | async-done | bytes 524320 | tf_op jit(solution)/shard_map/all_to_all | solution.py:220
  48.6 1.6 %gather_fusion.4 = f32[32,64,128]{2,1,0:T(8,128)} fusion(f32[16,64,128]{2,1,0:T(8,128)S(1)} %bitcast.164, s32[1024]{0:T(1024)S(1)} %pad_clamp_fusion.1), kind=kCustom, calls=%fused_computation.4 | custom fusion | bytes 2097280 | tf_op jit(solution)/shard_map/gather | solution.py:224
  50.2 3.1 %fusion.12 = f32[32,64,128]{2,1,0:T(8,128)S(1)} fusion(f32[32,64,128]{2,1,0:T(8,128)} %gather_fusion.4, f32[32,64,128]{2,1,0:T(8,128)S(1)} %gather_fusion.5, f32[32]{0:T(128)S(1)} %get-tuple-element.114, f32[32]{0:T(128)S(1)} %get-tuple-element.115, f32[32]{0:T(128)S(1)} %get-tuple-element.113, f32[32]{0:T(128)S(1)} %get-tuple-element.91, ...), kind=kOutput, calls=%fused_computation.46 | convolution fusion | flops 203554816 | bytes 3277856 | tf_op jit(solution)/shard_map/nij,njv->niv/dot_general | solution.py:88
  53.3 1.0 %fusion.151 = f32[32,1,128]{2,1,0:T(1,128)S(1)} fusion(f32[32,64,1]{1,2,0:T(1,128)S(1)} %bitcast.175, f32[32,64,128]{2,1,0:T(8,128)S(1)} %fusion.12), kind=kOutput, calls=%fused_computation.376 | convolution fusion | flops 3145728 | bytes 1073152 | tf_op jit(solution)/shard_map/pi,piv->pv/dot_general | solution.py:253
  54.7 1.2 %slice_multiply_fusion.11 = (f32[32,64,32]{2,1,0:T(8,128)S(1)}, f32[32,64,32]{2,1,0:T(8,128)S(1)}, f32[32,64,32]{2,1,0:T(8,128)S(1)}, f32[32,64,32]{2,1,0:T(8,12...) fusion(f32[32,64,128]{2,1,0:T(8,128)S(1)} %fusion.12, ...), kind=kLoop, calls=%fused_computation.97 | loop fusion | flops 458752 | bytes 2622336 | tf_op jit(solution)/shard_map/mul | solution.py:263
  56.9 1.1 %slice_multiply_fusion.15 = (f32[32,64,32]{2,1,0:T(8,128)S(1)}, f32[32,64,32]{2,1,0:T(8,128)S(1)}, f32[32,64,32]{2,1,0:T(8,128)S(1)}, f32[32,64,32]{2,1,0:T(8,12...) fusion(f32[32,64,128]{2,1,0:T(8,128)S(1)} %fusion.12, ...), kind=kLoop, calls=%fused_computation.101 | loop fusion | flops 589824 | bytes 3146880 | tf_op jit(solution)/shard_map/mul | solution.py:263
  61.8 3.3 %collective-permute-start.7 = (f32[4,32,1,128]{3,2,1,0:T(1,128)S(1)}, f32[4,32,1,128]{3,2,1,0:T(1,128)S(1)}, u32[]{:S(2)}, u32[]{:S(2)}) collective-permute-start(f32[4,32,1,128]{3,2,1,0:T(1,128)S(1)} %get-tuple-element.32), channel_id=1, source_target_pairs={{1,0},{2,1},{3,2},{0,3},{5,4},{6,5},{7,6},{4,7},{9,8},{10,9},{11,1... | collective-permute-start | bytes 196616 | tf_op jit(solution)/shard_map/ppermute | solution.py:44
  65.1 3.4 %collective-permute-start.5 = (f32[4,1,64,128]{3,2,1,0:T(8,128)S(1)}, f32[4,1,64,128]{3,2,1,0:T(8,128)S(1)}, u32[]{:S(2)}, u32[]{:S(2)}) collective-permute-start(f32[4,1,64,128]{3,2,1,0:T(8,128)S(1)} %get-tuple-element.30), channel_id=1, source_target_pairs={{4,0},{8,4},{12,8},{5,1},{9,5},{13,9},{6,2},{10,6},{14,10},{7,3},{... | collective-permute-start | bytes 393224 | tf_op jit(solution)/shard_map/ppermute | solution.py:44
  68.5 2.1 %collective-permute-start.6 = (f32[4,1,64,128]{3,2,1,0:T(8,128)S(1)}, f32[4,1,64,128]{3,2,1,0:T(8,128)S(1)}, u32[]{:S(2)}, u32[]{:S(2)}) collective-permute-start(f32[4,1,64,128]{3,2,1,0:T(8,128)S(1)} %get-tuple-element.31), channel_id=1, source_target_pairs={{0,4},{4,8},{8,12},{1,5},{5,9},{9,13},{2,6},{6,10},{10,14},{3,7},{... | collective-permute-start | bytes 393224 | tf_op jit(solution)/shard_map/ppermute | solution.py:42
  70.7 1.0 %collective-permute-done.5 = f32[4,1,64,128]{3,2,1,0:T(8,128)S(1)} collective-permute-done((f32[4,1,64,128]{3,2,1,0:T(8,128)S(1)}, f32[4,1,64,128]{3,2,1,0:T(8,128)S(1)}, u32[]{:S(2)}, u32[]{:S(2)}) %collective-permute-start.5) | collective-permute-done | bytes 131104 | tf_op jit(solution)/shard_map/ppermute | solution.py:44
  72.6 5.0 %fusion.3 = f32[4,32,64,128]{3,2,1,0:T(8,128)} fusion(f32[4,32,1,128]{3,2,1,0:T(1,128)S(1)} %collective-permute-done.8, f32[1,32,64,128]{3,2,1,0:T(8,128)S(1)} %bitcast.152, f32[1,32,64,128]{3,2,1,0:T(8,128)S(1)} %bitcast.154, f32[1,32,64,128]{3,2,1,0:T(8,128)S(1)} %bitcast.156, f32[1,32,64,128]{3,2,1,0:T(8,128)S(1)} %bitcast.158, ...), kind=kLoop, calls=%fused_computation.10 | loop fusion | flops 27262976 | bytes 8781952 | tf_op jit(solution)/shard_map/add | solution.py:155
  77.6 2.1 %collective-permute-start.9 = (f32[768]{0:T(1024)S(1)}, f32[768]{0:T(1024)S(1)}, u32[]{:S(2)}, u32[]{:S(2)}) collective-permute-start(f32[768]{0:T(1024)S(1)} %fusion.136), channel_id=1, source_target_pairs={{0,2},{1,3},{2,0},{3,1},{4,6},{5,7},{6,4},{7,5},{8,10},{9,11},{10,... | collective-permute-start | bytes 9224 | tf_op jit(solution)/shard_map/ppermute | solution.py:22
  79.7 1.3 %collective-permute-done.9 = f32[768]{0:T(1024)S(1)} collective-permute-done((f32[768]{0:T(1024)S(1)}, f32[768]{0:T(1024)S(1)}, u32[]{:S(2)}, u32[]{:S(2)}) %collective-permute-start.9) | collective-permute-done | bytes 3104 | tf_op jit(solution)/shard_map/ppermute | solution.py:22
  80.9 1.3 %collective-permute-start.10 = (f32[768]{0:T(1024)S(1)}, f32[768]{0:T(1024)S(1)}, u32[]{:S(2)}, u32[]{:S(2)}) collective-permute-start(f32[768]{0:T(1024)S(1)} %add.836), channel_id=1, source_target_pairs={{0,4},{4,0},{8,12},{12,8},{1,5},{5,1},{9,13},{13,9},{2,6},{6,2},{1... | collective-permute-start | bytes 9224 | tf_op jit(solution)/shard_map/ppermute | solution.py:22
  83.1 2.4 %collective-permute-start.11 = (f32[768]{0:T(1024)S(1)}, f32[768]{0:T(1024)S(1)}, u32[]{:S(2)}, u32[]{:S(2)}) collective-permute-start(f32[768]{0:T(1024)S(1)} %add.837), channel_id=1, source_target_pairs={{0,8},{4,12},{8,0},{12,4},{1,9},{5,13},{9,1},{13,5},{2,10},{6,14},... | collective-permute-start | bytes 9224 | tf_op jit(solution)/shard_map/ppermute | solution.py:22
  85.5 1.0 %collective-permute-done.11 = f32[768]{0:T(1024)S(1)} collective-permute-done((f32[768]{0:T(1024)S(1)}, f32[768]{0:T(1024)S(1)}, u32[]{:S(2)}, u32[]{:S(2)}) %collective-permute-start.11) | collective-permute-done | bytes 3104 | tf_op jit(solution)/shard_map/ppermute | solution.py:22
  86.9 2.9 %multiply_reduce_fusion = f32[32,64,128]{2,1,0:T(8,128)S(1)} fusion(f32[4,32,64,128]{3,2,1,0:T(8,128)} %fusion.3, f32[4,128]{1,0:T(4,128)S(1)} %tile.8), kind=kLoop, calls=%fused_computation.29 | loop fusion | flops 1835008 | bytes 5244928 | tf_op jit(solution)/shard_map/reduce_sum | solution.py:280
  89.7 1.1 %broadcast_multiply_fusion = f32[32,64,128]{2,1,0:T(8,128)} fusion(f32[32,64,128]{2,1,0:T(8,128)S(1)} %multiply_reduce_fusion, f32[128]{0:T(128)S(1)} %slice_divide_fusion.1), kind=kLoop, calls=%fused_computation.102 | loop fusion | flops 262144 | bytes 2097664 | tf_op jit(solution)/shard_map/mul | solution.py:281
  (127 shorter events, 18.0 us)
Async XLA Ops:
  0.0 9.2 %copy-start.1 = (f32[2,3,16,32]{3,2,1,0:T(8,128)S(1)}, f32[2,3,16,32]{3,2,1,0:T(8,128)}, u32[]{:S(2)}) copy-start(f32[2,3,16,32]{3,2,1,0:T(8,128)} %param.5) | copy-start | bytes 36868
  0.0 11.2 %copy-start.2 = (f32[32]{0:T(128)S(1)}, f32[32]{0:T(128)}, u32[]{:S(2)}) copy-start(f32[32]{0:T(128)} %param.6) | copy-start | bytes 388
  4.5 12.1 %all-to-all-start = ((f32[4,4,64,128]{3,2,1,0:T(8,128)}), f32[4,4,64,128]{3,2,1,0:T(8,128)S(1)}, u32[]{:S(2)}, u32[]{:S(2)}) async-start(f32[4,4,64,128]{3,2,1,0:T(8,128)} %bitcast.9), calls=%async_computation | async-start | bytes 1048576 | tf_op jit(solution)/shard_map/all_to_all | solution.py:220
  21.5 13.2 %copy-start = (f32[32,64,128]{2,1,0:T(8,128)S(1)}, f32[32,64,128]{2,1,0:T(8,128)}, u32[]{:S(2)}) copy-start(f32[32,64,128]{2,1,0:T(8,128)} %param.4) | copy-start | bytes 3145732
  22.6 12.1 %collective-permute-start.2 = (f32[32,1,128]{2,1,0:T(1,128)S(1)}, f32[32,1,128]{2,1,0:T(1,128)S(1)}, u32[]{:S(2)}, u32[]{:S(2)}) collective-permute-start(f32[32,1,128]{2,1,0:T(1,128)S(1)} %get-tuple-element.50), channel_id=1, source_target_pairs={{1,0},{2,1},{3,2},{0,3},{5,4},{6,5},{7,6},{4,7},{9,8},{10,9},{11,1... | collective-permute-start | bytes 49160 | tf_op jit(solution)/shard_map/ppermute | solution.py:44
  26.8 7.9 %collective-permute-start.3 = (f32[32,1,128]{2,1,0:T(1,128)S(1)}, f32[32,1,128]{2,1,0:T(1,128)S(1)}, u32[]{:S(2)}, u32[]{:S(2)}) collective-permute-start(f32[32,1,128]{2,1,0:T(1,128)S(1)} %get-tuple-element.51), channel_id=1, source_target_pairs={{0,1},{1,2},{2,3},{3,0},{4,5},{5,6},{6,7},{7,4},{8,9},{9,10},{10,1... | collective-permute-start | bytes 49160 | tf_op jit(solution)/shard_map/ppermute | solution.py:42
  27.5 6.3 %collective-permute-start = (f32[1,65,128]{2,1,0:T(8,128)S(1)}, f32[1,65,128]{2,1,0:T(8,128)S(1)}, u32[]{:S(2)}, u32[]{:S(2)}) collective-permute-start(f32[1,65,128]{2,1,0:T(8,128)S(1)} %concatenate.56), channel_id=1, source_target_pairs={{4,0},{8,4},{12,8},{5,1},{9,5},{13,9},{6,2},{10,6},{14,10},{7,3},{... | collective-permute-start | bytes 99848 | tf_op jit(solution)/shard_map/ppermute | solution.py:172
  31.2 3.6 %collective-permute-start.1 = (f32[1,65,128]{2,1,0:T(8,128)S(1)}, f32[1,65,128]{2,1,0:T(8,128)S(1)}, u32[]{:S(2)}, u32[]{:S(2)}) collective-permute-start(f32[1,65,128]{2,1,0:T(8,128)S(1)} %concatenate.58), channel_id=1, source_target_pairs={{0,4},{4,8},{8,12},{1,5},{5,9},{9,13},{2,6},{6,10},{10,14},{3,7},{... | collective-permute-start | bytes 99848 | tf_op jit(solution)/shard_map/ppermute | solution.py:167
  37.0 11.6 %all-to-all-start.1 = ((f32[4,4,64,128]{3,2,1,0:T(8,128)}), f32[4,4,64,128]{3,2,1,0:T(8,128)S(1)}, u32[]{:S(2)}, u32[]{:S(2)}) async-start(f32[4,4,64,128]{3,2,1,0:T(8,128)} %bitcast.41), calls=%async_computation.1 | async-start | bytes 1048576 | tf_op jit(solution)/shard_map/all_to_all | solution.py:220
  54.6 16.0 %collective-permute-start.4 = (f32[768]{0:T(1024)S(1)}, f32[768]{0:T(1024)S(1)}, u32[]{:S(2)}, u32[]{:S(2)}) collective-permute-start(f32[768]{0:T(1024)S(1)} %pad_maximum_fusion.26), channel_id=1, source_target_pairs={{0,1},{1,0},{2,3},{3,2},{4,5},{5,4},{6,7},{7,6},{8,9},{9,8},{10,11... | collective-permute-start | bytes 9224 | tf_op jit(solution)/shard_map/ppermute | solution.py:22
  61.8 8.9 %collective-permute-start.7 = (f32[4,32,1,128]{3,2,1,0:T(1,128)S(1)}, f32[4,32,1,128]{3,2,1,0:T(1,128)S(1)}, u32[]{:S(2)}, u32[]{:S(2)}) collective-permute-start(f32[4,32,1,128]{3,2,1,0:T(1,128)S(1)} %get-tuple-element.32), channel_id=1, source_target_pairs={{1,0},{2,1},{3,2},{0,3},{5,4},{6,5},{7,6},{4,7},{9,8},{10,9},{11,1... | collective-permute-start | bytes 196616 | tf_op jit(solution)/shard_map/ppermute | solution.py:44
  65.1 5.6 %collective-permute-start.8 = (f32[4,32,1,128]{3,2,1,0:T(1,128)S(1)}, f32[4,32,1,128]{3,2,1,0:T(1,128)S(1)}, u32[]{:S(2)}, u32[]{:S(2)}) collective-permute-start(f32[4,32,1,128]{3,2,1,0:T(1,128)S(1)} %get-tuple-element.33), channel_id=1, source_target_pairs={{0,1},{1,2},{2,3},{3,0},{4,5},{5,6},{6,7},{7,4},{8,9},{9,10},{10,1... | collective-permute-start | bytes 196616 | tf_op jit(solution)/shard_map/ppermute | solution.py:42
  65.1 6.6 %collective-permute-start.5 = (f32[4,1,64,128]{3,2,1,0:T(8,128)S(1)}, f32[4,1,64,128]{3,2,1,0:T(8,128)S(1)}, u32[]{:S(2)}, u32[]{:S(2)}) collective-permute-start(f32[4,1,64,128]{3,2,1,0:T(8,128)S(1)} %get-tuple-element.30), channel_id=1, source_target_pairs={{4,0},{8,4},{12,8},{5,1},{9,5},{13,9},{6,2},{10,6},{14,10},{7,3},{... | collective-permute-start | bytes 393224 | tf_op jit(solution)/shard_map/ppermute | solution.py:44
  68.5 4.0 %collective-permute-start.6 = (f32[4,1,64,128]{3,2,1,0:T(8,128)S(1)}, f32[4,1,64,128]{3,2,1,0:T(8,128)S(1)}, u32[]{:S(2)}, u32[]{:S(2)}) collective-permute-start(f32[4,1,64,128]{3,2,1,0:T(8,128)S(1)} %get-tuple-element.31), channel_id=1, source_target_pairs={{0,4},{4,8},{8,12},{1,5},{5,9},{9,13},{2,6},{6,10},{10,14},{3,7},{... | collective-permute-start | bytes 393224 | tf_op jit(solution)/shard_map/ppermute | solution.py:42
  77.6 3.4 %collective-permute-start.9 = (f32[768]{0:T(1024)S(1)}, f32[768]{0:T(1024)S(1)}, u32[]{:S(2)}, u32[]{:S(2)}) collective-permute-start(f32[768]{0:T(1024)S(1)} %fusion.136), channel_id=1, source_target_pairs={{0,2},{1,3},{2,0},{3,1},{4,6},{5,7},{6,4},{7,5},{8,10},{9,11},{10,... | collective-permute-start | bytes 9224 | tf_op jit(solution)/shard_map/ppermute | solution.py:22
  80.9 2.1 %collective-permute-start.10 = (f32[768]{0:T(1024)S(1)}, f32[768]{0:T(1024)S(1)}, u32[]{:S(2)}, u32[]{:S(2)}) collective-permute-start(f32[768]{0:T(1024)S(1)} %add.836), channel_id=1, source_target_pairs={{0,4},{4,0},{8,12},{12,8},{1,5},{5,1},{9,13},{13,9},{2,6},{6,2},{1... | collective-permute-start | bytes 9224 | tf_op jit(solution)/shard_map/ppermute | solution.py:22
  83.1 3.4 %collective-permute-start.11 = (f32[768]{0:T(1024)S(1)}, f32[768]{0:T(1024)S(1)}, u32[]{:S(2)}, u32[]{:S(2)}) collective-permute-start(f32[768]{0:T(1024)S(1)} %add.837), channel_id=1, source_target_pairs={{0,8},{4,12},{8,0},{12,4},{1,9},{5,13},{9,1},{13,5},{2,10},{6,14},... | collective-permute-start | bytes 9224 | tf_op jit(solution)/shard_map/ppermute | solution.py:22

commit v5 on v4

--- a/solution.py
+++ b/solution.py
@@ -256,29 +256,21 @@
     mix_part = jnp.einsum(
         "plm,pmt->lmt", weight_z, weighted, precision=lax.Precision.HIGHEST
     )
-    parts = []
-    for source_level in range(LEV):
-        block = planar[:, :, source_level * per_level : (source_level + 1) * per_level]
-        spread = jnp.concatenate(
-            [weight_z[:, level, source_level][:, None, None] * block for level in range(LEV)],
-            axis=2,
-        )
-        parts.append(from_patches(spread, band_rows, band_cols))
-    spread_diffused = diffuse(jnp.stack(parts), diffusivity, 1)
-    totals, spread_diffused = all_sum(
-        jnp.concatenate([target_part, first_part, mix_part.reshape(-1)]), ("lon", "lat"),
-        spread_diffused,
+    totals = all_sum(
+        jnp.concatenate([target_part, first_part, mix_part.reshape(-1)]), ("lon", "lat")
     )
     target = totals[:value_count]
     first_mass = totals[value_count : 2 * value_count]
     mix = totals[2 * value_count :].reshape(LEV, LEV, per_level)
-    first_ratio = (target / first_mass).reshape(LEV, per_level)
-    second_mass = jnp.sum(first_ratio[None] * mix, axis=1).reshape(value_count)
+    first_ratio = target / first_mass
+    second_mass = jnp.sum(first_ratio.reshape(LEV, per_level)[None] * mix, axis=1).reshape(
+        value_count
+    )
     second_ratio = target / second_mass
-
-    factor = jnp.tile(first_ratio, (1, LEV))
-    combined = jnp.sum(factor[:, None, None, :] * spread_diffused, axis=0)
-    return combined * second_ratio[None, None, :]
+    advected = from_patches(
+        levels(planar * first_ratio[None, None, :], frac[2]), band_rows, band_cols
+    )
+    return diffuse(advected, diffusivity, 0) * second_ratio[None, None, :]
 
 
 def solution(mesh):

time: 92.4 us -> 82.7 us (0.90); the launches traced: 90.8 us -> 82.2 us
  other arithmetic: 22.8 us -> 12.3 us
  waiting for transfers between devices: 14.5 us -> 21.1 us
  starting transfers between devices: 32.8 us -> 30.3 us
  matrix products: 6.15 us -> 4.93 us
  local copies, waits for them, and re-layouts: 13.9 us -> 12.9 us
    ppermute x4, waiting for transfers between devices: 3.08 us -> 8.4 us  [all_sum(): lax.ppermute(value, axis, [(i, i ^ distance) for i in range(count)])]
    add x1 -> x0, other arithmetic: 4.98 us -> none  [diffuse(): return advected + diffusivity.reshape(k_shape) * laplace]
    ppermute x3, starting transfers between devices: 11 us -> 7.27 us  [extended(): lax.ppermute(head, axis, [((i + 1) % count, i) for i in range(ends)])]
    ppermute x3, starting transfers between devices: 2.12 us -> 5.78 us  [extended(): lax.ppermute(tail, axis, [(i, (i + 1) % count) for i in range(ends)])]
    concatenate x4 -> x0, other arithmetic: 3.52 us -> none  [local(): jnp.concatenate([weight_z[:, level, source_level][:, None, None] * block...]
    reduce_sum x2 -> x1, other arithmetic: 2.87 us -> 0.02 us  [local(): jnp.sum(first_ratio.reshape(LEV, per_level)[None] * mix, axis=1)]
    ppermute x1, waiting for transfers between devices: 0.01 us -> 2.68 us  [diffuse_first(): lax.ppermute(pack(advected[:1], diffusivity[0]), 'lat', [(i + 1, i) for i...]
    add x2 -> x4, other arithmetic: 2.42 us -> 4.85 us  [levels(): acc = term if acc is None else acc + term]
  transfers between devices with their start and end apart: 14 -> 14, of which waited for: 8 -> 8; matrix products, arithmetic and copies ran while one was open for 16% -> 10% of each run, Pallas kernels for 0% -> 0%
where the time goes in v5:
time: 82.7 us; the launch traced here: 82.2 us
  starting transfers between devices  30.3 us (37%)
  waiting for transfers between devices  21.1 us (26%)
  local copies, waits for them, and re-layouts  12.9 us (16%)
  other arithmetic  12.3 us (15%)
  matrix products  4.93 us (6%)
    ppermute x4, waiting for transfers between devices, all_sum(): lax.ppermute(value, axis, [(i, i ^ distance) for i in range(count)])  8.4 us
    all_to_all x2, starting transfers between devices, departed(): lax.all_to_all(outgoing, 'lat', 0, 0, tiled=True)  8.04 us
    ppermute x3, starting transfers between devices, extended(): lax.ppermute(head, axis, [((i + 1) % count, i) for i in range(ends)])  7.27 us
    all_to_all x2, waiting for transfers between devices, departed(): lax.all_to_all(outgoing, 'lat', 0, 0, tiled=True)  6.95 us
    ppermute x3, starting transfers between devices, extended(): lax.ppermute(tail, axis, [(i, (i + 1) % count) for i in range(ends)])  5.78 us
    add x4, other arithmetic, levels(): acc = term if acc is None else acc + term  4.85 us
    ppermute x4, starting transfers between devices, all_sum(): lax.ppermute(value, axis, [(i, i ^ distance) for i in range(count)])  4.22 us
    dot_general x2, matrix products, spatial(): jnp.einsum('nij,njv->niv', plane_weights(fraction_y, fraction_x), patches...  3.79 us
  transfers between devices with their start and end apart: 14, of which 8 were waited for; matrix products, arithmetic and copies ran while one was open for 10% of the time, Pallas kernels for 0%

profile of v5, /device:TPU:1, one launch (start us, length us, event | category | flops | bytes accessed | tf_op | source)
XLA Modules:
  0.0 82.2 jit_solution(6165924283731308328)
XLA Ops:
  0.0 1.4 %copy.20 = f32[4,8,8,8,128]{4,3,2,1,0:T(8,128)S(1)} copy(f32[4,8,8,8,128]{4,3,1,2,0:T(8,128)} %bitcast.145) | data formatting | bytes 2097152 | tf_op jit(solution)/shard_map/transpose | solution.py:116
  2.4 1.4 %gather_fusion = f32[16,64,128]{2,1,0:T(8,128)} fusion(f32[32,64,128]{2,1,0:T(8,128)S(1)} %bitcast.131, s32[1024]{0:T(1024)S(1)} %pad_clamp_fusion.5), kind=kCustom, calls=%fused_computation | custom fusion | bytes 1048640 | tf_op jit(solution)/shard_map/gather | solution.py:214
  3.8 4.4 %all-to-all-start = ((f32[4,4,64,128]{3,2,1,0:T(8,128)}), f32[4,4,64,128]{3,2,1,0:T(8,128)S(1)}, u32[]{:S(2)}, u32[]{:S(2)}) async-start(f32[4,4,64,128]{3,2,1,0:T(8,128)} %bitcast.14), calls=%async_computation | async-start | bytes 1048576 | tf_op jit(solution)/shard_map/all_to_all | solution.py:220
  11.4 4.6 %all-to-all-done = f32[4,4,64,128]{3,2,1,0:T(8,128)S(1)} async-done(((f32[4,4,64,128]{3,2,1,0:T(8,128)}), f32[4,4,64,128]{3,2,1,0:T(8,128)S(1)}, u32[]{:S(2)}, u32[]{:S(2)}) %all-to-all-start) | async-done | bytes 524320 | tf_op jit(solution)/shard_map/all_to_all | solution.py:220
  16.6 1.9 %fusion.15 = f32[32,64,128]{2,1,0:T(8,128)S(1)} fusion(f32[32,64,128]{2,1,0:T(8,128)S(1)} %gather_fusion.1, f32[32,64,128]{2,1,0:T(8,128)S(1)} %gather_fusion.2, f32[32]{0:T(128)S(1)} %get-tuple-element.107, f32[32]{0:T(128)S(1)} %get-tuple-element.108, f32[32]{0:T(128)S(1)} %get-tuple-element.106, f32[32]{0:T(128)S(1)} %get-tuple-element.76, ...), kind=kOutput, calls=%fused_computation.42 | convolution fusion | flops 203554816 | bytes 3277856 | tf_op jit(solution)/shard_map/nij,njv->niv/dot_general | solution.py:88
  18.5 1.1 %multiply_add_fusion.6 = f32[32,64,32]{2,1,0:T(8,128)S(1)} fusion(f32[32,64,128]{2,1,0:T(8,128)S(1)} %fusion.15, f32[32]{0:T(128)S(1)} %get-tuple-element.64, f32[32]{0:T(128)S(1)} %get-tuple-element.65, f32[32]{0:T(128)S(1)} %get-tuple-element.66, f32[32]{0:T(128)S(1)} %get-tuple-element.67), kind=kLoop, calls=%fused_computation.40 | loop fusion | flops 458752 | bytes 1311232 | tf_op jit(solution)/shard_map/add | solution.py:106
  19.7 1.3 %multiply_add_fusion.7 = (f32[32,64,32]{2,1,0:T(8,128)S(1)}, f32[32,64,32]{2,1,0:T(8,128)S(1)}, f32[32,64,32]{2,1,0:T(8,128)S(1)}) fusion(f32[32,64,128]{2,1,0:T(8,128)S(1)} %fusion.15, f32[32]{0:T(128)S(1)} %get-tuple-element.68, f32[32]{0:T(128)S(1)} %get-tuple-element.69, f32[32]{0:T(128)S(1)} %get-tuple-element.58, f32[32]{0:T(128)S(1)} %get-tuple-element.61, ...), kind=kLoop, calls=%fused_computation.41 | loop fusion | flops 851968 | bytes 1836032 | tf_op jit(solution)/shard_map/add | solution.py:106
  21.0 0.9 %pad_maximum_fusion.8 = f32[32,64,128]{2,1,0:T(8,128)S(1)} fusion(f32[32,64,32]{2,1,0:T(8,128)S(1)} %get-tuple-element.39, f32[32,64,32]{2,1,0:T(8,128)S(1)} %get-tuple-element.38, f32[32,64,32]{2,1,0:T(8,128)S(1)} %multiply_add_fusion.6, f32[32,64,32]{2,1,0:T(8,128)S(1)} %get-tuple-element.37), kind=kLoop, calls=%fused_computation.28 | loop fusion | flops 786432 | bytes 2097152 | tf_op jit(solution)/shard_map/concatenate | solution.py:108
  22.0 2.2 %collective-permute-start.3 = (f32[32,1,128]{2,1,0:T(1,128)S(1)}, f32[32,1,128]{2,1,0:T(1,128)S(1)}, u32[]{:S(2)}, u32[]{:S(2)}) collective-permute-start(f32[32,1,128]{2,1,0:T(1,128)S(1)} %get-tuple-element.36), channel_id=1, source_target_pairs={{0,1},{1,2},{2,3},{3,0},{4,5},{5,6},{6,7},{7,4},{8,9},{9,10},{10,1... | collective-permute-start | bytes 49160 | tf_op jit(solution)/shard_map/ppermute | solution.py:42
  24.3 2.1 %collective-permute-start.2 = (f32[32,1,128]{2,1,0:T(1,128)S(1)}, f32[32,1,128]{2,1,0:T(1,128)S(1)}, u32[]{:S(2)}, u32[]{:S(2)}) collective-permute-start(f32[32,1,128]{2,1,0:T(1,128)S(1)} %get-tuple-element.35), channel_id=1, source_target_pairs={{1,0},{2,1},{3,2},{0,3},{5,4},{6,5},{7,6},{4,7},{9,8},{10,9},{11,1... | collective-permute-start | bytes 49160 | tf_op jit(solution)/shard_map/ppermute | solution.py:44
  27.0 3.0 %collective-permute-start.1 = (f32[1,65,128]{2,1,0:T(8,128)S(1)}, f32[1,65,128]{2,1,0:T(8,128)S(1)}, u32[]{:S(2)}, u32[]{:S(2)}) collective-permute-start(f32[1,65,128]{2,1,0:T(8,128)S(1)} %concatenate.49), channel_id=1, source_target_pairs={{0,4},{4,8},{8,12},{1,5},{5,9},{9,13},{2,6},{6,10},{10,14},{3,7},{... | collective-permute-start | bytes 99848 | tf_op jit(solution)/shard_map/ppermute | solution.py:167
  30.6 1.9 %collective-permute-start = (f32[1,65,128]{2,1,0:T(8,128)S(1)}, f32[1,65,128]{2,1,0:T(8,128)S(1)}, u32[]{:S(2)}, u32[]{:S(2)}) collective-permute-start(f32[1,65,128]{2,1,0:T(8,128)S(1)} %concatenate.47), channel_id=1, source_target_pairs={{4,0},{8,4},{12,8},{5,1},{9,5},{13,9},{6,2},{10,6},{14,10},{7,3},{... | collective-permute-start | bytes 99848 | tf_op jit(solution)/shard_map/ppermute | solution.py:172
  33.2 2.7 %collective-permute-done = f32[1,65,128]{2,1,0:T(8,128)S(1)} collective-permute-done((f32[1,65,128]{2,1,0:T(8,128)S(1)}, f32[1,65,128]{2,1,0:T(8,128)S(1)}, u32[]{:S(2)}, u32[]{:S(2)}) %collective-permute-start) | collective-permute-done | bytes 33312 | tf_op jit(solution)/shard_map/ppermute | solution.py:172
  37.5 1.4 %gather_fusion.3 = f32[16,64,128]{2,1,0:T(8,128)} fusion(f32[32,64,128]{2,1,0:T(8,128)S(1)} %bitcast.133, s32[1024]{0:T(1024)S(1)} %pad_clamp_fusion.2), kind=kCustom, calls=%fused_computation.3 | custom fusion | bytes 1048640 | tf_op jit(solution)/shard_map/gather | solution.py:214
  38.9 3.6 %all-to-all-start.1 = ((f32[4,4,64,128]{3,2,1,0:T(8,128)}), f32[4,4,64,128]{3,2,1,0:T(8,128)S(1)}, u32[]{:S(2)}, u32[]{:S(2)}) async-start(f32[4,4,64,128]{3,2,1,0:T(8,128)} %bitcast.40), calls=%async_computation.1 | async-start | bytes 1048576 | tf_op jit(solution)/shard_map/all_to_all | solution.py:220
  44.3 1.3 %maximum_multiply_fusion = f32[34]{0:T(128)S(1)} fusion(f32[1]{0:T(128)} %bitcast.47, f32[32]{0:T(128)S(1)} %copy-done.5, f32[1]{0:T(128)} %bitcast.46, s32[]{:T(128)S(6)} %sub.190), kind=kLoop, calls=%fused_computation.289 | loop fusion | flops 272 | bytes 276 | tf_op jit(solution)/shard_map/mul | solution.py:250
  46.1 2.3 %all-to-all-done.1 = f32[4,4,64,128]{3,2,1,0:T(8,128)S(1)} async-done(((f32[4,4,64,128]{3,2,1,0:T(8,128)}), f32[4,4,64,128]{3,2,1,0:T(8,128)S(1)}, u32[]{:S(2)}, u32[]{:S(2)}) %all-to-all-start.1) | async-done | bytes 524320 | tf_op jit(solution)/shard_map/all_to_all | solution.py:220
  49.0 1.9 %fusion.13 = f32[32,64,128]{2,1,0:T(8,128)S(1)} fusion(f32[32,64,128]{2,1,0:T(8,128)S(1)} %gather_fusion.4, f32[32,64,128]{2,1,0:T(8,128)S(1)} %gather_fusion.5, f32[64,64]{1,0:T(8,128)S(1)} %get-tuple-element.83, f32[32]{0:T(128)S(1)} %get-tuple-element.96, f32[64,64]{1,0:T(8,128)S(1)} %get-tuple-element.84, f32[32]{0:T(128)S(1)} %get-tuple-element.97, ...), kind=kOutput, calls=%fused_computation.36 | convolution fusion | flops 203554816 | bytes 3277856 | tf_op jit(solution)/shard_map/nij,njv->niv/dot_general | solution.py:88
  50.9 1.0 %fusion.152 = f32[32,1,128]{2,1,0:T(1,128)S(1)} fusion(f32[32,64,1]{1,2,0:T(1,128)S(1)} %bitcast.147, f32[32,64,128]{2,1,0:T(8,128)S(1)} %fusion.13), kind=kOutput, calls=%fused_computation.344 | convolution fusion | flops 3145728 | bytes 1073152 | tf_op jit(solution)/shard_map/pi,piv->pv/dot_general | solution.py:253
  52.4 2.4 %collective-permute-done.4 = f32[768]{0:T(1024)S(1)} collective-permute-done((f32[768]{0:T(1024)S(1)}, f32[768]{0:T(1024)S(1)}, u32[]{:S(2)}, u32[]{:S(2)}) %collective-permute-start.4) | collective-permute-done | bytes 3104 | tf_op jit(solution)/shard_map/ppermute | solution.py:22
  55.6 2.7 %collective-permute-done.5 = f32[768]{0:T(1024)S(1)} collective-permute-done((f32[768]{0:T(1024)S(1)}, f32[768]{0:T(1024)S(1)}, u32[]{:S(2)}, u32[]{:S(2)}) %collective-permute-start.5) | collective-permute-done | bytes 3104 | tf_op jit(solution)/shard_map/ppermute | solution.py:22
  58.3 3.4 %collective-permute-start.6 = (f32[768]{0:T(1024)S(1)}, f32[768]{0:T(1024)S(1)}, u32[]{:S(2)}, u32[]{:S(2)}) collective-permute-start(f32[768]{0:T(1024)S(1)} %add.862), channel_id=1, source_target_pairs={{0,4},{4,0},{8,12},{12,8},{1,5},{5,1},{9,13},{13,9},{2,6},{6,2},{1... | collective-permute-start | bytes 9224 | tf_op jit(solution)/shard_map/ppermute | solution.py:22
  61.7 0.8 %collective-permute-done.6 = f32[768]{0:T(1024)S(1)} collective-permute-done((f32[768]{0:T(1024)S(1)}, f32[768]{0:T(1024)S(1)}, u32[]{:S(2)}, u32[]{:S(2)}) %collective-permute-start.6) | collective-permute-done | bytes 3104 | tf_op jit(solution)/shard_map/ppermute | solution.py:22
  62.5 2.4 %collective-permute-done.7 = f32[768]{0:T(1024)S(1)} collective-permute-done((f32[768]{0:T(1024)S(1)}, f32[768]{0:T(1024)S(1)}, u32[]{:S(2)}, u32[]{:S(2)}) %collective-permute-start.7) | collective-permute-done | bytes 3104 | tf_op jit(solution)/shard_map/ppermute | solution.py:22
  65.1 1.1 %multiply_add_fusion.2 = f32[32,64,32]{2,1,0:T(8,128)S(1)} fusion(f32[32,64,128]{2,1,0:T(8,128)S(1)} %broadcast_multiply_fusion, f32[32]{0:T(128)S(1)} %get-tuple-element.50, f32[32]{0:T(128)S(1)} %get-tuple-element.51, f32[32]{0:T(128)S(1)} %get-tuple-element.52, f32[32]{0:T(128)S(1)} %get-tuple-element.53), kind=kLoop, calls=%fused_computation.32 | loop fusion | flops 458752 | bytes 1311232 | tf_op jit(solution)/shard_map/add | solution.py:106
  66.2 1.3 %multiply_add_fusion.3 = (f32[32,64,32]{2,1,0:T(8,128)S(1)}, f32[32,64,32]{2,1,0:T(8,128)S(1)}, f32[32,64,32]{2,1,0:T(8,128)S(1)}) fusion(f32[32,64,128]{2,1,0:T(8,128)S(1)} %broadcast_multiply_fusion, f32[32]{0:T(128)S(1)} %get-tuple-element.54, f32[32]{0:T(128)S(1)} %get-tuple-element.55, f32[32]{0:T(128)S(1)} %get-tuple-element.44, ...), kind=kLoop, calls=%fused_computation.33 | loop fusion | flops 851968 | bytes 1836032 | tf_op jit(solution)/shard_map/add | solution.py:106
  67.5 0.9 %pad_maximum_fusion.9 = f32[32,64,128]{2,1,0:T(8,128)S(1)} fusion(f32[32,64,32]{2,1,0:T(8,128)S(1)} %get-tuple-element.32, f32[32,64,32]{2,1,0:T(8,128)S(1)} %get-tuple-element.31, f32[32,64,32]{2,1,0:T(8,128)S(1)} %multiply_add_fusion.2, f32[32,64,32]{2,1,0:T(8,128)S(1)} %get-tuple-element.30), kind=kLoop, calls=%fused_computation.29 | loop fusion | flops 786432 | bytes 2097152 | tf_op jit(solution)/shard_map/concatenate | solution.py:108
  68.7 3.3 %collective-permute-start.10 = (f32[32,1,128]{2,1,0:T(1,128)S(1)}, f32[32,1,128]{2,1,0:T(1,128)S(1)}, u32[]{:S(2)}, u32[]{:S(2)}) collective-permute-start(f32[32,1,128]{2,1,0:T(1,128)S(1)} %get-tuple-element.28), channel_id=1, source_target_pairs={{1,0},{2,1},{3,2},{0,3},{5,4},{6,5},{7,6},{4,7},{9,8},{10,9},{11,1... | collective-permute-start | bytes 49160 | tf_op jit(solution)/shard_map/ppermute | solution.py:44
  71.9 3.6 %collective-permute-start.9 = (f32[1,64,128]{2,1,0:T(8,128)S(1)}, f32[1,64,128]{2,1,0:T(8,128)S(1)}, u32[]{:S(2)}, u32[]{:S(2)}) collective-permute-start(f32[1,64,128]{2,1,0:T(8,128)S(1)} %get-tuple-element.27), channel_id=1, source_target_pairs={{0,4},{4,8},{8,12},{1,5},{5,9},{9,13},{2,6},{6,10},{10,14},{3,7},{... | collective-permute-start | bytes 98312 | tf_op jit(solution)/shard_map/ppermute | solution.py:42
  75.5 1.9 %collective-permute-start.8 = (f32[1,64,128]{2,1,0:T(8,128)S(1)}, f32[1,64,128]{2,1,0:T(8,128)S(1)}, u32[]{:S(2)}, u32[]{:S(2)}) collective-permute-start(f32[1,64,128]{2,1,0:T(8,128)S(1)} %get-tuple-element.26), channel_id=1, source_target_pairs={{4,0},{8,4},{12,8},{5,1},{9,5},{13,9},{6,2},{10,6},{14,10},{7,3},{... | collective-permute-start | bytes 98312 | tf_op jit(solution)/shard_map/ppermute | solution.py:44
  77.7 3.1 %collective-permute-done.8 = f32[1,64,128]{2,1,0:T(8,128)S(1)} collective-permute-done((f32[1,64,128]{2,1,0:T(8,128)S(1)}, f32[1,64,128]{2,1,0:T(8,128)S(1)}, u32[]{:S(2)}, u32[]{:S(2)}) %collective-permute-start.8) | collective-permute-done | bytes 32800 | tf_op jit(solution)/shard_map/ppermute | solution.py:44
  80.7 1.4 %fusion.4 = f32[32,64,128]{2,1,0:T(8,128)} fusion(f32[32,64,128]{2,1,0:T(8,128)S(1)} %bitcast.139, f32[32,1,128]{2,1,0:T(1,128)S(1)} %collective-permute-done.11, f32[32,1,128]{2,1,0:T(1,128)S(1)} %collective-permute-done.10, f32[1,64,128]{2,1,0:T(8,128)S(1)} %collective-permute-done.9, f32[1,64,128]{2,1,0:T(8,128)S(1)} %collective-permute-done.8, ...), kind=kLoop, calls=%fused_computation.12 | loop fusion | flops 3145728 | bytes 2196096 | tf_op jit(solution)/shard_map/mul | solution.py:273
  (124 shorter events, 12.8 us)
Async XLA Ops:
  0.0 1.4 %copy-start.4 = (s32[2,16,32]{2,1,0:T(8,128)S(1)}, s32[2,16,32]{2,1,0:T(8,128)}, u32[]{:S(2)}) copy-start(s32[2,16,32]{2,1,0:T(8,128)} %param.7) | copy-start | bytes 12292
  3.8 4.5 %copy-start.3 = (f32[2,3,16,32]{3,2,1,0:T(8,128)S(1)}, f32[2,3,16,32]{3,2,1,0:T(8,128)}, u32[]{:S(2)}) copy-start(f32[2,3,16,32]{3,2,1,0:T(8,128)} %param.5) | copy-start | bytes 36868
  3.8 12.2 %all-to-all-start = ((f32[4,4,64,128]{3,2,1,0:T(8,128)}), f32[4,4,64,128]{3,2,1,0:T(8,128)S(1)}, u32[]{:S(2)}, u32[]{:S(2)}) async-start(f32[4,4,64,128]{3,2,1,0:T(8,128)} %bitcast.14), calls=%async_computation | async-start | bytes 1048576 | tf_op jit(solution)/shard_map/all_to_all | solution.py:220
  10.0 0.7 copy-start.5
  21.8 14.1 %copy-start = (f32[32,64,128]{2,1,0:T(8,128)S(1)}, f32[32,64,128]{2,1,0:T(8,128)}, u32[]{:S(2)}) copy-start(f32[32,64,128]{2,1,0:T(8,128)} %param.4) | copy-start | bytes 3145732
  22.0 13.9 %collective-permute-start.3 = (f32[32,1,128]{2,1,0:T(1,128)S(1)}, f32[32,1,128]{2,1,0:T(1,128)S(1)}, u32[]{:S(2)}, u32[]{:S(2)}) collective-permute-start(f32[32,1,128]{2,1,0:T(1,128)S(1)} %get-tuple-element.36), channel_id=1, source_target_pairs={{0,1},{1,2},{2,3},{3,0},{4,5},{5,6},{6,7},{7,4},{8,9},{9,10},{10,1... | collective-permute-start | bytes 49160 | tf_op jit(solution)/shard_map/ppermute | solution.py:42
  24.3 11.7 %collective-permute-start.2 = (f32[32,1,128]{2,1,0:T(1,128)S(1)}, f32[32,1,128]{2,1,0:T(1,128)S(1)}, u32[]{:S(2)}, u32[]{:S(2)}) collective-permute-start(f32[32,1,128]{2,1,0:T(1,128)S(1)} %get-tuple-element.35), channel_id=1, source_target_pairs={{1,0},{2,1},{3,2},{0,3},{5,4},{6,5},{7,6},{4,7},{9,8},{10,9},{11,1... | collective-permute-start | bytes 49160 | tf_op jit(solution)/shard_map/ppermute | solution.py:44
  27.0 5.7 %collective-permute-start.1 = (f32[1,65,128]{2,1,0:T(8,128)S(1)}, f32[1,65,128]{2,1,0:T(8,128)S(1)}, u32[]{:S(2)}, u32[]{:S(2)}) collective-permute-start(f32[1,65,128]{2,1,0:T(8,128)S(1)} %concatenate.49), channel_id=1, source_target_pairs={{0,4},{4,8},{8,12},{1,5},{5,9},{9,13},{2,6},{6,10},{10,14},{3,7},{... | collective-permute-start | bytes 99848 | tf_op jit(solution)/shard_map/ppermute | solution.py:167
  30.6 5.3 %collective-permute-start = (f32[1,65,128]{2,1,0:T(8,128)S(1)}, f32[1,65,128]{2,1,0:T(8,128)S(1)}, u32[]{:S(2)}, u32[]{:S(2)}) collective-permute-start(f32[1,65,128]{2,1,0:T(8,128)S(1)} %concatenate.47), channel_id=1, source_target_pairs={{4,0},{8,4},{12,8},{5,1},{9,5},{13,9},{6,2},{10,6},{14,10},{7,3},{... | collective-permute-start | bytes 99848 | tf_op jit(solution)/shard_map/ppermute | solution.py:172
  32.6 0.6 copy-start.1
  35.9 0.8 slice-start
  38.9 9.5 %all-to-all-start.1 = ((f32[4,4,64,128]{3,2,1,0:T(8,128)}), f32[4,4,64,128]{3,2,1,0:T(8,128)S(1)}, u32[]{:S(2)}, u32[]{:S(2)}) async-start(f32[4,4,64,128]{3,2,1,0:T(8,128)} %bitcast.40), calls=%async_computation.1 | async-start | bytes 1048576 | tf_op jit(solution)/shard_map/all_to_all | solution.py:220
  42.6 1.1 %copy-start.2 = (f32[1,65,128]{2,1,0:T(8,128)S(1)}, f32[1,65,128]{2,1,0:T(8,128)}, u32[]{:S(2)}) copy-start(f32[1,65,128]{2,1,0:T(8,128)} %copy-done.1) | copy-start | bytes 99844
  52.3 2.5 %collective-permute-start.4 = (f32[768]{0:T(1024)S(1)}, f32[768]{0:T(1024)S(1)}, u32[]{:S(2)}, u32[]{:S(2)}) collective-permute-start(f32[768]{0:T(1024)S(1)} %pad_maximum_fusion.10), channel_id=1, source_target_pairs={{0,1},{1,0},{2,3},{3,2},{4,5},{5,4},{6,7},{7,6},{8,9},{9,8},{10,11... | collective-permute-start | bytes 9224 | tf_op jit(solution)/shard_map/ppermute | solution.py:22
  54.8 3.4 %collective-permute-start.5 = (f32[768]{0:T(1024)S(1)}, f32[768]{0:T(1024)S(1)}, u32[]{:S(2)}, u32[]{:S(2)}) collective-permute-start(f32[768]{0:T(1024)S(1)} %fusion.137), channel_id=1, source_target_pairs={{0,2},{1,3},{2,0},{3,1},{4,6},{5,7},{6,4},{7,5},{8,10},{9,11},{10,... | collective-permute-start | bytes 9224 | tf_op jit(solution)/shard_map/ppermute | solution.py:22
  58.3 4.3 %collective-permute-start.6 = (f32[768]{0:T(1024)S(1)}, f32[768]{0:T(1024)S(1)}, u32[]{:S(2)}, u32[]{:S(2)}) collective-permute-start(f32[768]{0:T(1024)S(1)} %add.862), channel_id=1, source_target_pairs={{0,4},{4,0},{8,12},{12,8},{1,5},{5,1},{9,13},{13,9},{2,6},{6,2},{1... | collective-permute-start | bytes 9224 | tf_op jit(solution)/shard_map/ppermute | solution.py:22
  62.5 2.5 %collective-permute-start.7 = (f32[768]{0:T(1024)S(1)}, f32[768]{0:T(1024)S(1)}, u32[]{:S(2)}, u32[]{:S(2)}) collective-permute-start(f32[768]{0:T(1024)S(1)} %add.863), channel_id=1, source_target_pairs={{0,8},{4,12},{8,0},{12,4},{1,9},{5,13},{9,1},{13,5},{2,10},{6,14},... | collective-permute-start | bytes 9224 | tf_op jit(solution)/shard_map/ppermute | solution.py:22
  68.7 9.0 %collective-permute-start.11 = (f32[32,1,128]{2,1,0:T(1,128)S(1)}, f32[32,1,128]{2,1,0:T(1,128)S(1)}, u32[]{:S(2)}, u32[]{:S(2)}) collective-permute-start(f32[32,1,128]{2,1,0:T(1,128)S(1)} %get-tuple-element.29), channel_id=1, source_target_pairs={{0,1},{1,2},{2,3},{3,0},{4,5},{5,6},{6,7},{7,4},{8,9},{9,10},{10,1... | collective-permute-start | bytes 49160 | tf_op jit(solution)/shard_map/ppermute | solution.py:42
  68.7 9.0 %collective-permute-start.10 = (f32[32,1,128]{2,1,0:T(1,128)S(1)}, f32[32,1,128]{2,1,0:T(1,128)S(1)}, u32[]{:S(2)}, u32[]{:S(2)}) collective-permute-start(f32[32,1,128]{2,1,0:T(1,128)S(1)} %get-tuple-element.28), channel_id=1, source_target_pairs={{1,0},{2,1},{3,2},{0,3},{5,4},{6,5},{7,6},{4,7},{9,8},{10,9},{11,1... | collective-permute-start | bytes 49160 | tf_op jit(solution)/shard_map/ppermute | solution.py:44
  71.9 5.7 %collective-permute-start.9 = (f32[1,64,128]{2,1,0:T(8,128)S(1)}, f32[1,64,128]{2,1,0:T(8,128)S(1)}, u32[]{:S(2)}, u32[]{:S(2)}) collective-permute-start(f32[1,64,128]{2,1,0:T(8,128)S(1)} %get-tuple-element.27), channel_id=1, source_target_pairs={{0,4},{4,8},{8,12},{1,5},{5,9},{9,13},{2,6},{6,10},{10,14},{3,7},{... | collective-permute-start | bytes 98312 | tf_op jit(solution)/shard_map/ppermute | solution.py:42
  75.5 5.2 %collective-permute-start.8 = (f32[1,64,128]{2,1,0:T(8,128)S(1)}, f32[1,64,128]{2,1,0:T(8,128)S(1)}, u32[]{:S(2)}, u32[]{:S(2)}) collective-permute-start(f32[1,64,128]{2,1,0:T(8,128)S(1)} %get-tuple-element.26), channel_id=1, source_target_pairs={{4,0},{8,4},{12,8},{5,1},{9,5},{13,9},{6,2},{10,6},{14,10},{7,3},{... | collective-permute-start | bytes 98312 | tf_op jit(solution)/shard_map/ppermute | solution.py:44

commit v6 on v5

--- a/solution.py
+++ b/solution.py
@@ -221,8 +221,18 @@
         lat_count * CAP, 64, value_count
     )
     pick_index = my_dev * CAP + my_slot
-    patches = jnp.where(my_remote[:, None, None], arrived[pick_index], own_patches[my_local])
-    return patches, my_frac
+    slot_owner = (pick_index[None, :] == jnp.arange(lat_count * CAP)[:, None]) & my_remote[None, :]
+    slot_frac = jnp.sum(jnp.where(slot_owner[None], my_frac[:, None, :], 0.0), axis=2)
+    return own_patches[my_local], my_frac, arrived, slot_frac, pick_index, my_remote
+
+
+def gathered_spatial(state_field, source_ids, shifts_now):
+    near, frac, arrived, slot_frac, pick_index, remote = departed(
+        state_field, source_ids, shifts_now
+    )
+    near_done = spatial(near, frac[0], frac[1])
+    arrived_done = spatial(arrived, slot_frac[0], slot_frac[1])
+    return near_done, frac, arrived_done, slot_frac, pick_index, remote
 
 
 def local(tracers, shifts, diffusivity, source_patch):
@@ -237,13 +247,22 @@
     weights = column_area(lat_index * row_count, row_count, total_rows)
     target_part = column_mass(tracers, weights)
 
-    patches, frac = departed(tracers, source_patch[0], shifts[0])
-    advected = from_patches(levels(spatial(patches, frac[0], frac[1]), frac[2]), band_rows, band_cols)
+    near, frac, arrived, slot_frac, pick_index, remote = gathered_spatial(
+        tracers, source_patch[0], shifts[0]
+    )
+    finished = jnp.where(
+        remote[:, None, None],
+        levels(arrived, slot_frac[2])[pick_index],
+        levels(near, frac[2]),
+    )
+    advected = from_patches(finished, band_rows, band_cols)
     first, k_wide = diffuse_first(advected, diffusivity)
     first_part = column_mass(first, weights)
 
-    patches, frac = departed(first, source_patch[1], shifts[1])
-    planar = spatial(patches, frac[0], frac[1])
+    near, frac, arrived, _, pick_index, remote = gathered_spatial(
+        first, source_patch[1], shifts[1]
+    )
+    planar = jnp.where(remote[:, None, None], arrived[pick_index], near)
     weight_z = cubic_matrix(frac[2], LEV)
 
     area_wide = column_area(lat_index * row_count - 1, row_count + 2, total_rows)

time: 82.7 us -> 87.5 us (1.058)
  other arithmetic: 12.3 us -> 17.6 us
  waiting for transfers between devices: 21.1 us -> 16.3 us
  matrix products: 4.93 us -> 6.85 us
  local copies, waits for them, and re-layouts: 12.9 us -> 14.6 us
    all_to_all x2, waiting for transfers between devices: 6.95 us -> 2.16 us  [departed(): lax.all_to_all(outgoing, 'lat', 0, 0, tiled=True)]
    transpose x0 -> x1, other arithmetic: none -> 2.77 us  [from_patches(): return patches.reshape(band_rows, band_cols, 8, 8, -1).transpose(0, 2, 1,...]
    add x4 -> x6, other arithmetic: 4.85 us -> 7.41 us  [levels(): acc = term if acc is None else acc + term]
    dot_general x2 -> x4, matrix products: 3.79 us -> 5.71 us  [spatial(): jnp.einsum('nij,njv->niv', plane_weights(fraction_y, fraction_x), patches...]
    gather x2, local copies, waits for them, and re-layouts: 1.23 us -> 2.2 us  [the longest x1 1.58 us: local(): levels(arrived, slot_frac[2])[pick_index]]
  transfers between devices with their start and end apart: 14 -> 14, of which waited for: 8 -> 7; matrix products, arithmetic and copies ran while one was open for 10% -> 16% of each run, Pallas kernels for 0% -> 0%
where the time goes in v6:
time: 87.5 us; the launch traced here: 87 us
  starting transfers between devices  30.9 us (35%)
  other arithmetic  17.6 us (20%)
  waiting for transfers between devices  16.3 us (19%)
  local copies, waits for them, and re-layouts  14.6 us (17%)
  matrix products  6.85 us (8%)
    ppermute x4, waiting for transfers between devices, all_sum(): lax.ppermute(value, axis, [(i, i ^ distance) for i in range(count)])  8.4 us
    all_to_all x2, starting transfers between devices, departed(): lax.all_to_all(outgoing, 'lat', 0, 0, tiled=True)  8.04 us
    add x6, other arithmetic, levels(): acc = term if acc is None else acc + term  7.41 us
    ppermute x3, starting transfers between devices, extended(): lax.ppermute(head, axis, [((i + 1) % count, i) for i in range(ends)])  7.27 us
    dot_general x4, matrix products, spatial(): jnp.einsum('nij,njv->niv', plane_weights(fraction_y, fraction_x), patches...  5.71 us
    ppermute x3, starting transfers between devices, extended(): lax.ppermute(tail, axis, [(i, (i + 1) % count) for i in range(ends)])  5.59 us
    ppermute x4, starting transfers between devices, all_sum(): lax.ppermute(value, axis, [(i, i ^ distance) for i in range(count)])  4.22 us
    ppermute x1, starting transfers between devices, diffuse_first(): lax.ppermute(pack(advected[rows - 1:], diffusivity[rows - 1]), 'lat', [(i...  3.82 us
  transfers between devices with their start and end apart: 14, of which 7 were waited for; matrix products, arithmetic and copies ran while one was open for 16% of the time, Pallas kernels for 0%

profile of v6, /device:TPU:1, one launch (start us, length us, event | category | flops | bytes accessed | tf_op | source)
XLA Modules:
  0.0 87.0 jit_solution(10462386396171478338)
XLA Ops:
  0.0 1.4 %copy.20 = f32[4,8,8,8,128]{4,3,2,1,0:T(8,128)S(1)} copy(f32[4,8,8,8,128]{4,3,1,2,0:T(8,128)} %bitcast.382) | data formatting | bytes 2097152 | tf_op jit(solution)/shard_map/transpose | solution.py:116
  2.4 1.4 %gather_fusion = f32[16,64,128]{2,1,0:T(8,128)} fusion(f32[32,64,128]{2,1,0:T(8,128)S(1)} %bitcast.366, s32[1024]{0:T(1024)S(1)} %pad_clamp_fusion.5), kind=kCustom, calls=%fused_computation | custom fusion | bytes 1048640 | tf_op jit(solution)/shard_map/gather | solution.py:214
  3.8 4.4 %all-to-all-start = ((f32[4,4,64,128]{3,2,1,0:T(8,128)}), f32[4,4,64,128]{3,2,1,0:T(8,128)S(1)}, u32[]{:S(2)}, u32[]{:S(2)}) async-start(f32[4,4,64,128]{3,2,1,0:T(8,128)} %bitcast.16), calls=%async_computation | async-start | bytes 1048576 | tf_op jit(solution)/shard_map/all_to_all | solution.py:220
  12.4 1.8 %fusion.29 = f32[32,64,128]{2,1,0:T(8,128)S(1)} fusion(f32[32,64,128]{2,1,0:T(8,128)S(1)} %gather_fusion.2, f32[64,64]{1,0:T(8,128)S(1)} %get-tuple-element.121, f32[32]{0:T(128)S(1)} %get-tuple-element.147, f32[64,64]{1,0:T(8,128)S(1)} %get-tuple-element.122, f32[32]{0:T(128)S(1)} %get-tuple-element.148, f32[64,64]{1,0:T(8,128)S(1)} %get-tuple-element.123, ...), kind=kOutput, calls=%fused_computation.57 | convolution fusion | flops 203292672 | bytes 2229248 | tf_op jit(solution)/shard_map/nij,njv->niv/dot_general | solution.py:88
  14.2 1.1 %multiply_add_fusion.6 = f32[32,64,32]{2,1,0:T(8,128)S(1)} fusion(f32[32,64,128]{2,1,0:T(8,128)S(1)} %fusion.29, f32[32]{0:T(128)S(1)} %get-tuple-element.70, f32[32]{0:T(128)S(1)} %get-tuple-element.71, f32[32]{0:T(128)S(1)} %get-tuple-element.72, f32[32]{0:T(128)S(1)} %get-tuple-element.73), kind=kLoop, calls=%fused_computation.55 | loop fusion | flops 458752 | bytes 1311232 | tf_op jit(solution)/shard_map/add | solution.py:106
  15.4 2.7 %multiply_add_fusion.7 = (f32[32,64,32]{2,1,0:T(8,128)S(1)}, f32[32,64,32]{2,1,0:T(8,128)}, f32[32,64,32]{2,1,0:T(8,128)}) fusion(f32[32,64,128]{2,1,0:T(8,128)S(1)} %fusion.29, f32[32]{0:T(128)S(1)} %get-tuple-element.74, f32[32]{0:T(128)S(1)} %get-tuple-element.75, f32[32]{0:T(128)S(1)} %get-tuple-element.64, f32[32]{0:T(128)S(1)} %get-tuple-element.67, ...), kind=kLoop, calls=%fused_computation.56 | loop fusion | flops 851968 | bytes 1836032 | tf_op jit(solution)/shard_map/add | solution.py:106
  18.0 1.0 %fusion.77 = f32[16,64,128]{2,1,0:T(8,128)S(1)} fusion(f32[16,64,128]{2,1,0:T(8,128)S(1)} %bitcast.384, f32[16]{0:T(128)S(1)} %get-tuple-element.111, f32[16]{0:T(128)S(1)} %get-tuple-element.112, f32[16]{0:T(128)S(1)} %get-tuple-element.113, f32[16]{0:T(128)S(1)} %get-tuple-element.114, f32[16]{0:T(128)S(1)} %get-tuple-element.108, ...), kind=kOutput, calls=%fused_computation.111 | convolution fusion | flops 101646336 | bytes 1180160 | tf_op jit(solution)/shard_map/nij,njv->niv/dot_general | solution.py:88
  20.8 1.6 %gather_fusion.1 = f32[32,64,128]{2,1,0:T(8,128)} fusion(f32[16,64,128]{2,1,0:T(8,128)S(1)} %pad_maximum_fusion.9, s32[1024]{0:T(1024)S(1)} %pad_clamp_fusion.4), kind=kCustom, calls=%fused_computation.1 | custom fusion | bytes 2097280 | tf_op jit(solution)/shard_map/gather | solution.py:255
  22.3 2.8 %fusion.13 = f32[4,8,8,8,128]{4,3,1,2,0:T(8,128)S(1)} fusion(f32[4,8,8,8,128]{4,3,2,1,0:T(8,128)} %bitcast.380, f32[4,8,8,8,32]{4,3,2,1,0:T(8,128)} %bitcast.379, f32[4,8,8,8,32]{4,3,2,1,0:T(8,128)} %bitcast.378, f32[4,8,8,8,32]{4,3,2,1,0:T(8,128)S(1)} %bitcast.376, f32[4,8,8,8,32]{4,3,2,1,0:T(8,128)S(1)} %bitcast.377, pred[4,8]{1,0:T(4,128)(4,1)S(1)} %broadcast_in_dim.79), kind=kLoop, calls=%fused_computation.30 | loop fusion | flops 1048576 | bytes 3145760 | tf_op jit(solution)/shard_map/transpose | solution.py:124
  25.3 2.0 %collective-permute-start.3 = (f32[32,1,128]{2,1,0:T(1,128)S(1)}, f32[32,1,128]{2,1,0:T(1,128)S(1)}, u32[]{:S(2)}, u32[]{:S(2)}) collective-permute-start(f32[32,1,128]{2,1,0:T(1,128)S(1)} %get-tuple-element.39), channel_id=1, source_target_pairs={{0,1},{1,2},{2,3},{3,0},{4,5},{5,6},{6,7},{7,4},{8,9},{9,10},{10,1... | collective-permute-start | bytes 49160 | tf_op jit(solution)/shard_map/ppermute | solution.py:42
  27.3 2.1 %collective-permute-start.2 = (f32[32,1,128]{2,1,0:T(1,128)S(1)}, f32[32,1,128]{2,1,0:T(1,128)S(1)}, u32[]{:S(2)}, u32[]{:S(2)}) collective-permute-start(f32[32,1,128]{2,1,0:T(1,128)S(1)} %get-tuple-element.38), channel_id=1, source_target_pairs={{1,0},{2,1},{3,2},{0,3},{5,4},{6,5},{7,6},{4,7},{9,8},{10,9},{11,1... | collective-permute-start | bytes 49160 | tf_op jit(solution)/shard_map/ppermute | solution.py:44
  30.1 3.8 %collective-permute-start.1 = (f32[1,65,128]{2,1,0:T(8,128)S(1)}, f32[1,65,128]{2,1,0:T(8,128)S(1)}, u32[]{:S(2)}, u32[]{:S(2)}) collective-permute-start(f32[1,65,128]{2,1,0:T(8,128)S(1)} %concatenate.66), channel_id=1, source_target_pairs={{0,4},{4,8},{8,12},{1,5},{5,9},{9,13},{2,6},{6,10},{10,14},{3,7},{... | collective-permute-start | bytes 99848 | tf_op jit(solution)/shard_map/ppermute | solution.py:167
  34.5 1.9 %collective-permute-start = (f32[1,65,128]{2,1,0:T(8,128)S(1)}, f32[1,65,128]{2,1,0:T(8,128)S(1)}, u32[]{:S(2)}, u32[]{:S(2)}) collective-permute-start(f32[1,65,128]{2,1,0:T(8,128)S(1)} %concatenate.64), channel_id=1, source_target_pairs={{4,0},{8,4},{12,8},{5,1},{9,5},{13,9},{6,2},{10,6},{14,10},{7,3},{... | collective-permute-start | bytes 99848 | tf_op jit(solution)/shard_map/ppermute | solution.py:172
  37.1 2.7 %collective-permute-done = f32[1,65,128]{2,1,0:T(8,128)S(1)} collective-permute-done((f32[1,65,128]{2,1,0:T(8,128)S(1)}, f32[1,65,128]{2,1,0:T(8,128)S(1)}, u32[]{:S(2)}, u32[]{:S(2)}) %collective-permute-start) | collective-permute-done | bytes 33312 | tf_op jit(solution)/shard_map/ppermute | solution.py:172
  41.4 1.4 %gather_fusion.3 = f32[16,64,128]{2,1,0:T(8,128)} fusion(f32[32,64,128]{2,1,0:T(8,128)S(1)} %bitcast.368, s32[1024]{0:T(1024)S(1)} %pad_clamp_fusion.2), kind=kCustom, calls=%fused_computation.3 | custom fusion | bytes 1048640 | tf_op jit(solution)/shard_map/gather | solution.py:214
  42.8 3.6 %all-to-all-start.1 = ((f32[4,4,64,128]{3,2,1,0:T(8,128)}), f32[4,4,64,128]{3,2,1,0:T(8,128)S(1)}, u32[]{:S(2)}, u32[]{:S(2)}) async-start(f32[4,4,64,128]{3,2,1,0:T(8,128)} %bitcast.61), calls=%async_computation.1 | async-start | bytes 1048576 | tf_op jit(solution)/shard_map/all_to_all | solution.py:220
  48.2 1.4 %maximum_multiply_fusion = f32[34]{0:T(128)S(1)} fusion(f32[1]{0:T(128)} %bitcast.70, f32[32]{0:T(128)S(1)} %copy-done.5, f32[1]{0:T(128)} %bitcast.69, s32[]{:T(128)S(6)} %sub.274), kind=kLoop, calls=%fused_computation.377 | loop fusion | flops 272 | bytes 276 | tf_op jit(solution)/shard_map/mul | solution.py:269
  50.1 2.2 %all-to-all-done.1 = f32[4,4,64,128]{3,2,1,0:T(8,128)S(1)} async-done(((f32[4,4,64,128]{3,2,1,0:T(8,128)}), f32[4,4,64,128]{3,2,1,0:T(8,128)S(1)}, u32[]{:S(2)}, u32[]{:S(2)}) %all-to-all-start.1) | async-done | bytes 524320 | tf_op jit(solution)/shard_map/all_to_all | solution.py:220
  52.3 1.0 %fusion.93 = f32[16,64,128]{2,1,0:T(8,128)S(1)} fusion(f32[16,64,128]{2,1,0:T(8,128)S(1)} %bitcast.385, f32[64,64]{1,0:T(8,128)S(1)} %get-tuple-element.121, f32[16]{0:T(128)S(1)} %get-tuple-element.100, f32[64,64]{1,0:T(8,128)S(1)} %get-tuple-element.122, f32[16]{0:T(128)S(1)} %get-tuple-element.101, f32[64,64]{1,0:T(8,128)S(1)} %get-tuple-element.123, ...), kind=kOutput, calls=%fused_computation.127 | convolution fusion | flops 101646336 | bytes 1180160 | tf_op jit(solution)/shard_map/nij,njv->niv/dot_general | solution.py:88
  54.0 1.8 %convolution_select_fusion = f32[32,64,128]{2,1,0:T(8,128)S(1)} fusion(f32[32,64,128]{2,1,0:T(8,128)S(1)} %gather_fusion.4, f32[32,64,128]{2,1,0:T(8,128)S(1)} %gather_fusion.5, f32[32]{0:T(128)S(1)} %get-tuple-element.134, f32[32]{0:T(128)S(1)} %get-tuple-element.135, f32[32]{0:T(128)S(1)} %get-tuple-element.133, f32[32]{0:T(128)S(1)} %get-tuple-element.88, ...), kind=kOutput, calls=%fused_computation.6 | convolution fusion | flops 203554816 | bytes 3277856 | tf_op jit(solution)/shard_map/nij,njv->niv/dot_general | solution.py:88
  55.8 1.0 %fusion.252 = f32[32,1,128]{2,1,0:T(1,128)S(1)} fusion(f32[32,64,1]{1,2,0:T(1,128)S(1)} %bitcast.386, f32[32,64,128]{2,1,0:T(8,128)S(1)} %convolution_select_fusion), kind=kOutput, calls=%fused_computation.504 | convolution fusion | flops 3145728 | bytes 1073152 | tf_op jit(solution)/shard_map/pi,piv->pv/dot_general | solution.py:272
  57.2 2.4 %collective-permute-done.4 = f32[768]{0:T(1024)S(1)} collective-permute-done((f32[768]{0:T(1024)S(1)}, f32[768]{0:T(1024)S(1)}, u32[]{:S(2)}, u32[]{:S(2)}) %collective-permute-start.4) | collective-permute-done | bytes 3104 | tf_op jit(solution)/shard_map/ppermute | solution.py:22
  60.4 2.7 %collective-permute-done.5 = f32[768]{0:T(1024)S(1)} collective-permute-done((f32[768]{0:T(1024)S(1)}, f32[768]{0:T(1024)S(1)}, u32[]{:S(2)}, u32[]{:S(2)}) %collective-permute-start.5) | collective-permute-done | bytes 3104 | tf_op jit(solution)/shard_map/ppermute | solution.py:22
  63.1 3.4 %collective-permute-start.6 = (f32[768]{0:T(1024)S(1)}, f32[768]{0:T(1024)S(1)}, u32[]{:S(2)}, u32[]{:S(2)}) collective-permute-start(f32[768]{0:T(1024)S(1)} %add.1221), channel_id=1, source_target_pairs={{0,4},{4,0},{8,12},{12,8},{1,5},{5,1},{9,13},{13,9},{2,6},{6,2},{1... | collective-permute-start | bytes 9224 | tf_op jit(solution)/shard_map/ppermute | solution.py:22
  67.4 2.4 %collective-permute-done.7 = f32[768]{0:T(1024)S(1)} collective-permute-done((f32[768]{0:T(1024)S(1)}, f32[768]{0:T(1024)S(1)}, u32[]{:S(2)}, u32[]{:S(2)}) %collective-permute-start.7) | collective-permute-done | bytes 3104 | tf_op jit(solution)/shard_map/ppermute | solution.py:22
  69.9 1.1 %multiply_add_fusion.2 = f32[32,64,32]{2,1,0:T(8,128)S(1)} fusion(f32[32,64,128]{2,1,0:T(8,128)S(1)} %broadcast_multiply_fusion, f32[32]{0:T(128)S(1)} %get-tuple-element.56, f32[32]{0:T(128)S(1)} %get-tuple-element.57, f32[32]{0:T(128)S(1)} %get-tuple-element.58, f32[32]{0:T(128)S(1)} %get-tuple-element.59), kind=kLoop, calls=%fused_computation.34 | loop fusion | flops 458752 | bytes 1311232 | tf_op jit(solution)/shard_map/add | solution.py:106
  71.1 1.3 %multiply_add_fusion.3 = (f32[32,64,32]{2,1,0:T(8,128)S(1)}, f32[32,64,32]{2,1,0:T(8,128)S(1)}, f32[32,64,32]{2,1,0:T(8,128)S(1)}) fusion(f32[32,64,128]{2,1,0:T(8,128)S(1)} %broadcast_multiply_fusion, f32[32]{0:T(128)S(1)} %get-tuple-element.60, f32[32]{0:T(128)S(1)} %get-tuple-element.61, f32[32]{0:T(128)S(1)} %get-tuple-element.50, ...), kind=kLoop, calls=%fused_computation.35 | loop fusion | flops 851968 | bytes 1836032 | tf_op jit(solution)/shard_map/add | solution.py:106
  73.5 3.3 %collective-permute-start.10 = (f32[32,1,128]{2,1,0:T(1,128)S(1)}, f32[32,1,128]{2,1,0:T(1,128)S(1)}, u32[]{:S(2)}, u32[]{:S(2)}) collective-permute-start(f32[32,1,128]{2,1,0:T(1,128)S(1)} %get-tuple-element.31), channel_id=1, source_target_pairs={{1,0},{2,1},{3,2},{0,3},{5,4},{6,5},{7,6},{4,7},{9,8},{10,9},{11,1... | collective-permute-start | bytes 49160 | tf_op jit(solution)/shard_map/ppermute | solution.py:44
  76.8 3.6 %collective-permute-start.9 = (f32[1,64,128]{2,1,0:T(8,128)S(1)}, f32[1,64,128]{2,1,0:T(8,128)S(1)}, u32[]{:S(2)}, u32[]{:S(2)}) collective-permute-start(f32[1,64,128]{2,1,0:T(8,128)S(1)} %get-tuple-element.30), channel_id=1, source_target_pairs={{0,4},{4,8},{8,12},{1,5},{5,9},{9,13},{2,6},{6,10},{10,14},{3,7},{... | collective-permute-start | bytes 98312 | tf_op jit(solution)/shard_map/ppermute | solution.py:42
  80.3 1.9 %collective-permute-start.8 = (f32[1,64,128]{2,1,0:T(8,128)S(1)}, f32[1,64,128]{2,1,0:T(8,128)S(1)}, u32[]{:S(2)}, u32[]{:S(2)}) collective-permute-start(f32[1,64,128]{2,1,0:T(8,128)S(1)} %get-tuple-element.29), channel_id=1, source_target_pairs={{4,0},{8,4},{12,8},{5,1},{9,5},{13,9},{6,2},{10,6},{14,10},{7,3},{... | collective-permute-start | bytes 98312 | tf_op jit(solution)/shard_map/ppermute | solution.py:44
  82.5 3.1 %collective-permute-done.8 = f32[1,64,128]{2,1,0:T(8,128)S(1)} collective-permute-done((f32[1,64,128]{2,1,0:T(8,128)S(1)}, f32[1,64,128]{2,1,0:T(8,128)S(1)}, u32[]{:S(2)}, u32[]{:S(2)}) %collective-permute-start.8) | collective-permute-done | bytes 32800 | tf_op jit(solution)/shard_map/ppermute | solution.py:44
  85.6 1.4 %fusion.4 = f32[32,64,128]{2,1,0:T(8,128)} fusion(f32[32,64,128]{2,1,0:T(8,128)S(1)} %bitcast.372, f32[32,1,128]{2,1,0:T(1,128)S(1)} %collective-permute-done.11, f32[32,1,128]{2,1,0:T(1,128)S(1)} %collective-permute-done.10, f32[1,64,128]{2,1,0:T(8,128)S(1)} %collective-permute-done.9, f32[1,64,128]{2,1,0:T(8,128)S(1)} %collective-permute-done.8, ...), kind=kLoop, calls=%fused_computation.13 | loop fusion | flops 3145728 | bytes 2196096 | tf_op jit(solution)/shard_map/mul | solution.py:292
  (143 shorter events, 16.6 us)
Async XLA Ops:
  0.0 1.4 %copy-start.4 = (s32[2,16,32]{2,1,0:T(8,128)S(1)}, s32[2,16,32]{2,1,0:T(8,128)}, u32[]{:S(2)}) copy-start(s32[2,16,32]{2,1,0:T(8,128)} %param.7) | copy-start | bytes 12292
  3.8 4.5 %copy-start.3 = (f32[2,3,16,32]{3,2,1,0:T(8,128)S(1)}, f32[2,3,16,32]{3,2,1,0:T(8,128)}, u32[]{:S(2)}) copy-start(f32[2,3,16,32]{3,2,1,0:T(8,128)} %param.5) | copy-start | bytes 36868
  3.8 14.2 %all-to-all-start = ((f32[4,4,64,128]{3,2,1,0:T(8,128)}), f32[4,4,64,128]{3,2,1,0:T(8,128)S(1)}, u32[]{:S(2)}, u32[]{:S(2)}) async-start(f32[4,4,64,128]{3,2,1,0:T(8,128)} %bitcast.16), calls=%async_computation | async-start | bytes 1048576 | tf_op jit(solution)/shard_map/all_to_all | solution.py:220
  10.0 0.7 copy-start.5
  25.1 14.7 %copy-start = (f32[32,64,128]{2,1,0:T(8,128)S(1)}, f32[32,64,128]{2,1,0:T(8,128)}, u32[]{:S(2)}) copy-start(f32[32,64,128]{2,1,0:T(8,128)} %param.4) | copy-start | bytes 3145732
  25.3 14.5 %collective-permute-start.3 = (f32[32,1,128]{2,1,0:T(1,128)S(1)}, f32[32,1,128]{2,1,0:T(1,128)S(1)}, u32[]{:S(2)}, u32[]{:S(2)}) collective-permute-start(f32[32,1,128]{2,1,0:T(1,128)S(1)} %get-tuple-element.39), channel_id=1, source_target_pairs={{0,1},{1,2},{2,3},{3,0},{4,5},{5,6},{6,7},{7,4},{8,9},{9,10},{10,1... | collective-permute-start | bytes 49160 | tf_op jit(solution)/shard_map/ppermute | solution.py:42
  27.3 12.5 %collective-permute-start.2 = (f32[32,1,128]{2,1,0:T(1,128)S(1)}, f32[32,1,128]{2,1,0:T(1,128)S(1)}, u32[]{:S(2)}, u32[]{:S(2)}) collective-permute-start(f32[32,1,128]{2,1,0:T(1,128)S(1)} %get-tuple-element.38), channel_id=1, source_target_pairs={{1,0},{2,1},{3,2},{0,3},{5,4},{6,5},{7,6},{4,7},{9,8},{10,9},{11,1... | collective-permute-start | bytes 49160 | tf_op jit(solution)/shard_map/ppermute | solution.py:44
  30.1 6.4 %collective-permute-start.1 = (f32[1,65,128]{2,1,0:T(8,128)S(1)}, f32[1,65,128]{2,1,0:T(8,128)S(1)}, u32[]{:S(2)}, u32[]{:S(2)}) collective-permute-start(f32[1,65,128]{2,1,0:T(8,128)S(1)} %concatenate.66), channel_id=1, source_target_pairs={{0,4},{4,8},{8,12},{1,5},{5,9},{9,13},{2,6},{6,10},{10,14},{3,7},{... | collective-permute-start | bytes 99848 | tf_op jit(solution)/shard_map/ppermute | solution.py:167
  34.5 5.3 %collective-permute-start = (f32[1,65,128]{2,1,0:T(8,128)S(1)}, f32[1,65,128]{2,1,0:T(8,128)S(1)}, u32[]{:S(2)}, u32[]{:S(2)}) collective-permute-start(f32[1,65,128]{2,1,0:T(8,128)S(1)} %concatenate.64), channel_id=1, source_target_pairs={{4,0},{8,4},{12,8},{5,1},{9,5},{13,9},{6,2},{10,6},{14,10},{7,3},{... | collective-permute-start | bytes 99848 | tf_op jit(solution)/shard_map/ppermute | solution.py:172
  36.5 0.6 copy-start.1
  39.8 0.8 slice-start
  42.8 9.5 %all-to-all-start.1 = ((f32[4,4,64,128]{3,2,1,0:T(8,128)}), f32[4,4,64,128]{3,2,1,0:T(8,128)S(1)}, u32[]{:S(2)}, u32[]{:S(2)}) async-start(f32[4,4,64,128]{3,2,1,0:T(8,128)} %bitcast.61), calls=%async_computation.1 | async-start | bytes 1048576 | tf_op jit(solution)/shard_map/all_to_all | solution.py:220
  46.5 1.2 %copy-start.2 = (f32[1,65,128]{2,1,0:T(8,128)S(1)}, f32[1,65,128]{2,1,0:T(8,128)}, u32[]{:S(2)}) copy-start(f32[1,65,128]{2,1,0:T(8,128)} %copy-done.1) | copy-start | bytes 99844
  57.1 2.5 %collective-permute-start.4 = (f32[768]{0:T(1024)S(1)}, f32[768]{0:T(1024)S(1)}, u32[]{:S(2)}, u32[]{:S(2)}) collective-permute-start(f32[768]{0:T(1024)S(1)} %pad_maximum_fusion.10), channel_id=1, source_target_pairs={{0,1},{1,0},{2,3},{3,2},{4,5},{5,4},{6,7},{7,6},{8,9},{9,8},{10,11... | collective-permute-start | bytes 9224 | tf_op jit(solution)/shard_map/ppermute | solution.py:22
  59.7 3.4 %collective-permute-start.5 = (f32[768]{0:T(1024)S(1)}, f32[768]{0:T(1024)S(1)}, u32[]{:S(2)}, u32[]{:S(2)}) collective-permute-start(f32[768]{0:T(1024)S(1)} %fusion.235), channel_id=1, source_target_pairs={{0,2},{1,3},{2,0},{3,1},{4,6},{5,7},{6,4},{7,5},{8,10},{9,11},{10,... | collective-permute-start | bytes 9224 | tf_op jit(solution)/shard_map/ppermute | solution.py:22
  63.1 4.3 %collective-permute-start.6 = (f32[768]{0:T(1024)S(1)}, f32[768]{0:T(1024)S(1)}, u32[]{:S(2)}, u32[]{:S(2)}) collective-permute-start(f32[768]{0:T(1024)S(1)} %add.1221), channel_id=1, source_target_pairs={{0,4},{4,0},{8,12},{12,8},{1,5},{5,1},{9,13},{13,9},{2,6},{6,2},{1... | collective-permute-start | bytes 9224 | tf_op jit(solution)/shard_map/ppermute | solution.py:22
  67.3 2.5 %collective-permute-start.7 = (f32[768]{0:T(1024)S(1)}, f32[768]{0:T(1024)S(1)}, u32[]{:S(2)}, u32[]{:S(2)}) collective-permute-start(f32[768]{0:T(1024)S(1)} %add.1222), channel_id=1, source_target_pairs={{0,8},{4,12},{8,0},{12,4},{1,9},{5,13},{9,1},{13,5},{2,10},{6,14},... | collective-permute-start | bytes 9224 | tf_op jit(solution)/shard_map/ppermute | solution.py:22
  73.5 9.0 %collective-permute-start.11 = (f32[32,1,128]{2,1,0:T(1,128)S(1)}, f32[32,1,128]{2,1,0:T(1,128)S(1)}, u32[]{:S(2)}, u32[]{:S(2)}) collective-permute-start(f32[32,1,128]{2,1,0:T(1,128)S(1)} %get-tuple-element.32), channel_id=1, source_target_pairs={{0,1},{1,2},{2,3},{3,0},{4,5},{5,6},{6,7},{7,4},{8,9},{9,10},{10,1... | collective-permute-start | bytes 49160 | tf_op jit(solution)/shard_map/ppermute | solution.py:42
  73.5 9.0 %collective-permute-start.10 = (f32[32,1,128]{2,1,0:T(1,128)S(1)}, f32[32,1,128]{2,1,0:T(1,128)S(1)}, u32[]{:S(2)}, u32[]{:S(2)}) collective-permute-start(f32[32,1,128]{2,1,0:T(1,128)S(1)} %get-tuple-element.31), channel_id=1, source_target_pairs={{1,0},{2,1},{3,2},{0,3},{5,4},{6,5},{7,6},{4,7},{9,8},{10,9},{11,1... | collective-permute-start | bytes 49160 | tf_op jit(solution)/shard_map/ppermute | solution.py:44
  76.8 5.7 %collective-permute-start.9 = (f32[1,64,128]{2,1,0:T(8,128)S(1)}, f32[1,64,128]{2,1,0:T(8,128)S(1)}, u32[]{:S(2)}, u32[]{:S(2)}) collective-permute-start(f32[1,64,128]{2,1,0:T(8,128)S(1)} %get-tuple-element.30), channel_id=1, source_target_pairs={{0,4},{4,8},{8,12},{1,5},{5,9},{9,13},{2,6},{6,10},{10,14},{3,7},{... | collective-permute-start | bytes 98312 | tf_op jit(solution)/shard_map/ppermute | solution.py:42
  80.3 5.2 %collective-permute-start.8 = (f32[1,64,128]{2,1,0:T(8,128)S(1)}, f32[1,64,128]{2,1,0:T(8,128)S(1)}, u32[]{:S(2)}, u32[]{:S(2)}) collective-permute-start(f32[1,64,128]{2,1,0:T(8,128)S(1)} %get-tuple-element.29), channel_id=1, source_target_pairs={{4,0},{8,4},{12,8},{5,1},{9,5},{13,9},{6,2},{10,6},{14,10},{7,3},{... | collective-permute-start | bytes 98312 | tf_op jit(solution)/shard_map/ppermute | solution.py:44

commit v7 on v5

--- a/solution.py
+++ b/solution.py
@@ -153,6 +153,35 @@
     k_shape = [1] * advected.ndim
     k_shape[row_dim] = rows
     return advected + diffusivity.reshape(k_shape) * laplace
+
+
+def levels_cols(values, weight_z):
+    value_count = values.shape[-1]
+    per_level = value_count // LEV
+    blocks = [values[..., m * per_level : (m + 1) * per_level] for m in range(LEV)]
+    out = []
+    for level in range(LEV):
+        acc = None
+        for m in tap_sources(level, LEV):
+            term = weight_z[..., level, m][..., None] * blocks[m]
+            acc = term if acc is None else acc + term
+        out.append(acc)
+    return jnp.concatenate(out, axis=-1)
+
+
+def halos(field):
+    lat_count = lax.axis_size("lat")
+    lon_count = lax.axis_size("lon")
+    rows, cols = field.shape[0], field.shape[1]
+    above = lax.ppermute(field[rows - 1 :], "lat", [(i, i + 1) for i in range(lat_count - 1)])
+    below = lax.ppermute(field[:1], "lat", [(i + 1, i) for i in range(lat_count - 1)])
+    left = lax.ppermute(
+        field[:, cols - 1 :], "lon", [(i, (i + 1) % lon_count) for i in range(lon_count)]
+    )
+    right = lax.ppermute(
+        field[:, :1], "lon", [((i + 1) % lon_count, i) for i in range(lon_count)]
+    )
+    return above, below, left, right
 
 
 def diffuse_first(advected, diffusivity):
@@ -256,6 +285,28 @@
     mix_part = jnp.einsum(
         "plm,pmt->lmt", weight_z, weighted, precision=lax.Precision.HIGHEST
     )
+    field_planar = from_patches(planar, band_rows, band_cols)
+    above, below, left, right = halos(field_planar)
+    lon_index = lax.axis_index("lon")
+    fraction_z = shifts[1, 2]
+    patch_rows, patch_cols = fraction_z.shape
+    first_row = lat_index * band_rows
+    first_col = lon_index * band_cols
+    tile_cols = (first_col + jnp.arange(band_cols)) % patch_cols
+    band_patch_rows = first_row + jnp.arange(band_rows)
+    row_above = jnp.clip(first_row - 1, 0, patch_rows - 1)
+    row_below = jnp.clip(first_row + band_rows, 0, patch_rows - 1)
+    col_left = (first_col - 1) % patch_cols
+    col_right = (first_col + band_cols) % patch_cols
+    cz_own = cubic_matrix(fraction_z[band_patch_rows][:, tile_cols], LEV)
+    cz_above = jnp.repeat(cubic_matrix(fraction_z[row_above, tile_cols], LEV), 8, axis=0)[None]
+    cz_below = jnp.repeat(cubic_matrix(fraction_z[row_below, tile_cols], LEV), 8, axis=0)[None]
+    cz_left = jnp.repeat(cubic_matrix(fraction_z[band_patch_rows, col_left], LEV), 8, axis=0)[
+        :, None
+    ]
+    cz_right = jnp.repeat(cubic_matrix(fraction_z[band_patch_rows, col_right], LEV), 8, axis=0)[
+        :, None
+    ]
     totals = all_sum(
         jnp.concatenate([target_part, first_part, mix_part.reshape(-1)]), ("lon", "lat")
     )
@@ -267,10 +318,19 @@
         value_count
     )
     second_ratio = target / second_mass
-    advected = from_patches(
-        levels(planar * first_ratio[None, None, :], frac[2]), band_rows, band_cols
-    )
-    return diffuse(advected, diffusivity, 0) * second_ratio[None, None, :]
+    mixed = levels_cols(
+        (field_planar * first_ratio).reshape(band_rows, 8, band_cols, 8, value_count),
+        cz_own[:, None, :, None],
+    ).reshape(row_count, col_count, value_count)
+    above = levels_cols(above * first_ratio, cz_above)
+    below = levels_cols(below * first_ratio, cz_below)
+    left = levels_cols(left * first_ratio, cz_left)
+    right = levels_cols(right * first_ratio, cz_right)
+    lat_wide = jnp.concatenate([above, mixed, below], axis=0)
+    lon_wide = jnp.concatenate([left, mixed, right], axis=1)
+    laplace = lat_wide[2:] + lat_wide[:-2] + lon_wide[:, 2:] + lon_wide[:, :-2] - 4.0 * mixed
+    second = mixed + diffusivity[:, None, None] * laplace
+    return second * second_ratio[None, None, :]
 
 
 def solution(mesh):

time: 82.7 us -> 93.9 us (1.14)
  local copies, waits for them, and re-layouts: 12.9 us -> 26.4 us
  waiting for transfers between devices: 21.1 us -> 12.3 us
  other arithmetic: 12.3 us -> 20 us
  starting transfers between devices: 30.3 us -> 28.4 us
    ppermute x0 -> x4, starting transfers between devices: none -> 7.22 us  [the longest x1 3.19 us: halos(): lax.ppermute(field[rows - 1:], 'lat', [(i, i + 1) for i in range(lat_coun...]
    ppermute x3 -> x1, starting transfers between devices: 5.78 us -> 0.01 us  [extended(): lax.ppermute(tail, axis, [(i, (i + 1) % count) for i in range(ends)])]
    add x0 -> x10, other arithmetic: none -> 5.32 us  [levels_cols(): acc = term if acc is None else acc + term]
    unnamed x12 -> x80, local copies, waits for them, and re-layouts: 0.65 us -> 4.48 us
    gather x0 -> x7, local copies, waits for them, and re-layouts: none -> 3.76 us  [the longest x3 1.21 us: local(): cz_own = cubic_matrix(fraction_z[band_patch_rows][:, tile_cols], LEV)]
    ppermute x3 -> x1, waiting for transfers between devices: 0.01 us -> 3.52 us  [extended(): lax.ppermute(tail, axis, [(i, (i + 1) % count) for i in range(ends)])]
    all_to_all x2, waiting for transfers between devices: 6.95 us -> 3.61 us  [departed(): lax.all_to_all(outgoing, 'lat', 0, 0, tiled=True)]
    ppermute x3 -> x1, starting transfers between devices: 7.27 us -> 3.97 us  [extended(): lax.ppermute(head, axis, [((i + 1) % count, i) for i in range(ends)])]
  transfers between devices with their start and end apart: 14 -> 14, of which waited for: 8 -> 5; matrix products, arithmetic and copies ran while one was open for 10% -> 26% of each run, Pallas kernels for 0% -> 0%
where the time goes in v7:
time: 93.9 us; the launch traced here: 93.2 us
  starting transfers between devices  28.4 us (30%)
  local copies, waits for them, and re-layouts  26.4 us (28%)
  other arithmetic  20 us (21%)
  waiting for transfers between devices  12.3 us (13%)
  matrix products  4.95 us (5%)
  between operations  1.15 us (1%)
    all_to_all x2, starting transfers between devices, departed(): lax.all_to_all(outgoing, 'lat', 0, 0, tiled=True)  8.07 us
    add x10, other arithmetic, levels_cols(): acc = term if acc is None else acc + term  5.32 us
    ppermute x4, waiting for transfers between devices, all_sum(): lax.ppermute(value, axis, [(i, i ^ distance) for i in range(count)])  5.19 us
    unnamed x80, local copies, waits for them, and re-layouts  4.48 us
    ppermute x1, starting transfers between devices, extended(): lax.ppermute(head, axis, [((i + 1) % count, i) for i in range(ends)])  3.97 us
    dot_general x2, matrix products, spatial(): jnp.einsum('nij,njv->niv', plane_weights(fraction_y, fraction_x), patches...  3.82 us
    ppermute x1, starting transfers between devices, diffuse_first(): lax.ppermute(pack(advected[rows - 1:], diffusivity[rows - 1]), 'lat', [(i...  3.73 us
    all_to_all x2, waiting for transfers between devices, departed(): lax.all_to_all(outgoing, 'lat', 0, 0, tiled=True)  3.61 us
  transfers between devices with their start and end apart: 14, of which 5 were waited for; matrix products, arithmetic and copies ran while one was open for 26% of the time, Pallas kernels for 0%

profile of v7, /device:TPU:1, one launch (start us, length us, event | category | flops | bytes accessed | tf_op | source)
XLA Modules:
  0.0 93.2 jit_solution(6642261705656983512)
XLA Ops:
  1.7 1.3 %copy.73 = f32[4,8,8,8,128]{4,3,2,1,0:T(8,128)S(1)} copy(f32[4,8,8,8,128]{4,3,1,2,0:T(8,128)} %bitcast.297) | data formatting | bytes 2097152 | tf_op jit(solution)/shard_map/transpose | solution.py:116
  3.1 1.4 %gather_fusion.2 = f32[16,64,128]{2,1,0:T(8,128)} fusion(f32[32,64,128]{2,1,0:T(8,128)S(1)} %bitcast.286, s32[1024]{0:T(1024)S(1)} %pad_clamp_fusion.5), kind=kCustom, calls=%fused_computation.2 | custom fusion | bytes 1048640 | tf_op jit(solution)/shard_map/gather | solution.py:243
  4.5 4.4 %all-to-all-start = ((f32[4,4,64,128]{3,2,1,0:T(8,128)}), f32[4,4,64,128]{3,2,1,0:T(8,128)S(1)}, u32[]{:S(2)}, u32[]{:S(2)}) async-start(f32[4,4,64,128]{3,2,1,0:T(8,128)} %bitcast.17), calls=%async_computation | async-start | bytes 1048576 | tf_op jit(solution)/shard_map/all_to_all | solution.py:249
  22.9 1.9 %fusion.15 = f32[32,64,128]{2,1,0:T(8,128)S(1)} fusion(f32[32,64,128]{2,1,0:T(8,128)S(1)} %gather_fusion.3, f32[32,64,128]{2,1,0:T(8,128)S(1)} %gather_fusion.4, f32[32]{0:T(128)S(1)} %get-tuple-element.195, f32[32]{0:T(128)S(1)} %get-tuple-element.196, f32[32]{0:T(128)S(1)} %get-tuple-element.194, f32[32]{0:T(128)S(1)} %get-tuple-element.140, ...), kind=kOutput, calls=%fused_computation.49 | convolution fusion | flops 203554816 | bytes 3277856 | tf_op jit(solution)/shard_map/nij,njv->niv/dot_general | solution.py:88
  24.8 1.1 %multiply_add_fusion.6 = f32[32,64,32]{2,1,0:T(8,128)S(1)} fusion(f32[32,64,128]{2,1,0:T(8,128)S(1)} %fusion.15, f32[32]{0:T(128)S(1)} %get-tuple-element.128, f32[32]{0:T(128)S(1)} %get-tuple-element.129, f32[32]{0:T(128)S(1)} %get-tuple-element.130, f32[32]{0:T(128)S(1)} %get-tuple-element.131), kind=kLoop, calls=%fused_computation.47 | loop fusion | flops 458752 | bytes 1311232 | tf_op jit(solution)/shard_map/add | solution.py:106
  26.0 1.3 %multiply_add_fusion.7 = (f32[32,64,32]{2,1,0:T(8,128)S(1)}, f32[32,64,32]{2,1,0:T(8,128)S(1)}, f32[32,64,32]{2,1,0:T(8,128)S(1)}) fusion(f32[32,64,128]{2,1,0:T(8,128)S(1)} %fusion.15, f32[32]{0:T(128)S(1)} %get-tuple-element.132, f32[32]{0:T(128)S(1)} %get-tuple-element.133, f32[32]{0:T(128)S(1)} %get-tuple-element.122, f32[32]{0:T(128)S(1)} %get-tuple-element.125, ...), kind=kLoop, calls=%fused_computation.48 | loop fusion | flops 851968 | bytes 1836032 | tf_op jit(solution)/shard_map/add | solution.py:106
  27.3 0.9 pad_maximum_fusion.8
  29.1 1.9 %collective-permute-start = (f32[1,65,128]{2,1,0:T(8,128)S(1)}, f32[1,65,128]{2,1,0:T(8,128)S(1)}, u32[]{:S(2)}, u32[]{:S(2)}) collective-permute-start(f32[1,65,128]{2,1,0:T(8,128)S(1)} %concatenate.71), channel_id=1, source_target_pairs={{4,0},{8,4},{12,8},{5,1},{9,5},{13,9},{6,2},{10,6},{14,10},{7,3},{... | collective-permute-start | bytes 99848 | tf_op jit(solution)/shard_map/ppermute | solution.py:201
  31.6 3.7 %collective-permute-start.1 = (f32[1,65,128]{2,1,0:T(8,128)S(1)}, f32[1,65,128]{2,1,0:T(8,128)S(1)}, u32[]{:S(2)}, u32[]{:S(2)}) collective-permute-start(f32[1,65,128]{2,1,0:T(8,128)S(1)} %concatenate.73), channel_id=1, source_target_pairs={{0,4},{4,8},{8,12},{1,5},{5,9},{9,13},{2,6},{6,10},{10,14},{3,7},{... | collective-permute-start | bytes 99848 | tf_op jit(solution)/shard_map/ppermute | solution.py:196
  35.3 4.0 %collective-permute-start.2 = (f32[32,1,128]{2,1,0:T(1,128)S(1)}, f32[32,1,128]{2,1,0:T(1,128)S(1)}, u32[]{:S(2)}, u32[]{:S(2)}) collective-permute-start(f32[32,1,128]{2,1,0:T(1,128)S(1)} %get-tuple-element.33), channel_id=1, source_target_pairs={{1,0},{2,1},{3,2},{0,3},{5,4},{6,5},{7,6},{4,7},{9,8},{10,9},{11,1... | collective-permute-start | bytes 49160 | tf_op jit(solution)/shard_map/ppermute | solution.py:44
  40.2 3.5 %collective-permute-done.3 = f32[32,1,128]{2,1,0:T(1,128)S(1)} collective-permute-done((f32[32,1,128]{2,1,0:T(1,128)S(1)}, f32[32,1,128]{2,1,0:T(1,128)S(1)}, u32[]{:S(2)}, u32[]{:S(2)}) %collective-permute-start.3) | collective-permute-done | bytes 16416 | tf_op jit(solution)/shard_map/ppermute | solution.py:42
  43.7 1.3 %multiply_reduce_fusion.1 = (f32[128]{0:T(128)S(1)}, f32[128]{0:T(128)}, f32[32,64,128]{2,1,0:T(8,128)S(1)}) fusion(f32[32,64,128]{2,1,0:T(8,128)S(1)} %copy-done, f32[32]{0:T(128)S(1)} %add_cosine_fusion, f32[32,64,128]{2,1,0:T(8,128)S(1)} %bitcast.294, f32[32,1,128]{2,1,0:T(1,128)S(1)} %collective-permute-done.3, ...), kind=kLoop, calls=%fused_computation.42 | loop fusion | flops 3931904 | bytes 3245312 | tf_op jit(solution)/shard_map/reduce_sum | solution.py:137
  45.1 1.4 %gather_fusion.5 = f32[16,64,128]{2,1,0:T(8,128)} fusion(f32[32,64,128]{2,1,0:T(8,128)S(1)} %bitcast.288, s32[1024]{0:T(1024)S(1)} %pad_clamp_fusion.2), kind=kCustom, calls=%fused_computation.5 | custom fusion | bytes 1048640 | tf_op jit(solution)/shard_map/gather | solution.py:243
  46.5 3.7 %all-to-all-start.1 = ((f32[4,4,64,128]{3,2,1,0:T(8,128)}), f32[4,4,64,128]{3,2,1,0:T(8,128)S(1)}, u32[]{:S(2)}, u32[]{:S(2)}) async-start(f32[4,4,64,128]{3,2,1,0:T(8,128)} %bitcast.43), calls=%async_computation.1 | async-start | bytes 1048576 | tf_op jit(solution)/shard_map/all_to_all | solution.py:249
  50.2 0.9 gather_fusion.7
  52.2 1.3 %maximum_multiply_fusion = f32[34]{0:T(128)S(1)} fusion(f32[1]{0:T(128)} %bitcast.52, f32[32]{0:T(128)S(1)} %copy-done.4, f32[1]{0:T(128)} %bitcast.51, s32[]{:T(128)S(6)} %sub.240), kind=kLoop, calls=%fused_computation.397 | loop fusion | flops 272 | bytes 276 | tf_op jit(solution)/shard_map/mul | solution.py:279
  54.4 3.6 %all-to-all-done.1 = f32[4,4,64,128]{3,2,1,0:T(8,128)S(1)} async-done(((f32[4,4,64,128]{3,2,1,0:T(8,128)}), f32[4,4,64,128]{3,2,1,0:T(8,128)S(1)}, u32[]{:S(2)}, u32[]{:S(2)}) %all-to-all-start.1) | async-done | bytes 524320 | tf_op jit(solution)/shard_map/all_to_all | solution.py:249
  59.5 1.9 %fusion.13 = f32[32,64,128]{2,1,0:T(8,128)S(1)} fusion(f32[32,64,128]{2,1,0:T(8,128)S(1)} %gather_fusion.6, f32[32,64,128]{2,1,0:T(8,128)S(1)} %gather_fusion.7, f32[64,64]{1,0:T(8,128)S(1)} %get-tuple-element.151, f32[32]{0:T(128)S(1)} %copy-done.37, f32[64,64]{1,0:T(8,128)S(1)} %get-tuple-element.152, f32[32]{0:T(128)S(1)} %copy-done.38, ...), kind=kOutput, calls=%fused_computation.43 | convolution fusion | flops 203554816 | bytes 3277856 | tf_op jit(solution)/shard_map/nij,njv->niv/dot_general | solution.py:88
  61.4 1.0 %fusion.165 = f32[32,1,128]{2,1,0:T(1,128)S(1)} fusion(f32[32,64,1]{1,2,0:T(1,128)S(1)} %bitcast.305, f32[32,64,128]{2,1,0:T(8,128)S(1)} %fusion.13), kind=kOutput, calls=%fused_computation.484 | convolution fusion | flops 3145728 | bytes 1073152 | tf_op jit(solution)/shard_map/pi,piv->pv/dot_general | solution.py:282
  63.6 2.3 %collective-permute-done.4 = f32[768]{0:T(1024)S(1)} collective-permute-done((f32[768]{0:T(1024)S(1)}, f32[768]{0:T(1024)S(1)}, u32[]{:S(2)}, u32[]{:S(2)}) %collective-permute-start.4) | collective-permute-done | bytes 3104 | tf_op jit(solution)/shard_map/ppermute | solution.py:22
  67.1 2.2 %collective-permute-done.5 = f32[768]{0:T(1024)S(1)} collective-permute-done((f32[768]{0:T(1024)S(1)}, f32[768]{0:T(1024)S(1)}, u32[]{:S(2)}, u32[]{:S(2)}) %collective-permute-start.5) | collective-permute-done | bytes 3104 | tf_op jit(solution)/shard_map/ppermute | solution.py:22
  69.2 3.3 %collective-permute-start.6 = (f32[768]{0:T(1024)S(1)}, f32[768]{0:T(1024)S(1)}, u32[]{:S(2)}, u32[]{:S(2)}) collective-permute-start(f32[768]{0:T(1024)S(1)} %add.1347), channel_id=1, source_target_pairs={{0,4},{4,0},{8,12},{12,8},{1,5},{5,1},{9,13},{13,9},{2,6},{6,2},{1... | collective-permute-start | bytes 9224 | tf_op jit(solution)/shard_map/ppermute | solution.py:22
  72.6 0.8 collective-permute-done.6
  73.5 2.5 %collective-permute-start.8 = (f32[1,64,128]{2,0,1:T(1,128)S(1)}, f32[1,64,128]{2,0,1:T(1,128)S(1)}, u32[]{:S(2)}, u32[]{:S(2)}) collective-permute-start(f32[1,64,128]{2,0,1:T(1,128)S(1)} %get-tuple-element.26), channel_id=1, source_target_pairs={{4,0},{8,4},{12,8},{5,1},{9,5},{13,9},{6,2},{10,6},{14,10},{7,3},{... | collective-permute-start | bytes 98312 | tf_op jit(solution)/shard_map/ppermute | solution.py:177
  76.0 3.2 %collective-permute-start.9 = (f32[1,64,128]{2,0,1:T(1,128)S(1)}, f32[1,64,128]{2,0,1:T(1,128)S(1)}, u32[]{:S(2)}, u32[]{:S(2)}) collective-permute-start(f32[1,64,128]{2,0,1:T(1,128)S(1)} %get-tuple-element.27), channel_id=1, source_target_pairs={{0,4},{4,8},{8,12},{1,5},{5,9},{9,13},{2,6},{6,10},{10,14},{3,7},{... | collective-permute-start | bytes 98312 | tf_op jit(solution)/shard_map/ppermute | solution.py:176
  79.3 1.5 %collective-permute-start.11 = (f32[32,1,128]{2,0,1:T(8,128)S(1)}, f32[32,1,128]{2,0,1:T(8,128)S(1)}, u32[]{:S(2)}, u32[]{:S(2)}) collective-permute-start(f32[32,1,128]{2,0,1:T(8,128)S(1)} %get-tuple-element.29), channel_id=1, source_target_pairs={{0,1},{1,2},{2,3},{3,0},{4,5},{5,6},{6,7},{7,4},{8,9},{9,10},{10,1... | collective-permute-start | bytes 49160 | tf_op jit(solution)/shard_map/ppermute | solution.py:178
  81.2 1.0 %multiply_add_fusion.2 = f32[4,8,8,8,32]{4,1,0,3,2:T(8,128)S(1)} fusion(f32[4,8,8,8,128]{4,1,0,3,2:T(8,128)S(1)} %bitcast_multiply_fusion, f32[4,8]{0,1:T(8,128)S(1)} %copy.89, f32[4,8]{0,1:T(8,128)S(1)} %copy.88, f32[4,8]{0,1:T(8,128)S(1)} %copy.87, f32[4,8]{0,1:T(8,128)S(1)} %copy.86), kind=kLoop, calls=%fused_computation.39 | loop fusion | flops 458752 | bytes 1311232 | tf_op jit(solution)/shard_map/add | solution.py:167
  82.3 1.2 %multiply_add_fusion.3 = (f32[4,8,8,8,32]{4,1,0,3,2:T(8,128)S(1)}, f32[4,8,8,8,32]{4,1,0,3,2:T(8,128)S(1)}, f32[4,8,8,8,32]{4,1,0,3,2:T(8,128)S(1)}) fusion(f32[4,8,8,8,128]{4,1,0,3,2:T(8,128)S(1)} %bitcast_multiply_fusion, f32[4,8]{0,1:T(8,128)S(1)} %copy.85, f32[4,8]{0,1:T(8,128)S(1)} %copy.84, f32[4,8]{0,1:T(8,128)S(1)} %copy.72, f32[4,8]{0,1:T(8,128)S(1)} %copy.92, ...), kind=kLoop, calls=%fused_computation.40 | loop fusion | flops 851968 | bytes 1836032 | tf_op jit(solution)/shard_map/add | solution.py:167
  83.5 0.9 pad_maximum_fusion.9
  87.7 0.8 multiply_add_fusion.15
  90.7 0.8 multiply_add_fusion.11
  91.8 1.4 %fusion.4 = f32[32,64,128]{2,1,0:T(8,128)} fusion(f32[32,64,128]{2,1,0:T(8,128)S(1)} %bitcast.296, f32[32,1,128]{2,1,0:T(1,128)S(1)} %bitcast.304, f32[32,1,128]{2,1,0:T(1,128)S(1)} %bitcast.303, f32[1,64,128]{2,1,0:T(8,128)S(1)} %bitcast.302, f32[1,64,128]{2,1,0:T(8,128)S(1)} %bitcast.301, f32[128]{0:T(128)S(1)} %slice_divide_fusion.1, f32[32]{0:T(128)S(1)} %copy-done.4), kind=kLoop, calls=%fused_computation.18 | loop fusion | flops 3145728 | bytes 2196096 | tf_op jit(solution)/shard_map/mul | solution.py:333
  (261 shorter events, 29.8 us)
Async XLA Ops:
  4.5 4.5 %copy-start.3 = (f32[2,3,16,32]{3,2,1,0:T(8,128)S(1)}, f32[2,3,16,32]{3,2,1,0:T(8,128)}, u32[]{:S(2)}) copy-start(f32[2,3,16,32]{3,2,1,0:T(8,128)} %param.5) | copy-start | bytes 36868
  4.5 17.8 %all-to-all-start = ((f32[4,4,64,128]{3,2,1,0:T(8,128)}), f32[4,4,64,128]{3,2,1,0:T(8,128)S(1)}, u32[]{:S(2)}, u32[]{:S(2)}) async-start(f32[4,4,64,128]{3,2,1,0:T(8,128)} %bitcast.17), calls=%async_computation | async-start | bytes 1048576 | tf_op jit(solution)/shard_map/all_to_all | solution.py:249
  28.2 15.5 %copy-start = (f32[32,64,128]{2,1,0:T(8,128)S(1)}, f32[32,64,128]{2,1,0:T(8,128)}, u32[]{:S(2)}) copy-start(f32[32,64,128]{2,1,0:T(8,128)} %param.4) | copy-start | bytes 3145732
  29.1 10.4 %collective-permute-start = (f32[1,65,128]{2,1,0:T(8,128)S(1)}, f32[1,65,128]{2,1,0:T(8,128)S(1)}, u32[]{:S(2)}, u32[]{:S(2)}) collective-permute-start(f32[1,65,128]{2,1,0:T(8,128)S(1)} %concatenate.71), channel_id=1, source_target_pairs={{4,0},{8,4},{12,8},{5,1},{9,5},{13,9},{6,2},{10,6},{14,10},{7,3},{... | collective-permute-start | bytes 99848 | tf_op jit(solution)/shard_map/ppermute | solution.py:201
  31.6 8.6 %collective-permute-start.1 = (f32[1,65,128]{2,1,0:T(8,128)S(1)}, f32[1,65,128]{2,1,0:T(8,128)S(1)}, u32[]{:S(2)}, u32[]{:S(2)}) collective-permute-start(f32[1,65,128]{2,1,0:T(8,128)S(1)} %concatenate.73), channel_id=1, source_target_pairs={{0,4},{4,8},{8,12},{1,5},{5,9},{9,13},{2,6},{6,10},{10,14},{3,7},{... | collective-permute-start | bytes 99848 | tf_op jit(solution)/shard_map/ppermute | solution.py:196
  35.3 4.8 %collective-permute-start.2 = (f32[32,1,128]{2,1,0:T(1,128)S(1)}, f32[32,1,128]{2,1,0:T(1,128)S(1)}, u32[]{:S(2)}, u32[]{:S(2)}) collective-permute-start(f32[32,1,128]{2,1,0:T(1,128)S(1)} %get-tuple-element.33), channel_id=1, source_target_pairs={{1,0},{2,1},{3,2},{0,3},{5,4},{6,5},{7,6},{4,7},{9,8},{10,9},{11,1... | collective-permute-start | bytes 49160 | tf_op jit(solution)/shard_map/ppermute | solution.py:44
  39.3 4.4 %collective-permute-start.3 = (f32[32,1,128]{2,1,0:T(1,128)S(1)}, f32[32,1,128]{2,1,0:T(1,128)S(1)}, u32[]{:S(2)}, u32[]{:S(2)}) collective-permute-start(f32[32,1,128]{2,1,0:T(1,128)S(1)} %get-tuple-element.34), channel_id=1, source_target_pairs={{0,1},{1,2},{2,3},{3,0},{4,5},{5,6},{6,7},{7,4},{8,9},{9,10},{10,1... | collective-permute-start | bytes 49160 | tf_op jit(solution)/shard_map/ppermute | solution.py:42
  40.2 3.5 %slice-start = ((f32[1,65,128]{2,1,0:T(8,128)}), f32[1,64,128]{2,1,0:T(8,128)S(1)}, s32[]{:S(2)}) async-start(f32[1,65,128]{2,1,0:T(8,128)} %copy-done.1), calls=%async_computation.2 | async-start | bytes 65536 | tf_op jit(solution)/shard_map/slice | solution.py:204
  46.5 11.5 %all-to-all-start.1 = ((f32[4,4,64,128]{3,2,1,0:T(8,128)}), f32[4,4,64,128]{3,2,1,0:T(8,128)S(1)}, u32[]{:S(2)}, u32[]{:S(2)}) async-start(f32[4,4,64,128]{3,2,1,0:T(8,128)} %bitcast.43), calls=%async_computation.1 | async-start | bytes 1048576 | tf_op jit(solution)/shard_map/all_to_all | solution.py:249
  50.2 1.5 %copy-start.2 = (f32[1,65,128]{2,1,0:T(8,128)S(1)}, f32[1,65,128]{2,1,0:T(8,128)}, u32[]{:S(2)}) copy-start(f32[1,65,128]{2,1,0:T(8,128)} %copy-done.1) | copy-start | bytes 99844
  58.0 0.8 copy-start.38
  58.0 0.8 copy-start.39
  61.4 4.6 %copy-start.5 = (f32[4,8]{1,0:T(4,128)S(1)}, f32[4,8]{1,0:T(4,128)}, u32[]{:S(2)}) copy-start(f32[4,8]{1,0:T(4,128)} %get-tuple-element.48) | copy-start | bytes 388
  63.4 2.5 %collective-permute-start.4 = (f32[768]{0:T(1024)S(1)}, f32[768]{0:T(1024)S(1)}, u32[]{:S(2)}, u32[]{:S(2)}) collective-permute-start(f32[768]{0:T(1024)S(1)} %pad_maximum_fusion.14), channel_id=1, source_target_pairs={{0,1},{1,0},{2,3},{3,2},{4,5},{5,4},{6,7},{7,6},{8,9},{9,8},{10,11... | collective-permute-start | bytes 9224 | tf_op jit(solution)/shard_map/ppermute | solution.py:22
  65.8 3.4 %collective-permute-start.5 = (f32[768]{0:T(1024)S(1)}, f32[768]{0:T(1024)S(1)}, u32[]{:S(2)}, u32[]{:S(2)}) collective-permute-start(f32[768]{0:T(1024)S(1)} %fusion.150), channel_id=1, source_target_pairs={{0,2},{1,3},{2,0},{3,1},{4,6},{5,7},{6,4},{7,5},{8,10},{9,11},{10,... | collective-permute-start | bytes 9224 | tf_op jit(solution)/shard_map/ppermute | solution.py:22
  69.2 4.2 %collective-permute-start.6 = (f32[768]{0:T(1024)S(1)}, f32[768]{0:T(1024)S(1)}, u32[]{:S(2)}, u32[]{:S(2)}) collective-permute-start(f32[768]{0:T(1024)S(1)} %add.1347), channel_id=1, source_target_pairs={{0,4},{4,0},{8,12},{12,8},{1,5},{5,1},{9,13},{13,9},{2,6},{6,2},{1... | collective-permute-start | bytes 9224 | tf_op jit(solution)/shard_map/ppermute | solution.py:22
  73.4 7.3 %collective-permute-start.7 = (f32[768]{0:T(1024)S(1)}, f32[768]{0:T(1024)S(1)}, u32[]{:S(2)}, u32[]{:S(2)}) collective-permute-start(f32[768]{0:T(1024)S(1)} %add.1348), channel_id=1, source_target_pairs={{0,8},{4,12},{8,0},{12,4},{1,9},{5,13},{9,1},{13,5},{2,10},{6,14},... | collective-permute-start | bytes 9224 | tf_op jit(solution)/shard_map/ppermute | solution.py:22
  73.5 12.2 %collective-permute-start.8 = (f32[1,64,128]{2,0,1:T(1,128)S(1)}, f32[1,64,128]{2,0,1:T(1,128)S(1)}, u32[]{:S(2)}, u32[]{:S(2)}) collective-permute-start(f32[1,64,128]{2,0,1:T(1,128)S(1)} %get-tuple-element.26), channel_id=1, source_target_pairs={{4,0},{8,4},{12,8},{5,1},{9,5},{13,9},{6,2},{10,6},{14,10},{7,3},{... | collective-permute-start | bytes 98312 | tf_op jit(solution)/shard_map/ppermute | solution.py:177
  76.0 9.7 %collective-permute-start.9 = (f32[1,64,128]{2,0,1:T(1,128)S(1)}, f32[1,64,128]{2,0,1:T(1,128)S(1)}, u32[]{:S(2)}, u32[]{:S(2)}) collective-permute-start(f32[1,64,128]{2,0,1:T(1,128)S(1)} %get-tuple-element.27), channel_id=1, source_target_pairs={{0,4},{4,8},{8,12},{1,5},{5,9},{9,13},{2,6},{6,10},{10,14},{3,7},{... | collective-permute-start | bytes 98312 | tf_op jit(solution)/shard_map/ppermute | solution.py:176
  79.2 5.8 %collective-permute-start.10 = (f32[32,1,128]{2,0,1:T(8,128)S(1)}, f32[32,1,128]{2,0,1:T(8,128)S(1)}, u32[]{:S(2)}, u32[]{:S(2)}) collective-permute-start(f32[32,1,128]{2,0,1:T(8,128)S(1)} %get-tuple-element.28), channel_id=1, source_target_pairs={{1,0},{2,1},{3,2},{0,3},{5,4},{6,5},{7,6},{4,7},{9,8},{10,9},{11,1... | collective-permute-start | bytes 49160 | tf_op jit(solution)/shard_map/ppermute | solution.py:181
  79.3 5.7 %collective-permute-start.11 = (f32[32,1,128]{2,0,1:T(8,128)S(1)}, f32[32,1,128]{2,0,1:T(8,128)S(1)}, u32[]{:S(2)}, u32[]{:S(2)}) collective-permute-start(f32[32,1,128]{2,0,1:T(8,128)S(1)} %get-tuple-element.29), channel_id=1, source_target_pairs={{0,1},{1,2},{2,3},{3,0},{4,5},{5,6},{6,7},{7,4},{8,9},{9,10},{10,1... | collective-permute-start | bytes 49160 | tf_op jit(solution)/shard_map/ppermute | solution.py:178
  85.1 1.9 %copy-start.18 = (f32[64]{0:T(128)S(1)}, f32[64]{0:T(128)}, u32[]{:S(2)}) copy-start(f32[64]{0:T(128)} %get-tuple-element.71) | copy-start | bytes 772
  85.1 1.9 %copy-start.19 = (f32[64]{0:T(128)S(1)}, f32[64]{0:T(128)}, u32[]{:S(2)}) copy-start(f32[64]{0:T(128)} %get-tuple-element.72) | copy-start | bytes 772
  85.1 1.9 %copy-start.20 = (f32[64]{0:T(128)S(1)}, f32[64]{0:T(128)}, u32[]{:S(2)}) copy-start(f32[64]{0:T(128)} %get-tuple-element.73) | copy-start | bytes 772
  85.2 1.9 %copy-start.21 = (f32[64]{0:T(128)S(1)}, f32[64]{0:T(128)}, u32[]{:S(2)}) copy-start(f32[64]{0:T(128)} %get-tuple-element.78) | copy-start | bytes 772
  85.2 1.9 %copy-start.22 = (f32[64]{0:T(128)S(1)}, f32[64]{0:T(128)}, u32[]{:S(2)}) copy-start(f32[64]{0:T(128)} %get-tuple-element.79) | copy-start | bytes 772
  85.6 3.2 %copy-start.26 = (f32[64]{0:T(128)S(1)}, f32[64]{0:T(128)}, u32[]{:S(2)}) copy-start(f32[64]{0:T(128)} %get-tuple-element.91) | copy-start | bytes 772
  86.5 3.6 %copy-start.10 = (f32[64]{0:T(128)S(1)}, f32[64]{0:T(128)}, u32[]{:S(2)}) copy-start(f32[64]{0:T(128)} %get-tuple-element.85) | copy-start | bytes 772
  86.5 3.6 %copy-start.11 = (f32[64]{0:T(128)S(1)}, f32[64]{0:T(128)}, u32[]{:S(2)}) copy-start(f32[64]{0:T(128)} %get-tuple-element.86) | copy-start | bytes 772
  86.5 3.6 %copy-start.12 = (f32[64]{0:T(128)S(1)}, f32[64]{0:T(128)}, u32[]{:S(2)}) copy-start(f32[64]{0:T(128)} %get-tuple-element.87) | copy-start | bytes 772
  86.5 3.6 %copy-start.13 = (f32[64]{0:T(128)S(1)}, f32[64]{0:T(128)}, u32[]{:S(2)}) copy-start(f32[64]{0:T(128)} %get-tuple-element.92) | copy-start | bytes 772
  86.5 3.6 %copy-start.14 = (f32[64]{0:T(128)S(1)}, f32[64]{0:T(128)}, u32[]{:S(2)}) copy-start(f32[64]{0:T(128)} %get-tuple-element.93) | copy-start | bytes 772
  (23 other events, 15.9 us)

commit v8 on v5

--- a/solution.py
+++ b/solution.py
@@ -1,8 +1,11 @@
+import functools
 import math
 
 import jax
 import jax.numpy as jnp
 from jax import lax
+from jax.experimental import pallas as pl
+from jax.experimental.pallas import tpu as pltpu
 from jax.sharding import PartitionSpec as P
 
 LEV = 4
@@ -108,6 +111,95 @@
     return jnp.concatenate(out, axis=2)
 
 
+def level_rolls(fraction_z, value_count):
+    weight_z = cubic_matrix(fraction_z, LEV)
+    per_level = value_count // LEV
+    rows = []
+    for d in (-1, 0, 1, 2):
+        picked = [
+            weight_z[:, level, level + d] if 0 <= level + d < LEV else jnp.zeros_like(fraction_z)
+            for level in range(LEV)
+        ]
+        rows.append(jnp.repeat(jnp.stack(picked, axis=1), per_level, axis=1))
+    return jnp.stack(rows, axis=1)
+
+
+def _interp_kernel(local_ref, pick_ref, remote_ref, field_ref, arr_ref, pw_ref, *rest, band_cols):
+    out_ref = rest[-1]
+    coef_ref = rest[0] if len(rest) == 2 else None
+    value_count = field_ref.shape[2]
+    per_level = value_count // LEV
+
+    def body(q, carry):
+        source = local_ref[q]
+        src_row = pl.multiple_of((source // band_cols) * 8, 8)
+        src_col = pl.multiple_of((source % band_cols) * 8, 8)
+        own = field_ref[pl.ds(src_row, 8), pl.ds(src_col, 8), :].reshape(64, value_count)
+        got = arr_ref[pick_ref[q]]
+        patch = jnp.where(remote_ref[q] != 0, got, own)
+        out = jnp.dot(
+            pw_ref[q], patch, precision=lax.Precision.HIGHEST, preferred_element_type=jnp.float32
+        )
+        if coef_ref is not None:
+            coef = coef_ref[q]
+            mixed = coef[1:2, :] * out
+            for row, d in ((0, -1), (2, 1), (3, 2)):
+                rolled = pltpu.roll(out, (-d * per_level) % value_count, 1)
+                mixed = mixed + coef[row : row + 1, :] * rolled
+            out = mixed
+        dst_row = pl.multiple_of((q // band_cols) * 8, 8)
+        dst_col = pl.multiple_of((q % band_cols) * 8, 8)
+        out_ref[pl.ds(dst_row, 8), pl.ds(dst_col, 8), :] = out.reshape(8, 8, value_count)
+        return carry
+
+    lax.fori_loop(0, local_ref.shape[0], body, 0)
+
+
+def interpolate_into_field(local, pick, remote, field, arrived, plane, coef=None):
+    rows, cols, value_count = field.shape
+    smem = pl.BlockSpec(memory_space=pltpu.SMEM)
+    vmem = pl.BlockSpec(memory_space=pltpu.VMEM)
+    operands = [local, pick, remote, field, arrived, plane] + ([] if coef is None else [coef])
+    patch_count = local.shape[0]
+    return pl.pallas_call(
+        functools.partial(_interp_kernel, band_cols=cols // 8),
+        out_shape=jax.ShapeDtypeStruct(field.shape, jnp.float32),
+        in_specs=[smem] * 3 + [vmem] * (len(operands) - 3),
+        out_specs=vmem,
+        cost_estimate=pl.CostEstimate(
+            flops=patch_count * 2 * 64 * 64 * value_count * 6,
+            bytes_accessed=4 * (2 * field.size + arrived.size + plane.size),
+            transcendentals=0,
+        ),
+    )(*operands)
+
+
+def _gather_kernel(index_ref, field_ref, out_ref, *, band_cols):
+    value_count = field_ref.shape[2]
+
+    def body(s, carry):
+        source = index_ref[s]
+        src_row = pl.multiple_of((source // band_cols) * 8, 8)
+        src_col = pl.multiple_of((source % band_cols) * 8, 8)
+        out_ref[s] = field_ref[pl.ds(src_row, 8), pl.ds(src_col, 8), :].reshape(64, value_count)
+        return carry
+
+    lax.fori_loop(0, index_ref.shape[0], body, 0)
+
+
+def gather_patches(index, field):
+    rows, cols, value_count = field.shape
+    return pl.pallas_call(
+        functools.partial(_gather_kernel, band_cols=cols // 8),
+        out_shape=jax.ShapeDtypeStruct((index.shape[0], 64, value_count), jnp.float32),
+        in_specs=[pl.BlockSpec(memory_space=pltpu.SMEM), pl.BlockSpec(memory_space=pltpu.VMEM)],
+        out_specs=pl.BlockSpec(memory_space=pltpu.VMEM),
+        cost_estimate=pl.CostEstimate(
+            flops=0, bytes_accessed=8 * index.shape[0] * 64 * value_count, transcendentals=0
+        ),
+    )(index, field)
+
+
 def to_patches(state_field):
     band_rows = state_field.shape[0] // 8
     band_cols = state_field.shape[1] // 8
@@ -153,6 +245,20 @@
     k_shape = [1] * advected.ndim
     k_shape[row_dim] = rows
     return advected + diffusivity.reshape(k_shape) * laplace
+
+
+def levels_field(values, weight_z):
+    value_count = values.shape[-1]
+    per_level = value_count // LEV
+    blocks = [values[..., m * per_level : (m + 1) * per_level] for m in range(LEV)]
+    out = []
+    for level in range(LEV):
+        acc = None
+        for m in tap_sources(level, LEV):
+            term = weight_z[..., level, m][..., None] * blocks[m]
+            acc = term if acc is None else acc + term
+        out.append(acc)
+    return jnp.concatenate(out, axis=-1)
 
 
 def diffuse_first(advected, diffusivity):
@@ -210,8 +316,11 @@
     owned_here = remote & (source_dev == lat_index)
     sending = owned_here[:, :, None] & (slot_of[:, :, None] == slot_range[None, None, :])
     send_local = jnp.sum(jnp.where(sending, source_local[:, :, None], 0), axis=1)
-    own_patches = to_patches(state_field)
-    outgoing = own_patches[send_local.reshape(-1)].reshape(lat_count, CAP, 64, value_count)
+    outgoing = gather_patches(
+        jnp.clip(send_local.reshape(-1), 0, per_device - 1), state_field
+    ).reshape(
+        lat_count, CAP, 64, value_count
+    )
     my_dev = lax.dynamic_index_in_dim(source_dev, lat_index, 0, keepdims=False)
     my_slot = lax.dynamic_index_in_dim(slot_of, lat_index, 0, keepdims=False)
     my_local = lax.dynamic_index_in_dim(source_local, lat_index, 0, keepdims=False)
@@ -220,9 +329,9 @@
     arrived = lax.all_to_all(outgoing, "lat", 0, 0, tiled=True).reshape(
         lat_count * CAP, 64, value_count
     )
-    pick_index = my_dev * CAP + my_slot
-    patches = jnp.where(my_remote[:, None, None], arrived[pick_index], own_patches[my_local])
-    return patches, my_frac
+    pick_index = jnp.clip(my_dev * CAP + my_slot, 0, lat_count * CAP - 1)
+    my_local = jnp.clip(my_local, 0, per_device - 1)
+    return my_local, pick_index, my_remote.astype(jnp.int32), arrived, my_frac
 
 
 def local(tracers, shifts, diffusivity, source_patch):
@@ -237,21 +346,30 @@
     weights = column_area(lat_index * row_count, row_count, total_rows)
     target_part = column_mass(tracers, weights)
 
-    patches, frac = departed(tracers, source_patch[0], shifts[0])
-    advected = from_patches(levels(spatial(patches, frac[0], frac[1]), frac[2]), band_rows, band_cols)
+    near, pick, remote, arrived, frac = departed(tracers, source_patch[0], shifts[0])
+    advected = interpolate_into_field(
+        near,
+        pick,
+        remote,
+        tracers,
+        arrived,
+        plane_weights(frac[0], frac[1]),
+        level_rolls(frac[2], value_count),
+    )
     first, k_wide = diffuse_first(advected, diffusivity)
     first_part = column_mass(first, weights)
 
-    patches, frac = departed(first, source_patch[1], shifts[1])
-    planar = spatial(patches, frac[0], frac[1])
+    near, pick, remote, arrived, frac = departed(first, source_patch[1], shifts[1])
+    planar = interpolate_into_field(
+        near, pick, remote, first, arrived, plane_weights(frac[0], frac[1])
+    )
     weight_z = cubic_matrix(frac[2], LEV)
 
     area_wide = column_area(lat_index * row_count - 1, row_count + 2, total_rows)
     flux = area_wide * k_wide
     g = weights - 2.0 * flux[1:-1] + flux[:-2] + flux[2:]
-    g_cols = jnp.broadcast_to(g.reshape(band_rows, 1, 8, 1), (band_rows, band_cols, 8, 8))
-    weighted = jnp.einsum(
-        "pi,piv->pv", g_cols.reshape(per_device, 64), planar, precision=lax.Precision.HIGHEST
+    weighted = jnp.sum(
+        (g[:, None, None] * planar).reshape(band_rows, 8, band_cols, 8, value_count), axis=(1, 3)
     ).reshape(per_device, LEV, per_level)
     mix_part = jnp.einsum(
         "plm,pmt->lmt", weight_z, weighted, precision=lax.Precision.HIGHEST
@@ -267,9 +385,10 @@
         value_count
     )
     second_ratio = target / second_mass
-    advected = from_patches(
-        levels(planar * first_ratio[None, None, :], frac[2]), band_rows, band_cols
-    )
+    advected = levels_field(
+        (planar * first_ratio).reshape(band_rows, 8, band_cols, 8, value_count),
+        weight_z.reshape(band_rows, 1, band_cols, 1, LEV, LEV),
+    ).reshape(row_count, col_count, value_count)
     return diffuse(advected, diffusivity, 0) * second_ratio[None, None, :]
 
 

time: 82.7 us -> 107 us (1.29)
  Pallas kernels: 0 us -> 23.7 us
  other arithmetic: 12.3 us -> 21.3 us
  matrix products: 4.93 us -> 0.17 us
  waiting for transfers between devices: 21.1 us -> 16.6 us
    pallas_call x0 -> x4, Pallas kernels: none -> 23.7 us  [the longest x2 19.2 us: interpolate_into_field(): pl.pallas_call(functools.partial(_interp_kernel, band_cols=cols // 8), ou...]
    gather x6 -> x0, local copies, waits for them, and re-layouts: 5.21 us -> none  [the longest x2 2.75 us: departed(): own_patches[send_local.reshape(-1)].reshape(lat_count, CAP, 64, value_count)]
    dot_general x3 -> x0, matrix products: 4.75 us -> none  [the longest x2 3.79 us: spatial(): jnp.einsum('nij,njv->niv', plane_weights(fraction_y, fraction_x), patches...]
    mul x2 -> x4, other arithmetic: 0.17 us -> 4.73 us  [the longest x2 3.28 us: plane_weights(): along(fraction_y, rows // 8, cols // 8)]
    all_to_all x2, waiting for transfers between devices: 6.95 us -> 3.21 us  [departed(): lax.all_to_all(outgoing, 'lat', 0, 0, tiled=True)]
    reduce_sum x1, other arithmetic: 0.75 us -> 4.45 us  [column_mass(): return jnp.sum(weights[:, None, None] * state_field, axis=(0, 1))]
    add x4 -> x2, other arithmetic: 4.85 us -> 2.17 us  [levels_field(): acc = term if acc is None else acc + term]
    min x0 -> x6, other arithmetic: none -> 2.34 us  [the longest x2 1.2 us: departed(): my_local = jnp.clip(my_local, 0, per_device - 1)]
  transfers between devices with their start and end apart: 14 -> 14, of which waited for: 8 -> 7; matrix products, arithmetic and copies ran while one was open for 10% -> 16% of each run, Pallas kernels for 0% -> 0%
where the time goes in v8:
time: 107 us; the launch traced here: 106 us
  starting transfers between devices  30.4 us (28%)
  Pallas kernels  23.7 us (22%)
  other arithmetic  21.3 us (20%)
  waiting for transfers between devices  16.6 us (16%)
  local copies, waits for them, and re-layouts  13.6 us (13%)
    pallas_call x2, Pallas kernels, interpolate_into_field(): pl.pallas_call(functools.partial(_interp_kernel, band_cols=cols // 8), ou...  19.2 us
    ppermute x4, waiting for transfers between devices, all_sum(): lax.ppermute(value, axis, [(i, i ^ distance) for i in range(count)])  8.17 us
    all_to_all x2, starting transfers between devices, departed(): lax.all_to_all(outgoing, 'lat', 0, 0, tiled=True)  7.85 us
    ppermute x3, starting transfers between devices, extended(): lax.ppermute(head, axis, [((i + 1) % count, i) for i in range(ends)])  7.27 us
    ppermute x3, starting transfers between devices, extended(): lax.ppermute(tail, axis, [(i, (i + 1) % count) for i in range(ends)])  5.53 us
    pallas_call x2, Pallas kernels, gather_patches(): pl.pallas_call(functools.partial(_gather_kernel, band_cols=cols // 8), ou...  4.58 us
    reduce_sum x1, other arithmetic, column_mass(): return jnp.sum(weights[:, None, None] * state_field, axis=(0, 1))  4.45 us
    ppermute x4, starting transfers between devices, all_sum(): lax.ppermute(value, axis, [(i, i ^ distance) for i in range(count)])  4.02 us
  transfers between devices with their start and end apart: 14, of which 7 were waited for; matrix products, arithmetic and copies ran while one was open for 16% of the time, Pallas kernels for 0%

profile of v8, /device:TPU:1, one launch (start us, length us, event | category | flops | bytes accessed | tf_op | source)
XLA Modules:
  0.0 106.4 jit_solution(14108201362465553804)
XLA Ops:
  2.2 2.3 %shard_map.46 = f32[16,64,128]{2,1,0:T(8,128)} custom-call(s32[16]{0:T(128)} %min.175.index_ref, f32[32,64,128]{2,1,0:T(8,128)} %field_ref.3), custom_call_target="tpu_custom_call" | custom-call | bytes 1048576 | tf_op jit(solution)/shard_map/pallas_call | solution.py:192
  4.5 4.3 %all-to-all-start = ((f32[4,4,64,128]{3,2,1,0:T(8,128)}), f32[4,4,64,128]{3,2,1,0:T(8,128)S(1)}, u32[]{:S(2)}, u32[]{:S(2)}) async-start(f32[4,4,64,128]{3,2,1,0:T(8,128)} %bitcast.137), calls=%async_computation | async-start | bytes 1048576 | tf_op jit(solution)/shard_map/all_to_all | solution.py:329
  15.4 1.6 %add_multiply_fusion.1.pw_ref = f32[32,64,64]{2,1,0:T(8,128)} fusion(f32[64,64]{1,0:T(8,128)S(1)} %get-tuple-element.82, f32[32]{0:T(128)S(1)} %get-tuple-element.106, f32[64,64]{1,0:T(8,128)S(1)} %get-tuple-element.83, f32[32]{0:T(128)S(1)} %get-tuple-element.107, f32[64,64]{1,0:T(8,128)S(1)} %get-tuple-element.84, f32[32]{0:T(128)S(1)} %get-tuple-element.105, ...), kind=kLoop, calls=%fused_computation.30 | loop fusion | flops 1966080 | bytes 656384 | tf_op jit(solution)/shard_map/mul | solution.py:87
  19.4 1.7 %add_multiply_fusion.pw_ref = f32[32,64,64]{2,1,0:T(8,128)} fusion(f32[32]{0:T(128)S(1)} %get-tuple-element.93, f32[32]{0:T(128)S(1)} %get-tuple-element.94, f32[32]{0:T(128)S(1)} %get-tuple-element.92, f32[32]{0:T(128)S(1)} %get-tuple-element.67, f32[32]{0:T(128)S(1)} %get-tuple-element.90, f32[32]{0:T(128)S(1)} %get-tuple-element.91, ...), kind=kLoop, calls=%fused_computation.29 | loop fusion | flops 1966080 | bytes 656384 | tf_op jit(solution)/shard_map/mul | solution.py:87
  21.0 0.8 copy-done.2
  21.8 11.0 %shard_map.47 = f32[32,64,128]{2,1,0:T(8,128)} custom-call(s32[32]{0:T(128)} %fusion.67.local_ref, s32[32]{0:T(128)} %clamp_bitcast_fusion.pick_ref, s32[32]{0:T(128)} %fusion.58.remote_ref, f32[32,64,128]{2,1,0:T(8,128)} %field_ref.3, f32[16,64,128]{2,1,0:T(8,128)} %bitcast.139, f32[32,64,64]{2,1,0:T(8,128)} %add_multiply_fusion.1.pw_ref, ...), custom_call_target="tpu_custom_call" | custom-call | flops 201326592 | bytes 3145728 | tf_op jit(solution)/shard_map/pallas_call | solution.py:164
  32.8 1.0 fusion.91
  34.6 2.0 %collective-permute-start.3 = (f32[32,1,128]{2,1,0:T(1,128)S(1)}, f32[32,1,128]{2,1,0:T(1,128)S(1)}, u32[]{:S(2)}, u32[]{:S(2)}) collective-permute-start(f32[32,1,128]{2,1,0:T(1,128)S(1)} %get-tuple-element.36), channel_id=1, source_target_pairs={{0,1},{1,2},{2,3},{3,0},{4,5},{5,6},{6,7},{7,4},{8,9},{9,10},{10,1... | collective-permute-start | bytes 49160 | tf_op jit(solution)/shard_map/ppermute | solution.py:45
  36.6 2.1 %collective-permute-start.2 = (f32[32,1,128]{2,1,0:T(1,128)S(1)}, f32[32,1,128]{2,1,0:T(1,128)S(1)}, u32[]{:S(2)}, u32[]{:S(2)}) collective-permute-start(f32[32,1,128]{2,1,0:T(1,128)S(1)} %get-tuple-element.35), channel_id=1, source_target_pairs={{1,0},{2,1},{3,2},{0,3},{5,4},{6,5},{7,6},{4,7},{9,8},{10,9},{11,1... | collective-permute-start | bytes 49160 | tf_op jit(solution)/shard_map/ppermute | solution.py:47
  39.3 3.8 %collective-permute-start.1 = (f32[1,65,128]{2,1,0:T(8,128)S(1)}, f32[1,65,128]{2,1,0:T(8,128)S(1)}, u32[]{:S(2)}, u32[]{:S(2)}) collective-permute-start(f32[1,65,128]{2,1,0:T(8,128)S(1)} %concatenate.45), channel_id=1, source_target_pairs={{0,4},{4,8},{8,12},{1,5},{5,9},{9,13},{2,6},{6,10},{10,14},{3,7},{... | collective-permute-start | bytes 99848 | tf_op jit(solution)/shard_map/ppermute | solution.py:273
  43.7 1.9 %collective-permute-start = (f32[1,65,128]{2,1,0:T(8,128)S(1)}, f32[1,65,128]{2,1,0:T(8,128)S(1)}, u32[]{:S(2)}, u32[]{:S(2)}) collective-permute-start(f32[1,65,128]{2,1,0:T(8,128)S(1)} %concatenate.43), channel_id=1, source_target_pairs={{4,0},{8,4},{12,8},{5,1},{9,5},{13,9},{6,2},{10,6},{14,10},{7,3},{... | collective-permute-start | bytes 99848 | tf_op jit(solution)/shard_map/ppermute | solution.py:278
  46.9 2.1 %collective-permute-done = f32[1,65,128]{2,1,0:T(8,128)S(1)} collective-permute-done((f32[1,65,128]{2,1,0:T(8,128)S(1)}, f32[1,65,128]{2,1,0:T(8,128)S(1)}, u32[]{:S(2)}, u32[]{:S(2)}) %collective-permute-start) | collective-permute-done | bytes 33312 | tf_op jit(solution)/shard_map/ppermute | solution.py:278
  49.7 4.4 %multiply_reduce_fusion.1 = (f32[128]{0:T(128)S(1)}, f32[128]{0:T(128)S(1)}, f32[32,64,128]{2,1,0:T(8,128)}) fusion(f32[32,64,128]{2,1,0:T(8,128)S(1)} %copy-done.1, f32[32]{0:T(128)S(1)} %add_cosine_fusion, f32[32,64,128]{2,1,0:T(8,128)} %shard_map.47, f32[32,1,128]{2,1,0:T(1,128)S(1)} %collective-permute-done.3, ...), kind=kLoop, calls=%fused_computation.28 | loop fusion | flops 3931904 | bytes 3245312 | tf_op jit(solution)/shard_map/reduce_sum | solution.py:229
  54.2 2.3 %shard_map.48 = f32[16,64,128]{2,1,0:T(8,128)} custom-call(s32[16]{0:T(128)} %min.186.index_ref, f32[32,64,128]{2,1,0:T(8,128)} %get-tuple-element.9.field_ref), custom_call_target="tpu_custom_call" | custom-call | bytes 1048576 | tf_op jit(solution)/shard_map/pallas_call | solution.py:192
  56.4 3.6 %all-to-all-start.1 = ((f32[4,4,64,128]{3,2,1,0:T(8,128)}), f32[4,4,64,128]{3,2,1,0:T(8,128)S(1)}, u32[]{:S(2)}, u32[]{:S(2)}) async-start(f32[4,4,64,128]{3,2,1,0:T(8,128)} %bitcast.138), calls=%async_computation.1 | async-start | bytes 1048576 | tf_op jit(solution)/shard_map/all_to_all | solution.py:329
  61.7 1.3 %maximum_multiply_fusion = f32[34]{0:T(128)S(1)} fusion(f32[1]{0:T(128)} %bitcast.31, f32[32]{0:T(128)S(1)} %copy-done.7, f32[1]{0:T(128)} %bitcast.30, s32[]{:T(128)S(6)} %sub.181), kind=kLoop, calls=%fused_computation.216 | loop fusion | flops 272 | bytes 276 | tf_op jit(solution)/shard_map/mul | solution.py:369
  63.1 3.2 %all-to-all-done.1 = f32[4,4,64,128]{3,2,1,0:T(8,128)S(1)} async-done(((f32[4,4,64,128]{3,2,1,0:T(8,128)}), f32[4,4,64,128]{3,2,1,0:T(8,128)S(1)}, u32[]{:S(2)}, u32[]{:S(2)}) %all-to-all-start.1) | async-done | bytes 524320 | tf_op jit(solution)/shard_map/all_to_all | solution.py:329
  66.3 0.8 copy-done.3
  67.1 8.2 %shard_map.49 = f32[32,64,128]{2,1,0:T(8,128)} custom-call(s32[32]{0:T(128)} %fusion.62.local_ref, s32[32]{0:T(128)} %clamp_bitcast_fusion.1.pick_ref, s32[32]{0:T(128)} %fusion.59.remote_ref, f32[32,64,128]{2,1,0:T(8,128)} %get-tuple-element.9.field_ref, f32[16,64,128]{2,1,0:T(8,128)} %bitcast.140, f32[32,64,64]{2,1,0:T(8,128)} %add_multiply_fusion.pw_ref), custom_call_target="tpu_custom_call" | custom-call | flops 201326592 | bytes 3145728 | tf_op jit(solution)/shard_map/pallas_call | solution.py:164
  75.2 1.4 %broadcast_multiply_fusion.1 = f32[32,64,128]{2,1,0:T(8,128)S(1)} fusion(f32[32,64,128]{2,1,0:T(8,128)} %shard_map.49, f32[32]{0:T(128)S(1)} %slice_add_fusion), kind=kLoop, calls=%fused_computation.32 | loop fusion | flops 262144 | bytes 2097280 | tf_op jit(solution)/shard_map/mul | solution.py:372
  77.2 2.4 %collective-permute-done.4 = f32[768]{0:T(1024)S(1)} collective-permute-done((f32[768]{0:T(1024)S(1)}, f32[768]{0:T(1024)S(1)}, u32[]{:S(2)}, u32[]{:S(2)}) %collective-permute-start.4) | collective-permute-done | bytes 3104 | tf_op jit(solution)/shard_map/ppermute | solution.py:25
  80.4 2.7 %collective-permute-done.5 = f32[768]{0:T(1024)S(1)} collective-permute-done((f32[768]{0:T(1024)S(1)}, f32[768]{0:T(1024)S(1)}, u32[]{:S(2)}, u32[]{:S(2)}) %collective-permute-start.5) | collective-permute-done | bytes 3104 | tf_op jit(solution)/shard_map/ppermute | solution.py:25
  83.0 3.2 %collective-permute-start.6 = (f32[768]{0:T(1024)S(1)}, f32[768]{0:T(1024)S(1)}, u32[]{:S(2)}, u32[]{:S(2)}) collective-permute-start(f32[768]{0:T(1024)S(1)} %add.746), channel_id=1, source_target_pairs={{0,4},{4,0},{8,12},{12,8},{1,5},{5,1},{9,13},{13,9},{2,6},{6,2},{1... | collective-permute-start | bytes 9224 | tf_op jit(solution)/shard_map/ppermute | solution.py:25
  87.1 2.4 %collective-permute-done.7 = f32[768]{0:T(1024)S(1)} collective-permute-done((f32[768]{0:T(1024)S(1)}, f32[768]{0:T(1024)S(1)}, u32[]{:S(2)}, u32[]{:S(2)}) %collective-permute-start.7) | collective-permute-done | bytes 3104 | tf_op jit(solution)/shard_map/ppermute | solution.py:25
  89.7 1.0 multiply_add_fusion.2
  90.7 1.2 %multiply_add_fusion.3 = (f32[4,8,8,8,32]{4,3,2,1,0:T(8,128)S(1)}, f32[4,8,8,8,32]{4,3,2,1,0:T(8,128)S(1)}, f32[4,8,8,8,32]{4,3,2,1,0:T(8,128)S(1)}) fusion(f32[4,8,8,8,128]{4,3,2,1,0:T(8,128)S(1)} %bitcast.132, f32[4,8]{1,0:T(4,128)S(1)} %get-tuple-element.49, f32[4,8]{1,0:T(4,128)S(1)} %get-tuple-element.50, f32[4,8]{1,0:T(4,128)S(1)} %get-tuple-element.39, ...), kind=kLoop, calls=%fused_computation.26 | loop fusion | flops 851968 | bytes 1836032 | tf_op jit(solution)/shard_map/add | solution.py:259
  91.8 0.9 pad_maximum_fusion.8
  92.9 3.3 %collective-permute-start.10 = (f32[32,1,128]{2,1,0:T(1,128)S(1)}, f32[32,1,128]{2,1,0:T(1,128)S(1)}, u32[]{:S(2)}, u32[]{:S(2)}) collective-permute-start(f32[32,1,128]{2,1,0:T(1,128)S(1)} %get-tuple-element.28), channel_id=1, source_target_pairs={{1,0},{2,1},{3,2},{0,3},{5,4},{6,5},{7,6},{4,7},{9,8},{10,9},{11,1... | collective-permute-start | bytes 49160 | tf_op jit(solution)/shard_map/ppermute | solution.py:47
  96.1 3.6 %collective-permute-start.9 = (f32[1,64,128]{2,1,0:T(8,128)S(1)}, f32[1,64,128]{2,1,0:T(8,128)S(1)}, u32[]{:S(2)}, u32[]{:S(2)}) collective-permute-start(f32[1,64,128]{2,1,0:T(8,128)S(1)} %get-tuple-element.27), channel_id=1, source_target_pairs={{0,4},{4,8},{8,12},{1,5},{5,9},{9,13},{2,6},{6,10},{10,14},{3,7},{... | collective-permute-start | bytes 98312 | tf_op jit(solution)/shard_map/ppermute | solution.py:45
  99.7 1.9 %collective-permute-start.8 = (f32[1,64,128]{2,1,0:T(8,128)S(1)}, f32[1,64,128]{2,1,0:T(8,128)S(1)}, u32[]{:S(2)}, u32[]{:S(2)}) collective-permute-start(f32[1,64,128]{2,1,0:T(8,128)S(1)} %get-tuple-element.26), channel_id=1, source_target_pairs={{4,0},{8,4},{12,8},{5,1},{9,5},{13,9},{6,2},{10,6},{14,10},{7,3},{... | collective-permute-start | bytes 98312 | tf_op jit(solution)/shard_map/ppermute | solution.py:47
  101.8 3.1 %collective-permute-done.8 = f32[1,64,128]{2,1,0:T(8,128)S(1)} collective-permute-done((f32[1,64,128]{2,1,0:T(8,128)S(1)}, f32[1,64,128]{2,1,0:T(8,128)S(1)}, u32[]{:S(2)}, u32[]{:S(2)}) %collective-permute-start.8) | collective-permute-done | bytes 32800 | tf_op jit(solution)/shard_map/ppermute | solution.py:47
  104.9 1.4 %fusion.4 = f32[32,64,128]{2,1,0:T(8,128)} fusion(f32[32,64,128]{2,1,0:T(8,128)S(1)} %bitcast.135, f32[32,1,128]{2,1,0:T(1,128)S(1)} %collective-permute-done.11, f32[32,1,128]{2,1,0:T(1,128)S(1)} %collective-permute-done.10, f32[1,64,128]{2,1,0:T(8,128)S(1)} %collective-permute-done.9, f32[1,64,128]{2,1,0:T(8,128)S(1)} %collective-permute-done.8, ...), kind=kLoop, calls=%fused_computation.6 | loop fusion | flops 3145728 | bytes 2196096 | tf_op jit(solution)/shard_map/mul | solution.py:392
  (133 shorter events, 19.2 us)
Async XLA Ops:
  4.5 16.5 %all-to-all-start = ((f32[4,4,64,128]{3,2,1,0:T(8,128)}), f32[4,4,64,128]{3,2,1,0:T(8,128)S(1)}, u32[]{:S(2)}, u32[]{:S(2)}) async-start(f32[4,4,64,128]{3,2,1,0:T(8,128)} %bitcast.137), calls=%async_computation | async-start | bytes 1048576 | tf_op jit(solution)/shard_map/all_to_all | solution.py:329
  10.8 0.9 copy-start.6
  13.5 0.7 copy-start.7
  21.0 0.8 copy-start.2
  21.8 27.2 %copy-start.1 = (f32[32,64,128]{2,1,0:T(8,128)S(1)}, f32[32,64,128]{2,1,0:T(8,128)}, u32[]{:S(2)}) copy-start(f32[32,64,128]{2,1,0:T(8,128)} %field_ref.3) | copy-start | bytes 3145732
  34.6 14.4 %collective-permute-start.3 = (f32[32,1,128]{2,1,0:T(1,128)S(1)}, f32[32,1,128]{2,1,0:T(1,128)S(1)}, u32[]{:S(2)}, u32[]{:S(2)}) collective-permute-start(f32[32,1,128]{2,1,0:T(1,128)S(1)} %get-tuple-element.36), channel_id=1, source_target_pairs={{0,1},{1,2},{2,3},{3,0},{4,5},{5,6},{6,7},{7,4},{8,9},{9,10},{10,1... | collective-permute-start | bytes 49160 | tf_op jit(solution)/shard_map/ppermute | solution.py:45
  36.6 12.4 %collective-permute-start.2 = (f32[32,1,128]{2,1,0:T(1,128)S(1)}, f32[32,1,128]{2,1,0:T(1,128)S(1)}, u32[]{:S(2)}, u32[]{:S(2)}) collective-permute-start(f32[32,1,128]{2,1,0:T(1,128)S(1)} %get-tuple-element.35), channel_id=1, source_target_pairs={{1,0},{2,1},{3,2},{0,3},{5,4},{6,5},{7,6},{4,7},{9,8},{10,9},{11,1... | collective-permute-start | bytes 49160 | tf_op jit(solution)/shard_map/ppermute | solution.py:47
  39.3 7.0 %collective-permute-start.1 = (f32[1,65,128]{2,1,0:T(8,128)S(1)}, f32[1,65,128]{2,1,0:T(8,128)S(1)}, u32[]{:S(2)}, u32[]{:S(2)}) collective-permute-start(f32[1,65,128]{2,1,0:T(8,128)S(1)} %concatenate.45), channel_id=1, source_target_pairs={{0,4},{4,8},{8,12},{1,5},{5,9},{9,13},{2,6},{6,10},{10,14},{3,7},{... | collective-permute-start | bytes 99848 | tf_op jit(solution)/shard_map/ppermute | solution.py:273
  43.7 5.3 %collective-permute-start = (f32[1,65,128]{2,1,0:T(8,128)S(1)}, f32[1,65,128]{2,1,0:T(8,128)S(1)}, u32[]{:S(2)}, u32[]{:S(2)}) collective-permute-start(f32[1,65,128]{2,1,0:T(8,128)S(1)} %concatenate.43), channel_id=1, source_target_pairs={{4,0},{8,4},{12,8},{5,1},{9,5},{13,9},{6,2},{10,6},{14,10},{7,3},{... | collective-permute-start | bytes 99848 | tf_op jit(solution)/shard_map/ppermute | solution.py:278
  46.3 0.6 copy-start.4
  49.0 0.8 slice-start
  56.4 4.7 %copy-start.5 = (f32[1,65,128]{2,1,0:T(8,128)S(1)}, f32[1,65,128]{2,1,0:T(8,128)}, u32[]{:S(2)}) copy-start(f32[1,65,128]{2,1,0:T(8,128)} %copy-done.4) | copy-start | bytes 99844
  56.4 9.8 %all-to-all-start.1 = ((f32[4,4,64,128]{3,2,1,0:T(8,128)}), f32[4,4,64,128]{3,2,1,0:T(8,128)S(1)}, u32[]{:S(2)}, u32[]{:S(2)}) async-start(f32[4,4,64,128]{3,2,1,0:T(8,128)} %bitcast.138), calls=%async_computation.1 | async-start | bytes 1048576 | tf_op jit(solution)/shard_map/all_to_all | solution.py:329
  66.3 0.8 copy-start.3
  76.6 12.9 %copy-start = (f32[32,64,128]{2,1,0:T(8,128)S(1)}, f32[32,64,128]{2,1,0:T(8,128)}, u32[]{:S(2)}) copy-start(f32[32,64,128]{2,1,0:T(8,128)} %shard_map.49) | copy-start | bytes 3145732
  77.1 2.5 %collective-permute-start.4 = (f32[768]{0:T(1024)S(1)}, f32[768]{0:T(1024)S(1)}, u32[]{:S(2)}, u32[]{:S(2)}) collective-permute-start(f32[768]{0:T(1024)S(1)} %pad_maximum_fusion.10), channel_id=1, source_target_pairs={{0,1},{1,0},{2,3},{3,2},{4,5},{5,4},{6,7},{7,6},{8,9},{9,8},{10,11... | collective-permute-start | bytes 9224 | tf_op jit(solution)/shard_map/ppermute | solution.py:25
  79.6 3.4 %collective-permute-start.5 = (f32[768]{0:T(1024)S(1)}, f32[768]{0:T(1024)S(1)}, u32[]{:S(2)}, u32[]{:S(2)}) collective-permute-start(f32[768]{0:T(1024)S(1)} %fusion.80), channel_id=1, source_target_pairs={{0,2},{1,3},{2,0},{3,1},{4,6},{5,7},{6,4},{7,5},{8,10},{9,11},{10,... | collective-permute-start | bytes 9224 | tf_op jit(solution)/shard_map/ppermute | solution.py:25
  83.0 4.0 %collective-permute-start.6 = (f32[768]{0:T(1024)S(1)}, f32[768]{0:T(1024)S(1)}, u32[]{:S(2)}, u32[]{:S(2)}) collective-permute-start(f32[768]{0:T(1024)S(1)} %add.746), channel_id=1, source_target_pairs={{0,4},{4,0},{8,12},{12,8},{1,5},{5,1},{9,13},{13,9},{2,6},{6,2},{1... | collective-permute-start | bytes 9224 | tf_op jit(solution)/shard_map/ppermute | solution.py:25
  87.1 2.5 %collective-permute-start.7 = (f32[768]{0:T(1024)S(1)}, f32[768]{0:T(1024)S(1)}, u32[]{:S(2)}, u32[]{:S(2)}) collective-permute-start(f32[768]{0:T(1024)S(1)} %add.747), channel_id=1, source_target_pairs={{0,8},{4,12},{8,0},{12,4},{1,9},{5,13},{9,1},{13,5},{2,10},{6,14},... | collective-permute-start | bytes 9224 | tf_op jit(solution)/shard_map/ppermute | solution.py:25
  92.9 9.0 %collective-permute-start.11 = (f32[32,1,128]{2,1,0:T(1,128)S(1)}, f32[32,1,128]{2,1,0:T(1,128)S(1)}, u32[]{:S(2)}, u32[]{:S(2)}) collective-permute-start(f32[32,1,128]{2,1,0:T(1,128)S(1)} %get-tuple-element.29), channel_id=1, source_target_pairs={{0,1},{1,2},{2,3},{3,0},{4,5},{5,6},{6,7},{7,4},{8,9},{9,10},{10,1... | collective-permute-start | bytes 49160 | tf_op jit(solution)/shard_map/ppermute | solution.py:45
  92.9 9.0 %collective-permute-start.10 = (f32[32,1,128]{2,1,0:T(1,128)S(1)}, f32[32,1,128]{2,1,0:T(1,128)S(1)}, u32[]{:S(2)}, u32[]{:S(2)}) collective-permute-start(f32[32,1,128]{2,1,0:T(1,128)S(1)} %get-tuple-element.28), channel_id=1, source_target_pairs={{1,0},{2,1},{3,2},{0,3},{5,4},{6,5},{7,6},{4,7},{9,8},{10,9},{11,1... | collective-permute-start | bytes 49160 | tf_op jit(solution)/shard_map/ppermute | solution.py:47
  96.1 5.7 %collective-permute-start.9 = (f32[1,64,128]{2,1,0:T(8,128)S(1)}, f32[1,64,128]{2,1,0:T(8,128)S(1)}, u32[]{:S(2)}, u32[]{:S(2)}) collective-permute-start(f32[1,64,128]{2,1,0:T(8,128)S(1)} %get-tuple-element.27), channel_id=1, source_target_pairs={{0,4},{4,8},{8,12},{1,5},{5,9},{9,13},{2,6},{6,10},{10,14},{3,7},{... | collective-permute-start | bytes 98312 | tf_op jit(solution)/shard_map/ppermute | solution.py:45
  99.7 5.2 %collective-permute-start.8 = (f32[1,64,128]{2,1,0:T(8,128)S(1)}, f32[1,64,128]{2,1,0:T(8,128)S(1)}, u32[]{:S(2)}, u32[]{:S(2)}) collective-permute-start(f32[1,64,128]{2,1,0:T(8,128)S(1)} %get-tuple-element.26), channel_id=1, source_target_pairs={{4,0},{8,4},{12,8},{5,1},{9,5},{13,9},{6,2},{10,6},{14,10},{7,3},{... | collective-permute-start | bytes 98312 | tf_op jit(solution)/shard_map/ppermute | solution.py:47

commit v9 on v5

--- a/solution.py
+++ b/solution.py
@@ -238,7 +238,7 @@
     target_part = column_mass(tracers, weights)
 
     patches, frac = departed(tracers, source_patch[0], shifts[0])
-    advected = from_patches(levels(spatial(patches, frac[0], frac[1]), frac[2]), band_rows, band_cols)
+    advected = from_patches(spatial(levels(patches, frac[2]), frac[0], frac[1]), band_rows, band_cols)
     first, k_wide = diffuse_first(advected, diffusivity)
     first_part = column_mass(first, weights)
 

time: 82.7 us -> 88.1 us (1.065)
  the two profiles are of different devices: /device:TPU:1 before, /device:TPU:0 now
where the time goes in v9:
time: 88.1 us; the launch traced here: 87.5 us
  waiting for transfers between devices  31.6 us (36%)
  starting transfers between devices  22.9 us (26%)
  local copies, waits for them, and re-layouts  14.2 us (16%)
  other arithmetic  11.8 us (13%)
  matrix products  6.5 us (7%)
    ppermute x4, waiting for transfers between devices, all_sum(): lax.ppermute(value, axis, [(i, i ^ distance) for i in range(count)])  12.5 us
    all_to_all x2, waiting for transfers between devices, departed(): lax.all_to_all(outgoing, 'lat', 0, 0, tiled=True)  10.7 us
    all_to_all x2, starting transfers between devices, departed(): lax.all_to_all(outgoing, 'lat', 0, 0, tiled=True)  8.82 us
    ppermute x3, waiting for transfers between devices, extended(): lax.ppermute(tail, axis, [(i, (i + 1) % count) for i in range(ends)])  5.96 us
    ppermute x3, starting transfers between devices, extended(): lax.ppermute(head, axis, [((i + 1) % count, i) for i in range(ends)])  5.87 us
    dot_general x2, matrix products, spatial(): jnp.einsum('nij,njv->niv', plane_weights(fraction_y, fraction_x), patches...  5.36 us
    ppermute x3, starting transfers between devices, extended(): lax.ppermute(tail, axis, [(i, (i + 1) % count) for i in range(ends)])  5.05 us
    add x4, other arithmetic, levels(): acc = term if acc is None else acc + term  4.85 us
  transfers between devices with their start and end apart: 14, of which 10 were waited for; matrix products, arithmetic and copies ran while one was open for 9% of the time, Pallas kernels for 0%

profile of v9, /device:TPU:0, one launch (start us, length us, event | category | flops | bytes accessed | tf_op | source)
XLA Modules:
  0.0 87.5 jit_solution(4256310545471302645)
XLA Ops:
  1.7 1.4 %copy.20 = f32[4,8,8,8,128]{4,3,2,1,0:T(8,128)S(1)} copy(f32[4,8,8,8,128]{4,3,1,2,0:T(8,128)} %bitcast.144) | data formatting | bytes 2097152 | tf_op jit(solution)/shard_map/transpose | solution.py:116
  3.1 1.4 %gather_fusion = f32[16,64,128]{2,1,0:T(8,128)} fusion(f32[32,64,128]{2,1,0:T(8,128)S(1)} %bitcast.131, s32[1024]{0:T(1024)S(1)} %pad_clamp_fusion.5), kind=kCustom, calls=%fused_computation | custom fusion | bytes 1048640 | tf_op jit(solution)/shard_map/gather | solution.py:214
  4.5 4.3 %all-to-all-start = ((f32[4,4,64,128]{3,2,1,0:T(8,128)}), f32[4,4,64,128]{3,2,1,0:T(8,128)S(1)}, u32[]{:S(2)}, u32[]{:S(2)}) async-start(f32[4,4,64,128]{3,2,1,0:T(8,128)} %bitcast.14), calls=%async_computation | async-start | bytes 1048576 | tf_op jit(solution)/shard_map/all_to_all | solution.py:220
  12.0 5.7 %all-to-all-done = f32[4,4,64,128]{3,2,1,0:T(8,128)S(1)} async-done(((f32[4,4,64,128]{3,2,1,0:T(8,128)}), f32[4,4,64,128]{3,2,1,0:T(8,128)S(1)}, u32[]{:S(2)}, u32[]{:S(2)}) %all-to-all-start) | async-done | bytes 524320 | tf_op jit(solution)/shard_map/all_to_all | solution.py:220
  18.5 1.1 %multiply_add_fusion.6 = f32[32,64,32]{2,1,0:T(8,128)S(1)} fusion(f32[32,64,128]{2,1,0:T(8,128)S(1)} %broadcast_select_fusion, f32[32]{0:T(128)S(1)} %get-tuple-element.64, f32[32]{0:T(128)S(1)} %get-tuple-element.65, f32[32]{0:T(128)S(1)} %get-tuple-element.66, f32[32]{0:T(128)S(1)} %get-tuple-element.67), kind=kLoop, calls=%fused_computation.47 | loop fusion | flops 458752 | bytes 1311232 | tf_op jit(solution)/shard_map/add | solution.py:106
  19.6 1.3 %multiply_add_fusion.7 = (f32[32,64,32]{2,1,0:T(8,128)S(1)}, f32[32,64,32]{2,1,0:T(8,128)S(1)}, f32[32,64,32]{2,1,0:T(8,128)S(1)}) fusion(f32[32,64,128]{2,1,0:T(8,128)S(1)} %broadcast_select_fusion, f32[32]{0:T(128)S(1)} %get-tuple-element.68, f32[32]{0:T(128)S(1)} %get-tuple-element.69, f32[32]{0:T(128)S(1)} %get-tuple-element.58, ...), kind=kLoop, calls=%fused_computation.48 | loop fusion | flops 851968 | bytes 1836032 | tf_op jit(solution)/shard_map/add | solution.py:106
  20.9 2.3 %fusion.13 = f32[32,64,128]{2,1,0:T(8,128)S(1)} fusion(f32[32,64,32]{2,1,0:T(8,128)S(1)} %get-tuple-element.39, f32[32,64,32]{2,1,0:T(8,128)S(1)} %get-tuple-element.38, f32[32,64,32]{2,1,0:T(8,128)S(1)} %multiply_add_fusion.6, f32[32,64,32]{2,1,0:T(8,128)S(1)} %get-tuple-element.37, f32[32]{0:T(128)S(1)} %get-tuple-element.104, ...), kind=kOutput, calls=%fused_computation.28 | convolution fusion | flops 204079104 | bytes 2229248 | tf_op jit(solution)/shard_map/nij,njv->niv/dot_general | solution.py:88
  24.1 1.4 %collective-permute-start.1 = (f32[1,65,128]{2,1,0:T(8,128)S(1)}, f32[1,65,128]{2,1,0:T(8,128)S(1)}, u32[]{:S(2)}, u32[]{:S(2)}) collective-permute-start(f32[1,65,128]{2,1,0:T(8,128)S(1)} %concatenate.49), channel_id=1, source_target_pairs={{0,4},{4,8},{8,12},{1,5},{5,9},{9,13},{2,6},{6,10},{10,14},{3,7},{... | collective-permute-start | bytes 99848 | tf_op jit(solution)/shard_map/ppermute | solution.py:167
  26.2 1.3 %collective-permute-start = (f32[1,65,128]{2,1,0:T(8,128)S(1)}, f32[1,65,128]{2,1,0:T(8,128)S(1)}, u32[]{:S(2)}, u32[]{:S(2)}) collective-permute-start(f32[1,65,128]{2,1,0:T(8,128)S(1)} %concatenate.47), channel_id=1, source_target_pairs={{4,0},{8,4},{12,8},{5,1},{9,5},{13,9},{6,2},{10,6},{14,10},{7,3},{... | collective-permute-start | bytes 99848 | tf_op jit(solution)/shard_map/ppermute | solution.py:172
  27.5 4.5 %collective-permute-start.2 = (f32[32,1,128]{2,1,0:T(1,128)S(1)}, f32[32,1,128]{2,1,0:T(1,128)S(1)}, u32[]{:S(2)}, u32[]{:S(2)}) collective-permute-start(f32[32,1,128]{2,1,0:T(1,128)S(1)} %get-tuple-element.35), channel_id=1, source_target_pairs={{1,0},{2,1},{3,2},{0,3},{5,4},{6,5},{7,6},{4,7},{9,8},{10,9},{11,1... | collective-permute-start | bytes 49160 | tf_op jit(solution)/shard_map/ppermute | solution.py:44
  32.7 0.8 collective-permute-done.2
  33.4 4.1 %collective-permute-done.3 = f32[32,1,128]{2,1,0:T(1,128)S(1)} collective-permute-done((f32[32,1,128]{2,1,0:T(1,128)S(1)}, f32[32,1,128]{2,1,0:T(1,128)S(1)}, u32[]{:S(2)}, u32[]{:S(2)}) %collective-permute-start.3) | collective-permute-done | bytes 16416 | tf_op jit(solution)/shard_map/ppermute | solution.py:42
  38.4 1.4 %gather_fusion.3 = f32[16,64,128]{2,1,0:T(8,128)} fusion(f32[32,64,128]{2,1,0:T(8,128)S(1)} %bitcast.133, s32[1024]{0:T(1024)S(1)} %pad_clamp_fusion.2), kind=kCustom, calls=%fused_computation.3 | custom fusion | bytes 1048640 | tf_op jit(solution)/shard_map/gather | solution.py:214
  39.8 4.5 %all-to-all-start.1 = ((f32[4,4,64,128]{3,2,1,0:T(8,128)}), f32[4,4,64,128]{3,2,1,0:T(8,128)S(1)}, u32[]{:S(2)}, u32[]{:S(2)}) async-start(f32[4,4,64,128]{3,2,1,0:T(8,128)} %bitcast.40), calls=%async_computation.1 | async-start | bytes 1048576 | tf_op jit(solution)/shard_map/all_to_all | solution.py:220
  45.5 1.4 %maximum_multiply_fusion = f32[34]{0:T(128)S(1)} fusion(f32[1]{0:T(128)} %bitcast.47, f32[32]{0:T(128)S(1)} %copy-done.4, f32[1]{0:T(128)} %bitcast.46, s32[]{:T(128)S(6)} %sub.190), kind=kLoop, calls=%fused_computation.294 | loop fusion | flops 272 | bytes 276 | tf_op jit(solution)/shard_map/mul | solution.py:250
  48.1 5.0 %all-to-all-done.1 = f32[4,4,64,128]{3,2,1,0:T(8,128)S(1)} async-done(((f32[4,4,64,128]{3,2,1,0:T(8,128)}), f32[4,4,64,128]{3,2,1,0:T(8,128)S(1)}, u32[]{:S(2)}, u32[]{:S(2)}) %all-to-all-start.1) | async-done | bytes 524320 | tf_op jit(solution)/shard_map/all_to_all | solution.py:220
  53.1 1.6 %gather_fusion.4 = f32[32,64,128]{2,1,0:T(8,128)} fusion(f32[16,64,128]{2,1,0:T(8,128)S(1)} %bitcast.136, s32[1024]{0:T(1024)S(1)} %pad_clamp_fusion.1), kind=kCustom, calls=%fused_computation.4 | custom fusion | bytes 2097280 | tf_op jit(solution)/shard_map/gather | solution.py:224
  54.7 3.1 %fusion.21 = f32[32,64,128]{2,1,0:T(8,128)S(1)} fusion(f32[32,64,128]{2,1,0:T(8,128)} %gather_fusion.4, f32[32,64,128]{2,1,0:T(8,128)S(1)} %gather_fusion.5, f32[64,64]{1,0:T(8,128)S(1)} %get-tuple-element.83, f32[32]{0:T(128)S(1)} %get-tuple-element.96, f32[64,64]{1,0:T(8,128)S(1)} %get-tuple-element.84, f32[32]{0:T(128)S(1)} %get-tuple-element.97, ...), kind=kOutput, calls=%fused_computation.43 | convolution fusion | flops 203554816 | bytes 3277856 | tf_op jit(solution)/shard_map/nij,njv->niv/dot_general | solution.py:88
  57.8 1.0 %fusion.158 = f32[32,1,128]{2,1,0:T(1,128)S(1)} fusion(f32[32,64,1]{1,2,0:T(1,128)S(1)} %bitcast.147, f32[32,64,128]{2,1,0:T(8,128)S(1)} %fusion.21), kind=kOutput, calls=%fused_computation.350 | convolution fusion | flops 3145728 | bytes 1073152 | tf_op jit(solution)/shard_map/pi,piv->pv/dot_general | solution.py:253
  59.3 3.6 %collective-permute-done.4 = f32[768]{0:T(1024)S(1)} collective-permute-done((f32[768]{0:T(1024)S(1)}, f32[768]{0:T(1024)S(1)}, u32[]{:S(2)}, u32[]{:S(2)}) %collective-permute-start.4) | collective-permute-done | bytes 3104 | tf_op jit(solution)/shard_map/ppermute | solution.py:22
  62.9 4.5 %collective-permute-done.5 = f32[768]{0:T(1024)S(1)} collective-permute-done((f32[768]{0:T(1024)S(1)}, f32[768]{0:T(1024)S(1)}, u32[]{:S(2)}, u32[]{:S(2)}) %collective-permute-start.5) | collective-permute-done | bytes 3104 | tf_op jit(solution)/shard_map/ppermute | solution.py:22
  67.4 1.2 %collective-permute-done.6 = f32[768]{0:T(1024)S(1)} collective-permute-done((f32[768]{0:T(1024)S(1)}, f32[768]{0:T(1024)S(1)}, u32[]{:S(2)}, u32[]{:S(2)}) %collective-permute-start.6) | collective-permute-done | bytes 3104 | tf_op jit(solution)/shard_map/ppermute | solution.py:22
  69.0 3.2 %collective-permute-done.7 = f32[768]{0:T(1024)S(1)} collective-permute-done((f32[768]{0:T(1024)S(1)}, f32[768]{0:T(1024)S(1)}, u32[]{:S(2)}, u32[]{:S(2)}) %collective-permute-start.7) | collective-permute-done | bytes 3104 | tf_op jit(solution)/shard_map/ppermute | solution.py:22
  72.4 1.1 %multiply_add_fusion.2 = f32[32,64,32]{2,1,0:T(8,128)S(1)} fusion(f32[32,64,128]{2,1,0:T(8,128)S(1)} %broadcast_multiply_fusion, f32[32]{0:T(128)S(1)} %get-tuple-element.50, f32[32]{0:T(128)S(1)} %get-tuple-element.51, f32[32]{0:T(128)S(1)} %get-tuple-element.52, f32[32]{0:T(128)S(1)} %get-tuple-element.53), kind=kLoop, calls=%fused_computation.39 | loop fusion | flops 458752 | bytes 1311232 | tf_op jit(solution)/shard_map/add | solution.py:106
  73.5 1.3 %multiply_add_fusion.3 = (f32[32,64,32]{2,1,0:T(8,128)S(1)}, f32[32,64,32]{2,1,0:T(8,128)S(1)}, f32[32,64,32]{2,1,0:T(8,128)S(1)}) fusion(f32[32,64,128]{2,1,0:T(8,128)S(1)} %broadcast_multiply_fusion, f32[32]{0:T(128)S(1)} %get-tuple-element.54, f32[32]{0:T(128)S(1)} %get-tuple-element.55, f32[32]{0:T(128)S(1)} %get-tuple-element.44, ...), kind=kLoop, calls=%fused_computation.40 | loop fusion | flops 851968 | bytes 1836032 | tf_op jit(solution)/shard_map/add | solution.py:106
  74.8 0.9 %pad_maximum_fusion.8 = f32[32,64,128]{2,1,0:T(8,128)S(1)} fusion(f32[32,64,32]{2,1,0:T(8,128)S(1)} %get-tuple-element.32, f32[32,64,32]{2,1,0:T(8,128)S(1)} %get-tuple-element.31, f32[32,64,32]{2,1,0:T(8,128)S(1)} %multiply_add_fusion.2, f32[32,64,32]{2,1,0:T(8,128)S(1)} %get-tuple-element.30), kind=kLoop, calls=%fused_computation.36 | loop fusion | flops 786432 | bytes 2097152 | tf_op jit(solution)/shard_map/concatenate | solution.py:108
  76.1 1.3 %collective-permute-start.8 = (f32[1,64,128]{2,1,0:T(8,128)S(1)}, f32[1,64,128]{2,1,0:T(8,128)S(1)}, u32[]{:S(2)}, u32[]{:S(2)}) collective-permute-start(f32[1,64,128]{2,1,0:T(8,128)S(1)} %get-tuple-element.26), channel_id=1, source_target_pairs={{4,0},{8,4},{12,8},{5,1},{9,5},{13,9},{6,2},{10,6},{14,10},{7,3},{... | collective-permute-start | bytes 98312 | tf_op jit(solution)/shard_map/ppermute | solution.py:44
  77.4 3.0 %collective-permute-start.9 = (f32[1,64,128]{2,1,0:T(8,128)S(1)}, f32[1,64,128]{2,1,0:T(8,128)S(1)}, u32[]{:S(2)}, u32[]{:S(2)}) collective-permute-start(f32[1,64,128]{2,1,0:T(8,128)S(1)} %get-tuple-element.27), channel_id=1, source_target_pairs={{0,4},{4,8},{8,12},{1,5},{5,9},{9,13},{2,6},{6,10},{10,14},{3,7},{... | collective-permute-start | bytes 98312 | tf_op jit(solution)/shard_map/ppermute | solution.py:42
  80.5 2.0 %collective-permute-start.11 = (f32[32,1,128]{2,1,0:T(1,128)S(1)}, f32[32,1,128]{2,1,0:T(1,128)S(1)}, u32[]{:S(2)}, u32[]{:S(2)}) collective-permute-start(f32[32,1,128]{2,1,0:T(1,128)S(1)} %get-tuple-element.29), channel_id=1, source_target_pairs={{0,1},{1,2},{2,3},{3,0},{4,5},{5,6},{6,7},{7,4},{8,9},{9,10},{10,1... | collective-permute-start | bytes 49160 | tf_op jit(solution)/shard_map/ppermute | solution.py:42
  82.5 1.7 %collective-permute-done.10 = f32[32,1,128]{2,1,0:T(1,128)S(1)} collective-permute-done((f32[32,1,128]{2,1,0:T(1,128)S(1)}, f32[32,1,128]{2,1,0:T(1,128)S(1)}, u32[]{:S(2)}, u32[]{:S(2)}) %collective-permute-start.10) | collective-permute-done | bytes 16416 | tf_op jit(solution)/shard_map/ppermute | solution.py:44
  84.2 1.9 %collective-permute-done.11 = f32[32,1,128]{2,1,0:T(1,128)S(1)} collective-permute-done((f32[32,1,128]{2,1,0:T(1,128)S(1)}, f32[32,1,128]{2,1,0:T(1,128)S(1)}, u32[]{:S(2)}, u32[]{:S(2)}) %collective-permute-start.11) | collective-permute-done | bytes 16416 | tf_op jit(solution)/shard_map/ppermute | solution.py:42
  86.1 1.4 %fusion.4 = f32[32,64,128]{2,1,0:T(8,128)} fusion(f32[32,64,128]{2,1,0:T(8,128)S(1)} %bitcast.139, f32[32,1,128]{2,1,0:T(1,128)S(1)} %collective-permute-done.11, f32[32,1,128]{2,1,0:T(1,128)S(1)} %collective-permute-done.10, f32[1,64,128]{2,1,0:T(8,128)S(1)} %collective-permute-done.9, f32[1,64,128]{2,1,0:T(8,128)S(1)} %collective-permute-done.8, ...), kind=kLoop, calls=%fused_computation.12 | loop fusion | flops 3145728 | bytes 2196096 | tf_op jit(solution)/shard_map/mul | solution.py:273
  (122 shorter events, 12.4 us)
Async XLA Ops:
  4.5 4.5 %copy-start.3 = (f32[2,3,16,32]{3,2,1,0:T(8,128)S(1)}, f32[2,3,16,32]{3,2,1,0:T(8,128)}, u32[]{:S(2)}) copy-start(f32[2,3,16,32]{3,2,1,0:T(8,128)} %param.5) | copy-start | bytes 36868
  4.5 13.2 %all-to-all-start = ((f32[4,4,64,128]{3,2,1,0:T(8,128)}), f32[4,4,64,128]{3,2,1,0:T(8,128)S(1)}, u32[]{:S(2)}, u32[]{:S(2)}) async-start(f32[4,4,64,128]{3,2,1,0:T(8,128)} %bitcast.14), calls=%async_computation | async-start | bytes 1048576 | tf_op jit(solution)/shard_map/all_to_all | solution.py:220
  10.6 0.7 copy-start.4
  23.2 14.4 %copy-start = (f32[32,64,128]{2,1,0:T(8,128)S(1)}, f32[32,64,128]{2,1,0:T(8,128)}, u32[]{:S(2)}) copy-start(f32[32,64,128]{2,1,0:T(8,128)} %param.4) | copy-start | bytes 3145732
  24.1 8.6 %collective-permute-start.1 = (f32[1,65,128]{2,1,0:T(8,128)S(1)}, f32[1,65,128]{2,1,0:T(8,128)S(1)}, u32[]{:S(2)}, u32[]{:S(2)}) collective-permute-start(f32[1,65,128]{2,1,0:T(8,128)S(1)} %concatenate.49), channel_id=1, source_target_pairs={{0,4},{4,8},{8,12},{1,5},{5,9},{9,13},{2,6},{6,10},{10,14},{3,7},{... | collective-permute-start | bytes 99848 | tf_op jit(solution)/shard_map/ppermute | solution.py:167
  26.2 5.9 %collective-permute-start = (f32[1,65,128]{2,1,0:T(8,128)S(1)}, f32[1,65,128]{2,1,0:T(8,128)S(1)}, u32[]{:S(2)}, u32[]{:S(2)}) collective-permute-start(f32[1,65,128]{2,1,0:T(8,128)S(1)} %concatenate.47), channel_id=1, source_target_pairs={{4,0},{8,4},{12,8},{5,1},{9,5},{13,9},{6,2},{10,6},{14,10},{7,3},{... | collective-permute-start | bytes 99848 | tf_op jit(solution)/shard_map/ppermute | solution.py:172
  27.5 6.0 %collective-permute-start.2 = (f32[32,1,128]{2,1,0:T(1,128)S(1)}, f32[32,1,128]{2,1,0:T(1,128)S(1)}, u32[]{:S(2)}, u32[]{:S(2)}) collective-permute-start(f32[32,1,128]{2,1,0:T(1,128)S(1)} %get-tuple-element.35), channel_id=1, source_target_pairs={{1,0},{2,1},{3,2},{0,3},{5,4},{6,5},{7,6},{4,7},{9,8},{10,9},{11,1... | collective-permute-start | bytes 49160 | tf_op jit(solution)/shard_map/ppermute | solution.py:44
  32.0 5.5 %collective-permute-start.3 = (f32[32,1,128]{2,1,0:T(1,128)S(1)}, f32[32,1,128]{2,1,0:T(1,128)S(1)}, u32[]{:S(2)}, u32[]{:S(2)}) collective-permute-start(f32[32,1,128]{2,1,0:T(1,128)S(1)} %get-tuple-element.36), channel_id=1, source_target_pairs={{0,1},{1,2},{2,3},{3,0},{4,5},{5,6},{6,7},{7,4},{8,9},{9,10},{10,1... | collective-permute-start | bytes 49160 | tf_op jit(solution)/shard_map/ppermute | solution.py:42
  32.0 0.6 copy-start.1
  32.7 4.9 %slice-start = ((f32[1,65,128]{2,1,0:T(8,128)}), f32[1,64,128]{2,1,0:T(8,128)S(1)}, s32[]{:S(2)}) async-start(f32[1,65,128]{2,1,0:T(8,128)} %copy-done.1), calls=%async_computation.2 | async-start | bytes 65536 | tf_op jit(solution)/shard_map/slice | solution.py:175
  39.8 5.1 %copy-start.2 = (f32[1,65,128]{2,1,0:T(8,128)S(1)}, f32[1,65,128]{2,1,0:T(8,128)}, u32[]{:S(2)}) copy-start(f32[1,65,128]{2,1,0:T(8,128)} %copy-done.1) | copy-start | bytes 99844
  39.8 13.3 %all-to-all-start.1 = ((f32[4,4,64,128]{3,2,1,0:T(8,128)}), f32[4,4,64,128]{3,2,1,0:T(8,128)S(1)}, u32[]{:S(2)}, u32[]{:S(2)}) async-start(f32[4,4,64,128]{3,2,1,0:T(8,128)} %bitcast.40), calls=%async_computation.1 | async-start | bytes 1048576 | tf_op jit(solution)/shard_map/all_to_all | solution.py:220
  59.2 3.7 %collective-permute-start.4 = (f32[768]{0:T(1024)S(1)}, f32[768]{0:T(1024)S(1)}, u32[]{:S(2)}, u32[]{:S(2)}) collective-permute-start(f32[768]{0:T(1024)S(1)} %pad_maximum_fusion.9), channel_id=1, source_target_pairs={{0,1},{1,0},{2,3},{3,2},{4,5},{5,4},{6,7},{7,6},{8,9},{9,8},{10,11... | collective-permute-start | bytes 9224 | tf_op jit(solution)/shard_map/ppermute | solution.py:22
  62.9 4.6 %collective-permute-start.5 = (f32[768]{0:T(1024)S(1)}, f32[768]{0:T(1024)S(1)}, u32[]{:S(2)}, u32[]{:S(2)}) collective-permute-start(f32[768]{0:T(1024)S(1)} %fusion.143), channel_id=1, source_target_pairs={{0,2},{1,3},{2,0},{3,1},{4,6},{5,7},{6,4},{7,5},{8,10},{9,11},{10,... | collective-permute-start | bytes 9224 | tf_op jit(solution)/shard_map/ppermute | solution.py:22
  67.4 1.2 %collective-permute-start.6 = (f32[768]{0:T(1024)S(1)}, f32[768]{0:T(1024)S(1)}, u32[]{:S(2)}, u32[]{:S(2)}) collective-permute-start(f32[768]{0:T(1024)S(1)} %add.862), channel_id=1, source_target_pairs={{0,4},{4,0},{8,12},{12,8},{1,5},{5,1},{9,13},{13,9},{2,6},{6,2},{1... | collective-permute-start | bytes 9224 | tf_op jit(solution)/shard_map/ppermute | solution.py:22
  68.6 3.6 %collective-permute-start.7 = (f32[768]{0:T(1024)S(1)}, f32[768]{0:T(1024)S(1)}, u32[]{:S(2)}, u32[]{:S(2)}) collective-permute-start(f32[768]{0:T(1024)S(1)} %add.863), channel_id=1, source_target_pairs={{0,8},{4,12},{8,0},{12,4},{1,9},{5,13},{9,1},{13,5},{2,10},{6,14},... | collective-permute-start | bytes 9224 | tf_op jit(solution)/shard_map/ppermute | solution.py:22
  76.1 10.0 %collective-permute-start.8 = (f32[1,64,128]{2,1,0:T(8,128)S(1)}, f32[1,64,128]{2,1,0:T(8,128)S(1)}, u32[]{:S(2)}, u32[]{:S(2)}) collective-permute-start(f32[1,64,128]{2,1,0:T(8,128)S(1)} %get-tuple-element.26), channel_id=1, source_target_pairs={{4,0},{8,4},{12,8},{5,1},{9,5},{13,9},{6,2},{10,6},{14,10},{7,3},{... | collective-permute-start | bytes 98312 | tf_op jit(solution)/shard_map/ppermute | solution.py:44
  77.4 8.7 %collective-permute-start.9 = (f32[1,64,128]{2,1,0:T(8,128)S(1)}, f32[1,64,128]{2,1,0:T(8,128)S(1)}, u32[]{:S(2)}, u32[]{:S(2)}) collective-permute-start(f32[1,64,128]{2,1,0:T(8,128)S(1)} %get-tuple-element.27), channel_id=1, source_target_pairs={{0,4},{4,8},{8,12},{1,5},{5,9},{9,13},{2,6},{6,10},{10,14},{3,7},{... | collective-permute-start | bytes 98312 | tf_op jit(solution)/shard_map/ppermute | solution.py:42
  80.4 3.8 %collective-permute-start.10 = (f32[32,1,128]{2,1,0:T(1,128)S(1)}, f32[32,1,128]{2,1,0:T(1,128)S(1)}, u32[]{:S(2)}, u32[]{:S(2)}) collective-permute-start(f32[32,1,128]{2,1,0:T(1,128)S(1)} %get-tuple-element.28), channel_id=1, source_target_pairs={{1,0},{2,1},{3,2},{0,3},{5,4},{6,5},{7,6},{4,7},{9,8},{10,9},{11,1... | collective-permute-start | bytes 49160 | tf_op jit(solution)/shard_map/ppermute | solution.py:44
  80.5 5.6 %collective-permute-start.11 = (f32[32,1,128]{2,1,0:T(1,128)S(1)}, f32[32,1,128]{2,1,0:T(1,128)S(1)}, u32[]{:S(2)}, u32[]{:S(2)}) collective-permute-start(f32[32,1,128]{2,1,0:T(1,128)S(1)} %get-tuple-element.29), channel_id=1, source_target_pairs={{0,1},{1,2},{2,3},{3,0},{4,5},{5,6},{6,7},{7,4},{8,9},{9,10},{10,1... | collective-permute-start | bytes 49160 | tf_op jit(solution)/shard_map/ppermute | solution.py:42

commit v10 on v5

--- a/solution.py
+++ b/solution.py
@@ -257,7 +257,7 @@
         "plm,pmt->lmt", weight_z, weighted, precision=lax.Precision.HIGHEST
     )
     totals = all_sum(
-        jnp.concatenate([target_part, first_part, mix_part.reshape(-1)]), ("lon", "lat")
+        jnp.concatenate([target_part, first_part, mix_part.reshape(-1)]), ("lat", "lon")
     )
     target = totals[:value_count]
     first_mass = totals[value_count : 2 * value_count]

time: 82.7 us -> 82.7 us (level)
    ppermute x3, starting transfers between devices: 5.78 us -> 8.14 us  [extended(): lax.ppermute(tail, axis, [(i, (i + 1) % count) for i in range(ends)])]
    ppermute x4, starting transfers between devices: 4.22 us -> 1.86 us  [all_sum(): lax.ppermute(value, axis, [(i, i ^ distance) for i in range(count)])]
where the time goes in v10:
time: 82.7 us; the launch traced here: 82.2 us
  starting transfers between devices  30.3 us (37%)
  waiting for transfers between devices  21.1 us (26%)
  local copies, waits for them, and re-layouts  12.9 us (16%)
  other arithmetic  12.3 us (15%)
  matrix products  4.93 us (6%)
    ppermute x4, waiting for transfers between devices, all_sum(): lax.ppermute(value, axis, [(i, i ^ distance) for i in range(count)])  8.41 us
    ppermute x3, starting transfers between devices, extended(): lax.ppermute(tail, axis, [(i, (i + 1) % count) for i in range(ends)])  8.14 us
    all_to_all x2, starting transfers between devices, departed(): lax.all_to_all(outgoing, 'lat', 0, 0, tiled=True)  8.04 us
    ppermute x3, starting transfers between devices, extended(): lax.ppermute(head, axis, [((i + 1) % count, i) for i in range(ends)])  7.27 us
    all_to_all x2, waiting for transfers between devices, departed(): lax.all_to_all(outgoing, 'lat', 0, 0, tiled=True)  6.95 us
    add x4, other arithmetic, levels(): acc = term if acc is None else acc + term  4.85 us
    dot_general x2, matrix products, spatial(): jnp.einsum('nij,njv->niv', plane_weights(fraction_y, fraction_x), patches...  3.79 us
    ppermute x3, waiting for transfers between devices, extended(): lax.ppermute(head, axis, [((i + 1) % count, i) for i in range(ends)])  3.09 us
  transfers between devices with their start and end apart: 14, of which 8 were waited for; matrix products, arithmetic and copies ran while one was open for 10% of the time, Pallas kernels for 0%

profile of v10, /device:TPU:1, one launch (start us, length us, event | category | flops | bytes accessed | tf_op | source)
XLA Modules:
  0.0 82.2 jit_solution(12907675000594777284)
XLA Ops:
  0.0 1.4 %copy.20 = f32[4,8,8,8,128]{4,3,2,1,0:T(8,128)S(1)} copy(f32[4,8,8,8,128]{4,3,1,2,0:T(8,128)} %bitcast.145) | data formatting | bytes 2097152 | tf_op jit(solution)/shard_map/transpose | solution.py:116
  2.4 1.4 %gather_fusion = f32[16,64,128]{2,1,0:T(8,128)} fusion(f32[32,64,128]{2,1,0:T(8,128)S(1)} %bitcast.131, s32[1024]{0:T(1024)S(1)} %pad_clamp_fusion.5), kind=kCustom, calls=%fused_computation | custom fusion | bytes 1048640 | tf_op jit(solution)/shard_map/gather | solution.py:214
  3.8 4.4 %all-to-all-start = ((f32[4,4,64,128]{3,2,1,0:T(8,128)}), f32[4,4,64,128]{3,2,1,0:T(8,128)S(1)}, u32[]{:S(2)}, u32[]{:S(2)}) async-start(f32[4,4,64,128]{3,2,1,0:T(8,128)} %bitcast.14), calls=%async_computation | async-start | bytes 1048576 | tf_op jit(solution)/shard_map/all_to_all | solution.py:220
  11.4 4.6 %all-to-all-done = f32[4,4,64,128]{3,2,1,0:T(8,128)S(1)} async-done(((f32[4,4,64,128]{3,2,1,0:T(8,128)}), f32[4,4,64,128]{3,2,1,0:T(8,128)S(1)}, u32[]{:S(2)}, u32[]{:S(2)}) %all-to-all-start) | async-done | bytes 524320 | tf_op jit(solution)/shard_map/all_to_all | solution.py:220
  16.6 1.9 %fusion.15 = f32[32,64,128]{2,1,0:T(8,128)S(1)} fusion(f32[32,64,128]{2,1,0:T(8,128)S(1)} %gather_fusion.1, f32[32,64,128]{2,1,0:T(8,128)S(1)} %gather_fusion.2, f32[32]{0:T(128)S(1)} %get-tuple-element.107, f32[32]{0:T(128)S(1)} %get-tuple-element.108, f32[32]{0:T(128)S(1)} %get-tuple-element.106, f32[32]{0:T(128)S(1)} %get-tuple-element.76, ...), kind=kOutput, calls=%fused_computation.42 | convolution fusion | flops 203554816 | bytes 3277856 | tf_op jit(solution)/shard_map/nij,njv->niv/dot_general | solution.py:88
  18.5 1.1 %multiply_add_fusion.6 = f32[32,64,32]{2,1,0:T(8,128)S(1)} fusion(f32[32,64,128]{2,1,0:T(8,128)S(1)} %fusion.15, f32[32]{0:T(128)S(1)} %get-tuple-element.64, f32[32]{0:T(128)S(1)} %get-tuple-element.65, f32[32]{0:T(128)S(1)} %get-tuple-element.66, f32[32]{0:T(128)S(1)} %get-tuple-element.67), kind=kLoop, calls=%fused_computation.40 | loop fusion | flops 458752 | bytes 1311232 | tf_op jit(solution)/shard_map/add | solution.py:106
  19.7 1.3 %multiply_add_fusion.7 = (f32[32,64,32]{2,1,0:T(8,128)S(1)}, f32[32,64,32]{2,1,0:T(8,128)S(1)}, f32[32,64,32]{2,1,0:T(8,128)S(1)}) fusion(f32[32,64,128]{2,1,0:T(8,128)S(1)} %fusion.15, f32[32]{0:T(128)S(1)} %get-tuple-element.68, f32[32]{0:T(128)S(1)} %get-tuple-element.69, f32[32]{0:T(128)S(1)} %get-tuple-element.58, f32[32]{0:T(128)S(1)} %get-tuple-element.61, ...), kind=kLoop, calls=%fused_computation.41 | loop fusion | flops 851968 | bytes 1836032 | tf_op jit(solution)/shard_map/add | solution.py:106
  21.0 0.9 %pad_maximum_fusion.8 = f32[32,64,128]{2,1,0:T(8,128)S(1)} fusion(f32[32,64,32]{2,1,0:T(8,128)S(1)} %get-tuple-element.39, f32[32,64,32]{2,1,0:T(8,128)S(1)} %get-tuple-element.38, f32[32,64,32]{2,1,0:T(8,128)S(1)} %multiply_add_fusion.6, f32[32,64,32]{2,1,0:T(8,128)S(1)} %get-tuple-element.37), kind=kLoop, calls=%fused_computation.28 | loop fusion | flops 786432 | bytes 2097152 | tf_op jit(solution)/shard_map/concatenate | solution.py:108
  22.0 2.2 %collective-permute-start.3 = (f32[32,1,128]{2,1,0:T(1,128)S(1)}, f32[32,1,128]{2,1,0:T(1,128)S(1)}, u32[]{:S(2)}, u32[]{:S(2)}) collective-permute-start(f32[32,1,128]{2,1,0:T(1,128)S(1)} %get-tuple-element.36), channel_id=1, source_target_pairs={{0,1},{1,2},{2,3},{3,0},{4,5},{5,6},{6,7},{7,4},{8,9},{9,10},{10,1... | collective-permute-start | bytes 49160 | tf_op jit(solution)/shard_map/ppermute | solution.py:42
  24.3 2.1 %collective-permute-start.2 = (f32[32,1,128]{2,1,0:T(1,128)S(1)}, f32[32,1,128]{2,1,0:T(1,128)S(1)}, u32[]{:S(2)}, u32[]{:S(2)}) collective-permute-start(f32[32,1,128]{2,1,0:T(1,128)S(1)} %get-tuple-element.35), channel_id=1, source_target_pairs={{1,0},{2,1},{3,2},{0,3},{5,4},{6,5},{7,6},{4,7},{9,8},{10,9},{11,1... | collective-permute-start | bytes 49160 | tf_op jit(solution)/shard_map/ppermute | solution.py:44
  27.0 3.0 %collective-permute-start.1 = (f32[1,65,128]{2,1,0:T(8,128)S(1)}, f32[1,65,128]{2,1,0:T(8,128)S(1)}, u32[]{:S(2)}, u32[]{:S(2)}) collective-permute-start(f32[1,65,128]{2,1,0:T(8,128)S(1)} %concatenate.49), channel_id=1, source_target_pairs={{0,4},{4,8},{8,12},{1,5},{5,9},{9,13},{2,6},{6,10},{10,14},{3,7},{... | collective-permute-start | bytes 99848 | tf_op jit(solution)/shard_map/ppermute | solution.py:167
  30.6 1.9 %collective-permute-start = (f32[1,65,128]{2,1,0:T(8,128)S(1)}, f32[1,65,128]{2,1,0:T(8,128)S(1)}, u32[]{:S(2)}, u32[]{:S(2)}) collective-permute-start(f32[1,65,128]{2,1,0:T(8,128)S(1)} %concatenate.47), channel_id=1, source_target_pairs={{4,0},{8,4},{12,8},{5,1},{9,5},{13,9},{6,2},{10,6},{14,10},{7,3},{... | collective-permute-start | bytes 99848 | tf_op jit(solution)/shard_map/ppermute | solution.py:172
  33.2 2.7 %collective-permute-done = f32[1,65,128]{2,1,0:T(8,128)S(1)} collective-permute-done((f32[1,65,128]{2,1,0:T(8,128)S(1)}, f32[1,65,128]{2,1,0:T(8,128)S(1)}, u32[]{:S(2)}, u32[]{:S(2)}) %collective-permute-start) | collective-permute-done | bytes 33312 | tf_op jit(solution)/shard_map/ppermute | solution.py:172
  37.5 1.4 %gather_fusion.3 = f32[16,64,128]{2,1,0:T(8,128)} fusion(f32[32,64,128]{2,1,0:T(8,128)S(1)} %bitcast.133, s32[1024]{0:T(1024)S(1)} %pad_clamp_fusion.2), kind=kCustom, calls=%fused_computation.3 | custom fusion | bytes 1048640 | tf_op jit(solution)/shard_map/gather | solution.py:214
  38.9 3.6 %all-to-all-start.1 = ((f32[4,4,64,128]{3,2,1,0:T(8,128)}), f32[4,4,64,128]{3,2,1,0:T(8,128)S(1)}, u32[]{:S(2)}, u32[]{:S(2)}) async-start(f32[4,4,64,128]{3,2,1,0:T(8,128)} %bitcast.40), calls=%async_computation.1 | async-start | bytes 1048576 | tf_op jit(solution)/shard_map/all_to_all | solution.py:220
  44.3 1.3 %maximum_multiply_fusion = f32[34]{0:T(128)S(1)} fusion(f32[1]{0:T(128)} %bitcast.47, f32[32]{0:T(128)S(1)} %copy-done.5, f32[1]{0:T(128)} %bitcast.46, s32[]{:T(128)S(6)} %sub.190), kind=kLoop, calls=%fused_computation.289 | loop fusion | flops 272 | bytes 276 | tf_op jit(solution)/shard_map/mul | solution.py:250
  46.1 2.3 %all-to-all-done.1 = f32[4,4,64,128]{3,2,1,0:T(8,128)S(1)} async-done(((f32[4,4,64,128]{3,2,1,0:T(8,128)}), f32[4,4,64,128]{3,2,1,0:T(8,128)S(1)}, u32[]{:S(2)}, u32[]{:S(2)}) %all-to-all-start.1) | async-done | bytes 524320 | tf_op jit(solution)/shard_map/all_to_all | solution.py:220
  49.0 1.9 %fusion.13 = f32[32,64,128]{2,1,0:T(8,128)S(1)} fusion(f32[32,64,128]{2,1,0:T(8,128)S(1)} %gather_fusion.4, f32[32,64,128]{2,1,0:T(8,128)S(1)} %gather_fusion.5, f32[64,64]{1,0:T(8,128)S(1)} %get-tuple-element.83, f32[32]{0:T(128)S(1)} %get-tuple-element.96, f32[64,64]{1,0:T(8,128)S(1)} %get-tuple-element.84, f32[32]{0:T(128)S(1)} %get-tuple-element.97, ...), kind=kOutput, calls=%fused_computation.36 | convolution fusion | flops 203554816 | bytes 3277856 | tf_op jit(solution)/shard_map/nij,njv->niv/dot_general | solution.py:88
  50.9 1.0 %fusion.152 = f32[32,1,128]{2,1,0:T(1,128)S(1)} fusion(f32[32,64,1]{1,2,0:T(1,128)S(1)} %bitcast.147, f32[32,64,128]{2,1,0:T(8,128)S(1)} %fusion.13), kind=kOutput, calls=%fused_computation.344 | convolution fusion | flops 3145728 | bytes 1073152 | tf_op jit(solution)/shard_map/pi,piv->pv/dot_general | solution.py:253
  52.3 1.2 %collective-permute-start.4 = (f32[768]{0:T(1024)S(1)}, f32[768]{0:T(1024)S(1)}, u32[]{:S(2)}, u32[]{:S(2)}) collective-permute-start(f32[768]{0:T(1024)S(1)} %pad_maximum_fusion.10), channel_id=1, source_target_pairs={{0,4},{4,0},{8,12},{12,8},{1,5},{5,1},{9,13},{13,9},{2,6},{6,2},{1... | collective-permute-start | bytes 9224 | tf_op jit(solution)/shard_map/ppermute | solution.py:22
  53.5 0.8 %collective-permute-done.4 = f32[768]{0:T(1024)S(1)} collective-permute-done((f32[768]{0:T(1024)S(1)}, f32[768]{0:T(1024)S(1)}, u32[]{:S(2)}, u32[]{:S(2)}) %collective-permute-start.4) | collective-permute-done | bytes 3104 | tf_op jit(solution)/shard_map/ppermute | solution.py:22
  54.3 2.5 %collective-permute-done.5 = f32[768]{0:T(1024)S(1)} collective-permute-done((f32[768]{0:T(1024)S(1)}, f32[768]{0:T(1024)S(1)}, u32[]{:S(2)}, u32[]{:S(2)}) %collective-permute-start.5) | collective-permute-done | bytes 3104 | tf_op jit(solution)/shard_map/ppermute | solution.py:22
  56.8 2.5 %collective-permute-done.6 = f32[768]{0:T(1024)S(1)} collective-permute-done((f32[768]{0:T(1024)S(1)}, f32[768]{0:T(1024)S(1)}, u32[]{:S(2)}, u32[]{:S(2)}) %collective-permute-start.6) | collective-permute-done | bytes 3104 | tf_op jit(solution)/shard_map/ppermute | solution.py:22
  59.9 2.7 %collective-permute-done.7 = f32[768]{0:T(1024)S(1)} collective-permute-done((f32[768]{0:T(1024)S(1)}, f32[768]{0:T(1024)S(1)}, u32[]{:S(2)}, u32[]{:S(2)}) %collective-permute-start.7) | collective-permute-done | bytes 3104 | tf_op jit(solution)/shard_map/ppermute | solution.py:22
  62.7 1.1 %multiply_add_fusion.2 = f32[32,64,32]{2,1,0:T(8,128)S(1)} fusion(f32[32,64,128]{2,1,0:T(8,128)S(1)} %broadcast_multiply_fusion, f32[32]{0:T(128)S(1)} %get-tuple-element.50, f32[32]{0:T(128)S(1)} %get-tuple-element.51, f32[32]{0:T(128)S(1)} %get-tuple-element.52, f32[32]{0:T(128)S(1)} %get-tuple-element.53), kind=kLoop, calls=%fused_computation.32 | loop fusion | flops 458752 | bytes 1311232 | tf_op jit(solution)/shard_map/add | solution.py:106
  63.9 1.3 %multiply_add_fusion.3 = (f32[32,64,32]{2,1,0:T(8,128)S(1)}, f32[32,64,32]{2,1,0:T(8,128)S(1)}, f32[32,64,32]{2,1,0:T(8,128)S(1)}) fusion(f32[32,64,128]{2,1,0:T(8,128)S(1)} %broadcast_multiply_fusion, f32[32]{0:T(128)S(1)} %get-tuple-element.54, f32[32]{0:T(128)S(1)} %get-tuple-element.55, f32[32]{0:T(128)S(1)} %get-tuple-element.44, ...), kind=kLoop, calls=%fused_computation.33 | loop fusion | flops 851968 | bytes 1836032 | tf_op jit(solution)/shard_map/add | solution.py:106
  65.2 0.9 %pad_maximum_fusion.9 = f32[32,64,128]{2,1,0:T(8,128)S(1)} fusion(f32[32,64,32]{2,1,0:T(8,128)S(1)} %get-tuple-element.32, f32[32,64,32]{2,1,0:T(8,128)S(1)} %get-tuple-element.31, f32[32,64,32]{2,1,0:T(8,128)S(1)} %multiply_add_fusion.2, f32[32,64,32]{2,1,0:T(8,128)S(1)} %get-tuple-element.30), kind=kLoop, calls=%fused_computation.29 | loop fusion | flops 786432 | bytes 2097152 | tf_op jit(solution)/shard_map/concatenate | solution.py:108
  66.3 3.3 %collective-permute-start.10 = (f32[32,1,128]{2,1,0:T(1,128)S(1)}, f32[32,1,128]{2,1,0:T(1,128)S(1)}, u32[]{:S(2)}, u32[]{:S(2)}) collective-permute-start(f32[32,1,128]{2,1,0:T(1,128)S(1)} %get-tuple-element.28), channel_id=1, source_target_pairs={{1,0},{2,1},{3,2},{0,3},{5,4},{6,5},{7,6},{4,7},{9,8},{10,9},{11,1... | collective-permute-start | bytes 49160 | tf_op jit(solution)/shard_map/ppermute | solution.py:44
  69.6 5.9 %collective-permute-start.9 = (f32[1,64,128]{2,1,0:T(8,128)S(1)}, f32[1,64,128]{2,1,0:T(8,128)S(1)}, u32[]{:S(2)}, u32[]{:S(2)}) collective-permute-start(f32[1,64,128]{2,1,0:T(8,128)S(1)} %get-tuple-element.27), channel_id=1, source_target_pairs={{0,4},{4,8},{8,12},{1,5},{5,9},{9,13},{2,6},{6,10},{10,14},{3,7},{... | collective-permute-start | bytes 98312 | tf_op jit(solution)/shard_map/ppermute | solution.py:42
  75.5 1.9 %collective-permute-start.8 = (f32[1,64,128]{2,1,0:T(8,128)S(1)}, f32[1,64,128]{2,1,0:T(8,128)S(1)}, u32[]{:S(2)}, u32[]{:S(2)}) collective-permute-start(f32[1,64,128]{2,1,0:T(8,128)S(1)} %get-tuple-element.26), channel_id=1, source_target_pairs={{4,0},{8,4},{12,8},{5,1},{9,5},{13,9},{6,2},{10,6},{14,10},{7,3},{... | collective-permute-start | bytes 98312 | tf_op jit(solution)/shard_map/ppermute | solution.py:44
  77.7 3.1 %collective-permute-done.8 = f32[1,64,128]{2,1,0:T(8,128)S(1)} collective-permute-done((f32[1,64,128]{2,1,0:T(8,128)S(1)}, f32[1,64,128]{2,1,0:T(8,128)S(1)}, u32[]{:S(2)}, u32[]{:S(2)}) %collective-permute-start.8) | collective-permute-done | bytes 32800 | tf_op jit(solution)/shard_map/ppermute | solution.py:44
  80.7 1.4 %fusion.4 = f32[32,64,128]{2,1,0:T(8,128)} fusion(f32[32,64,128]{2,1,0:T(8,128)S(1)} %bitcast.139, f32[32,1,128]{2,1,0:T(1,128)S(1)} %collective-permute-done.11, f32[32,1,128]{2,1,0:T(1,128)S(1)} %collective-permute-done.10, f32[1,64,128]{2,1,0:T(8,128)S(1)} %collective-permute-done.9, f32[1,64,128]{2,1,0:T(8,128)S(1)} %collective-permute-done.8, ...), kind=kLoop, calls=%fused_computation.12 | loop fusion | flops 3145728 | bytes 2196096 | tf_op jit(solution)/shard_map/mul | solution.py:273
  (124 shorter events, 12.7 us)
Async XLA Ops:
  0.0 1.4 %copy-start.4 = (s32[2,16,32]{2,1,0:T(8,128)S(1)}, s32[2,16,32]{2,1,0:T(8,128)}, u32[]{:S(2)}) copy-start(s32[2,16,32]{2,1,0:T(8,128)} %param.7) | copy-start | bytes 12292
  3.8 4.5 %copy-start.3 = (f32[2,3,16,32]{3,2,1,0:T(8,128)S(1)}, f32[2,3,16,32]{3,2,1,0:T(8,128)}, u32[]{:S(2)}) copy-start(f32[2,3,16,32]{3,2,1,0:T(8,128)} %param.5) | copy-start | bytes 36868
  3.8 12.2 %all-to-all-start = ((f32[4,4,64,128]{3,2,1,0:T(8,128)}), f32[4,4,64,128]{3,2,1,0:T(8,128)S(1)}, u32[]{:S(2)}, u32[]{:S(2)}) async-start(f32[4,4,64,128]{3,2,1,0:T(8,128)} %bitcast.14), calls=%async_computation | async-start | bytes 1048576 | tf_op jit(solution)/shard_map/all_to_all | solution.py:220
  10.0 0.7 copy-start.5
  21.8 14.1 %copy-start = (f32[32,64,128]{2,1,0:T(8,128)S(1)}, f32[32,64,128]{2,1,0:T(8,128)}, u32[]{:S(2)}) copy-start(f32[32,64,128]{2,1,0:T(8,128)} %param.4) | copy-start | bytes 3145732
  22.0 13.9 %collective-permute-start.3 = (f32[32,1,128]{2,1,0:T(1,128)S(1)}, f32[32,1,128]{2,1,0:T(1,128)S(1)}, u32[]{:S(2)}, u32[]{:S(2)}) collective-permute-start(f32[32,1,128]{2,1,0:T(1,128)S(1)} %get-tuple-element.36), channel_id=1, source_target_pairs={{0,1},{1,2},{2,3},{3,0},{4,5},{5,6},{6,7},{7,4},{8,9},{9,10},{10,1... | collective-permute-start | bytes 49160 | tf_op jit(solution)/shard_map/ppermute | solution.py:42
  24.3 11.7 %collective-permute-start.2 = (f32[32,1,128]{2,1,0:T(1,128)S(1)}, f32[32,1,128]{2,1,0:T(1,128)S(1)}, u32[]{:S(2)}, u32[]{:S(2)}) collective-permute-start(f32[32,1,128]{2,1,0:T(1,128)S(1)} %get-tuple-element.35), channel_id=1, source_target_pairs={{1,0},{2,1},{3,2},{0,3},{5,4},{6,5},{7,6},{4,7},{9,8},{10,9},{11,1... | collective-permute-start | bytes 49160 | tf_op jit(solution)/shard_map/ppermute | solution.py:44
  27.0 5.7 %collective-permute-start.1 = (f32[1,65,128]{2,1,0:T(8,128)S(1)}, f32[1,65,128]{2,1,0:T(8,128)S(1)}, u32[]{:S(2)}, u32[]{:S(2)}) collective-permute-start(f32[1,65,128]{2,1,0:T(8,128)S(1)} %concatenate.49), channel_id=1, source_target_pairs={{0,4},{4,8},{8,12},{1,5},{5,9},{9,13},{2,6},{6,10},{10,14},{3,7},{... | collective-permute-start | bytes 99848 | tf_op jit(solution)/shard_map/ppermute | solution.py:167
  30.6 5.3 %collective-permute-start = (f32[1,65,128]{2,1,0:T(8,128)S(1)}, f32[1,65,128]{2,1,0:T(8,128)S(1)}, u32[]{:S(2)}, u32[]{:S(2)}) collective-permute-start(f32[1,65,128]{2,1,0:T(8,128)S(1)} %concatenate.47), channel_id=1, source_target_pairs={{4,0},{8,4},{12,8},{5,1},{9,5},{13,9},{6,2},{10,6},{14,10},{7,3},{... | collective-permute-start | bytes 99848 | tf_op jit(solution)/shard_map/ppermute | solution.py:172
  32.6 0.6 copy-start.1
  35.9 0.8 slice-start
  38.9 9.5 %all-to-all-start.1 = ((f32[4,4,64,128]{3,2,1,0:T(8,128)}), f32[4,4,64,128]{3,2,1,0:T(8,128)S(1)}, u32[]{:S(2)}, u32[]{:S(2)}) async-start(f32[4,4,64,128]{3,2,1,0:T(8,128)} %bitcast.40), calls=%async_computation.1 | async-start | bytes 1048576 | tf_op jit(solution)/shard_map/all_to_all | solution.py:220
  42.6 1.1 %copy-start.2 = (f32[1,65,128]{2,1,0:T(8,128)S(1)}, f32[1,65,128]{2,1,0:T(8,128)}, u32[]{:S(2)}) copy-start(f32[1,65,128]{2,1,0:T(8,128)} %copy-done.1) | copy-start | bytes 99844
  52.3 2.0 %collective-permute-start.4 = (f32[768]{0:T(1024)S(1)}, f32[768]{0:T(1024)S(1)}, u32[]{:S(2)}, u32[]{:S(2)}) collective-permute-start(f32[768]{0:T(1024)S(1)} %pad_maximum_fusion.10), channel_id=1, source_target_pairs={{0,4},{4,0},{8,12},{12,8},{1,5},{5,1},{9,13},{13,9},{2,6},{6,2},{1... | collective-permute-start | bytes 9224 | tf_op jit(solution)/shard_map/ppermute | solution.py:22
  54.3 2.5 %collective-permute-start.5 = (f32[768]{0:T(1024)S(1)}, f32[768]{0:T(1024)S(1)}, u32[]{:S(2)}, u32[]{:S(2)}) collective-permute-start(f32[768]{0:T(1024)S(1)} %fusion.137), channel_id=1, source_target_pairs={{0,8},{4,12},{8,0},{12,4},{1,9},{5,13},{9,1},{13,5},{2,10},{6,14},... | collective-permute-start | bytes 9224 | tf_op jit(solution)/shard_map/ppermute | solution.py:22
  56.8 2.5 %collective-permute-start.6 = (f32[768]{0:T(1024)S(1)}, f32[768]{0:T(1024)S(1)}, u32[]{:S(2)}, u32[]{:S(2)}) collective-permute-start(f32[768]{0:T(1024)S(1)} %add.862), channel_id=1, source_target_pairs={{0,1},{1,0},{2,3},{3,2},{4,5},{5,4},{6,7},{7,6},{8,9},{9,8},{10,11... | collective-permute-start | bytes 9224 | tf_op jit(solution)/shard_map/ppermute | solution.py:22
  59.3 3.4 %collective-permute-start.7 = (f32[768]{0:T(1024)S(1)}, f32[768]{0:T(1024)S(1)}, u32[]{:S(2)}, u32[]{:S(2)}) collective-permute-start(f32[768]{0:T(1024)S(1)} %add.863), channel_id=1, source_target_pairs={{0,2},{1,3},{2,0},{3,1},{4,6},{5,7},{6,4},{7,5},{8,10},{9,11},{10,... | collective-permute-start | bytes 9224 | tf_op jit(solution)/shard_map/ppermute | solution.py:22
  66.3 11.3 %collective-permute-start.11 = (f32[32,1,128]{2,1,0:T(1,128)S(1)}, f32[32,1,128]{2,1,0:T(1,128)S(1)}, u32[]{:S(2)}, u32[]{:S(2)}) collective-permute-start(f32[32,1,128]{2,1,0:T(1,128)S(1)} %get-tuple-element.29), channel_id=1, source_target_pairs={{0,1},{1,2},{2,3},{3,0},{4,5},{5,6},{6,7},{7,4},{8,9},{9,10},{10,1... | collective-permute-start | bytes 49160 | tf_op jit(solution)/shard_map/ppermute | solution.py:42
  66.3 11.3 %collective-permute-start.10 = (f32[32,1,128]{2,1,0:T(1,128)S(1)}, f32[32,1,128]{2,1,0:T(1,128)S(1)}, u32[]{:S(2)}, u32[]{:S(2)}) collective-permute-start(f32[32,1,128]{2,1,0:T(1,128)S(1)} %get-tuple-element.28), channel_id=1, source_target_pairs={{1,0},{2,1},{3,2},{0,3},{5,4},{6,5},{7,6},{4,7},{9,8},{10,9},{11,1... | collective-permute-start | bytes 49160 | tf_op jit(solution)/shard_map/ppermute | solution.py:44
  69.6 8.1 %collective-permute-start.9 = (f32[1,64,128]{2,1,0:T(8,128)S(1)}, f32[1,64,128]{2,1,0:T(8,128)S(1)}, u32[]{:S(2)}, u32[]{:S(2)}) collective-permute-start(f32[1,64,128]{2,1,0:T(8,128)S(1)} %get-tuple-element.27), channel_id=1, source_target_pairs={{0,4},{4,8},{8,12},{1,5},{5,9},{9,13},{2,6},{6,10},{10,14},{3,7},{... | collective-permute-start | bytes 98312 | tf_op jit(solution)/shard_map/ppermute | solution.py:42
  75.5 5.2 %collective-permute-start.8 = (f32[1,64,128]{2,1,0:T(8,128)S(1)}, f32[1,64,128]{2,1,0:T(8,128)S(1)}, u32[]{:S(2)}, u32[]{:S(2)}) collective-permute-start(f32[1,64,128]{2,1,0:T(8,128)S(1)} %get-tuple-element.26), channel_id=1, source_target_pairs={{4,0},{8,4},{12,8},{5,1},{9,5},{13,9},{6,2},{10,6},{14,10},{7,3},{... | collective-permute-start | bytes 98312 | tf_op jit(solution)/shard_map/ppermute | solution.py:44

commit v11 on v5

--- a/solution.py
+++ b/solution.py
@@ -210,8 +210,13 @@
     owned_here = remote & (source_dev == lat_index)
     sending = owned_here[:, :, None] & (slot_of[:, :, None] == slot_range[None, None, :])
     send_local = jnp.sum(jnp.where(sending, source_local[:, :, None], 0), axis=1)
-    own_patches = to_patches(state_field)
-    outgoing = own_patches[send_local.reshape(-1)].reshape(lat_count, CAP, 64, value_count)
+    field_view = state_field.reshape(band_rows, 8, band_cols, 8, value_count)
+
+    def pick_patches(local_index):
+        picked = field_view[local_index // band_cols, :, local_index % band_cols]
+        return picked.reshape(local_index.shape[0], 64, value_count)
+
+    outgoing = pick_patches(send_local.reshape(-1)).reshape(lat_count, CAP, 64, value_count)
     my_dev = lax.dynamic_index_in_dim(source_dev, lat_index, 0, keepdims=False)
     my_slot = lax.dynamic_index_in_dim(slot_of, lat_index, 0, keepdims=False)
     my_local = lax.dynamic_index_in_dim(source_local, lat_index, 0, keepdims=False)
@@ -221,7 +226,7 @@
         lat_count * CAP, 64, value_count
     )
     pick_index = my_dev * CAP + my_slot
-    patches = jnp.where(my_remote[:, None, None], arrived[pick_index], own_patches[my_local])
+    patches = jnp.where(my_remote[:, None, None], arrived[pick_index], pick_patches(my_local))
     return patches, my_frac
 
 

time: 82.7 us -> 85.1 us (1.029)
  waiting for transfers between devices: 21.1 us -> 17.7 us
  local copies, waits for them, and re-layouts: 12.9 us -> 15.8 us
  other arithmetic: 12.3 us -> 14.1 us
  matrix products: 4.93 us -> 6.15 us
    all_to_all x2, waiting for transfers between devices: 6.95 us -> 4 us  [departed(): lax.all_to_all(outgoing, 'lat', 0, 0, tiled=True)]
    gather x4, local copies, waits for them, and re-layouts: 3.99 us -> 6.38 us  [pick_patches(): picked = field_view[local_index // band_cols, :, local_index % band_cols]]
    transpose x2 -> x0, local copies, waits for them, and re-layouts: 1.48 us -> none  [to_patches(): return state_field.reshape(band_rows, 8, band_cols, 8, -1).transpose(0, 2...]
    dot_general x2, matrix products: 3.79 us -> 5.01 us  [spatial(): jnp.einsum('nij,njv->niv', plane_weights(fraction_y, fraction_x), patches...]
    div x6, other arithmetic: 0.05 us -> 1.2 us  [cubic_weights(): second_term = (fraction + 1.0) * (fraction - 1.0) * (fraction - 2.0) / 2.0]
  transfers between devices with their start and end apart: 14 -> 14, of which waited for: 8 -> 8; matrix products, arithmetic and copies ran while one was open for 10% -> 13% of each run, Pallas kernels for 0% -> 0%
where the time goes in v11:
time: 85.1 us; the launch traced here: 84.6 us
  starting transfers between devices  30.2 us (35%)
  waiting for transfers between devices  17.7 us (21%)
  local copies, waits for them, and re-layouts  15.8 us (19%)
  other arithmetic  14.1 us (17%)
  matrix products  6.15 us (7%)
    ppermute x4, waiting for transfers between devices, all_sum(): lax.ppermute(value, axis, [(i, i ^ distance) for i in range(count)])  8.4 us
    all_to_all x2, starting transfers between devices, departed(): lax.all_to_all(outgoing, 'lat', 0, 0, tiled=True)  8.04 us
    ppermute x3, starting transfers between devices, extended(): lax.ppermute(head, axis, [((i + 1) % count, i) for i in range(ends)])  7.27 us
    gather x4, local copies, waits for them, and re-layouts, pick_patches(): picked = field_view[local_index // band_cols, :, local_index % band_cols]  6.38 us
    ppermute x3, starting transfers between devices, extended(): lax.ppermute(tail, axis, [(i, (i + 1) % count) for i in range(ends)])  5.77 us
    dot_general x2, matrix products, spatial(): jnp.einsum('nij,njv->niv', plane_weights(fraction_y, fraction_x), patches...  5.01 us
    add x4, other arithmetic, levels(): acc = term if acc is None else acc + term  4.85 us
    ppermute x4, starting transfers between devices, all_sum(): lax.ppermute(value, axis, [(i, i ^ distance) for i in range(count)])  4.22 us
  transfers between devices with their start and end apart: 14, of which 8 were waited for; matrix products, arithmetic and copies ran while one was open for 13% of the time, Pallas kernels for 0%

profile of v11, /device:TPU:1, one launch (start us, length us, event | category | flops | bytes accessed | tf_op | source)
XLA Modules:
  0.0 84.6 jit_solution(11966059878261925497)
XLA Ops:
  1.8 2.6 %gather_fusion = f32[16,8,8,128]{3,2,1,0:T(8,128)} fusion(f32[4,8,8,8,128]{4,3,2,1,0:T(8,128)} %bitcast.135, s32[16]{0:T(128)S(1)} %fusion.152), kind=kCustom, calls=%fused_computation | custom fusion | bytes 1048704 | tf_op jit(solution)/shard_map/gather | solution.py:216
  4.4 4.4 %all-to-all-start = ((f32[4,4,64,128]{3,2,1,0:T(8,128)}), f32[4,4,64,128]{3,2,1,0:T(8,128)S(1)}, u32[]{:S(2)}, u32[]{:S(2)}) async-start(f32[4,4,64,128]{3,2,1,0:T(8,128)} %bitcast.12), calls=%async_computation | async-start | bytes 1048576 | tf_op jit(solution)/shard_map/all_to_all | solution.py:225
  12.3 1.6 %gather_fusion.2 = f32[32,8,8,128]{3,2,1,0:T(8,128)} fusion(f32[4,8,8,8,128]{4,3,2,1,0:T(8,128)S(1)} %bitcast.136, s32[32]{0:T(128)S(1)} %fusion.154), kind=kCustom, calls=%fused_computation.2 | custom fusion | bytes 2097408 | tf_op jit(solution)/shard_map/gather | solution.py:216
  14.7 1.9 %all-to-all-done = f32[4,4,64,128]{3,2,1,0:T(8,128)S(1)} async-done(((f32[4,4,64,128]{3,2,1,0:T(8,128)}), f32[4,4,64,128]{3,2,1,0:T(8,128)S(1)}, u32[]{:S(2)}, u32[]{:S(2)}) %all-to-all-start) | async-done | bytes 524320 | tf_op jit(solution)/shard_map/all_to_all | solution.py:225
  17.2 3.1 %fusion.14 = f32[32,64,128]{2,1,0:T(8,128)S(1)} fusion(f32[32,64,128]{2,1,0:T(8,128)S(1)} %gather_fusion.1, f32[32,8,8,128]{3,2,1,0:T(8,128)} %gather_fusion.2, f32[32]{0:T(128)S(1)} %get-tuple-element.107, f32[32]{0:T(128)S(1)} %get-tuple-element.108, f32[32]{0:T(128)S(1)} %get-tuple-element.106, f32[32]{0:T(128)S(1)} %get-tuple-element.76, ...), kind=kOutput, calls=%fused_computation.33 | convolution fusion | flops 203554816 | bytes 3277856 | tf_op jit(solution)/shard_map/nij,njv->niv/dot_general | solution.py:88
  20.4 1.1 %multiply_add_fusion.6 = f32[32,64,32]{2,1,0:T(8,128)S(1)} fusion(f32[32,64,128]{2,1,0:T(8,128)S(1)} %fusion.14, f32[32]{0:T(128)S(1)} %get-tuple-element.64, f32[32]{0:T(128)S(1)} %get-tuple-element.65, f32[32]{0:T(128)S(1)} %get-tuple-element.66, f32[32]{0:T(128)S(1)} %get-tuple-element.67), kind=kLoop, calls=%fused_computation.42 | loop fusion | flops 458752 | bytes 1311232 | tf_op jit(solution)/shard_map/add | solution.py:106
  21.5 1.3 %multiply_add_fusion.7 = (f32[32,64,32]{2,1,0:T(8,128)S(1)}, f32[32,64,32]{2,1,0:T(8,128)S(1)}, f32[32,64,32]{2,1,0:T(8,128)S(1)}) fusion(f32[32,64,128]{2,1,0:T(8,128)S(1)} %fusion.14, f32[32]{0:T(128)S(1)} %get-tuple-element.68, f32[32]{0:T(128)S(1)} %get-tuple-element.69, f32[32]{0:T(128)S(1)} %get-tuple-element.58, f32[32]{0:T(128)S(1)} %get-tuple-element.61, ...), kind=kLoop, calls=%fused_computation.43 | loop fusion | flops 851968 | bytes 1836032 | tf_op jit(solution)/shard_map/add | solution.py:106
  22.8 0.9 %pad_maximum_fusion.8 = f32[32,64,128]{2,1,0:T(8,128)S(1)} fusion(f32[32,64,32]{2,1,0:T(8,128)S(1)} %get-tuple-element.39, f32[32,64,32]{2,1,0:T(8,128)S(1)} %get-tuple-element.38, f32[32,64,32]{2,1,0:T(8,128)S(1)} %multiply_add_fusion.6, f32[32,64,32]{2,1,0:T(8,128)S(1)} %get-tuple-element.37), kind=kLoop, calls=%fused_computation.28 | loop fusion | flops 786432 | bytes 2097152 | tf_op jit(solution)/shard_map/concatenate | solution.py:108
  23.9 2.2 %collective-permute-start.3 = (f32[32,1,128]{2,1,0:T(1,128)S(1)}, f32[32,1,128]{2,1,0:T(1,128)S(1)}, u32[]{:S(2)}, u32[]{:S(2)}) collective-permute-start(f32[32,1,128]{2,1,0:T(1,128)S(1)} %get-tuple-element.36), channel_id=1, source_target_pairs={{0,1},{1,2},{2,3},{3,0},{4,5},{5,6},{6,7},{7,4},{8,9},{9,10},{10,1... | collective-permute-start | bytes 49160 | tf_op jit(solution)/shard_map/ppermute | solution.py:42
  26.1 2.1 %collective-permute-start.2 = (f32[32,1,128]{2,1,0:T(1,128)S(1)}, f32[32,1,128]{2,1,0:T(1,128)S(1)}, u32[]{:S(2)}, u32[]{:S(2)}) collective-permute-start(f32[32,1,128]{2,1,0:T(1,128)S(1)} %get-tuple-element.35), channel_id=1, source_target_pairs={{1,0},{2,1},{3,2},{0,3},{5,4},{6,5},{7,6},{4,7},{9,8},{10,9},{11,1... | collective-permute-start | bytes 49160 | tf_op jit(solution)/shard_map/ppermute | solution.py:44
  28.8 3.0 %collective-permute-start.1 = (f32[1,65,128]{2,1,0:T(8,128)S(1)}, f32[1,65,128]{2,1,0:T(8,128)S(1)}, u32[]{:S(2)}, u32[]{:S(2)}) collective-permute-start(f32[1,65,128]{2,1,0:T(8,128)S(1)} %concatenate.63), channel_id=1, source_target_pairs={{0,4},{4,8},{8,12},{1,5},{5,9},{9,13},{2,6},{6,10},{10,14},{3,7},{... | collective-permute-start | bytes 99848 | tf_op jit(solution)/shard_map/ppermute | solution.py:167
  32.4 1.9 %collective-permute-start = (f32[1,65,128]{2,1,0:T(8,128)S(1)}, f32[1,65,128]{2,1,0:T(8,128)S(1)}, u32[]{:S(2)}, u32[]{:S(2)}) collective-permute-start(f32[1,65,128]{2,1,0:T(8,128)S(1)} %concatenate.61), channel_id=1, source_target_pairs={{4,0},{8,4},{12,8},{5,1},{9,5},{13,9},{6,2},{10,6},{14,10},{7,3},{... | collective-permute-start | bytes 99848 | tf_op jit(solution)/shard_map/ppermute | solution.py:172
  35.5 2.2 %collective-permute-done = f32[1,65,128]{2,1,0:T(8,128)S(1)} collective-permute-done((f32[1,65,128]{2,1,0:T(8,128)S(1)}, f32[1,65,128]{2,1,0:T(8,128)S(1)}, u32[]{:S(2)}, u32[]{:S(2)}) %collective-permute-start) | collective-permute-done | bytes 33312 | tf_op jit(solution)/shard_map/ppermute | solution.py:172
  39.2 1.4 %gather_fusion.3 = f32[16,8,8,128]{3,2,1,0:T(8,128)} fusion(f32[4,8,8,8,128]{4,3,2,1,0:T(8,128)S(1)} %bitcast.137, s32[16]{0:T(128)S(1)} %fusion.151), kind=kCustom, calls=%fused_computation.3 | custom fusion | bytes 1048704 | tf_op jit(solution)/shard_map/gather | solution.py:216
  40.6 3.6 %all-to-all-start.1 = ((f32[4,4,64,128]{3,2,1,0:T(8,128)}), f32[4,4,64,128]{3,2,1,0:T(8,128)S(1)}, u32[]{:S(2)}, u32[]{:S(2)}) async-start(f32[4,4,64,128]{3,2,1,0:T(8,128)} %bitcast.37), calls=%async_computation.1 | async-start | bytes 1048576 | tf_op jit(solution)/shard_map/all_to_all | solution.py:225
  46.1 1.4 %maximum_multiply_fusion = f32[34]{0:T(128)S(1)} fusion(f32[1]{0:T(128)} %bitcast.45, f32[32]{0:T(128)S(1)} %copy-done.4, f32[1]{0:T(128)} %bitcast.44, s32[]{:T(128)S(6)} %sub.211), kind=kLoop, calls=%fused_computation.325 | loop fusion | flops 272 | bytes 276 | tf_op jit(solution)/shard_map/mul | solution.py:255
  48.0 2.1 %all-to-all-done.1 = f32[4,4,64,128]{3,2,1,0:T(8,128)S(1)} async-done(((f32[4,4,64,128]{3,2,1,0:T(8,128)}), f32[4,4,64,128]{3,2,1,0:T(8,128)S(1)}, u32[]{:S(2)}, u32[]{:S(2)}) %all-to-all-start.1) | async-done | bytes 524320 | tf_op jit(solution)/shard_map/all_to_all | solution.py:225
  51.4 1.9 %fusion.13 = f32[32,64,128]{2,1,0:T(8,128)S(1)} fusion(f32[32,64,128]{2,1,0:T(8,128)S(1)} %gather_fusion.4, f32[32,8,8,128]{3,2,1,0:T(8,128)S(1)} %gather_fusion.5, f32[64,64]{1,0:T(8,128)S(1)} %get-tuple-element.83, f32[32]{0:T(128)S(1)} %copy-done.5, f32[64,64]{1,0:T(8,128)S(1)} %get-tuple-element.84, f32[32]{0:T(128)S(1)} %copy-done.6, ...), kind=kOutput, calls=%fused_computation.31 | convolution fusion | flops 203554816 | bytes 3277856 | tf_op jit(solution)/shard_map/nij,njv->niv/dot_general | solution.py:88
  53.3 1.0 %fusion.170 = f32[32,1,128]{2,1,0:T(1,128)S(1)} fusion(f32[32,64,1]{1,2,0:T(1,128)S(1)} %bitcast.149, f32[32,64,128]{2,1,0:T(8,128)S(1)} %fusion.13), kind=kOutput, calls=%fused_computation.384 | convolution fusion | flops 3145728 | bytes 1073152 | tf_op jit(solution)/shard_map/pi,piv->pv/dot_general | solution.py:258
  54.8 2.4 %collective-permute-done.4 = f32[768]{0:T(1024)S(1)} collective-permute-done((f32[768]{0:T(1024)S(1)}, f32[768]{0:T(1024)S(1)}, u32[]{:S(2)}, u32[]{:S(2)}) %collective-permute-start.4) | collective-permute-done | bytes 3104 | tf_op jit(solution)/shard_map/ppermute | solution.py:22
  58.0 2.7 %collective-permute-done.5 = f32[768]{0:T(1024)S(1)} collective-permute-done((f32[768]{0:T(1024)S(1)}, f32[768]{0:T(1024)S(1)}, u32[]{:S(2)}, u32[]{:S(2)}) %collective-permute-start.5) | collective-permute-done | bytes 3104 | tf_op jit(solution)/shard_map/ppermute | solution.py:22
  60.6 3.4 %collective-permute-start.6 = (f32[768]{0:T(1024)S(1)}, f32[768]{0:T(1024)S(1)}, u32[]{:S(2)}, u32[]{:S(2)}) collective-permute-start(f32[768]{0:T(1024)S(1)} %add.990), channel_id=1, source_target_pairs={{0,4},{4,0},{8,12},{12,8},{1,5},{5,1},{9,13},{13,9},{2,6},{6,2},{1... | collective-permute-start | bytes 9224 | tf_op jit(solution)/shard_map/ppermute | solution.py:22
  64.1 0.8 collective-permute-done.6
  64.9 2.4 %collective-permute-done.7 = f32[768]{0:T(1024)S(1)} collective-permute-done((f32[768]{0:T(1024)S(1)}, f32[768]{0:T(1024)S(1)}, u32[]{:S(2)}, u32[]{:S(2)}) %collective-permute-start.7) | collective-permute-done | bytes 3104 | tf_op jit(solution)/shard_map/ppermute | solution.py:22
  67.5 1.1 %multiply_add_fusion.2 = f32[32,64,32]{2,1,0:T(8,128)S(1)} fusion(f32[32,64,128]{2,1,0:T(8,128)S(1)} %broadcast_multiply_fusion, f32[32]{0:T(128)S(1)} %get-tuple-element.50, f32[32]{0:T(128)S(1)} %get-tuple-element.51, f32[32]{0:T(128)S(1)} %get-tuple-element.52, f32[32]{0:T(128)S(1)} %get-tuple-element.53), kind=kLoop, calls=%fused_computation.36 | loop fusion | flops 458752 | bytes 1311232 | tf_op jit(solution)/shard_map/add | solution.py:106
  68.6 1.3 %multiply_add_fusion.3 = (f32[32,64,32]{2,1,0:T(8,128)S(1)}, f32[32,64,32]{2,1,0:T(8,128)S(1)}, f32[32,64,32]{2,1,0:T(8,128)S(1)}) fusion(f32[32,64,128]{2,1,0:T(8,128)S(1)} %broadcast_multiply_fusion, f32[32]{0:T(128)S(1)} %get-tuple-element.54, f32[32]{0:T(128)S(1)} %get-tuple-element.55, f32[32]{0:T(128)S(1)} %get-tuple-element.44, ...), kind=kLoop, calls=%fused_computation.37 | loop fusion | flops 851968 | bytes 1836032 | tf_op jit(solution)/shard_map/add | solution.py:106
  69.9 0.9 %pad_maximum_fusion.9 = f32[32,64,128]{2,1,0:T(8,128)S(1)} fusion(f32[32,64,32]{2,1,0:T(8,128)S(1)} %get-tuple-element.32, f32[32,64,32]{2,1,0:T(8,128)S(1)} %get-tuple-element.31, f32[32,64,32]{2,1,0:T(8,128)S(1)} %multiply_add_fusion.2, f32[32,64,32]{2,1,0:T(8,128)S(1)} %get-tuple-element.30), kind=kLoop, calls=%fused_computation.29 | loop fusion | flops 786432 | bytes 2097152 | tf_op jit(solution)/shard_map/concatenate | solution.py:108
  71.1 3.3 %collective-permute-start.10 = (f32[32,1,128]{2,1,0:T(1,128)S(1)}, f32[32,1,128]{2,1,0:T(1,128)S(1)}, u32[]{:S(2)}, u32[]{:S(2)}) collective-permute-start(f32[32,1,128]{2,1,0:T(1,128)S(1)} %get-tuple-element.28), channel_id=1, source_target_pairs={{1,0},{2,1},{3,2},{0,3},{5,4},{6,5},{7,6},{4,7},{9,8},{10,9},{11,1... | collective-permute-start | bytes 49160 | tf_op jit(solution)/shard_map/ppermute | solution.py:44
  74.3 3.6 %collective-permute-start.9 = (f32[1,64,128]{2,1,0:T(8,128)S(1)}, f32[1,64,128]{2,1,0:T(8,128)S(1)}, u32[]{:S(2)}, u32[]{:S(2)}) collective-permute-start(f32[1,64,128]{2,1,0:T(8,128)S(1)} %get-tuple-element.27), channel_id=1, source_target_pairs={{0,4},{4,8},{8,12},{1,5},{5,9},{9,13},{2,6},{6,10},{10,14},{3,7},{... | collective-permute-start | bytes 98312 | tf_op jit(solution)/shard_map/ppermute | solution.py:42
  77.9 1.9 %collective-permute-start.8 = (f32[1,64,128]{2,1,0:T(8,128)S(1)}, f32[1,64,128]{2,1,0:T(8,128)S(1)}, u32[]{:S(2)}, u32[]{:S(2)}) collective-permute-start(f32[1,64,128]{2,1,0:T(8,128)S(1)} %get-tuple-element.26), channel_id=1, source_target_pairs={{4,0},{8,4},{12,8},{5,1},{9,5},{13,9},{6,2},{10,6},{14,10},{7,3},{... | collective-permute-start | bytes 98312 | tf_op jit(solution)/shard_map/ppermute | solution.py:44
  80.1 3.1 %collective-permute-done.8 = f32[1,64,128]{2,1,0:T(8,128)S(1)} collective-permute-done((f32[1,64,128]{2,1,0:T(8,128)S(1)}, f32[1,64,128]{2,1,0:T(8,128)S(1)}, u32[]{:S(2)}, u32[]{:S(2)}) %collective-permute-start.8) | collective-permute-done | bytes 32800 | tf_op jit(solution)/shard_map/ppermute | solution.py:44
  83.1 1.4 %fusion.4 = f32[32,64,128]{2,1,0:T(8,128)} fusion(f32[32,64,128]{2,1,0:T(8,128)S(1)} %bitcast.143, f32[32,1,128]{2,1,0:T(1,128)S(1)} %collective-permute-done.11, f32[32,1,128]{2,1,0:T(1,128)S(1)} %collective-permute-done.10, f32[1,64,128]{2,1,0:T(8,128)S(1)} %collective-permute-done.9, f32[1,64,128]{2,1,0:T(8,128)S(1)} %collective-permute-done.8, ...), kind=kLoop, calls=%fused_computation.12 | loop fusion | flops 3145728 | bytes 2196096 | tf_op jit(solution)/shard_map/mul | solution.py:278
  (131 shorter events, 15.8 us)
Async XLA Ops:
  1.8 7.2 %copy-start.3 = (f32[2,3,16,32]{3,2,1,0:T(8,128)S(1)}, f32[2,3,16,32]{3,2,1,0:T(8,128)}, u32[]{:S(2)}) copy-start(f32[2,3,16,32]{3,2,1,0:T(8,128)} %param.5) | copy-start | bytes 36868
  4.4 7.9 %copy-start = (f32[32,64,128]{2,1,0:T(8,128)S(1)}, f32[32,64,128]{2,1,0:T(8,128)}, u32[]{:S(2)}) copy-start(f32[32,64,128]{2,1,0:T(8,128)} %param.4) | copy-start | bytes 3145732
  4.4 12.2 %all-to-all-start = ((f32[4,4,64,128]{3,2,1,0:T(8,128)}), f32[4,4,64,128]{3,2,1,0:T(8,128)S(1)}, u32[]{:S(2)}, u32[]{:S(2)}) async-start(f32[4,4,64,128]{3,2,1,0:T(8,128)} %bitcast.12), calls=%async_computation | async-start | bytes 1048576 | tf_op jit(solution)/shard_map/all_to_all | solution.py:225
  12.3 1.7 %copy-start.4 = (f32[32]{0:T(128)S(1)}, f32[32]{0:T(128)}, u32[]{:S(2)}) copy-start(f32[32]{0:T(128)} %param.6) | copy-start | bytes 388
  23.9 13.9 %collective-permute-start.3 = (f32[32,1,128]{2,1,0:T(1,128)S(1)}, f32[32,1,128]{2,1,0:T(1,128)S(1)}, u32[]{:S(2)}, u32[]{:S(2)}) collective-permute-start(f32[32,1,128]{2,1,0:T(1,128)S(1)} %get-tuple-element.36), channel_id=1, source_target_pairs={{0,1},{1,2},{2,3},{3,0},{4,5},{5,6},{6,7},{7,4},{8,9},{9,10},{10,1... | collective-permute-start | bytes 49160 | tf_op jit(solution)/shard_map/ppermute | solution.py:42
  26.1 11.7 %collective-permute-start.2 = (f32[32,1,128]{2,1,0:T(1,128)S(1)}, f32[32,1,128]{2,1,0:T(1,128)S(1)}, u32[]{:S(2)}, u32[]{:S(2)}) collective-permute-start(f32[32,1,128]{2,1,0:T(1,128)S(1)} %get-tuple-element.35), channel_id=1, source_target_pairs={{1,0},{2,1},{3,2},{0,3},{5,4},{6,5},{7,6},{4,7},{9,8},{10,9},{11,1... | collective-permute-start | bytes 49160 | tf_op jit(solution)/shard_map/ppermute | solution.py:44
  28.8 6.2 %collective-permute-start.1 = (f32[1,65,128]{2,1,0:T(8,128)S(1)}, f32[1,65,128]{2,1,0:T(8,128)S(1)}, u32[]{:S(2)}, u32[]{:S(2)}) collective-permute-start(f32[1,65,128]{2,1,0:T(8,128)S(1)} %concatenate.63), channel_id=1, source_target_pairs={{0,4},{4,8},{8,12},{1,5},{5,9},{9,13},{2,6},{6,10},{10,14},{3,7},{... | collective-permute-start | bytes 99848 | tf_op jit(solution)/shard_map/ppermute | solution.py:167
  32.4 5.3 %collective-permute-start = (f32[1,65,128]{2,1,0:T(8,128)S(1)}, f32[1,65,128]{2,1,0:T(8,128)S(1)}, u32[]{:S(2)}, u32[]{:S(2)}) collective-permute-start(f32[1,65,128]{2,1,0:T(8,128)S(1)} %concatenate.61), channel_id=1, source_target_pairs={{4,0},{8,4},{12,8},{5,1},{9,5},{13,9},{6,2},{10,6},{14,10},{7,3},{... | collective-permute-start | bytes 99848 | tf_op jit(solution)/shard_map/ppermute | solution.py:172
  34.9 0.6 copy-start.1
  35.5 2.2 %copy-start.10 = (f32[32]{0:T(128)S(1)}, f32[32]{0:T(128)}, u32[]{:S(2)}) copy-start(f32[32]{0:T(128)} %add_cosine_fusion) | copy-start | bytes 388
  37.7 0.8 slice-start
  40.6 9.5 %all-to-all-start.1 = ((f32[4,4,64,128]{3,2,1,0:T(8,128)}), f32[4,4,64,128]{3,2,1,0:T(8,128)S(1)}, u32[]{:S(2)}, u32[]{:S(2)}) async-start(f32[4,4,64,128]{3,2,1,0:T(8,128)} %bitcast.37), calls=%async_computation.1 | async-start | bytes 1048576 | tf_op jit(solution)/shard_map/all_to_all | solution.py:225
  44.3 1.3 %copy-start.2 = (f32[1,65,128]{2,1,0:T(8,128)S(1)}, f32[1,65,128]{2,1,0:T(8,128)}, u32[]{:S(2)}) copy-start(f32[1,65,128]{2,1,0:T(8,128)} %copy-done.1) | copy-start | bytes 99844
  50.1 0.7 copy-start.8
  50.1 0.7 copy-start.9
  50.1 0.7 copy-start.11
  50.8 0.7 copy-start.5
  50.8 0.7 copy-start.6
  50.8 0.7 copy-start.7
  54.7 2.5 %collective-permute-start.4 = (f32[768]{0:T(1024)S(1)}, f32[768]{0:T(1024)S(1)}, u32[]{:S(2)}, u32[]{:S(2)}) collective-permute-start(f32[768]{0:T(1024)S(1)} %pad_maximum_fusion.10), channel_id=1, source_target_pairs={{0,1},{1,0},{2,3},{3,2},{4,5},{5,4},{6,7},{7,6},{8,9},{9,8},{10,11... | collective-permute-start | bytes 9224 | tf_op jit(solution)/shard_map/ppermute | solution.py:22
  57.2 3.4 %collective-permute-start.5 = (f32[768]{0:T(1024)S(1)}, f32[768]{0:T(1024)S(1)}, u32[]{:S(2)}, u32[]{:S(2)}) collective-permute-start(f32[768]{0:T(1024)S(1)} %fusion.155), channel_id=1, source_target_pairs={{0,2},{1,3},{2,0},{3,1},{4,6},{5,7},{6,4},{7,5},{8,10},{9,11},{10,... | collective-permute-start | bytes 9224 | tf_op jit(solution)/shard_map/ppermute | solution.py:22
  60.6 4.3 %collective-permute-start.6 = (f32[768]{0:T(1024)S(1)}, f32[768]{0:T(1024)S(1)}, u32[]{:S(2)}, u32[]{:S(2)}) collective-permute-start(f32[768]{0:T(1024)S(1)} %add.990), channel_id=1, source_target_pairs={{0,4},{4,0},{8,12},{12,8},{1,5},{5,1},{9,13},{13,9},{2,6},{6,2},{1... | collective-permute-start | bytes 9224 | tf_op jit(solution)/shard_map/ppermute | solution.py:22
  64.9 2.5 %collective-permute-start.7 = (f32[768]{0:T(1024)S(1)}, f32[768]{0:T(1024)S(1)}, u32[]{:S(2)}, u32[]{:S(2)}) collective-permute-start(f32[768]{0:T(1024)S(1)} %add.991), channel_id=1, source_target_pairs={{0,8},{4,12},{8,0},{12,4},{1,9},{5,13},{9,1},{13,5},{2,10},{6,14},... | collective-permute-start | bytes 9224 | tf_op jit(solution)/shard_map/ppermute | solution.py:22
  71.1 9.0 %collective-permute-start.11 = (f32[32,1,128]{2,1,0:T(1,128)S(1)}, f32[32,1,128]{2,1,0:T(1,128)S(1)}, u32[]{:S(2)}, u32[]{:S(2)}) collective-permute-start(f32[32,1,128]{2,1,0:T(1,128)S(1)} %get-tuple-element.29), channel_id=1, source_target_pairs={{0,1},{1,2},{2,3},{3,0},{4,5},{5,6},{6,7},{7,4},{8,9},{9,10},{10,1... | collective-permute-start | bytes 49160 | tf_op jit(solution)/shard_map/ppermute | solution.py:42
  71.1 9.0 %collective-permute-start.10 = (f32[32,1,128]{2,1,0:T(1,128)S(1)}, f32[32,1,128]{2,1,0:T(1,128)S(1)}, u32[]{:S(2)}, u32[]{:S(2)}) collective-permute-start(f32[32,1,128]{2,1,0:T(1,128)S(1)} %get-tuple-element.28), channel_id=1, source_target_pairs={{1,0},{2,1},{3,2},{0,3},{5,4},{6,5},{7,6},{4,7},{9,8},{10,9},{11,1... | collective-permute-start | bytes 49160 | tf_op jit(solution)/shard_map/ppermute | solution.py:44
  74.3 5.7 %collective-permute-start.9 = (f32[1,64,128]{2,1,0:T(8,128)S(1)}, f32[1,64,128]{2,1,0:T(8,128)S(1)}, u32[]{:S(2)}, u32[]{:S(2)}) collective-permute-start(f32[1,64,128]{2,1,0:T(8,128)S(1)} %get-tuple-element.27), channel_id=1, source_target_pairs={{0,4},{4,8},{8,12},{1,5},{5,9},{9,13},{2,6},{6,10},{10,14},{3,7},{... | collective-permute-start | bytes 98312 | tf_op jit(solution)/shard_map/ppermute | solution.py:42
  77.9 5.2 %collective-permute-start.8 = (f32[1,64,128]{2,1,0:T(8,128)S(1)}, f32[1,64,128]{2,1,0:T(8,128)S(1)}, u32[]{:S(2)}, u32[]{:S(2)}) collective-permute-start(f32[1,64,128]{2,1,0:T(8,128)S(1)} %get-tuple-element.26), channel_id=1, source_target_pairs={{4,0},{8,4},{12,8},{5,1},{9,5},{13,9},{6,2},{10,6},{14,10},{7,3},{... | collective-permute-start | bytes 98312 | tf_op jit(solution)/shard_map/ppermute | solution.py:44

commit v12 on v5

--- a/solution.py
+++ b/solution.py
@@ -31,20 +31,35 @@
     return value, rider if rider_done is None else rider_done
 
 
+def neighbour_halos(lo_edge, hi_edge, axis, closed):
+    count = lax.axis_size(axis)
+    if count % 2:
+        ends = count if closed else count - 1
+        from_lo = lax.ppermute(hi_edge, axis, [(i, (i + 1) % count) for i in range(ends)])
+        from_hi = lax.ppermute(lo_edge, axis, [((i + 1) % count, i) for i in range(ends)])
+        return from_lo, from_hi
+    even = lax.axis_index(axis) % 2 == 0
+    first = lax.ppermute(
+        jnp.where(even, hi_edge, lo_edge), axis, [(i, i ^ 1) for i in range(count)]
+    )
+    pairs = []
+    for i in range(1, count, 2):
+        if i + 1 < count:
+            pairs += [(i, i + 1), (i + 1, i)]
+        elif closed:
+            pairs += [(i, 0), (0, i)]
+    second = lax.ppermute(jnp.where(even, lo_edge, hi_edge), axis, pairs)
+    return jnp.where(even, second, first), jnp.where(even, first, second)
+
+
 def extended(cells, sides, width, closed):
     for axis, dim in sides:
         count = lax.axis_size(axis)
         ends = count if closed else count - 1
         head = lax.slice_in_dim(cells, 0, width, axis=dim)
         tail = lax.slice_in_dim(cells, cells.shape[dim] - width, cells.shape[dim], axis=dim)
-        cells = jnp.concatenate(
-            [
-                lax.ppermute(tail, axis, [(i, (i + 1) % count) for i in range(ends)]),
-                cells,
-                lax.ppermute(head, axis, [((i + 1) % count, i) for i in range(ends)]),
-            ],
-            axis=dim,
-        )
+        from_lo, from_hi = neighbour_halos(head, tail, axis, closed)
+        cells = jnp.concatenate([from_lo, cells, from_hi], axis=dim)
     return cells
 
 
@@ -164,13 +179,11 @@
             [row, jnp.broadcast_to(number, (1, 1, value_count))], axis=1
         )
 
-    from_above = lax.ppermute(
+    from_above, from_below = neighbour_halos(
+        pack(advected[:1], diffusivity[0]),
         pack(advected[rows - 1 :], diffusivity[rows - 1]),
         "lat",
-        [(i, i + 1) for i in range(count - 1)],
-    )
-    from_below = lax.ppermute(
-        pack(advected[:1], diffusivity[0]), "lat", [(i + 1, i) for i in range(count - 1)]
+        False,
     )
     lat_wide = jnp.concatenate([from_above[:, :cols], advected, from_below[:, :cols]], axis=0)
     k_wide = jnp.concatenate([from_above[0, cols, :1], diffusivity, from_below[0, cols, :1]])

time: 82.7 us -> 82.3 us (level)
  starting transfers between devices: 30.3 us -> 24.8 us
  matrix products: 4.93 us -> 7.36 us
  other arithmetic: 12.3 us -> 13.9 us
  waiting for transfers between devices: 21.1 us -> 22.2 us
    ppermute x8, starting transfers between devices: 18 us -> 12.8 us  [the longest x4 6.76 us: neighbour_halos(): second = lax.ppermute(jnp.where(even, lo_edge, hi_edge), axis, pairs)]
    dot_general x2, matrix products: 3.79 us -> 6.22 us  [spatial(): jnp.einsum('nij,njv->niv', plane_weights(fraction_y, fraction_x), patches...]
    gather x2, local copies, waits for them, and re-layouts: 1.23 us -> 3.17 us  [departed(): arrived[pick_index]]
    select_n x0 -> x8, other arithmetic: none -> 1.4 us  [the longest x4 1.37 us: neighbour_halos(): jnp.where(even, hi_edge, lo_edge)]
    concatenate x2 -> x0, local copies, waits for them, and re-layouts: 1.25 us -> none  [pack(): jnp.concatenate([row, jnp.broadcast_to(number, (1, 1, value_count))], axi...]
  transfers between devices with their start and end apart: 14 -> 14, of which waited for: 8 -> 8; matrix products, arithmetic and copies ran while one was open for 10% -> 9% of each run, Pallas kernels for 0% -> 0%
where the time goes in v12:
time: 82.3 us; the launch traced here: 81.8 us
  starting transfers between devices  24.8 us (30%)
  waiting for transfers between devices  22.2 us (27%)
  other arithmetic  13.9 us (17%)
  local copies, waits for them, and re-layouts  12.9 us (16%)
  matrix products  7.36 us (9%)
    ppermute x4, waiting for transfers between devices, all_sum(): lax.ppermute(value, axis, [(i, i ^ distance) for i in range(count)])  8.67 us
    all_to_all x2, starting transfers between devices, departed(): lax.all_to_all(outgoing, 'lat', 0, 0, tiled=True)  8.04 us
    all_to_all x2, waiting for transfers between devices, departed(): lax.all_to_all(outgoing, 'lat', 0, 0, tiled=True)  7.19 us
    ppermute x4, starting transfers between devices, neighbour_halos(): second = lax.ppermute(jnp.where(even, lo_edge, hi_edge), axis, pairs)  6.76 us
    ppermute x4, waiting for transfers between devices, neighbour_halos(): second = lax.ppermute(jnp.where(even, lo_edge, hi_edge), axis, pairs)  6.38 us
    dot_general x2, matrix products, spatial(): jnp.einsum('nij,njv->niv', plane_weights(fraction_y, fraction_x), patches...  6.22 us
    ppermute x4, starting transfers between devices, neighbour_halos(): lax.ppermute(jnp.where(even, hi_edge, lo_edge), axis, [(i, i ^ 1) for i i...  6.06 us
    add x4, other arithmetic, levels(): acc = term if acc is None else acc + term  4.83 us
  transfers between devices with their start and end apart: 14, of which 8 were waited for; matrix products, arithmetic and copies ran while one was open for 9% of the time, Pallas kernels for 0%

profile of v12, /device:TPU:1, one launch (start us, length us, event | category | flops | bytes accessed | tf_op | source)
XLA Modules:
  0.0 81.8 jit_solution(11504563909065750344)
XLA Ops:
  0.0 1.4 %copy.20 = f32[4,8,8,8,128]{4,3,2,1,0:T(8,128)S(1)} copy(f32[4,8,8,8,128]{4,3,1,2,0:T(8,128)} %bitcast.153) | data formatting | bytes 2097152 | tf_op jit(solution)/shard_map/transpose | solution.py:131
  2.4 1.4 %gather_fusion = f32[16,64,128]{2,1,0:T(8,128)} fusion(f32[32,64,128]{2,1,0:T(8,128)S(1)} %bitcast.139, s32[1024]{0:T(1024)S(1)} %pad_clamp_fusion.5), kind=kCustom, calls=%fused_computation | custom fusion | bytes 1048640 | tf_op jit(solution)/shard_map/gather | solution.py:227
  3.8 4.4 %all-to-all-start = ((f32[4,4,64,128]{3,2,1,0:T(8,128)}), f32[4,4,64,128]{3,2,1,0:T(8,128)S(1)}, u32[]{:S(2)}, u32[]{:S(2)}) async-start(f32[4,4,64,128]{3,2,1,0:T(8,128)} %bitcast.14), calls=%async_computation | async-start | bytes 1048576 | tf_op jit(solution)/shard_map/all_to_all | solution.py:233
  12.1 3.9 %all-to-all-done = f32[4,4,64,128]{3,2,1,0:T(8,128)S(1)} async-done(((f32[4,4,64,128]{3,2,1,0:T(8,128)}), f32[4,4,64,128]{3,2,1,0:T(8,128)S(1)}, u32[]{:S(2)}, u32[]{:S(2)}) %all-to-all-start) | async-done | bytes 524320 | tf_op jit(solution)/shard_map/all_to_all | solution.py:233
  16.0 1.6 %gather_fusion.1 = f32[32,64,128]{2,1,0:T(8,128)} fusion(f32[16,64,128]{2,1,0:T(8,128)S(1)} %bitcast.143, s32[1024]{0:T(1024)S(1)} %pad_clamp_fusion.4), kind=kCustom, calls=%fused_computation.1 | custom fusion | bytes 2097280 | tf_op jit(solution)/shard_map/gather | solution.py:237
  17.6 3.1 %fusion.15 = f32[32,64,128]{2,1,0:T(8,128)S(1)} fusion(f32[32,64,128]{2,1,0:T(8,128)} %gather_fusion.1, f32[32,64,128]{2,1,0:T(8,128)S(1)} %gather_fusion.2, f32[32]{0:T(128)S(1)} %get-tuple-element.117, f32[32]{0:T(128)S(1)} %get-tuple-element.118, f32[32]{0:T(128)S(1)} %get-tuple-element.116, f32[32]{0:T(128)S(1)} %get-tuple-element.86, ...), kind=kOutput, calls=%fused_computation.42 | convolution fusion | flops 203554816 | bytes 3277856 | tf_op jit(solution)/shard_map/nij,njv->niv/dot_general | solution.py:103
  20.7 1.1 %multiply_add_fusion.6 = f32[32,64,32]{2,1,0:T(8,128)S(1)} fusion(f32[32,64,128]{2,1,0:T(8,128)S(1)} %fusion.15, f32[32]{0:T(128)S(1)} %get-tuple-element.74, f32[32]{0:T(128)S(1)} %get-tuple-element.75, f32[32]{0:T(128)S(1)} %get-tuple-element.76, f32[32]{0:T(128)S(1)} %get-tuple-element.77), kind=kLoop, calls=%fused_computation.40 | loop fusion | flops 458752 | bytes 1311232 | tf_op jit(solution)/shard_map/add | solution.py:121
  21.8 1.3 %multiply_add_fusion.7 = (f32[32,64,32]{2,1,0:T(8,128)S(1)}, f32[32,64,32]{2,1,0:T(8,128)S(1)}, f32[32,64,32]{2,1,0:T(8,128)S(1)}) fusion(f32[32,64,128]{2,1,0:T(8,128)S(1)} %fusion.15, f32[32]{0:T(128)S(1)} %get-tuple-element.78, f32[32]{0:T(128)S(1)} %get-tuple-element.79, f32[32]{0:T(128)S(1)} %get-tuple-element.68, f32[32]{0:T(128)S(1)} %get-tuple-element.71, ...), kind=kLoop, calls=%fused_computation.41 | loop fusion | flops 851968 | bytes 1836032 | tf_op jit(solution)/shard_map/add | solution.py:121
  24.2 2.2 %collective-permute-start.2 = (f32[32,1,128]{2,1,0:T(1,128)S(1)}, f32[32,1,128]{2,1,0:T(1,128)S(1)}, u32[]{:S(2)}, u32[]{:S(2)}) collective-permute-start(f32[32,1,128]{2,1,0:T(1,128)S(1)} %get-tuple-element.35), channel_id=1, source_target_pairs={{0,1},{1,0},{2,3},{3,2},{4,5},{5,4},{6,7},{7,6},{8,9},{9,8},{10,11... | collective-permute-start | bytes 49160 | tf_op jit(solution)/shard_map/ppermute | solution.py:42
  26.4 2.2 %collective-permute-start.3 = (f32[32,1,128]{2,1,0:T(1,128)S(1)}, f32[32,1,128]{2,1,0:T(1,128)S(1)}, u32[]{:S(2)}, u32[]{:S(2)}) collective-permute-start(f32[32,1,128]{2,1,0:T(1,128)S(1)} %get-tuple-element.36), channel_id=1, source_target_pairs={{1,2},{2,1},{3,0},{0,3},{5,6},{6,5},{7,4},{4,7},{9,10},{10,9},{11,... | collective-permute-start | bytes 49160 | tf_op jit(solution)/shard_map/ppermute | solution.py:51
  28.6 1.3 %pad_select_fusion.1 = (f32[1,65,128]{2,1,0:T(8,128)S(1)}, f32[1,65,128]{2,1,0:T(8,128)S(1)}) fusion(f32[1,64,128]{2,1,0:T(8,128)S(1)} %get-tuple-element.34, f32[]{:T(128)} %bitcast.35, f32[1,64,128]{2,1,0:T(8,128)S(1)} %get-tuple-element.33, f32[]{:T(128)} %bitcast.34, pred[]{:T(512)S(6)} %eq.357), kind=kLoop, calls=%fused_computation.141 | loop fusion | flops 16640 | bytes 132105 | tf_op jit(solution)/shard_map/jit(_where)/select_n | solution.py:43
  29.9 1.5 %collective-permute-start = (f32[1,65,128]{2,1,0:T(8,128)S(1)}, f32[1,65,128]{2,1,0:T(8,128)S(1)}, u32[]{:S(2)}, u32[]{:S(2)}) collective-permute-start(f32[1,65,128]{2,1,0:T(8,128)S(1)} %get-tuple-element.44), channel_id=1, source_target_pairs={{0,4},{4,0},{8,12},{12,8},{1,5},{5,1},{9,13},{13,9},{2,6},{6,2},{1... | collective-permute-start | bytes 99848 | tf_op jit(solution)/shard_map/ppermute | solution.py:42
  31.4 1.9 %collective-permute-start.1 = (f32[1,65,128]{2,1,0:T(8,128)S(1)}, f32[1,65,128]{2,1,0:T(8,128)S(1)}, u32[]{:S(2)}, u32[]{:S(2)}) collective-permute-start(f32[1,65,128]{2,1,0:T(8,128)S(1)} %get-tuple-element.45), channel_id=1, source_target_pairs={{4,8},{8,4},{5,9},{9,5},{6,10},{10,6},{7,11},{11,7},{20,24},{24,20... | collective-permute-start | bytes 99848 | tf_op jit(solution)/shard_map/ppermute | solution.py:51
  33.4 3.3 %collective-permute-done.1 = f32[1,65,128]{2,1,0:T(8,128)S(1)} collective-permute-done((f32[1,65,128]{2,1,0:T(8,128)S(1)}, f32[1,65,128]{2,1,0:T(8,128)S(1)}, u32[]{:S(2)}, u32[]{:S(2)}) %collective-permute-start.1) | collective-permute-done | bytes 33312 | tf_op jit(solution)/shard_map/ppermute | solution.py:51
  38.7 1.4 %gather_fusion.3 = f32[16,64,128]{2,1,0:T(8,128)} fusion(f32[32,64,128]{2,1,0:T(8,128)S(1)} %bitcast.141, s32[1024]{0:T(1024)S(1)} %pad_clamp_fusion.2), kind=kCustom, calls=%fused_computation.3 | custom fusion | bytes 1048640 | tf_op jit(solution)/shard_map/gather | solution.py:227
  40.1 3.6 %all-to-all-start.1 = ((f32[4,4,64,128]{3,2,1,0:T(8,128)}), f32[4,4,64,128]{3,2,1,0:T(8,128)S(1)}, u32[]{:S(2)}, u32[]{:S(2)}) async-start(f32[4,4,64,128]{3,2,1,0:T(8,128)} %bitcast.40), calls=%async_computation.1 | async-start | bytes 1048576 | tf_op jit(solution)/shard_map/all_to_all | solution.py:233
  44.4 1.4 %maximum_multiply_fusion = f32[34]{0:T(128)S(1)} fusion(f32[1]{0:T(128)} %bitcast.47, f32[32]{0:T(128)S(1)} %copy-done.3, f32[1]{0:T(128)} %bitcast.46, s32[]{:T(128)S(6)} %sub.190), kind=kLoop, calls=%fused_computation.305 | loop fusion | flops 272 | bytes 276 | tf_op jit(solution)/shard_map/mul | solution.py:263
  46.4 3.3 %all-to-all-done.1 = f32[4,4,64,128]{3,2,1,0:T(8,128)S(1)} async-done(((f32[4,4,64,128]{3,2,1,0:T(8,128)}), f32[4,4,64,128]{3,2,1,0:T(8,128)S(1)}, u32[]{:S(2)}, u32[]{:S(2)}) %all-to-all-start.1) | async-done | bytes 524320 | tf_op jit(solution)/shard_map/all_to_all | solution.py:233
  49.6 1.6 %gather_fusion.4 = f32[32,64,128]{2,1,0:T(8,128)} fusion(f32[16,64,128]{2,1,0:T(8,128)S(1)} %bitcast.144, s32[1024]{0:T(1024)S(1)} %pad_clamp_fusion.1), kind=kCustom, calls=%fused_computation.4 | custom fusion | bytes 2097280 | tf_op jit(solution)/shard_map/gather | solution.py:237
  51.2 3.1 %fusion.13 = f32[32,64,128]{2,1,0:T(8,128)S(1)} fusion(f32[32,64,128]{2,1,0:T(8,128)} %gather_fusion.4, f32[32,64,128]{2,1,0:T(8,128)S(1)} %gather_fusion.5, f32[64,64]{1,0:T(8,128)S(1)} %get-tuple-element.93, f32[32]{0:T(128)S(1)} %get-tuple-element.106, f32[64,64]{1,0:T(8,128)S(1)} %get-tuple-element.94, f32[32]{0:T(128)S(1)} %get-tuple-element.107, ...), kind=kOutput, calls=%fused_computation.36 | convolution fusion | flops 203554816 | bytes 3277856 | tf_op jit(solution)/shard_map/nij,njv->niv/dot_general | solution.py:103
  54.3 1.0 %fusion.149 = f32[32,1,128]{2,1,0:T(1,128)S(1)} fusion(f32[32,64,1]{1,2,0:T(1,128)S(1)} %bitcast.155, f32[32,64,128]{2,1,0:T(8,128)S(1)} %fusion.13), kind=kOutput, calls=%fused_computation.357 | convolution fusion | flops 3145728 | bytes 1073152 | tf_op jit(solution)/shard_map/pi,piv->pv/dot_general | solution.py:266
  56.1 2.1 %collective-permute-done.4 = f32[768]{0:T(1024)S(1)} collective-permute-done((f32[768]{0:T(1024)S(1)}, f32[768]{0:T(1024)S(1)}, u32[]{:S(2)}, u32[]{:S(2)}) %collective-permute-start.4) | collective-permute-done | bytes 3104 | tf_op jit(solution)/shard_map/ppermute | solution.py:22
  58.3 3.3 %collective-permute-done.5 = f32[768]{0:T(1024)S(1)} collective-permute-done((f32[768]{0:T(1024)S(1)}, f32[768]{0:T(1024)S(1)}, u32[]{:S(2)}, u32[]{:S(2)}) %collective-permute-start.5) | collective-permute-done | bytes 3104 | tf_op jit(solution)/shard_map/ppermute | solution.py:22
  61.6 3.4 %collective-permute-start.6 = (f32[768]{0:T(1024)S(1)}, f32[768]{0:T(1024)S(1)}, u32[]{:S(2)}, u32[]{:S(2)}) collective-permute-start(f32[768]{0:T(1024)S(1)} %add.873), channel_id=1, source_target_pairs={{0,4},{4,0},{8,12},{12,8},{1,5},{5,1},{9,13},{13,9},{2,6},{6,2},{1... | collective-permute-start | bytes 9224 | tf_op jit(solution)/shard_map/ppermute | solution.py:22
  65.9 2.4 %collective-permute-done.7 = f32[768]{0:T(1024)S(1)} collective-permute-done((f32[768]{0:T(1024)S(1)}, f32[768]{0:T(1024)S(1)}, u32[]{:S(2)}, u32[]{:S(2)}) %collective-permute-start.7) | collective-permute-done | bytes 3104 | tf_op jit(solution)/shard_map/ppermute | solution.py:22
  68.5 1.1 %multiply_add_fusion.2 = f32[32,64,32]{2,1,0:T(8,128)S(1)} fusion(f32[32,64,128]{2,1,0:T(8,128)S(1)} %broadcast_multiply_fusion, f32[32]{0:T(128)S(1)} %get-tuple-element.60, f32[32]{0:T(128)S(1)} %get-tuple-element.61, f32[32]{0:T(128)S(1)} %get-tuple-element.62, f32[32]{0:T(128)S(1)} %get-tuple-element.63), kind=kLoop, calls=%fused_computation.32 | loop fusion | flops 458752 | bytes 1311232 | tf_op jit(solution)/shard_map/add | solution.py:121
  69.6 1.3 %multiply_add_fusion.3 = (f32[32,64,32]{2,1,0:T(8,128)S(1)}, f32[32,64,32]{2,1,0:T(8,128)S(1)}, f32[32,64,32]{2,1,0:T(8,128)S(1)}) fusion(f32[32,64,128]{2,1,0:T(8,128)S(1)} %broadcast_multiply_fusion, f32[32]{0:T(128)S(1)} %get-tuple-element.64, f32[32]{0:T(128)S(1)} %get-tuple-element.65, f32[32]{0:T(128)S(1)} %get-tuple-element.54, ...), kind=kLoop, calls=%fused_computation.33 | loop fusion | flops 851968 | bytes 1836032 | tf_op jit(solution)/shard_map/add | solution.py:121
  70.9 0.9 %pad_maximum_fusion.9 = f32[32,64,128]{2,1,0:T(8,128)S(1)} fusion(f32[32,64,32]{2,1,0:T(8,128)S(1)} %get-tuple-element.32, f32[32,64,32]{2,1,0:T(8,128)S(1)} %get-tuple-element.31, f32[32,64,32]{2,1,0:T(8,128)S(1)} %multiply_add_fusion.2, f32[32,64,32]{2,1,0:T(8,128)S(1)} %get-tuple-element.30), kind=kLoop, calls=%fused_computation.29 | loop fusion | flops 786432 | bytes 2097152 | tf_op jit(solution)/shard_map/concatenate | solution.py:123
  73.2 1.9 %collective-permute-start.8 = (f32[1,64,128]{2,1,0:T(8,128)S(1)}, f32[1,64,128]{2,1,0:T(8,128)S(1)}, u32[]{:S(2)}, u32[]{:S(2)}) collective-permute-start(f32[1,64,128]{2,1,0:T(8,128)S(1)} %get-tuple-element.26), channel_id=1, source_target_pairs={{0,4},{4,0},{8,12},{12,8},{1,5},{5,1},{9,13},{13,9},{2,6},{6,2},{1... | collective-permute-start | bytes 98312 | tf_op jit(solution)/shard_map/ppermute | solution.py:42
  75.2 1.9 %collective-permute-start.9 = (f32[1,64,128]{2,1,0:T(8,128)S(1)}, f32[1,64,128]{2,1,0:T(8,128)S(1)}, u32[]{:S(2)}, u32[]{:S(2)}) collective-permute-start(f32[1,64,128]{2,1,0:T(8,128)S(1)} %get-tuple-element.27), channel_id=1, source_target_pairs={{4,8},{8,4},{5,9},{9,5},{6,10},{10,6},{7,11},{11,7},{20,24},{24,20... | collective-permute-start | bytes 98312 | tf_op jit(solution)/shard_map/ppermute | solution.py:51
  77.3 3.1 %collective-permute-done.9 = f32[1,64,128]{2,1,0:T(8,128)S(1)} collective-permute-done((f32[1,64,128]{2,1,0:T(8,128)S(1)}, f32[1,64,128]{2,1,0:T(8,128)S(1)}, u32[]{:S(2)}, u32[]{:S(2)}) %collective-permute-start.9) | collective-permute-done | bytes 32800 | tf_op jit(solution)/shard_map/ppermute | solution.py:51
  80.4 1.4 %fusion.4 = f32[32,64,128]{2,1,0:T(8,128)} fusion(f32[32,64,128]{2,1,0:T(8,128)S(1)} %bitcast.147, f32[32,1,128]{2,1,0:T(1,128)S(1)} %bitcast.160, f32[32,1,128]{2,1,0:T(1,128)S(1)} %bitcast.159, f32[1,64,128]{2,1,0:T(8,128)S(1)} %get-tuple-element.43, f32[1,64,128]{2,1,0:T(8,128)S(1)} %get-tuple-element.42, f32[128]{0:T(128)S(1)} %slice_divide_fusion.1, ...), kind=kLoop, calls=%fused_computation.12 | loop fusion | flops 3145728 | bytes 2196096 | tf_op jit(solution)/shard_map/mul | solution.py:286
  (122 shorter events, 12.4 us)
Async XLA Ops:
  0.0 1.4 %copy-start.2 = (s32[2,16,32]{2,1,0:T(8,128)S(1)}, s32[2,16,32]{2,1,0:T(8,128)}, u32[]{:S(2)}) copy-start(s32[2,16,32]{2,1,0:T(8,128)} %param.7) | copy-start | bytes 12292
  3.8 4.5 %copy-start.1 = (f32[2,3,16,32]{3,2,1,0:T(8,128)S(1)}, f32[2,3,16,32]{3,2,1,0:T(8,128)}, u32[]{:S(2)}) copy-start(f32[2,3,16,32]{3,2,1,0:T(8,128)} %param.5) | copy-start | bytes 36868
  3.8 12.2 %all-to-all-start = ((f32[4,4,64,128]{3,2,1,0:T(8,128)}), f32[4,4,64,128]{3,2,1,0:T(8,128)S(1)}, u32[]{:S(2)}, u32[]{:S(2)}) async-start(f32[4,4,64,128]{3,2,1,0:T(8,128)} %bitcast.14), calls=%async_computation | async-start | bytes 1048576 | tf_op jit(solution)/shard_map/all_to_all | solution.py:233
  10.7 0.7 copy-start.3
  24.0 13.9 %copy-start = (f32[32,64,128]{2,1,0:T(8,128)S(1)}, f32[32,64,128]{2,1,0:T(8,128)}, u32[]{:S(2)}) copy-start(f32[32,64,128]{2,1,0:T(8,128)} %param.4) | copy-start | bytes 3145732
  24.2 9.2 %collective-permute-start.2 = (f32[32,1,128]{2,1,0:T(1,128)S(1)}, f32[32,1,128]{2,1,0:T(1,128)S(1)}, u32[]{:S(2)}, u32[]{:S(2)}) collective-permute-start(f32[32,1,128]{2,1,0:T(1,128)S(1)} %get-tuple-element.35), channel_id=1, source_target_pairs={{0,1},{1,0},{2,3},{3,2},{4,5},{5,4},{6,7},{7,6},{8,9},{9,8},{10,11... | collective-permute-start | bytes 49160 | tf_op jit(solution)/shard_map/ppermute | solution.py:42
  26.4 6.9 %collective-permute-start.3 = (f32[32,1,128]{2,1,0:T(1,128)S(1)}, f32[32,1,128]{2,1,0:T(1,128)S(1)}, u32[]{:S(2)}, u32[]{:S(2)}) collective-permute-start(f32[32,1,128]{2,1,0:T(1,128)S(1)} %get-tuple-element.36), channel_id=1, source_target_pairs={{1,2},{2,1},{3,0},{0,3},{5,6},{6,5},{7,4},{4,7},{9,10},{10,9},{11,... | collective-permute-start | bytes 49160 | tf_op jit(solution)/shard_map/ppermute | solution.py:51
  29.9 3.5 %collective-permute-start = (f32[1,65,128]{2,1,0:T(8,128)S(1)}, f32[1,65,128]{2,1,0:T(8,128)S(1)}, u32[]{:S(2)}, u32[]{:S(2)}) collective-permute-start(f32[1,65,128]{2,1,0:T(8,128)S(1)} %get-tuple-element.44), channel_id=1, source_target_pairs={{0,4},{4,0},{8,12},{12,8},{1,5},{5,1},{9,13},{13,9},{2,6},{6,2},{1... | collective-permute-start | bytes 99848 | tf_op jit(solution)/shard_map/ppermute | solution.py:42
  31.4 5.3 %collective-permute-start.1 = (f32[1,65,128]{2,1,0:T(8,128)S(1)}, f32[1,65,128]{2,1,0:T(8,128)S(1)}, u32[]{:S(2)}, u32[]{:S(2)}) collective-permute-start(f32[1,65,128]{2,1,0:T(8,128)S(1)} %get-tuple-element.45), channel_id=1, source_target_pairs={{4,8},{8,4},{5,9},{9,5},{6,10},{10,6},{7,11},{11,7},{20,24},{24,20... | collective-permute-start | bytes 99848 | tf_op jit(solution)/shard_map/ppermute | solution.py:51
  40.1 9.5 %all-to-all-start.1 = ((f32[4,4,64,128]{3,2,1,0:T(8,128)}), f32[4,4,64,128]{3,2,1,0:T(8,128)S(1)}, u32[]{:S(2)}, u32[]{:S(2)}) async-start(f32[4,4,64,128]{3,2,1,0:T(8,128)} %bitcast.40), calls=%async_computation.1 | async-start | bytes 1048576 | tf_op jit(solution)/shard_map/all_to_all | solution.py:233
  55.7 2.5 %collective-permute-start.4 = (f32[768]{0:T(1024)S(1)}, f32[768]{0:T(1024)S(1)}, u32[]{:S(2)}, u32[]{:S(2)}) collective-permute-start(f32[768]{0:T(1024)S(1)} %pad_maximum_fusion.10), channel_id=1, source_target_pairs={{0,1},{1,0},{2,3},{3,2},{4,5},{5,4},{6,7},{7,6},{8,9},{9,8},{10,11... | collective-permute-start | bytes 9224 | tf_op jit(solution)/shard_map/ppermute | solution.py:22
  58.2 3.4 %collective-permute-start.5 = (f32[768]{0:T(1024)S(1)}, f32[768]{0:T(1024)S(1)}, u32[]{:S(2)}, u32[]{:S(2)}) collective-permute-start(f32[768]{0:T(1024)S(1)} %fusion.137), channel_id=1, source_target_pairs={{0,2},{1,3},{2,0},{3,1},{4,6},{5,7},{6,4},{7,5},{8,10},{9,11},{10,... | collective-permute-start | bytes 9224 | tf_op jit(solution)/shard_map/ppermute | solution.py:22
  61.6 4.3 %collective-permute-start.6 = (f32[768]{0:T(1024)S(1)}, f32[768]{0:T(1024)S(1)}, u32[]{:S(2)}, u32[]{:S(2)}) collective-permute-start(f32[768]{0:T(1024)S(1)} %add.873), channel_id=1, source_target_pairs={{0,4},{4,0},{8,12},{12,8},{1,5},{5,1},{9,13},{13,9},{2,6},{6,2},{1... | collective-permute-start | bytes 9224 | tf_op jit(solution)/shard_map/ppermute | solution.py:22
  65.9 2.5 %collective-permute-start.7 = (f32[768]{0:T(1024)S(1)}, f32[768]{0:T(1024)S(1)}, u32[]{:S(2)}, u32[]{:S(2)}) collective-permute-start(f32[768]{0:T(1024)S(1)} %add.874), channel_id=1, source_target_pairs={{0,8},{4,12},{8,0},{12,4},{1,9},{5,13},{9,1},{13,5},{2,10},{6,14},... | collective-permute-start | bytes 9224 | tf_op jit(solution)/shard_map/ppermute | solution.py:22
  72.1 5.2 %collective-permute-start.10 = (f32[32,1,128]{2,1,0:T(1,128)S(1)}, f32[32,1,128]{2,1,0:T(1,128)S(1)}, u32[]{:S(2)}, u32[]{:S(2)}) collective-permute-start(f32[32,1,128]{2,1,0:T(1,128)S(1)} %get-tuple-element.28), channel_id=1, source_target_pairs={{0,1},{1,0},{2,3},{3,2},{4,5},{5,4},{6,7},{7,6},{8,9},{9,8},{10,11... | collective-permute-start | bytes 49160 | tf_op jit(solution)/shard_map/ppermute | solution.py:42
  72.5 4.8 %collective-permute-start.11 = (f32[32,1,128]{2,1,0:T(1,128)S(1)}, f32[32,1,128]{2,1,0:T(1,128)S(1)}, u32[]{:S(2)}, u32[]{:S(2)}) collective-permute-start(f32[32,1,128]{2,1,0:T(1,128)S(1)} %get-tuple-element.29), channel_id=1, source_target_pairs={{1,2},{2,1},{3,0},{0,3},{5,6},{6,5},{7,4},{4,7},{9,10},{10,9},{11,... | collective-permute-start | bytes 49160 | tf_op jit(solution)/shard_map/ppermute | solution.py:51
  73.2 4.1 %collective-permute-start.8 = (f32[1,64,128]{2,1,0:T(8,128)S(1)}, f32[1,64,128]{2,1,0:T(8,128)S(1)}, u32[]{:S(2)}, u32[]{:S(2)}) collective-permute-start(f32[1,64,128]{2,1,0:T(8,128)S(1)} %get-tuple-element.26), channel_id=1, source_target_pairs={{0,4},{4,0},{8,12},{12,8},{1,5},{5,1},{9,13},{13,9},{2,6},{6,2},{1... | collective-permute-start | bytes 98312 | tf_op jit(solution)/shard_map/ppermute | solution.py:42
  75.2 5.2 %collective-permute-start.9 = (f32[1,64,128]{2,1,0:T(8,128)S(1)}, f32[1,64,128]{2,1,0:T(8,128)S(1)}, u32[]{:S(2)}, u32[]{:S(2)}) collective-permute-start(f32[1,64,128]{2,1,0:T(8,128)S(1)} %get-tuple-element.27), channel_id=1, source_target_pairs={{4,8},{8,4},{5,9},{9,5},{6,10},{10,6},{7,11},{11,7},{20,24},{24,20... | collective-permute-start | bytes 98312 | tf_op jit(solution)/shard_map/ppermute | solution.py:51

commit v13 on v12

--- a/solution.py
+++ b/solution.py
@@ -234,7 +234,20 @@
         lat_count * CAP, 64, value_count
     )
     pick_index = my_dev * CAP + my_slot
-    patches = jnp.where(my_remote[:, None, None], arrived[pick_index], own_patches[my_local])
+    take_near = (my_local[:, None] == jnp.arange(per_device)[None, :]) & ~my_remote[:, None]
+    take_far = (pick_index[:, None] == jnp.arange(lat_count * CAP)[None, :]) & my_remote[:, None]
+    patches = (
+        jnp.dot(
+            take_near.astype(jnp.float32),
+            own_patches.reshape(per_device, -1),
+            precision=lax.Precision.HIGHEST,
+        )
+        + jnp.dot(
+            take_far.astype(jnp.float32),
+            arrived.reshape(lat_count * CAP, -1),
+            precision=lax.Precision.HIGHEST,
+        )
+    ).reshape(per_device, 64, value_count)
     return patches, my_frac
 
 

time: 82.3 us -> 78.6 us (0.955)
  local copies, waits for them, and re-layouts: 12.9 us -> 9.21 us
    gather x4 -> x0, local copies, waits for them, and re-layouts: 4.4 us -> none  [the longest x2 3.17 us: departed(): arrived[pick_index]]
    dot_general x0 -> x4, matrix products: none -> 2.9 us  [the longest x2 1.66 us: departed(): jnp.dot(take_far.astype(jnp.float32), arrived.reshape(lat_count * CAP, -1...]
    dot_general x2, matrix products: 6.22 us -> 3.69 us  [spatial(): jnp.einsum('nij,njv->niv', plane_weights(fraction_y, fraction_x), patches...]
where the time goes in v13:
time: 78.6 us; the launch traced here: 78.2 us
  starting transfers between devices  24.8 us (32%)
  waiting for transfers between devices  22.3 us (28%)
  other arithmetic  13.6 us (17%)
  local copies, waits for them, and re-layouts  9.21 us (12%)
  matrix products  7.72 us (10%)
    ppermute x4, waiting for transfers between devices, all_sum(): lax.ppermute(value, axis, [(i, i ^ distance) for i in range(count)])  8.67 us
    all_to_all x2, starting transfers between devices, departed(): lax.all_to_all(outgoing, 'lat', 0, 0, tiled=True)  8.04 us
    all_to_all x2, waiting for transfers between devices, departed(): lax.all_to_all(outgoing, 'lat', 0, 0, tiled=True)  7.19 us
    ppermute x4, starting transfers between devices, neighbour_halos(): second = lax.ppermute(jnp.where(even, lo_edge, hi_edge), axis, pairs)  6.76 us
    ppermute x4, waiting for transfers between devices, neighbour_halos(): second = lax.ppermute(jnp.where(even, lo_edge, hi_edge), axis, pairs)  6.38 us
    ppermute x4, starting transfers between devices, neighbour_halos(): lax.ppermute(jnp.where(even, hi_edge, lo_edge), axis, [(i, i ^ 1) for i i...  6.05 us
    add x4, other arithmetic, levels(): acc = term if acc is None else acc + term  4.85 us
    ppermute x4, starting transfers between devices, all_sum(): lax.ppermute(value, axis, [(i, i ^ distance) for i in range(count)])  3.97 us
  transfers between devices with their start and end apart: 14, of which 8 were waited for; matrix products, arithmetic and copies ran while one was open for 9% of the time, Pallas kernels for 0%

profile of v13, /device:TPU:1, one launch (start us, length us, event | category | flops | bytes accessed | tf_op | source)
XLA Modules:
  0.0 78.2 jit_solution(7460721866577726759)
XLA Ops:
  0.0 1.4 %copy.22 = f32[4,8,8,8,128]{4,3,2,1,0:T(8,128)S(1)} copy(f32[4,8,8,8,128]{4,3,1,2,0:T(8,128)} %bitcast.161) | data formatting | bytes 2097152 | tf_op jit(solution)/shard_map/transpose | solution.py:131
  2.4 1.4 %gather_fusion = f32[16,64,128]{2,1,0:T(8,128)} fusion(f32[32,64,128]{2,1,0:T(8,128)S(1)} %bitcast.151, s32[1024]{0:T(1024)S(1)} %pad_clamp_fusion.1), kind=kCustom, calls=%fused_computation | custom fusion | bytes 1048640 | tf_op jit(solution)/shard_map/gather | solution.py:227
  3.8 4.4 %all-to-all-start = ((f32[4,4,64,128]{3,2,1,0:T(8,128)}), f32[4,4,64,128]{3,2,1,0:T(8,128)S(1)}, u32[]{:S(2)}, u32[]{:S(2)}) async-start(f32[4,4,64,128]{3,2,1,0:T(8,128)} %bitcast.18), calls=%async_computation | async-start | bytes 1048576 | tf_op jit(solution)/shard_map/all_to_all | solution.py:233
  12.2 3.8 %all-to-all-done = f32[4,4,64,128]{3,2,1,0:T(8,128)S(1)} async-done(((f32[4,4,64,128]{3,2,1,0:T(8,128)}), f32[4,4,64,128]{3,2,1,0:T(8,128)S(1)}, u32[]{:S(2)}, u32[]{:S(2)}) %all-to-all-start) | async-done | bytes 524320 | tf_op jit(solution)/shard_map/all_to_all | solution.py:233
  17.0 1.8 %fusion.15 = f32[32,64,128]{2,1,0:T(8,128)S(1)} fusion(f32[32,64,128]{2,1,0:T(8,128)S(1)} %bitcast.166, f32[32]{0:T(128)S(1)} %get-tuple-element.121, f32[32]{0:T(128)S(1)} %get-tuple-element.122, f32[32]{0:T(128)S(1)} %get-tuple-element.120, f32[32]{0:T(128)S(1)} %get-tuple-element.90, f32[32]{0:T(128)S(1)} %get-tuple-element.118, ...), kind=kOutput, calls=%fused_computation.40 | convolution fusion | flops 203292672 | bytes 2229248 | tf_op jit(solution)/shard_map/nij,njv->niv/dot_general | solution.py:103
  18.9 1.1 %multiply_add_fusion.6 = f32[32,64,32]{2,1,0:T(8,128)S(1)} fusion(f32[32,64,128]{2,1,0:T(8,128)S(1)} %fusion.15, f32[32]{0:T(128)S(1)} %get-tuple-element.78, f32[32]{0:T(128)S(1)} %get-tuple-element.79, f32[32]{0:T(128)S(1)} %get-tuple-element.80, f32[32]{0:T(128)S(1)} %get-tuple-element.81), kind=kLoop, calls=%fused_computation.38 | loop fusion | flops 458752 | bytes 1311232 | tf_op jit(solution)/shard_map/add | solution.py:121
  20.0 1.3 %multiply_add_fusion.7 = (f32[32,64,32]{2,1,0:T(8,128)S(1)}, f32[32,64,32]{2,1,0:T(8,128)S(1)}, f32[32,64,32]{2,1,0:T(8,128)S(1)}) fusion(f32[32,64,128]{2,1,0:T(8,128)S(1)} %fusion.15, f32[32]{0:T(128)S(1)} %get-tuple-element.82, f32[32]{0:T(128)S(1)} %get-tuple-element.83, f32[32]{0:T(128)S(1)} %get-tuple-element.72, f32[32]{0:T(128)S(1)} %get-tuple-element.75, ...), kind=kLoop, calls=%fused_computation.39 | loop fusion | flops 851968 | bytes 1836032 | tf_op jit(solution)/shard_map/add | solution.py:121
  21.3 0.9 %pad_maximum_fusion.8 = f32[32,64,128]{2,1,0:T(8,128)S(1)} fusion(f32[32,64,32]{2,1,0:T(8,128)S(1)} %get-tuple-element.43, f32[32,64,32]{2,1,0:T(8,128)S(1)} %get-tuple-element.42, f32[32,64,32]{2,1,0:T(8,128)S(1)} %multiply_add_fusion.6, f32[32,64,32]{2,1,0:T(8,128)S(1)} %get-tuple-element.41), kind=kLoop, calls=%fused_computation.28 | loop fusion | flops 786432 | bytes 2097152 | tf_op jit(solution)/shard_map/concatenate | solution.py:123
  22.4 2.2 %collective-permute-start.2 = (f32[32,1,128]{2,1,0:T(1,128)S(1)}, f32[32,1,128]{2,1,0:T(1,128)S(1)}, u32[]{:S(2)}, u32[]{:S(2)}) collective-permute-start(f32[32,1,128]{2,1,0:T(1,128)S(1)} %get-tuple-element.39), channel_id=1, source_target_pairs={{0,1},{1,0},{2,3},{3,2},{4,5},{5,4},{6,7},{7,6},{8,9},{9,8},{10,11... | collective-permute-start | bytes 49160 | tf_op jit(solution)/shard_map/ppermute | solution.py:42
  24.6 2.2 %collective-permute-start.3 = (f32[32,1,128]{2,1,0:T(1,128)S(1)}, f32[32,1,128]{2,1,0:T(1,128)S(1)}, u32[]{:S(2)}, u32[]{:S(2)}) collective-permute-start(f32[32,1,128]{2,1,0:T(1,128)S(1)} %get-tuple-element.40), channel_id=1, source_target_pairs={{1,2},{2,1},{3,0},{0,3},{5,6},{6,5},{7,4},{4,7},{9,10},{10,9},{11,... | collective-permute-start | bytes 49160 | tf_op jit(solution)/shard_map/ppermute | solution.py:51
  26.8 1.2 %pad_select_fusion.1 = (f32[1,65,128]{2,1,0:T(8,128)S(1)}, f32[1,65,128]{2,1,0:T(8,128)S(1)}) fusion(f32[1,64,128]{2,1,0:T(8,128)S(1)} %get-tuple-element.38, f32[]{:T(128)} %bitcast.34, f32[1,64,128]{2,1,0:T(8,128)S(1)} %get-tuple-element.37, f32[]{:T(128)} %bitcast.33, pred[]{:T(512)S(6)} %eq.424), kind=kLoop, calls=%fused_computation.141 | loop fusion | flops 16640 | bytes 132105 | tf_op jit(solution)/shard_map/jit(_where)/select_n | solution.py:43
  28.0 1.5 %collective-permute-start = (f32[1,65,128]{2,1,0:T(8,128)S(1)}, f32[1,65,128]{2,1,0:T(8,128)S(1)}, u32[]{:S(2)}, u32[]{:S(2)}) collective-permute-start(f32[1,65,128]{2,1,0:T(8,128)S(1)} %get-tuple-element.48), channel_id=1, source_target_pairs={{0,4},{4,0},{8,12},{12,8},{1,5},{5,1},{9,13},{13,9},{2,6},{6,2},{1... | collective-permute-start | bytes 99848 | tf_op jit(solution)/shard_map/ppermute | solution.py:42
  29.5 1.9 %collective-permute-start.1 = (f32[1,65,128]{2,1,0:T(8,128)S(1)}, f32[1,65,128]{2,1,0:T(8,128)S(1)}, u32[]{:S(2)}, u32[]{:S(2)}) collective-permute-start(f32[1,65,128]{2,1,0:T(8,128)S(1)} %get-tuple-element.49), channel_id=1, source_target_pairs={{4,8},{8,4},{5,9},{9,5},{6,10},{10,6},{7,11},{11,7},{20,24},{24,20... | collective-permute-start | bytes 99848 | tf_op jit(solution)/shard_map/ppermute | solution.py:51
  31.5 3.3 %collective-permute-done.1 = f32[1,65,128]{2,1,0:T(8,128)S(1)} collective-permute-done((f32[1,65,128]{2,1,0:T(8,128)S(1)}, f32[1,65,128]{2,1,0:T(8,128)S(1)}, u32[]{:S(2)}, u32[]{:S(2)}) %collective-permute-start.1) | collective-permute-done | bytes 33312 | tf_op jit(solution)/shard_map/ppermute | solution.py:51
  37.0 1.4 %gather_fusion.1 = f32[16,64,128]{2,1,0:T(8,128)} fusion(f32[32,64,128]{2,1,0:T(8,128)S(1)} %bitcast.152, s32[1024]{0:T(1024)S(1)} %pad_clamp_fusion), kind=kCustom, calls=%fused_computation.1 | custom fusion | bytes 1048640 | tf_op jit(solution)/shard_map/gather | solution.py:227
  38.4 3.6 %all-to-all-start.1 = ((f32[4,4,64,128]{3,2,1,0:T(8,128)}), f32[4,4,64,128]{3,2,1,0:T(8,128)S(1)}, u32[]{:S(2)}, u32[]{:S(2)}) async-start(f32[4,4,64,128]{3,2,1,0:T(8,128)} %bitcast.41), calls=%async_computation.1 | async-start | bytes 1048576 | tf_op jit(solution)/shard_map/all_to_all | solution.py:233
  42.0 1.3 %maximum_multiply_fusion = f32[34]{0:T(128)S(1)} fusion(f32[1]{0:T(128)} %bitcast.43, f32[32]{0:T(128)S(1)} %copy-done.3, f32[1]{0:T(128)} %bitcast.42, s32[]{:T(128)S(6)} %sub.190), kind=kLoop, calls=%fused_computation.311 | loop fusion | flops 272 | bytes 276 | tf_op jit(solution)/shard_map/mul | solution.py:276
  44.5 3.4 %all-to-all-done.1 = f32[4,4,64,128]{3,2,1,0:T(8,128)S(1)} async-done(((f32[4,4,64,128]{3,2,1,0:T(8,128)}), f32[4,4,64,128]{3,2,1,0:T(8,128)S(1)}, u32[]{:S(2)}, u32[]{:S(2)}) %all-to-all-start.1) | async-done | bytes 524320 | tf_op jit(solution)/shard_map/all_to_all | solution.py:233
  47.8 0.8 %fusion.1 = f32[4,8,64,128]{3,1,2,0:T(8,128)S(1)} fusion(f32[32,8192]{1,0:T(8,128)S(1)} %fusion.105, f32[2,8,64,128]{3,2,1,0:T(8,128)S(1)} %bitcast.164, s32[32]{0:T(128)S(1)} %fusion.153, pred[32]{0:T(512)(128)(4,1)S(1)} %get-tuple-element.18), kind=kOutput, calls=%fused_computation.5 | convolution fusion | flops 50594816 | bytes 2621600 | tf_op jit(solution)/shard_map/dot_general | solution.py:245
  48.9 1.8 %fusion.31 = f32[32,64,128]{2,1,0:T(8,128)S(1)} fusion(f32[32,64,128]{2,1,0:T(8,128)S(1)} %bitcast.165, f32[64,64]{1,0:T(8,128)S(1)} %get-tuple-element.97, f32[32]{0:T(128)S(1)} %get-tuple-element.110, f32[64,64]{1,0:T(8,128)S(1)} %get-tuple-element.98, f32[32]{0:T(128)S(1)} %get-tuple-element.111, f32[64,64]{1,0:T(8,128)S(1)} %get-tuple-element.99, ...), kind=kOutput, calls=%fused_computation.56 | convolution fusion | flops 203292672 | bytes 2229248 | tf_op jit(solution)/shard_map/nij,njv->niv/dot_general | solution.py:103
  50.7 1.0 %fusion.171 = f32[32,1,128]{2,1,0:T(1,128)S(1)} fusion(f32[32,64,1]{1,2,0:T(1,128)S(1)} %bitcast.167, f32[32,64,128]{2,1,0:T(8,128)S(1)} %fusion.31), kind=kOutput, calls=%fused_computation.367 | convolution fusion | flops 3145728 | bytes 1073152 | tf_op jit(solution)/shard_map/pi,piv->pv/dot_general | solution.py:279
  52.5 2.1 %collective-permute-done.4 = f32[768]{0:T(1024)S(1)} collective-permute-done((f32[768]{0:T(1024)S(1)}, f32[768]{0:T(1024)S(1)}, u32[]{:S(2)}, u32[]{:S(2)}) %collective-permute-start.4) | collective-permute-done | bytes 3104 | tf_op jit(solution)/shard_map/ppermute | solution.py:22
  54.7 3.3 %collective-permute-done.5 = f32[768]{0:T(1024)S(1)} collective-permute-done((f32[768]{0:T(1024)S(1)}, f32[768]{0:T(1024)S(1)}, u32[]{:S(2)}, u32[]{:S(2)}) %collective-permute-start.5) | collective-permute-done | bytes 3104 | tf_op jit(solution)/shard_map/ppermute | solution.py:22
  58.0 3.4 %collective-permute-start.6 = (f32[768]{0:T(1024)S(1)}, f32[768]{0:T(1024)S(1)}, u32[]{:S(2)}, u32[]{:S(2)}) collective-permute-start(f32[768]{0:T(1024)S(1)} %add.831), channel_id=1, source_target_pairs={{0,4},{4,0},{8,12},{12,8},{1,5},{5,1},{9,13},{13,9},{2,6},{6,2},{1... | collective-permute-start | bytes 9224 | tf_op jit(solution)/shard_map/ppermute | solution.py:22
  62.3 2.4 %collective-permute-done.7 = f32[768]{0:T(1024)S(1)} collective-permute-done((f32[768]{0:T(1024)S(1)}, f32[768]{0:T(1024)S(1)}, u32[]{:S(2)}, u32[]{:S(2)}) %collective-permute-start.7) | collective-permute-done | bytes 3104 | tf_op jit(solution)/shard_map/ppermute | solution.py:22
  64.9 1.1 %multiply_add_fusion.2 = f32[32,64,32]{2,1,0:T(8,128)S(1)} fusion(f32[32,64,128]{2,1,0:T(8,128)S(1)} %broadcast_multiply_fusion, f32[32]{0:T(128)S(1)} %get-tuple-element.64, f32[32]{0:T(128)S(1)} %get-tuple-element.65, f32[32]{0:T(128)S(1)} %get-tuple-element.66, f32[32]{0:T(128)S(1)} %get-tuple-element.67), kind=kLoop, calls=%fused_computation.32 | loop fusion | flops 458752 | bytes 1311232 | tf_op jit(solution)/shard_map/add | solution.py:121
  66.0 1.3 %multiply_add_fusion.3 = (f32[32,64,32]{2,1,0:T(8,128)S(1)}, f32[32,64,32]{2,1,0:T(8,128)S(1)}, f32[32,64,32]{2,1,0:T(8,128)S(1)}) fusion(f32[32,64,128]{2,1,0:T(8,128)S(1)} %broadcast_multiply_fusion, f32[32]{0:T(128)S(1)} %get-tuple-element.68, f32[32]{0:T(128)S(1)} %get-tuple-element.69, f32[32]{0:T(128)S(1)} %get-tuple-element.58, ...), kind=kLoop, calls=%fused_computation.33 | loop fusion | flops 851968 | bytes 1836032 | tf_op jit(solution)/shard_map/add | solution.py:121
  67.3 0.9 %pad_maximum_fusion.9 = f32[32,64,128]{2,1,0:T(8,128)S(1)} fusion(f32[32,64,32]{2,1,0:T(8,128)S(1)} %get-tuple-element.36, f32[32,64,32]{2,1,0:T(8,128)S(1)} %get-tuple-element.35, f32[32,64,32]{2,1,0:T(8,128)S(1)} %multiply_add_fusion.2, f32[32,64,32]{2,1,0:T(8,128)S(1)} %get-tuple-element.34), kind=kLoop, calls=%fused_computation.29 | loop fusion | flops 786432 | bytes 2097152 | tf_op jit(solution)/shard_map/concatenate | solution.py:123
  69.6 1.9 %collective-permute-start.8 = (f32[1,64,128]{2,1,0:T(8,128)S(1)}, f32[1,64,128]{2,1,0:T(8,128)S(1)}, u32[]{:S(2)}, u32[]{:S(2)}) collective-permute-start(f32[1,64,128]{2,1,0:T(8,128)S(1)} %get-tuple-element.30), channel_id=1, source_target_pairs={{0,4},{4,0},{8,12},{12,8},{1,5},{5,1},{9,13},{13,9},{2,6},{6,2},{1... | collective-permute-start | bytes 98312 | tf_op jit(solution)/shard_map/ppermute | solution.py:42
  71.6 1.9 %collective-permute-start.9 = (f32[1,64,128]{2,1,0:T(8,128)S(1)}, f32[1,64,128]{2,1,0:T(8,128)S(1)}, u32[]{:S(2)}, u32[]{:S(2)}) collective-permute-start(f32[1,64,128]{2,1,0:T(8,128)S(1)} %get-tuple-element.31), channel_id=1, source_target_pairs={{4,8},{8,4},{5,9},{9,5},{6,10},{10,6},{7,11},{11,7},{20,24},{24,20... | collective-permute-start | bytes 98312 | tf_op jit(solution)/shard_map/ppermute | solution.py:51
  73.7 3.1 %collective-permute-done.9 = f32[1,64,128]{2,1,0:T(8,128)S(1)} collective-permute-done((f32[1,64,128]{2,1,0:T(8,128)S(1)}, f32[1,64,128]{2,1,0:T(8,128)S(1)}, u32[]{:S(2)}, u32[]{:S(2)}) %collective-permute-start.9) | collective-permute-done | bytes 32800 | tf_op jit(solution)/shard_map/ppermute | solution.py:51
  76.8 1.4 %fusion.6 = f32[32,64,128]{2,1,0:T(8,128)} fusion(f32[32,64,128]{2,1,0:T(8,128)S(1)} %bitcast.155, f32[32,1,128]{2,1,0:T(1,128)S(1)} %bitcast.172, f32[32,1,128]{2,1,0:T(1,128)S(1)} %bitcast.171, f32[1,64,128]{2,1,0:T(8,128)S(1)} %get-tuple-element.47, f32[1,64,128]{2,1,0:T(8,128)S(1)} %get-tuple-element.46, f32[128]{0:T(128)S(1)} %slice_divide_fusion.1, ...), kind=kLoop, calls=%fused_computation.12 | loop fusion | flops 3145728 | bytes 2196096 | tf_op jit(solution)/shard_map/mul | solution.py:299
  (122 shorter events, 12.9 us)
Async XLA Ops:
  0.0 1.4 %copy-start.2 = (s32[2,16,32]{2,1,0:T(8,128)S(1)}, s32[2,16,32]{2,1,0:T(8,128)}, u32[]{:S(2)}) copy-start(s32[2,16,32]{2,1,0:T(8,128)} %param.7) | copy-start | bytes 12292
  3.8 4.5 %copy-start.1 = (f32[2,3,16,32]{3,2,1,0:T(8,128)S(1)}, f32[2,3,16,32]{3,2,1,0:T(8,128)}, u32[]{:S(2)}) copy-start(f32[2,3,16,32]{3,2,1,0:T(8,128)} %param.5) | copy-start | bytes 36868
  3.8 12.2 %all-to-all-start = ((f32[4,4,64,128]{3,2,1,0:T(8,128)}), f32[4,4,64,128]{3,2,1,0:T(8,128)S(1)}, u32[]{:S(2)}, u32[]{:S(2)}) async-start(f32[4,4,64,128]{3,2,1,0:T(8,128)} %bitcast.18), calls=%async_computation | async-start | bytes 1048576 | tf_op jit(solution)/shard_map/all_to_all | solution.py:233
  10.3 0.7 copy-start.3
  22.2 13.7 %copy-start = (f32[32,64,128]{2,1,0:T(8,128)S(1)}, f32[32,64,128]{2,1,0:T(8,128)}, u32[]{:S(2)}) copy-start(f32[32,64,128]{2,1,0:T(8,128)} %param.4) | copy-start | bytes 3145732
  22.4 9.1 %collective-permute-start.2 = (f32[32,1,128]{2,1,0:T(1,128)S(1)}, f32[32,1,128]{2,1,0:T(1,128)S(1)}, u32[]{:S(2)}, u32[]{:S(2)}) collective-permute-start(f32[32,1,128]{2,1,0:T(1,128)S(1)} %get-tuple-element.39), channel_id=1, source_target_pairs={{0,1},{1,0},{2,3},{3,2},{4,5},{5,4},{6,7},{7,6},{8,9},{9,8},{10,11... | collective-permute-start | bytes 49160 | tf_op jit(solution)/shard_map/ppermute | solution.py:42
  24.6 6.8 %collective-permute-start.3 = (f32[32,1,128]{2,1,0:T(1,128)S(1)}, f32[32,1,128]{2,1,0:T(1,128)S(1)}, u32[]{:S(2)}, u32[]{:S(2)}) collective-permute-start(f32[32,1,128]{2,1,0:T(1,128)S(1)} %get-tuple-element.40), channel_id=1, source_target_pairs={{1,2},{2,1},{3,0},{0,3},{5,6},{6,5},{7,4},{4,7},{9,10},{10,9},{11,... | collective-permute-start | bytes 49160 | tf_op jit(solution)/shard_map/ppermute | solution.py:51
  28.0 3.5 %collective-permute-start = (f32[1,65,128]{2,1,0:T(8,128)S(1)}, f32[1,65,128]{2,1,0:T(8,128)S(1)}, u32[]{:S(2)}, u32[]{:S(2)}) collective-permute-start(f32[1,65,128]{2,1,0:T(8,128)S(1)} %get-tuple-element.48), channel_id=1, source_target_pairs={{0,4},{4,0},{8,12},{12,8},{1,5},{5,1},{9,13},{13,9},{2,6},{6,2},{1... | collective-permute-start | bytes 99848 | tf_op jit(solution)/shard_map/ppermute | solution.py:42
  29.5 5.3 %collective-permute-start.1 = (f32[1,65,128]{2,1,0:T(8,128)S(1)}, f32[1,65,128]{2,1,0:T(8,128)S(1)}, u32[]{:S(2)}, u32[]{:S(2)}) collective-permute-start(f32[1,65,128]{2,1,0:T(8,128)S(1)} %get-tuple-element.49), channel_id=1, source_target_pairs={{4,8},{8,4},{5,9},{9,5},{6,10},{10,6},{7,11},{11,7},{20,24},{24,20... | collective-permute-start | bytes 99848 | tf_op jit(solution)/shard_map/ppermute | solution.py:51
  38.4 9.5 %all-to-all-start.1 = ((f32[4,4,64,128]{3,2,1,0:T(8,128)}), f32[4,4,64,128]{3,2,1,0:T(8,128)S(1)}, u32[]{:S(2)}, u32[]{:S(2)}) async-start(f32[4,4,64,128]{3,2,1,0:T(8,128)} %bitcast.41), calls=%async_computation.1 | async-start | bytes 1048576 | tf_op jit(solution)/shard_map/all_to_all | solution.py:233
  52.1 2.5 %collective-permute-start.4 = (f32[768]{0:T(1024)S(1)}, f32[768]{0:T(1024)S(1)}, u32[]{:S(2)}, u32[]{:S(2)}) collective-permute-start(f32[768]{0:T(1024)S(1)} %pad_maximum_fusion.10), channel_id=1, source_target_pairs={{0,1},{1,0},{2,3},{3,2},{4,5},{5,4},{6,7},{7,6},{8,9},{9,8},{10,11... | collective-permute-start | bytes 9224 | tf_op jit(solution)/shard_map/ppermute | solution.py:22
  54.6 3.4 %collective-permute-start.5 = (f32[768]{0:T(1024)S(1)}, f32[768]{0:T(1024)S(1)}, u32[]{:S(2)}, u32[]{:S(2)}) collective-permute-start(f32[768]{0:T(1024)S(1)} %fusion.155), channel_id=1, source_target_pairs={{0,2},{1,3},{2,0},{3,1},{4,6},{5,7},{6,4},{7,5},{8,10},{9,11},{10,... | collective-permute-start | bytes 9224 | tf_op jit(solution)/shard_map/ppermute | solution.py:22
  58.0 4.3 %collective-permute-start.6 = (f32[768]{0:T(1024)S(1)}, f32[768]{0:T(1024)S(1)}, u32[]{:S(2)}, u32[]{:S(2)}) collective-permute-start(f32[768]{0:T(1024)S(1)} %add.831), channel_id=1, source_target_pairs={{0,4},{4,0},{8,12},{12,8},{1,5},{5,1},{9,13},{13,9},{2,6},{6,2},{1... | collective-permute-start | bytes 9224 | tf_op jit(solution)/shard_map/ppermute | solution.py:22
  62.3 2.5 %collective-permute-start.7 = (f32[768]{0:T(1024)S(1)}, f32[768]{0:T(1024)S(1)}, u32[]{:S(2)}, u32[]{:S(2)}) collective-permute-start(f32[768]{0:T(1024)S(1)} %add.832), channel_id=1, source_target_pairs={{0,8},{4,12},{8,0},{12,4},{1,9},{5,13},{9,1},{13,5},{2,10},{6,14},... | collective-permute-start | bytes 9224 | tf_op jit(solution)/shard_map/ppermute | solution.py:22
  68.5 5.2 %collective-permute-start.10 = (f32[32,1,128]{2,1,0:T(1,128)S(1)}, f32[32,1,128]{2,1,0:T(1,128)S(1)}, u32[]{:S(2)}, u32[]{:S(2)}) collective-permute-start(f32[32,1,128]{2,1,0:T(1,128)S(1)} %get-tuple-element.32), channel_id=1, source_target_pairs={{0,1},{1,0},{2,3},{3,2},{4,5},{5,4},{6,7},{7,6},{8,9},{9,8},{10,11... | collective-permute-start | bytes 49160 | tf_op jit(solution)/shard_map/ppermute | solution.py:42
  68.9 4.8 %collective-permute-start.11 = (f32[32,1,128]{2,1,0:T(1,128)S(1)}, f32[32,1,128]{2,1,0:T(1,128)S(1)}, u32[]{:S(2)}, u32[]{:S(2)}) collective-permute-start(f32[32,1,128]{2,1,0:T(1,128)S(1)} %get-tuple-element.33), channel_id=1, source_target_pairs={{1,2},{2,1},{3,0},{0,3},{5,6},{6,5},{7,4},{4,7},{9,10},{10,9},{11,... | collective-permute-start | bytes 49160 | tf_op jit(solution)/shard_map/ppermute | solution.py:51
  69.6 4.1 %collective-permute-start.8 = (f32[1,64,128]{2,1,0:T(8,128)S(1)}, f32[1,64,128]{2,1,0:T(8,128)S(1)}, u32[]{:S(2)}, u32[]{:S(2)}) collective-permute-start(f32[1,64,128]{2,1,0:T(8,128)S(1)} %get-tuple-element.30), channel_id=1, source_target_pairs={{0,4},{4,0},{8,12},{12,8},{1,5},{5,1},{9,13},{13,9},{2,6},{6,2},{1... | collective-permute-start | bytes 98312 | tf_op jit(solution)/shard_map/ppermute | solution.py:42
  71.6 5.2 %collective-permute-start.9 = (f32[1,64,128]{2,1,0:T(8,128)S(1)}, f32[1,64,128]{2,1,0:T(8,128)S(1)}, u32[]{:S(2)}, u32[]{:S(2)}) collective-permute-start(f32[1,64,128]{2,1,0:T(8,128)S(1)} %get-tuple-element.31), channel_id=1, source_target_pairs={{4,8},{8,4},{5,9},{9,5},{6,10},{10,6},{7,11},{11,7},{20,24},{24,20... | collective-permute-start | bytes 98312 | tf_op jit(solution)/shard_map/ppermute | solution.py:51

commit v14 on v13

--- a/solution.py
+++ b/solution.py
@@ -224,7 +224,12 @@
     sending = owned_here[:, :, None] & (slot_of[:, :, None] == slot_range[None, None, :])
     send_local = jnp.sum(jnp.where(sending, source_local[:, :, None], 0), axis=1)
     own_patches = to_patches(state_field)
-    outgoing = own_patches[send_local.reshape(-1)].reshape(lat_count, CAP, 64, value_count)
+    send_flat = send_local.reshape(-1)
+    outgoing = jnp.dot(
+        (send_flat[:, None] == jnp.arange(per_device)[None, :]).astype(jnp.float32),
+        own_patches.reshape(per_device, -1),
+        precision=lax.Precision.HIGHEST,
+    ).reshape(lat_count, CAP, 64, value_count)
     my_dev = lax.dynamic_index_in_dim(source_dev, lat_index, 0, keepdims=False)
     my_slot = lax.dynamic_index_in_dim(slot_of, lat_index, 0, keepdims=False)
     my_local = lax.dynamic_index_in_dim(source_local, lat_index, 0, keepdims=False)

time: 78.6 us -> 79.2 us (level)
  matrix products: 7.72 us -> 10.5 us
  local copies, waits for them, and re-layouts: 9.21 us -> 7.51 us
    gather x2 -> x0, local copies, waits for them, and re-layouts: 2.75 us -> none  [departed(): own_patches[send_local.reshape(-1)].reshape(lat_count, CAP, 64, value_count)]
    dot_general x0 -> x2, matrix products: none -> 2.73 us  [departed(): jnp.dot((send_flat[:, None] == jnp.arange(per_device)[None, :]).astype(jn...]
    transpose x2 -> x0, local copies, waits for them, and re-layouts: 1.48 us -> none  [to_patches(): return state_field.reshape(band_rows, 8, band_cols, 8, -1).transpose(0, 2...]
    reshape x2, local copies, waits for them, and re-layouts: 0.17 us -> 1.47 us  [to_patches(): state_field.reshape(band_rows, 8, band_cols, 8, -1).transpose(0, 2, 1, 3, 4)]
    unnamed x10, local copies, waits for them, and re-layouts: 1.04 us -> 2.18 us
  transfers between devices with their start and end apart: 14 -> 14, of which waited for: 8 -> 8; matrix products, arithmetic and copies ran while one was open for 9% -> 8% of each run, Pallas kernels for 0% -> 0%
where the time goes in v14:
time: 79.2 us; the launch traced here: 78.8 us
  starting transfers between devices  24.7 us (31%)
  waiting for transfers between devices  22 us (28%)
  other arithmetic  13.6 us (17%)
  matrix products  10.5 us (13%)
  local copies, waits for them, and re-layouts  7.51 us (9%)
    ppermute x4, waiting for transfers between devices, all_sum(): lax.ppermute(value, axis, [(i, i ^ distance) for i in range(count)])  8.67 us
    all_to_all x2, starting transfers between devices, departed(): lax.all_to_all(outgoing, 'lat', 0, 0, tiled=True)  7.9 us
    all_to_all x2, waiting for transfers between devices, departed(): lax.all_to_all(outgoing, 'lat', 0, 0, tiled=True)  6.89 us
    ppermute x4, starting transfers between devices, neighbour_halos(): second = lax.ppermute(jnp.where(even, lo_edge, hi_edge), axis, pairs)  6.76 us
    ppermute x4, waiting for transfers between devices, neighbour_halos(): second = lax.ppermute(jnp.where(even, lo_edge, hi_edge), axis, pairs)  6.38 us
    ppermute x4, starting transfers between devices, neighbour_halos(): lax.ppermute(jnp.where(even, hi_edge, lo_edge), axis, [(i, i ^ 1) for i i...  6.05 us
    add x4, other arithmetic, levels(): acc = term if acc is None else acc + term  4.85 us
    ppermute x4, starting transfers between devices, all_sum(): lax.ppermute(value, axis, [(i, i ^ distance) for i in range(count)])  3.97 us
  transfers between devices with their start and end apart: 14, of which 8 were waited for; matrix products, arithmetic and copies ran while one was open for 8% of the time, Pallas kernels for 0%

profile of v14, /device:TPU:1, one launch (start us, length us, event | category | flops | bytes accessed | tf_op | source)
XLA Modules:
  0.0 78.8 jit_solution(13817202855893274921)
XLA Ops:
  0.0 1.3 %copy.63 = f32[4,8,8,8,128]{4,3,1,2,0:T(8,128)S(1)} copy(f32[4,8,8,8,128]{4,3,2,1,0:T(8,128)} %bitcast.189) | data formatting | bytes 2097152 | tf_op jit(solution)/shard_map/reshape | solution.py:130
  3.0 1.4 %fusion.4 = f32[4,4,64,128]{3,1,2,0:T(4,128)} fusion(s32[4,4]{1,0:T(4,128)S(1)} %select_reduce_fusion.2, f32[32,8192]{1,0:T(8,128)S(1)} %reshape_reshape.14), kind=kOutput, calls=%fused_computation.9 | convolution fusion | flops 50332160 | bytes 1572928 | tf_op jit(solution)/shard_map/dot_general | solution.py:228
  4.4 4.3 %all-to-all-start = ((f32[4,4,64,128]{3,1,2,0:T(4,128)}), f32[4,4,64,128]{3,1,2,0:T(4,128)S(1)}, u32[]{:S(2)}, u32[]{:S(2)}) async-start(f32[4,4,64,128]{3,1,2,0:T(4,128)} %fusion.4), calls=%async_computation | async-start | bytes 1048576 | tf_op jit(solution)/shard_map/all_to_all | solution.py:238
  12.9 3.5 %all-to-all-done = f32[4,4,64,128]{3,1,2,0:T(4,128)S(1)} async-done(((f32[4,4,64,128]{3,1,2,0:T(4,128)}), f32[4,4,64,128]{3,1,2,0:T(4,128)S(1)}, u32[]{:S(2)}, u32[]{:S(2)}) %all-to-all-start) | async-done | bytes 524320 | tf_op jit(solution)/shard_map/all_to_all | solution.py:238
  17.5 1.8 %fusion.19 = f32[32,64,128]{2,1,0:T(8,128)S(1)} fusion(f32[32,64,128]{2,1,0:T(8,128)S(1)} %bitcast.194, f32[32]{0:T(128)S(1)} %get-tuple-element.121, f32[32]{0:T(128)S(1)} %get-tuple-element.122, f32[32]{0:T(128)S(1)} %get-tuple-element.120, f32[32]{0:T(128)S(1)} %get-tuple-element.90, f32[32]{0:T(128)S(1)} %get-tuple-element.118, ...), kind=kOutput, calls=%fused_computation.46 | convolution fusion | flops 203292672 | bytes 2229248 | tf_op jit(solution)/shard_map/nij,njv->niv/dot_general | solution.py:103
  19.4 1.1 %multiply_add_fusion.6 = f32[32,64,32]{2,1,0:T(8,128)S(1)} fusion(f32[32,64,128]{2,1,0:T(8,128)S(1)} %fusion.19, f32[32]{0:T(128)S(1)} %get-tuple-element.78, f32[32]{0:T(128)S(1)} %get-tuple-element.79, f32[32]{0:T(128)S(1)} %get-tuple-element.80, f32[32]{0:T(128)S(1)} %get-tuple-element.81), kind=kLoop, calls=%fused_computation.44 | loop fusion | flops 458752 | bytes 1311232 | tf_op jit(solution)/shard_map/add | solution.py:121
  20.5 1.3 %multiply_add_fusion.7 = (f32[32,64,32]{2,1,0:T(8,128)S(1)}, f32[32,64,32]{2,1,0:T(8,128)S(1)}, f32[32,64,32]{2,1,0:T(8,128)S(1)}) fusion(f32[32,64,128]{2,1,0:T(8,128)S(1)} %fusion.19, f32[32]{0:T(128)S(1)} %get-tuple-element.82, f32[32]{0:T(128)S(1)} %get-tuple-element.83, f32[32]{0:T(128)S(1)} %get-tuple-element.72, f32[32]{0:T(128)S(1)} %get-tuple-element.75, ...), kind=kLoop, calls=%fused_computation.45 | loop fusion | flops 851968 | bytes 1836032 | tf_op jit(solution)/shard_map/add | solution.py:121
  21.8 0.9 %pad_maximum_fusion.8 = f32[32,64,128]{2,1,0:T(8,128)S(1)} fusion(f32[32,64,32]{2,1,0:T(8,128)S(1)} %get-tuple-element.43, f32[32,64,32]{2,1,0:T(8,128)S(1)} %get-tuple-element.42, f32[32,64,32]{2,1,0:T(8,128)S(1)} %multiply_add_fusion.6, f32[32,64,32]{2,1,0:T(8,128)S(1)} %get-tuple-element.41), kind=kLoop, calls=%fused_computation.32 | loop fusion | flops 786432 | bytes 2097152 | tf_op jit(solution)/shard_map/concatenate | solution.py:123
  22.9 2.2 %collective-permute-start.2 = (f32[32,1,128]{2,1,0:T(1,128)S(1)}, f32[32,1,128]{2,1,0:T(1,128)S(1)}, u32[]{:S(2)}, u32[]{:S(2)}) collective-permute-start(f32[32,1,128]{2,1,0:T(1,128)S(1)} %get-tuple-element.39), channel_id=1, source_target_pairs={{0,1},{1,0},{2,3},{3,2},{4,5},{5,4},{6,7},{7,6},{8,9},{9,8},{10,11... | collective-permute-start | bytes 49160 | tf_op jit(solution)/shard_map/ppermute | solution.py:42
  25.1 2.2 %collective-permute-start.3 = (f32[32,1,128]{2,1,0:T(1,128)S(1)}, f32[32,1,128]{2,1,0:T(1,128)S(1)}, u32[]{:S(2)}, u32[]{:S(2)}) collective-permute-start(f32[32,1,128]{2,1,0:T(1,128)S(1)} %get-tuple-element.40), channel_id=1, source_target_pairs={{1,2},{2,1},{3,0},{0,3},{5,6},{6,5},{7,4},{4,7},{9,10},{10,9},{11,... | collective-permute-start | bytes 49160 | tf_op jit(solution)/shard_map/ppermute | solution.py:51
  27.3 1.2 %pad_select_fusion.1 = (f32[1,65,128]{2,1,0:T(8,128)S(1)}, f32[1,65,128]{2,1,0:T(8,128)S(1)}) fusion(f32[1,64,128]{2,1,0:T(8,128)S(1)} %get-tuple-element.38, f32[]{:T(128)} %bitcast.35, f32[1,64,128]{2,1,0:T(8,128)S(1)} %get-tuple-element.37, f32[]{:T(128)} %bitcast.34, pred[]{:T(512)S(6)} %eq.486), kind=kLoop, calls=%fused_computation.147 | loop fusion | flops 16640 | bytes 132105 | tf_op jit(solution)/shard_map/jit(_where)/select_n | solution.py:43
  28.5 1.5 %collective-permute-start = (f32[1,65,128]{2,1,0:T(8,128)S(1)}, f32[1,65,128]{2,1,0:T(8,128)S(1)}, u32[]{:S(2)}, u32[]{:S(2)}) collective-permute-start(f32[1,65,128]{2,1,0:T(8,128)S(1)} %get-tuple-element.48), channel_id=1, source_target_pairs={{0,4},{4,0},{8,12},{12,8},{1,5},{5,1},{9,13},{13,9},{2,6},{6,2},{1... | collective-permute-start | bytes 99848 | tf_op jit(solution)/shard_map/ppermute | solution.py:42
  30.0 1.9 %collective-permute-start.1 = (f32[1,65,128]{2,1,0:T(8,128)S(1)}, f32[1,65,128]{2,1,0:T(8,128)S(1)}, u32[]{:S(2)}, u32[]{:S(2)}) collective-permute-start(f32[1,65,128]{2,1,0:T(8,128)S(1)} %get-tuple-element.49), channel_id=1, source_target_pairs={{4,8},{8,4},{5,9},{9,5},{6,10},{10,6},{7,11},{11,7},{20,24},{24,20... | collective-permute-start | bytes 99848 | tf_op jit(solution)/shard_map/ppermute | solution.py:51
  32.0 3.3 %collective-permute-done.1 = f32[1,65,128]{2,1,0:T(8,128)S(1)} collective-permute-done((f32[1,65,128]{2,1,0:T(8,128)S(1)}, f32[1,65,128]{2,1,0:T(8,128)S(1)}, u32[]{:S(2)}, u32[]{:S(2)}) %collective-permute-start.1) | collective-permute-done | bytes 33312 | tf_op jit(solution)/shard_map/ppermute | solution.py:51
  37.5 1.4 %fusion.2 = f32[4,4,64,128]{3,1,2,0:T(4,128)} fusion(s32[4,4]{1,0:T(4,128)S(1)} %select_reduce_fusion, f32[32,8192]{1,0:T(8,128)S(1)} %reshape_reshape.16), kind=kOutput, calls=%fused_computation.6 | convolution fusion | flops 50332160 | bytes 1572928 | tf_op jit(solution)/shard_map/dot_general | solution.py:228
  38.9 3.6 %all-to-all-start.1 = ((f32[4,4,64,128]{3,1,2,0:T(4,128)}), f32[4,4,64,128]{3,1,2,0:T(4,128)S(1)}, u32[]{:S(2)}, u32[]{:S(2)}) async-start(f32[4,4,64,128]{3,1,2,0:T(4,128)} %fusion.2), calls=%async_computation.1 | async-start | bytes 1048576 | tf_op jit(solution)/shard_map/all_to_all | solution.py:238
  42.5 1.3 %maximum_multiply_fusion = f32[34]{0:T(128)S(1)} fusion(f32[1]{0:T(128)} %bitcast.45, f32[32]{0:T(128)S(1)} %copy-done.3, f32[1]{0:T(128)} %bitcast.44, s32[]{:T(128)S(6)} %sub.190), kind=kLoop, calls=%fused_computation.317 | loop fusion | flops 272 | bytes 276 | tf_op jit(solution)/shard_map/mul | solution.py:281
  45.0 3.4 %all-to-all-done.1 = f32[4,4,64,128]{3,1,2,0:T(4,128)S(1)} async-done(((f32[4,4,64,128]{3,1,2,0:T(4,128)}), f32[4,4,64,128]{3,1,2,0:T(4,128)S(1)}, u32[]{:S(2)}, u32[]{:S(2)}) %all-to-all-start.1) | async-done | bytes 524320 | tf_op jit(solution)/shard_map/all_to_all | solution.py:238
  48.4 0.8 %fusion.1 = f32[4,8,64,128]{3,1,2,0:T(8,128)S(1)} fusion(f32[32,8192]{1,0:T(8,128)S(1)} %fusion.109, f32[2,8,64,128]{3,2,1,0:T(8,128)S(1)} %bitcast.192, s32[32]{0:T(128)S(1)} %fusion.161, pred[32]{0:T(512)(128)(4,1)S(1)} %get-tuple-element.18), kind=kOutput, calls=%fused_computation.3 | convolution fusion | flops 50594816 | bytes 2621600 | tf_op jit(solution)/shard_map/dot_general | solution.py:250
  49.4 1.8 %fusion.35 = f32[32,64,128]{2,1,0:T(8,128)S(1)} fusion(f32[32,64,128]{2,1,0:T(8,128)S(1)} %bitcast.193, f32[64,64]{1,0:T(8,128)S(1)} %get-tuple-element.97, f32[32]{0:T(128)S(1)} %get-tuple-element.110, f32[64,64]{1,0:T(8,128)S(1)} %get-tuple-element.98, f32[32]{0:T(128)S(1)} %get-tuple-element.111, f32[64,64]{1,0:T(8,128)S(1)} %get-tuple-element.99, ...), kind=kOutput, calls=%fused_computation.62 | convolution fusion | flops 203292672 | bytes 2229248 | tf_op jit(solution)/shard_map/nij,njv->niv/dot_general | solution.py:103
  51.3 1.0 %fusion.179 = f32[32,1,128]{2,1,0:T(1,128)S(1)} fusion(f32[32,64,1]{1,2,0:T(1,128)S(1)} %bitcast.195, f32[32,64,128]{2,1,0:T(8,128)S(1)} %fusion.35), kind=kOutput, calls=%fused_computation.373 | convolution fusion | flops 3145728 | bytes 1073152 | tf_op jit(solution)/shard_map/pi,piv->pv/dot_general | solution.py:284
  53.1 2.1 %collective-permute-done.4 = f32[768]{0:T(1024)S(1)} collective-permute-done((f32[768]{0:T(1024)S(1)}, f32[768]{0:T(1024)S(1)}, u32[]{:S(2)}, u32[]{:S(2)}) %collective-permute-start.4) | collective-permute-done | bytes 3104 | tf_op jit(solution)/shard_map/ppermute | solution.py:22
  55.2 3.3 %collective-permute-done.5 = f32[768]{0:T(1024)S(1)} collective-permute-done((f32[768]{0:T(1024)S(1)}, f32[768]{0:T(1024)S(1)}, u32[]{:S(2)}, u32[]{:S(2)}) %collective-permute-start.5) | collective-permute-done | bytes 3104 | tf_op jit(solution)/shard_map/ppermute | solution.py:22
  58.6 3.4 %collective-permute-start.6 = (f32[768]{0:T(1024)S(1)}, f32[768]{0:T(1024)S(1)}, u32[]{:S(2)}, u32[]{:S(2)}) collective-permute-start(f32[768]{0:T(1024)S(1)} %add.809), channel_id=1, source_target_pairs={{0,4},{4,0},{8,12},{12,8},{1,5},{5,1},{9,13},{13,9},{2,6},{6,2},{1... | collective-permute-start | bytes 9224 | tf_op jit(solution)/shard_map/ppermute | solution.py:22
  62.9 2.4 %collective-permute-done.7 = f32[768]{0:T(1024)S(1)} collective-permute-done((f32[768]{0:T(1024)S(1)}, f32[768]{0:T(1024)S(1)}, u32[]{:S(2)}, u32[]{:S(2)}) %collective-permute-start.7) | collective-permute-done | bytes 3104 | tf_op jit(solution)/shard_map/ppermute | solution.py:22
  65.4 1.1 %multiply_add_fusion.2 = f32[32,64,32]{2,1,0:T(8,128)S(1)} fusion(f32[32,64,128]{2,1,0:T(8,128)S(1)} %broadcast_multiply_fusion, f32[32]{0:T(128)S(1)} %get-tuple-element.64, f32[32]{0:T(128)S(1)} %get-tuple-element.65, f32[32]{0:T(128)S(1)} %get-tuple-element.66, f32[32]{0:T(128)S(1)} %get-tuple-element.67), kind=kLoop, calls=%fused_computation.38 | loop fusion | flops 458752 | bytes 1311232 | tf_op jit(solution)/shard_map/add | solution.py:121
  66.6 1.3 %multiply_add_fusion.3 = (f32[32,64,32]{2,1,0:T(8,128)S(1)}, f32[32,64,32]{2,1,0:T(8,128)S(1)}, f32[32,64,32]{2,1,0:T(8,128)S(1)}) fusion(f32[32,64,128]{2,1,0:T(8,128)S(1)} %broadcast_multiply_fusion, f32[32]{0:T(128)S(1)} %get-tuple-element.68, f32[32]{0:T(128)S(1)} %get-tuple-element.69, f32[32]{0:T(128)S(1)} %get-tuple-element.58, ...), kind=kLoop, calls=%fused_computation.39 | loop fusion | flops 851968 | bytes 1836032 | tf_op jit(solution)/shard_map/add | solution.py:121
  67.9 0.9 %pad_maximum_fusion.9 = f32[32,64,128]{2,1,0:T(8,128)S(1)} fusion(f32[32,64,32]{2,1,0:T(8,128)S(1)} %get-tuple-element.36, f32[32,64,32]{2,1,0:T(8,128)S(1)} %get-tuple-element.35, f32[32,64,32]{2,1,0:T(8,128)S(1)} %multiply_add_fusion.2, f32[32,64,32]{2,1,0:T(8,128)S(1)} %get-tuple-element.34), kind=kLoop, calls=%fused_computation.33 | loop fusion | flops 786432 | bytes 2097152 | tf_op jit(solution)/shard_map/concatenate | solution.py:123
  70.2 1.9 %collective-permute-start.8 = (f32[1,64,128]{2,1,0:T(8,128)S(1)}, f32[1,64,128]{2,1,0:T(8,128)S(1)}, u32[]{:S(2)}, u32[]{:S(2)}) collective-permute-start(f32[1,64,128]{2,1,0:T(8,128)S(1)} %get-tuple-element.30), channel_id=1, source_target_pairs={{0,4},{4,0},{8,12},{12,8},{1,5},{5,1},{9,13},{13,9},{2,6},{6,2},{1... | collective-permute-start | bytes 98312 | tf_op jit(solution)/shard_map/ppermute | solution.py:42
  72.1 1.9 %collective-permute-start.9 = (f32[1,64,128]{2,1,0:T(8,128)S(1)}, f32[1,64,128]{2,1,0:T(8,128)S(1)}, u32[]{:S(2)}, u32[]{:S(2)}) collective-permute-start(f32[1,64,128]{2,1,0:T(8,128)S(1)} %get-tuple-element.31), channel_id=1, source_target_pairs={{4,8},{8,4},{5,9},{9,5},{6,10},{10,6},{7,11},{11,7},{20,24},{24,20... | collective-permute-start | bytes 98312 | tf_op jit(solution)/shard_map/ppermute | solution.py:51
  74.3 3.1 %collective-permute-done.9 = f32[1,64,128]{2,1,0:T(8,128)S(1)} collective-permute-done((f32[1,64,128]{2,1,0:T(8,128)S(1)}, f32[1,64,128]{2,1,0:T(8,128)S(1)}, u32[]{:S(2)}, u32[]{:S(2)}) %collective-permute-start.9) | collective-permute-done | bytes 32800 | tf_op jit(solution)/shard_map/ppermute | solution.py:51
  77.3 1.4 %fusion.10 = f32[32,64,128]{2,1,0:T(8,128)} fusion(f32[32,64,128]{2,1,0:T(8,128)S(1)} %bitcast.181, f32[32,1,128]{2,1,0:T(1,128)S(1)} %bitcast.200, f32[32,1,128]{2,1,0:T(1,128)S(1)} %bitcast.199, f32[1,64,128]{2,1,0:T(8,128)S(1)} %get-tuple-element.47, f32[1,64,128]{2,1,0:T(8,128)S(1)} %get-tuple-element.46, f32[128]{0:T(128)S(1)} %slice_divide_fusion.1, ...), kind=kLoop, calls=%fused_computation.16 | loop fusion | flops 3145728 | bytes 2196096 | tf_op jit(solution)/shard_map/mul | solution.py:304
  (118 shorter events, 14.0 us)
Async XLA Ops:
  1.4 0.7 copy-start.2
  4.4 12.1 %all-to-all-start = ((f32[4,4,64,128]{3,1,2,0:T(4,128)}), f32[4,4,64,128]{3,1,2,0:T(4,128)S(1)}, u32[]{:S(2)}, u32[]{:S(2)}) async-start(f32[4,4,64,128]{3,1,2,0:T(4,128)} %fusion.4), calls=%async_computation | async-start | bytes 1048576 | tf_op jit(solution)/shard_map/all_to_all | solution.py:238
  8.6 0.8 %copy-start.1 = (f32[2,3,16,32]{3,2,1,0:T(8,128)S(1)}, f32[2,3,16,32]{3,2,1,0:T(8,128)}, u32[]{:S(2)}) copy-start(f32[2,3,16,32]{3,2,1,0:T(8,128)} %param.5) | copy-start | bytes 36868
  10.2 0.7 copy-start.3
  22.7 13.7 %copy-start = (f32[32,64,128]{2,1,0:T(8,128)S(1)}, f32[32,64,128]{2,1,0:T(8,128)}, u32[]{:S(2)}) copy-start(f32[32,64,128]{2,1,0:T(8,128)} %param.4) | copy-start | bytes 3145732
  22.9 9.1 %collective-permute-start.2 = (f32[32,1,128]{2,1,0:T(1,128)S(1)}, f32[32,1,128]{2,1,0:T(1,128)S(1)}, u32[]{:S(2)}, u32[]{:S(2)}) collective-permute-start(f32[32,1,128]{2,1,0:T(1,128)S(1)} %get-tuple-element.39), channel_id=1, source_target_pairs={{0,1},{1,0},{2,3},{3,2},{4,5},{5,4},{6,7},{7,6},{8,9},{9,8},{10,11... | collective-permute-start | bytes 49160 | tf_op jit(solution)/shard_map/ppermute | solution.py:42
  25.1 6.8 %collective-permute-start.3 = (f32[32,1,128]{2,1,0:T(1,128)S(1)}, f32[32,1,128]{2,1,0:T(1,128)S(1)}, u32[]{:S(2)}, u32[]{:S(2)}) collective-permute-start(f32[32,1,128]{2,1,0:T(1,128)S(1)} %get-tuple-element.40), channel_id=1, source_target_pairs={{1,2},{2,1},{3,0},{0,3},{5,6},{6,5},{7,4},{4,7},{9,10},{10,9},{11,... | collective-permute-start | bytes 49160 | tf_op jit(solution)/shard_map/ppermute | solution.py:51
  28.5 3.5 %collective-permute-start = (f32[1,65,128]{2,1,0:T(8,128)S(1)}, f32[1,65,128]{2,1,0:T(8,128)S(1)}, u32[]{:S(2)}, u32[]{:S(2)}) collective-permute-start(f32[1,65,128]{2,1,0:T(8,128)S(1)} %get-tuple-element.48), channel_id=1, source_target_pairs={{0,4},{4,0},{8,12},{12,8},{1,5},{5,1},{9,13},{13,9},{2,6},{6,2},{1... | collective-permute-start | bytes 99848 | tf_op jit(solution)/shard_map/ppermute | solution.py:42
  30.0 5.3 %collective-permute-start.1 = (f32[1,65,128]{2,1,0:T(8,128)S(1)}, f32[1,65,128]{2,1,0:T(8,128)S(1)}, u32[]{:S(2)}, u32[]{:S(2)}) collective-permute-start(f32[1,65,128]{2,1,0:T(8,128)S(1)} %get-tuple-element.49), channel_id=1, source_target_pairs={{4,8},{8,4},{5,9},{9,5},{6,10},{10,6},{7,11},{11,7},{20,24},{24,20... | collective-permute-start | bytes 99848 | tf_op jit(solution)/shard_map/ppermute | solution.py:51
  38.9 9.5 %all-to-all-start.1 = ((f32[4,4,64,128]{3,1,2,0:T(4,128)}), f32[4,4,64,128]{3,1,2,0:T(4,128)S(1)}, u32[]{:S(2)}, u32[]{:S(2)}) async-start(f32[4,4,64,128]{3,1,2,0:T(4,128)} %fusion.2), calls=%async_computation.1 | async-start | bytes 1048576 | tf_op jit(solution)/shard_map/all_to_all | solution.py:238
  52.6 2.5 %collective-permute-start.4 = (f32[768]{0:T(1024)S(1)}, f32[768]{0:T(1024)S(1)}, u32[]{:S(2)}, u32[]{:S(2)}) collective-permute-start(f32[768]{0:T(1024)S(1)} %pad_maximum_fusion.10), channel_id=1, source_target_pairs={{0,1},{1,0},{2,3},{3,2},{4,5},{5,4},{6,7},{7,6},{8,9},{9,8},{10,11... | collective-permute-start | bytes 9224 | tf_op jit(solution)/shard_map/ppermute | solution.py:22
  55.2 3.4 %collective-permute-start.5 = (f32[768]{0:T(1024)S(1)}, f32[768]{0:T(1024)S(1)}, u32[]{:S(2)}, u32[]{:S(2)}) collective-permute-start(f32[768]{0:T(1024)S(1)} %fusion.163), channel_id=1, source_target_pairs={{0,2},{1,3},{2,0},{3,1},{4,6},{5,7},{6,4},{7,5},{8,10},{9,11},{10,... | collective-permute-start | bytes 9224 | tf_op jit(solution)/shard_map/ppermute | solution.py:22
  58.6 4.3 %collective-permute-start.6 = (f32[768]{0:T(1024)S(1)}, f32[768]{0:T(1024)S(1)}, u32[]{:S(2)}, u32[]{:S(2)}) collective-permute-start(f32[768]{0:T(1024)S(1)} %add.809), channel_id=1, source_target_pairs={{0,4},{4,0},{8,12},{12,8},{1,5},{5,1},{9,13},{13,9},{2,6},{6,2},{1... | collective-permute-start | bytes 9224 | tf_op jit(solution)/shard_map/ppermute | solution.py:22
  62.9 2.5 %collective-permute-start.7 = (f32[768]{0:T(1024)S(1)}, f32[768]{0:T(1024)S(1)}, u32[]{:S(2)}, u32[]{:S(2)}) collective-permute-start(f32[768]{0:T(1024)S(1)} %add.810), channel_id=1, source_target_pairs={{0,8},{4,12},{8,0},{12,4},{1,9},{5,13},{9,1},{13,5},{2,10},{6,14},... | collective-permute-start | bytes 9224 | tf_op jit(solution)/shard_map/ppermute | solution.py:22
  69.0 5.2 %collective-permute-start.10 = (f32[32,1,128]{2,1,0:T(1,128)S(1)}, f32[32,1,128]{2,1,0:T(1,128)S(1)}, u32[]{:S(2)}, u32[]{:S(2)}) collective-permute-start(f32[32,1,128]{2,1,0:T(1,128)S(1)} %get-tuple-element.32), channel_id=1, source_target_pairs={{0,1},{1,0},{2,3},{3,2},{4,5},{5,4},{6,7},{7,6},{8,9},{9,8},{10,11... | collective-permute-start | bytes 49160 | tf_op jit(solution)/shard_map/ppermute | solution.py:42
  69.4 4.8 %collective-permute-start.11 = (f32[32,1,128]{2,1,0:T(1,128)S(1)}, f32[32,1,128]{2,1,0:T(1,128)S(1)}, u32[]{:S(2)}, u32[]{:S(2)}) collective-permute-start(f32[32,1,128]{2,1,0:T(1,128)S(1)} %get-tuple-element.33), channel_id=1, source_target_pairs={{1,2},{2,1},{3,0},{0,3},{5,6},{6,5},{7,4},{4,7},{9,10},{10,9},{11,... | collective-permute-start | bytes 49160 | tf_op jit(solution)/shard_map/ppermute | solution.py:51
  70.2 4.1 %collective-permute-start.8 = (f32[1,64,128]{2,1,0:T(8,128)S(1)}, f32[1,64,128]{2,1,0:T(8,128)S(1)}, u32[]{:S(2)}, u32[]{:S(2)}) collective-permute-start(f32[1,64,128]{2,1,0:T(8,128)S(1)} %get-tuple-element.30), channel_id=1, source_target_pairs={{0,4},{4,0},{8,12},{12,8},{1,5},{5,1},{9,13},{13,9},{2,6},{6,2},{1... | collective-permute-start | bytes 98312 | tf_op jit(solution)/shard_map/ppermute | solution.py:42
  72.1 5.2 %collective-permute-start.9 = (f32[1,64,128]{2,1,0:T(8,128)S(1)}, f32[1,64,128]{2,1,0:T(8,128)S(1)}, u32[]{:S(2)}, u32[]{:S(2)}) collective-permute-start(f32[1,64,128]{2,1,0:T(8,128)S(1)} %get-tuple-element.31), channel_id=1, source_target_pairs={{4,8},{8,4},{5,9},{9,5},{6,10},{10,6},{7,11},{11,7},{20,24},{24,20... | collective-permute-start | bytes 98312 | tf_op jit(solution)/shard_map/ppermute | solution.py:51

commit v15 on v13

--- a/solution.py
+++ b/solution.py
@@ -282,8 +282,13 @@
     mix_part = jnp.einsum(
         "plm,pmt->lmt", weight_z, weighted, precision=lax.Precision.HIGHEST
     )
-    totals = all_sum(
-        jnp.concatenate([target_part, first_part, mix_part.reshape(-1)]), ("lon", "lat")
+    partial = jnp.concatenate([target_part, first_part, mix_part.reshape(-1)])
+    members = lat_count * lax.axis_size("lon")
+    totals = jnp.sum(
+        lax.all_to_all(
+            jnp.broadcast_to(partial, (members,) + partial.shape), ("lat", "lon"), 0, 0, tiled=True
+        ),
+        axis=0,
     )
     target = totals[:value_count]
     first_mass = totals[value_count : 2 * value_count]

time: 78.6 us -> 77.1 us (0.981)
  waiting for transfers between devices: 22.3 us -> 19.4 us
  local copies, waits for them, and re-layouts: 9.21 us -> 10 us
    ppermute x4 -> x0, waiting for transfers between devices: 8.67 us -> none  [all_sum(): lax.ppermute(value, axis, [(i, i ^ distance) for i in range(count)])]
    all_to_all x0 -> x1, waiting for transfers between devices: none -> 6.31 us  [local(): lax.all_to_all(jnp.broadcast_to(partial, (members,) + partial.shape), ('l...]
    all_to_all x0 -> x1, starting transfers between devices: none -> 4.46 us  [local(): lax.all_to_all(jnp.broadcast_to(partial, (members,) + partial.shape), ('l...]
    ppermute x4 -> x0, starting transfers between devices: 3.97 us -> none  [all_sum(): lax.ppermute(value, axis, [(i, i ^ distance) for i in range(count)])]
    ppermute x4, starting transfers between devices: 6.05 us -> 4.81 us  [neighbour_halos(): lax.ppermute(jnp.where(even, hi_edge, lo_edge), axis, [(i, i ^ 1) for i i...]
    ppermute x4, starting transfers between devices: 6.76 us -> 7.68 us  [neighbour_halos(): second = lax.ppermute(jnp.where(even, lo_edge, hi_edge), axis, pairs)]
  transfers between devices with their start and end apart: 14 -> 11, of which waited for: 8 -> 5; matrix products, arithmetic and copies ran while one was open for 9% -> 10% of each run, Pallas kernels for 0% -> 0%
where the time goes in v15:
time: 77.1 us; the launch traced here: 76.6 us
  starting transfers between devices  25 us (32%)
  waiting for transfers between devices  19.4 us (25%)
  other arithmetic  13.9 us (18%)
  local copies, waits for them, and re-layouts  10 us (13%)
  matrix products  7.72 us (10%)
    all_to_all x2, starting transfers between devices, departed(): lax.all_to_all(outgoing, 'lat', 0, 0, tiled=True)  8.04 us
    ppermute x4, starting transfers between devices, neighbour_halos(): second = lax.ppermute(jnp.where(even, lo_edge, hi_edge), axis, pairs)  7.68 us
    all_to_all x2, waiting for transfers between devices, departed(): lax.all_to_all(outgoing, 'lat', 0, 0, tiled=True)  6.97 us
    all_to_all x1, waiting for transfers between devices, local(): lax.all_to_all(jnp.broadcast_to(partial, (members,) + partial.shape), ('l...  6.31 us
    ppermute x4, waiting for transfers between devices, neighbour_halos(): second = lax.ppermute(jnp.where(even, lo_edge, hi_edge), axis, pairs)  6.09 us
    add x4, other arithmetic, levels(): acc = term if acc is None else acc + term  4.85 us
    ppermute x4, starting transfers between devices, neighbour_halos(): lax.ppermute(jnp.where(even, hi_edge, lo_edge), axis, [(i, i ^ 1) for i i...  4.81 us
    all_to_all x1, starting transfers between devices, local(): lax.all_to_all(jnp.broadcast_to(partial, (members,) + partial.shape), ('l...  4.46 us
  transfers between devices with their start and end apart: 11, of which 5 were waited for; matrix products, arithmetic and copies ran while one was open for 10% of the time, Pallas kernels for 0%

profile of v15, /device:TPU:1, one launch (start us, length us, event | category | flops | bytes accessed | tf_op | source)
XLA Modules:
  0.0 76.6 jit_solution(8866131495800008873)
XLA Ops:
  0.0 1.4 %copy.31 = f32[4,8,8,8,128]{4,3,2,1,0:T(8,128)S(1)} copy(f32[4,8,8,8,128]{4,3,1,2,0:T(8,128)} %bitcast.161) | data formatting | bytes 2097152 | tf_op jit(solution)/shard_map/transpose | solution.py:131
  2.4 1.4 %gather_fusion = f32[16,64,128]{2,1,0:T(8,128)} fusion(f32[32,64,128]{2,1,0:T(8,128)S(1)} %bitcast.151, s32[1024]{0:T(1024)S(1)} %pad_clamp_fusion.1), kind=kCustom, calls=%fused_computation | custom fusion | bytes 1048640 | tf_op jit(solution)/shard_map/gather | solution.py:227
  3.8 4.4 %all-to-all-start = ((f32[4,4,64,128]{3,2,1,0:T(8,128)}), f32[4,4,64,128]{3,2,1,0:T(8,128)S(1)}, u32[]{:S(2)}, u32[]{:S(2)}) async-start(f32[4,4,64,128]{3,2,1,0:T(8,128)} %bitcast.18), calls=%async_computation | async-start | bytes 1048576 | tf_op jit(solution)/shard_map/all_to_all | solution.py:233
  12.2 3.8 %all-to-all-done = f32[4,4,64,128]{3,2,1,0:T(8,128)S(1)} async-done(((f32[4,4,64,128]{3,2,1,0:T(8,128)}), f32[4,4,64,128]{3,2,1,0:T(8,128)S(1)}, u32[]{:S(2)}, u32[]{:S(2)}) %all-to-all-start) | async-done | bytes 524320 | tf_op jit(solution)/shard_map/all_to_all | solution.py:233
  16.0 0.8 %fusion = f32[4,8,64,128]{3,1,2,0:T(8,128)S(1)} fusion(f32[32,8192]{1,0:T(8,128)S(1)} %fusion.108, f32[2,8,64,128]{3,2,1,0:T(8,128)S(1)} %bitcast.163, s32[32]{0:T(128)S(1)} %fusion.154, pred[32]{0:T(512)(128)(4,1)S(1)} %get-tuple-element.29), kind=kOutput, calls=%fused_computation.4 | convolution fusion | flops 50594816 | bytes 2621600 | tf_op jit(solution)/shard_map/dot_general | solution.py:245
  17.0 1.8 %fusion.15 = f32[32,64,128]{2,1,0:T(8,128)S(1)} fusion(f32[32,64,128]{2,1,0:T(8,128)S(1)} %bitcast.166, f32[32]{0:T(128)S(1)} %get-tuple-element.121, f32[32]{0:T(128)S(1)} %get-tuple-element.122, f32[32]{0:T(128)S(1)} %get-tuple-element.120, f32[32]{0:T(128)S(1)} %get-tuple-element.90, f32[32]{0:T(128)S(1)} %get-tuple-element.118, ...), kind=kOutput, calls=%fused_computation.40 | convolution fusion | flops 203292672 | bytes 2229248 | tf_op jit(solution)/shard_map/nij,njv->niv/dot_general | solution.py:103
  18.9 1.1 %multiply_add_fusion.6 = f32[32,64,32]{2,1,0:T(8,128)S(1)} fusion(f32[32,64,128]{2,1,0:T(8,128)S(1)} %fusion.15, f32[32]{0:T(128)S(1)} %get-tuple-element.78, f32[32]{0:T(128)S(1)} %get-tuple-element.79, f32[32]{0:T(128)S(1)} %get-tuple-element.80, f32[32]{0:T(128)S(1)} %get-tuple-element.81), kind=kLoop, calls=%fused_computation.38 | loop fusion | flops 458752 | bytes 1311232 | tf_op jit(solution)/shard_map/add | solution.py:121
  20.0 1.3 %multiply_add_fusion.7 = (f32[32,64,32]{2,1,0:T(8,128)S(1)}, f32[32,64,32]{2,1,0:T(8,128)S(1)}, f32[32,64,32]{2,1,0:T(8,128)S(1)}) fusion(f32[32,64,128]{2,1,0:T(8,128)S(1)} %fusion.15, f32[32]{0:T(128)S(1)} %get-tuple-element.82, f32[32]{0:T(128)S(1)} %get-tuple-element.83, f32[32]{0:T(128)S(1)} %get-tuple-element.72, f32[32]{0:T(128)S(1)} %get-tuple-element.75, ...), kind=kLoop, calls=%fused_computation.39 | loop fusion | flops 851968 | bytes 1836032 | tf_op jit(solution)/shard_map/add | solution.py:121
  21.3 0.9 %pad_maximum_fusion.8 = f32[32,64,128]{2,1,0:T(8,128)S(1)} fusion(f32[32,64,32]{2,1,0:T(8,128)S(1)} %get-tuple-element.43, f32[32,64,32]{2,1,0:T(8,128)S(1)} %get-tuple-element.42, f32[32,64,32]{2,1,0:T(8,128)S(1)} %multiply_add_fusion.6, f32[32,64,32]{2,1,0:T(8,128)S(1)} %get-tuple-element.41), kind=kLoop, calls=%fused_computation.28 | loop fusion | flops 786432 | bytes 2097152 | tf_op jit(solution)/shard_map/concatenate | solution.py:123
  22.4 2.2 %collective-permute-start.2 = (f32[32,1,128]{2,1,0:T(1,128)S(1)}, f32[32,1,128]{2,1,0:T(1,128)S(1)}, u32[]{:S(2)}, u32[]{:S(2)}) collective-permute-start(f32[32,1,128]{2,1,0:T(1,128)S(1)} %get-tuple-element.39), channel_id=1, source_target_pairs={{0,1},{1,0},{2,3},{3,2},{4,5},{5,4},{6,7},{7,6},{8,9},{9,8},{10,11... | collective-permute-start | bytes 49160 | tf_op jit(solution)/shard_map/ppermute | solution.py:42
  24.6 2.2 %collective-permute-start.3 = (f32[32,1,128]{2,1,0:T(1,128)S(1)}, f32[32,1,128]{2,1,0:T(1,128)S(1)}, u32[]{:S(2)}, u32[]{:S(2)}) collective-permute-start(f32[32,1,128]{2,1,0:T(1,128)S(1)} %get-tuple-element.40), channel_id=1, source_target_pairs={{1,2},{2,1},{3,0},{0,3},{5,6},{6,5},{7,4},{4,7},{9,10},{10,9},{11,... | collective-permute-start | bytes 49160 | tf_op jit(solution)/shard_map/ppermute | solution.py:51
  26.8 1.4 %pad_select_fusion.1 = (f32[1,65,128]{2,1,0:T(8,128)S(1)}, f32[1,65,128]{2,1,0:T(8,128)S(1)}) fusion(f32[1,64,128]{2,1,0:T(8,128)S(1)} %get-tuple-element.38, f32[]{:T(128)} %bitcast.34, f32[1,64,128]{2,1,0:T(8,128)S(1)} %get-tuple-element.37, f32[]{:T(128)} %bitcast.33, pred[]{:T(512)S(6)} %eq.424), kind=kLoop, calls=%fused_computation.141 | loop fusion | flops 16640 | bytes 132105 | tf_op jit(solution)/shard_map/jit(_where)/select_n | solution.py:43
  28.2 1.5 %collective-permute-start = (f32[1,65,128]{2,1,0:T(8,128)S(1)}, f32[1,65,128]{2,1,0:T(8,128)S(1)}, u32[]{:S(2)}, u32[]{:S(2)}) collective-permute-start(f32[1,65,128]{2,1,0:T(8,128)S(1)} %get-tuple-element.48), channel_id=1, source_target_pairs={{0,4},{4,0},{8,12},{12,8},{1,5},{5,1},{9,13},{13,9},{2,6},{6,2},{1... | collective-permute-start | bytes 99848 | tf_op jit(solution)/shard_map/ppermute | solution.py:42
  29.7 1.9 %collective-permute-start.1 = (f32[1,65,128]{2,1,0:T(8,128)S(1)}, f32[1,65,128]{2,1,0:T(8,128)S(1)}, u32[]{:S(2)}, u32[]{:S(2)}) collective-permute-start(f32[1,65,128]{2,1,0:T(8,128)S(1)} %get-tuple-element.49), channel_id=1, source_target_pairs={{4,8},{8,4},{5,9},{9,5},{6,10},{10,6},{7,11},{11,7},{20,24},{24,20... | collective-permute-start | bytes 99848 | tf_op jit(solution)/shard_map/ppermute | solution.py:51
  31.7 3.3 %collective-permute-done.1 = f32[1,65,128]{2,1,0:T(8,128)S(1)} collective-permute-done((f32[1,65,128]{2,1,0:T(8,128)S(1)}, f32[1,65,128]{2,1,0:T(8,128)S(1)}, u32[]{:S(2)}, u32[]{:S(2)}) %collective-permute-start.1) | collective-permute-done | bytes 33312 | tf_op jit(solution)/shard_map/ppermute | solution.py:51
  37.2 1.4 %gather_fusion.1 = f32[16,64,128]{2,1,0:T(8,128)} fusion(f32[32,64,128]{2,1,0:T(8,128)S(1)} %bitcast.152, s32[1024]{0:T(1024)S(1)} %pad_clamp_fusion), kind=kCustom, calls=%fused_computation.1 | custom fusion | bytes 1048640 | tf_op jit(solution)/shard_map/gather | solution.py:227
  38.6 3.6 %all-to-all-start.1 = ((f32[4,4,64,128]{3,2,1,0:T(8,128)}), f32[4,4,64,128]{3,2,1,0:T(8,128)S(1)}, u32[]{:S(2)}, u32[]{:S(2)}) async-start(f32[4,4,64,128]{3,2,1,0:T(8,128)} %bitcast.41), calls=%async_computation.1 | async-start | bytes 1048576 | tf_op jit(solution)/shard_map/all_to_all | solution.py:233
  42.3 1.4 %maximum_multiply_fusion = f32[34]{0:T(128)S(1)} fusion(f32[1]{0:T(128)} %bitcast.43, f32[32]{0:T(128)S(1)} %copy-done.3, f32[1]{0:T(128)} %bitcast.42, s32[]{:T(128)S(6)} %sub.190), kind=kLoop, calls=%fused_computation.311 | loop fusion | flops 272 | bytes 276 | tf_op jit(solution)/shard_map/mul | solution.py:276
  44.9 3.2 %all-to-all-done.1 = f32[4,4,64,128]{3,2,1,0:T(8,128)S(1)} async-done(((f32[4,4,64,128]{3,2,1,0:T(8,128)}), f32[4,4,64,128]{3,2,1,0:T(8,128)S(1)}, u32[]{:S(2)}, u32[]{:S(2)}) %all-to-all-start.1) | async-done | bytes 524320 | tf_op jit(solution)/shard_map/all_to_all | solution.py:233
  48.1 0.8 %fusion.1 = f32[4,8,64,128]{3,1,2,0:T(8,128)S(1)} fusion(f32[32,8192]{1,0:T(8,128)S(1)} %fusion.105, f32[2,8,64,128]{3,2,1,0:T(8,128)S(1)} %bitcast.164, s32[32]{0:T(128)S(1)} %fusion.153, pred[32]{0:T(512)(128)(4,1)S(1)} %get-tuple-element.18), kind=kOutput, calls=%fused_computation.5 | convolution fusion | flops 50594816 | bytes 2621600 | tf_op jit(solution)/shard_map/dot_general | solution.py:245
  49.1 1.8 %fusion.31 = f32[32,64,128]{2,1,0:T(8,128)S(1)} fusion(f32[32,64,128]{2,1,0:T(8,128)S(1)} %bitcast.165, f32[64,64]{1,0:T(8,128)S(1)} %get-tuple-element.97, f32[32]{0:T(128)S(1)} %get-tuple-element.110, f32[64,64]{1,0:T(8,128)S(1)} %get-tuple-element.98, f32[32]{0:T(128)S(1)} %get-tuple-element.111, f32[64,64]{1,0:T(8,128)S(1)} %get-tuple-element.99, ...), kind=kOutput, calls=%fused_computation.56 | convolution fusion | flops 203292672 | bytes 2229248 | tf_op jit(solution)/shard_map/nij,njv->niv/dot_general | solution.py:103
  51.0 1.0 %fusion.170 = f32[32,1,128]{2,1,0:T(1,128)S(1)} fusion(f32[32,64,1]{1,2,0:T(1,128)S(1)} %bitcast.167, f32[32,64,128]{2,1,0:T(8,128)S(1)} %fusion.31), kind=kOutput, calls=%fused_computation.366 | convolution fusion | flops 3145728 | bytes 1073152 | tf_op jit(solution)/shard_map/pi,piv->pv/dot_general | solution.py:279
  53.0 4.5 %all-to-all-start.2 = ((f32[16,1,768]{2,1,0:T(1,128)}), f32[16,1,768]{2,1,0:T(1,128)S(1)}, u32[]{:S(2)}, u32[]{:S(2)}) async-start(f32[16,1,768]{2,1,0:T(1,128)} %broadcast_in_dim.35), calls=%async_computation.2 | async-start | bytes 98304 | tf_op jit(solution)/shard_map/all_to_all | solution.py:288
  57.4 6.3 %all-to-all-done.2 = f32[16,1,768]{2,1,0:T(1,128)S(1)} async-done(((f32[16,1,768]{2,1,0:T(1,128)}), f32[16,1,768]{2,1,0:T(1,128)S(1)}, u32[]{:S(2)}, u32[]{:S(2)}) %all-to-all-start.2) | async-done | bytes 49184 | tf_op jit(solution)/shard_map/all_to_all | solution.py:288
  63.9 1.1 %multiply_add_fusion.2 = f32[32,64,32]{2,1,0:T(8,128)S(1)} fusion(f32[32,64,128]{2,1,0:T(8,128)S(1)} %broadcast_multiply_fusion, f32[32]{0:T(128)S(1)} %get-tuple-element.64, f32[32]{0:T(128)S(1)} %get-tuple-element.65, f32[32]{0:T(128)S(1)} %get-tuple-element.66, f32[32]{0:T(128)S(1)} %get-tuple-element.67), kind=kLoop, calls=%fused_computation.32 | loop fusion | flops 458752 | bytes 1311232 | tf_op jit(solution)/shard_map/add | solution.py:121
  65.0 1.3 %multiply_add_fusion.3 = (f32[32,64,32]{2,1,0:T(8,128)S(1)}, f32[32,64,32]{2,1,0:T(8,128)S(1)}, f32[32,64,32]{2,1,0:T(8,128)S(1)}) fusion(f32[32,64,128]{2,1,0:T(8,128)S(1)} %broadcast_multiply_fusion, f32[32]{0:T(128)S(1)} %get-tuple-element.68, f32[32]{0:T(128)S(1)} %get-tuple-element.69, f32[32]{0:T(128)S(1)} %get-tuple-element.58, ...), kind=kLoop, calls=%fused_computation.33 | loop fusion | flops 851968 | bytes 1836032 | tf_op jit(solution)/shard_map/add | solution.py:121
  66.3 0.9 %pad_maximum_fusion.9 = f32[32,64,128]{2,1,0:T(8,128)S(1)} fusion(f32[32,64,32]{2,1,0:T(8,128)S(1)} %get-tuple-element.36, f32[32,64,32]{2,1,0:T(8,128)S(1)} %get-tuple-element.35, f32[32,64,32]{2,1,0:T(8,128)S(1)} %multiply_add_fusion.2, f32[32,64,32]{2,1,0:T(8,128)S(1)} %get-tuple-element.34), kind=kLoop, calls=%fused_computation.29 | loop fusion | flops 786432 | bytes 2097152 | tf_op jit(solution)/shard_map/concatenate | solution.py:123
  67.6 1.4 %collective-permute-start.7 = (f32[32,1,128]{2,1,0:T(1,128)S(1)}, f32[32,1,128]{2,1,0:T(1,128)S(1)}, u32[]{:S(2)}, u32[]{:S(2)}) collective-permute-start(f32[32,1,128]{2,1,0:T(1,128)S(1)} %get-tuple-element.33), channel_id=1, source_target_pairs={{1,2},{2,1},{3,0},{0,3},{5,6},{6,5},{7,4},{4,7},{9,10},{10,9},{11,... | collective-permute-start | bytes 49160 | tf_op jit(solution)/shard_map/ppermute | solution.py:51
  69.0 1.0 %collective-permute-start.4 = (f32[1,64,128]{2,1,0:T(8,128)S(1)}, f32[1,64,128]{2,1,0:T(8,128)S(1)}, u32[]{:S(2)}, u32[]{:S(2)}) collective-permute-start(f32[1,64,128]{2,1,0:T(8,128)S(1)} %get-tuple-element.30), channel_id=1, source_target_pairs={{0,4},{4,0},{8,12},{12,8},{1,5},{5,1},{9,13},{13,9},{2,6},{6,2},{1... | collective-permute-start | bytes 98312 | tf_op jit(solution)/shard_map/ppermute | solution.py:42
  70.0 2.2 %collective-permute-start.5 = (f32[1,64,128]{2,1,0:T(8,128)S(1)}, f32[1,64,128]{2,1,0:T(8,128)S(1)}, u32[]{:S(2)}, u32[]{:S(2)}) collective-permute-start(f32[1,64,128]{2,1,0:T(8,128)S(1)} %get-tuple-element.31), channel_id=1, source_target_pairs={{4,8},{8,4},{5,9},{9,5},{6,10},{10,6},{7,11},{11,7},{20,24},{24,20... | collective-permute-start | bytes 98312 | tf_op jit(solution)/shard_map/ppermute | solution.py:51
  72.4 2.8 %collective-permute-done.5 = f32[1,64,128]{2,1,0:T(8,128)S(1)} collective-permute-done((f32[1,64,128]{2,1,0:T(8,128)S(1)}, f32[1,64,128]{2,1,0:T(8,128)S(1)}, u32[]{:S(2)}, u32[]{:S(2)}) %collective-permute-start.5) | collective-permute-done | bytes 32800 | tf_op jit(solution)/shard_map/ppermute | solution.py:51
  75.2 1.4 %fusion.6 = f32[32,64,128]{2,1,0:T(8,128)} fusion(f32[32,64,128]{2,1,0:T(8,128)S(1)} %bitcast.155, f32[32,1,128]{2,1,0:T(1,128)S(1)} %bitcast.172, f32[32,1,128]{2,1,0:T(1,128)S(1)} %bitcast.171, f32[1,64,128]{2,1,0:T(8,128)S(1)} %get-tuple-element.47, f32[1,64,128]{2,1,0:T(8,128)S(1)} %get-tuple-element.46, f32[128]{0:T(128)S(1)} %slice_divide_fusion.1, ...), kind=kLoop, calls=%fused_computation.12 | loop fusion | flops 3145728 | bytes 2196096 | tf_op jit(solution)/shard_map/mul | solution.py:304
  (114 shorter events, 10.5 us)
Async XLA Ops:
  0.0 1.4 %copy-start.2 = (s32[2,16,32]{2,1,0:T(8,128)S(1)}, s32[2,16,32]{2,1,0:T(8,128)}, u32[]{:S(2)}) copy-start(s32[2,16,32]{2,1,0:T(8,128)} %param.7) | copy-start | bytes 12292
  3.8 4.5 %copy-start.1 = (f32[2,3,16,32]{3,2,1,0:T(8,128)S(1)}, f32[2,3,16,32]{3,2,1,0:T(8,128)}, u32[]{:S(2)}) copy-start(f32[2,3,16,32]{3,2,1,0:T(8,128)} %param.5) | copy-start | bytes 36868
  3.8 12.2 %all-to-all-start = ((f32[4,4,64,128]{3,2,1,0:T(8,128)}), f32[4,4,64,128]{3,2,1,0:T(8,128)S(1)}, u32[]{:S(2)}, u32[]{:S(2)}) async-start(f32[4,4,64,128]{3,2,1,0:T(8,128)} %bitcast.18), calls=%async_computation | async-start | bytes 1048576 | tf_op jit(solution)/shard_map/all_to_all | solution.py:233
  10.3 0.7 copy-start.3
  22.2 14.0 %copy-start = (f32[32,64,128]{2,1,0:T(8,128)S(1)}, f32[32,64,128]{2,1,0:T(8,128)}, u32[]{:S(2)}) copy-start(f32[32,64,128]{2,1,0:T(8,128)} %param.4) | copy-start | bytes 3145732
  22.4 9.2 %collective-permute-start.2 = (f32[32,1,128]{2,1,0:T(1,128)S(1)}, f32[32,1,128]{2,1,0:T(1,128)S(1)}, u32[]{:S(2)}, u32[]{:S(2)}) collective-permute-start(f32[32,1,128]{2,1,0:T(1,128)S(1)} %get-tuple-element.39), channel_id=1, source_target_pairs={{0,1},{1,0},{2,3},{3,2},{4,5},{5,4},{6,7},{7,6},{8,9},{9,8},{10,11... | collective-permute-start | bytes 49160 | tf_op jit(solution)/shard_map/ppermute | solution.py:42
  24.6 7.0 %collective-permute-start.3 = (f32[32,1,128]{2,1,0:T(1,128)S(1)}, f32[32,1,128]{2,1,0:T(1,128)S(1)}, u32[]{:S(2)}, u32[]{:S(2)}) collective-permute-start(f32[32,1,128]{2,1,0:T(1,128)S(1)} %get-tuple-element.40), channel_id=1, source_target_pairs={{1,2},{2,1},{3,0},{0,3},{5,6},{6,5},{7,4},{4,7},{9,10},{10,9},{11,... | collective-permute-start | bytes 49160 | tf_op jit(solution)/shard_map/ppermute | solution.py:51
  28.2 3.5 %collective-permute-start = (f32[1,65,128]{2,1,0:T(8,128)S(1)}, f32[1,65,128]{2,1,0:T(8,128)S(1)}, u32[]{:S(2)}, u32[]{:S(2)}) collective-permute-start(f32[1,65,128]{2,1,0:T(8,128)S(1)} %get-tuple-element.48), channel_id=1, source_target_pairs={{0,4},{4,0},{8,12},{12,8},{1,5},{5,1},{9,13},{13,9},{2,6},{6,2},{1... | collective-permute-start | bytes 99848 | tf_op jit(solution)/shard_map/ppermute | solution.py:42
  29.7 5.3 %collective-permute-start.1 = (f32[1,65,128]{2,1,0:T(8,128)S(1)}, f32[1,65,128]{2,1,0:T(8,128)S(1)}, u32[]{:S(2)}, u32[]{:S(2)}) collective-permute-start(f32[1,65,128]{2,1,0:T(8,128)S(1)} %get-tuple-element.49), channel_id=1, source_target_pairs={{4,8},{8,4},{5,9},{9,5},{6,10},{10,6},{7,11},{11,7},{20,24},{24,20... | collective-permute-start | bytes 99848 | tf_op jit(solution)/shard_map/ppermute | solution.py:51
  38.6 9.5 %all-to-all-start.1 = ((f32[4,4,64,128]{3,2,1,0:T(8,128)}), f32[4,4,64,128]{3,2,1,0:T(8,128)S(1)}, u32[]{:S(2)}, u32[]{:S(2)}) async-start(f32[4,4,64,128]{3,2,1,0:T(8,128)} %bitcast.41), calls=%async_computation.1 | async-start | bytes 1048576 | tf_op jit(solution)/shard_map/all_to_all | solution.py:233
  53.0 10.8 %all-to-all-start.2 = ((f32[16,1,768]{2,1,0:T(1,128)}), f32[16,1,768]{2,1,0:T(1,128)S(1)}, u32[]{:S(2)}, u32[]{:S(2)}) async-start(f32[16,1,768]{2,1,0:T(1,128)} %broadcast_in_dim.35), calls=%async_computation.2 | async-start | bytes 98304 | tf_op jit(solution)/shard_map/all_to_all | solution.py:288
  67.5 4.9 %collective-permute-start.6 = (f32[32,1,128]{2,1,0:T(1,128)S(1)}, f32[32,1,128]{2,1,0:T(1,128)S(1)}, u32[]{:S(2)}, u32[]{:S(2)}) collective-permute-start(f32[32,1,128]{2,1,0:T(1,128)S(1)} %get-tuple-element.32), channel_id=1, source_target_pairs={{0,1},{1,0},{2,3},{3,2},{4,5},{5,4},{6,7},{7,6},{8,9},{9,8},{10,11... | collective-permute-start | bytes 49160 | tf_op jit(solution)/shard_map/ppermute | solution.py:42
  67.6 4.7 %collective-permute-start.7 = (f32[32,1,128]{2,1,0:T(1,128)S(1)}, f32[32,1,128]{2,1,0:T(1,128)S(1)}, u32[]{:S(2)}, u32[]{:S(2)}) collective-permute-start(f32[32,1,128]{2,1,0:T(1,128)S(1)} %get-tuple-element.33), channel_id=1, source_target_pairs={{1,2},{2,1},{3,0},{0,3},{5,6},{6,5},{7,4},{4,7},{9,10},{10,9},{11,... | collective-permute-start | bytes 49160 | tf_op jit(solution)/shard_map/ppermute | solution.py:51
  69.0 3.4 %collective-permute-start.4 = (f32[1,64,128]{2,1,0:T(8,128)S(1)}, f32[1,64,128]{2,1,0:T(8,128)S(1)}, u32[]{:S(2)}, u32[]{:S(2)}) collective-permute-start(f32[1,64,128]{2,1,0:T(8,128)S(1)} %get-tuple-element.30), channel_id=1, source_target_pairs={{0,4},{4,0},{8,12},{12,8},{1,5},{5,1},{9,13},{13,9},{2,6},{6,2},{1... | collective-permute-start | bytes 98312 | tf_op jit(solution)/shard_map/ppermute | solution.py:42
  70.0 5.2 %collective-permute-start.5 = (f32[1,64,128]{2,1,0:T(8,128)S(1)}, f32[1,64,128]{2,1,0:T(8,128)S(1)}, u32[]{:S(2)}, u32[]{:S(2)}) collective-permute-start(f32[1,64,128]{2,1,0:T(8,128)S(1)} %get-tuple-element.31), channel_id=1, source_target_pairs={{4,8},{8,4},{5,9},{9,5},{6,10},{10,6},{7,11},{11,7},{20,24},{24,20... | collective-permute-start | bytes 98312 | tf_op jit(solution)/shard_map/ppermute | solution.py:51

commit v16 on v15

--- a/solution.py
+++ b/solution.py
@@ -168,6 +168,20 @@
     k_shape = [1] * advected.ndim
     k_shape[row_dim] = rows
     return advected + diffusivity.reshape(k_shape) * laplace
+
+
+def levels_cols(values, weight_z):
+    value_count = values.shape[-1]
+    per_level = value_count // LEV
+    blocks = [values[..., m * per_level : (m + 1) * per_level] for m in range(LEV)]
+    out = []
+    for level in range(LEV):
+        acc = None
+        for m in tap_sources(level, LEV):
+            term = weight_z[..., level, m][..., None] * blocks[m]
+            acc = term if acc is None else acc + term
+        out.append(acc)
+    return jnp.concatenate(out, axis=-1)
 
 
 def diffuse_first(advected, diffusivity):
@@ -282,6 +296,28 @@
     mix_part = jnp.einsum(
         "plm,pmt->lmt", weight_z, weighted, precision=lax.Precision.HIGHEST
     )
+    field_planar = from_patches(planar, band_rows, band_cols)
+    above, below = neighbour_halos(field_planar[:1], field_planar[row_count - 1 :], "lat", False)
+    left, right = neighbour_halos(
+        field_planar[:, :1], field_planar[:, col_count - 1 :], "lon", True
+    )
+    corner = jnp.zeros((1, 1, value_count), jnp.float32)
+    wide = jnp.concatenate(
+        [
+            jnp.concatenate([corner, left, corner], axis=0),
+            jnp.concatenate([above, field_planar, below], axis=0),
+            jnp.concatenate([corner, right, corner], axis=0),
+        ],
+        axis=1,
+    )
+    fraction_z = shifts[1, 2]
+    patch_rows, patch_cols = fraction_z.shape
+    lon_index = lax.axis_index("lon")
+    wide_rows = jnp.clip(
+        lat_index * band_rows + (jnp.arange(row_count + 2) - 1) // 8, 0, patch_rows - 1
+    )
+    wide_cols = (lon_index * band_cols + (jnp.arange(col_count + 2) - 1) // 8) % patch_cols
+    weight_wide = cubic_matrix(fraction_z[wide_rows][:, wide_cols], LEV)
     partial = jnp.concatenate([target_part, first_part, mix_part.reshape(-1)])
     members = lat_count * lax.axis_size("lon")
     totals = jnp.sum(
@@ -298,10 +334,13 @@
         value_count
     )
     second_ratio = target / second_mass
-    advected = from_patches(
-        levels(planar * first_ratio[None, None, :], frac[2]), band_rows, band_cols
-    )
-    return diffuse(advected, diffusivity, 0) * second_ratio[None, None, :]
+    mixed = levels_cols(wide * first_ratio, weight_wide)
+    centre = mixed[1:-1, 1:-1]
+    laplace = (
+        mixed[2:, 1:-1] + mixed[:-2, 1:-1] + mixed[1:-1, 2:] + mixed[1:-1, :-2] - 4.0 * centre
+    )
+    second = centre + diffusivity[:, None, None] * laplace
+    return second * second_ratio[None, None, :]
 
 
 def solution(mesh):

time: 77.1 us -> 78.5 us (1.018)
  other arithmetic: 13.9 us -> 18.6 us
  waiting for transfers between devices: 19.4 us -> 15.4 us
  local copies, waits for them, and re-layouts: 10 us -> 10.8 us
    add x0 -> x2, other arithmetic: none -> 6.63 us  [levels_cols(): acc = term if acc is None else acc + term]
    ppermute x4, waiting for transfers between devices: 6.09 us -> 3.31 us  [neighbour_halos(): second = lax.ppermute(jnp.where(even, lo_edge, hi_edge), axis, pairs)]
    add x4 -> x2, other arithmetic: 4.85 us -> 2.42 us  [levels(): acc = term if acc is None else acc + term]
    gather x0 -> x4, local copies, waits for them, and re-layouts: none -> 1.34 us  [local(): weight_wide = cubic_matrix(fraction_z[wide_rows][:, wide_cols], LEV)]
    all_to_all x2, waiting for transfers between devices: 6.97 us -> 5.86 us  [departed(): lax.all_to_all(outgoing, 'lat', 0, 0, tiled=True)]
    concatenate x0 -> x1, other arithmetic: none -> 1.08 us  [levels_cols(): return jnp.concatenate(out, axis=-1)]
    ppermute x4, starting transfers between devices: 4.81 us -> 3.8 us  [neighbour_halos(): lax.ppermute(jnp.where(even, hi_edge, lo_edge), axis, [(i, i ^ 1) for i i...]
    concatenate x2 -> x1, other arithmetic: 1.76 us -> 0.88 us  [levels(): return jnp.concatenate(out, axis=2)]
  transfers between devices with their start and end apart: 11 -> 11, of which waited for: 5 -> 4; matrix products, arithmetic and copies ran while one was open for 10% -> 14% of each run, Pallas kernels for 0% -> 0%
where the time goes in v16:
time: 78.5 us; the launch traced here: 77.8 us
  starting transfers between devices  24.6 us (31%)
  other arithmetic  18.6 us (24%)
  waiting for transfers between devices  15.4 us (20%)
  local copies, waits for them, and re-layouts  10.8 us (14%)
  matrix products  7.73 us (10%)
    all_to_all x2, starting transfers between devices, departed(): lax.all_to_all(outgoing, 'lat', 0, 0, tiled=True)  7.9 us
    ppermute x4, starting transfers between devices, neighbour_halos(): second = lax.ppermute(jnp.where(even, lo_edge, hi_edge), axis, pairs)  7.82 us
    add x2, other arithmetic, levels_cols(): acc = term if acc is None else acc + term  6.63 us
    all_to_all x1, waiting for transfers between devices, local(): lax.all_to_all(jnp.broadcast_to(partial, (members,) + partial.shape), ('l...  6.2 us
    all_to_all x2, waiting for transfers between devices, departed(): lax.all_to_all(outgoing, 'lat', 0, 0, tiled=True)  5.86 us
    all_to_all x1, starting transfers between devices, local(): lax.all_to_all(jnp.broadcast_to(partial, (members,) + partial.shape), ('l...  5.04 us
    ppermute x4, starting transfers between devices, neighbour_halos(): lax.ppermute(jnp.where(even, hi_edge, lo_edge), axis, [(i, i ^ 1) for i i...  3.8 us
    dot_general x2, matrix products, spatial(): jnp.einsum('nij,njv->niv', plane_weights(fraction_y, fraction_x), patches...  3.69 us
  transfers between devices with their start and end apart: 11, of which 4 were waited for; matrix products, arithmetic and copies ran while one was open for 14% of the time, Pallas kernels for 0%

profile of v16, /device:TPU:1, one launch (start us, length us, event | category | flops | bytes accessed | tf_op | source)
XLA Modules:
  0.0 77.8 jit_solution(2339449693204044556)
XLA Ops:
  0.0 1.4 %copy.68 = f32[4,8,8,8,128]{4,3,2,1,0:T(8,128)S(1)} copy(f32[4,8,8,8,128]{4,3,1,2,0:T(8,128)} %bitcast.192) | data formatting | bytes 2097152 | tf_op jit(solution)/shard_map/transpose | solution.py:131
  2.4 1.4 %gather_fusion.2 = f32[16,64,128]{2,1,0:T(8,128)} fusion(f32[32,64,128]{2,1,0:T(8,128)S(1)} %bitcast.182, s32[1024]{0:T(1024)S(1)} %pad_clamp_fusion.1), kind=kCustom, calls=%fused_computation.2 | custom fusion | bytes 1048640 | tf_op jit(solution)/shard_map/gather | solution.py:241
  3.8 4.3 %all-to-all-start = ((f32[4,4,64,128]{3,2,1,0:T(8,128)}), f32[4,4,64,128]{3,2,1,0:T(8,128)S(1)}, u32[]{:S(2)}, u32[]{:S(2)}) async-start(f32[4,4,64,128]{3,2,1,0:T(8,128)} %bitcast.21), calls=%async_computation | async-start | bytes 1048576 | tf_op jit(solution)/shard_map/all_to_all | solution.py:247
  12.0 0.7 fusion.179
  13.2 2.6 %all-to-all-done = f32[4,4,64,128]{3,2,1,0:T(8,128)S(1)} async-done(((f32[4,4,64,128]{3,2,1,0:T(8,128)}), f32[4,4,64,128]{3,2,1,0:T(8,128)S(1)}, u32[]{:S(2)}, u32[]{:S(2)}) %all-to-all-start) | async-done | bytes 524320 | tf_op jit(solution)/shard_map/all_to_all | solution.py:247
  15.9 0.8 %fusion = f32[4,8,64,128]{3,1,2,0:T(8,128)S(1)} fusion(f32[32,8192]{1,0:T(8,128)S(1)} %fusion.115, f32[2,8,64,128]{3,2,1,0:T(8,128)S(1)} %bitcast.194, s32[32]{0:T(128)S(1)} %fusion.164, pred[32]{0:T(512)(128)(4,1)S(1)} %get-tuple-element.29), kind=kOutput, calls=%fused_computation.6 | convolution fusion | flops 50594816 | bytes 2621600 | tf_op jit(solution)/shard_map/dot_general | solution.py:259
  16.9 1.8 %fusion.12 = f32[32,64,128]{2,1,0:T(8,128)S(1)} fusion(f32[32,64,128]{2,1,0:T(8,128)S(1)} %bitcast.197, f32[32]{0:T(128)S(1)} %get-tuple-element.125, f32[32]{0:T(128)S(1)} %get-tuple-element.126, f32[32]{0:T(128)S(1)} %get-tuple-element.124, f32[32]{0:T(128)S(1)} %get-tuple-element.94, f32[32]{0:T(128)S(1)} %get-tuple-element.122, ...), kind=kOutput, calls=%fused_computation.39 | convolution fusion | flops 203292672 | bytes 2229248 | tf_op jit(solution)/shard_map/nij,njv->niv/dot_general | solution.py:103
  18.8 1.1 %multiply_add_fusion.6 = f32[32,64,32]{2,1,0:T(8,128)S(1)} fusion(f32[32,64,128]{2,1,0:T(8,128)S(1)} %fusion.12, f32[32]{0:T(128)S(1)} %get-tuple-element.82, f32[32]{0:T(128)S(1)} %get-tuple-element.83, f32[32]{0:T(128)S(1)} %get-tuple-element.84, f32[32]{0:T(128)S(1)} %get-tuple-element.85), kind=kLoop, calls=%fused_computation.37 | loop fusion | flops 458752 | bytes 1311232 | tf_op jit(solution)/shard_map/add | solution.py:121
  19.9 1.3 %multiply_add_fusion.7 = (f32[32,64,32]{2,1,0:T(8,128)S(1)}, f32[32,64,32]{2,1,0:T(8,128)S(1)}, f32[32,64,32]{2,1,0:T(8,128)S(1)}) fusion(f32[32,64,128]{2,1,0:T(8,128)S(1)} %fusion.12, f32[32]{0:T(128)S(1)} %get-tuple-element.86, f32[32]{0:T(128)S(1)} %get-tuple-element.87, f32[32]{0:T(128)S(1)} %get-tuple-element.76, f32[32]{0:T(128)S(1)} %get-tuple-element.79, ...), kind=kLoop, calls=%fused_computation.38 | loop fusion | flops 851968 | bytes 1836032 | tf_op jit(solution)/shard_map/add | solution.py:121
  21.2 0.9 %pad_maximum_fusion.5 = f32[32,64,128]{2,1,0:T(8,128)S(1)} fusion(f32[32,64,32]{2,1,0:T(8,128)S(1)} %get-tuple-element.43, f32[32,64,32]{2,1,0:T(8,128)S(1)} %get-tuple-element.42, f32[32,64,32]{2,1,0:T(8,128)S(1)} %multiply_add_fusion.6, f32[32,64,32]{2,1,0:T(8,128)S(1)} %get-tuple-element.41), kind=kLoop, calls=%fused_computation.32 | loop fusion | flops 786432 | bytes 2097152 | tf_op jit(solution)/shard_map/concatenate | solution.py:123
  22.3 2.2 %collective-permute-start.2 = (f32[32,1,128]{2,1,0:T(1,128)S(1)}, f32[32,1,128]{2,1,0:T(1,128)S(1)}, u32[]{:S(2)}, u32[]{:S(2)}) collective-permute-start(f32[32,1,128]{2,1,0:T(1,128)S(1)} %get-tuple-element.39), channel_id=1, source_target_pairs={{0,1},{1,0},{2,3},{3,2},{4,5},{5,4},{6,7},{7,6},{8,9},{9,8},{10,11... | collective-permute-start | bytes 49160 | tf_op jit(solution)/shard_map/ppermute | solution.py:42
  24.5 2.2 %collective-permute-start.3 = (f32[32,1,128]{2,1,0:T(1,128)S(1)}, f32[32,1,128]{2,1,0:T(1,128)S(1)}, u32[]{:S(2)}, u32[]{:S(2)}) collective-permute-start(f32[32,1,128]{2,1,0:T(1,128)S(1)} %get-tuple-element.40), channel_id=1, source_target_pairs={{1,2},{2,1},{3,0},{0,3},{5,6},{6,5},{7,4},{4,7},{9,10},{10,9},{11,... | collective-permute-start | bytes 49160 | tf_op jit(solution)/shard_map/ppermute | solution.py:51
  26.7 1.3 %pad_select_fusion.1 = (f32[1,65,128]{2,1,0:T(8,128)S(1)}, f32[1,65,128]{2,1,0:T(8,128)S(1)}) fusion(f32[1,64,128]{2,1,0:T(8,128)S(1)} %get-tuple-element.38, f32[]{:T(128)} %bitcast.37, f32[1,64,128]{2,1,0:T(8,128)S(1)} %get-tuple-element.37, f32[]{:T(128)} %bitcast.36, pred[]{:T(512)S(6)} %eq.467), kind=kLoop, calls=%fused_computation.140 | loop fusion | flops 16640 | bytes 132105 | tf_op jit(solution)/shard_map/jit(_where)/select_n | solution.py:43
  28.0 1.5 %collective-permute-start = (f32[1,65,128]{2,1,0:T(8,128)S(1)}, f32[1,65,128]{2,1,0:T(8,128)S(1)}, u32[]{:S(2)}, u32[]{:S(2)}) collective-permute-start(f32[1,65,128]{2,1,0:T(8,128)S(1)} %get-tuple-element.60), channel_id=1, source_target_pairs={{0,4},{4,0},{8,12},{12,8},{1,5},{5,1},{9,13},{13,9},{2,6},{6,2},{1... | collective-permute-start | bytes 99848 | tf_op jit(solution)/shard_map/ppermute | solution.py:42
  29.5 1.9 %collective-permute-start.1 = (f32[1,65,128]{2,1,0:T(8,128)S(1)}, f32[1,65,128]{2,1,0:T(8,128)S(1)}, u32[]{:S(2)}, u32[]{:S(2)}) collective-permute-start(f32[1,65,128]{2,1,0:T(8,128)S(1)} %get-tuple-element.61), channel_id=1, source_target_pairs={{4,8},{8,4},{5,9},{9,5},{6,10},{10,6},{7,11},{11,7},{20,24},{24,20... | collective-permute-start | bytes 99848 | tf_op jit(solution)/shard_map/ppermute | solution.py:51
  31.5 3.3 %collective-permute-done.1 = f32[1,65,128]{2,1,0:T(8,128)S(1)} collective-permute-done((f32[1,65,128]{2,1,0:T(8,128)S(1)}, f32[1,65,128]{2,1,0:T(8,128)S(1)}, u32[]{:S(2)}, u32[]{:S(2)}) %collective-permute-start.1) | collective-permute-done | bytes 33312 | tf_op jit(solution)/shard_map/ppermute | solution.py:51
  36.0 0.7 multiply_reduce_fusion.1
  37.0 1.4 %gather_fusion.3 = f32[16,64,128]{2,1,0:T(8,128)} fusion(f32[32,64,128]{2,1,0:T(8,128)S(1)} %bitcast.183, s32[1024]{0:T(1024)S(1)} %pad_clamp_fusion), kind=kCustom, calls=%fused_computation.3 | custom fusion | bytes 1048640 | tf_op jit(solution)/shard_map/gather | solution.py:241
  38.4 3.6 %all-to-all-start.1 = ((f32[4,4,64,128]{3,2,1,0:T(8,128)}), f32[4,4,64,128]{3,2,1,0:T(8,128)S(1)}, u32[]{:S(2)}, u32[]{:S(2)}) async-start(f32[4,4,64,128]{3,2,1,0:T(8,128)} %bitcast.44), calls=%async_computation.1 | async-start | bytes 1048576 | tf_op jit(solution)/shard_map/all_to_all | solution.py:247
  42.1 1.4 %maximum_multiply_fusion.1 = f32[34]{0:T(128)S(1)} fusion(f32[1]{0:T(128)} %bitcast.49, f32[32]{0:T(128)S(1)} %copy-done.3, f32[1]{0:T(128)} %bitcast.48, s32[]{:T(128)S(6)} %sub.218), kind=kLoop, calls=%fused_computation.345 | loop fusion | flops 272 | bytes 276 | tf_op jit(solution)/shard_map/mul | solution.py:290
  44.6 3.2 %all-to-all-done.1 = f32[4,4,64,128]{3,2,1,0:T(8,128)S(1)} async-done(((f32[4,4,64,128]{3,2,1,0:T(8,128)}), f32[4,4,64,128]{3,2,1,0:T(8,128)S(1)}, u32[]{:S(2)}, u32[]{:S(2)}) %all-to-all-start.1) | async-done | bytes 524320 | tf_op jit(solution)/shard_map/all_to_all | solution.py:247
  47.9 0.8 %fusion.1 = f32[4,8,64,128]{3,1,2,0:T(8,128)S(1)} fusion(f32[32,8192]{1,0:T(8,128)S(1)} %fusion.112, f32[2,8,64,128]{3,2,1,0:T(8,128)S(1)} %bitcast.195, s32[32]{0:T(128)S(1)} %fusion.163, pred[32]{0:T(512)(128)(4,1)S(1)} %get-tuple-element.18), kind=kOutput, calls=%fused_computation.7 | convolution fusion | flops 50594816 | bytes 2621600 | tf_op jit(solution)/shard_map/dot_general | solution.py:259
  48.9 1.8 %fusion.28 = f32[32,64,128]{2,1,0:T(8,128)S(1)} fusion(f32[32,64,128]{2,1,0:T(8,128)S(1)} %bitcast.196, f32[64,64]{1,0:T(8,128)S(1)} %get-tuple-element.101, f32[32]{0:T(128)S(1)} %get-tuple-element.114, f32[64,64]{1,0:T(8,128)S(1)} %get-tuple-element.102, f32[32]{0:T(128)S(1)} %get-tuple-element.115, f32[64,64]{1,0:T(8,128)S(1)} %get-tuple-element.103, ...), kind=kOutput, calls=%fused_computation.55 | convolution fusion | flops 203292672 | bytes 2229248 | tf_op jit(solution)/shard_map/nij,njv->niv/dot_general | solution.py:103
  51.0 1.1 %collective-permute-start.4 = (f32[32,1,128]{2,1,0:T(1,128)S(1)}, f32[32,1,128]{2,1,0:T(1,128)S(1)}, u32[]{:S(2)}, u32[]{:S(2)}) collective-permute-start(f32[32,1,128]{2,1,0:T(1,128)S(1)} %get-tuple-element.35), channel_id=1, source_target_pairs={{1,2},{2,1},{3,0},{0,3},{5,6},{6,5},{7,4},{4,7},{9,10},{10,9},{11,... | collective-permute-start | bytes 49160 | tf_op jit(solution)/shard_map/ppermute | solution.py:51
  52.1 2.6 %collective-permute-start.6 = (f32[1,64,128]{2,1,0:T(8,128)S(1)}, f32[1,64,128]{2,1,0:T(8,128)S(1)}, u32[]{:S(2)}, u32[]{:S(2)}) collective-permute-start(f32[1,64,128]{2,1,0:T(8,128)S(1)} %get-tuple-element.33), channel_id=1, source_target_pairs={{4,8},{8,4},{5,9},{9,5},{6,10},{10,6},{7,11},{11,7},{20,24},{24,20... | collective-permute-start | bytes 98312 | tf_op jit(solution)/shard_map/ppermute | solution.py:51
  54.8 1.0 %fusion.180 = f32[32,1,128]{2,1,0:T(1,128)S(1)} fusion(f32[32,64,1]{1,2,0:T(1,128)S(1)} %bitcast.198, f32[32,64,128]{2,1,0:T(8,128)S(1)} %fusion.28), kind=kOutput, calls=%fused_computation.400 | convolution fusion | flops 3145728 | bytes 1073152 | tf_op jit(solution)/shard_map/pi,piv->pv/dot_general | solution.py:293
  56.8 5.0 %all-to-all-start.2 = ((f32[16,1,768]{2,1,0:T(1,128)}), f32[16,1,768]{2,1,0:T(1,128)S(1)}, u32[]{:S(2)}, u32[]{:S(2)}) async-start(f32[16,1,768]{2,1,0:T(1,128)} %broadcast_in_dim.38), calls=%async_computation.2 | async-start | bytes 98304 | tf_op jit(solution)/shard_map/all_to_all | solution.py:324
  61.9 6.2 %all-to-all-done.2 = f32[16,1,768]{2,1,0:T(1,128)S(1)} async-done(((f32[16,1,768]{2,1,0:T(1,128)}), f32[16,1,768]{2,1,0:T(1,128)S(1)}, u32[]{:S(2)}, u32[]{:S(2)}) %all-to-all-start.2) | async-done | bytes 49184 | tf_op jit(solution)/shard_map/all_to_all | solution.py:324
  68.6 2.5 %multiply_add_fusion.2 = f32[34,66,32]{2,1,0:T(8,128)S(1)} fusion(f32[34,66,128]{2,1,0:T(8,128)S(1)} %maximum_multiply_fusion, f32[34,66]{1,0:T(8,128)S(1)} %get-tuple-element.50, f32[34,66]{1,0:T(8,128)S(1)} %get-tuple-element.51, f32[34,66]{1,0:T(8,128)S(1)} %get-tuple-element.52, f32[34,66]{1,0:T(8,128)S(1)} %get-tuple-element.53), kind=kLoop, calls=%fused_computation.12 | loop fusion | flops 502656 | bytes 1472064 | tf_op jit(solution)/shard_map/add | solution.py:182
  71.2 4.1 %multiply_add_fusion.3 = (f32[34,66,32]{2,1,0:T(8,128)S(1)}, f32[34,66,32]{2,1,0:T(8,128)S(1)}, f32[34,66,32]{2,1,0:T(8,128)S(1)}) fusion(f32[34,66,128]{2,1,0:T(8,128)S(1)} %maximum_multiply_fusion, f32[34,66]{1,0:T(8,128)S(1)} %get-tuple-element.54, f32[34,66]{1,0:T(8,128)S(1)} %get-tuple-element.55, f32[34,66]{1,0:T(8,128)S(1)} %get-tuple-element.44, ...), kind=kLoop, calls=%fused_computation.13 | loop fusion | flops 933504 | bytes 2082432 | tf_op jit(solution)/shard_map/add | solution.py:182
  75.3 1.1 %pad_maximum_fusion = f32[34,66,128]{2,1,0:T(8,128)S(1)} fusion(f32[34,66,32]{2,1,0:T(8,128)S(1)} %get-tuple-element.32, f32[34,66,32]{2,1,0:T(8,128)S(1)} %get-tuple-element.31, f32[34,66,32]{2,1,0:T(8,128)S(1)} %multiply_add_fusion.2, f32[34,66,32]{2,1,0:T(8,128)S(1)} %get-tuple-element.30), kind=kLoop, calls=%fused_computation.9 | loop fusion | flops 861696 | bytes 2297856 | tf_op jit(solution)/shard_map/concatenate | solution.py:184
  76.3 1.4 %fusion.5 = f32[32,64,128]{2,1,0:T(8,128)} fusion(f32[34,66,128]{2,1,0:T(8,128)S(1)} %pad_maximum_fusion, f32[128]{0:T(128)S(1)} %slice_divide_fusion.1, f32[32]{0:T(128)S(1)} %copy-done.3), kind=kLoop, calls=%fused_computation.19 | loop fusion | flops 2097152 | bytes 6292096 | tf_op jit(solution)/shard_map/mul | solution.py:343
  (126 shorter events, 10.2 us)
Async XLA Ops:
  0.0 1.4 %copy-start.2 = (s32[2,16,32]{2,1,0:T(8,128)S(1)}, s32[2,16,32]{2,1,0:T(8,128)}, u32[]{:S(2)}) copy-start(s32[2,16,32]{2,1,0:T(8,128)} %param.7) | copy-start | bytes 12292
  1.4 6.8 %copy-start.1 = (f32[2,3,16,32]{3,2,1,0:T(8,128)S(1)}, f32[2,3,16,32]{3,2,1,0:T(8,128)}, u32[]{:S(2)}) copy-start(f32[2,3,16,32]{3,2,1,0:T(8,128)} %param.5) | copy-start | bytes 36868
  3.8 12.1 %all-to-all-start = ((f32[4,4,64,128]{3,2,1,0:T(8,128)}), f32[4,4,64,128]{3,2,1,0:T(8,128)S(1)}, u32[]{:S(2)}, u32[]{:S(2)}) async-start(f32[4,4,64,128]{3,2,1,0:T(8,128)} %bitcast.21), calls=%async_computation | async-start | bytes 1048576 | tf_op jit(solution)/shard_map/all_to_all | solution.py:247
  11.3 0.7 copy-start.3
  22.1 13.9 %copy-start = (f32[32,64,128]{2,1,0:T(8,128)S(1)}, f32[32,64,128]{2,1,0:T(8,128)}, u32[]{:S(2)}) copy-start(f32[32,64,128]{2,1,0:T(8,128)} %param.4) | copy-start | bytes 3145732
  22.3 9.2 %collective-permute-start.2 = (f32[32,1,128]{2,1,0:T(1,128)S(1)}, f32[32,1,128]{2,1,0:T(1,128)S(1)}, u32[]{:S(2)}, u32[]{:S(2)}) collective-permute-start(f32[32,1,128]{2,1,0:T(1,128)S(1)} %get-tuple-element.39), channel_id=1, source_target_pairs={{0,1},{1,0},{2,3},{3,2},{4,5},{5,4},{6,7},{7,6},{8,9},{9,8},{10,11... | collective-permute-start | bytes 49160 | tf_op jit(solution)/shard_map/ppermute | solution.py:42
  24.5 7.0 %collective-permute-start.3 = (f32[32,1,128]{2,1,0:T(1,128)S(1)}, f32[32,1,128]{2,1,0:T(1,128)S(1)}, u32[]{:S(2)}, u32[]{:S(2)}) collective-permute-start(f32[32,1,128]{2,1,0:T(1,128)S(1)} %get-tuple-element.40), channel_id=1, source_target_pairs={{1,2},{2,1},{3,0},{0,3},{5,6},{6,5},{7,4},{4,7},{9,10},{10,9},{11,... | collective-permute-start | bytes 49160 | tf_op jit(solution)/shard_map/ppermute | solution.py:51
  28.0 3.5 %collective-permute-start = (f32[1,65,128]{2,1,0:T(8,128)S(1)}, f32[1,65,128]{2,1,0:T(8,128)S(1)}, u32[]{:S(2)}, u32[]{:S(2)}) collective-permute-start(f32[1,65,128]{2,1,0:T(8,128)S(1)} %get-tuple-element.60), channel_id=1, source_target_pairs={{0,4},{4,0},{8,12},{12,8},{1,5},{5,1},{9,13},{13,9},{2,6},{6,2},{1... | collective-permute-start | bytes 99848 | tf_op jit(solution)/shard_map/ppermute | solution.py:42
  29.5 5.3 %collective-permute-start.1 = (f32[1,65,128]{2,1,0:T(8,128)S(1)}, f32[1,65,128]{2,1,0:T(8,128)S(1)}, u32[]{:S(2)}, u32[]{:S(2)}) collective-permute-start(f32[1,65,128]{2,1,0:T(8,128)S(1)} %get-tuple-element.61), channel_id=1, source_target_pairs={{4,8},{8,4},{5,9},{9,5},{6,10},{10,6},{7,11},{11,7},{20,24},{24,20... | collective-permute-start | bytes 99848 | tf_op jit(solution)/shard_map/ppermute | solution.py:51
  38.4 9.5 %all-to-all-start.1 = ((f32[4,4,64,128]{3,2,1,0:T(8,128)}), f32[4,4,64,128]{3,2,1,0:T(8,128)S(1)}, u32[]{:S(2)}, u32[]{:S(2)}) async-start(f32[4,4,64,128]{3,2,1,0:T(8,128)} %bitcast.44), calls=%async_computation.1 | async-start | bytes 1048576 | tf_op jit(solution)/shard_map/all_to_all | solution.py:247
  51.0 10.9 %collective-permute-start.4 = (f32[32,1,128]{2,1,0:T(1,128)S(1)}, f32[32,1,128]{2,1,0:T(1,128)S(1)}, u32[]{:S(2)}, u32[]{:S(2)}) collective-permute-start(f32[32,1,128]{2,1,0:T(1,128)S(1)} %get-tuple-element.35), channel_id=1, source_target_pairs={{1,2},{2,1},{3,0},{0,3},{5,6},{6,5},{7,4},{4,7},{9,10},{10,9},{11,... | collective-permute-start | bytes 49160 | tf_op jit(solution)/shard_map/ppermute | solution.py:51
  52.1 9.7 %collective-permute-start.5 = (f32[32,1,128]{2,1,0:T(1,128)S(1)}, f32[32,1,128]{2,1,0:T(1,128)S(1)}, u32[]{:S(2)}, u32[]{:S(2)}) collective-permute-start(f32[32,1,128]{2,1,0:T(1,128)S(1)} %get-tuple-element.36), channel_id=1, source_target_pairs={{0,1},{1,0},{2,3},{3,2},{4,5},{5,4},{6,7},{7,6},{8,9},{9,8},{10,11... | collective-permute-start | bytes 49160 | tf_op jit(solution)/shard_map/ppermute | solution.py:42
  52.1 9.8 %collective-permute-start.6 = (f32[1,64,128]{2,1,0:T(8,128)S(1)}, f32[1,64,128]{2,1,0:T(8,128)S(1)}, u32[]{:S(2)}, u32[]{:S(2)}) collective-permute-start(f32[1,64,128]{2,1,0:T(8,128)S(1)} %get-tuple-element.33), channel_id=1, source_target_pairs={{4,8},{8,4},{5,9},{9,5},{6,10},{10,6},{7,11},{11,7},{20,24},{24,20... | collective-permute-start | bytes 98312 | tf_op jit(solution)/shard_map/ppermute | solution.py:51
  54.7 7.2 %collective-permute-start.7 = (f32[1,64,128]{2,1,0:T(8,128)S(1)}, f32[1,64,128]{2,1,0:T(8,128)S(1)}, u32[]{:S(2)}, u32[]{:S(2)}) collective-permute-start(f32[1,64,128]{2,1,0:T(8,128)S(1)} %get-tuple-element.34), channel_id=1, source_target_pairs={{0,4},{4,0},{8,12},{12,8},{1,5},{5,1},{9,13},{13,9},{2,6},{6,2},{1... | collective-permute-start | bytes 98312 | tf_op jit(solution)/shard_map/ppermute | solution.py:42
  56.8 11.3 %all-to-all-start.2 = ((f32[16,1,768]{2,1,0:T(1,128)}), f32[16,1,768]{2,1,0:T(1,128)S(1)}, u32[]{:S(2)}, u32[]{:S(2)}) async-start(f32[16,1,768]{2,1,0:T(1,128)} %broadcast_in_dim.38), calls=%async_computation.2 | async-start | bytes 98304 | tf_op jit(solution)/shard_map/all_to_all | solution.py:324

commit v17 on v13

--- a/solution.py
+++ b/solution.py
@@ -265,16 +265,21 @@
 
     patches, frac = departed(tracers, source_patch[0], shifts[0])
     advected = from_patches(levels(spatial(patches, frac[0], frac[1]), frac[2]), band_rows, band_cols)
-    first, k_wide = diffuse_first(advected, diffusivity)
+    first = diffuse(advected, diffusivity, 0)
     first_part = column_mass(first, weights)
 
     patches, frac = departed(first, source_patch[1], shifts[1])
     planar = spatial(patches, frac[0], frac[1])
     weight_z = cubic_matrix(frac[2], LEV)
 
-    area_wide = column_area(lat_index * row_count - 1, row_count + 2, total_rows)
-    flux = area_wide * k_wide
-    g = weights - 2.0 * flux[1:-1] + flux[:-2] + flux[2:]
+    flux = weights * diffusivity
+    zero = jnp.zeros((1,), jnp.float32)
+    g = (
+        weights
+        - 2.0 * flux
+        + jnp.concatenate([zero, flux[:-1]])
+        + jnp.concatenate([flux[1:], zero])
+    )
     g_cols = jnp.broadcast_to(g.reshape(band_rows, 1, 8, 1), (band_rows, band_cols, 8, 8))
     weighted = jnp.einsum(
         "pi,piv->pv", g_cols.reshape(per_device, 64), planar, precision=lax.Precision.HIGHEST
@@ -282,9 +287,57 @@
     mix_part = jnp.einsum(
         "plm,pmt->lmt", weight_z, weighted, precision=lax.Precision.HIGHEST
     )
-    totals = all_sum(
-        jnp.concatenate([target_part, first_part, mix_part.reshape(-1)]), ("lon", "lat")
-    )
+    top_row = jnp.sum(planar[:band_cols, :8], axis=1).reshape(band_cols, LEV, per_level)
+    bottom_row = jnp.sum(planar[per_device - band_cols :, 56:], axis=1).reshape(
+        band_cols, LEV, per_level
+    )
+    top_part = jnp.einsum(
+        "plm,pmt->lmt", weight_z[:band_cols], top_row, precision=lax.Precision.HIGHEST
+    )
+    bottom_part = jnp.einsum(
+        "plm,pmt->lmt",
+        weight_z[per_device - band_cols :],
+        bottom_row,
+        precision=lax.Precision.HIGHEST,
+    )
+    mix_size = LEV * value_count
+    tag = jnp.zeros((value_count,), jnp.float32)
+    tag = tag.at[0].set(diffusivity[0]).at[1].set(diffusivity[row_count - 1])
+    tag = tag.at[2].set(lat_index.astype(jnp.float32))
+    partial = jnp.concatenate(
+        [
+            target_part,
+            first_part,
+            mix_part.reshape(-1),
+            top_part.reshape(-1),
+            bottom_part.reshape(-1),
+            tag,
+        ]
+    )
+    members = lat_count * lax.axis_size("lon")
+    everyone = lax.all_to_all(
+        jnp.broadcast_to(partial, (members,) + partial.shape), ("lat", "lon"), 0, 0, tiled=True
+    ).reshape(members, -1)
+    head = 2 * value_count + mix_size
+    tags = everyone[:, head + 2 * mix_size :]
+    band_of = tags[:, 2]
+    k_first, k_last = tags[:, 0], tags[:, 1]
+    above_k = jnp.max(
+        jnp.where(band_of[None, :] == band_of[:, None] - 1.0, k_last[None, :], 0.0), axis=1
+    )
+    below_k = jnp.max(
+        jnp.where(band_of[None, :] == band_of[:, None] + 1.0, k_first[None, :], 0.0), axis=1
+    )
+    angle = math.pi / total_rows
+    above_area = jnp.cos((band_of * row_count - 0.5) * angle - 0.5 * math.pi)
+    below_area = jnp.cos((band_of * row_count + row_count + 0.5) * angle - 0.5 * math.pi)
+    edge_terms = jnp.sum(
+        (above_area * above_k)[:, None] * everyone[:, head : head + mix_size]
+        + (below_area * below_k)[:, None] * everyone[:, head + mix_size : head + 2 * mix_size],
+        axis=0,
+    )
+    totals = jnp.sum(everyone[:, :head], axis=0)
+    totals = totals.at[2 * value_count :].add(edge_terms)
     target = totals[:value_count]
     first_mass = totals[value_count : 2 * value_count]
     mix = totals[2 * value_count :].reshape(LEV, LEV, per_level)

time: 78.6 us -> 77.8 us (0.990)
  other arithmetic: 13.6 us -> 11.4 us
    ppermute x4 -> x0, waiting for transfers between devices: 8.67 us -> none  [all_sum(): lax.ppermute(value, axis, [(i, i ^ distance) for i in range(count)])]
    all_to_all x0 -> x1, waiting for transfers between devices: none -> 7.03 us  [local(): lax.all_to_all(jnp.broadcast_to(partial, (members,) + partial.shape), ('l...]
    all_to_all x0 -> x1, starting transfers between devices: none -> 4.46 us  [local(): lax.all_to_all(jnp.broadcast_to(partial, (members,) + partial.shape), ('l...]
    ppermute x4 -> x0, starting transfers between devices: 3.97 us -> none  [all_sum(): lax.ppermute(value, axis, [(i, i ^ distance) for i in range(count)])]
    slice x10 -> x1, local copies, waits for them, and re-layouts: 1.93 us -> 0.07 us  [local(): flux[1:]]
    all_to_all x2, waiting for transfers between devices: 7.19 us -> 8.94 us  [departed(): lax.all_to_all(outgoing, 'lat', 0, 0, tiled=True)]
    ppermute x4, starting transfers between devices: 6.05 us -> 4.72 us  [neighbour_halos(): lax.ppermute(jnp.where(even, hi_edge, lo_edge), axis, [(i, i ^ 1) for i i...]
    ppermute x4, starting transfers between devices: 6.76 us -> 8.04 us  [neighbour_halos(): second = lax.ppermute(jnp.where(even, lo_edge, hi_edge), axis, pairs)]
  transfers between devices with their start and end apart: 14 -> 11, of which waited for: 8 -> 5; matrix products, arithmetic and copies ran while one was open for 9% -> 5% of each run, Pallas kernels for 0% -> 0%
where the time goes in v17:
time: 77.8 us; the launch traced here: 77.3 us
  starting transfers between devices  25.3 us (33%)
  waiting for transfers between devices  22 us (28%)
  other arithmetic  11.4 us (15%)
  local copies, waits for them, and re-layouts  9.77 us (13%)
  matrix products  8.13 us (10%)
    all_to_all x2, waiting for transfers between devices, departed(): lax.all_to_all(outgoing, 'lat', 0, 0, tiled=True)  8.94 us
    ppermute x4, starting transfers between devices, neighbour_halos(): second = lax.ppermute(jnp.where(even, lo_edge, hi_edge), axis, pairs)  8.04 us
    all_to_all x2, starting transfers between devices, departed(): lax.all_to_all(outgoing, 'lat', 0, 0, tiled=True)  8.04 us
    all_to_all x1, waiting for transfers between devices, local(): lax.all_to_all(jnp.broadcast_to(partial, (members,) + partial.shape), ('l...  7.03 us
    ppermute x4, waiting for transfers between devices, neighbour_halos(): second = lax.ppermute(jnp.where(even, lo_edge, hi_edge), axis, pairs)  6.07 us
    add x4, other arithmetic, levels(): acc = term if acc is None else acc + term  4.85 us
    ppermute x4, starting transfers between devices, neighbour_halos(): lax.ppermute(jnp.where(even, hi_edge, lo_edge), axis, [(i, i ^ 1) for i i...  4.72 us
    all_to_all x1, starting transfers between devices, local(): lax.all_to_all(jnp.broadcast_to(partial, (members,) + partial.shape), ('l...  4.46 us
  transfers between devices with their start and end apart: 11, of which 5 were waited for; matrix products, arithmetic and copies ran while one was open for 5% of the time, Pallas kernels for 0%

profile of v17, /device:TPU:1, one launch (start us, length us, event | category | flops | bytes accessed | tf_op | source)
XLA Modules:
  0.0 77.3 jit_solution(15736037571749941503)
XLA Ops:
  0.0 0.7 fusion.176
  1.7 1.4 %copy.40 = f32[4,8,8,8,128]{4,3,2,1,0:T(8,128)S(1)} copy(f32[4,8,8,8,128]{4,3,1,2,0:T(8,128)} %bitcast.187) | data formatting | bytes 2097152 | tf_op jit(solution)/shard_map/transpose | solution.py:131
  3.1 1.4 %gather_fusion = f32[16,64,128]{2,1,0:T(8,128)} fusion(f32[32,64,128]{2,1,0:T(8,128)S(1)} %bitcast.177, s32[1024]{0:T(1024)S(1)} %pad_clamp_fusion.1), kind=kCustom, calls=%fused_computation | custom fusion | bytes 1048640 | tf_op jit(solution)/shard_map/gather | solution.py:227
  4.5 4.4 %all-to-all-start = ((f32[4,4,64,128]{3,2,1,0:T(8,128)}), f32[4,4,64,128]{3,2,1,0:T(8,128)S(1)}, u32[]{:S(2)}, u32[]{:S(2)}) async-start(f32[4,4,64,128]{3,2,1,0:T(8,128)} %bitcast.18), calls=%async_computation | async-start | bytes 1048576 | tf_op jit(solution)/shard_map/all_to_all | solution.py:233
  12.7 4.0 %all-to-all-done = f32[4,4,64,128]{3,2,1,0:T(8,128)S(1)} async-done(((f32[4,4,64,128]{3,2,1,0:T(8,128)}), f32[4,4,64,128]{3,2,1,0:T(8,128)S(1)}, u32[]{:S(2)}, u32[]{:S(2)}) %all-to-all-start) | async-done | bytes 524320 | tf_op jit(solution)/shard_map/all_to_all | solution.py:233
  16.7 0.8 %fusion = f32[4,8,64,128]{3,1,2,0:T(8,128)S(1)} fusion(f32[32,8192]{1,0:T(8,128)S(1)} %fusion.112, f32[2,8,64,128]{3,2,1,0:T(8,128)S(1)} %bitcast.193, s32[32]{0:T(128)S(1)} %fusion.162, pred[32]{0:T(512)(128)(4,1)S(1)} %get-tuple-element.81), kind=kOutput, calls=%fused_computation.4 | convolution fusion | flops 50594816 | bytes 2621600 | tf_op jit(solution)/shard_map/dot_general | solution.py:245
  17.7 1.8 %fusion.15 = f32[32,64,128]{2,1,0:T(8,128)S(1)} fusion(f32[32,64,128]{2,1,0:T(8,128)S(1)} %bitcast.196, f32[32]{0:T(128)S(1)} %get-tuple-element.175, f32[32]{0:T(128)S(1)} %get-tuple-element.176, f32[32]{0:T(128)S(1)} %get-tuple-element.174, f32[32]{0:T(128)S(1)} %get-tuple-element.147, f32[32]{0:T(128)S(1)} %get-tuple-element.172, ...), kind=kOutput, calls=%fused_computation.42 | convolution fusion | flops 203292672 | bytes 2229248 | tf_op jit(solution)/shard_map/nij,njv->niv/dot_general | solution.py:103
  19.6 1.1 %multiply_add_fusion.6 = f32[32,64,32]{2,1,0:T(8,128)S(1)} fusion(f32[32,64,128]{2,1,0:T(8,128)S(1)} %fusion.15, f32[32]{0:T(128)S(1)} %get-tuple-element.135, f32[32]{0:T(128)S(1)} %get-tuple-element.136, f32[32]{0:T(128)S(1)} %get-tuple-element.137, f32[32]{0:T(128)S(1)} %get-tuple-element.138), kind=kLoop, calls=%fused_computation.40 | loop fusion | flops 458752 | bytes 1311232 | tf_op jit(solution)/shard_map/add | solution.py:121
  20.7 1.3 %multiply_add_fusion.7 = (f32[32,64,32]{2,1,0:T(8,128)S(1)}, f32[32,64,32]{2,1,0:T(8,128)S(1)}, f32[32,64,32]{2,1,0:T(8,128)S(1)}) fusion(f32[32,64,128]{2,1,0:T(8,128)S(1)} %fusion.15, f32[32]{0:T(128)S(1)} %get-tuple-element.139, f32[32]{0:T(128)S(1)} %get-tuple-element.140, f32[32]{0:T(128)S(1)} %get-tuple-element.129, f32[32]{0:T(128)S(1)} %get-tuple-element.132, ...), kind=kLoop, calls=%fused_computation.41 | loop fusion | flops 851968 | bytes 1836032 | tf_op jit(solution)/shard_map/add | solution.py:121
  22.0 0.9 %pad_maximum_fusion.8 = f32[32,64,128]{2,1,0:T(8,128)S(1)} fusion(f32[32,64,32]{2,1,0:T(8,128)S(1)} %get-tuple-element.95, f32[32,64,32]{2,1,0:T(8,128)S(1)} %get-tuple-element.94, f32[32,64,32]{2,1,0:T(8,128)S(1)} %multiply_add_fusion.6, f32[32,64,32]{2,1,0:T(8,128)S(1)} %get-tuple-element.93), kind=kLoop, calls=%fused_computation.30 | loop fusion | flops 786432 | bytes 2097152 | tf_op jit(solution)/shard_map/concatenate | solution.py:123
  23.1 2.2 %collective-permute-start.2 = (f32[32,1,128]{2,1,0:T(1,128)S(1)}, f32[32,1,128]{2,1,0:T(1,128)S(1)}, u32[]{:S(2)}, u32[]{:S(2)}) collective-permute-start(f32[32,1,128]{2,1,0:T(1,128)S(1)} %get-tuple-element.91), channel_id=1, source_target_pairs={{0,1},{1,0},{2,3},{3,2},{4,5},{5,4},{6,7},{7,6},{8,9},{9,8},{10,11... | collective-permute-start | bytes 49160 | tf_op jit(solution)/shard_map/ppermute | solution.py:42
  25.3 2.2 %collective-permute-start.3 = (f32[32,1,128]{2,1,0:T(1,128)S(1)}, f32[32,1,128]{2,1,0:T(1,128)S(1)}, u32[]{:S(2)}, u32[]{:S(2)}) collective-permute-start(f32[32,1,128]{2,1,0:T(1,128)S(1)} %get-tuple-element.92), channel_id=1, source_target_pairs={{1,2},{2,1},{3,0},{0,3},{5,6},{6,5},{7,4},{4,7},{9,10},{10,9},{11,... | collective-permute-start | bytes 49160 | tf_op jit(solution)/shard_map/ppermute | solution.py:51
  27.5 1.5 %collective-permute-start = (f32[1,64,128]{2,1,0:T(8,128)S(1)}, f32[1,64,128]{2,1,0:T(8,128)S(1)}, u32[]{:S(2)}, u32[]{:S(2)}) collective-permute-start(f32[1,64,128]{2,1,0:T(8,128)S(1)} %get-tuple-element.89), channel_id=1, source_target_pairs={{0,4},{4,0},{8,12},{12,8},{1,5},{5,1},{9,13},{13,9},{2,6},{6,2},{1... | collective-permute-start | bytes 98312 | tf_op jit(solution)/shard_map/ppermute | solution.py:42
  29.0 1.9 %collective-permute-start.1 = (f32[1,64,128]{2,1,0:T(8,128)S(1)}, f32[1,64,128]{2,1,0:T(8,128)S(1)}, u32[]{:S(2)}, u32[]{:S(2)}) collective-permute-start(f32[1,64,128]{2,1,0:T(8,128)S(1)} %get-tuple-element.90), channel_id=1, source_target_pairs={{4,8},{8,4},{5,9},{9,5},{6,10},{10,6},{7,11},{11,7},{20,24},{24,20... | collective-permute-start | bytes 98312 | tf_op jit(solution)/shard_map/ppermute | solution.py:51
  31.0 3.3 %collective-permute-done.1 = f32[1,64,128]{2,1,0:T(8,128)S(1)} collective-permute-done((f32[1,64,128]{2,1,0:T(8,128)S(1)}, f32[1,64,128]{2,1,0:T(8,128)S(1)}, u32[]{:S(2)}, u32[]{:S(2)}) %collective-permute-start.1) | collective-permute-done | bytes 32800 | tf_op jit(solution)/shard_map/ppermute | solution.py:51
  34.2 0.7 multiply_reduce_fusion
  35.1 1.4 %gather_fusion.1 = f32[16,64,128]{2,1,0:T(8,128)} fusion(f32[32,64,128]{2,1,0:T(8,128)S(1)} %bitcast.178, s32[1024]{0:T(1024)S(1)} %pad_clamp_fusion), kind=kCustom, calls=%fused_computation.1 | custom fusion | bytes 1048640 | tf_op jit(solution)/shard_map/gather | solution.py:227
  36.5 3.6 %all-to-all-start.1 = ((f32[4,4,64,128]{3,2,1,0:T(8,128)}), f32[4,4,64,128]{3,2,1,0:T(8,128)S(1)}, u32[]{:S(2)}, u32[]{:S(2)}) async-start(f32[4,4,64,128]{3,2,1,0:T(8,128)} %bitcast.39), calls=%async_computation.1 | async-start | bytes 1048576 | tf_op jit(solution)/shard_map/all_to_all | solution.py:233
  41.0 5.0 %all-to-all-done.1 = f32[4,4,64,128]{3,2,1,0:T(8,128)S(1)} async-done(((f32[4,4,64,128]{3,2,1,0:T(8,128)}), f32[4,4,64,128]{3,2,1,0:T(8,128)S(1)}, u32[]{:S(2)}, u32[]{:S(2)}) %all-to-all-start.1) | async-done | bytes 524320 | tf_op jit(solution)/shard_map/all_to_all | solution.py:233
  46.0 0.8 %fusion.1 = f32[4,8,64,128]{3,1,2,0:T(8,128)S(1)} fusion(f32[32,8192]{1,0:T(8,128)S(1)} %fusion.109, f32[2,8,64,128]{3,2,1,0:T(8,128)S(1)} %bitcast.194, s32[32]{0:T(128)S(1)} %fusion.161, pred[32]{0:T(512)(128)(4,1)S(1)} %get-tuple-element.70), kind=kOutput, calls=%fused_computation.5 | convolution fusion | flops 50594816 | bytes 2621600 | tf_op jit(solution)/shard_map/dot_general | solution.py:245
  47.0 1.8 %fusion.31 = f32[32,64,128]{2,1,0:T(8,128)S(1)} fusion(f32[32,64,128]{2,1,0:T(8,128)S(1)} %bitcast.195, f32[64,64]{1,0:T(8,128)S(1)} %get-tuple-element.154, f32[32]{0:T(128)S(1)} %get-tuple-element.166, f32[64,64]{1,0:T(8,128)S(1)} %get-tuple-element.155, f32[32]{0:T(128)S(1)} %get-tuple-element.167, f32[64,64]{1,0:T(8,128)S(1)} %get-tuple-element.156, ...), kind=kOutput, calls=%fused_computation.58 | convolution fusion | flops 203292672 | bytes 2229248 | tf_op jit(solution)/shard_map/nij,njv->niv/dot_general | solution.py:103
  49.6 1.0 %fusion.178 = f32[32,1,128]{2,1,0:T(1,128)S(1)} fusion(f32[32,64,1]{1,2,0:T(1,128)S(1)} %bitcast.197, f32[32,64,128]{2,1,0:T(8,128)S(1)} %fusion.31), kind=kOutput, calls=%fused_computation.396 | convolution fusion | flops 3145728 | bytes 1073152 | tf_op jit(solution)/shard_map/pi,piv->pv/dot_general | solution.py:284
  51.7 4.5 %all-to-all-start.2 = ((f32[16,1,1920]{2,1,0:T(1,128)}), f32[16,1,1920]{2,1,0:T(1,128)S(1)}, u32[]{:S(2)}, u32[]{:S(2)}) async-start(f32[16,1,1920]{2,1,0:T(1,128)} %broadcast_in_dim.56), calls=%async_computation.2 | async-start | bytes 245760 | tf_op jit(solution)/shard_map/all_to_all | solution.py:318
  56.2 7.0 %all-to-all-done.2 = f32[16,1,1920]{2,1,0:T(1,128)S(1)} async-done(((f32[16,1,1920]{2,1,0:T(1,128)}), f32[16,1,1920]{2,1,0:T(1,128)S(1)}, u32[]{:S(2)}, u32[]{:S(2)}) %all-to-all-start.2) | async-done | bytes 122912 | tf_op jit(solution)/shard_map/all_to_all | solution.py:318
  64.0 1.1 %multiply_add_fusion.2 = f32[32,64,32]{2,1,0:T(8,128)S(1)} fusion(f32[32,64,128]{2,1,0:T(8,128)S(1)} %broadcast_multiply_fusion, f32[32]{0:T(128)S(1)} %get-tuple-element.121, f32[32]{0:T(128)S(1)} %get-tuple-element.122, f32[32]{0:T(128)S(1)} %get-tuple-element.123, f32[32]{0:T(128)S(1)} %get-tuple-element.124), kind=kLoop, calls=%fused_computation.34 | loop fusion | flops 458752 | bytes 1311232 | tf_op jit(solution)/shard_map/add | solution.py:121
  65.1 1.3 %multiply_add_fusion.3 = (f32[32,64,32]{2,1,0:T(8,128)S(1)}, f32[32,64,32]{2,1,0:T(8,128)S(1)}, f32[32,64,32]{2,1,0:T(8,128)S(1)}) fusion(f32[32,64,128]{2,1,0:T(8,128)S(1)} %broadcast_multiply_fusion, f32[32]{0:T(128)S(1)} %get-tuple-element.125, f32[32]{0:T(128)S(1)} %get-tuple-element.126, f32[32]{0:T(128)S(1)} %get-tuple-element.115, ...), kind=kLoop, calls=%fused_computation.35 | loop fusion | flops 851968 | bytes 1836032 | tf_op jit(solution)/shard_map/add | solution.py:121
  66.4 0.9 %pad_maximum_fusion.9 = f32[32,64,128]{2,1,0:T(8,128)S(1)} fusion(f32[32,64,32]{2,1,0:T(8,128)S(1)} %get-tuple-element.88, f32[32,64,32]{2,1,0:T(8,128)S(1)} %get-tuple-element.87, f32[32,64,32]{2,1,0:T(8,128)S(1)} %multiply_add_fusion.2, f32[32,64,32]{2,1,0:T(8,128)S(1)} %get-tuple-element.86), kind=kLoop, calls=%fused_computation.31 | loop fusion | flops 786432 | bytes 2097152 | tf_op jit(solution)/shard_map/concatenate | solution.py:123
  68.1 1.6 %collective-permute-start.7 = (f32[32,1,128]{2,1,0:T(1,128)S(1)}, f32[32,1,128]{2,1,0:T(1,128)S(1)}, u32[]{:S(2)}, u32[]{:S(2)}) collective-permute-start(f32[32,1,128]{2,1,0:T(1,128)S(1)} %get-tuple-element.85), channel_id=1, source_target_pairs={{1,2},{2,1},{3,0},{0,3},{5,6},{6,5},{7,4},{4,7},{9,10},{10,9},{11,... | collective-permute-start | bytes 49160 | tf_op jit(solution)/shard_map/ppermute | solution.py:51
  69.7 1.0 %collective-permute-start.4 = (f32[1,64,128]{2,1,0:T(8,128)S(1)}, f32[1,64,128]{2,1,0:T(8,128)S(1)}, u32[]{:S(2)}, u32[]{:S(2)}) collective-permute-start(f32[1,64,128]{2,1,0:T(8,128)S(1)} %get-tuple-element.82), channel_id=1, source_target_pairs={{0,4},{4,0},{8,12},{12,8},{1,5},{5,1},{9,13},{13,9},{2,6},{6,2},{1... | collective-permute-start | bytes 98312 | tf_op jit(solution)/shard_map/ppermute | solution.py:42
  70.7 2.4 %collective-permute-start.5 = (f32[1,64,128]{2,1,0:T(8,128)S(1)}, f32[1,64,128]{2,1,0:T(8,128)S(1)}, u32[]{:S(2)}, u32[]{:S(2)}) collective-permute-start(f32[1,64,128]{2,1,0:T(8,128)S(1)} %get-tuple-element.83), channel_id=1, source_target_pairs={{4,8},{8,4},{5,9},{9,5},{6,10},{10,6},{7,11},{11,7},{20,24},{24,20... | collective-permute-start | bytes 98312 | tf_op jit(solution)/shard_map/ppermute | solution.py:51
  73.1 2.8 %collective-permute-done.5 = f32[1,64,128]{2,1,0:T(8,128)S(1)} collective-permute-done((f32[1,64,128]{2,1,0:T(8,128)S(1)}, f32[1,64,128]{2,1,0:T(8,128)S(1)}, u32[]{:S(2)}, u32[]{:S(2)}) %collective-permute-start.5) | collective-permute-done | bytes 32800 | tf_op jit(solution)/shard_map/ppermute | solution.py:51
  75.9 1.4 %fusion.6 = f32[32,64,128]{2,1,0:T(8,128)} fusion(f32[32,64,128]{2,1,0:T(8,128)S(1)} %bitcast.181, f32[32,1,128]{2,1,0:T(1,128)S(1)} %bitcast.202, f32[32,1,128]{2,1,0:T(1,128)S(1)} %bitcast.201, f32[1,64,128]{2,1,0:T(8,128)S(1)} %get-tuple-element.104, f32[1,64,128]{2,1,0:T(8,128)S(1)} %get-tuple-element.103, f32[128]{0:T(128)S(1)} %slice_divide_fusion.1, ...), kind=kLoop, calls=%fused_computation.14 | loop fusion | flops 3145728 | bytes 2196096 | tf_op jit(solution)/shard_map/mul | solution.py:352
  (127 shorter events, 9.4 us)
Async XLA Ops:
  4.5 4.5 %copy-start.1 = (f32[2,3,16,32]{3,2,1,0:T(8,128)S(1)}, f32[2,3,16,32]{3,2,1,0:T(8,128)}, u32[]{:S(2)}) copy-start(f32[2,3,16,32]{3,2,1,0:T(8,128)} %param.13) | copy-start | bytes 36868
  4.5 12.2 %all-to-all-start = ((f32[4,4,64,128]{3,2,1,0:T(8,128)}), f32[4,4,64,128]{3,2,1,0:T(8,128)S(1)}, u32[]{:S(2)}, u32[]{:S(2)}) async-start(f32[4,4,64,128]{3,2,1,0:T(8,128)} %bitcast.18), calls=%async_computation | async-start | bytes 1048576 | tf_op jit(solution)/shard_map/all_to_all | solution.py:233
  10.2 0.7 copy-start.2
  22.9 11.3 %copy-start = (f32[32,64,128]{2,1,0:T(8,128)S(1)}, f32[32,64,128]{2,1,0:T(8,128)}, u32[]{:S(2)}) copy-start(f32[32,64,128]{2,1,0:T(8,128)} %param.12) | copy-start | bytes 3145732
  23.1 7.8 %collective-permute-start.2 = (f32[32,1,128]{2,1,0:T(1,128)S(1)}, f32[32,1,128]{2,1,0:T(1,128)S(1)}, u32[]{:S(2)}, u32[]{:S(2)}) collective-permute-start(f32[32,1,128]{2,1,0:T(1,128)S(1)} %get-tuple-element.91), channel_id=1, source_target_pairs={{0,1},{1,0},{2,3},{3,2},{4,5},{5,4},{6,7},{7,6},{8,9},{9,8},{10,11... | collective-permute-start | bytes 49160 | tf_op jit(solution)/shard_map/ppermute | solution.py:42
  25.3 5.6 %collective-permute-start.3 = (f32[32,1,128]{2,1,0:T(1,128)S(1)}, f32[32,1,128]{2,1,0:T(1,128)S(1)}, u32[]{:S(2)}, u32[]{:S(2)}) collective-permute-start(f32[32,1,128]{2,1,0:T(1,128)S(1)} %get-tuple-element.92), channel_id=1, source_target_pairs={{1,2},{2,1},{3,0},{0,3},{5,6},{6,5},{7,4},{4,7},{9,10},{10,9},{11,... | collective-permute-start | bytes 49160 | tf_op jit(solution)/shard_map/ppermute | solution.py:51
  27.5 3.4 %collective-permute-start = (f32[1,64,128]{2,1,0:T(8,128)S(1)}, f32[1,64,128]{2,1,0:T(8,128)S(1)}, u32[]{:S(2)}, u32[]{:S(2)}) collective-permute-start(f32[1,64,128]{2,1,0:T(8,128)S(1)} %get-tuple-element.89), channel_id=1, source_target_pairs={{0,4},{4,0},{8,12},{12,8},{1,5},{5,1},{9,13},{13,9},{2,6},{6,2},{1... | collective-permute-start | bytes 98312 | tf_op jit(solution)/shard_map/ppermute | solution.py:42
  29.0 5.2 %collective-permute-start.1 = (f32[1,64,128]{2,1,0:T(8,128)S(1)}, f32[1,64,128]{2,1,0:T(8,128)S(1)}, u32[]{:S(2)}, u32[]{:S(2)}) collective-permute-start(f32[1,64,128]{2,1,0:T(8,128)S(1)} %get-tuple-element.90), channel_id=1, source_target_pairs={{4,8},{8,4},{5,9},{9,5},{6,10},{10,6},{7,11},{11,7},{20,24},{24,20... | collective-permute-start | bytes 98312 | tf_op jit(solution)/shard_map/ppermute | solution.py:51
  36.5 9.5 %all-to-all-start.1 = ((f32[4,4,64,128]{3,2,1,0:T(8,128)}), f32[4,4,64,128]{3,2,1,0:T(8,128)S(1)}, u32[]{:S(2)}, u32[]{:S(2)}) async-start(f32[4,4,64,128]{3,2,1,0:T(8,128)} %bitcast.39), calls=%async_computation.1 | async-start | bytes 1048576 | tf_op jit(solution)/shard_map/all_to_all | solution.py:233
  51.7 11.5 %all-to-all-start.2 = ((f32[16,1,1920]{2,1,0:T(1,128)}), f32[16,1,1920]{2,1,0:T(1,128)S(1)}, u32[]{:S(2)}, u32[]{:S(2)}) async-start(f32[16,1,1920]{2,1,0:T(1,128)} %broadcast_in_dim.56), calls=%async_computation.2 | async-start | bytes 245760 | tf_op jit(solution)/shard_map/all_to_all | solution.py:318
  68.1 5.0 %collective-permute-start.6 = (f32[32,1,128]{2,1,0:T(1,128)S(1)}, f32[32,1,128]{2,1,0:T(1,128)S(1)}, u32[]{:S(2)}, u32[]{:S(2)}) collective-permute-start(f32[32,1,128]{2,1,0:T(1,128)S(1)} %get-tuple-element.84), channel_id=1, source_target_pairs={{0,1},{1,0},{2,3},{3,2},{4,5},{5,4},{6,7},{7,6},{8,9},{9,8},{10,11... | collective-permute-start | bytes 49160 | tf_op jit(solution)/shard_map/ppermute | solution.py:42
  68.1 5.0 %collective-permute-start.7 = (f32[32,1,128]{2,1,0:T(1,128)S(1)}, f32[32,1,128]{2,1,0:T(1,128)S(1)}, u32[]{:S(2)}, u32[]{:S(2)}) collective-permute-start(f32[32,1,128]{2,1,0:T(1,128)S(1)} %get-tuple-element.85), channel_id=1, source_target_pairs={{1,2},{2,1},{3,0},{0,3},{5,6},{6,5},{7,4},{4,7},{9,10},{10,9},{11,... | collective-permute-start | bytes 49160 | tf_op jit(solution)/shard_map/ppermute | solution.py:51
  69.7 3.4 %collective-permute-start.4 = (f32[1,64,128]{2,1,0:T(8,128)S(1)}, f32[1,64,128]{2,1,0:T(8,128)S(1)}, u32[]{:S(2)}, u32[]{:S(2)}) collective-permute-start(f32[1,64,128]{2,1,0:T(8,128)S(1)} %get-tuple-element.82), channel_id=1, source_target_pairs={{0,4},{4,0},{8,12},{12,8},{1,5},{5,1},{9,13},{13,9},{2,6},{6,2},{1... | collective-permute-start | bytes 98312 | tf_op jit(solution)/shard_map/ppermute | solution.py:42
  70.7 5.2 %collective-permute-start.5 = (f32[1,64,128]{2,1,0:T(8,128)S(1)}, f32[1,64,128]{2,1,0:T(8,128)S(1)}, u32[]{:S(2)}, u32[]{:S(2)}) collective-permute-start(f32[1,64,128]{2,1,0:T(8,128)S(1)} %get-tuple-element.83), channel_id=1, source_target_pairs={{4,8},{8,4},{5,9},{9,5},{6,10},{10,6},{7,11},{11,7},{20,24},{24,20... | collective-permute-start | bytes 98312 | tf_op jit(solution)/shard_map/ppermute | solution.py:51

commit v18 on v15

--- a/solution.py
+++ b/solution.py
@@ -168,6 +168,20 @@
     k_shape = [1] * advected.ndim
     k_shape[row_dim] = rows
     return advected + diffusivity.reshape(k_shape) * laplace
+
+
+def levels_cols(values, weight_z):
+    value_count = values.shape[-1]
+    per_level = value_count // LEV
+    blocks = [values[..., m * per_level : (m + 1) * per_level] for m in range(LEV)]
+    out = []
+    for level in range(LEV):
+        acc = None
+        for m in tap_sources(level, LEV):
+            term = weight_z[..., level, m][..., None] * blocks[m]
+            acc = term if acc is None else acc + term
+        out.append(acc)
+    return jnp.concatenate(out, axis=-1)
 
 
 def diffuse_first(advected, diffusivity):
@@ -282,6 +296,7 @@
     mix_part = jnp.einsum(
         "plm,pmt->lmt", weight_z, weighted, precision=lax.Precision.HIGHEST
     )
+    field_planar = from_patches(planar, band_rows, band_cols)
     partial = jnp.concatenate([target_part, first_part, mix_part.reshape(-1)])
     members = lat_count * lax.axis_size("lon")
     totals = jnp.sum(
@@ -298,9 +313,10 @@
         value_count
     )
     second_ratio = target / second_mass
-    advected = from_patches(
-        levels(planar * first_ratio[None, None, :], frac[2]), band_rows, band_cols
-    )
+    advected = levels_cols(
+        (field_planar * first_ratio).reshape(band_rows, 8, band_cols, 8, value_count),
+        weight_z.reshape(band_rows, 1, band_cols, 1, LEV, LEV),
+    ).reshape(row_count, col_count, value_count)
     return diffuse(advected, diffusivity, 0) * second_ratio[None, None, :]
 
 

time: 77.1 us -> 76.9 us (level)
  waiting for transfers between devices: 19.4 us -> 18.2 us
  local copies, waits for them, and re-layouts: 10 us -> 11.1 us
    add x0 -> x2, other arithmetic: none -> 2.44 us  [levels_cols(): acc = term if acc is None else acc + term]
    add x4 -> x2, other arithmetic: 4.85 us -> 2.42 us  [levels(): acc = term if acc is None else acc + term]
    all_to_all x2, waiting for transfers between devices: 6.97 us -> 5.81 us  [departed(): lax.all_to_all(outgoing, 'lat', 0, 0, tiled=True)]
    slice x0 -> x2, local copies, waits for them, and re-layouts: none -> 1.11 us  [local(): weight_z = cubic_matrix(frac[2], LEV)]
    concatenate x0 -> x1, other arithmetic: none -> 0.88 us  [levels_cols(): return jnp.concatenate(out, axis=-1)]
    concatenate x2 -> x1, other arithmetic: 1.76 us -> 0.88 us  [levels(): return jnp.concatenate(out, axis=2)]
  transfers between devices with their start and end apart: 11 -> 11, of which waited for: 5 -> 5; matrix products, arithmetic and copies ran while one was open for 10% -> 11% of each run, Pallas kernels for 0% -> 0%
where the time goes in v18:
time: 76.9 us; the launch traced here: 76.5 us
  starting transfers between devices  25 us (33%)
  waiting for transfers between devices  18.2 us (24%)
  other arithmetic  13.9 us (18%)
  local copies, waits for them, and re-layouts  11.1 us (14%)
  matrix products  7.72 us (10%)
    all_to_all x2, starting transfers between devices, departed(): lax.all_to_all(outgoing, 'lat', 0, 0, tiled=True)  8.04 us
    ppermute x4, starting transfers between devices, neighbour_halos(): second = lax.ppermute(jnp.where(even, lo_edge, hi_edge), axis, pairs)  7.68 us
    all_to_all x1, waiting for transfers between devices, local(): lax.all_to_all(jnp.broadcast_to(partial, (members,) + partial.shape), ('l...  6.31 us
    ppermute x4, waiting for transfers between devices, neighbour_halos(): second = lax.ppermute(jnp.where(even, lo_edge, hi_edge), axis, pairs)  6.09 us
    all_to_all x2, waiting for transfers between devices, departed(): lax.all_to_all(outgoing, 'lat', 0, 0, tiled=True)  5.81 us
    ppermute x4, starting transfers between devices, neighbour_halos(): lax.ppermute(jnp.where(even, hi_edge, lo_edge), axis, [(i, i ^ 1) for i i...  4.81 us
    all_to_all x1, starting transfers between devices, local(): lax.all_to_all(jnp.broadcast_to(partial, (members,) + partial.shape), ('l...  4.45 us
    dot_general x2, matrix products, spatial(): jnp.einsum('nij,njv->niv', plane_weights(fraction_y, fraction_x), patches...  3.69 us
  transfers between devices with their start and end apart: 11, of which 5 were waited for; matrix products, arithmetic and copies ran while one was open for 11% of the time, Pallas kernels for 0%

profile of v18, /device:TPU:1, one launch (start us, length us, event | category | flops | bytes accessed | tf_op | source)
XLA Modules:
  0.0 76.5 jit_solution(2655650772275585338)
XLA Ops:
  0.0 1.4 %copy.31 = f32[4,8,8,8,128]{4,3,2,1,0:T(8,128)S(1)} copy(f32[4,8,8,8,128]{4,3,1,2,0:T(8,128)} %bitcast.197) | data formatting | bytes 2097152 | tf_op jit(solution)/shard_map/transpose | solution.py:131
  2.4 1.4 %gather_fusion = f32[16,64,128]{2,1,0:T(8,128)} fusion(f32[32,64,128]{2,1,0:T(8,128)S(1)} %bitcast.187, s32[1024]{0:T(1024)S(1)} %pad_clamp_fusion.1), kind=kCustom, calls=%fused_computation | custom fusion | bytes 1048640 | tf_op jit(solution)/shard_map/gather | solution.py:241
  3.8 4.4 %all-to-all-start = ((f32[4,4,64,128]{3,2,1,0:T(8,128)}), f32[4,4,64,128]{3,2,1,0:T(8,128)S(1)}, u32[]{:S(2)}, u32[]{:S(2)}) async-start(f32[4,4,64,128]{3,2,1,0:T(8,128)} %bitcast.17), calls=%async_computation | async-start | bytes 1048576 | tf_op jit(solution)/shard_map/all_to_all | solution.py:247
  13.5 2.5 %all-to-all-done = f32[4,4,64,128]{3,2,1,0:T(8,128)S(1)} async-done(((f32[4,4,64,128]{3,2,1,0:T(8,128)}), f32[4,4,64,128]{3,2,1,0:T(8,128)S(1)}, u32[]{:S(2)}, u32[]{:S(2)}) %all-to-all-start) | async-done | bytes 524320 | tf_op jit(solution)/shard_map/all_to_all | solution.py:247
  16.0 0.8 %fusion = f32[4,8,64,128]{3,1,2,0:T(8,128)S(1)} fusion(f32[32,8192]{1,0:T(8,128)S(1)} %fusion.108, f32[2,8,64,128]{3,2,1,0:T(8,128)S(1)} %bitcast.199, s32[32]{0:T(128)S(1)} %fusion.167, pred[32]{0:T(512)(128)(4,1)S(1)} %get-tuple-element.29), kind=kOutput, calls=%fused_computation.4 | convolution fusion | flops 50594816 | bytes 2621600 | tf_op jit(solution)/shard_map/dot_general | solution.py:259
  17.0 1.8 %fusion.15 = f32[32,64,128]{2,1,0:T(8,128)S(1)} fusion(f32[32,64,128]{2,1,0:T(8,128)S(1)} %bitcast.202, f32[32]{0:T(128)S(1)} %get-tuple-element.124, f32[32]{0:T(128)S(1)} %get-tuple-element.125, f32[32]{0:T(128)S(1)} %get-tuple-element.123, f32[32]{0:T(128)S(1)} %get-tuple-element.88, f32[32]{0:T(128)S(1)} %get-tuple-element.121, ...), kind=kOutput, calls=%fused_computation.41 | convolution fusion | flops 203292672 | bytes 2229248 | tf_op jit(solution)/shard_map/nij,njv->niv/dot_general | solution.py:103
  18.9 1.1 %multiply_add_fusion.6 = f32[32,64,32]{2,1,0:T(8,128)S(1)} fusion(f32[32,64,128]{2,1,0:T(8,128)S(1)} %fusion.15, f32[32]{0:T(128)S(1)} %get-tuple-element.78, f32[32]{0:T(128)S(1)} %get-tuple-element.79, f32[32]{0:T(128)S(1)} %get-tuple-element.80, f32[32]{0:T(128)S(1)} %get-tuple-element.81), kind=kLoop, calls=%fused_computation.39 | loop fusion | flops 458752 | bytes 1311232 | tf_op jit(solution)/shard_map/add | solution.py:121
  20.0 1.3 %multiply_add_fusion.7 = (f32[32,64,32]{2,1,0:T(8,128)S(1)}, f32[32,64,32]{2,1,0:T(8,128)S(1)}, f32[32,64,32]{2,1,0:T(8,128)S(1)}) fusion(f32[32,64,128]{2,1,0:T(8,128)S(1)} %fusion.15, f32[32]{0:T(128)S(1)} %get-tuple-element.82, f32[32]{0:T(128)S(1)} %get-tuple-element.83, f32[32]{0:T(128)S(1)} %get-tuple-element.72, f32[32]{0:T(128)S(1)} %get-tuple-element.75, ...), kind=kLoop, calls=%fused_computation.40 | loop fusion | flops 851968 | bytes 1836032 | tf_op jit(solution)/shard_map/add | solution.py:121
  21.3 0.9 %pad_maximum_fusion.8 = f32[32,64,128]{2,1,0:T(8,128)S(1)} fusion(f32[32,64,32]{2,1,0:T(8,128)S(1)} %get-tuple-element.43, f32[32,64,32]{2,1,0:T(8,128)S(1)} %get-tuple-element.42, f32[32,64,32]{2,1,0:T(8,128)S(1)} %multiply_add_fusion.6, f32[32,64,32]{2,1,0:T(8,128)S(1)} %get-tuple-element.41), kind=kLoop, calls=%fused_computation.28 | loop fusion | flops 786432 | bytes 2097152 | tf_op jit(solution)/shard_map/concatenate | solution.py:123
  22.4 2.2 %collective-permute-start.2 = (f32[32,1,128]{2,1,0:T(1,128)S(1)}, f32[32,1,128]{2,1,0:T(1,128)S(1)}, u32[]{:S(2)}, u32[]{:S(2)}) collective-permute-start(f32[32,1,128]{2,1,0:T(1,128)S(1)} %get-tuple-element.39), channel_id=1, source_target_pairs={{0,1},{1,0},{2,3},{3,2},{4,5},{5,4},{6,7},{7,6},{8,9},{9,8},{10,11... | collective-permute-start | bytes 49160 | tf_op jit(solution)/shard_map/ppermute | solution.py:42
  24.6 2.2 %collective-permute-start.3 = (f32[32,1,128]{2,1,0:T(1,128)S(1)}, f32[32,1,128]{2,1,0:T(1,128)S(1)}, u32[]{:S(2)}, u32[]{:S(2)}) collective-permute-start(f32[32,1,128]{2,1,0:T(1,128)S(1)} %get-tuple-element.40), channel_id=1, source_target_pairs={{1,2},{2,1},{3,0},{0,3},{5,6},{6,5},{7,4},{4,7},{9,10},{10,9},{11,... | collective-permute-start | bytes 49160 | tf_op jit(solution)/shard_map/ppermute | solution.py:51
  26.8 1.2 %pad_select_fusion.1 = (f32[1,65,128]{2,1,0:T(8,128)S(1)}, f32[1,65,128]{2,1,0:T(8,128)S(1)}) fusion(f32[1,64,128]{2,1,0:T(8,128)S(1)} %get-tuple-element.38, f32[]{:T(128)} %bitcast.33, f32[1,64,128]{2,1,0:T(8,128)S(1)} %get-tuple-element.37, f32[]{:T(128)} %bitcast.32, pred[]{:T(512)S(6)} %eq.420), kind=kLoop, calls=%fused_computation.141 | loop fusion | flops 16640 | bytes 132105 | tf_op jit(solution)/shard_map/jit(_where)/select_n | solution.py:43
  28.1 1.5 %collective-permute-start = (f32[1,65,128]{2,1,0:T(8,128)S(1)}, f32[1,65,128]{2,1,0:T(8,128)S(1)}, u32[]{:S(2)}, u32[]{:S(2)}) collective-permute-start(f32[1,65,128]{2,1,0:T(8,128)S(1)} %get-tuple-element.48), channel_id=1, source_target_pairs={{0,4},{4,0},{8,12},{12,8},{1,5},{5,1},{9,13},{13,9},{2,6},{6,2},{1... | collective-permute-start | bytes 99848 | tf_op jit(solution)/shard_map/ppermute | solution.py:42
  29.6 1.9 %collective-permute-start.1 = (f32[1,65,128]{2,1,0:T(8,128)S(1)}, f32[1,65,128]{2,1,0:T(8,128)S(1)}, u32[]{:S(2)}, u32[]{:S(2)}) collective-permute-start(f32[1,65,128]{2,1,0:T(8,128)S(1)} %get-tuple-element.49), channel_id=1, source_target_pairs={{4,8},{8,4},{5,9},{9,5},{6,10},{10,6},{7,11},{11,7},{20,24},{24,20... | collective-permute-start | bytes 99848 | tf_op jit(solution)/shard_map/ppermute | solution.py:51
  31.5 3.3 %collective-permute-done.1 = f32[1,65,128]{2,1,0:T(8,128)S(1)} collective-permute-done((f32[1,65,128]{2,1,0:T(8,128)S(1)}, f32[1,65,128]{2,1,0:T(8,128)S(1)}, u32[]{:S(2)}, u32[]{:S(2)}) %collective-permute-start.1) | collective-permute-done | bytes 33312 | tf_op jit(solution)/shard_map/ppermute | solution.py:51
  37.0 1.4 %gather_fusion.1 = f32[16,64,128]{2,1,0:T(8,128)} fusion(f32[32,64,128]{2,1,0:T(8,128)S(1)} %bitcast.188, s32[1024]{0:T(1024)S(1)} %pad_clamp_fusion), kind=kCustom, calls=%fused_computation.1 | custom fusion | bytes 1048640 | tf_op jit(solution)/shard_map/gather | solution.py:241
  38.4 3.6 %all-to-all-start.1 = ((f32[4,4,64,128]{3,2,1,0:T(8,128)}), f32[4,4,64,128]{3,2,1,0:T(8,128)S(1)}, u32[]{:S(2)}, u32[]{:S(2)}) async-start(f32[4,4,64,128]{3,2,1,0:T(8,128)} %bitcast.40), calls=%async_computation.1 | async-start | bytes 1048576 | tf_op jit(solution)/shard_map/all_to_all | solution.py:247
  42.1 1.3 %maximum_multiply_fusion = f32[34]{0:T(128)S(1)} fusion(f32[1]{0:T(128)} %bitcast.43, f32[32]{0:T(128)S(1)} %copy-done.3, f32[1]{0:T(128)} %bitcast.42, s32[]{:T(128)S(6)} %sub.188), kind=kLoop, calls=%fused_computation.322 | loop fusion | flops 272 | bytes 276 | tf_op jit(solution)/shard_map/mul | solution.py:290
  44.6 3.3 %all-to-all-done.1 = f32[4,4,64,128]{3,2,1,0:T(8,128)S(1)} async-done(((f32[4,4,64,128]{3,2,1,0:T(8,128)}), f32[4,4,64,128]{3,2,1,0:T(8,128)S(1)}, u32[]{:S(2)}, u32[]{:S(2)}) %all-to-all-start.1) | async-done | bytes 524320 | tf_op jit(solution)/shard_map/all_to_all | solution.py:247
  47.9 0.8 %fusion.1 = f32[4,8,64,128]{3,1,2,0:T(8,128)S(1)} fusion(f32[32,8192]{1,0:T(8,128)S(1)} %fusion.105, f32[2,8,64,128]{3,2,1,0:T(8,128)S(1)} %bitcast.200, s32[32]{0:T(128)S(1)} %fusion.166, pred[32]{0:T(512)(128)(4,1)S(1)} %get-tuple-element.18), kind=kOutput, calls=%fused_computation.5 | convolution fusion | flops 50594816 | bytes 2621600 | tf_op jit(solution)/shard_map/dot_general | solution.py:259
  48.9 1.8 %fusion.31 = f32[32,64,128]{2,1,0:T(8,128)S(1)} fusion(f32[32,64,128]{2,1,0:T(8,128)S(1)} %bitcast.201, f32[64,64]{1,0:T(8,128)S(1)} %get-tuple-element.99, f32[32]{0:T(128)S(1)} %get-tuple-element.113, f32[64,64]{1,0:T(8,128)S(1)} %get-tuple-element.100, f32[32]{0:T(128)S(1)} %get-tuple-element.114, f32[64,64]{1,0:T(8,128)S(1)} %get-tuple-element.101, ...), kind=kOutput, calls=%fused_computation.57 | convolution fusion | flops 203292672 | bytes 2229248 | tf_op jit(solution)/shard_map/nij,njv->niv/dot_general | solution.py:103
  50.8 1.0 %fusion.183 = f32[32,1,128]{2,1,0:T(1,128)S(1)} fusion(f32[32,64,1]{1,2,0:T(1,128)S(1)} %bitcast.203, f32[32,64,128]{2,1,0:T(8,128)S(1)} %fusion.31), kind=kOutput, calls=%fused_computation.386 | convolution fusion | flops 3145728 | bytes 1073152 | tf_op jit(solution)/shard_map/pi,piv->pv/dot_general | solution.py:293
  52.8 4.5 %all-to-all-start.2 = ((f32[16,1,768]{2,1,0:T(1,128)}), f32[16,1,768]{2,1,0:T(1,128)S(1)}, u32[]{:S(2)}, u32[]{:S(2)}) async-start(f32[16,1,768]{2,1,0:T(1,128)} %broadcast_in_dim.35), calls=%async_computation.2 | async-start | bytes 98304 | tf_op jit(solution)/shard_map/all_to_all | solution.py:303
  57.3 6.3 %all-to-all-done.2 = f32[16,1,768]{2,1,0:T(1,128)S(1)} async-done(((f32[16,1,768]{2,1,0:T(1,128)}), f32[16,1,768]{2,1,0:T(1,128)S(1)}, u32[]{:S(2)}, u32[]{:S(2)}) %all-to-all-start.2) | async-done | bytes 49184 | tf_op jit(solution)/shard_map/all_to_all | solution.py:303
  63.7 1.1 %multiply_add_fusion.2 = f32[4,8,8,8,32]{4,3,1,2,0:T(8,128)S(1)} fusion(f32[4,8,8,8,128]{4,3,1,2,0:T(8,128)S(1)} %multiply_bitcast_fusion, f32[4,8]{1,0:T(4,128)S(1)} %get-tuple-element.60, f32[4,8]{1,0:T(4,128)S(1)} %get-tuple-element.61, f32[4,8]{1,0:T(4,128)S(1)} %get-tuple-element.62, f32[4,8]{1,0:T(4,128)S(1)} %get-tuple-element.63), kind=kLoop, calls=%fused_computation.32 | loop fusion | flops 458752 | bytes 1311232 | tf_op jit(solution)/shard_map/add | solution.py:182
  64.8 1.3 %multiply_add_fusion.3 = (f32[4,8,8,8,32]{4,3,1,2,0:T(8,128)S(1)}, f32[4,8,8,8,32]{4,3,1,2,0:T(8,128)S(1)}, f32[4,8,8,8,32]{4,3,1,2,0:T(8,128)S(1)}) fusion(f32[4,8,8,8,128]{4,3,1,2,0:T(8,128)S(1)} %multiply_bitcast_fusion, f32[4,8]{1,0:T(4,128)S(1)} %get-tuple-element.64, f32[4,8]{1,0:T(4,128)S(1)} %get-tuple-element.65, f32[4,8]{1,0:T(4,128)S(1)} %get-tuple-element.54, ...), kind=kLoop, calls=%fused_computation.33 | loop fusion | flops 851968 | bytes 1836032 | tf_op jit(solution)/shard_map/add | solution.py:182
  66.2 0.9 %pad_maximum_fusion.9 = f32[4,8,8,8,128]{4,3,1,2,0:T(8,128)S(1)} fusion(f32[4,8,8,8,32]{4,3,1,2,0:T(8,128)S(1)} %get-tuple-element.36, f32[4,8,8,8,32]{4,3,1,2,0:T(8,128)S(1)} %get-tuple-element.35, f32[4,8,8,8,32]{4,3,1,2,0:T(8,128)S(1)} %multiply_add_fusion.2, f32[4,8,8,8,32]{4,3,1,2,0:T(8,128)S(1)} %get-tuple-element.34), kind=kLoop, calls=%fused_computation.29 | loop fusion | flops 786432 | bytes 2097152 | tf_op jit(solution)/shard_map/concatenate | solution.py:184
  67.5 1.4 %collective-permute-start.7 = (f32[32,1,128]{2,1,0:T(1,128)S(1)}, f32[32,1,128]{2,1,0:T(1,128)S(1)}, u32[]{:S(2)}, u32[]{:S(2)}) collective-permute-start(f32[32,1,128]{2,1,0:T(1,128)S(1)} %get-tuple-element.33), channel_id=1, source_target_pairs={{1,2},{2,1},{3,0},{0,3},{5,6},{6,5},{7,4},{4,7},{9,10},{10,9},{11,... | collective-permute-start | bytes 49160 | tf_op jit(solution)/shard_map/ppermute | solution.py:51
  68.8 1.0 %collective-permute-start.4 = (f32[1,64,128]{2,1,0:T(8,128)S(1)}, f32[1,64,128]{2,1,0:T(8,128)S(1)}, u32[]{:S(2)}, u32[]{:S(2)}) collective-permute-start(f32[1,64,128]{2,1,0:T(8,128)S(1)} %get-tuple-element.30), channel_id=1, source_target_pairs={{0,4},{4,0},{8,12},{12,8},{1,5},{5,1},{9,13},{13,9},{2,6},{6,2},{1... | collective-permute-start | bytes 98312 | tf_op jit(solution)/shard_map/ppermute | solution.py:42
  69.8 2.2 %collective-permute-start.5 = (f32[1,64,128]{2,1,0:T(8,128)S(1)}, f32[1,64,128]{2,1,0:T(8,128)S(1)}, u32[]{:S(2)}, u32[]{:S(2)}) collective-permute-start(f32[1,64,128]{2,1,0:T(8,128)S(1)} %get-tuple-element.31), channel_id=1, source_target_pairs={{4,8},{8,4},{5,9},{9,5},{6,10},{10,6},{7,11},{11,7},{20,24},{24,20... | collective-permute-start | bytes 98312 | tf_op jit(solution)/shard_map/ppermute | solution.py:51
  72.2 2.8 %collective-permute-done.5 = f32[1,64,128]{2,1,0:T(8,128)S(1)} collective-permute-done((f32[1,64,128]{2,1,0:T(8,128)S(1)}, f32[1,64,128]{2,1,0:T(8,128)S(1)}, u32[]{:S(2)}, u32[]{:S(2)}) %collective-permute-start.5) | collective-permute-done | bytes 32800 | tf_op jit(solution)/shard_map/ppermute | solution.py:51
  75.0 1.4 %fusion.6 = f32[32,64,128]{2,1,0:T(8,128)} fusion(f32[32,64,128]{2,1,0:T(8,128)S(1)} %bitcast.191, f32[32,1,128]{2,1,0:T(1,128)S(1)} %bitcast.208, f32[32,1,128]{2,1,0:T(1,128)S(1)} %bitcast.207, f32[1,64,128]{2,1,0:T(8,128)S(1)} %get-tuple-element.47, f32[1,64,128]{2,1,0:T(8,128)S(1)} %get-tuple-element.46, f32[128]{0:T(128)S(1)} %slice_divide_fusion.1, ...), kind=kLoop, calls=%fused_computation.12 | loop fusion | flops 3145728 | bytes 2196096 | tf_op jit(solution)/shard_map/mul | solution.py:320
  (119 shorter events, 11.7 us)
Async XLA Ops:
  0.0 1.4 %copy-start.2 = (s32[2,16,32]{2,1,0:T(8,128)S(1)}, s32[2,16,32]{2,1,0:T(8,128)}, u32[]{:S(2)}) copy-start(s32[2,16,32]{2,1,0:T(8,128)} %param.7) | copy-start | bytes 12292
  3.8 4.5 %copy-start.1 = (f32[2,3,16,32]{3,2,1,0:T(8,128)S(1)}, f32[2,3,16,32]{3,2,1,0:T(8,128)}, u32[]{:S(2)}) copy-start(f32[2,3,16,32]{3,2,1,0:T(8,128)} %param.5) | copy-start | bytes 36868
  3.8 12.2 %all-to-all-start = ((f32[4,4,64,128]{3,2,1,0:T(8,128)}), f32[4,4,64,128]{3,2,1,0:T(8,128)S(1)}, u32[]{:S(2)}, u32[]{:S(2)}) async-start(f32[4,4,64,128]{3,2,1,0:T(8,128)} %bitcast.17), calls=%async_computation | async-start | bytes 1048576 | tf_op jit(solution)/shard_map/all_to_all | solution.py:247
  11.6 0.7 copy-start.3
  22.2 13.8 %copy-start = (f32[32,64,128]{2,1,0:T(8,128)S(1)}, f32[32,64,128]{2,1,0:T(8,128)}, u32[]{:S(2)}) copy-start(f32[32,64,128]{2,1,0:T(8,128)} %param.4) | copy-start | bytes 3145732
  22.4 9.1 %collective-permute-start.2 = (f32[32,1,128]{2,1,0:T(1,128)S(1)}, f32[32,1,128]{2,1,0:T(1,128)S(1)}, u32[]{:S(2)}, u32[]{:S(2)}) collective-permute-start(f32[32,1,128]{2,1,0:T(1,128)S(1)} %get-tuple-element.39), channel_id=1, source_target_pairs={{0,1},{1,0},{2,3},{3,2},{4,5},{5,4},{6,7},{7,6},{8,9},{9,8},{10,11... | collective-permute-start | bytes 49160 | tf_op jit(solution)/shard_map/ppermute | solution.py:42
  24.6 6.9 %collective-permute-start.3 = (f32[32,1,128]{2,1,0:T(1,128)S(1)}, f32[32,1,128]{2,1,0:T(1,128)S(1)}, u32[]{:S(2)}, u32[]{:S(2)}) collective-permute-start(f32[32,1,128]{2,1,0:T(1,128)S(1)} %get-tuple-element.40), channel_id=1, source_target_pairs={{1,2},{2,1},{3,0},{0,3},{5,6},{6,5},{7,4},{4,7},{9,10},{10,9},{11,... | collective-permute-start | bytes 49160 | tf_op jit(solution)/shard_map/ppermute | solution.py:51
  28.1 3.5 %collective-permute-start = (f32[1,65,128]{2,1,0:T(8,128)S(1)}, f32[1,65,128]{2,1,0:T(8,128)S(1)}, u32[]{:S(2)}, u32[]{:S(2)}) collective-permute-start(f32[1,65,128]{2,1,0:T(8,128)S(1)} %get-tuple-element.48), channel_id=1, source_target_pairs={{0,4},{4,0},{8,12},{12,8},{1,5},{5,1},{9,13},{13,9},{2,6},{6,2},{1... | collective-permute-start | bytes 99848 | tf_op jit(solution)/shard_map/ppermute | solution.py:42
  29.6 5.3 %collective-permute-start.1 = (f32[1,65,128]{2,1,0:T(8,128)S(1)}, f32[1,65,128]{2,1,0:T(8,128)S(1)}, u32[]{:S(2)}, u32[]{:S(2)}) collective-permute-start(f32[1,65,128]{2,1,0:T(8,128)S(1)} %get-tuple-element.49), channel_id=1, source_target_pairs={{4,8},{8,4},{5,9},{9,5},{6,10},{10,6},{7,11},{11,7},{20,24},{24,20... | collective-permute-start | bytes 99848 | tf_op jit(solution)/shard_map/ppermute | solution.py:51
  38.4 9.5 %all-to-all-start.1 = ((f32[4,4,64,128]{3,2,1,0:T(8,128)}), f32[4,4,64,128]{3,2,1,0:T(8,128)S(1)}, u32[]{:S(2)}, u32[]{:S(2)}) async-start(f32[4,4,64,128]{3,2,1,0:T(8,128)} %bitcast.40), calls=%async_computation.1 | async-start | bytes 1048576 | tf_op jit(solution)/shard_map/all_to_all | solution.py:247
  52.8 10.8 %all-to-all-start.2 = ((f32[16,1,768]{2,1,0:T(1,128)}), f32[16,1,768]{2,1,0:T(1,128)S(1)}, u32[]{:S(2)}, u32[]{:S(2)}) async-start(f32[16,1,768]{2,1,0:T(1,128)} %broadcast_in_dim.35), calls=%async_computation.2 | async-start | bytes 98304 | tf_op jit(solution)/shard_map/all_to_all | solution.py:303
  67.3 4.9 %collective-permute-start.6 = (f32[32,1,128]{2,1,0:T(1,128)S(1)}, f32[32,1,128]{2,1,0:T(1,128)S(1)}, u32[]{:S(2)}, u32[]{:S(2)}) collective-permute-start(f32[32,1,128]{2,1,0:T(1,128)S(1)} %get-tuple-element.32), channel_id=1, source_target_pairs={{0,1},{1,0},{2,3},{3,2},{4,5},{5,4},{6,7},{7,6},{8,9},{9,8},{10,11... | collective-permute-start | bytes 49160 | tf_op jit(solution)/shard_map/ppermute | solution.py:42
  67.5 4.7 %collective-permute-start.7 = (f32[32,1,128]{2,1,0:T(1,128)S(1)}, f32[32,1,128]{2,1,0:T(1,128)S(1)}, u32[]{:S(2)}, u32[]{:S(2)}) collective-permute-start(f32[32,1,128]{2,1,0:T(1,128)S(1)} %get-tuple-element.33), channel_id=1, source_target_pairs={{1,2},{2,1},{3,0},{0,3},{5,6},{6,5},{7,4},{4,7},{9,10},{10,9},{11,... | collective-permute-start | bytes 49160 | tf_op jit(solution)/shard_map/ppermute | solution.py:51
  68.8 3.4 %collective-permute-start.4 = (f32[1,64,128]{2,1,0:T(8,128)S(1)}, f32[1,64,128]{2,1,0:T(8,128)S(1)}, u32[]{:S(2)}, u32[]{:S(2)}) collective-permute-start(f32[1,64,128]{2,1,0:T(8,128)S(1)} %get-tuple-element.30), channel_id=1, source_target_pairs={{0,4},{4,0},{8,12},{12,8},{1,5},{5,1},{9,13},{13,9},{2,6},{6,2},{1... | collective-permute-start | bytes 98312 | tf_op jit(solution)/shard_map/ppermute | solution.py:42
  69.8 5.2 %collective-permute-start.5 = (f32[1,64,128]{2,1,0:T(8,128)S(1)}, f32[1,64,128]{2,1,0:T(8,128)S(1)}, u32[]{:S(2)}, u32[]{:S(2)}) collective-permute-start(f32[1,64,128]{2,1,0:T(8,128)S(1)} %get-tuple-element.31), channel_id=1, source_target_pairs={{4,8},{8,4},{5,9},{9,5},{6,10},{10,6},{7,11},{11,7},{20,24},{24,20... | collective-permute-start | bytes 98312 | tf_op jit(solution)/shard_map/ppermute | solution.py:51

commit v19 on v18

--- a/solution.py
+++ b/solution.py
@@ -283,15 +283,19 @@
     first_part = column_mass(first, weights)
 
     patches, frac = departed(first, source_patch[1], shifts[1])
-    planar = spatial(patches, frac[0], frac[1])
+    plane = plane_weights(frac[0], frac[1])
+    planar = jnp.einsum("nij,njv->niv", plane, patches, precision=lax.Precision.HIGHEST)
     weight_z = cubic_matrix(frac[2], LEV)
 
     area_wide = column_area(lat_index * row_count - 1, row_count + 2, total_rows)
     flux = area_wide * k_wide
     g = weights - 2.0 * flux[1:-1] + flux[:-2] + flux[2:]
     g_cols = jnp.broadcast_to(g.reshape(band_rows, 1, 8, 1), (band_rows, band_cols, 8, 8))
+    row_weights = jnp.einsum(
+        "pi,pij->pj", g_cols.reshape(per_device, 64), plane, precision=lax.Precision.HIGHEST
+    )
     weighted = jnp.einsum(
-        "pi,piv->pv", g_cols.reshape(per_device, 64), planar, precision=lax.Precision.HIGHEST
+        "pj,pjv->pv", row_weights, patches, precision=lax.Precision.HIGHEST
     ).reshape(per_device, LEV, per_level)
     mix_part = jnp.einsum(
         "plm,pmt->lmt", weight_z, weighted, precision=lax.Precision.HIGHEST

time: 76.9 us -> 74.8 us (0.973)
  waiting for transfers between devices: 18.2 us -> 14.6 us
  matrix products: 7.72 us -> 9.28 us
    dot_general x1 -> x3, matrix products: 0.96 us -> 4.36 us  [the longest x1 1.84 us: local(): jnp.einsum('nij,njv->niv', plane, patches, precision=lax.Precision.HIGHEST)]
    dot_general x2 -> x1, matrix products: 3.69 us -> 1.85 us  [spatial(): jnp.einsum('nij,njv->niv', plane_weights(fraction_y, fraction_x), patches...]
    all_to_all x1, waiting for transfers between devices: 6.31 us -> 4.47 us  [local(): lax.all_to_all(jnp.broadcast_to(partial, (members,) + partial.shape), ('l...]
    all_to_all x2, waiting for transfers between devices: 5.81 us -> 4.03 us  [departed(): lax.all_to_all(outgoing, 'lat', 0, 0, tiled=True)]
  transfers between devices with their start and end apart: 11 -> 11, of which waited for: 5 -> 5; matrix products, arithmetic and copies ran while one was open for 11% -> 16% of each run, Pallas kernels for 0% -> 0%
where the time goes in v19:
time: 74.8 us; the launch traced here: 74.4 us
  starting transfers between devices  25 us (33%)
  waiting for transfers between devices  14.6 us (20%)
  other arithmetic  13.9 us (19%)
  local copies, waits for them, and re-layouts  11.1 us (15%)
  matrix products  9.28 us (12%)
    all_to_all x2, starting transfers between devices, departed(): lax.all_to_all(outgoing, 'lat', 0, 0, tiled=True)  8.04 us
    ppermute x4, starting transfers between devices, neighbour_halos(): second = lax.ppermute(jnp.where(even, lo_edge, hi_edge), axis, pairs)  7.68 us
    ppermute x4, waiting for transfers between devices, neighbour_halos(): second = lax.ppermute(jnp.where(even, lo_edge, hi_edge), axis, pairs)  6.09 us
    ppermute x4, starting transfers between devices, neighbour_halos(): lax.ppermute(jnp.where(even, hi_edge, lo_edge), axis, [(i, i ^ 1) for i i...  4.8 us
    all_to_all x1, waiting for transfers between devices, local(): lax.all_to_all(jnp.broadcast_to(partial, (members,) + partial.shape), ('l...  4.47 us
    all_to_all x1, starting transfers between devices, local(): lax.all_to_all(jnp.broadcast_to(partial, (members,) + partial.shape), ('l...  4.46 us
    all_to_all x2, waiting for transfers between devices, departed(): lax.all_to_all(outgoing, 'lat', 0, 0, tiled=True)  4.03 us
    gather x2, local copies, waits for them, and re-layouts, departed(): own_patches[send_local.reshape(-1)].reshape(lat_count, CAP, 64, value_count)  2.75 us
  transfers between devices with their start and end apart: 11, of which 5 were waited for; matrix products, arithmetic and copies ran while one was open for 16% of the time, Pallas kernels for 0%

profile of v19, /device:TPU:1, one launch (start us, length us, event | category | flops | bytes accessed | tf_op | source)
XLA Modules:
  0.0 74.4 jit_solution(3564179147466779741)
XLA Ops:
  0.0 1.4 %copy.31 = f32[4,8,8,8,128]{4,3,2,1,0:T(8,128)S(1)} copy(f32[4,8,8,8,128]{4,3,1,2,0:T(8,128)} %bitcast.205) | data formatting | bytes 2097152 | tf_op jit(solution)/shard_map/transpose | solution.py:131
  2.4 1.4 %gather_fusion = f32[16,64,128]{2,1,0:T(8,128)} fusion(f32[32,64,128]{2,1,0:T(8,128)S(1)} %bitcast.194, s32[1024]{0:T(1024)S(1)} %pad_clamp_fusion.1), kind=kCustom, calls=%fused_computation | custom fusion | bytes 1048640 | tf_op jit(solution)/shard_map/gather | solution.py:241
  3.8 4.4 %all-to-all-start = ((f32[4,4,64,128]{3,2,1,0:T(8,128)}), f32[4,4,64,128]{3,2,1,0:T(8,128)S(1)}, u32[]{:S(2)}, u32[]{:S(2)}) async-start(f32[4,4,64,128]{3,2,1,0:T(8,128)} %bitcast.17), calls=%async_computation | async-start | bytes 1048576 | tf_op jit(solution)/shard_map/all_to_all | solution.py:247
  13.5 2.5 %all-to-all-done = f32[4,4,64,128]{3,2,1,0:T(8,128)S(1)} async-done(((f32[4,4,64,128]{3,2,1,0:T(8,128)}), f32[4,4,64,128]{3,2,1,0:T(8,128)S(1)}, u32[]{:S(2)}, u32[]{:S(2)}) %all-to-all-start) | async-done | bytes 524320 | tf_op jit(solution)/shard_map/all_to_all | solution.py:247
  16.0 0.8 %fusion = f32[4,8,64,128]{3,1,2,0:T(8,128)S(1)} fusion(f32[32,8192]{1,0:T(8,128)S(1)} %fusion.109, f32[2,8,64,128]{3,2,1,0:T(8,128)S(1)} %bitcast.207, s32[32]{0:T(128)S(1)} %fusion.168, pred[32]{0:T(512)(128)(4,1)S(1)} %get-tuple-element.29), kind=kOutput, calls=%fused_computation.4 | convolution fusion | flops 50594816 | bytes 2621600 | tf_op jit(solution)/shard_map/dot_general | solution.py:259
  17.0 1.8 %fusion.15 = f32[32,64,128]{2,1,0:T(8,128)S(1)} fusion(f32[32,64,128]{2,1,0:T(8,128)S(1)} %bitcast.210, f32[32]{0:T(128)S(1)} %get-tuple-element.124, f32[32]{0:T(128)S(1)} %get-tuple-element.125, f32[32]{0:T(128)S(1)} %get-tuple-element.123, f32[32]{0:T(128)S(1)} %get-tuple-element.88, f32[32]{0:T(128)S(1)} %get-tuple-element.121, ...), kind=kOutput, calls=%fused_computation.42 | convolution fusion | flops 203292672 | bytes 2229248 | tf_op jit(solution)/shard_map/nij,njv->niv/dot_general | solution.py:103
  18.9 1.1 %multiply_add_fusion.6 = f32[32,64,32]{2,1,0:T(8,128)S(1)} fusion(f32[32,64,128]{2,1,0:T(8,128)S(1)} %fusion.15, f32[32]{0:T(128)S(1)} %get-tuple-element.78, f32[32]{0:T(128)S(1)} %get-tuple-element.79, f32[32]{0:T(128)S(1)} %get-tuple-element.80, f32[32]{0:T(128)S(1)} %get-tuple-element.81), kind=kLoop, calls=%fused_computation.40 | loop fusion | flops 458752 | bytes 1311232 | tf_op jit(solution)/shard_map/add | solution.py:121
  20.0 1.3 %multiply_add_fusion.7 = (f32[32,64,32]{2,1,0:T(8,128)S(1)}, f32[32,64,32]{2,1,0:T(8,128)S(1)}, f32[32,64,32]{2,1,0:T(8,128)S(1)}) fusion(f32[32,64,128]{2,1,0:T(8,128)S(1)} %fusion.15, f32[32]{0:T(128)S(1)} %get-tuple-element.82, f32[32]{0:T(128)S(1)} %get-tuple-element.83, f32[32]{0:T(128)S(1)} %get-tuple-element.72, f32[32]{0:T(128)S(1)} %get-tuple-element.75, ...), kind=kLoop, calls=%fused_computation.41 | loop fusion | flops 851968 | bytes 1836032 | tf_op jit(solution)/shard_map/add | solution.py:121
  21.3 0.9 %pad_maximum_fusion.8 = f32[32,64,128]{2,1,0:T(8,128)S(1)} fusion(f32[32,64,32]{2,1,0:T(8,128)S(1)} %get-tuple-element.43, f32[32,64,32]{2,1,0:T(8,128)S(1)} %get-tuple-element.42, f32[32,64,32]{2,1,0:T(8,128)S(1)} %multiply_add_fusion.6, f32[32,64,32]{2,1,0:T(8,128)S(1)} %get-tuple-element.41), kind=kLoop, calls=%fused_computation.29 | loop fusion | flops 786432 | bytes 2097152 | tf_op jit(solution)/shard_map/concatenate | solution.py:123
  22.4 2.2 %collective-permute-start.2 = (f32[32,1,128]{2,1,0:T(1,128)S(1)}, f32[32,1,128]{2,1,0:T(1,128)S(1)}, u32[]{:S(2)}, u32[]{:S(2)}) collective-permute-start(f32[32,1,128]{2,1,0:T(1,128)S(1)} %get-tuple-element.39), channel_id=1, source_target_pairs={{0,1},{1,0},{2,3},{3,2},{4,5},{5,4},{6,7},{7,6},{8,9},{9,8},{10,11... | collective-permute-start | bytes 49160 | tf_op jit(solution)/shard_map/ppermute | solution.py:42
  24.6 2.2 %collective-permute-start.3 = (f32[32,1,128]{2,1,0:T(1,128)S(1)}, f32[32,1,128]{2,1,0:T(1,128)S(1)}, u32[]{:S(2)}, u32[]{:S(2)}) collective-permute-start(f32[32,1,128]{2,1,0:T(1,128)S(1)} %get-tuple-element.40), channel_id=1, source_target_pairs={{1,2},{2,1},{3,0},{0,3},{5,6},{6,5},{7,4},{4,7},{9,10},{10,9},{11,... | collective-permute-start | bytes 49160 | tf_op jit(solution)/shard_map/ppermute | solution.py:51
  26.8 1.2 %pad_select_fusion.1 = (f32[1,65,128]{2,1,0:T(8,128)S(1)}, f32[1,65,128]{2,1,0:T(8,128)S(1)}) fusion(f32[1,64,128]{2,1,0:T(8,128)S(1)} %get-tuple-element.38, f32[]{:T(128)} %bitcast.33, f32[1,64,128]{2,1,0:T(8,128)S(1)} %get-tuple-element.37, f32[]{:T(128)} %bitcast.32, pred[]{:T(512)S(6)} %eq.420), kind=kLoop, calls=%fused_computation.144 | loop fusion | flops 16640 | bytes 132105 | tf_op jit(solution)/shard_map/jit(_where)/select_n | solution.py:43
  28.1 1.5 %collective-permute-start = (f32[1,65,128]{2,1,0:T(8,128)S(1)}, f32[1,65,128]{2,1,0:T(8,128)S(1)}, u32[]{:S(2)}, u32[]{:S(2)}) collective-permute-start(f32[1,65,128]{2,1,0:T(8,128)S(1)} %get-tuple-element.48), channel_id=1, source_target_pairs={{0,4},{4,0},{8,12},{12,8},{1,5},{5,1},{9,13},{13,9},{2,6},{6,2},{1... | collective-permute-start | bytes 99848 | tf_op jit(solution)/shard_map/ppermute | solution.py:42
  29.6 1.9 %collective-permute-start.1 = (f32[1,65,128]{2,1,0:T(8,128)S(1)}, f32[1,65,128]{2,1,0:T(8,128)S(1)}, u32[]{:S(2)}, u32[]{:S(2)}) collective-permute-start(f32[1,65,128]{2,1,0:T(8,128)S(1)} %get-tuple-element.49), channel_id=1, source_target_pairs={{4,8},{8,4},{5,9},{9,5},{6,10},{10,6},{7,11},{11,7},{20,24},{24,20... | collective-permute-start | bytes 99848 | tf_op jit(solution)/shard_map/ppermute | solution.py:51
  31.5 3.3 %collective-permute-done.1 = f32[1,65,128]{2,1,0:T(8,128)S(1)} collective-permute-done((f32[1,65,128]{2,1,0:T(8,128)S(1)}, f32[1,65,128]{2,1,0:T(8,128)S(1)}, u32[]{:S(2)}, u32[]{:S(2)}) %collective-permute-start.1) | collective-permute-done | bytes 33312 | tf_op jit(solution)/shard_map/ppermute | solution.py:51
  36.8 1.4 %gather_fusion.1 = f32[16,64,128]{2,1,0:T(8,128)} fusion(f32[32,64,128]{2,1,0:T(8,128)S(1)} %bitcast.195, s32[1024]{0:T(1024)S(1)} %pad_clamp_fusion), kind=kCustom, calls=%fused_computation.1 | custom fusion | bytes 1048640 | tf_op jit(solution)/shard_map/gather | solution.py:241
  38.2 3.6 %all-to-all-start.1 = ((f32[4,4,64,128]{3,2,1,0:T(8,128)}), f32[4,4,64,128]{3,2,1,0:T(8,128)S(1)}, u32[]{:S(2)}, u32[]{:S(2)}) async-start(f32[4,4,64,128]{3,2,1,0:T(8,128)} %bitcast.40), calls=%async_computation.1 | async-start | bytes 1048576 | tf_op jit(solution)/shard_map/all_to_all | solution.py:247
  41.9 1.3 %maximum_multiply_fusion = f32[34]{0:T(128)S(1)} fusion(f32[1]{0:T(128)} %bitcast.43, f32[32]{0:T(128)S(1)} %copy-done.3, f32[1]{0:T(128)} %bitcast.42, s32[]{:T(128)S(6)} %sub.188), kind=kLoop, calls=%fused_computation.325 | loop fusion | flops 272 | bytes 276 | tf_op jit(solution)/shard_map/mul | solution.py:291
  43.8 1.6 %convolution_bitcast_fusion = f32[32,64,1]{1,2,0:T(1,128)S(1)} fusion(f32[32,64,1]{1,2,0:T(1,128)S(1)} %bitcast.216, f32[64,64]{1,0:T(8,128)S(1)} %get-tuple-element.99, f32[32]{0:T(128)S(1)} %get-tuple-element.113, f32[64,64]{1,0:T(8,128)S(1)} %get-tuple-element.100, f32[32]{0:T(128)S(1)} %get-tuple-element.114, f32[64,64]{1,0:T(8,128)S(1)} %get-tuple-element.101, ...), kind=kOutput, calls=%fused_computation.6 | convolution fusion | flops 3538944 | bytes 148480 | tf_op jit(solution)/shard_map/pi,pij->pj/dot_general | solution.py:294
  46.1 1.6 %all-to-all-done.1 = f32[4,4,64,128]{3,2,1,0:T(8,128)S(1)} async-done(((f32[4,4,64,128]{3,2,1,0:T(8,128)}), f32[4,4,64,128]{3,2,1,0:T(8,128)S(1)}, u32[]{:S(2)}, u32[]{:S(2)}) %all-to-all-start.1) | async-done | bytes 524320 | tf_op jit(solution)/shard_map/all_to_all | solution.py:247
  48.7 1.0 %fusion.184 = f32[32,1,128]{2,1,0:T(1,128)S(1)} fusion(f32[32,64,1]{1,2,0:T(1,128)S(1)} %convolution_bitcast_fusion, f32[32,64,128]{2,1,0:T(8,128)S(1)} %bitcast.203), kind=kOutput, calls=%fused_computation.389 | convolution fusion | flops 3145728 | bytes 1073152 | tf_op jit(solution)/shard_map/pj,pjv->pv/dot_general | solution.py:297
  50.7 4.5 %all-to-all-start.2 = ((f32[16,1,768]{2,1,0:T(1,128)}), f32[16,1,768]{2,1,0:T(1,128)S(1)}, u32[]{:S(2)}, u32[]{:S(2)}) async-start(f32[16,1,768]{2,1,0:T(1,128)} %broadcast_in_dim.35), calls=%async_computation.2 | async-start | bytes 98304 | tf_op jit(solution)/shard_map/all_to_all | solution.py:307
  55.2 1.8 %fusion.31 = f32[32,64,128]{2,1,0:T(8,128)S(1)} fusion(f32[32,64,128]{2,1,0:T(8,128)S(1)} %bitcast.204, f32[64,64]{1,0:T(8,128)S(1)} %get-tuple-element.99, f32[32]{0:T(128)S(1)} %get-tuple-element.113, f32[64,64]{1,0:T(8,128)S(1)} %get-tuple-element.100, f32[32]{0:T(128)S(1)} %get-tuple-element.114, f32[64,64]{1,0:T(8,128)S(1)} %get-tuple-element.101, ...), kind=kOutput, calls=%fused_computation.59 | convolution fusion | flops 203292672 | bytes 2229248 | tf_op jit(solution)/shard_map/nij,njv->niv/dot_general | solution.py:287
  57.0 4.5 %all-to-all-done.2 = f32[16,1,768]{2,1,0:T(1,128)S(1)} async-done(((f32[16,1,768]{2,1,0:T(1,128)}), f32[16,1,768]{2,1,0:T(1,128)S(1)}, u32[]{:S(2)}, u32[]{:S(2)}) %all-to-all-start.2) | async-done | bytes 49184 | tf_op jit(solution)/shard_map/all_to_all | solution.py:307
  61.7 1.1 %multiply_add_fusion.2 = f32[4,8,8,8,32]{4,3,1,2,0:T(8,128)S(1)} fusion(f32[4,8,8,8,128]{4,3,1,2,0:T(8,128)S(1)} %multiply_bitcast_fusion, f32[4,8]{1,0:T(4,128)S(1)} %get-tuple-element.60, f32[4,8]{1,0:T(4,128)S(1)} %get-tuple-element.61, f32[4,8]{1,0:T(4,128)S(1)} %get-tuple-element.62, f32[4,8]{1,0:T(4,128)S(1)} %get-tuple-element.63), kind=kLoop, calls=%fused_computation.33 | loop fusion | flops 458752 | bytes 1311232 | tf_op jit(solution)/shard_map/add | solution.py:182
  62.8 1.3 %multiply_add_fusion.3 = (f32[4,8,8,8,32]{4,3,1,2,0:T(8,128)S(1)}, f32[4,8,8,8,32]{4,3,1,2,0:T(8,128)S(1)}, f32[4,8,8,8,32]{4,3,1,2,0:T(8,128)S(1)}) fusion(f32[4,8,8,8,128]{4,3,1,2,0:T(8,128)S(1)} %multiply_bitcast_fusion, f32[4,8]{1,0:T(4,128)S(1)} %get-tuple-element.64, f32[4,8]{1,0:T(4,128)S(1)} %get-tuple-element.65, f32[4,8]{1,0:T(4,128)S(1)} %get-tuple-element.54, ...), kind=kLoop, calls=%fused_computation.34 | loop fusion | flops 851968 | bytes 1836032 | tf_op jit(solution)/shard_map/add | solution.py:182
  64.1 0.9 %pad_maximum_fusion.9 = f32[4,8,8,8,128]{4,3,1,2,0:T(8,128)S(1)} fusion(f32[4,8,8,8,32]{4,3,1,2,0:T(8,128)S(1)} %get-tuple-element.36, f32[4,8,8,8,32]{4,3,1,2,0:T(8,128)S(1)} %get-tuple-element.35, f32[4,8,8,8,32]{4,3,1,2,0:T(8,128)S(1)} %multiply_add_fusion.2, f32[4,8,8,8,32]{4,3,1,2,0:T(8,128)S(1)} %get-tuple-element.34), kind=kLoop, calls=%fused_computation.30 | loop fusion | flops 786432 | bytes 2097152 | tf_op jit(solution)/shard_map/concatenate | solution.py:184
  65.4 1.4 %collective-permute-start.7 = (f32[32,1,128]{2,1,0:T(1,128)S(1)}, f32[32,1,128]{2,1,0:T(1,128)S(1)}, u32[]{:S(2)}, u32[]{:S(2)}) collective-permute-start(f32[32,1,128]{2,1,0:T(1,128)S(1)} %get-tuple-element.33), channel_id=1, source_target_pairs={{1,2},{2,1},{3,0},{0,3},{5,6},{6,5},{7,4},{4,7},{9,10},{10,9},{11,... | collective-permute-start | bytes 49160 | tf_op jit(solution)/shard_map/ppermute | solution.py:51
  66.8 1.0 %collective-permute-start.4 = (f32[1,64,128]{2,1,0:T(8,128)S(1)}, f32[1,64,128]{2,1,0:T(8,128)S(1)}, u32[]{:S(2)}, u32[]{:S(2)}) collective-permute-start(f32[1,64,128]{2,1,0:T(8,128)S(1)} %get-tuple-element.30), channel_id=1, source_target_pairs={{0,4},{4,0},{8,12},{12,8},{1,5},{5,1},{9,13},{13,9},{2,6},{6,2},{1... | collective-permute-start | bytes 98312 | tf_op jit(solution)/shard_map/ppermute | solution.py:42
  67.7 2.2 %collective-permute-start.5 = (f32[1,64,128]{2,1,0:T(8,128)S(1)}, f32[1,64,128]{2,1,0:T(8,128)S(1)}, u32[]{:S(2)}, u32[]{:S(2)}) collective-permute-start(f32[1,64,128]{2,1,0:T(8,128)S(1)} %get-tuple-element.31), channel_id=1, source_target_pairs={{4,8},{8,4},{5,9},{9,5},{6,10},{10,6},{7,11},{11,7},{20,24},{24,20... | collective-permute-start | bytes 98312 | tf_op jit(solution)/shard_map/ppermute | solution.py:51
  70.2 2.8 %collective-permute-done.5 = f32[1,64,128]{2,1,0:T(8,128)S(1)} collective-permute-done((f32[1,64,128]{2,1,0:T(8,128)S(1)}, f32[1,64,128]{2,1,0:T(8,128)S(1)}, u32[]{:S(2)}, u32[]{:S(2)}) %collective-permute-start.5) | collective-permute-done | bytes 32800 | tf_op jit(solution)/shard_map/ppermute | solution.py:51
  73.0 1.4 %fusion.6 = f32[32,64,128]{2,1,0:T(8,128)} fusion(f32[32,64,128]{2,1,0:T(8,128)S(1)} %bitcast.198, f32[32,1,128]{2,1,0:T(1,128)S(1)} %bitcast.215, f32[32,1,128]{2,1,0:T(1,128)S(1)} %bitcast.214, f32[1,64,128]{2,1,0:T(8,128)S(1)} %get-tuple-element.47, f32[1,64,128]{2,1,0:T(8,128)S(1)} %get-tuple-element.46, f32[128]{0:T(128)S(1)} %slice_divide_fusion.1, ...), kind=kLoop, calls=%fused_computation.13 | loop fusion | flops 3145728 | bytes 2196096 | tf_op jit(solution)/shard_map/mul | solution.py:324
  (120 shorter events, 12.6 us)
Async XLA Ops:
  0.0 1.4 %copy-start.2 = (s32[2,16,32]{2,1,0:T(8,128)S(1)}, s32[2,16,32]{2,1,0:T(8,128)}, u32[]{:S(2)}) copy-start(s32[2,16,32]{2,1,0:T(8,128)} %param.7) | copy-start | bytes 12292
  3.8 4.5 %copy-start.1 = (f32[2,3,16,32]{3,2,1,0:T(8,128)S(1)}, f32[2,3,16,32]{3,2,1,0:T(8,128)}, u32[]{:S(2)}) copy-start(f32[2,3,16,32]{3,2,1,0:T(8,128)} %param.5) | copy-start | bytes 36868
  3.8 12.2 %all-to-all-start = ((f32[4,4,64,128]{3,2,1,0:T(8,128)}), f32[4,4,64,128]{3,2,1,0:T(8,128)S(1)}, u32[]{:S(2)}, u32[]{:S(2)}) async-start(f32[4,4,64,128]{3,2,1,0:T(8,128)} %bitcast.17), calls=%async_computation | async-start | bytes 1048576 | tf_op jit(solution)/shard_map/all_to_all | solution.py:247
  11.6 0.7 copy-start.3
  22.2 13.8 %copy-start = (f32[32,64,128]{2,1,0:T(8,128)S(1)}, f32[32,64,128]{2,1,0:T(8,128)}, u32[]{:S(2)}) copy-start(f32[32,64,128]{2,1,0:T(8,128)} %param.4) | copy-start | bytes 3145732
  22.4 9.1 %collective-permute-start.2 = (f32[32,1,128]{2,1,0:T(1,128)S(1)}, f32[32,1,128]{2,1,0:T(1,128)S(1)}, u32[]{:S(2)}, u32[]{:S(2)}) collective-permute-start(f32[32,1,128]{2,1,0:T(1,128)S(1)} %get-tuple-element.39), channel_id=1, source_target_pairs={{0,1},{1,0},{2,3},{3,2},{4,5},{5,4},{6,7},{7,6},{8,9},{9,8},{10,11... | collective-permute-start | bytes 49160 | tf_op jit(solution)/shard_map/ppermute | solution.py:42
  24.6 6.9 %collective-permute-start.3 = (f32[32,1,128]{2,1,0:T(1,128)S(1)}, f32[32,1,128]{2,1,0:T(1,128)S(1)}, u32[]{:S(2)}, u32[]{:S(2)}) collective-permute-start(f32[32,1,128]{2,1,0:T(1,128)S(1)} %get-tuple-element.40), channel_id=1, source_target_pairs={{1,2},{2,1},{3,0},{0,3},{5,6},{6,5},{7,4},{4,7},{9,10},{10,9},{11,... | collective-permute-start | bytes 49160 | tf_op jit(solution)/shard_map/ppermute | solution.py:51
  28.1 3.5 %collective-permute-start = (f32[1,65,128]{2,1,0:T(8,128)S(1)}, f32[1,65,128]{2,1,0:T(8,128)S(1)}, u32[]{:S(2)}, u32[]{:S(2)}) collective-permute-start(f32[1,65,128]{2,1,0:T(8,128)S(1)} %get-tuple-element.48), channel_id=1, source_target_pairs={{0,4},{4,0},{8,12},{12,8},{1,5},{5,1},{9,13},{13,9},{2,6},{6,2},{1... | collective-permute-start | bytes 99848 | tf_op jit(solution)/shard_map/ppermute | solution.py:42
  29.6 5.3 %collective-permute-start.1 = (f32[1,65,128]{2,1,0:T(8,128)S(1)}, f32[1,65,128]{2,1,0:T(8,128)S(1)}, u32[]{:S(2)}, u32[]{:S(2)}) collective-permute-start(f32[1,65,128]{2,1,0:T(8,128)S(1)} %get-tuple-element.49), channel_id=1, source_target_pairs={{4,8},{8,4},{5,9},{9,5},{6,10},{10,6},{7,11},{11,7},{20,24},{24,20... | collective-permute-start | bytes 99848 | tf_op jit(solution)/shard_map/ppermute | solution.py:51
  38.2 9.5 %all-to-all-start.1 = ((f32[4,4,64,128]{3,2,1,0:T(8,128)}), f32[4,4,64,128]{3,2,1,0:T(8,128)S(1)}, u32[]{:S(2)}, u32[]{:S(2)}) async-start(f32[4,4,64,128]{3,2,1,0:T(8,128)} %bitcast.40), calls=%async_computation.1 | async-start | bytes 1048576 | tf_op jit(solution)/shard_map/all_to_all | solution.py:247
  50.7 10.8 %all-to-all-start.2 = ((f32[16,1,768]{2,1,0:T(1,128)}), f32[16,1,768]{2,1,0:T(1,128)S(1)}, u32[]{:S(2)}, u32[]{:S(2)}) async-start(f32[16,1,768]{2,1,0:T(1,128)} %broadcast_in_dim.35), calls=%async_computation.2 | async-start | bytes 98304 | tf_op jit(solution)/shard_map/all_to_all | solution.py:307
  65.3 4.9 %collective-permute-start.6 = (f32[32,1,128]{2,1,0:T(1,128)S(1)}, f32[32,1,128]{2,1,0:T(1,128)S(1)}, u32[]{:S(2)}, u32[]{:S(2)}) collective-permute-start(f32[32,1,128]{2,1,0:T(1,128)S(1)} %get-tuple-element.32), channel_id=1, source_target_pairs={{0,1},{1,0},{2,3},{3,2},{4,5},{5,4},{6,7},{7,6},{8,9},{9,8},{10,11... | collective-permute-start | bytes 49160 | tf_op jit(solution)/shard_map/ppermute | solution.py:42
  65.4 4.7 %collective-permute-start.7 = (f32[32,1,128]{2,1,0:T(1,128)S(1)}, f32[32,1,128]{2,1,0:T(1,128)S(1)}, u32[]{:S(2)}, u32[]{:S(2)}) collective-permute-start(f32[32,1,128]{2,1,0:T(1,128)S(1)} %get-tuple-element.33), channel_id=1, source_target_pairs={{1,2},{2,1},{3,0},{0,3},{5,6},{6,5},{7,4},{4,7},{9,10},{10,9},{11,... | collective-permute-start | bytes 49160 | tf_op jit(solution)/shard_map/ppermute | solution.py:51
  66.8 3.4 %collective-permute-start.4 = (f32[1,64,128]{2,1,0:T(8,128)S(1)}, f32[1,64,128]{2,1,0:T(8,128)S(1)}, u32[]{:S(2)}, u32[]{:S(2)}) collective-permute-start(f32[1,64,128]{2,1,0:T(8,128)S(1)} %get-tuple-element.30), channel_id=1, source_target_pairs={{0,4},{4,0},{8,12},{12,8},{1,5},{5,1},{9,13},{13,9},{2,6},{6,2},{1... | collective-permute-start | bytes 98312 | tf_op jit(solution)/shard_map/ppermute | solution.py:42
  67.7 5.2 %collective-permute-start.5 = (f32[1,64,128]{2,1,0:T(8,128)S(1)}, f32[1,64,128]{2,1,0:T(8,128)S(1)}, u32[]{:S(2)}, u32[]{:S(2)}) collective-permute-start(f32[1,64,128]{2,1,0:T(8,128)S(1)} %get-tuple-element.31), channel_id=1, source_target_pairs={{4,8},{8,4},{5,9},{9,5},{6,10},{10,6},{7,11},{11,7},{20,24},{24,20... | collective-permute-start | bytes 98312 | tf_op jit(solution)/shard_map/ppermute | solution.py:51

commit v20 on v19

--- a/solution.py
+++ b/solution.py
@@ -300,7 +300,7 @@
     mix_part = jnp.einsum(
         "plm,pmt->lmt", weight_z, weighted, precision=lax.Precision.HIGHEST
     )
-    field_planar = from_patches(planar, band_rows, band_cols)
+    field_planar = lax.optimization_barrier(from_patches(planar, band_rows, band_cols))
     partial = jnp.concatenate([target_part, first_part, mix_part.reshape(-1)])
     members = lat_count * lax.axis_size("lon")
     totals = jnp.sum(

time: 74.8 us -> 74.4 us (level)
  no operation moved by 1% of the time
where the time goes in v20:
time: 74.4 us; the launch traced here: 74 us
  starting transfers between devices  25 us (34%)
  waiting for transfers between devices  14.5 us (19%)
  other arithmetic  13.6 us (18%)
  local copies, waits for them, and re-layouts  11.1 us (15%)
  matrix products  9.28 us (12%)
    all_to_all x2, starting transfers between devices, departed(): lax.all_to_all(outgoing, 'lat', 0, 0, tiled=True)  8.04 us
    ppermute x4, starting transfers between devices, neighbour_halos(): second = lax.ppermute(jnp.where(even, lo_edge, hi_edge), axis, pairs)  7.68 us
    ppermute x4, waiting for transfers between devices, neighbour_halos(): second = lax.ppermute(jnp.where(even, lo_edge, hi_edge), axis, pairs)  6.09 us
    ppermute x4, starting transfers between devices, neighbour_halos(): lax.ppermute(jnp.where(even, hi_edge, lo_edge), axis, [(i, i ^ 1) for i i...  4.8 us
    all_to_all x1, starting transfers between devices, local(): lax.all_to_all(jnp.broadcast_to(partial, (members,) + partial.shape), ('l...  4.46 us
    all_to_all x1, waiting for transfers between devices, local(): lax.all_to_all(jnp.broadcast_to(partial, (members,) + partial.shape), ('l...  4.34 us
    all_to_all x2, waiting for transfers between devices, departed(): lax.all_to_all(outgoing, 'lat', 0, 0, tiled=True)  4.03 us
    gather x2, local copies, waits for them, and re-layouts, departed(): own_patches[send_local.reshape(-1)].reshape(lat_count, CAP, 64, value_count)  2.75 us
  transfers between devices with their start and end apart: 11, of which 5 were waited for; matrix products, arithmetic and copies ran while one was open for 16% of the time, Pallas kernels for 0%

profile of v20, /device:TPU:1, one launch (start us, length us, event | category | flops | bytes accessed | tf_op | source)
XLA Modules:
  0.0 74.0 jit_solution(360855936052198206)
XLA Ops:
  0.0 1.4 %copy.30 = f32[4,8,8,8,128]{4,3,2,1,0:T(8,128)S(1)} copy(f32[4,8,8,8,128]{4,3,1,2,0:T(8,128)} %bitcast.210) | data formatting | bytes 2097152 | tf_op jit(solution)/shard_map/transpose | solution.py:131
  2.4 1.4 %gather_fusion = f32[16,64,128]{2,1,0:T(8,128)} fusion(f32[32,64,128]{2,1,0:T(8,128)S(1)} %bitcast.198, s32[1024]{0:T(1024)S(1)} %pad_clamp_fusion.1), kind=kCustom, calls=%fused_computation | custom fusion | bytes 1048640 | tf_op jit(solution)/shard_map/gather | solution.py:241
  3.8 4.4 %all-to-all-start = ((f32[4,4,64,128]{3,2,1,0:T(8,128)}), f32[4,4,64,128]{3,2,1,0:T(8,128)S(1)}, u32[]{:S(2)}, u32[]{:S(2)}) async-start(f32[4,4,64,128]{3,2,1,0:T(8,128)} %bitcast.17), calls=%async_computation | async-start | bytes 1048576 | tf_op jit(solution)/shard_map/all_to_all | solution.py:247
  13.5 2.5 %all-to-all-done = f32[4,4,64,128]{3,2,1,0:T(8,128)S(1)} async-done(((f32[4,4,64,128]{3,2,1,0:T(8,128)}), f32[4,4,64,128]{3,2,1,0:T(8,128)S(1)}, u32[]{:S(2)}, u32[]{:S(2)}) %all-to-all-start) | async-done | bytes 524320 | tf_op jit(solution)/shard_map/all_to_all | solution.py:247
  16.0 0.8 %fusion = f32[4,8,64,128]{3,1,2,0:T(8,128)S(1)} fusion(f32[32,8192]{1,0:T(8,128)S(1)} %fusion.109, f32[2,8,64,128]{3,2,1,0:T(8,128)S(1)} %bitcast.212, s32[32]{0:T(128)S(1)} %fusion.168, pred[32]{0:T(512)(128)(4,1)S(1)} %get-tuple-element.29), kind=kOutput, calls=%fused_computation.4 | convolution fusion | flops 50594816 | bytes 2621600 | tf_op jit(solution)/shard_map/dot_general | solution.py:259
  17.0 1.8 %fusion.15 = f32[32,64,128]{2,1,0:T(8,128)S(1)} fusion(f32[32,64,128]{2,1,0:T(8,128)S(1)} %bitcast.215, f32[32]{0:T(128)S(1)} %get-tuple-element.124, f32[32]{0:T(128)S(1)} %get-tuple-element.125, f32[32]{0:T(128)S(1)} %get-tuple-element.123, f32[32]{0:T(128)S(1)} %get-tuple-element.88, f32[32]{0:T(128)S(1)} %get-tuple-element.121, ...), kind=kOutput, calls=%fused_computation.41 | convolution fusion | flops 203292672 | bytes 2229248 | tf_op jit(solution)/shard_map/nij,njv->niv/dot_general | solution.py:103
  18.9 1.1 %multiply_add_fusion.6 = f32[32,64,32]{2,1,0:T(8,128)S(1)} fusion(f32[32,64,128]{2,1,0:T(8,128)S(1)} %fusion.15, f32[32]{0:T(128)S(1)} %get-tuple-element.78, f32[32]{0:T(128)S(1)} %get-tuple-element.79, f32[32]{0:T(128)S(1)} %get-tuple-element.80, f32[32]{0:T(128)S(1)} %get-tuple-element.81), kind=kLoop, calls=%fused_computation.39 | loop fusion | flops 458752 | bytes 1311232 | tf_op jit(solution)/shard_map/add | solution.py:121
  20.0 1.3 %multiply_add_fusion.7 = (f32[32,64,32]{2,1,0:T(8,128)S(1)}, f32[32,64,32]{2,1,0:T(8,128)S(1)}, f32[32,64,32]{2,1,0:T(8,128)S(1)}) fusion(f32[32,64,128]{2,1,0:T(8,128)S(1)} %fusion.15, f32[32]{0:T(128)S(1)} %get-tuple-element.82, f32[32]{0:T(128)S(1)} %get-tuple-element.83, f32[32]{0:T(128)S(1)} %get-tuple-element.72, f32[32]{0:T(128)S(1)} %get-tuple-element.75, ...), kind=kLoop, calls=%fused_computation.40 | loop fusion | flops 851968 | bytes 1836032 | tf_op jit(solution)/shard_map/add | solution.py:121
  21.3 0.9 %pad_maximum_fusion.8 = f32[32,64,128]{2,1,0:T(8,128)S(1)} fusion(f32[32,64,32]{2,1,0:T(8,128)S(1)} %get-tuple-element.43, f32[32,64,32]{2,1,0:T(8,128)S(1)} %get-tuple-element.42, f32[32,64,32]{2,1,0:T(8,128)S(1)} %multiply_add_fusion.6, f32[32,64,32]{2,1,0:T(8,128)S(1)} %get-tuple-element.41), kind=kLoop, calls=%fused_computation.29 | loop fusion | flops 786432 | bytes 2097152 | tf_op jit(solution)/shard_map/concatenate | solution.py:123
  22.4 2.2 %collective-permute-start.2 = (f32[32,1,128]{2,1,0:T(1,128)S(1)}, f32[32,1,128]{2,1,0:T(1,128)S(1)}, u32[]{:S(2)}, u32[]{:S(2)}) collective-permute-start(f32[32,1,128]{2,1,0:T(1,128)S(1)} %get-tuple-element.39), channel_id=1, source_target_pairs={{0,1},{1,0},{2,3},{3,2},{4,5},{5,4},{6,7},{7,6},{8,9},{9,8},{10,11... | collective-permute-start | bytes 49160 | tf_op jit(solution)/shard_map/ppermute | solution.py:42
  24.6 2.2 %collective-permute-start.3 = (f32[32,1,128]{2,1,0:T(1,128)S(1)}, f32[32,1,128]{2,1,0:T(1,128)S(1)}, u32[]{:S(2)}, u32[]{:S(2)}) collective-permute-start(f32[32,1,128]{2,1,0:T(1,128)S(1)} %get-tuple-element.40), channel_id=1, source_target_pairs={{1,2},{2,1},{3,0},{0,3},{5,6},{6,5},{7,4},{4,7},{9,10},{10,9},{11,... | collective-permute-start | bytes 49160 | tf_op jit(solution)/shard_map/ppermute | solution.py:51
  26.8 1.2 %pad_select_fusion.1 = (f32[1,65,128]{2,1,0:T(8,128)S(1)}, f32[1,65,128]{2,1,0:T(8,128)S(1)}) fusion(f32[1,64,128]{2,1,0:T(8,128)S(1)} %get-tuple-element.38, f32[]{:T(128)} %bitcast.33, f32[1,64,128]{2,1,0:T(8,128)S(1)} %get-tuple-element.37, f32[]{:T(128)} %bitcast.32, pred[]{:T(512)S(6)} %eq.420), kind=kLoop, calls=%fused_computation.144 | loop fusion | flops 16640 | bytes 132105 | tf_op jit(solution)/shard_map/jit(_where)/select_n | solution.py:43
  28.1 1.5 %collective-permute-start = (f32[1,65,128]{2,1,0:T(8,128)S(1)}, f32[1,65,128]{2,1,0:T(8,128)S(1)}, u32[]{:S(2)}, u32[]{:S(2)}) collective-permute-start(f32[1,65,128]{2,1,0:T(8,128)S(1)} %get-tuple-element.48), channel_id=1, source_target_pairs={{0,4},{4,0},{8,12},{12,8},{1,5},{5,1},{9,13},{13,9},{2,6},{6,2},{1... | collective-permute-start | bytes 99848 | tf_op jit(solution)/shard_map/ppermute | solution.py:42
  29.6 1.9 %collective-permute-start.1 = (f32[1,65,128]{2,1,0:T(8,128)S(1)}, f32[1,65,128]{2,1,0:T(8,128)S(1)}, u32[]{:S(2)}, u32[]{:S(2)}) collective-permute-start(f32[1,65,128]{2,1,0:T(8,128)S(1)} %get-tuple-element.49), channel_id=1, source_target_pairs={{4,8},{8,4},{5,9},{9,5},{6,10},{10,6},{7,11},{11,7},{20,24},{24,20... | collective-permute-start | bytes 99848 | tf_op jit(solution)/shard_map/ppermute | solution.py:51
  31.5 3.3 %collective-permute-done.1 = f32[1,65,128]{2,1,0:T(8,128)S(1)} collective-permute-done((f32[1,65,128]{2,1,0:T(8,128)S(1)}, f32[1,65,128]{2,1,0:T(8,128)S(1)}, u32[]{:S(2)}, u32[]{:S(2)}) %collective-permute-start.1) | collective-permute-done | bytes 33312 | tf_op jit(solution)/shard_map/ppermute | solution.py:51
  36.8 1.4 %gather_fusion.1 = f32[16,64,128]{2,1,0:T(8,128)} fusion(f32[32,64,128]{2,1,0:T(8,128)S(1)} %bitcast.199, s32[1024]{0:T(1024)S(1)} %pad_clamp_fusion), kind=kCustom, calls=%fused_computation.1 | custom fusion | bytes 1048640 | tf_op jit(solution)/shard_map/gather | solution.py:241
  38.2 3.6 %all-to-all-start.1 = ((f32[4,4,64,128]{3,2,1,0:T(8,128)}), f32[4,4,64,128]{3,2,1,0:T(8,128)S(1)}, u32[]{:S(2)}, u32[]{:S(2)}) async-start(f32[4,4,64,128]{3,2,1,0:T(8,128)} %bitcast.40), calls=%async_computation.1 | async-start | bytes 1048576 | tf_op jit(solution)/shard_map/all_to_all | solution.py:247
  41.9 1.3 %maximum_multiply_fusion = f32[34]{0:T(128)S(1)} fusion(f32[1]{0:T(128)} %bitcast.45, f32[32]{0:T(128)S(1)} %copy-done.3, f32[1]{0:T(128)} %bitcast.44, s32[]{:T(128)S(6)} %sub.188), kind=kLoop, calls=%fused_computation.325 | loop fusion | flops 272 | bytes 276 | tf_op jit(solution)/shard_map/mul | solution.py:291
  43.8 1.6 %convolution_bitcast_fusion = f32[32,64,1]{1,2,0:T(1,128)S(1)} fusion(f32[32,64,1]{1,2,0:T(1,128)S(1)} %bitcast.221, f32[64,64]{1,0:T(8,128)S(1)} %get-tuple-element.99, f32[32]{0:T(128)S(1)} %get-tuple-element.113, f32[64,64]{1,0:T(8,128)S(1)} %get-tuple-element.100, f32[32]{0:T(128)S(1)} %get-tuple-element.114, f32[64,64]{1,0:T(8,128)S(1)} %get-tuple-element.101, ...), kind=kOutput, calls=%fused_computation.6 | convolution fusion | flops 3538944 | bytes 148480 | tf_op jit(solution)/shard_map/pi,pij->pj/dot_general | solution.py:294
  46.1 1.6 %all-to-all-done.1 = f32[4,4,64,128]{3,2,1,0:T(8,128)S(1)} async-done(((f32[4,4,64,128]{3,2,1,0:T(8,128)}), f32[4,4,64,128]{3,2,1,0:T(8,128)S(1)}, u32[]{:S(2)}, u32[]{:S(2)}) %all-to-all-start.1) | async-done | bytes 524320 | tf_op jit(solution)/shard_map/all_to_all | solution.py:247
  48.7 1.0 %fusion.184 = f32[32,1,128]{2,1,0:T(1,128)S(1)} fusion(f32[32,64,1]{1,2,0:T(1,128)S(1)} %convolution_bitcast_fusion, f32[32,64,128]{2,1,0:T(8,128)S(1)} %bitcast.208), kind=kOutput, calls=%fused_computation.389 | convolution fusion | flops 3145728 | bytes 1073152 | tf_op jit(solution)/shard_map/pj,pjv->pv/dot_general | solution.py:297
  50.7 4.5 %all-to-all-start.2 = ((f32[16,1,768]{2,1,0:T(1,128)}), f32[16,1,768]{2,1,0:T(1,128)S(1)}, u32[]{:S(2)}, u32[]{:S(2)}) async-start(f32[16,1,768]{2,1,0:T(1,128)} %broadcast_in_dim.35), calls=%async_computation.2 | async-start | bytes 98304 | tf_op jit(solution)/shard_map/all_to_all | solution.py:307
  55.2 1.8 %fusion.31 = f32[32,64,128]{2,1,0:T(8,128)S(1)} fusion(f32[32,64,128]{2,1,0:T(8,128)S(1)} %bitcast.209, f32[64,64]{1,0:T(8,128)S(1)} %get-tuple-element.99, f32[32]{0:T(128)S(1)} %get-tuple-element.113, f32[64,64]{1,0:T(8,128)S(1)} %get-tuple-element.100, f32[32]{0:T(128)S(1)} %get-tuple-element.114, f32[64,64]{1,0:T(8,128)S(1)} %get-tuple-element.101, ...), kind=kOutput, calls=%fused_computation.58 | convolution fusion | flops 203292672 | bytes 2229248 | tf_op jit(solution)/shard_map/nij,njv->niv/dot_general | solution.py:287
  57.2 4.3 %all-to-all-done.2 = f32[16,1,768]{2,1,0:T(1,128)S(1)} async-done(((f32[16,1,768]{2,1,0:T(1,128)}), f32[16,1,768]{2,1,0:T(1,128)S(1)}, u32[]{:S(2)}, u32[]{:S(2)}) %all-to-all-start.2) | async-done | bytes 49184 | tf_op jit(solution)/shard_map/all_to_all | solution.py:307
  61.7 1.0 %multiply_add_fusion.2 = f32[4,8,8,8,32]{4,3,2,1,0:T(8,128)S(1)} fusion(f32[4,8,8,8,128]{4,3,2,1,0:T(8,128)S(1)} %bitcast.196, f32[4,8]{1,0:T(4,128)S(1)} %get-tuple-element.60, f32[4,8]{1,0:T(4,128)S(1)} %get-tuple-element.61, f32[4,8]{1,0:T(4,128)S(1)} %get-tuple-element.62, f32[4,8]{1,0:T(4,128)S(1)} %get-tuple-element.63), kind=kLoop, calls=%fused_computation.33 | loop fusion | flops 458752 | bytes 1311232 | tf_op jit(solution)/shard_map/add | solution.py:182
  62.7 1.2 %multiply_add_fusion.3 = (f32[4,8,8,8,32]{4,3,2,1,0:T(8,128)S(1)}, f32[4,8,8,8,32]{4,3,2,1,0:T(8,128)S(1)}, f32[4,8,8,8,32]{4,3,2,1,0:T(8,128)S(1)}) fusion(f32[4,8,8,8,128]{4,3,2,1,0:T(8,128)S(1)} %bitcast.197, f32[4,8]{1,0:T(4,128)S(1)} %get-tuple-element.64, f32[4,8]{1,0:T(4,128)S(1)} %get-tuple-element.65, f32[4,8]{1,0:T(4,128)S(1)} %get-tuple-element.54, ...), kind=kLoop, calls=%fused_computation.34 | loop fusion | flops 851968 | bytes 1836032 | tf_op jit(solution)/shard_map/add | solution.py:182
  63.9 0.9 %pad_maximum_fusion.9 = f32[4,8,8,8,128]{4,3,2,1,0:T(8,128)S(1)} fusion(f32[4,8,8,8,32]{4,3,2,1,0:T(8,128)S(1)} %get-tuple-element.36, f32[4,8,8,8,32]{4,3,2,1,0:T(8,128)S(1)} %get-tuple-element.35, f32[4,8,8,8,32]{4,3,2,1,0:T(8,128)S(1)} %multiply_add_fusion.2, f32[4,8,8,8,32]{4,3,2,1,0:T(8,128)S(1)} %get-tuple-element.34), kind=kLoop, calls=%fused_computation.30 | loop fusion | flops 786432 | bytes 2097152 | tf_op jit(solution)/shard_map/concatenate | solution.py:184
  65.0 1.4 %collective-permute-start.7 = (f32[32,1,128]{2,1,0:T(1,128)S(1)}, f32[32,1,128]{2,1,0:T(1,128)S(1)}, u32[]{:S(2)}, u32[]{:S(2)}) collective-permute-start(f32[32,1,128]{2,1,0:T(1,128)S(1)} %get-tuple-element.33), channel_id=1, source_target_pairs={{1,2},{2,1},{3,0},{0,3},{5,6},{6,5},{7,4},{4,7},{9,10},{10,9},{11,... | collective-permute-start | bytes 49160 | tf_op jit(solution)/shard_map/ppermute | solution.py:51
  66.4 1.0 %collective-permute-start.4 = (f32[1,64,128]{2,1,0:T(8,128)S(1)}, f32[1,64,128]{2,1,0:T(8,128)S(1)}, u32[]{:S(2)}, u32[]{:S(2)}) collective-permute-start(f32[1,64,128]{2,1,0:T(8,128)S(1)} %get-tuple-element.30), channel_id=1, source_target_pairs={{0,4},{4,0},{8,12},{12,8},{1,5},{5,1},{9,13},{13,9},{2,6},{6,2},{1... | collective-permute-start | bytes 98312 | tf_op jit(solution)/shard_map/ppermute | solution.py:42
  67.3 2.2 %collective-permute-start.5 = (f32[1,64,128]{2,1,0:T(8,128)S(1)}, f32[1,64,128]{2,1,0:T(8,128)S(1)}, u32[]{:S(2)}, u32[]{:S(2)}) collective-permute-start(f32[1,64,128]{2,1,0:T(8,128)S(1)} %get-tuple-element.31), channel_id=1, source_target_pairs={{4,8},{8,4},{5,9},{9,5},{6,10},{10,6},{7,11},{11,7},{20,24},{24,20... | collective-permute-start | bytes 98312 | tf_op jit(solution)/shard_map/ppermute | solution.py:51
  69.8 2.8 %collective-permute-done.5 = f32[1,64,128]{2,1,0:T(8,128)S(1)} collective-permute-done((f32[1,64,128]{2,1,0:T(8,128)S(1)}, f32[1,64,128]{2,1,0:T(8,128)S(1)}, u32[]{:S(2)}, u32[]{:S(2)}) %collective-permute-start.5) | collective-permute-done | bytes 32800 | tf_op jit(solution)/shard_map/ppermute | solution.py:51
  72.6 1.4 %fusion.6 = f32[32,64,128]{2,1,0:T(8,128)} fusion(f32[32,64,128]{2,1,0:T(8,128)S(1)} %bitcast.202, f32[32,1,128]{2,1,0:T(1,128)S(1)} %bitcast.220, f32[32,1,128]{2,1,0:T(1,128)S(1)} %bitcast.219, f32[1,64,128]{2,1,0:T(8,128)S(1)} %get-tuple-element.47, f32[1,64,128]{2,1,0:T(8,128)S(1)} %get-tuple-element.46, f32[128]{0:T(128)S(1)} %slice_divide_fusion.1, ...), kind=kLoop, calls=%fused_computation.13 | loop fusion | flops 3145728 | bytes 2196096 | tf_op jit(solution)/shard_map/mul | solution.py:324
  (120 shorter events, 12.6 us)
Async XLA Ops:
  0.0 1.4 %copy-start.2 = (s32[2,16,32]{2,1,0:T(8,128)S(1)}, s32[2,16,32]{2,1,0:T(8,128)}, u32[]{:S(2)}) copy-start(s32[2,16,32]{2,1,0:T(8,128)} %param.7) | copy-start | bytes 12292
  3.8 4.5 %copy-start.1 = (f32[2,3,16,32]{3,2,1,0:T(8,128)S(1)}, f32[2,3,16,32]{3,2,1,0:T(8,128)}, u32[]{:S(2)}) copy-start(f32[2,3,16,32]{3,2,1,0:T(8,128)} %param.5) | copy-start | bytes 36868
  3.8 12.2 %all-to-all-start = ((f32[4,4,64,128]{3,2,1,0:T(8,128)}), f32[4,4,64,128]{3,2,1,0:T(8,128)S(1)}, u32[]{:S(2)}, u32[]{:S(2)}) async-start(f32[4,4,64,128]{3,2,1,0:T(8,128)} %bitcast.17), calls=%async_computation | async-start | bytes 1048576 | tf_op jit(solution)/shard_map/all_to_all | solution.py:247
  11.6 0.7 copy-start.3
  22.2 13.8 %copy-start = (f32[32,64,128]{2,1,0:T(8,128)S(1)}, f32[32,64,128]{2,1,0:T(8,128)}, u32[]{:S(2)}) copy-start(f32[32,64,128]{2,1,0:T(8,128)} %param.4) | copy-start | bytes 3145732
  22.4 9.1 %collective-permute-start.2 = (f32[32,1,128]{2,1,0:T(1,128)S(1)}, f32[32,1,128]{2,1,0:T(1,128)S(1)}, u32[]{:S(2)}, u32[]{:S(2)}) collective-permute-start(f32[32,1,128]{2,1,0:T(1,128)S(1)} %get-tuple-element.39), channel_id=1, source_target_pairs={{0,1},{1,0},{2,3},{3,2},{4,5},{5,4},{6,7},{7,6},{8,9},{9,8},{10,11... | collective-permute-start | bytes 49160 | tf_op jit(solution)/shard_map/ppermute | solution.py:42
  24.6 6.9 %collective-permute-start.3 = (f32[32,1,128]{2,1,0:T(1,128)S(1)}, f32[32,1,128]{2,1,0:T(1,128)S(1)}, u32[]{:S(2)}, u32[]{:S(2)}) collective-permute-start(f32[32,1,128]{2,1,0:T(1,128)S(1)} %get-tuple-element.40), channel_id=1, source_target_pairs={{1,2},{2,1},{3,0},{0,3},{5,6},{6,5},{7,4},{4,7},{9,10},{10,9},{11,... | collective-permute-start | bytes 49160 | tf_op jit(solution)/shard_map/ppermute | solution.py:51
  28.1 3.5 %collective-permute-start = (f32[1,65,128]{2,1,0:T(8,128)S(1)}, f32[1,65,128]{2,1,0:T(8,128)S(1)}, u32[]{:S(2)}, u32[]{:S(2)}) collective-permute-start(f32[1,65,128]{2,1,0:T(8,128)S(1)} %get-tuple-element.48), channel_id=1, source_target_pairs={{0,4},{4,0},{8,12},{12,8},{1,5},{5,1},{9,13},{13,9},{2,6},{6,2},{1... | collective-permute-start | bytes 99848 | tf_op jit(solution)/shard_map/ppermute | solution.py:42
  29.6 5.3 %collective-permute-start.1 = (f32[1,65,128]{2,1,0:T(8,128)S(1)}, f32[1,65,128]{2,1,0:T(8,128)S(1)}, u32[]{:S(2)}, u32[]{:S(2)}) collective-permute-start(f32[1,65,128]{2,1,0:T(8,128)S(1)} %get-tuple-element.49), channel_id=1, source_target_pairs={{4,8},{8,4},{5,9},{9,5},{6,10},{10,6},{7,11},{11,7},{20,24},{24,20... | collective-permute-start | bytes 99848 | tf_op jit(solution)/shard_map/ppermute | solution.py:51
  38.2 9.5 %all-to-all-start.1 = ((f32[4,4,64,128]{3,2,1,0:T(8,128)}), f32[4,4,64,128]{3,2,1,0:T(8,128)S(1)}, u32[]{:S(2)}, u32[]{:S(2)}) async-start(f32[4,4,64,128]{3,2,1,0:T(8,128)} %bitcast.40), calls=%async_computation.1 | async-start | bytes 1048576 | tf_op jit(solution)/shard_map/all_to_all | solution.py:247
  50.7 10.8 %all-to-all-start.2 = ((f32[16,1,768]{2,1,0:T(1,128)}), f32[16,1,768]{2,1,0:T(1,128)S(1)}, u32[]{:S(2)}, u32[]{:S(2)}) async-start(f32[16,1,768]{2,1,0:T(1,128)} %broadcast_in_dim.35), calls=%async_computation.2 | async-start | bytes 98304 | tf_op jit(solution)/shard_map/all_to_all | solution.py:307
  64.9 4.9 %collective-permute-start.6 = (f32[32,1,128]{2,1,0:T(1,128)S(1)}, f32[32,1,128]{2,1,0:T(1,128)S(1)}, u32[]{:S(2)}, u32[]{:S(2)}) collective-permute-start(f32[32,1,128]{2,1,0:T(1,128)S(1)} %get-tuple-element.32), channel_id=1, source_target_pairs={{0,1},{1,0},{2,3},{3,2},{4,5},{5,4},{6,7},{7,6},{8,9},{9,8},{10,11... | collective-permute-start | bytes 49160 | tf_op jit(solution)/shard_map/ppermute | solution.py:42
  65.0 4.7 %collective-permute-start.7 = (f32[32,1,128]{2,1,0:T(1,128)S(1)}, f32[32,1,128]{2,1,0:T(1,128)S(1)}, u32[]{:S(2)}, u32[]{:S(2)}) collective-permute-start(f32[32,1,128]{2,1,0:T(1,128)S(1)} %get-tuple-element.33), channel_id=1, source_target_pairs={{1,2},{2,1},{3,0},{0,3},{5,6},{6,5},{7,4},{4,7},{9,10},{10,9},{11,... | collective-permute-start | bytes 49160 | tf_op jit(solution)/shard_map/ppermute | solution.py:51
  66.4 3.4 %collective-permute-start.4 = (f32[1,64,128]{2,1,0:T(8,128)S(1)}, f32[1,64,128]{2,1,0:T(8,128)S(1)}, u32[]{:S(2)}, u32[]{:S(2)}) collective-permute-start(f32[1,64,128]{2,1,0:T(8,128)S(1)} %get-tuple-element.30), channel_id=1, source_target_pairs={{0,4},{4,0},{8,12},{12,8},{1,5},{5,1},{9,13},{13,9},{2,6},{6,2},{1... | collective-permute-start | bytes 98312 | tf_op jit(solution)/shard_map/ppermute | solution.py:42
  67.3 5.2 %collective-permute-start.5 = (f32[1,64,128]{2,1,0:T(8,128)S(1)}, f32[1,64,128]{2,1,0:T(8,128)S(1)}, u32[]{:S(2)}, u32[]{:S(2)}) collective-permute-start(f32[1,64,128]{2,1,0:T(8,128)S(1)} %get-tuple-element.31), channel_id=1, source_target_pairs={{4,8},{8,4},{5,9},{9,5},{6,10},{10,6},{7,11},{11,7},{20,24},{24,20... | collective-permute-start | bytes 98312 | tf_op jit(solution)/shard_map/ppermute | solution.py:51

commit v21 on v20

--- a/solution.py
+++ b/solution.py
@@ -170,10 +170,14 @@
     return advected + diffusivity.reshape(k_shape) * laplace
 
 
-def levels_cols(values, weight_z):
+def levels_cols(values, weight_z, scale=None):
     value_count = values.shape[-1]
     per_level = value_count // LEV
     blocks = [values[..., m * per_level : (m + 1) * per_level] for m in range(LEV)]
+    if scale is not None:
+        blocks = [
+            block * scale[m * per_level : (m + 1) * per_level] for m, block in enumerate(blocks)
+        ]
     out = []
     for level in range(LEV):
         acc = None
@@ -318,8 +322,9 @@
     )
     second_ratio = target / second_mass
     advected = levels_cols(
-        (field_planar * first_ratio).reshape(band_rows, 8, band_cols, 8, value_count),
+        field_planar.reshape(band_rows, 8, band_cols, 8, value_count),
         weight_z.reshape(band_rows, 1, band_cols, 1, LEV, LEV),
+        first_ratio,
     ).reshape(row_count, col_count, value_count)
     return diffuse(advected, diffusivity, 0) * second_ratio[None, None, :]
 

time: 74.4 us -> 74.6 us (level)
  other arithmetic: 13.6 us -> 14.4 us
  transfers between devices with their start and end apart: 11 -> 11, of which waited for: 5 -> 5; matrix products, arithmetic and copies ran while one was open for 16% -> 17% of each run, Pallas kernels for 0% -> 0%
where the time goes in v21:
time: 74.6 us; the launch traced here: 74.2 us
  starting transfers between devices  25 us (34%)
  other arithmetic  14.4 us (19%)
  waiting for transfers between devices  14.1 us (19%)
  local copies, waits for them, and re-layouts  10.7 us (14%)
  matrix products  9.28 us (12%)
    all_to_all x2, starting transfers between devices, departed(): lax.all_to_all(outgoing, 'lat', 0, 0, tiled=True)  8.04 us
    ppermute x4, starting transfers between devices, neighbour_halos(): second = lax.ppermute(jnp.where(even, lo_edge, hi_edge), axis, pairs)  7.68 us
    ppermute x4, waiting for transfers between devices, neighbour_halos(): second = lax.ppermute(jnp.where(even, lo_edge, hi_edge), axis, pairs)  6.09 us
    ppermute x4, starting transfers between devices, neighbour_halos(): lax.ppermute(jnp.where(even, hi_edge, lo_edge), axis, [(i, i ^ 1) for i i...  4.8 us
    all_to_all x1, starting transfers between devices, local(): lax.all_to_all(jnp.broadcast_to(partial, (members,) + partial.shape), ('l...  4.45 us
    all_to_all x1, waiting for transfers between devices, local(): lax.all_to_all(jnp.broadcast_to(partial, (members,) + partial.shape), ('l...  4.34 us
    all_to_all x2, waiting for transfers between devices, departed(): lax.all_to_all(outgoing, 'lat', 0, 0, tiled=True)  3.69 us
    gather x2, local copies, waits for them, and re-layouts, departed(): own_patches[send_local.reshape(-1)].reshape(lat_count, CAP, 64, value_count)  2.75 us
  transfers between devices with their start and end apart: 11, of which 5 were waited for; matrix products, arithmetic and copies ran while one was open for 17% of the time, Pallas kernels for 0%

profile of v21, /device:TPU:1, one launch (start us, length us, event | category | flops | bytes accessed | tf_op | source)
XLA Modules:
  0.0 74.2 jit_solution(532149142625207080)
XLA Ops:
  0.0 1.4 %copy.30 = f32[4,8,8,8,128]{4,3,2,1,0:T(8,128)S(1)} copy(f32[4,8,8,8,128]{4,3,1,2,0:T(8,128)} %bitcast.209) | data formatting | bytes 2097152 | tf_op jit(solution)/shard_map/transpose | solution.py:131
  2.4 1.4 %gather_fusion = f32[16,64,128]{2,1,0:T(8,128)} fusion(f32[32,64,128]{2,1,0:T(8,128)S(1)} %bitcast.198, s32[1024]{0:T(1024)S(1)} %pad_clamp_fusion.1), kind=kCustom, calls=%fused_computation | custom fusion | bytes 1048640 | tf_op jit(solution)/shard_map/gather | solution.py:245
  3.8 4.4 %all-to-all-start = ((f32[4,4,64,128]{3,2,1,0:T(8,128)}), f32[4,4,64,128]{3,2,1,0:T(8,128)S(1)}, u32[]{:S(2)}, u32[]{:S(2)}) async-start(f32[4,4,64,128]{3,2,1,0:T(8,128)} %bitcast.17), calls=%async_computation | async-start | bytes 1048576 | tf_op jit(solution)/shard_map/all_to_all | solution.py:251
  13.7 2.3 %all-to-all-done = f32[4,4,64,128]{3,2,1,0:T(8,128)S(1)} async-done(((f32[4,4,64,128]{3,2,1,0:T(8,128)}), f32[4,4,64,128]{3,2,1,0:T(8,128)S(1)}, u32[]{:S(2)}, u32[]{:S(2)}) %all-to-all-start) | async-done | bytes 524320 | tf_op jit(solution)/shard_map/all_to_all | solution.py:251
  16.0 0.8 %fusion = f32[4,8,64,128]{3,1,2,0:T(8,128)S(1)} fusion(f32[32,8192]{1,0:T(8,128)S(1)} %fusion.109, f32[2,8,64,128]{3,2,1,0:T(8,128)S(1)} %bitcast.211, s32[32]{0:T(128)S(1)} %fusion.168, pred[32]{0:T(512)(128)(4,1)S(1)} %get-tuple-element.29), kind=kOutput, calls=%fused_computation.4 | convolution fusion | flops 50594816 | bytes 2621600 | tf_op jit(solution)/shard_map/dot_general | solution.py:263
  17.0 1.8 %fusion.15 = f32[32,64,128]{2,1,0:T(8,128)S(1)} fusion(f32[32,64,128]{2,1,0:T(8,128)S(1)} %bitcast.214, f32[32]{0:T(128)S(1)} %get-tuple-element.130, f32[32]{0:T(128)S(1)} %get-tuple-element.131, f32[32]{0:T(128)S(1)} %get-tuple-element.129, f32[32]{0:T(128)S(1)} %get-tuple-element.91, f32[32]{0:T(128)S(1)} %get-tuple-element.127, ...), kind=kOutput, calls=%fused_computation.45 | convolution fusion | flops 203292672 | bytes 2229248 | tf_op jit(solution)/shard_map/nij,njv->niv/dot_general | solution.py:103
  18.9 1.1 %multiply_add_fusion.6 = f32[32,64,32]{2,1,0:T(8,128)S(1)} fusion(f32[32,64,128]{2,1,0:T(8,128)S(1)} %fusion.15, f32[32]{0:T(128)S(1)} %get-tuple-element.79, f32[32]{0:T(128)S(1)} %get-tuple-element.80, f32[32]{0:T(128)S(1)} %get-tuple-element.81, f32[32]{0:T(128)S(1)} %get-tuple-element.82), kind=kLoop, calls=%fused_computation.43 | loop fusion | flops 458752 | bytes 1311232 | tf_op jit(solution)/shard_map/add | solution.py:121
  20.0 1.3 %multiply_add_fusion.7 = (f32[32,64,32]{2,1,0:T(8,128)S(1)}, f32[32,64,32]{2,1,0:T(8,128)S(1)}, f32[32,64,32]{2,1,0:T(8,128)S(1)}) fusion(f32[32,64,128]{2,1,0:T(8,128)S(1)} %fusion.15, f32[32]{0:T(128)S(1)} %get-tuple-element.83, f32[32]{0:T(128)S(1)} %get-tuple-element.84, f32[32]{0:T(128)S(1)} %get-tuple-element.73, f32[32]{0:T(128)S(1)} %get-tuple-element.76, ...), kind=kLoop, calls=%fused_computation.44 | loop fusion | flops 851968 | bytes 1836032 | tf_op jit(solution)/shard_map/add | solution.py:121
  21.3 0.9 %pad_maximum_fusion.8 = f32[32,64,128]{2,1,0:T(8,128)S(1)} fusion(f32[32,64,32]{2,1,0:T(8,128)S(1)} %get-tuple-element.44, f32[32,64,32]{2,1,0:T(8,128)S(1)} %get-tuple-element.43, f32[32,64,32]{2,1,0:T(8,128)S(1)} %multiply_add_fusion.6, f32[32,64,32]{2,1,0:T(8,128)S(1)} %get-tuple-element.42), kind=kLoop, calls=%fused_computation.33 | loop fusion | flops 786432 | bytes 2097152 | tf_op jit(solution)/shard_map/concatenate | solution.py:123
  22.4 2.2 %collective-permute-start.2 = (f32[32,1,128]{2,1,0:T(1,128)S(1)}, f32[32,1,128]{2,1,0:T(1,128)S(1)}, u32[]{:S(2)}, u32[]{:S(2)}) collective-permute-start(f32[32,1,128]{2,1,0:T(1,128)S(1)} %get-tuple-element.40), channel_id=1, source_target_pairs={{0,1},{1,0},{2,3},{3,2},{4,5},{5,4},{6,7},{7,6},{8,9},{9,8},{10,11... | collective-permute-start | bytes 49160 | tf_op jit(solution)/shard_map/ppermute | solution.py:42
  24.6 2.2 %collective-permute-start.3 = (f32[32,1,128]{2,1,0:T(1,128)S(1)}, f32[32,1,128]{2,1,0:T(1,128)S(1)}, u32[]{:S(2)}, u32[]{:S(2)}) collective-permute-start(f32[32,1,128]{2,1,0:T(1,128)S(1)} %get-tuple-element.41), channel_id=1, source_target_pairs={{1,2},{2,1},{3,0},{0,3},{5,6},{6,5},{7,4},{4,7},{9,10},{10,9},{11,... | collective-permute-start | bytes 49160 | tf_op jit(solution)/shard_map/ppermute | solution.py:51
  26.8 1.4 %pad_select_fusion.1 = (f32[1,65,128]{2,1,0:T(8,128)S(1)}, f32[1,65,128]{2,1,0:T(8,128)S(1)}) fusion(f32[1,64,128]{2,1,0:T(8,128)S(1)} %get-tuple-element.39, f32[]{:T(128)} %bitcast.33, f32[1,64,128]{2,1,0:T(8,128)S(1)} %get-tuple-element.38, f32[]{:T(128)} %bitcast.32, pred[]{:T(512)S(6)} %eq.420), kind=kLoop, calls=%fused_computation.147 | loop fusion | flops 16640 | bytes 132105 | tf_op jit(solution)/shard_map/jit(_where)/select_n | solution.py:43
  28.2 1.5 %collective-permute-start = (f32[1,65,128]{2,1,0:T(8,128)S(1)}, f32[1,65,128]{2,1,0:T(8,128)S(1)}, u32[]{:S(2)}, u32[]{:S(2)}) collective-permute-start(f32[1,65,128]{2,1,0:T(8,128)S(1)} %get-tuple-element.49), channel_id=1, source_target_pairs={{0,4},{4,0},{8,12},{12,8},{1,5},{5,1},{9,13},{13,9},{2,6},{6,2},{1... | collective-permute-start | bytes 99848 | tf_op jit(solution)/shard_map/ppermute | solution.py:42
  29.7 1.9 %collective-permute-start.1 = (f32[1,65,128]{2,1,0:T(8,128)S(1)}, f32[1,65,128]{2,1,0:T(8,128)S(1)}, u32[]{:S(2)}, u32[]{:S(2)}) collective-permute-start(f32[1,65,128]{2,1,0:T(8,128)S(1)} %get-tuple-element.50), channel_id=1, source_target_pairs={{4,8},{8,4},{5,9},{9,5},{6,10},{10,6},{7,11},{11,7},{20,24},{24,20... | collective-permute-start | bytes 99848 | tf_op jit(solution)/shard_map/ppermute | solution.py:51
  31.7 3.3 %collective-permute-done.1 = f32[1,65,128]{2,1,0:T(8,128)S(1)} collective-permute-done((f32[1,65,128]{2,1,0:T(8,128)S(1)}, f32[1,65,128]{2,1,0:T(8,128)S(1)}, u32[]{:S(2)}, u32[]{:S(2)}) %collective-permute-start.1) | collective-permute-done | bytes 33312 | tf_op jit(solution)/shard_map/ppermute | solution.py:51
  37.0 1.4 %gather_fusion.1 = f32[16,64,128]{2,1,0:T(8,128)} fusion(f32[32,64,128]{2,1,0:T(8,128)S(1)} %bitcast.199, s32[1024]{0:T(1024)S(1)} %pad_clamp_fusion), kind=kCustom, calls=%fused_computation.1 | custom fusion | bytes 1048640 | tf_op jit(solution)/shard_map/gather | solution.py:245
  38.4 3.6 %all-to-all-start.1 = ((f32[4,4,64,128]{3,2,1,0:T(8,128)}), f32[4,4,64,128]{3,2,1,0:T(8,128)S(1)}, u32[]{:S(2)}, u32[]{:S(2)}) async-start(f32[4,4,64,128]{3,2,1,0:T(8,128)} %bitcast.40), calls=%async_computation.1 | async-start | bytes 1048576 | tf_op jit(solution)/shard_map/all_to_all | solution.py:251
  42.1 1.4 %maximum_multiply_fusion = f32[34]{0:T(128)S(1)} fusion(f32[1]{0:T(128)} %bitcast.46, f32[32]{0:T(128)S(1)} %copy-done.3, f32[1]{0:T(128)} %bitcast.45, s32[]{:T(128)S(6)} %sub.188), kind=kLoop, calls=%fused_computation.328 | loop fusion | flops 272 | bytes 276 | tf_op jit(solution)/shard_map/mul | solution.py:295
  44.1 1.6 %convolution_bitcast_fusion = f32[32,64,1]{1,2,0:T(1,128)S(1)} fusion(f32[32,64,1]{1,2,0:T(1,128)S(1)} %bitcast.220, f32[64,64]{1,0:T(8,128)S(1)} %get-tuple-element.102, f32[32]{0:T(128)S(1)} %get-tuple-element.119, f32[64,64]{1,0:T(8,128)S(1)} %get-tuple-element.103, f32[32]{0:T(128)S(1)} %get-tuple-element.120, f32[64,64]{1,0:T(8,128)S(1)} %get-tuple-element.104, ...), kind=kOutput, calls=%fused_computation.6 | convolution fusion | flops 3538944 | bytes 148480 | tf_op jit(solution)/shard_map/pi,pij->pj/dot_general | solution.py:298
  46.5 1.4 %all-to-all-done.1 = f32[4,4,64,128]{3,2,1,0:T(8,128)S(1)} async-done(((f32[4,4,64,128]{3,2,1,0:T(8,128)}), f32[4,4,64,128]{3,2,1,0:T(8,128)S(1)}, u32[]{:S(2)}, u32[]{:S(2)}) %all-to-all-start.1) | async-done | bytes 524320 | tf_op jit(solution)/shard_map/all_to_all | solution.py:251
  48.9 1.0 %fusion.184 = f32[32,1,128]{2,1,0:T(1,128)S(1)} fusion(f32[32,64,1]{1,2,0:T(1,128)S(1)} %convolution_bitcast_fusion, f32[32,64,128]{2,1,0:T(8,128)S(1)} %bitcast.207), kind=kOutput, calls=%fused_computation.392 | convolution fusion | flops 3145728 | bytes 1073152 | tf_op jit(solution)/shard_map/pj,pjv->pv/dot_general | solution.py:301
  50.9 4.5 %all-to-all-start.2 = ((f32[16,1,768]{2,1,0:T(1,128)}), f32[16,1,768]{2,1,0:T(1,128)S(1)}, u32[]{:S(2)}, u32[]{:S(2)}) async-start(f32[16,1,768]{2,1,0:T(1,128)} %broadcast_in_dim.35), calls=%async_computation.2 | async-start | bytes 98304 | tf_op jit(solution)/shard_map/all_to_all | solution.py:311
  55.4 1.8 %fusion.31 = f32[32,64,128]{2,1,0:T(8,128)S(1)} fusion(f32[32,64,128]{2,1,0:T(8,128)S(1)} %bitcast.208, f32[64,64]{1,0:T(8,128)S(1)} %get-tuple-element.102, f32[32]{0:T(128)S(1)} %get-tuple-element.119, f32[64,64]{1,0:T(8,128)S(1)} %get-tuple-element.103, f32[32]{0:T(128)S(1)} %get-tuple-element.120, f32[64,64]{1,0:T(8,128)S(1)} %get-tuple-element.104, ...), kind=kOutput, calls=%fused_computation.62 | convolution fusion | flops 203292672 | bytes 2229248 | tf_op jit(solution)/shard_map/nij,njv->niv/dot_general | solution.py:291
  57.4 4.3 %all-to-all-done.2 = f32[16,1,768]{2,1,0:T(1,128)S(1)} async-done(((f32[16,1,768]{2,1,0:T(1,128)}), f32[16,1,768]{2,1,0:T(1,128)S(1)}, u32[]{:S(2)}, u32[]{:S(2)}) %all-to-all-start.2) | async-done | bytes 49184 | tf_op jit(solution)/shard_map/all_to_all | solution.py:311
  61.8 1.0 %multiply_add_fusion.1 = (f32[4,8,8,8,32]{4,3,2,1,0:T(8,128)S(1)}, f32[4,8,8,8,32]{4,3,2,1,0:T(8,128)S(1)}) fusion(f32[4,8,8,8,128]{4,3,2,1,0:T(8,128)S(1)} %bitcast.196, f32[4,8]{1,0:T(4,128)S(1)} %get-tuple-element.58, f32[4,8]{1,0:T(4,128)S(1)} %get-tuple-element.59, f32[4,8]{1,0:T(4,128)S(1)} %get-tuple-element.60, f32[32]{0:T(128)S(1)} %get-tuple-element.106, ...), kind=kLoop, calls=%fused_computation.36 | loop fusion | flops 720896 | bytes 1311744 | tf_op jit(solution)/shard_map/add | solution.py:186
  62.9 1.1 %multiply_add_fusion.3 = (f32[4,8,8,8,32]{4,3,2,1,0:T(8,128)S(1)}, f32[4,8,8,8,32]{4,3,2,1,0:T(8,128)S(1)}) fusion(f32[4,8,8,8,128]{4,3,2,1,0:T(8,128)S(1)} %bitcast.197, f32[32]{0:T(128)S(1)} %get-tuple-element.107, f32[4,8]{1,0:T(4,128)S(1)} %get-tuple-element.65, f32[32]{0:T(128)S(1)} %get-tuple-element.108, f32[4,8]{1,0:T(4,128)S(1)} %get-tuple-element.66, ...), kind=kLoop, calls=%fused_computation.38 | loop fusion | flops 1048576 | bytes 1574272 | tf_op jit(solution)/shard_map/add | solution.py:186
  64.0 0.9 %pad_maximum_fusion.9 = f32[4,8,8,8,128]{4,3,2,1,0:T(8,128)S(1)} fusion(f32[4,8,8,8,32]{4,3,2,1,0:T(8,128)S(1)} %get-tuple-element.33, f32[4,8,8,8,32]{4,3,2,1,0:T(8,128)S(1)} %get-tuple-element.32, f32[4,8,8,8,32]{4,3,2,1,0:T(8,128)S(1)} %get-tuple-element.31, f32[4,8,8,8,32]{4,3,2,1,0:T(8,128)S(1)} %get-tuple-element.30), kind=kLoop, calls=%fused_computation.34 | loop fusion | flops 786432 | bytes 2097152 | tf_op jit(solution)/shard_map/concatenate | solution.py:188
  65.2 1.4 %collective-permute-start.7 = (f32[32,1,128]{2,1,0:T(1,128)S(1)}, f32[32,1,128]{2,1,0:T(1,128)S(1)}, u32[]{:S(2)}, u32[]{:S(2)}) collective-permute-start(f32[32,1,128]{2,1,0:T(1,128)S(1)} %get-tuple-element.37), channel_id=1, source_target_pairs={{1,2},{2,1},{3,0},{0,3},{5,6},{6,5},{7,4},{4,7},{9,10},{10,9},{11,... | collective-permute-start | bytes 49160 | tf_op jit(solution)/shard_map/ppermute | solution.py:51
  66.6 1.0 %collective-permute-start.4 = (f32[1,64,128]{2,1,0:T(8,128)S(1)}, f32[1,64,128]{2,1,0:T(8,128)S(1)}, u32[]{:S(2)}, u32[]{:S(2)}) collective-permute-start(f32[1,64,128]{2,1,0:T(8,128)S(1)} %get-tuple-element.34), channel_id=1, source_target_pairs={{0,4},{4,0},{8,12},{12,8},{1,5},{5,1},{9,13},{13,9},{2,6},{6,2},{1... | collective-permute-start | bytes 98312 | tf_op jit(solution)/shard_map/ppermute | solution.py:42
  67.5 2.2 %collective-permute-start.5 = (f32[1,64,128]{2,1,0:T(8,128)S(1)}, f32[1,64,128]{2,1,0:T(8,128)S(1)}, u32[]{:S(2)}, u32[]{:S(2)}) collective-permute-start(f32[1,64,128]{2,1,0:T(8,128)S(1)} %get-tuple-element.35), channel_id=1, source_target_pairs={{4,8},{8,4},{5,9},{9,5},{6,10},{10,6},{7,11},{11,7},{20,24},{24,20... | collective-permute-start | bytes 98312 | tf_op jit(solution)/shard_map/ppermute | solution.py:51
  70.0 2.8 %collective-permute-done.5 = f32[1,64,128]{2,1,0:T(8,128)S(1)} collective-permute-done((f32[1,64,128]{2,1,0:T(8,128)S(1)}, f32[1,64,128]{2,1,0:T(8,128)S(1)}, u32[]{:S(2)}, u32[]{:S(2)}) %collective-permute-start.5) | collective-permute-done | bytes 32800 | tf_op jit(solution)/shard_map/ppermute | solution.py:51
  72.8 1.4 %fusion.6 = f32[32,64,128]{2,1,0:T(8,128)} fusion(f32[32,64,128]{2,1,0:T(8,128)S(1)} %bitcast.202, f32[32,1,128]{2,1,0:T(1,128)S(1)} %bitcast.219, f32[32,1,128]{2,1,0:T(1,128)S(1)} %bitcast.218, f32[1,64,128]{2,1,0:T(8,128)S(1)} %get-tuple-element.48, f32[1,64,128]{2,1,0:T(8,128)S(1)} %get-tuple-element.47, f32[128]{0:T(128)S(1)} %slice_divide_fusion.1, ...), kind=kLoop, calls=%fused_computation.13 | loop fusion | flops 3145728 | bytes 2196096 | tf_op jit(solution)/shard_map/mul | solution.py:329
  (120 shorter events, 12.9 us)
Async XLA Ops:
  0.0 1.4 %copy-start.2 = (s32[2,16,32]{2,1,0:T(8,128)S(1)}, s32[2,16,32]{2,1,0:T(8,128)}, u32[]{:S(2)}) copy-start(s32[2,16,32]{2,1,0:T(8,128)} %param.7) | copy-start | bytes 12292
  3.8 4.5 %copy-start.1 = (f32[2,3,16,32]{3,2,1,0:T(8,128)S(1)}, f32[2,3,16,32]{3,2,1,0:T(8,128)}, u32[]{:S(2)}) copy-start(f32[2,3,16,32]{3,2,1,0:T(8,128)} %param.5) | copy-start | bytes 36868
  3.8 12.2 %all-to-all-start = ((f32[4,4,64,128]{3,2,1,0:T(8,128)}), f32[4,4,64,128]{3,2,1,0:T(8,128)S(1)}, u32[]{:S(2)}, u32[]{:S(2)}) async-start(f32[4,4,64,128]{3,2,1,0:T(8,128)} %bitcast.17), calls=%async_computation | async-start | bytes 1048576 | tf_op jit(solution)/shard_map/all_to_all | solution.py:251
  11.8 0.7 copy-start.3
  22.2 14.0 %copy-start = (f32[32,64,128]{2,1,0:T(8,128)S(1)}, f32[32,64,128]{2,1,0:T(8,128)}, u32[]{:S(2)}) copy-start(f32[32,64,128]{2,1,0:T(8,128)} %param.4) | copy-start | bytes 3145732
  22.4 9.2 %collective-permute-start.2 = (f32[32,1,128]{2,1,0:T(1,128)S(1)}, f32[32,1,128]{2,1,0:T(1,128)S(1)}, u32[]{:S(2)}, u32[]{:S(2)}) collective-permute-start(f32[32,1,128]{2,1,0:T(1,128)S(1)} %get-tuple-element.40), channel_id=1, source_target_pairs={{0,1},{1,0},{2,3},{3,2},{4,5},{5,4},{6,7},{7,6},{8,9},{9,8},{10,11... | collective-permute-start | bytes 49160 | tf_op jit(solution)/shard_map/ppermute | solution.py:42
  24.6 7.0 %collective-permute-start.3 = (f32[32,1,128]{2,1,0:T(1,128)S(1)}, f32[32,1,128]{2,1,0:T(1,128)S(1)}, u32[]{:S(2)}, u32[]{:S(2)}) collective-permute-start(f32[32,1,128]{2,1,0:T(1,128)S(1)} %get-tuple-element.41), channel_id=1, source_target_pairs={{1,2},{2,1},{3,0},{0,3},{5,6},{6,5},{7,4},{4,7},{9,10},{10,9},{11,... | collective-permute-start | bytes 49160 | tf_op jit(solution)/shard_map/ppermute | solution.py:51
  28.2 3.5 %collective-permute-start = (f32[1,65,128]{2,1,0:T(8,128)S(1)}, f32[1,65,128]{2,1,0:T(8,128)S(1)}, u32[]{:S(2)}, u32[]{:S(2)}) collective-permute-start(f32[1,65,128]{2,1,0:T(8,128)S(1)} %get-tuple-element.49), channel_id=1, source_target_pairs={{0,4},{4,0},{8,12},{12,8},{1,5},{5,1},{9,13},{13,9},{2,6},{6,2},{1... | collective-permute-start | bytes 99848 | tf_op jit(solution)/shard_map/ppermute | solution.py:42
  29.7 5.3 %collective-permute-start.1 = (f32[1,65,128]{2,1,0:T(8,128)S(1)}, f32[1,65,128]{2,1,0:T(8,128)S(1)}, u32[]{:S(2)}, u32[]{:S(2)}) collective-permute-start(f32[1,65,128]{2,1,0:T(8,128)S(1)} %get-tuple-element.50), channel_id=1, source_target_pairs={{4,8},{8,4},{5,9},{9,5},{6,10},{10,6},{7,11},{11,7},{20,24},{24,20... | collective-permute-start | bytes 99848 | tf_op jit(solution)/shard_map/ppermute | solution.py:51
  38.4 9.5 %all-to-all-start.1 = ((f32[4,4,64,128]{3,2,1,0:T(8,128)}), f32[4,4,64,128]{3,2,1,0:T(8,128)S(1)}, u32[]{:S(2)}, u32[]{:S(2)}) async-start(f32[4,4,64,128]{3,2,1,0:T(8,128)} %bitcast.40), calls=%async_computation.1 | async-start | bytes 1048576 | tf_op jit(solution)/shard_map/all_to_all | solution.py:251
  50.9 10.8 %all-to-all-start.2 = ((f32[16,1,768]{2,1,0:T(1,128)}), f32[16,1,768]{2,1,0:T(1,128)S(1)}, u32[]{:S(2)}, u32[]{:S(2)}) async-start(f32[16,1,768]{2,1,0:T(1,128)} %broadcast_in_dim.35), calls=%async_computation.2 | async-start | bytes 98304 | tf_op jit(solution)/shard_map/all_to_all | solution.py:311
  65.1 4.9 %collective-permute-start.6 = (f32[32,1,128]{2,1,0:T(1,128)S(1)}, f32[32,1,128]{2,1,0:T(1,128)S(1)}, u32[]{:S(2)}, u32[]{:S(2)}) collective-permute-start(f32[32,1,128]{2,1,0:T(1,128)S(1)} %get-tuple-element.36), channel_id=1, source_target_pairs={{0,1},{1,0},{2,3},{3,2},{4,5},{5,4},{6,7},{7,6},{8,9},{9,8},{10,11... | collective-permute-start | bytes 49160 | tf_op jit(solution)/shard_map/ppermute | solution.py:42
  65.2 4.7 %collective-permute-start.7 = (f32[32,1,128]{2,1,0:T(1,128)S(1)}, f32[32,1,128]{2,1,0:T(1,128)S(1)}, u32[]{:S(2)}, u32[]{:S(2)}) collective-permute-start(f32[32,1,128]{2,1,0:T(1,128)S(1)} %get-tuple-element.37), channel_id=1, source_target_pairs={{1,2},{2,1},{3,0},{0,3},{5,6},{6,5},{7,4},{4,7},{9,10},{10,9},{11,... | collective-permute-start | bytes 49160 | tf_op jit(solution)/shard_map/ppermute | solution.py:51
  66.6 3.4 %collective-permute-start.4 = (f32[1,64,128]{2,1,0:T(8,128)S(1)}, f32[1,64,128]{2,1,0:T(8,128)S(1)}, u32[]{:S(2)}, u32[]{:S(2)}) collective-permute-start(f32[1,64,128]{2,1,0:T(8,128)S(1)} %get-tuple-element.34), channel_id=1, source_target_pairs={{0,4},{4,0},{8,12},{12,8},{1,5},{5,1},{9,13},{13,9},{2,6},{6,2},{1... | collective-permute-start | bytes 98312 | tf_op jit(solution)/shard_map/ppermute | solution.py:42
  67.5 5.2 %collective-permute-start.5 = (f32[1,64,128]{2,1,0:T(8,128)S(1)}, f32[1,64,128]{2,1,0:T(8,128)S(1)}, u32[]{:S(2)}, u32[]{:S(2)}) collective-permute-start(f32[1,64,128]{2,1,0:T(8,128)S(1)} %get-tuple-element.35), channel_id=1, source_target_pairs={{4,8},{8,4},{5,9},{9,5},{6,10},{10,6},{7,11},{11,7},{20,24},{24,20... | collective-permute-start | bytes 98312 | tf_op jit(solution)/shard_map/ppermute | solution.py:51

commit v22 on v20

--- a/solution.py
+++ b/solution.py
@@ -208,7 +208,7 @@
     return advected + diffusivity[:, None, None] * laplace, k_wide
 
 
-def departed(state_field, source_ids, shifts_now):
+def departed(state_field, source_ids, shifts_now, premix=False):
     lat_count = lax.axis_size("lat")
     lat_index = lax.axis_index("lat")
     lon_index = lax.axis_index("lon")
@@ -250,17 +250,19 @@
     pick_index = my_dev * CAP + my_slot
     take_near = (my_local[:, None] == jnp.arange(per_device)[None, :]) & ~my_remote[:, None]
     take_far = (pick_index[:, None] == jnp.arange(lat_count * CAP)[None, :]) & my_remote[:, None]
-    patches = (
-        jnp.dot(
-            take_near.astype(jnp.float32),
-            own_patches.reshape(per_device, -1),
-            precision=lax.Precision.HIGHEST,
-        )
-        + jnp.dot(
-            take_far.astype(jnp.float32),
-            arrived.reshape(lat_count * CAP, -1),
-            precision=lax.Precision.HIGHEST,
-        )
+    near = jnp.dot(
+        take_near.astype(jnp.float32),
+        own_patches.reshape(per_device, -1),
+        precision=lax.Precision.HIGHEST,
+    ).reshape(per_device, 64, value_count)
+    if premix:
+        near = levels(near, my_frac[2])
+        slot_z = jnp.sum(jnp.where(take_far, my_frac[2][:, None], 0.0), axis=0)
+        arrived = levels(arrived, slot_z)
+    patches = near + jnp.dot(
+        take_far.astype(jnp.float32),
+        arrived.reshape(lat_count * CAP, -1),
+        precision=lax.Precision.HIGHEST,
     ).reshape(per_device, 64, value_count)
     return patches, my_frac
 
@@ -277,8 +279,8 @@
     weights = column_area(lat_index * row_count, row_count, total_rows)
     target_part = column_mass(tracers, weights)
 
-    patches, frac = departed(tracers, source_patch[0], shifts[0])
-    advected = from_patches(levels(spatial(patches, frac[0], frac[1]), frac[2]), band_rows, band_cols)
+    patches, frac = departed(tracers, source_patch[0], shifts[0], premix=True)
+    advected = from_patches(spatial(patches, frac[0], frac[1]), band_rows, band_cols)
     first, k_wide = diffuse_first(advected, diffusivity)
     first_part = column_mass(first, weights)
 

time: 74.4 us -> 81 us (1.089)
  matrix products: 9.28 us -> 12.2 us
  waiting for transfers between devices: 14.5 us -> 12 us
  local copies, waits for them, and re-layouts: 11.1 us -> 13.1 us
  starting transfers between devices: 25 us -> 27 us
  other arithmetic: 13.6 us -> 15.4 us
    add x2 -> x4, other arithmetic: 2.42 us -> 4.38 us  [levels(): acc = term if acc is None else acc + term]
    ppermute x4, starting transfers between devices: 7.68 us -> 9.26 us  [neighbour_halos(): second = lax.ppermute(jnp.where(even, lo_edge, hi_edge), axis, pairs)]
    dot_general x2, matrix products: 1.66 us -> 3.13 us  [departed(): jnp.dot(take_far.astype(jnp.float32), arrived.reshape(lat_count * CAP, -1...]
    ppermute x4, waiting for transfers between devices: 6.09 us -> 4.69 us  [neighbour_halos(): second = lax.ppermute(jnp.where(even, lo_edge, hi_edge), axis, pairs)]
    unnamed x10, local copies, waits for them, and re-layouts: 1.04 us -> 2.25 us
    ppermute x4, starting transfers between devices: 4.8 us -> 3.81 us  [neighbour_halos(): lax.ppermute(jnp.where(even, hi_edge, lo_edge), axis, [(i, i ^ 1) for i i...]
    all_to_all x1, starting transfers between devices: 4.46 us -> 5.4 us  [local(): lax.all_to_all(jnp.broadcast_to(partial, (members,) + partial.shape), ('l...]
  transfers between devices with their start and end apart: 11 -> 11, of which waited for: 5 -> 4; matrix products, arithmetic and copies ran while one was open for 16% -> 17% of each run, Pallas kernels for 0% -> 0%
where the time goes in v22:
time: 81 us; the launch traced here: 80.4 us
  starting transfers between devices  27 us (33%)
  other arithmetic  15.4 us (19%)
  local copies, waits for them, and re-layouts  13.1 us (16%)
  matrix products  12.2 us (15%)
  waiting for transfers between devices  12 us (15%)
    ppermute x4, starting transfers between devices, neighbour_halos(): second = lax.ppermute(jnp.where(even, lo_edge, hi_edge), axis, pairs)  9.26 us
    all_to_all x2, starting transfers between devices, departed(): lax.all_to_all(outgoing, 'lat', 0, 0, tiled=True)  8.56 us
    all_to_all x1, starting transfers between devices, local(): lax.all_to_all(jnp.broadcast_to(partial, (members,) + partial.shape), ('l...  5.4 us
    ppermute x4, waiting for transfers between devices, neighbour_halos(): second = lax.ppermute(jnp.where(even, lo_edge, hi_edge), axis, pairs)  4.69 us
    add x4, other arithmetic, levels(): acc = term if acc is None else acc + term  4.38 us
    all_to_all x1, waiting for transfers between devices, local(): lax.all_to_all(jnp.broadcast_to(partial, (members,) + partial.shape), ('l...  3.89 us
    ppermute x4, starting transfers between devices, neighbour_halos(): lax.ppermute(jnp.where(even, hi_edge, lo_edge), axis, [(i, i ^ 1) for i i...  3.81 us
    all_to_all x2, waiting for transfers between devices, departed(): lax.all_to_all(outgoing, 'lat', 0, 0, tiled=True)  3.43 us
  transfers between devices with their start and end apart: 11, of which 4 were waited for; matrix products, arithmetic and copies ran while one was open for 17% of the time, Pallas kernels for 0%

profile of v22, /device:TPU:1, one launch (start us, length us, event | category | flops | bytes accessed | tf_op | source)
XLA Modules:
  0.0 80.4 jit_solution(5695589683023114232)
XLA Ops:
  1.7 1.4 %copy.63 = f32[4,8,8,8,128]{4,3,2,1,0:T(8,128)S(1)} copy(f32[4,8,8,8,128]{4,3,1,2,0:T(8,128)} %bitcast.268) | data formatting | bytes 2097152 | tf_op jit(solution)/shard_map/transpose | solution.py:131
  3.1 1.4 %gather_fusion = f32[16,64,128]{2,1,0:T(8,128)} fusion(f32[32,64,128]{2,1,0:T(8,128)S(1)} %bitcast.259, s32[1024]{0:T(1024)S(1)} %pad_clamp_fusion.1), kind=kCustom, calls=%fused_computation | custom fusion | bytes 1048640 | tf_op jit(solution)/shard_map/gather | solution.py:241
  4.5 4.3 %all-to-all-start = ((f32[4,4,64,128]{3,2,1,0:T(8,128)}), f32[4,4,64,128]{3,2,1,0:T(8,128)S(1)}, u32[]{:S(2)}, u32[]{:S(2)}) async-start(f32[4,4,64,128]{3,2,1,0:T(8,128)} %bitcast.33), calls=%async_computation | async-start | bytes 1048576 | tf_op jit(solution)/shard_map/all_to_all | solution.py:247
  15.0 0.9 %multiply_add_fusion.6 = f32[32,64,32]{2,0,1:T(8,128)S(1)} fusion(f32[32,64,128]{2,0,1:T(8,128)S(1)} %fusion.3, f32[32]{0:T(128)S(1)} %get-tuple-element.93, f32[32]{0:T(128)S(1)} %get-tuple-element.94, f32[32]{0:T(128)S(1)} %get-tuple-element.95, f32[32]{0:T(128)S(1)} %get-tuple-element.96), kind=kLoop, calls=%fused_computation.44 | loop fusion | flops 458752 | bytes 1311232 | tf_op jit(solution)/shard_map/add | solution.py:121
  15.9 2.3 %multiply_add_fusion.7 = (f32[32,64,32]{2,0,1:T(8,128)S(1)}, f32[32,64,32]{2,0,1:T(8,128)}, f32[32,64,32]{2,0,1:T(8,128)}) fusion(f32[32,64,128]{2,0,1:T(8,128)S(1)} %fusion.3, f32[32]{0:T(128)S(1)} %get-tuple-element.97, f32[32]{0:T(128)S(1)} %get-tuple-element.98, f32[32]{0:T(128)S(1)} %get-tuple-element.87, f32[32]{0:T(128)S(1)} %get-tuple-element.90, ...), kind=kLoop, calls=%fused_computation.45 | loop fusion | flops 851968 | bytes 1836032 | tf_op jit(solution)/shard_map/add | solution.py:121
  19.9 0.7 copy-done
  20.9 1.3 %convolution_add_fusion.1 = f32[32,64,128]{2,0,1:T(8,128)S(1)} fusion(f32[32,64,32]{2,0,1:T(8,128)S(1)} %copy-done.1, f32[32,64,32]{2,0,1:T(8,128)S(1)} %copy-done, f32[32,64,32]{2,0,1:T(8,128)S(1)} %multiply_add_fusion.6, f32[32,64,32]{2,0,1:T(8,128)S(1)} %get-tuple-element.41, s32[32]{0:T(128)S(1)} %fusion.178, pred[32]{0:T(512)(128)(4,1)S(1)} %get-tuple-element.29, ...), kind=kOutput, calls=%fused_computation.3 | convolution fusion | flops 51381248 | bytes 2621600 | tf_op jit(solution)/shard_map/dot_general | solution.py:262
  22.2 2.3 %fusion.19 = f32[32,64,128]{2,1,0:T(8,128)S(1)} fusion(f32[32,64,128]{2,0,1:T(8,128)S(1)} %convolution_add_fusion.1, f32[32]{0:T(128)S(1)} %get-tuple-element.136, f32[32]{0:T(128)S(1)} %get-tuple-element.137, f32[32]{0:T(128)S(1)} %get-tuple-element.135, f32[32]{0:T(128)S(1)} %get-tuple-element.101, f32[32]{0:T(128)S(1)} %get-tuple-element.133, ...), kind=kOutput, calls=%fused_computation.34 | convolution fusion | flops 203292672 | bytes 2229248 | tf_op jit(solution)/shard_map/nij,njv->niv/dot_general | solution.py:103
  24.7 2.0 %collective-permute-start.2 = (f32[32,1,128]{2,1,0:T(1,128)S(1)}, f32[32,1,128]{2,1,0:T(1,128)S(1)}, u32[]{:S(2)}, u32[]{:S(2)}) collective-permute-start(f32[32,1,128]{2,1,0:T(1,128)S(1)} %get-tuple-element.39), channel_id=1, source_target_pairs={{0,1},{1,0},{2,3},{3,2},{4,5},{5,4},{6,7},{7,6},{8,9},{9,8},{10,11... | collective-permute-start | bytes 49160 | tf_op jit(solution)/shard_map/ppermute | solution.py:42
  26.8 2.2 %collective-permute-start.3 = (f32[32,1,128]{2,1,0:T(1,128)S(1)}, f32[32,1,128]{2,1,0:T(1,128)S(1)}, u32[]{:S(2)}, u32[]{:S(2)}) collective-permute-start(f32[32,1,128]{2,1,0:T(1,128)S(1)} %get-tuple-element.40), channel_id=1, source_target_pairs={{1,2},{2,1},{3,0},{0,3},{5,6},{6,5},{7,4},{4,7},{9,10},{10,9},{11,... | collective-permute-start | bytes 49160 | tf_op jit(solution)/shard_map/ppermute | solution.py:51
  29.0 1.2 %pad_select_fusion.1 = (f32[1,65,128]{2,1,0:T(8,128)S(1)}, f32[1,65,128]{2,1,0:T(8,128)S(1)}) fusion(f32[1,64,128]{2,1,0:T(8,128)S(1)} %get-tuple-element.38, f32[]{:T(128)} %bitcast.51, f32[1,64,128]{2,1,0:T(8,128)S(1)} %get-tuple-element.37, f32[]{:T(128)} %bitcast.50, pred[]{:T(512)S(6)} %eq.472), kind=kLoop, calls=%fused_computation.158 | loop fusion | flops 16640 | bytes 132105 | tf_op jit(solution)/shard_map/jit(_where)/select_n | solution.py:43
  30.9 3.5 %collective-permute-start.1 = (f32[1,65,128]{2,1,0:T(8,128)S(1)}, f32[1,65,128]{2,1,0:T(8,128)S(1)}, u32[]{:S(2)}, u32[]{:S(2)}) collective-permute-start(f32[1,65,128]{2,1,0:T(8,128)S(1)} %get-tuple-element.52), channel_id=1, source_target_pairs={{4,8},{8,4},{5,9},{9,5},{6,10},{10,6},{7,11},{11,7},{20,24},{24,20... | collective-permute-start | bytes 99848 | tf_op jit(solution)/shard_map/ppermute | solution.py:51
  34.4 1.7 %collective-permute-done.1 = f32[1,65,128]{2,1,0:T(8,128)S(1)} collective-permute-done((f32[1,65,128]{2,1,0:T(8,128)S(1)}, f32[1,65,128]{2,1,0:T(8,128)S(1)}, u32[]{:S(2)}, u32[]{:S(2)}) %collective-permute-start.1) | collective-permute-done | bytes 33312 | tf_op jit(solution)/shard_map/ppermute | solution.py:51
  37.3 1.4 %maximum_multiply_fusion = f32[34]{0:T(128)S(1)} fusion(f32[1]{0:T(128)} %bitcast.66, f32[32]{0:T(128)S(1)} %copy-done.4, f32[1]{0:T(128)} %bitcast.65, s32[]{:T(128)S(6)} %sub.200), kind=kLoop, calls=%fused_computation.355 | loop fusion | flops 272 | bytes 276 | tf_op jit(solution)/shard_map/mul | solution.py:293
  39.2 0.7 multiply_reduce_fusion.1
  40.1 1.4 %gather_fusion.1 = f32[16,64,128]{2,1,0:T(8,128)} fusion(f32[32,64,128]{2,1,0:T(8,128)S(1)} %bitcast.260, s32[1024]{0:T(1024)S(1)} %pad_clamp_fusion), kind=kCustom, calls=%fused_computation.1 | custom fusion | bytes 1048640 | tf_op jit(solution)/shard_map/gather | solution.py:241
  41.5 4.3 %all-to-all-start.1 = ((f32[4,4,64,128]{3,2,1,0:T(8,128)}), f32[4,4,64,128]{3,2,1,0:T(8,128)}, u32[]{:S(2)}, u32[]{:S(2)}) async-start(f32[4,4,64,128]{3,2,1,0:T(8,128)} %bitcast.60), calls=%async_computation.1 | async-start | bytes 1048576 | tf_op jit(solution)/shard_map/all_to_all | solution.py:247
  45.8 1.6 %convolution_bitcast_fusion = f32[32,64,1]{1,2,0:T(1,128)S(1)} fusion(f32[32,64,1]{1,2,0:T(1,128)S(1)} %bitcast.278, f32[64,64]{1,0:T(8,128)S(1)} %get-tuple-element.114, f32[32]{0:T(128)S(1)} %get-tuple-element.128, f32[64,64]{1,0:T(8,128)S(1)} %get-tuple-element.115, f32[32]{0:T(128)S(1)} %get-tuple-element.129, f32[64,64]{1,0:T(8,128)S(1)} %get-tuple-element.116, ...), kind=kOutput, calls=%fused_computation.4 | convolution fusion | flops 3538944 | bytes 148480 | tf_op jit(solution)/shard_map/pi,pij->pj/dot_general | solution.py:296
  48.2 3.4 %all-to-all-done.1 = f32[4,4,64,128]{3,2,1,0:T(8,128)} async-done(((f32[4,4,64,128]{3,2,1,0:T(8,128)}), f32[4,4,64,128]{3,2,1,0:T(8,128)}, u32[]{:S(2)}, u32[]{:S(2)}) %all-to-all-start.1) | async-done | bytes 524320 | tf_op jit(solution)/shard_map/all_to_all | solution.py:247
  51.6 1.9 %convolution_add_fusion = f32[32,64,128]{2,0,1:T(8,128)S(1)} fusion(f32[32,64,128]{2,0,1:T(8,128)S(1)} %fusion, s32[32]{0:T(128)S(1)} %fusion.177, pred[32]{0:T(512)(128)(4,1)S(1)} %get-tuple-element.18, f32[2,8,64,128]{3,2,1,0:T(8,128)} %bitcast.107), kind=kOutput, calls=%fused_computation.2 | convolution fusion | flops 50594816 | bytes 2621600 | tf_op jit(solution)/shard_map/dot_general | solution.py:262
  53.5 1.5 %fusion.36 = f32[32,1,128]{2,1,0:T(1,128)S(1)} fusion(f32[32,64,1]{1,2,0:T(1,128)S(1)} %convolution_bitcast_fusion, f32[32,64,128]{2,0,1:T(8,128)S(1)} %convolution_add_fusion), kind=kOutput, calls=%fused_computation.62 | convolution fusion | flops 3145728 | bytes 1073152 | tf_op jit(solution)/shard_map/pj,pjv->pv/dot_general | solution.py:299
  56.0 5.4 %all-to-all-start.2 = ((f32[16,1,768]{2,1,0:T(1,128)}), f32[16,1,768]{2,1,0:T(1,128)S(1)}, u32[]{:S(2)}, u32[]{:S(2)}) async-start(f32[16,1,768]{2,1,0:T(1,128)} %broadcast_in_dim.45), calls=%async_computation.2 | async-start | bytes 98304 | tf_op jit(solution)/shard_map/all_to_all | solution.py:309
  61.4 2.3 %fusion.38 = f32[32,64,128]{2,1,0:T(8,128)S(1)} fusion(f32[32,64,128]{2,0,1:T(8,128)S(1)} %convolution_add_fusion, f32[64,64]{1,0:T(8,128)S(1)} %get-tuple-element.114, f32[32]{0:T(128)S(1)} %get-tuple-element.128, f32[64,64]{1,0:T(8,128)S(1)} %get-tuple-element.115, f32[32]{0:T(128)S(1)} %get-tuple-element.129, f32[64,64]{1,0:T(8,128)S(1)} %get-tuple-element.116, ...), kind=kOutput, calls=%fused_computation.64 | convolution fusion | flops 203292672 | bytes 2229248 | tf_op jit(solution)/shard_map/nij,njv->niv/dot_general | solution.py:289
  63.8 3.9 %all-to-all-done.2 = f32[16,1,768]{2,1,0:T(1,128)S(1)} async-done(((f32[16,1,768]{2,1,0:T(1,128)}), f32[16,1,768]{2,1,0:T(1,128)S(1)}, u32[]{:S(2)}, u32[]{:S(2)}) %all-to-all-start.2) | async-done | bytes 49184 | tf_op jit(solution)/shard_map/all_to_all | solution.py:309
  68.0 1.0 %multiply_add_fusion.2 = f32[4,8,8,8,32]{4,3,2,1,0:T(8,128)S(1)} fusion(f32[4,8,8,8,128]{4,3,2,1,0:T(8,128)S(1)} %bitcast.255, f32[4,8]{1,0:T(4,128)S(1)} %get-tuple-element.63, f32[4,8]{1,0:T(4,128)S(1)} %get-tuple-element.64, f32[4,8]{1,0:T(4,128)S(1)} %get-tuple-element.65, f32[4,8]{1,0:T(4,128)S(1)} %get-tuple-element.66), kind=kLoop, calls=%fused_computation.38 | loop fusion | flops 458752 | bytes 1311232 | tf_op jit(solution)/shard_map/add | solution.py:182
  69.0 1.2 %multiply_add_fusion.3 = (f32[4,8,8,8,32]{4,3,2,1,0:T(8,128)S(1)}, f32[4,8,8,8,32]{4,3,2,1,0:T(8,128)S(1)}, f32[4,8,8,8,32]{4,3,2,1,0:T(8,128)S(1)}) fusion(f32[4,8,8,8,128]{4,3,2,1,0:T(8,128)S(1)} %bitcast.256, f32[4,8]{1,0:T(4,128)S(1)} %get-tuple-element.67, f32[4,8]{1,0:T(4,128)S(1)} %get-tuple-element.68, f32[4,8]{1,0:T(4,128)S(1)} %get-tuple-element.57, ...), kind=kLoop, calls=%fused_computation.39 | loop fusion | flops 851968 | bytes 1836032 | tf_op jit(solution)/shard_map/add | solution.py:182
  70.1 0.9 %pad_maximum_fusion.8 = f32[4,8,8,8,128]{4,3,2,1,0:T(8,128)S(1)} fusion(f32[4,8,8,8,32]{4,3,2,1,0:T(8,128)S(1)} %get-tuple-element.36, f32[4,8,8,8,32]{4,3,2,1,0:T(8,128)S(1)} %get-tuple-element.35, f32[4,8,8,8,32]{4,3,2,1,0:T(8,128)S(1)} %multiply_add_fusion.2, f32[4,8,8,8,32]{4,3,2,1,0:T(8,128)S(1)} %get-tuple-element.34), kind=kLoop, calls=%fused_computation.33 | loop fusion | flops 786432 | bytes 2097152 | tf_op jit(solution)/shard_map/concatenate | solution.py:184
  71.4 1.4 %collective-permute-start.7 = (f32[32,1,128]{2,1,0:T(1,128)S(1)}, f32[32,1,128]{2,1,0:T(1,128)S(1)}, u32[]{:S(2)}, u32[]{:S(2)}) collective-permute-start(f32[32,1,128]{2,1,0:T(1,128)S(1)} %get-tuple-element.33), channel_id=1, source_target_pairs={{1,2},{2,1},{3,0},{0,3},{5,6},{6,5},{7,4},{4,7},{9,10},{10,9},{11,... | collective-permute-start | bytes 49160 | tf_op jit(solution)/shard_map/ppermute | solution.py:51
  72.8 1.0 %collective-permute-start.4 = (f32[1,64,128]{2,1,0:T(8,128)S(1)}, f32[1,64,128]{2,1,0:T(8,128)S(1)}, u32[]{:S(2)}, u32[]{:S(2)}) collective-permute-start(f32[1,64,128]{2,1,0:T(8,128)S(1)} %get-tuple-element.30), channel_id=1, source_target_pairs={{0,4},{4,0},{8,12},{12,8},{1,5},{5,1},{9,13},{13,9},{2,6},{6,2},{1... | collective-permute-start | bytes 98312 | tf_op jit(solution)/shard_map/ppermute | solution.py:42
  73.7 2.2 %collective-permute-start.5 = (f32[1,64,128]{2,1,0:T(8,128)S(1)}, f32[1,64,128]{2,1,0:T(8,128)S(1)}, u32[]{:S(2)}, u32[]{:S(2)}) collective-permute-start(f32[1,64,128]{2,1,0:T(8,128)S(1)} %get-tuple-element.31), channel_id=1, source_target_pairs={{4,8},{8,4},{5,9},{9,5},{6,10},{10,6},{7,11},{11,7},{20,24},{24,20... | collective-permute-start | bytes 98312 | tf_op jit(solution)/shard_map/ppermute | solution.py:51
  76.0 3.0 %collective-permute-done.5 = f32[1,64,128]{2,1,0:T(8,128)S(1)} collective-permute-done((f32[1,64,128]{2,1,0:T(8,128)S(1)}, f32[1,64,128]{2,1,0:T(8,128)S(1)}, u32[]{:S(2)}, u32[]{:S(2)}) %collective-permute-start.5) | collective-permute-done | bytes 32800 | tf_op jit(solution)/shard_map/ppermute | solution.py:51
  79.0 1.4 %fusion.10 = f32[32,64,128]{2,1,0:T(8,128)} fusion(f32[32,64,128]{2,1,0:T(8,128)S(1)} %bitcast.263, f32[32,1,128]{2,1,0:T(1,128)S(1)} %bitcast.277, f32[32,1,128]{2,1,0:T(1,128)S(1)} %bitcast.276, f32[1,64,128]{2,1,0:T(8,128)S(1)} %get-tuple-element.50, f32[1,64,128]{2,1,0:T(8,128)S(1)} %get-tuple-element.49, f32[128]{0:T(128)S(1)} %slice_divide_fusion.1, ...), kind=kLoop, calls=%fused_computation.17 | loop fusion | flops 3145728 | bytes 2196096 | tf_op jit(solution)/shard_map/mul | solution.py:326
  (126 shorter events, 14.9 us)
Async XLA Ops:
  4.5 13.7 %all-to-all-start = ((f32[4,4,64,128]{3,2,1,0:T(8,128)}), f32[4,4,64,128]{3,2,1,0:T(8,128)S(1)}, u32[]{:S(2)}, u32[]{:S(2)}) async-start(f32[4,4,64,128]{3,2,1,0:T(8,128)} %bitcast.33), calls=%async_computation | async-start | bytes 1048576 | tf_op jit(solution)/shard_map/all_to_all | solution.py:247
  8.8 0.8 copy-start.3
  11.8 0.7 copy-start.4
  19.4 1.2 %copy-start = (f32[32,64,32]{2,0,1:T(8,128)S(1)}, f32[32,64,32]{2,0,1:T(8,128)}, u32[]{:S(2)}) copy-start(f32[32,64,32]{2,0,1:T(8,128)} %get-tuple-element.42) | copy-start | bytes 786436
  19.4 1.5 %copy-start.1 = (f32[32,64,32]{2,0,1:T(8,128)S(1)}, f32[32,64,32]{2,0,1:T(8,128)}, u32[]{:S(2)}) copy-start(f32[32,64,32]{2,0,1:T(8,128)} %get-tuple-element.43) | copy-start | bytes 786436
  24.5 14.7 %copy-start.2 = (f32[32,64,128]{2,1,0:T(8,128)S(1)}, f32[32,64,128]{2,1,0:T(8,128)}, u32[]{:S(2)}) copy-start(f32[32,64,128]{2,1,0:T(8,128)} %param.4) | copy-start | bytes 3145732
  24.7 9.7 %collective-permute-start.2 = (f32[32,1,128]{2,1,0:T(1,128)S(1)}, f32[32,1,128]{2,1,0:T(1,128)S(1)}, u32[]{:S(2)}, u32[]{:S(2)}) collective-permute-start(f32[32,1,128]{2,1,0:T(1,128)S(1)} %get-tuple-element.39), channel_id=1, source_target_pairs={{0,1},{1,0},{2,3},{3,2},{4,5},{5,4},{6,7},{7,6},{8,9},{9,8},{10,11... | collective-permute-start | bytes 49160 | tf_op jit(solution)/shard_map/ppermute | solution.py:42
  26.8 7.6 %collective-permute-start.3 = (f32[32,1,128]{2,1,0:T(1,128)S(1)}, f32[32,1,128]{2,1,0:T(1,128)S(1)}, u32[]{:S(2)}, u32[]{:S(2)}) collective-permute-start(f32[32,1,128]{2,1,0:T(1,128)S(1)} %get-tuple-element.40), channel_id=1, source_target_pairs={{1,2},{2,1},{3,0},{0,3},{5,6},{6,5},{7,4},{4,7},{9,10},{10,9},{11,... | collective-permute-start | bytes 49160 | tf_op jit(solution)/shard_map/ppermute | solution.py:51
  30.2 4.2 %collective-permute-start = (f32[1,65,128]{2,1,0:T(8,128)S(1)}, f32[1,65,128]{2,1,0:T(8,128)S(1)}, u32[]{:S(2)}, u32[]{:S(2)}) collective-permute-start(f32[1,65,128]{2,1,0:T(8,128)S(1)} %get-tuple-element.51), channel_id=1, source_target_pairs={{0,4},{4,0},{8,12},{12,8},{1,5},{5,1},{9,13},{13,9},{2,6},{6,2},{1... | collective-permute-start | bytes 99848 | tf_op jit(solution)/shard_map/ppermute | solution.py:42
  30.9 5.3 %collective-permute-start.1 = (f32[1,65,128]{2,1,0:T(8,128)S(1)}, f32[1,65,128]{2,1,0:T(8,128)S(1)}, u32[]{:S(2)}, u32[]{:S(2)}) collective-permute-start(f32[1,65,128]{2,1,0:T(8,128)S(1)} %get-tuple-element.52), channel_id=1, source_target_pairs={{4,8},{8,4},{5,9},{9,5},{6,10},{10,6},{7,11},{11,7},{20,24},{24,20... | collective-permute-start | bytes 99848 | tf_op jit(solution)/shard_map/ppermute | solution.py:51
  41.5 10.1 %all-to-all-start.1 = ((f32[4,4,64,128]{3,2,1,0:T(8,128)}), f32[4,4,64,128]{3,2,1,0:T(8,128)}, u32[]{:S(2)}, u32[]{:S(2)}) async-start(f32[4,4,64,128]{3,2,1,0:T(8,128)} %bitcast.60), calls=%async_computation.1 | async-start | bytes 1048576 | tf_op jit(solution)/shard_map/all_to_all | solution.py:247
  56.0 11.7 %all-to-all-start.2 = ((f32[16,1,768]{2,1,0:T(1,128)}), f32[16,1,768]{2,1,0:T(1,128)S(1)}, u32[]{:S(2)}, u32[]{:S(2)}) async-start(f32[16,1,768]{2,1,0:T(1,128)} %broadcast_in_dim.45), calls=%async_computation.2 | async-start | bytes 98304 | tf_op jit(solution)/shard_map/all_to_all | solution.py:309
  71.3 4.7 %collective-permute-start.6 = (f32[32,1,128]{2,1,0:T(1,128)S(1)}, f32[32,1,128]{2,1,0:T(1,128)S(1)}, u32[]{:S(2)}, u32[]{:S(2)}) collective-permute-start(f32[32,1,128]{2,1,0:T(1,128)S(1)} %get-tuple-element.32), channel_id=1, source_target_pairs={{0,1},{1,0},{2,3},{3,2},{4,5},{5,4},{6,7},{7,6},{8,9},{9,8},{10,11... | collective-permute-start | bytes 49160 | tf_op jit(solution)/shard_map/ppermute | solution.py:42
  71.4 4.6 %collective-permute-start.7 = (f32[32,1,128]{2,1,0:T(1,128)S(1)}, f32[32,1,128]{2,1,0:T(1,128)S(1)}, u32[]{:S(2)}, u32[]{:S(2)}) collective-permute-start(f32[32,1,128]{2,1,0:T(1,128)S(1)} %get-tuple-element.33), channel_id=1, source_target_pairs={{1,2},{2,1},{3,0},{0,3},{5,6},{6,5},{7,4},{4,7},{9,10},{10,9},{11,... | collective-permute-start | bytes 49160 | tf_op jit(solution)/shard_map/ppermute | solution.py:51
  72.8 3.2 %collective-permute-start.4 = (f32[1,64,128]{2,1,0:T(8,128)S(1)}, f32[1,64,128]{2,1,0:T(8,128)S(1)}, u32[]{:S(2)}, u32[]{:S(2)}) collective-permute-start(f32[1,64,128]{2,1,0:T(8,128)S(1)} %get-tuple-element.30), channel_id=1, source_target_pairs={{0,4},{4,0},{8,12},{12,8},{1,5},{5,1},{9,13},{13,9},{2,6},{6,2},{1... | collective-permute-start | bytes 98312 | tf_op jit(solution)/shard_map/ppermute | solution.py:42
  73.7 5.2 %collective-permute-start.5 = (f32[1,64,128]{2,1,0:T(8,128)S(1)}, f32[1,64,128]{2,1,0:T(8,128)S(1)}, u32[]{:S(2)}, u32[]{:S(2)}) collective-permute-start(f32[1,64,128]{2,1,0:T(8,128)S(1)} %get-tuple-element.31), channel_id=1, source_target_pairs={{4,8},{8,4},{5,9},{9,5},{6,10},{10,6},{7,11},{11,7},{20,24},{24,20... | collective-permute-start | bytes 98312 | tf_op jit(solution)/shard_map/ppermute | solution.py:51

commit v23 on v20

--- a/solution.py
+++ b/solution.py
@@ -303,10 +303,11 @@
     field_planar = lax.optimization_barrier(from_patches(planar, band_rows, band_cols))
     partial = jnp.concatenate([target_part, first_part, mix_part.reshape(-1)])
     members = lat_count * lax.axis_size("lon")
+    rows = partial.reshape(-1, value_count)
     totals = jnp.sum(
         lax.all_to_all(
-            jnp.broadcast_to(partial, (members,) + partial.shape), ("lat", "lon"), 0, 0, tiled=True
-        ),
+            jnp.broadcast_to(rows[None], (members,) + rows.shape), ("lat", "lon"), 0, 0, tiled=True
+        ).reshape(members, -1),
         axis=0,
     )
     target = totals[:value_count]

time: 74.4 us -> 74.9 us (level)
  no operation moved by 1% of the time
where the time goes in v23:
time: 74.9 us; the launch traced here: 74.5 us
  starting transfers between devices  25.2 us (34%)
  waiting for transfers between devices  14.5 us (19%)
  other arithmetic  13.7 us (18%)
  local copies, waits for them, and re-layouts  11.2 us (15%)
  matrix products  9.28 us (12%)
    all_to_all x2, starting transfers between devices, departed(): lax.all_to_all(outgoing, 'lat', 0, 0, tiled=True)  8.04 us
    ppermute x4, starting transfers between devices, neighbour_halos(): second = lax.ppermute(jnp.where(even, lo_edge, hi_edge), axis, pairs)  7.81 us
    ppermute x4, waiting for transfers between devices, neighbour_halos(): second = lax.ppermute(jnp.where(even, lo_edge, hi_edge), axis, pairs)  6.21 us
    ppermute x4, starting transfers between devices, neighbour_halos(): lax.ppermute(jnp.where(even, hi_edge, lo_edge), axis, [(i, i ^ 1) for i i...  4.87 us
    all_to_all x1, starting transfers between devices, local(): lax.all_to_all(jnp.broadcast_to(rows[None], (members,) + rows.shape), ('l...  4.46 us
    all_to_all x1, waiting for transfers between devices, local(): lax.all_to_all(jnp.broadcast_to(rows[None], (members,) + rows.shape), ('l...  4.41 us
    all_to_all x2, waiting for transfers between devices, departed(): lax.all_to_all(outgoing, 'lat', 0, 0, tiled=True)  3.89 us
    gather x2, local copies, waits for them, and re-layouts, departed(): own_patches[send_local.reshape(-1)].reshape(lat_count, CAP, 64, value_count)  2.75 us
  transfers between devices with their start and end apart: 11, of which 5 were waited for; matrix products, arithmetic and copies ran while one was open for 16% of the time, Pallas kernels for 0%

profile of v23, /device:TPU:1, one launch (start us, length us, event | category | flops | bytes accessed | tf_op | source)
XLA Modules:
  0.0 74.5 jit_solution(4203317237908861099)
XLA Ops:
  0.0 1.4 %copy.30 = f32[4,8,8,8,128]{4,3,2,1,0:T(8,128)S(1)} copy(f32[4,8,8,8,128]{4,3,1,2,0:T(8,128)} %bitcast.217) | data formatting | bytes 2097152 | tf_op jit(solution)/shard_map/transpose | solution.py:131
  2.4 1.4 %gather_fusion = f32[16,64,128]{2,1,0:T(8,128)} fusion(f32[32,64,128]{2,1,0:T(8,128)S(1)} %bitcast.205, s32[1024]{0:T(1024)S(1)} %pad_clamp_fusion.1), kind=kCustom, calls=%fused_computation | custom fusion | bytes 1048640 | tf_op jit(solution)/shard_map/gather | solution.py:241
  3.8 4.4 %all-to-all-start = ((f32[4,4,64,128]{3,2,1,0:T(8,128)}), f32[4,4,64,128]{3,2,1,0:T(8,128)S(1)}, u32[]{:S(2)}, u32[]{:S(2)}) async-start(f32[4,4,64,128]{3,2,1,0:T(8,128)} %bitcast.17), calls=%async_computation | async-start | bytes 1048576 | tf_op jit(solution)/shard_map/all_to_all | solution.py:247
  13.6 2.4 %all-to-all-done = f32[4,4,64,128]{3,2,1,0:T(8,128)S(1)} async-done(((f32[4,4,64,128]{3,2,1,0:T(8,128)}), f32[4,4,64,128]{3,2,1,0:T(8,128)S(1)}, u32[]{:S(2)}, u32[]{:S(2)}) %all-to-all-start) | async-done | bytes 524320 | tf_op jit(solution)/shard_map/all_to_all | solution.py:247
  16.0 0.8 %fusion = f32[4,8,64,128]{3,1,2,0:T(8,128)S(1)} fusion(f32[32,8192]{1,0:T(8,128)S(1)} %fusion.109, f32[2,8,64,128]{3,2,1,0:T(8,128)S(1)} %bitcast.219, s32[32]{0:T(128)S(1)} %fusion.168, pred[32]{0:T(512)(128)(4,1)S(1)} %get-tuple-element.29), kind=kOutput, calls=%fused_computation.4 | convolution fusion | flops 50594816 | bytes 2621600 | tf_op jit(solution)/shard_map/dot_general | solution.py:259
  17.0 1.8 %fusion.15 = f32[32,64,128]{2,1,0:T(8,128)S(1)} fusion(f32[32,64,128]{2,1,0:T(8,128)S(1)} %bitcast.222, f32[32]{0:T(128)S(1)} %get-tuple-element.126, f32[32]{0:T(128)S(1)} %get-tuple-element.127, f32[32]{0:T(128)S(1)} %get-tuple-element.125, f32[32]{0:T(128)S(1)} %get-tuple-element.88, f32[32]{0:T(128)S(1)} %get-tuple-element.123, ...), kind=kOutput, calls=%fused_computation.41 | convolution fusion | flops 203292672 | bytes 2229248 | tf_op jit(solution)/shard_map/nij,njv->niv/dot_general | solution.py:103
  18.9 1.1 %multiply_add_fusion.6 = f32[32,64,32]{2,1,0:T(8,128)S(1)} fusion(f32[32,64,128]{2,1,0:T(8,128)S(1)} %fusion.15, f32[32]{0:T(128)S(1)} %get-tuple-element.78, f32[32]{0:T(128)S(1)} %get-tuple-element.79, f32[32]{0:T(128)S(1)} %get-tuple-element.80, f32[32]{0:T(128)S(1)} %get-tuple-element.81), kind=kLoop, calls=%fused_computation.39 | loop fusion | flops 458752 | bytes 1311232 | tf_op jit(solution)/shard_map/add | solution.py:121
  20.0 1.3 %multiply_add_fusion.7 = (f32[32,64,32]{2,1,0:T(8,128)S(1)}, f32[32,64,32]{2,1,0:T(8,128)S(1)}, f32[32,64,32]{2,1,0:T(8,128)S(1)}) fusion(f32[32,64,128]{2,1,0:T(8,128)S(1)} %fusion.15, f32[32]{0:T(128)S(1)} %get-tuple-element.82, f32[32]{0:T(128)S(1)} %get-tuple-element.83, f32[32]{0:T(128)S(1)} %get-tuple-element.72, f32[32]{0:T(128)S(1)} %get-tuple-element.75, ...), kind=kLoop, calls=%fused_computation.40 | loop fusion | flops 851968 | bytes 1836032 | tf_op jit(solution)/shard_map/add | solution.py:121
  21.3 0.9 %pad_maximum_fusion.8 = f32[32,64,128]{2,1,0:T(8,128)S(1)} fusion(f32[32,64,32]{2,1,0:T(8,128)S(1)} %get-tuple-element.43, f32[32,64,32]{2,1,0:T(8,128)S(1)} %get-tuple-element.42, f32[32,64,32]{2,1,0:T(8,128)S(1)} %multiply_add_fusion.6, f32[32,64,32]{2,1,0:T(8,128)S(1)} %get-tuple-element.41), kind=kLoop, calls=%fused_computation.29 | loop fusion | flops 786432 | bytes 2097152 | tf_op jit(solution)/shard_map/concatenate | solution.py:123
  22.4 2.2 %collective-permute-start.2 = (f32[32,1,128]{2,1,0:T(1,128)S(1)}, f32[32,1,128]{2,1,0:T(1,128)S(1)}, u32[]{:S(2)}, u32[]{:S(2)}) collective-permute-start(f32[32,1,128]{2,1,0:T(1,128)S(1)} %get-tuple-element.39), channel_id=1, source_target_pairs={{0,1},{1,0},{2,3},{3,2},{4,5},{5,4},{6,7},{7,6},{8,9},{9,8},{10,11... | collective-permute-start | bytes 49160 | tf_op jit(solution)/shard_map/ppermute | solution.py:42
  24.6 2.2 %collective-permute-start.3 = (f32[32,1,128]{2,1,0:T(1,128)S(1)}, f32[32,1,128]{2,1,0:T(1,128)S(1)}, u32[]{:S(2)}, u32[]{:S(2)}) collective-permute-start(f32[32,1,128]{2,1,0:T(1,128)S(1)} %get-tuple-element.40), channel_id=1, source_target_pairs={{1,2},{2,1},{3,0},{0,3},{5,6},{6,5},{7,4},{4,7},{9,10},{10,9},{11,... | collective-permute-start | bytes 49160 | tf_op jit(solution)/shard_map/ppermute | solution.py:51
  26.8 1.3 %pad_select_fusion.1 = (f32[1,65,128]{2,1,0:T(8,128)S(1)}, f32[1,65,128]{2,1,0:T(8,128)S(1)}) fusion(f32[1,64,128]{2,1,0:T(8,128)S(1)} %get-tuple-element.38, f32[]{:T(128)} %bitcast.33, f32[1,64,128]{2,1,0:T(8,128)S(1)} %get-tuple-element.37, f32[]{:T(128)} %bitcast.32, pred[]{:T(512)S(6)} %eq.420), kind=kLoop, calls=%fused_computation.144 | loop fusion | flops 16640 | bytes 132105 | tf_op jit(solution)/shard_map/jit(_where)/select_n | solution.py:43
  28.1 1.5 %collective-permute-start = (f32[1,65,128]{2,1,0:T(8,128)S(1)}, f32[1,65,128]{2,1,0:T(8,128)S(1)}, u32[]{:S(2)}, u32[]{:S(2)}) collective-permute-start(f32[1,65,128]{2,1,0:T(8,128)S(1)} %get-tuple-element.48), channel_id=1, source_target_pairs={{0,4},{4,0},{8,12},{12,8},{1,5},{5,1},{9,13},{13,9},{2,6},{6,2},{1... | collective-permute-start | bytes 99848 | tf_op jit(solution)/shard_map/ppermute | solution.py:42
  29.6 1.9 %collective-permute-start.1 = (f32[1,65,128]{2,1,0:T(8,128)S(1)}, f32[1,65,128]{2,1,0:T(8,128)S(1)}, u32[]{:S(2)}, u32[]{:S(2)}) collective-permute-start(f32[1,65,128]{2,1,0:T(8,128)S(1)} %get-tuple-element.49), channel_id=1, source_target_pairs={{4,8},{8,4},{5,9},{9,5},{6,10},{10,6},{7,11},{11,7},{20,24},{24,20... | collective-permute-start | bytes 99848 | tf_op jit(solution)/shard_map/ppermute | solution.py:51
  31.6 3.3 %collective-permute-done.1 = f32[1,65,128]{2,1,0:T(8,128)S(1)} collective-permute-done((f32[1,65,128]{2,1,0:T(8,128)S(1)}, f32[1,65,128]{2,1,0:T(8,128)S(1)}, u32[]{:S(2)}, u32[]{:S(2)}) %collective-permute-start.1) | collective-permute-done | bytes 33312 | tf_op jit(solution)/shard_map/ppermute | solution.py:51
  36.9 1.4 %gather_fusion.1 = f32[16,64,128]{2,1,0:T(8,128)} fusion(f32[32,64,128]{2,1,0:T(8,128)S(1)} %bitcast.206, s32[1024]{0:T(1024)S(1)} %pad_clamp_fusion), kind=kCustom, calls=%fused_computation.1 | custom fusion | bytes 1048640 | tf_op jit(solution)/shard_map/gather | solution.py:241
  38.3 3.6 %all-to-all-start.1 = ((f32[4,4,64,128]{3,2,1,0:T(8,128)}), f32[4,4,64,128]{3,2,1,0:T(8,128)S(1)}, u32[]{:S(2)}, u32[]{:S(2)}) async-start(f32[4,4,64,128]{3,2,1,0:T(8,128)} %bitcast.40), calls=%async_computation.1 | async-start | bytes 1048576 | tf_op jit(solution)/shard_map/all_to_all | solution.py:247
  42.0 1.4 %maximum_multiply_fusion = f32[34]{0:T(128)S(1)} fusion(f32[1]{0:T(128)} %bitcast.45, f32[32]{0:T(128)S(1)} %copy-done.3, f32[1]{0:T(128)} %bitcast.44, s32[]{:T(128)S(6)} %sub.188), kind=kLoop, calls=%fused_computation.325 | loop fusion | flops 272 | bytes 276 | tf_op jit(solution)/shard_map/mul | solution.py:291
  43.9 1.6 %convolution_bitcast_fusion = f32[32,64,1]{1,2,0:T(1,128)S(1)} fusion(f32[32,64,1]{1,2,0:T(1,128)S(1)} %bitcast.228, f32[64,64]{1,0:T(8,128)S(1)} %get-tuple-element.101, f32[32]{0:T(128)S(1)} %get-tuple-element.115, f32[64,64]{1,0:T(8,128)S(1)} %get-tuple-element.102, f32[32]{0:T(128)S(1)} %get-tuple-element.116, f32[64,64]{1,0:T(8,128)S(1)} %get-tuple-element.103, ...), kind=kOutput, calls=%fused_computation.6 | convolution fusion | flops 3538944 | bytes 148480 | tf_op jit(solution)/shard_map/pi,pij->pj/dot_general | solution.py:294
  46.3 1.5 %all-to-all-done.1 = f32[4,4,64,128]{3,2,1,0:T(8,128)S(1)} async-done(((f32[4,4,64,128]{3,2,1,0:T(8,128)}), f32[4,4,64,128]{3,2,1,0:T(8,128)S(1)}, u32[]{:S(2)}, u32[]{:S(2)}) %all-to-all-start.1) | async-done | bytes 524320 | tf_op jit(solution)/shard_map/all_to_all | solution.py:247
  48.8 1.0 %fusion.184 = f32[32,1,128]{2,1,0:T(1,128)S(1)} fusion(f32[32,64,1]{1,2,0:T(1,128)S(1)} %convolution_bitcast_fusion, f32[32,64,128]{2,1,0:T(8,128)S(1)} %bitcast.215), kind=kOutput, calls=%fused_computation.390 | convolution fusion | flops 3145728 | bytes 1073152 | tf_op jit(solution)/shard_map/pj,pjv->pv/dot_general | solution.py:297
  50.8 4.5 %all-to-all-start.2 = ((f32[16,6,128]{2,1,0:T(8,128)}), f32[16,6,128]{2,1,0:T(8,128)S(1)}, u32[]{:S(2)}, u32[]{:S(2)}) async-start(f32[16,6,128]{2,1,0:T(8,128)} %broadcast_in_dim.38), calls=%async_computation.2 | async-start | bytes 131072 | tf_op jit(solution)/shard_map/all_to_all | solution.py:308
  55.3 1.8 %fusion.31 = f32[32,64,128]{2,1,0:T(8,128)S(1)} fusion(f32[32,64,128]{2,1,0:T(8,128)S(1)} %bitcast.216, f32[64,64]{1,0:T(8,128)S(1)} %get-tuple-element.101, f32[32]{0:T(128)S(1)} %get-tuple-element.115, f32[64,64]{1,0:T(8,128)S(1)} %get-tuple-element.102, f32[32]{0:T(128)S(1)} %get-tuple-element.116, f32[64,64]{1,0:T(8,128)S(1)} %get-tuple-element.103, ...), kind=kOutput, calls=%fused_computation.58 | convolution fusion | flops 203292672 | bytes 2229248 | tf_op jit(solution)/shard_map/nij,njv->niv/dot_general | solution.py:287
  57.3 4.4 %all-to-all-done.2 = f32[16,6,128]{2,1,0:T(8,128)S(1)} async-done(((f32[16,6,128]{2,1,0:T(8,128)}), f32[16,6,128]{2,1,0:T(8,128)S(1)}, u32[]{:S(2)}, u32[]{:S(2)}) %all-to-all-start.2) | async-done | bytes 49184 | tf_op jit(solution)/shard_map/all_to_all | solution.py:308
  62.1 1.0 %multiply_add_fusion.2 = f32[4,8,8,8,32]{4,3,2,1,0:T(8,128)S(1)} fusion(f32[4,8,8,8,128]{4,3,2,1,0:T(8,128)S(1)} %bitcast.203, f32[4,8]{1,0:T(4,128)S(1)} %get-tuple-element.60, f32[4,8]{1,0:T(4,128)S(1)} %get-tuple-element.61, f32[4,8]{1,0:T(4,128)S(1)} %get-tuple-element.62, f32[4,8]{1,0:T(4,128)S(1)} %get-tuple-element.63), kind=kLoop, calls=%fused_computation.33 | loop fusion | flops 458752 | bytes 1311232 | tf_op jit(solution)/shard_map/add | solution.py:182
  63.1 1.2 %multiply_add_fusion.3 = (f32[4,8,8,8,32]{4,3,2,1,0:T(8,128)S(1)}, f32[4,8,8,8,32]{4,3,2,1,0:T(8,128)S(1)}, f32[4,8,8,8,32]{4,3,2,1,0:T(8,128)S(1)}) fusion(f32[4,8,8,8,128]{4,3,2,1,0:T(8,128)S(1)} %bitcast.204, f32[4,8]{1,0:T(4,128)S(1)} %get-tuple-element.64, f32[4,8]{1,0:T(4,128)S(1)} %get-tuple-element.65, f32[4,8]{1,0:T(4,128)S(1)} %get-tuple-element.54, ...), kind=kLoop, calls=%fused_computation.34 | loop fusion | flops 851968 | bytes 1836032 | tf_op jit(solution)/shard_map/add | solution.py:182
  64.3 0.9 %pad_maximum_fusion.9 = f32[4,8,8,8,128]{4,3,2,1,0:T(8,128)S(1)} fusion(f32[4,8,8,8,32]{4,3,2,1,0:T(8,128)S(1)} %get-tuple-element.36, f32[4,8,8,8,32]{4,3,2,1,0:T(8,128)S(1)} %get-tuple-element.35, f32[4,8,8,8,32]{4,3,2,1,0:T(8,128)S(1)} %multiply_add_fusion.2, f32[4,8,8,8,32]{4,3,2,1,0:T(8,128)S(1)} %get-tuple-element.34), kind=kLoop, calls=%fused_computation.30 | loop fusion | flops 786432 | bytes 2097152 | tf_op jit(solution)/shard_map/concatenate | solution.py:184
  65.3 1.4 %collective-permute-start.7 = (f32[32,1,128]{2,1,0:T(1,128)S(1)}, f32[32,1,128]{2,1,0:T(1,128)S(1)}, u32[]{:S(2)}, u32[]{:S(2)}) collective-permute-start(f32[32,1,128]{2,1,0:T(1,128)S(1)} %get-tuple-element.33), channel_id=1, source_target_pairs={{1,2},{2,1},{3,0},{0,3},{5,6},{6,5},{7,4},{4,7},{9,10},{10,9},{11,... | collective-permute-start | bytes 49160 | tf_op jit(solution)/shard_map/ppermute | solution.py:51
  66.8 1.0 %collective-permute-start.4 = (f32[1,64,128]{2,1,0:T(8,128)S(1)}, f32[1,64,128]{2,1,0:T(8,128)S(1)}, u32[]{:S(2)}, u32[]{:S(2)}) collective-permute-start(f32[1,64,128]{2,1,0:T(8,128)S(1)} %get-tuple-element.30), channel_id=1, source_target_pairs={{0,4},{4,0},{8,12},{12,8},{1,5},{5,1},{9,13},{13,9},{2,6},{6,2},{1... | collective-permute-start | bytes 98312 | tf_op jit(solution)/shard_map/ppermute | solution.py:42
  67.8 2.3 %collective-permute-start.5 = (f32[1,64,128]{2,1,0:T(8,128)S(1)}, f32[1,64,128]{2,1,0:T(8,128)S(1)}, u32[]{:S(2)}, u32[]{:S(2)}) collective-permute-start(f32[1,64,128]{2,1,0:T(8,128)S(1)} %get-tuple-element.31), channel_id=1, source_target_pairs={{4,8},{8,4},{5,9},{9,5},{6,10},{10,6},{7,11},{11,7},{20,24},{24,20... | collective-permute-start | bytes 98312 | tf_op jit(solution)/shard_map/ppermute | solution.py:51
  70.1 2.9 %collective-permute-done.5 = f32[1,64,128]{2,1,0:T(8,128)S(1)} collective-permute-done((f32[1,64,128]{2,1,0:T(8,128)S(1)}, f32[1,64,128]{2,1,0:T(8,128)S(1)}, u32[]{:S(2)}, u32[]{:S(2)}) %collective-permute-start.5) | collective-permute-done | bytes 32800 | tf_op jit(solution)/shard_map/ppermute | solution.py:51
  73.0 1.4 %fusion.6 = f32[32,64,128]{2,1,0:T(8,128)} fusion(f32[32,64,128]{2,1,0:T(8,128)S(1)} %bitcast.209, f32[32,1,128]{2,1,0:T(1,128)S(1)} %bitcast.227, f32[32,1,128]{2,1,0:T(1,128)S(1)} %bitcast.226, f32[1,64,128]{2,1,0:T(8,128)S(1)} %get-tuple-element.47, f32[1,64,128]{2,1,0:T(8,128)S(1)} %get-tuple-element.46, f32[128]{0:T(128)S(1)} %get-tuple-element.90, ...), kind=kLoop, calls=%fused_computation.13 | loop fusion | flops 3145728 | bytes 2196096 | tf_op jit(solution)/shard_map/mul | solution.py:325
  (120 shorter events, 12.7 us)
Async XLA Ops:
  0.0 1.4 %copy-start.2 = (s32[2,16,32]{2,1,0:T(8,128)S(1)}, s32[2,16,32]{2,1,0:T(8,128)}, u32[]{:S(2)}) copy-start(s32[2,16,32]{2,1,0:T(8,128)} %param.7) | copy-start | bytes 12292
  3.8 4.5 %copy-start.1 = (f32[2,3,16,32]{3,2,1,0:T(8,128)S(1)}, f32[2,3,16,32]{3,2,1,0:T(8,128)}, u32[]{:S(2)}) copy-start(f32[2,3,16,32]{3,2,1,0:T(8,128)} %param.5) | copy-start | bytes 36868
  3.8 12.2 %all-to-all-start = ((f32[4,4,64,128]{3,2,1,0:T(8,128)}), f32[4,4,64,128]{3,2,1,0:T(8,128)S(1)}, u32[]{:S(2)}, u32[]{:S(2)}) async-start(f32[4,4,64,128]{3,2,1,0:T(8,128)} %bitcast.17), calls=%async_computation | async-start | bytes 1048576 | tf_op jit(solution)/shard_map/all_to_all | solution.py:247
  11.7 0.7 copy-start.3
  22.2 13.9 %copy-start = (f32[32,64,128]{2,1,0:T(8,128)S(1)}, f32[32,64,128]{2,1,0:T(8,128)}, u32[]{:S(2)}) copy-start(f32[32,64,128]{2,1,0:T(8,128)} %param.4) | copy-start | bytes 3145732
  22.4 9.2 %collective-permute-start.2 = (f32[32,1,128]{2,1,0:T(1,128)S(1)}, f32[32,1,128]{2,1,0:T(1,128)S(1)}, u32[]{:S(2)}, u32[]{:S(2)}) collective-permute-start(f32[32,1,128]{2,1,0:T(1,128)S(1)} %get-tuple-element.39), channel_id=1, source_target_pairs={{0,1},{1,0},{2,3},{3,2},{4,5},{5,4},{6,7},{7,6},{8,9},{9,8},{10,11... | collective-permute-start | bytes 49160 | tf_op jit(solution)/shard_map/ppermute | solution.py:42
  24.6 6.9 %collective-permute-start.3 = (f32[32,1,128]{2,1,0:T(1,128)S(1)}, f32[32,1,128]{2,1,0:T(1,128)S(1)}, u32[]{:S(2)}, u32[]{:S(2)}) collective-permute-start(f32[32,1,128]{2,1,0:T(1,128)S(1)} %get-tuple-element.40), channel_id=1, source_target_pairs={{1,2},{2,1},{3,0},{0,3},{5,6},{6,5},{7,4},{4,7},{9,10},{10,9},{11,... | collective-permute-start | bytes 49160 | tf_op jit(solution)/shard_map/ppermute | solution.py:51
  28.1 3.5 %collective-permute-start = (f32[1,65,128]{2,1,0:T(8,128)S(1)}, f32[1,65,128]{2,1,0:T(8,128)S(1)}, u32[]{:S(2)}, u32[]{:S(2)}) collective-permute-start(f32[1,65,128]{2,1,0:T(8,128)S(1)} %get-tuple-element.48), channel_id=1, source_target_pairs={{0,4},{4,0},{8,12},{12,8},{1,5},{5,1},{9,13},{13,9},{2,6},{6,2},{1... | collective-permute-start | bytes 99848 | tf_op jit(solution)/shard_map/ppermute | solution.py:42
  29.6 5.3 %collective-permute-start.1 = (f32[1,65,128]{2,1,0:T(8,128)S(1)}, f32[1,65,128]{2,1,0:T(8,128)S(1)}, u32[]{:S(2)}, u32[]{:S(2)}) collective-permute-start(f32[1,65,128]{2,1,0:T(8,128)S(1)} %get-tuple-element.49), channel_id=1, source_target_pairs={{4,8},{8,4},{5,9},{9,5},{6,10},{10,6},{7,11},{11,7},{20,24},{24,20... | collective-permute-start | bytes 99848 | tf_op jit(solution)/shard_map/ppermute | solution.py:51
  38.3 9.5 %all-to-all-start.1 = ((f32[4,4,64,128]{3,2,1,0:T(8,128)}), f32[4,4,64,128]{3,2,1,0:T(8,128)S(1)}, u32[]{:S(2)}, u32[]{:S(2)}) async-start(f32[4,4,64,128]{3,2,1,0:T(8,128)} %bitcast.40), calls=%async_computation.1 | async-start | bytes 1048576 | tf_op jit(solution)/shard_map/all_to_all | solution.py:247
  50.8 10.8 %all-to-all-start.2 = ((f32[16,6,128]{2,1,0:T(8,128)}), f32[16,6,128]{2,1,0:T(8,128)S(1)}, u32[]{:S(2)}, u32[]{:S(2)}) async-start(f32[16,6,128]{2,1,0:T(8,128)} %broadcast_in_dim.38), calls=%async_computation.2 | async-start | bytes 131072 | tf_op jit(solution)/shard_map/all_to_all | solution.py:308
  65.2 4.9 %collective-permute-start.6 = (f32[32,1,128]{2,1,0:T(1,128)S(1)}, f32[32,1,128]{2,1,0:T(1,128)S(1)}, u32[]{:S(2)}, u32[]{:S(2)}) collective-permute-start(f32[32,1,128]{2,1,0:T(1,128)S(1)} %get-tuple-element.32), channel_id=1, source_target_pairs={{0,1},{1,0},{2,3},{3,2},{4,5},{5,4},{6,7},{7,6},{8,9},{9,8},{10,11... | collective-permute-start | bytes 49160 | tf_op jit(solution)/shard_map/ppermute | solution.py:42
  65.3 4.8 %collective-permute-start.7 = (f32[32,1,128]{2,1,0:T(1,128)S(1)}, f32[32,1,128]{2,1,0:T(1,128)S(1)}, u32[]{:S(2)}, u32[]{:S(2)}) collective-permute-start(f32[32,1,128]{2,1,0:T(1,128)S(1)} %get-tuple-element.33), channel_id=1, source_target_pairs={{1,2},{2,1},{3,0},{0,3},{5,6},{6,5},{7,4},{4,7},{9,10},{10,9},{11,... | collective-permute-start | bytes 49160 | tf_op jit(solution)/shard_map/ppermute | solution.py:51
  66.8 3.3 %collective-permute-start.4 = (f32[1,64,128]{2,1,0:T(8,128)S(1)}, f32[1,64,128]{2,1,0:T(8,128)S(1)}, u32[]{:S(2)}, u32[]{:S(2)}) collective-permute-start(f32[1,64,128]{2,1,0:T(8,128)S(1)} %get-tuple-element.30), channel_id=1, source_target_pairs={{0,4},{4,0},{8,12},{12,8},{1,5},{5,1},{9,13},{13,9},{2,6},{6,2},{1... | collective-permute-start | bytes 98312 | tf_op jit(solution)/shard_map/ppermute | solution.py:42
  67.8 5.2 %collective-permute-start.5 = (f32[1,64,128]{2,1,0:T(8,128)S(1)}, f32[1,64,128]{2,1,0:T(8,128)S(1)}, u32[]{:S(2)}, u32[]{:S(2)}) collective-permute-start(f32[1,64,128]{2,1,0:T(8,128)S(1)} %get-tuple-element.31), channel_id=1, source_target_pairs={{4,8},{8,4},{5,9},{9,5},{6,10},{10,6},{7,11},{11,7},{20,24},{24,20... | collective-permute-start | bytes 98312 | tf_op jit(solution)/shard_map/ppermute | solution.py:51

commit v24 on v22

--- a/solution.py
+++ b/solution.py
@@ -208,7 +208,7 @@
     return advected + diffusivity[:, None, None] * laplace, k_wide
 
 
-def departed(state_field, source_ids, shifts_now, premix=False):
+def departed(state_field, source_ids, shifts_now, parts=False):
     lat_count = lax.axis_size("lat")
     lat_index = lax.axis_index("lat")
     lon_index = lax.axis_index("lon")
@@ -255,15 +255,13 @@
         own_patches.reshape(per_device, -1),
         precision=lax.Precision.HIGHEST,
     ).reshape(per_device, 64, value_count)
-    if premix:
-        near = levels(near, my_frac[2])
-        slot_z = jnp.sum(jnp.where(take_far, my_frac[2][:, None], 0.0), axis=0)
-        arrived = levels(arrived, slot_z)
     patches = near + jnp.dot(
         take_far.astype(jnp.float32),
         arrived.reshape(lat_count * CAP, -1),
         precision=lax.Precision.HIGHEST,
     ).reshape(per_device, 64, value_count)
+    if parts:
+        return patches, my_frac, (near, take_far.astype(jnp.float32), arrived)
     return patches, my_frac
 
 
@@ -279,12 +277,14 @@
     weights = column_area(lat_index * row_count, row_count, total_rows)
     target_part = column_mass(tracers, weights)
 
-    patches, frac = departed(tracers, source_patch[0], shifts[0], premix=True)
-    advected = from_patches(spatial(patches, frac[0], frac[1]), band_rows, band_cols)
+    patches, frac = departed(tracers, source_patch[0], shifts[0])
+    advected = from_patches(levels(spatial(patches, frac[0], frac[1]), frac[2]), band_rows, band_cols)
     first, k_wide = diffuse_first(advected, diffusivity)
     first_part = column_mass(first, weights)
 
-    patches, frac = departed(first, source_patch[1], shifts[1])
+    patches, frac, (near, take_far, arrived) = departed(
+        first, source_patch[1], shifts[1], parts=True
+    )
     plane = plane_weights(frac[0], frac[1])
     planar = jnp.einsum("nij,njv->niv", plane, patches, precision=lax.Precision.HIGHEST)
     weight_z = cubic_matrix(frac[2], LEV)
@@ -296,11 +296,19 @@
     row_weights = jnp.einsum(
         "pi,pij->pj", g_cols.reshape(per_device, 64), plane, precision=lax.Precision.HIGHEST
     )
-    weighted = jnp.einsum(
-        "pj,pjv->pv", row_weights, patches, precision=lax.Precision.HIGHEST
-    ).reshape(per_device, LEV, per_level)
-    mix_part = jnp.einsum(
-        "plm,pmt->lmt", weight_z, weighted, precision=lax.Precision.HIGHEST
+    hi = lax.Precision.HIGHEST
+    weighted_near = jnp.einsum("pj,pjv->pv", row_weights, near, precision=hi)
+    mix_near = jnp.einsum(
+        "plm,pmt->lmt", weight_z, weighted_near.reshape(per_device, LEV, per_level), precision=hi
+    )
+    slot_rows = jnp.einsum("ps,pj->sj", take_far, row_weights, precision=hi)
+    slot_z = jnp.einsum("ps,plm->slm", take_far, weight_z, precision=hi)
+    weighted_far = jnp.einsum("sj,sjv->sv", slot_rows, arrived, precision=hi)
+    mix_part = mix_near + jnp.einsum(
+        "slm,smt->lmt",
+        slot_z,
+        weighted_far.reshape(slot_z.shape[0], LEV, per_level),
+        precision=hi,
     )
     field_planar = lax.optimization_barrier(from_patches(planar, band_rows, band_cols))
     partial = jnp.concatenate([target_part, first_part, mix_part.reshape(-1)])

time: 81 us -> 76.3 us (0.942)
  starting transfers between devices: 27 us -> 25 us
  other arithmetic: 15.4 us -> 13.7 us
  local copies, waits for them, and re-layouts: 13.1 us -> 11.8 us
  waiting for transfers between devices: 12 us -> 13.2 us
    add x4 -> x2, other arithmetic: 4.38 us -> 2.42 us  [levels(): acc = term if acc is None else acc + term]
    unnamed x10 -> x6, local copies, waits for them, and re-layouts: 2.25 us -> 0.66 us
    ppermute x4, waiting for transfers between devices: 4.69 us -> 6.27 us  [neighbour_halos(): second = lax.ppermute(jnp.where(even, lo_edge, hi_edge), axis, pairs)]
    ppermute x4, starting transfers between devices: 9.26 us -> 7.68 us  [neighbour_halos(): second = lax.ppermute(jnp.where(even, lo_edge, hi_edge), axis, pairs)]
    dot_general x2, matrix products: 3.13 us -> 1.66 us  [departed(): jnp.dot(take_far.astype(jnp.float32), arrived.reshape(lat_count * CAP, -1...]
    ppermute x4, starting transfers between devices: 3.81 us -> 4.81 us  [neighbour_halos(): lax.ppermute(jnp.where(even, hi_edge, lo_edge), axis, [(i, i ^ 1) for i i...]
    all_to_all x1, starting transfers between devices: 5.4 us -> 4.45 us  [local(): lax.all_to_all(jnp.broadcast_to(partial, (members,) + partial.shape), ('l...]
    dot_general x2 -> x6, matrix products: 1.65 us -> 2.59 us  [the longest x1 1.48 us: local(): weighted_near = jnp.einsum('pj,pjv->pv', row_weights, near, precision=hi)]
  transfers between devices with their start and end apart: 11 -> 11, of which waited for: 4 -> 5; matrix products, arithmetic and copies ran while one was open for 17% -> 18% of each run, Pallas kernels for 0% -> 0%
where the time goes in v24:
time: 76.3 us; the launch traced here: 75.8 us
  starting transfers between devices  25 us (33%)
  other arithmetic  13.7 us (18%)
  waiting for transfers between devices  13.2 us (17%)
  local copies, waits for them, and re-layouts  11.8 us (15%)
  matrix products  11.5 us (15%)
    all_to_all x2, starting transfers between devices, departed(): lax.all_to_all(outgoing, 'lat', 0, 0, tiled=True)  8.04 us
    ppermute x4, starting transfers between devices, neighbour_halos(): second = lax.ppermute(jnp.where(even, lo_edge, hi_edge), axis, pairs)  7.68 us
    ppermute x4, waiting for transfers between devices, neighbour_halos(): second = lax.ppermute(jnp.where(even, lo_edge, hi_edge), axis, pairs)  6.27 us
    ppermute x4, starting transfers between devices, neighbour_halos(): lax.ppermute(jnp.where(even, hi_edge, lo_edge), axis, [(i, i ^ 1) for i i...  4.81 us
    all_to_all x1, starting transfers between devices, local(): lax.all_to_all(jnp.broadcast_to(partial, (members,) + partial.shape), ('l...  4.45 us
    all_to_all x2, waiting for transfers between devices, departed(): lax.all_to_all(outgoing, 'lat', 0, 0, tiled=True)  3.83 us
    all_to_all x1, waiting for transfers between devices, local(): lax.all_to_all(jnp.broadcast_to(partial, (members,) + partial.shape), ('l...  3.12 us
    gather x2, local copies, waits for them, and re-layouts, departed(): own_patches[send_local.reshape(-1)].reshape(lat_count, CAP, 64, value_count)  2.75 us
  transfers between devices with their start and end apart: 11, of which 5 were waited for; matrix products, arithmetic and copies ran while one was open for 18% of the time, Pallas kernels for 0%

profile of v24, /device:TPU:1, one launch (start us, length us, event | category | flops | bytes accessed | tf_op | source)
XLA Modules:
  0.0 75.8 jit_solution(8871217842999302866)
XLA Ops:
  1.7 1.4 %copy.65 = f32[4,8,8,8,128]{4,3,2,1,0:T(8,128)S(1)} copy(f32[4,8,8,8,128]{4,3,1,2,0:T(8,128)} %bitcast.256) | data formatting | bytes 2097152 | tf_op jit(solution)/shard_map/transpose | solution.py:131
  3.1 1.4 %gather_fusion = f32[16,64,128]{2,1,0:T(8,128)} fusion(f32[32,64,128]{2,1,0:T(8,128)S(1)} %bitcast.244, s32[1024]{0:T(1024)S(1)} %pad_clamp_fusion.1), kind=kCustom, calls=%fused_computation | custom fusion | bytes 1048640 | tf_op jit(solution)/shard_map/gather | solution.py:241
  4.5 4.4 %all-to-all-start = ((f32[4,4,64,128]{3,2,1,0:T(8,128)}), f32[4,4,64,128]{3,2,1,0:T(8,128)S(1)}, u32[]{:S(2)}, u32[]{:S(2)}) async-start(f32[4,4,64,128]{3,2,1,0:T(8,128)} %bitcast.21), calls=%async_computation | async-start | bytes 1048576 | tf_op jit(solution)/shard_map/all_to_all | solution.py:247
  14.6 2.0 %all-to-all-done = f32[4,4,64,128]{3,2,1,0:T(8,128)S(1)} async-done(((f32[4,4,64,128]{3,2,1,0:T(8,128)}), f32[4,4,64,128]{3,2,1,0:T(8,128)S(1)}, u32[]{:S(2)}, u32[]{:S(2)}) %all-to-all-start) | async-done | bytes 524320 | tf_op jit(solution)/shard_map/all_to_all | solution.py:247
  17.5 2.2 %fusion.24 = f32[32,64,128]{2,1,0:T(8,128)S(1)} fusion(f32[32,64,128]{2,0,1:T(8,128)S(1)} %convolution_add_fusion.1, f32[32]{0:T(128)S(1)} %get-tuple-element.124, f32[32]{0:T(128)S(1)} %get-tuple-element.125, f32[32]{0:T(128)S(1)} %get-tuple-element.123, f32[32]{0:T(128)S(1)} %get-tuple-element.88, f32[32]{0:T(128)S(1)} %get-tuple-element.121, ...), kind=kOutput, calls=%fused_computation.39 | convolution fusion | flops 203292672 | bytes 2229248 | tf_op jit(solution)/shard_map/nij,njv->niv/dot_general | solution.py:103
  19.7 1.1 %multiply_add_fusion.6 = f32[32,64,32]{2,1,0:T(8,128)S(1)} fusion(f32[32,64,128]{2,1,0:T(8,128)S(1)} %fusion.24, f32[32]{0:T(128)S(1)} %get-tuple-element.78, f32[32]{0:T(128)S(1)} %get-tuple-element.79, f32[32]{0:T(128)S(1)} %get-tuple-element.80, f32[32]{0:T(128)S(1)} %get-tuple-element.81), kind=kLoop, calls=%fused_computation.49 | loop fusion | flops 458752 | bytes 1311232 | tf_op jit(solution)/shard_map/add | solution.py:121
  20.9 1.3 %multiply_add_fusion.7 = (f32[32,64,32]{2,1,0:T(8,128)S(1)}, f32[32,64,32]{2,1,0:T(8,128)S(1)}, f32[32,64,32]{2,1,0:T(8,128)S(1)}) fusion(f32[32,64,128]{2,1,0:T(8,128)S(1)} %fusion.24, f32[32]{0:T(128)S(1)} %get-tuple-element.82, f32[32]{0:T(128)S(1)} %get-tuple-element.83, f32[32]{0:T(128)S(1)} %get-tuple-element.72, f32[32]{0:T(128)S(1)} %get-tuple-element.75, ...), kind=kLoop, calls=%fused_computation.50 | loop fusion | flops 851968 | bytes 1836032 | tf_op jit(solution)/shard_map/add | solution.py:121
  22.2 0.9 %pad_maximum_fusion.8 = f32[32,64,128]{2,1,0:T(8,128)S(1)} fusion(f32[32,64,32]{2,1,0:T(8,128)S(1)} %get-tuple-element.43, f32[32,64,32]{2,1,0:T(8,128)S(1)} %get-tuple-element.42, f32[32,64,32]{2,1,0:T(8,128)S(1)} %multiply_add_fusion.6, f32[32,64,32]{2,1,0:T(8,128)S(1)} %get-tuple-element.41), kind=kLoop, calls=%fused_computation.33 | loop fusion | flops 786432 | bytes 2097152 | tf_op jit(solution)/shard_map/concatenate | solution.py:123
  23.3 2.2 %collective-permute-start.2 = (f32[32,1,128]{2,1,0:T(1,128)S(1)}, f32[32,1,128]{2,1,0:T(1,128)S(1)}, u32[]{:S(2)}, u32[]{:S(2)}) collective-permute-start(f32[32,1,128]{2,1,0:T(1,128)S(1)} %get-tuple-element.39), channel_id=1, source_target_pairs={{0,1},{1,0},{2,3},{3,2},{4,5},{5,4},{6,7},{7,6},{8,9},{9,8},{10,11... | collective-permute-start | bytes 49160 | tf_op jit(solution)/shard_map/ppermute | solution.py:42
  25.5 2.2 %collective-permute-start.3 = (f32[32,1,128]{2,1,0:T(1,128)S(1)}, f32[32,1,128]{2,1,0:T(1,128)S(1)}, u32[]{:S(2)}, u32[]{:S(2)}) collective-permute-start(f32[32,1,128]{2,1,0:T(1,128)S(1)} %get-tuple-element.40), channel_id=1, source_target_pairs={{1,2},{2,1},{3,0},{0,3},{5,6},{6,5},{7,4},{4,7},{9,10},{10,9},{11,... | collective-permute-start | bytes 49160 | tf_op jit(solution)/shard_map/ppermute | solution.py:51
  27.7 1.3 %pad_select_fusion.1 = (f32[1,65,128]{2,1,0:T(8,128)S(1)}, f32[1,65,128]{2,1,0:T(8,128)S(1)}) fusion(f32[1,64,128]{2,1,0:T(8,128)S(1)} %get-tuple-element.38, f32[]{:T(128)} %bitcast.38, f32[1,64,128]{2,1,0:T(8,128)S(1)} %get-tuple-element.37, f32[]{:T(128)} %bitcast.37, pred[]{:T(512)S(6)} %eq.420), kind=kLoop, calls=%fused_computation.156 | loop fusion | flops 16640 | bytes 132105 | tf_op jit(solution)/shard_map/jit(_where)/select_n | solution.py:43
  29.0 1.5 %collective-permute-start = (f32[1,65,128]{2,1,0:T(8,128)S(1)}, f32[1,65,128]{2,1,0:T(8,128)S(1)}, u32[]{:S(2)}, u32[]{:S(2)}) collective-permute-start(f32[1,65,128]{2,1,0:T(8,128)S(1)} %get-tuple-element.48), channel_id=1, source_target_pairs={{0,4},{4,0},{8,12},{12,8},{1,5},{5,1},{9,13},{13,9},{2,6},{6,2},{1... | collective-permute-start | bytes 99848 | tf_op jit(solution)/shard_map/ppermute | solution.py:42
  30.5 1.9 %collective-permute-start.1 = (f32[1,65,128]{2,1,0:T(8,128)S(1)}, f32[1,65,128]{2,1,0:T(8,128)S(1)}, u32[]{:S(2)}, u32[]{:S(2)}) collective-permute-start(f32[1,65,128]{2,1,0:T(8,128)S(1)} %get-tuple-element.49), channel_id=1, source_target_pairs={{4,8},{8,4},{5,9},{9,5},{6,10},{10,6},{7,11},{11,7},{20,24},{24,20... | collective-permute-start | bytes 99848 | tf_op jit(solution)/shard_map/ppermute | solution.py:51
  32.4 3.3 %collective-permute-done.1 = f32[1,65,128]{2,1,0:T(8,128)S(1)} collective-permute-done((f32[1,65,128]{2,1,0:T(8,128)S(1)}, f32[1,65,128]{2,1,0:T(8,128)S(1)}, u32[]{:S(2)}, u32[]{:S(2)}) %collective-permute-start.1) | collective-permute-done | bytes 33312 | tf_op jit(solution)/shard_map/ppermute | solution.py:51
  36.8 1.4 %maximum_multiply_fusion = f32[34]{0:T(128)S(1)} fusion(f32[1]{0:T(128)} %bitcast.53, f32[32]{0:T(128)S(1)} %copy-done.2, f32[1]{0:T(128)} %bitcast.52, s32[]{:T(128)S(6)} %sub.188), kind=kLoop, calls=%fused_computation.348 | loop fusion | flops 272 | bytes 276 | tf_op jit(solution)/shard_map/mul | solution.py:293
  39.9 1.4 %gather_fusion.1 = f32[16,64,128]{2,1,0:T(8,128)} fusion(f32[32,64,128]{2,1,0:T(8,128)S(1)} %bitcast.245, s32[1024]{0:T(1024)S(1)} %pad_clamp_fusion), kind=kCustom, calls=%fused_computation.1 | custom fusion | bytes 1048640 | tf_op jit(solution)/shard_map/gather | solution.py:241
  41.3 3.6 %all-to-all-start.1 = ((f32[4,4,64,128]{3,2,1,0:T(8,128)}), f32[4,4,64,128]{3,2,1,0:T(8,128)S(1)}, u32[]{:S(2)}, u32[]{:S(2)}) async-start(f32[4,4,64,128]{3,2,1,0:T(8,128)} %bitcast.47), calls=%async_computation.1 | async-start | bytes 1048576 | tf_op jit(solution)/shard_map/all_to_all | solution.py:247
  45.6 1.5 %fusion.41 = f32[32,1,64]{2,1,0:T(1,128)S(1)} fusion(f32[32,64,1]{1,2,0:T(1,128)S(1)} %bitcast.268, f32[64,64]{1,0:T(8,128)S(1)} %get-tuple-element.99, f32[32]{0:T(128)S(1)} %get-tuple-element.113, f32[64,64]{1,0:T(8,128)S(1)} %get-tuple-element.100, f32[32]{0:T(128)S(1)} %get-tuple-element.114, f32[64,64]{1,0:T(8,128)S(1)} %get-tuple-element.101, ...), kind=kOutput, calls=%fused_computation.67 | convolution fusion | flops 3538944 | bytes 148480 | tf_op jit(solution)/shard_map/pi,pij->pj/dot_general | solution.py:296
  47.1 1.5 %fusion.20 = f32[32,1,128]{2,1,0:T(1,128)S(1)} fusion(f32[32,64,128]{2,0,1:T(8,128)S(1)} %fusion.1, f32[32,1,64]{2,1,0:T(1,128)S(1)} %fusion.41), kind=kOutput, calls=%fused_computation.35 | convolution fusion | flops 3145728 | bytes 1073152 | tf_op jit(solution)/shard_map/pj,pjv->pv/dot_general | solution.py:300
  49.0 1.8 %all-to-all-done.1 = f32[4,4,64,128]{3,2,1,0:T(8,128)S(1)} async-done(((f32[4,4,64,128]{3,2,1,0:T(8,128)}), f32[4,4,64,128]{3,2,1,0:T(8,128)S(1)}, u32[]{:S(2)}, u32[]{:S(2)}) %all-to-all-start.1) | async-done | bytes 524320 | tf_op jit(solution)/shard_map/all_to_all | solution.py:247
  52.3 4.5 %all-to-all-start.2 = ((f32[16,1,768]{2,1,0:T(1,128)}), f32[16,1,768]{2,1,0:T(1,128)S(1)}, u32[]{:S(2)}, u32[]{:S(2)}) async-start(f32[16,1,768]{2,1,0:T(1,128)} %broadcast_in_dim.35), calls=%async_computation.2 | async-start | bytes 98304 | tf_op jit(solution)/shard_map/all_to_all | solution.py:317
  56.8 0.8 %convolution_add_fusion = f32[32,64,128]{2,0,1:T(8,128)S(1)} fusion(f32[32,64,128]{2,0,1:T(8,128)S(1)} %fusion.1, s32[32]{0:T(128)S(1)} %fusion.191, pred[32]{0:T(512)(128)(4,1)S(1)} %get-tuple-element.18, f32[2,8,64,128]{3,2,1,0:T(8,128)S(1)} %bitcast.247), kind=kOutput, calls=%fused_computation.2 | convolution fusion | flops 50594816 | bytes 2621600 | tf_op jit(solution)/shard_map/dot_general | solution.py:258
  57.6 2.2 %fusion.22 = f32[32,64,128]{2,1,0:T(8,128)S(1)} fusion(f32[32,64,128]{2,0,1:T(8,128)S(1)} %convolution_add_fusion, f32[64,64]{1,0:T(8,128)S(1)} %get-tuple-element.99, f32[32]{0:T(128)S(1)} %get-tuple-element.113, f32[64,64]{1,0:T(8,128)S(1)} %get-tuple-element.100, f32[32]{0:T(128)S(1)} %get-tuple-element.114, f32[64,64]{1,0:T(8,128)S(1)} %get-tuple-element.101, ...), kind=kOutput, calls=%fused_computation.37 | convolution fusion | flops 203292672 | bytes 2229248 | tf_op jit(solution)/shard_map/nij,njv->niv/dot_general | solution.py:289
  60.0 3.1 %all-to-all-done.2 = f32[16,1,768]{2,1,0:T(1,128)S(1)} async-done(((f32[16,1,768]{2,1,0:T(1,128)}), f32[16,1,768]{2,1,0:T(1,128)S(1)}, u32[]{:S(2)}, u32[]{:S(2)}) %all-to-all-start.2) | async-done | bytes 49184 | tf_op jit(solution)/shard_map/all_to_all | solution.py:317
  63.3 1.0 %multiply_add_fusion.2 = f32[4,8,8,8,32]{4,3,2,1,0:T(8,128)S(1)} fusion(f32[4,8,8,8,128]{4,3,2,1,0:T(8,128)S(1)} %bitcast.242, f32[4,8]{1,0:T(4,128)S(1)} %get-tuple-element.60, f32[4,8]{1,0:T(4,128)S(1)} %get-tuple-element.61, f32[4,8]{1,0:T(4,128)S(1)} %get-tuple-element.62, f32[4,8]{1,0:T(4,128)S(1)} %get-tuple-element.63), kind=kLoop, calls=%fused_computation.43 | loop fusion | flops 458752 | bytes 1311232 | tf_op jit(solution)/shard_map/add | solution.py:182
  64.4 1.1 %multiply_add_fusion.3 = (f32[4,8,8,8,32]{4,3,2,1,0:T(8,128)S(1)}, f32[4,8,8,8,32]{4,3,2,1,0:T(8,128)S(1)}, f32[4,8,8,8,32]{4,3,2,1,0:T(8,128)S(1)}) fusion(f32[4,8,8,8,128]{4,3,2,1,0:T(8,128)S(1)} %bitcast.243, f32[4,8]{1,0:T(4,128)S(1)} %get-tuple-element.64, f32[4,8]{1,0:T(4,128)S(1)} %get-tuple-element.65, f32[4,8]{1,0:T(4,128)S(1)} %get-tuple-element.54, ...), kind=kLoop, calls=%fused_computation.44 | loop fusion | flops 851968 | bytes 1836032 | tf_op jit(solution)/shard_map/add | solution.py:182
  65.5 0.9 %pad_maximum_fusion.9 = f32[4,8,8,8,128]{4,3,2,1,0:T(8,128)S(1)} fusion(f32[4,8,8,8,32]{4,3,2,1,0:T(8,128)S(1)} %get-tuple-element.36, f32[4,8,8,8,32]{4,3,2,1,0:T(8,128)S(1)} %get-tuple-element.35, f32[4,8,8,8,32]{4,3,2,1,0:T(8,128)S(1)} %multiply_add_fusion.2, f32[4,8,8,8,32]{4,3,2,1,0:T(8,128)S(1)} %get-tuple-element.34), kind=kLoop, calls=%fused_computation.34 | loop fusion | flops 786432 | bytes 2097152 | tf_op jit(solution)/shard_map/concatenate | solution.py:184
  66.8 1.4 %collective-permute-start.7 = (f32[32,1,128]{2,1,0:T(1,128)S(1)}, f32[32,1,128]{2,1,0:T(1,128)S(1)}, u32[]{:S(2)}, u32[]{:S(2)}) collective-permute-start(f32[32,1,128]{2,1,0:T(1,128)S(1)} %get-tuple-element.33), channel_id=1, source_target_pairs={{1,2},{2,1},{3,0},{0,3},{5,6},{6,5},{7,4},{4,7},{9,10},{10,9},{11,... | collective-permute-start | bytes 49160 | tf_op jit(solution)/shard_map/ppermute | solution.py:51
  68.1 1.0 %collective-permute-start.4 = (f32[1,64,128]{2,1,0:T(8,128)S(1)}, f32[1,64,128]{2,1,0:T(8,128)S(1)}, u32[]{:S(2)}, u32[]{:S(2)}) collective-permute-start(f32[1,64,128]{2,1,0:T(8,128)S(1)} %get-tuple-element.30), channel_id=1, source_target_pairs={{0,4},{4,0},{8,12},{12,8},{1,5},{5,1},{9,13},{13,9},{2,6},{6,2},{1... | collective-permute-start | bytes 98312 | tf_op jit(solution)/shard_map/ppermute | solution.py:42
  69.1 2.2 %collective-permute-start.5 = (f32[1,64,128]{2,1,0:T(8,128)S(1)}, f32[1,64,128]{2,1,0:T(8,128)S(1)}, u32[]{:S(2)}, u32[]{:S(2)}) collective-permute-start(f32[1,64,128]{2,1,0:T(8,128)S(1)} %get-tuple-element.31), channel_id=1, source_target_pairs={{4,8},{8,4},{5,9},{9,5},{6,10},{10,6},{7,11},{11,7},{20,24},{24,20... | collective-permute-start | bytes 98312 | tf_op jit(solution)/shard_map/ppermute | solution.py:51
  71.4 3.0 %collective-permute-done.5 = f32[1,64,128]{2,1,0:T(8,128)S(1)} collective-permute-done((f32[1,64,128]{2,1,0:T(8,128)S(1)}, f32[1,64,128]{2,1,0:T(8,128)S(1)}, u32[]{:S(2)}, u32[]{:S(2)}) %collective-permute-start.5) | collective-permute-done | bytes 32800 | tf_op jit(solution)/shard_map/ppermute | solution.py:51
  74.3 1.4 %fusion.11 = f32[32,64,128]{2,1,0:T(8,128)} fusion(f32[32,64,128]{2,1,0:T(8,128)S(1)} %bitcast.250, f32[32,1,128]{2,1,0:T(1,128)S(1)} %bitcast.265, f32[32,1,128]{2,1,0:T(1,128)S(1)} %bitcast.264, f32[1,64,128]{2,1,0:T(8,128)S(1)} %get-tuple-element.47, f32[1,64,128]{2,1,0:T(8,128)S(1)} %get-tuple-element.46, f32[128]{0:T(128)S(1)} %slice_divide_fusion.1, ...), kind=kLoop, calls=%fused_computation.17 | loop fusion | flops 3145728 | bytes 2196096 | tf_op jit(solution)/shard_map/mul | solution.py:334
  (121 shorter events, 14.2 us)
Async XLA Ops:
  4.5 4.5 %copy-start.1 = (f32[2,3,16,32]{3,2,1,0:T(8,128)S(1)}, f32[2,3,16,32]{3,2,1,0:T(8,128)}, u32[]{:S(2)}) copy-start(f32[2,3,16,32]{3,2,1,0:T(8,128)} %param.5) | copy-start | bytes 36868
  4.5 12.2 %all-to-all-start = ((f32[4,4,64,128]{3,2,1,0:T(8,128)}), f32[4,4,64,128]{3,2,1,0:T(8,128)S(1)}, u32[]{:S(2)}, u32[]{:S(2)}) async-start(f32[4,4,64,128]{3,2,1,0:T(8,128)} %bitcast.21), calls=%async_computation | async-start | bytes 1048576 | tf_op jit(solution)/shard_map/all_to_all | solution.py:247
  12.7 0.7 copy-start.2
  23.1 15.8 %copy-start = (f32[32,64,128]{2,1,0:T(8,128)S(1)}, f32[32,64,128]{2,1,0:T(8,128)}, u32[]{:S(2)}) copy-start(f32[32,64,128]{2,1,0:T(8,128)} %param.4) | copy-start | bytes 3145732
  23.3 9.1 %collective-permute-start.2 = (f32[32,1,128]{2,1,0:T(1,128)S(1)}, f32[32,1,128]{2,1,0:T(1,128)S(1)}, u32[]{:S(2)}, u32[]{:S(2)}) collective-permute-start(f32[32,1,128]{2,1,0:T(1,128)S(1)} %get-tuple-element.39), channel_id=1, source_target_pairs={{0,1},{1,0},{2,3},{3,2},{4,5},{5,4},{6,7},{7,6},{8,9},{9,8},{10,11... | collective-permute-start | bytes 49160 | tf_op jit(solution)/shard_map/ppermute | solution.py:42
  25.5 6.9 %collective-permute-start.3 = (f32[32,1,128]{2,1,0:T(1,128)S(1)}, f32[32,1,128]{2,1,0:T(1,128)S(1)}, u32[]{:S(2)}, u32[]{:S(2)}) collective-permute-start(f32[32,1,128]{2,1,0:T(1,128)S(1)} %get-tuple-element.40), channel_id=1, source_target_pairs={{1,2},{2,1},{3,0},{0,3},{5,6},{6,5},{7,4},{4,7},{9,10},{10,9},{11,... | collective-permute-start | bytes 49160 | tf_op jit(solution)/shard_map/ppermute | solution.py:51
  29.0 3.5 %collective-permute-start = (f32[1,65,128]{2,1,0:T(8,128)S(1)}, f32[1,65,128]{2,1,0:T(8,128)S(1)}, u32[]{:S(2)}, u32[]{:S(2)}) collective-permute-start(f32[1,65,128]{2,1,0:T(8,128)S(1)} %get-tuple-element.48), channel_id=1, source_target_pairs={{0,4},{4,0},{8,12},{12,8},{1,5},{5,1},{9,13},{13,9},{2,6},{6,2},{1... | collective-permute-start | bytes 99848 | tf_op jit(solution)/shard_map/ppermute | solution.py:42
  30.5 5.3 %collective-permute-start.1 = (f32[1,65,128]{2,1,0:T(8,128)S(1)}, f32[1,65,128]{2,1,0:T(8,128)S(1)}, u32[]{:S(2)}, u32[]{:S(2)}) collective-permute-start(f32[1,65,128]{2,1,0:T(8,128)S(1)} %get-tuple-element.49), channel_id=1, source_target_pairs={{4,8},{8,4},{5,9},{9,5},{6,10},{10,6},{7,11},{11,7},{20,24},{24,20... | collective-permute-start | bytes 99848 | tf_op jit(solution)/shard_map/ppermute | solution.py:51
  41.3 9.5 %all-to-all-start.1 = ((f32[4,4,64,128]{3,2,1,0:T(8,128)}), f32[4,4,64,128]{3,2,1,0:T(8,128)S(1)}, u32[]{:S(2)}, u32[]{:S(2)}) async-start(f32[4,4,64,128]{3,2,1,0:T(8,128)} %bitcast.47), calls=%async_computation.1 | async-start | bytes 1048576 | tf_op jit(solution)/shard_map/all_to_all | solution.py:247
  52.3 10.8 %all-to-all-start.2 = ((f32[16,1,768]{2,1,0:T(1,128)}), f32[16,1,768]{2,1,0:T(1,128)S(1)}, u32[]{:S(2)}, u32[]{:S(2)}) async-start(f32[16,1,768]{2,1,0:T(1,128)} %broadcast_in_dim.35), calls=%async_computation.2 | async-start | bytes 98304 | tf_op jit(solution)/shard_map/all_to_all | solution.py:317
  66.6 4.7 %collective-permute-start.6 = (f32[32,1,128]{2,1,0:T(1,128)S(1)}, f32[32,1,128]{2,1,0:T(1,128)S(1)}, u32[]{:S(2)}, u32[]{:S(2)}) collective-permute-start(f32[32,1,128]{2,1,0:T(1,128)S(1)} %get-tuple-element.32), channel_id=1, source_target_pairs={{0,1},{1,0},{2,3},{3,2},{4,5},{5,4},{6,7},{7,6},{8,9},{9,8},{10,11... | collective-permute-start | bytes 49160 | tf_op jit(solution)/shard_map/ppermute | solution.py:42
  66.8 4.6 %collective-permute-start.7 = (f32[32,1,128]{2,1,0:T(1,128)S(1)}, f32[32,1,128]{2,1,0:T(1,128)S(1)}, u32[]{:S(2)}, u32[]{:S(2)}) collective-permute-start(f32[32,1,128]{2,1,0:T(1,128)S(1)} %get-tuple-element.33), channel_id=1, source_target_pairs={{1,2},{2,1},{3,0},{0,3},{5,6},{6,5},{7,4},{4,7},{9,10},{10,9},{11,... | collective-permute-start | bytes 49160 | tf_op jit(solution)/shard_map/ppermute | solution.py:51
  68.1 3.2 %collective-permute-start.4 = (f32[1,64,128]{2,1,0:T(8,128)S(1)}, f32[1,64,128]{2,1,0:T(8,128)S(1)}, u32[]{:S(2)}, u32[]{:S(2)}) collective-permute-start(f32[1,64,128]{2,1,0:T(8,128)S(1)} %get-tuple-element.30), channel_id=1, source_target_pairs={{0,4},{4,0},{8,12},{12,8},{1,5},{5,1},{9,13},{13,9},{2,6},{6,2},{1... | collective-permute-start | bytes 98312 | tf_op jit(solution)/shard_map/ppermute | solution.py:42
  69.1 5.2 %collective-permute-start.5 = (f32[1,64,128]{2,1,0:T(8,128)S(1)}, f32[1,64,128]{2,1,0:T(8,128)S(1)}, u32[]{:S(2)}, u32[]{:S(2)}) collective-permute-start(f32[1,64,128]{2,1,0:T(8,128)S(1)} %get-tuple-element.31), channel_id=1, source_target_pairs={{4,8},{8,4},{5,9},{9,5},{6,10},{10,6},{7,11},{11,7},{20,24},{24,20... | collective-permute-start | bytes 98312 | tf_op jit(solution)/shard_map/ppermute | solution.py:51
